TPU v7x, 32 devices: a whole 2x2x4 slice. The times are simulated.
32 devices in a mesh: group: 2 (over y), row: 16 (over z, x, core).
Axes of the slice: x: 2, y: 2, z: 4, core: 2. Of those that a mesh axis runs over, the one named last changes fastest.
Arguments:
- image: bfloat16 [128, 256, 256], P(('group', 'row')), parts along dimension 0, may hold values from -6 to 6
- tissue: int32 [32, 2], P(('group', 'row')), parts along dimension 0, may hold values from 0 to 1, as said below
- kernel: float32 [7, 7, 256], replicated, may hold values from -0.875 to 0.875
- ln_gain: float32 [256], replicated, may hold values from 0.5 to 1.5
- w_in: bfloat16 [256, 1024], replicated, may hold values from -0.375 to 0.375
- w_out: bfloat16 [1024, 256], replicated, may hold values from -0.1875 to 0.1875
- layer_scale: float32 [256], replicated, may hold values from 0.5 to 1.5
- cotangent: bfloat16 [128, 256, 256], P(('group', 'row')), parts along dimension 0, may hold values from -6 to 6
Outputs:
- block_out: bfloat16 [128, 256, 256], P(('group', 'row')), parts along dimension 0
- grad_image: bfloat16 [128, 256, 256], P(('group', 'row')), parts along dimension 0
- grad_w_in: float32 [512, 1024], P(('group', 'row')), parts along dimension 0
- grad_w_out: float32 [2048, 256], P(('group', 'row')), parts along dimension 0
- small_grads: float32 [102, 256], P('group'), parts along dimension 0
There are 2 independent parts, one for each index of `group`. A program takes and returns all parts, laid end to end along the dimension named above; an argument that names none is the same for every part. Nothing has to cross between parts.
Inputs may be any that keep to these rules, and one draw needn't show every extreme that they name: 1 marks a tile of 4 x 128 positions that holds tissue, 0 one without. Among the 2 tiles of the 4 rows of one device, at least one is 0 and at least one is 1.
All inputs are finite; a program needn't handle non-finite values.
Results may differ from a plain program's by a relative error of at most 0.0063.
Values may be sent and summed in bfloat16 or wider, within the bound.
No kernel may reach another device: no remote copies, remote signals or barrier semaphores. Data moves between devices by JAX's collectives and lax.ppermute only.
A program may use at most 64 MiB of HBM per device.

v0:
```python
import jax
import jax.numpy as jnp
from jax import lax
from jax.sharding import PartitionSpec as P

KERNEL = 7
TILE_ROWS = 4
TILE_COLS = 128


EPSILON = 1e-06
ROOT_TWO_PI = 0.7978845608028654
CUBIC_TERM = 0.044715


def padded_2(block, sides, width):
    for axis, dim in sides:
        count = lax.axis_size(axis)
        forward = [(i, i + 1) for i in range(count - 1)]
        backward = [(target, source) for source, target in forward]
        low = lax.ppermute(
            lax.slice_in_dim(block, block.shape[dim] - width, None, axis=dim), axis, forward
        )
        high = lax.ppermute(lax.slice_in_dim(block, 0, width, axis=dim), axis, backward)
        block = jnp.concatenate([low, block, high], axis=dim)
    return block


def gelu_value(inputs):
    tangent = jnp.tanh(ROOT_TWO_PI * (inputs + CUBIC_TERM * inputs * inputs * inputs))
    return 0.5 * inputs * (1.0 + tangent)


def gelu_slope(inputs):
    tangent = jnp.tanh(ROOT_TWO_PI * (inputs + CUBIC_TERM * inputs * inputs * inputs))
    return 0.5 * (1.0 + tangent) + 0.5 * inputs * (1.0 - tangent * tangent) * ROOT_TWO_PI * (
        1.0 + 3.0 * CUBIC_TERM * inputs * inputs
    )


def depthwise(padded, kernel, image_rows, image_cols):
    total = jnp.zeros((image_rows, image_cols, kernel.shape[-1]), jnp.float32)
    for row_tap in range(KERNEL):
        for col_tap in range(KERNEL):
            total = (
                total
                + padded[row_tap : row_tap + image_rows, col_tap : col_tap + image_cols]
                * kernel[row_tap, col_tap]
            )
    return total


def kernel_terms(padded, grads, image_rows, image_cols):
    collected = []
    for row_tap in range(KERNEL):
        for col_tap in range(KERNEL):
            collected.append(
                jnp.sum(
                    padded[row_tap : row_tap + image_rows, col_tap : col_tap + image_cols] * grads,
                    axis=(0, 1),
                )
            )
    return jnp.stack(collected)


def shards(image, tissue, kernel, ln_gain, w_in, w_out, layer_scale, cotangent):
    half_width = KERNEL // 2
    image_rows, image_cols, channels = image.shape
    hidden = w_in.shape[1]
    tile_size = TILE_ROWS * TILE_COLS

    def to_tiles(values):
        depth_last = values.shape[-1]
        values = values.reshape(
            image_rows // TILE_ROWS, TILE_ROWS, image_cols // TILE_COLS, TILE_COLS, depth_last
        )
        return values.transpose(0, 2, 1, 3, 4).reshape(-1, tile_size, depth_last)

    def from_tiles(values):
        depth_last = values.shape[-1]
        values = values.reshape(
            image_rows // TILE_ROWS, image_cols // TILE_COLS, TILE_ROWS, TILE_COLS, depth_last
        )
        return values.transpose(0, 2, 1, 3, 4).reshape(image_rows, image_cols, depth_last)

    extended = padded_2(image, (("row", 0),), half_width)
    padded = jnp.pad(extended.astype(jnp.float32), ((0, 0), (half_width, half_width), (0, 0)))
    filtered = depthwise(padded, kernel, image_rows, image_cols)
    centre = jnp.mean(filtered, axis=-1, keepdims=True)
    centered = filtered - centre
    inv_std = lax.rsqrt(jnp.mean(centered * centered, axis=-1, keepdims=True) + EPSILON)
    standard = centered * inv_std
    normed = (standard * ln_gain).astype(jnp.bfloat16)
    tissue_at = jnp.repeat(jnp.repeat(tissue, TILE_ROWS, axis=0), TILE_COLS, axis=1).astype(
        jnp.float32
    )[:, :, None]
    upstream = cotangent.astype(jnp.float32)
    grad_out = (tissue_at * layer_scale * upstream).astype(jnp.bfloat16)
    normed_tiles = to_tiles(normed)
    grad_tiles = to_tiles(grad_out)
    has_tissue = tissue.reshape(-1)

    def tile_work(normed_blk, grad_blk):
        pre_act = jnp.dot(normed_blk, w_in, preferred_element_type=jnp.float32)
        activation = gelu_value(pre_act).astype(jnp.bfloat16)
        branch = jnp.dot(activation, w_out, preferred_element_type=jnp.float32)
        grad_act = jnp.dot(grad_blk, w_out.T, preferred_element_type=jnp.float32)
        grad_pre = (grad_act * gelu_slope(pre_act)).astype(jnp.bfloat16)
        grad_norm = jnp.dot(grad_pre, w_in.T, preferred_element_type=jnp.float32)
        return (activation, branch, grad_pre, grad_norm)

    def per_tile(record):
        return tile_work(record[0], record[1])

    act_tiles, branch_tiles, pre_tiles, norm_tiles = lax.map(
        per_tile, (normed_tiles, grad_tiles, has_tissue)
    )
    normed_flat = normed_tiles.reshape(-1, channels)
    grad_flat = grad_tiles.reshape(-1, channels)
    act_flat = act_tiles.reshape(-1, hidden)
    pre_flat = pre_tiles.reshape(-1, hidden)
    section = normed_flat
    grad_w_in = lax.psum_scatter(
        lax.dot_general(
            section, pre_flat, (((0,), (0,)), ((), ())), preferred_element_type=jnp.float32
        ),
        "row",
        scatter_dimension=0,
        tiled=True,
    )
    section = act_flat
    grad_w_out = lax.psum_scatter(
        lax.dot_general(
            section, grad_flat, (((0,), (0,)), ((), ())), preferred_element_type=jnp.float32
        ),
        "row",
        scatter_dimension=0,
        tiled=True,
    )
    branch = from_tiles(branch_tiles)
    grad_norm = from_tiles(norm_tiles)
    block_out = (image.astype(jnp.float32) + tissue_at * layer_scale * branch).astype(jnp.bfloat16)
    scale_grad = jnp.sum(tissue_at * branch * upstream, axis=(0, 1))
    gain_grad = jnp.sum(grad_norm * standard, axis=(0, 1))
    grad_std = grad_norm * ln_gain
    grad_conv = (
        inv_std
        * (
            grad_std
            - jnp.mean(grad_std, axis=-1, keepdims=True)
            - standard * jnp.mean(grad_std * standard, axis=-1, keepdims=True)
        )
    ).astype(jnp.bfloat16)
    grad_float = grad_conv.astype(jnp.float32)
    kernel_grad = kernel_terms(padded, grad_float, image_rows, image_cols)
    packed = jnp.concatenate([kernel_grad, gain_grad[None], scale_grad[None]], axis=0)
    small_grads = lax.psum(packed, "row")
    grad_ext = padded_2(grad_conv, (("row", 0),), half_width)
    grad_padded = jnp.pad(grad_ext.astype(jnp.float32), ((0, 0), (half_width, half_width), (0, 0)))
    conv_back = depthwise(grad_padded, kernel[::-1, ::-1], image_rows, image_cols)
    grad_image = (upstream + conv_back).astype(jnp.bfloat16)
    return (block_out, grad_image, grad_w_in, grad_w_out, small_grads)


def solution(mesh):
    placed = (
        P(("group", "row"), None, None),
        P(("group", "row"), None),
        P(),
        P(),
        P(),
        P(),
        P(),
        P(("group", "row"), None, None),
    )
    return jax.shard_map(
        shards,
        mesh=mesh,
        in_specs=placed,
        out_specs=(
            P(("group", "row"), None, None),
            P(("group", "row"), None, None),
            P(("group", "row"), None),
            P(("group", "row"), None),
            P("group", None),
        ),
        check_vma=False,
    )
```

profile of v0, /device:TPU:0, one launch (start us, length us, event | category | flops | bytes accessed | tf_op | source)
XLA Modules:
  0.0 192.2 jit_solution(3248807306275557346)
XLA Ops:
  7.2 1.2 fusion.134
  8.5 2.4 %collective-permute-start = (bf16[3,256,256]{2,1,0:T(8,128)(2,1)S(1)}, bf16[3,256,256]{2,1,0:T(8,128)(2,1)S(1)}, u32[]{:S(2)}, u32[]{:S(2)}) collective-permute-start(bf16[3,256,256]{2,1,0:T(8,128)(2,1)S(1)} %get-tuple-element.138), channel_id=1, source_target_pairs={{0,1},{1,2},{2,3},{3,4},{4,5},{5,6},{6,7},{7,8},{8,9},{9,10},{10,1... | collective-permute-start | bytes 1179656 | tf_op jit(solution)/shard_map/ppermute | solution.py:21
  10.8 1.3 collective-permute-start.1
  12.2 0.7 convert_bitcast_fusion
  12.9 1.6 fusion.135
  14.5 1.2 fusion.18
  15.7 0.8 copy.24
  16.6 0.6 fusion.137
  17.2 0.7 fusion.136
  17.9 1.2 maximum_convert_fusion
  19.1 10.2 %fusion.132 = (f32[4,256]{1,0:T(4,128)S(1)}, f32[4,256,256]{2,1,0:T(8,128)}) fusion(f32[256]{0:T(256)} %bitcast.255, f32[256]{0:T(256)} %bitcast.257, f32[256]{0:T(256)S(1)} %bitcast.201, f32[256]{0:T(256)S(1)} %bitcast.203, f32[10,256,256]{2,1,0:T(8,128)S(1)} %maximum_convert_fusion, f32[256]{0:T(256)S(1)} %bitcast.205, f32[256]{0:T(256)} %bitcast.207, ...), kind=kLoop, calls=%fused_computation.229 | loop fusion | flops 25689088 | bytes 11064320 | tf_op jit(solution)/shard_map/reduce_sum | solution.py:89
  29.3 1.7 multiply_reduce_fusion.2
  31.0 1.6 multiply_convert_fusion.3
  32.5 0.8 copy.23
  33.4 16.7 %while.16 = (s32[]{:T(128)}, bf16[2,512,1024]{2,1,0:T(8,128)(2,1)}, f32[2,512,256]{2,1,0:T(8,128)}, bf16[2,512,1024]{2,1,0:T(8,128)(2,1)}, f32[2,512,256]{2,1,0:...) while((s32[]{:T(128)}, bf16[2,512,1024]{2,1,0:T(8,128)(2,1)}, ...), condition=%wide.region_3.4_spmd, body=%wide.region_2.3_spmd.sunk | while | flops 1093140480 | bytes 51906900 | solution.py:115
  33.4 2.9 %bitcast_dynamic-update-slice_fusion.4 = (bf16[2,512,1024]{2,1,0:T(8,128)(2,1)}, f32[512,1024]{1,0:T(8,128)S(1)}) fusion(bf16[2,512,1024]{2,1,0:T(8,128)(2,1)} %get-tuple-element.263, s32[]{:T(128)S(6)} %copy.42, bf16[256,1024]{1,0:T(8,128)(2,1)S(1)} %get-tuple-element.278, bf16[2,512,256]{2,1,0:T(8,128)(2,1)} %get-tuple-element.277), kind=kOutput, calls=%fused_computation.15.clone.1 | convolution fusion | flops 273154048 | bytes 3933184 | tf_op jit(solution)/shard_map/while/body/eval_jaxpr/dot_general | solution.py:104
  36.3 0.8 fusion.161
  37.1 0.8 copy-done.7
  37.9 1.4 bitcast_dynamic-update-slice_fusion.5
  39.5 0.5 fusion.162
  40.0 0.7 copy-done.8
  40.7 1.0 copy-done.6
  41.7 2.9 %bitcast_dynamic-update-slice_fusion.4 = (bf16[2,512,1024]{2,1,0:T(8,128)(2,1)}, f32[512,1024]{1,0:T(8,128)S(1)}) fusion(bf16[2,512,1024]{2,1,0:T(8,128)(2,1)} %get-tuple-element.263, s32[]{:T(128)S(6)} %copy.42, bf16[256,1024]{1,0:T(8,128)(2,1)S(1)} %get-tuple-element.278, bf16[2,512,256]{2,1,0:T(8,128)(2,1)} %get-tuple-element.277), kind=kOutput, calls=%fused_computation.15.clone.1 | convolution fusion | flops 273154048 | bytes 3933184 | tf_op jit(solution)/shard_map/while/body/eval_jaxpr/dot_general | solution.py:104
  44.6 0.8 fusion.161
  45.5 0.8 copy-done.7
  46.3 1.4 bitcast_dynamic-update-slice_fusion.5
  48.4 0.7 copy-done.8
  49.1 1.0 copy-done.6
  50.1 1.5 fusion.116
  51.6 1.3 copy.26
  53.0 0.9 multiply_reduce_fusion
  53.8 2.3 %fusion.65 = (f32[256]{0:T(256)}, f32[256]{0:T(256)}, f32[256]{0:T(256)}, f32[256]{0:T(256)}, f32[256]{0:T(256)}, /*index=5*/f32[256]{0:T(256)}, f32[256]{0:T(25...) fusion(f32[10,256,256]{2,1,0:T(8,128)S(1)} %maximum_convert_fusion, f32[4,256]{1,0:T(4,128)S(1)} %broadcast_multiply_fusion, ...), kind=kLoop, calls=%fused_computation.127 | loop fusion | flops 7075584 | bytes 6318080 | tf_op jit(solution)/shard_map/reduce_sum | solution.py:58
  56.1 1.9 fusion.67
  58.0 0.8 fusion.133
  58.8 1.7 fusion.139
  60.6 7.4 %collective-permute-start.2 = (bf16[3,256,256]{2,1,0:T(8,128)(2,1)}, bf16[3,256,256]{2,1,0:T(8,128)(2,1)}, u32[]{:S(2)}, u32[]{:S(2)}) collective-permute-start(bf16[3,256,256]{2,1,0:T(8,128)(2,1)} %get-tuple-element.136), channel_id=1, source_target_pairs={{0,1},{1,2},{2,3},{3,4},{4,5},{5,6},{6,7},{7,8},{8,9},{9,10},{10,1... | collective-permute-start | bytes 1179656 | tf_op jit(solution)/shard_map/ppermute | solution.py:21
  68.0 1.5 collective-permute-start.3
  69.5 3.5 %fusion.138 = f32[256,1024]{1,0:T(8,128)} fusion(bf16[1024,256]{1,0:T(8,128)(2,1)} %bitcast.192, bf16[1024,1024]{1,0:T(8,128)(2,1)} %bitcast.190), kind=kOutput, calls=%fused_computation.235 | convolution fusion | flops 536870912 | bytes 3670016 | tf_op jit(solution)/shard_map/dot_general | solution.py:124
  73.0 1.9 %fusion.68 = (f32[256]{0:T(256)}, f32[256]{0:T(256)}, f32[256]{0:T(256)}, f32[256]{0:T(256)}, f32[256]{0:T(256)}, /*index=5*/f32[256]{0:T(256)}, f32[256]{0:T(256)}, f32[256]{0:T(256)}, f32[256]{0:T(256)}, f32[256]{0:T(256)}) fusion(bf16[4,256,256]{2,1,0:T(8,128)(2,1)S(1)} %get-tuple-element.127, f32[10,256,256]{2,1,0:T(8,128)S(1)} %maximum_convert_fusion), kind=kLoop, calls=%fused_computation.130 | loop fusion | flops 5502464 | bytes 5253120 | tf_op jit(solution)/shard_map/reduce_sum | solution.py:58
  75.0 1.9 %fusion.69 = (f32[256]{0:T(256)}, f32[256]{0:T(256)}, f32[256]{0:T(256)}, f32[256]{0:T(256)}, f32[256]{0:T(256)}, /*index=5*/f32[256]{0:T(256)}, f32[256]{0:T(256)}, f32[256]{0:T(256)}, f32[256]{0:T(256)}, f32[256]{0:T(256)}) fusion(bf16[4,256,256]{2,1,0:T(8,128)(2,1)S(1)} %get-tuple-element.127, f32[10,256,256]{2,1,0:T(8,128)S(1)} %maximum_convert_fusion), kind=kLoop, calls=%fused_computation.131 | loop fusion | flops 5502464 | bytes 5253120 | tf_op jit(solution)/shard_map/reduce_sum | solution.py:58
  76.9 2.0 %fusion.66 = (f32[256]{0:T(256)}, f32[256]{0:T(256)}, f32[256]{0:T(256)}, f32[256]{0:T(256)}, f32[256]{0:T(256)}, /*index=5*/f32[256]{0:T(256)}, f32[256]{0:T(256)}, f32[256]{0:T(256)}, f32[256]{0:T(256)}, f32[256]{0:T(256)}) fusion(bf16[4,256,256]{2,1,0:T(8,128)(2,1)S(1)} %get-tuple-element.127, f32[10,256,256]{2,1,0:T(8,128)S(1)} %maximum_convert_fusion), kind=kLoop, calls=%fused_computation.128 | loop fusion | flops 5502464 | bytes 5253120 | tf_op jit(solution)/shard_map/reduce_sum | solution.py:58
  78.9 0.8 fusion.21
  81.0 1.8 fusion.20
  83.2 3.5 %concatenate.11 = f32[51,256]{1,0:T(8,128)S(1)} concatenate(f32[1,256]{1,0:T(1,128)} %bitcast.346, f32[1,256]{1,0:T(1,128)S(1)} %bitcast.327, f32[1,256]{1,0:T(1,128)S(1)} %bitcast.328, f32[1,256]{1,0:T(1,128)S(1)} %bitcast.329, f32[1,256]{1,0:T(1,128)S(1)} %bitcast.330, f32[1,256]{1,0:T(1,128)S(1)} %bitcast.331, f32[1,256]{1,0:T(1,128)S(1)} %bitcast.332, ...), dimensions={0} | concatenate | bytes 104448 | tf_op jit(solution)/shard_map/concatenate | solution.py:156
  86.7 62.9 %psum.7 = f32[51,256]{1,0:T(8,128)} all-reduce(f32[51,256]{1,0:T(8,128)S(1)} %concatenate.11), channel_id=1, replica_groups=mesh['group'=2,'row'=16] {'row'}, use_global_device_ids=true, to_apply=%region_59.60 | all-reduce | flops 13056 | bytes 104448 | tf_op jit(solution)/shard_map/psum | solution.py:157
  149.6 1.3 maximum_convert_fusion.1
  150.9 10.1 %fusion.19 = bf16[4,256,256]{2,1,0:T(8,128)(2,1)} fusion(bf16[4,256,256]{2,1,0:T(8,128)(2,1)} %param.17, f32[10,256,256]{2,1,0:T(8,128)S(1)} %maximum_convert_fusion.1, f32[256]{0:T(256)} %bitcast.256, f32[256]{0:T(256)} %bitcast.258, f32[256]{0:T(256)S(1)} %bitcast.202, f32[256]{0:T(256)S(1)} %bitcast.204, f32[256]{0:T(256)S(1)} %bitcast.206, ...), kind=kLoop, calls=%fused_computation.81 | loop fusion | flops 26214400 | bytes 11060224 | tf_op jit(solution)/shard_map/convert_element_type | solution.py:161
  161.0 24.4 %reduce-scatter.3.cloned.1.call-done = f32[16,1024]{1,0:T(8,128)} async-done(((f32[256,1024]{1,0:T(8,128)}), f32[16,1024]{1,0:T(8,128)}) %reduce-scatter.3.cloned.1.call-update) | async-done | bytes 65552 | tf_op jit(solution)/shard_map/reduce_scatter | solution.py:123
  (145 shorter events, 2.3 us)
Async XLA Ops:
  7.2 10.7 %copy-start.2 = (bf16[4,256,256]{2,1,0:T(8,128)(2,1)S(1)}, bf16[4,256,256]{2,1,0:T(8,128)(2,1)}, u32[]{:S(2)}) copy-start(bf16[4,256,256]{2,1,0:T(8,128)(2,1)} %param.10) | copy-start | bytes 1572868
  7.2 9.4 %copy-start.14 = (f32[7,7,256]{2,1,0:T(8,128)S(1)}, f32[7,7,256]{2,1,0:T(8,128)}, u32[]{:S(2)}) copy-start(f32[7,7,256]{2,1,0:T(8,128)} %param.12) | copy-start | bytes 150532
  7.2 153.8 %reduce-scatter.5.cloned.1.call-start = ((), (), s32[]{:S(2)}) async-start(), calls=%async_computation.3 | async-start | bytes 1114112 | tf_op jit(solution)/shard_map/reduce_scatter | solution.py:132
  8.5 9.4 %collective-permute-start = (bf16[3,256,256]{2,1,0:T(8,128)(2,1)S(1)}, bf16[3,256,256]{2,1,0:T(8,128)(2,1)S(1)}, u32[]{:S(2)}, u32[]{:S(2)}) collective-permute-start(bf16[3,256,256]{2,1,0:T(8,128)(2,1)S(1)} %get-tuple-element.138), channel_id=1, source_target_pairs={{0,1},{1,2},{2,3},{3,4},{4,5},{5,6},{6,7},{7,8},{8,9},{9,10},{10,1... | collective-permute-start | bytes 1179656 | tf_op jit(solution)/shard_map/ppermute | solution.py:21
  10.8 7.0 %collective-permute-start.1 = (bf16[3,256,256]{2,1,0:T(8,128)(2,1)S(1)}, bf16[3,256,256]{2,1,0:T(8,128)(2,1)}, u32[]{:S(2)}, u32[]{:S(2)}) collective-permute-start(bf16[3,256,256]{2,1,0:T(8,128)(2,1)S(1)} %get-tuple-element.139), channel_id=1, source_target_pairs={{1,0},{2,1},{3,2},{4,3},{5,4},{6,5},{7,6},{8,7},{9,8},{10,9},{11,1... | collective-permute-start | bytes 1179656 | tf_op jit(solution)/shard_map/ppermute | solution.py:24
  12.9 5.0 %copy-start.54 = (f32[256]{0:T(256)}, f32[256]{0:T(256)S(1)}, u32[]{:S(2)}) copy-start(f32[256]{0:T(256)S(1)} %broadcast_bitcast_fusion) | copy-start | bytes 3076
  19.1 11.9 %copy-start.15 = (f32[256]{0:T(256)S(1)}, f32[256]{0:T(256)}, u32[]{:S(2)}) copy-start(f32[256]{0:T(256)} %param.13) | copy-start | bytes 3076
  29.3 4.1 %copy-start.1 = (bf16[256,1024]{1,0:T(8,128)(2,1)S(1)}, bf16[256,1024]{1,0:T(8,128)(2,1)}, u32[]{:S(2)}) copy-start(bf16[256,1024]{1,0:T(8,128)(2,1)} %param.14) | copy-start | bytes 1572868
  33.4 2.9 %copy-start.9 = (f32[2,512,256]{2,1,0:T(8,128)S(1)}, f32[2,512,256]{2,1,0:T(8,128)}, u32[]{:S(2)}) copy-start(f32[2,512,256]{2,1,0:T(8,128)} %get-tuple-element.264) | copy-start | bytes 3145732 | tf_op jit(solution)/shard_map/while
  33.4 2.9 %copy-start.55 = (bf16[1024,256]{1,0:T(8,128)(2,1)S(1)}, bf16[1024,256]{1,0:T(8,128)(2,1)}, u32[]{:S(2)}) copy-start(bf16[1024,256]{1,0:T(8,128)(2,1)} %get-tuple-element.279) | copy-start | bytes 1572868 | tf_op jit(solution)/shard_map/while
  41.7 2.9 %copy-start.9 = (f32[2,512,256]{2,1,0:T(8,128)S(1)}, f32[2,512,256]{2,1,0:T(8,128)}, u32[]{:S(2)}) copy-start(f32[2,512,256]{2,1,0:T(8,128)} %get-tuple-element.264) | copy-start | bytes 3145732 | tf_op jit(solution)/shard_map/while
  41.7 2.9 %copy-start.55 = (bf16[1024,256]{1,0:T(8,128)(2,1)S(1)}, bf16[1024,256]{1,0:T(8,128)(2,1)}, u32[]{:S(2)}) copy-start(bf16[1024,256]{1,0:T(8,128)(2,1)} %get-tuple-element.279) | copy-start | bytes 1572868 | tf_op jit(solution)/shard_map/while
  50.1 2.9 %copy-start = (f32[4,256,256]{2,1,0:T(8,128)S(1)}, f32[4,256,256]{2,1,0:T(8,128)}, u32[]{:S(2)}) copy-start(f32[4,256,256]{2,1,0:T(8,128)} %get-tuple-element.129) | copy-start | bytes 3145732
  56.1 2.7 %copy-start.13 = (bf16[2,512,256]{2,1,0:T(8,128)(2,1)S(1)}, bf16[2,512,256]{2,1,0:T(8,128)(2,1)}, u32[]{:S(2)}) copy-start(bf16[2,512,256]{2,1,0:T(8,128)(2,1)} %get-tuple-element.289) | copy-start | bytes 1572868
  56.1 2.7 %copy-start.56 = (bf16[2,512,1024]{2,1,0:T(8,128)(2,1)S(1)}, bf16[2,512,1024]{2,1,0:T(8,128)(2,1)}, u32[]{:S(2)}) copy-start(bf16[2,512,1024]{2,1,0:T(8,128)(2,1)} %get-tuple-element.58) | copy-start | bytes 6291460
  60.6 124.8 %reduce-scatter.3.cloned.1.call-start = ((), (), s32[]{:S(2)}) async-start(), calls=%async_computation.2 | async-start | bytes 1114112 | tf_op jit(solution)/shard_map/reduce_scatter | solution.py:123
  60.6 88.9 %collective-permute-start.2 = (bf16[3,256,256]{2,1,0:T(8,128)(2,1)}, bf16[3,256,256]{2,1,0:T(8,128)(2,1)}, u32[]{:S(2)}, u32[]{:S(2)}) collective-permute-start(bf16[3,256,256]{2,1,0:T(8,128)(2,1)} %get-tuple-element.136), channel_id=1, source_target_pairs={{0,1},{1,2},{2,3},{3,4},{4,5},{5,6},{6,7},{7,8},{8,9},{9,10},{10,1... | collective-permute-start | bytes 1179656 | tf_op jit(solution)/shard_map/ppermute | solution.py:21
  68.0 81.6 %collective-permute-start.3 = (bf16[3,256,256]{2,1,0:T(8,128)(2,1)S(1)}, bf16[3,256,256]{2,1,0:T(8,128)(2,1)}, u32[]{:S(2)}, u32[]{:S(2)}) collective-permute-start(bf16[3,256,256]{2,1,0:T(8,128)(2,1)S(1)} %get-tuple-element.137), channel_id=1, source_target_pairs={{1,0},{2,1},{3,2},{4,3},{5,4},{6,5},{7,6},{8,7},{9,8},{10,9},{11,1... | collective-permute-start | bytes 1179656 | tf_op jit(solution)/shard_map/ppermute | solution.py:24
  80.2 2.6 %copy-start.16 = (f32[256]{0:T(256)S(1)}, f32[256]{0:T(256)}, u32[]{:S(2)}) copy-start(f32[256]{0:T(256)} %get-tuple-element.107) | copy-start | bytes 3076
  80.3 2.6 %copy-start.17 = (f32[256]{0:T(256)S(1)}, f32[256]{0:T(256)}, u32[]{:S(2)}) copy-start(f32[256]{0:T(256)} %get-tuple-element.98) | copy-start | bytes 3076
  80.3 2.6 %copy-start.18 = (f32[256]{0:T(256)S(1)}, f32[256]{0:T(256)}, u32[]{:S(2)}) copy-start(f32[256]{0:T(256)} %get-tuple-element.99) | copy-start | bytes 3076
  80.3 2.6 %copy-start.19 = (f32[256]{0:T(256)S(1)}, f32[256]{0:T(256)}, u32[]{:S(2)}) copy-start(f32[256]{0:T(256)} %get-tuple-element.100) | copy-start | bytes 3076
  80.3 2.6 %copy-start.20 = (f32[256]{0:T(256)S(1)}, f32[256]{0:T(256)}, u32[]{:S(2)}) copy-start(f32[256]{0:T(256)} %get-tuple-element.101) | copy-start | bytes 3076
  80.3 2.6 %copy-start.21 = (f32[256]{0:T(256)S(1)}, f32[256]{0:T(256)}, u32[]{:S(2)}) copy-start(f32[256]{0:T(256)} %get-tuple-element.102) | copy-start | bytes 3076
  80.3 2.6 %copy-start.22 = (f32[256]{0:T(256)S(1)}, f32[256]{0:T(256)}, u32[]{:S(2)}) copy-start(f32[256]{0:T(256)} %get-tuple-element.103) | copy-start | bytes 3076
  80.3 2.6 %copy-start.23 = (f32[256]{0:T(256)S(1)}, f32[256]{0:T(256)}, u32[]{:S(2)}) copy-start(f32[256]{0:T(256)} %get-tuple-element.104) | copy-start | bytes 3076
  80.3 2.6 %copy-start.24 = (f32[256]{0:T(256)S(1)}, f32[256]{0:T(256)}, u32[]{:S(2)}) copy-start(f32[256]{0:T(256)} %get-tuple-element.105) | copy-start | bytes 3076
  80.3 2.6 %copy-start.25 = (f32[256]{0:T(256)S(1)}, f32[256]{0:T(256)}, u32[]{:S(2)}) copy-start(f32[256]{0:T(256)} %get-tuple-element.106) | copy-start | bytes 3076
  80.3 2.6 %copy-start.26 = (f32[256]{0:T(256)S(1)}, f32[256]{0:T(256)}, u32[]{:S(2)}) copy-start(f32[256]{0:T(256)} %get-tuple-element.79) | copy-start | bytes 3076
  80.4 2.6 %copy-start.27 = (f32[256]{0:T(256)S(1)}, f32[256]{0:T(256)}, u32[]{:S(2)}) copy-start(f32[256]{0:T(256)} %get-tuple-element.80) | copy-start | bytes 3076
  80.4 2.6 %copy-start.28 = (f32[256]{0:T(256)S(1)}, f32[256]{0:T(256)}, u32[]{:S(2)}) copy-start(f32[256]{0:T(256)} %get-tuple-element.81) | copy-start | bytes 3076
  80.4 2.6 %copy-start.29 = (f32[256]{0:T(256)S(1)}, f32[256]{0:T(256)}, u32[]{:S(2)}) copy-start(f32[256]{0:T(256)} %get-tuple-element.82) | copy-start | bytes 3076
  80.4 2.6 %copy-start.30 = (f32[256]{0:T(256)S(1)}, f32[256]{0:T(256)}, u32[]{:S(2)}) copy-start(f32[256]{0:T(256)} %get-tuple-element.83) | copy-start | bytes 3076
  80.4 2.6 %copy-start.31 = (f32[256]{0:T(256)S(1)}, f32[256]{0:T(256)}, u32[]{:S(2)}) copy-start(f32[256]{0:T(256)} %get-tuple-element.84) | copy-start | bytes 3076
  80.4 2.6 %copy-start.32 = (f32[256]{0:T(256)S(1)}, f32[256]{0:T(256)}, u32[]{:S(2)}) copy-start(f32[256]{0:T(256)} %get-tuple-element.85) | copy-start | bytes 3076
  80.4 2.6 %copy-start.33 = (f32[256]{0:T(256)S(1)}, f32[256]{0:T(256)}, u32[]{:S(2)}) copy-start(f32[256]{0:T(256)} %get-tuple-element.86) | copy-start | bytes 3076
  80.4 2.6 %copy-start.34 = (f32[256]{0:T(256)S(1)}, f32[256]{0:T(256)}, u32[]{:S(2)}) copy-start(f32[256]{0:T(256)} %get-tuple-element.87) | copy-start | bytes 3076
  80.4 2.6 %copy-start.35 = (f32[256]{0:T(256)S(1)}, f32[256]{0:T(256)}, u32[]{:S(2)}) copy-start(f32[256]{0:T(256)} %get-tuple-element.69) | copy-start | bytes 3076
  80.4 2.6 %copy-start.36 = (f32[256]{0:T(256)S(1)}, f32[256]{0:T(256)}, u32[]{:S(2)}) copy-start(f32[256]{0:T(256)} %get-tuple-element.70) | copy-start | bytes 3076
  80.5 2.6 %copy-start.37 = (f32[256]{0:T(256)S(1)}, f32[256]{0:T(256)}, u32[]{:S(2)}) copy-start(f32[256]{0:T(256)} %get-tuple-element.71) | copy-start | bytes 3076
  80.5 2.6 %copy-start.38 = (f32[256]{0:T(256)S(1)}, f32[256]{0:T(256)}, u32[]{:S(2)}) copy-start(f32[256]{0:T(256)} %get-tuple-element.72) | copy-start | bytes 3076
  80.5 2.6 %copy-start.39 = (f32[256]{0:T(256)S(1)}, f32[256]{0:T(256)}, u32[]{:S(2)}) copy-start(f32[256]{0:T(256)} %get-tuple-element.73) | copy-start | bytes 3076
  80.5 2.6 %copy-start.40 = (f32[256]{0:T(256)S(1)}, f32[256]{0:T(256)}, u32[]{:S(2)}) copy-start(f32[256]{0:T(256)} %get-tuple-element.74) | copy-start | bytes 3076
  80.5 2.6 %copy-start.41 = (f32[256]{0:T(256)S(1)}, f32[256]{0:T(256)}, u32[]{:S(2)}) copy-start(f32[256]{0:T(256)} %get-tuple-element.75) | copy-start | bytes 3076
  80.5 2.6 %copy-start.42 = (f32[256]{0:T(256)S(1)}, f32[256]{0:T(256)}, u32[]{:S(2)}) copy-start(f32[256]{0:T(256)} %get-tuple-element.76) | copy-start | bytes 3076
  80.5 2.6 %copy-start.43 = (f32[256]{0:T(256)S(1)}, f32[256]{0:T(256)}, u32[]{:S(2)}) copy-start(f32[256]{0:T(256)} %get-tuple-element.77) | copy-start | bytes 3076
  80.5 2.6 %copy-start.44 = (f32[256]{0:T(256)S(1)}, f32[256]{0:T(256)}, u32[]{:S(2)}) copy-start(f32[256]{0:T(256)} %get-tuple-element.78) | copy-start | bytes 3076
  80.5 2.6 %copy-start.45 = (f32[256]{0:T(256)S(1)}, f32[256]{0:T(256)}, u32[]{:S(2)}) copy-start(f32[256]{0:T(256)} %get-tuple-element.59) | copy-start | bytes 3076
  (23 other events, 41.5 us)
Sparse Core Ops, SparseCore 0:
  60.7 63.5 reduce-scatter.4
  128.9 56.4 reduce-scatter.2
where the time goes:
time: 193 us; the launch traced here: 192 us
  blocking collectives  62.9 us (33%)
  other arithmetic  43 us (22%)
  waiting for transfers between devices  24.4 us (13%)
  local copies, waits for them, and re-layouts  17.9 us (9%)
  matrix products  16.5 us (9%)
  between operations  14.9 us (8%)
  starting transfers between devices  12.6 us (7%)
    psum x1, blocking collectives, shards(): small_grads = lax.psum(packed, 'row')  62.9 us
    reduce_scatter x1, waiting for transfers between devices, shards(): lax.psum_scatter(lax.dot_general(section, pre_flat, (((0,), (0,)), ((), (...  24.4 us
    reduce_sum x6, other arithmetic, kernel_terms(): jnp.sum(padded[row_tap:row_tap + image_rows, col_tap:col_tap + image_cols...  10.9 us
    reduce_sum x1, other arithmetic, shards(): centre = jnp.mean(filtered, axis=-1, keepdims=True)  10.2 us
    convert_element_type x1, other arithmetic, shards(): grad_image = (upstream + conv_back).astype(jnp.bfloat16)  10.1 us
    ppermute x2, starting transfers between devices, padded_2(): lax.ppermute(lax.slice_in_dim(block, block.shape[dim] - width, None, axis...  9.77 us
    dot_general x2, matrix products, tile_work(): pre_act = jnp.dot(normed_blk, w_in, preferred_element_type=jnp.float32)  5.8 us
    while x32, local copies, waits for them, and re-layouts  5.38 us
  transfers between devices with their start and end apart: 6, of which 1 were waited for; matrix products, arithmetic and copies ran while one was open for 17% of the time, Pallas kernels for 0%

commit v1 on v0

--- a/solution.py
+++ b/solution.py
@@ -24,6 +24,24 @@
         high = lax.ppermute(lax.slice_in_dim(block, 0, width, axis=dim), axis, backward)
         block = jnp.concatenate([low, block, high], axis=dim)
     return block
+
+
+def halving_reduce(blocks, whole, axis):
+    count = lax.axis_size(axis)
+    steps = count.bit_length() - 1
+    if (1 << steps) != count:
+        return lax.psum_scatter(blocks, axis, scatter_dimension=0, tiled=True), lax.psum(whole, axis)
+    me = lax.axis_index(axis)
+    for step in range(steps):
+        bit = (me >> step) & 1
+        pairs = [(i, i ^ (1 << step)) for i in range(count)]
+        halves = blocks.reshape(blocks.shape[0] // 2, 2, -1)
+        keep = lax.dynamic_index_in_dim(halves, bit, axis=1, keepdims=False)
+        give = lax.dynamic_index_in_dim(halves, 1 - bit, axis=1, keepdims=False)
+        got, got_whole = lax.ppermute((give, whole), axis, pairs)
+        blocks = keep + got
+        whole = whole + got_whole
+    return blocks, whole
 
 
 def gelu_value(inputs):
@@ -119,23 +137,11 @@
     grad_flat = grad_tiles.reshape(-1, channels)
     act_flat = act_tiles.reshape(-1, hidden)
     pre_flat = pre_tiles.reshape(-1, hidden)
-    section = normed_flat
-    grad_w_in = lax.psum_scatter(
-        lax.dot_general(
-            section, pre_flat, (((0,), (0,)), ((), ())), preferred_element_type=jnp.float32
-        ),
-        "row",
-        scatter_dimension=0,
-        tiled=True,
-    )
-    section = act_flat
-    grad_w_out = lax.psum_scatter(
-        lax.dot_general(
-            section, grad_flat, (((0,), (0,)), ((), ())), preferred_element_type=jnp.float32
-        ),
-        "row",
-        scatter_dimension=0,
-        tiled=True,
+    partial_in = lax.dot_general(
+        normed_flat, pre_flat, (((0,), (0,)), ((), ())), preferred_element_type=jnp.float32
+    )
+    partial_out = lax.dot_general(
+        act_flat, grad_flat, (((0,), (0,)), ((), ())), preferred_element_type=jnp.float32
     )
     branch = from_tiles(branch_tiles)
     grad_norm = from_tiles(norm_tiles)
@@ -154,7 +160,14 @@
     grad_float = grad_conv.astype(jnp.float32)
     kernel_grad = kernel_terms(padded, grad_float, image_rows, image_cols)
     packed = jnp.concatenate([kernel_grad, gain_grad[None], scale_grad[None]], axis=0)
-    small_grads = lax.psum(packed, "row")
+    count = lax.axis_size("row")
+    merged = jnp.concatenate(
+        [partial_in.reshape(count, -1), partial_out.reshape(count, -1)], axis=1
+    )
+    owned, small_grads = halving_reduce(merged, packed, "row")
+    split_at = partial_in.size // count
+    grad_w_in = owned[0, :split_at].reshape(-1, hidden)
+    grad_w_out = owned[0, split_at:].reshape(-1, channels)
     grad_ext = padded_2(grad_conv, (("row", 0),), half_width)
     grad_padded = jnp.pad(grad_ext.astype(jnp.float32), ((0, 0), (half_width, half_width), (0, 0)))
     conv_back = depthwise(grad_padded, kernel[::-1, ::-1], image_rows, image_cols)

time: 193 us -> 140 us (0.73)
  blocking collectives: 62.9 us -> 0 us
  local copies, waits for them, and re-layouts: 17.9 us -> 37.9 us
  between operations: 14.9 us -> 1.51 us
  starting transfers between devices: 12.6 us -> 23 us
  waiting for transfers between devices: 24.4 us -> 16.2 us
    psum x1 -> x0, blocking collectives: 62.9 us -> none  [shards(): small_grads = lax.psum(packed, 'row')]
    reduce_scatter x2 -> x0, waiting for transfers between devices: 24.4 us -> none  [the longest x1 24.4 us: shards(): lax.psum_scatter(lax.dot_general(section, pre_flat, (((0,), (0,)), ((), (...]
    ppermute x0 -> x8, waiting for transfers between devices: none -> 16.2 us  [halving_reduce(): got, got_whole = lax.ppermute((give, whole), axis, pairs)]
    ppermute x0 -> x8, starting transfers between devices: none -> 16 us  [halving_reduce(): got, got_whole = lax.ppermute((give, whole), axis, pairs)]
    dynamic_slice x0 -> x3, local copies, waits for them, and re-layouts: none -> 8.42 us  [halving_reduce(): keep = lax.dynamic_index_in_dim(halves, bit, axis=1, keepdims=False)]
    concatenate x0 -> x3, local copies, waits for them, and re-layouts: none -> 8.25 us  [shards(): jnp.concatenate([partial_in.reshape(count, -1), partial_out.reshape(count...]
    ppermute x2, starting transfers between devices: 9.77 us -> 4.42 us  [padded_2(): lax.ppermute(lax.slice_in_dim(block, block.shape[dim] - width, None, axis...]
    while x32 -> x24, local copies, waits for them, and re-layouts: 5.38 us -> 0.05 us
  transfers between devices with their start and end apart: 6 -> 12, of which waited for: 1 -> 3; matrix products, arithmetic and copies ran while one was open for 17% -> 19% of each run, Pallas kernels for 0% -> 0%
where the time goes in v1:
time: 140 us; the launch traced here: 139 us
  other arithmetic  42.2 us (30%)
  local copies, waits for them, and re-layouts  37.9 us (27%)
  starting transfers between devices  23 us (16%)
  matrix products  18 us (13%)
  waiting for transfers between devices  16.2 us (12%)
  between operations  1.51 us (1%)
    ppermute x8, waiting for transfers between devices, halving_reduce(): got, got_whole = lax.ppermute((give, whole), axis, pairs)  16.2 us
    ppermute x8, starting transfers between devices, halving_reduce(): got, got_whole = lax.ppermute((give, whole), axis, pairs)  16 us
    reduce_sum x1, other arithmetic, shards(): centre = jnp.mean(filtered, axis=-1, keepdims=True)  10.2 us
    convert_element_type x1, other arithmetic, shards(): grad_image = (upstream + conv_back).astype(jnp.bfloat16)  9.61 us
    dynamic_slice x3, local copies, waits for them, and re-layouts, halving_reduce(): keep = lax.dynamic_index_in_dim(halves, bit, axis=1, keepdims=False)  8.42 us
    concatenate x3, local copies, waits for them, and re-layouts, shards(): jnp.concatenate([partial_in.reshape(count, -1), partial_out.reshape(count...  8.25 us
    reduce_sum x6, other arithmetic, kernel_terms(): jnp.sum(padded[row_tap:row_tap + image_rows, col_tap:col_tap + image_cols...  7.76 us
    unnamed x103, local copies, waits for them, and re-layouts  6.1 us
  transfers between devices with their start and end apart: 12, of which 3 were waited for; matrix products, arithmetic and copies ran while one was open for 19% of the time, Pallas kernels for 0%

profile of v1, /device:TPU:0, one launch (start us, length us, event | category | flops | bytes accessed | tf_op | source)
XLA Modules:
  0.0 139.0 jit_solution(11804123662673007545)
XLA Ops:
  0.7 1.2 fusion.134
  1.9 2.4 %collective-permute-start = (bf16[3,256,256]{2,1,0:T(8,128)(2,1)S(1)}, bf16[3,256,256]{2,1,0:T(8,128)(2,1)S(1)}, u32[]{:S(2)}, u32[]{:S(2)}) collective-permute-start(bf16[3,256,256]{2,1,0:T(8,128)(2,1)S(1)} %get-tuple-element.146), channel_id=1, source_target_pairs={{0,1},{1,2},{2,3},{3,4},{4,5},{5,6},{6,7},{7,8},{8,9},{9,10},{10,1... | collective-permute-start | bytes 1179656 | tf_op jit(solution)/shard_map/ppermute | solution.py:21
  4.3 1.3 collective-permute-start.1
  5.6 1.7 %fusion.136 = (f32[1,1,256]{2,1,0:T(1,128)S(1)}, f32[1,1,256]{2,1,0:T(1,128)S(1)}, f32[1,1,256]{2,1,0:T(1,128)S(1)}, f32[1,1,256]{2,1,0:T(1,128)S(1)}, f32[1,1,2...) fusion(f32[7,7,256]{2,1,0:T(8,128)} %param.12), kind=kLoop, calls=%fused_computation.251 | loop fusion | bytes 38912 | tf_op jit(solution)/shard_map/slice | solution.py:66
  8.0 1.2 fusion.18
  11.4 1.2 maximum_convert_fusion
  12.6 10.2 %fusion.132 = (f32[4,256]{1,0:T(4,128)S(1)}, f32[4,256,256]{2,1,0:T(8,128)}) fusion(f32[256]{0:T(256)} %bitcast.270, f32[256]{0:T(256)} %bitcast.272, f32[256]{0:T(256)} %bitcast.276, f32[256]{0:T(256)} %bitcast.278, f32[10,256,256]{2,1,0:T(8,128)S(1)} %maximum_convert_fusion, f32[256]{0:T(256)} %bitcast.280, f32[256]{0:T(256)} %bitcast.282, ...), kind=kLoop, calls=%fused_computation.247 | loop fusion | flops 25689088 | bytes 11064320 | tf_op jit(solution)/shard_map/reduce_sum | solution.py:107
  22.8 1.7 %multiply_reduce_fusion.2 = f32[4,256]{1,0:T(4,128)S(1)} fusion(f32[4,256,256]{2,1,0:T(8,128)} %get-tuple-element.131, f32[4,256]{1,0:T(4,128)S(1)} %broadcast_multiply_fusion.1), kind=kLoop, calls=%fused_computation.221 | loop fusion | flops 785408 | bytes 1056768 | tf_op jit(solution)/shard_map/reduce_sum | solution.py:109
  24.5 1.6 %multiply_convert_fusion.3 = bf16[4,256,256]{2,1,0:T(8,128)(2,1)S(1)} fusion(f32[4,256,256]{2,1,0:T(8,128)} %get-tuple-element.131, f32[256]{0:T(256)S(1)} %copy-done.18, f32[4,256]{1,0:T(4,128)S(1)} %add_rsqrt_fusion, f32[4,256]{1,0:T(4,128)S(1)} %broadcast_multiply_fusion.1), kind=kLoop, calls=%fused_computation.220 | loop fusion | flops 1048576 | bytes 1582080 | tf_op jit(solution)/shard_map/convert_element_type | solution.py:111
  26.9 13.1 %while.16 = (s32[]{:T(128)}, bf16[2,512,1024]{2,1,0:T(8,128)(2,1)}, f32[2,512,256]{2,1,0:T(8,128)}, bf16[2,512,1024]{2,1,0:T(8,128)(2,1)}, f32[2,512,256]{2,1,0:...) while((s32[]{:T(128)}, bf16[2,512,1024]{2,1,0:T(8,128)(2,1)}, ...), condition=%wide.region_3.4_spmd, body=%wide.region_2.3_spmd.sunk | while | flops 1093140480 | bytes 43518736 | solution.py:133
  26.9 2.9 %bitcast_dynamic-update-slice_fusion.4 = (bf16[2,512,1024]{2,1,0:T(8,128)(2,1)}, f32[512,1024]{1,0:T(8,128)S(1)}) fusion(bf16[2,512,1024]{2,1,0:T(8,128)(2,1)} %get-tuple-element.271, s32[]{:T(128)} %get-tuple-element.270, bf16[256,1024]{1,0:T(8,128)(2,1)S(1)} %get-tuple-element.286, bf16[2,512,256]{2,1,0:T(8,128)(2,1)} %get-tuple-element.285), kind=kOutput, calls=%fused_computation.15.clone.1 | convolution fusion | flops 273154048 | bytes 3933184 | tf_op jit(solution)/shard_map/while/body/eval_jaxpr/dot_general | solution.py:122
  29.8 1.4 %bitcast_dynamic-update-slice_fusion.5 = (bf16[2,512,1024]{2,1,0:T(8,128)(2,1)S(1)}, bf16[512,1024]{1,0:T(8,128)(2,1)S(1)}) fusion(bf16[2,512,1024]{2,1,0:T(8,128)(2,1)S(1)} %copy-done.9, s32[]{:T(128)} %get-tuple-element.270, f32[512,1024]{1,0:T(8,128)S(1)} %get-tuple-element.257, bf16[1024,256]{1,0:T(8,128)(2,1)S(1)} %copy-done.54, ...), kind=kOutput, calls=%fused_computation.14.clone.1 | convolution fusion | flops 278396928 | bytes 4981760 | tf_op jit(solution)/shard_map/while/body/eval_jaxpr/dot_general | solution.py:125
  31.8 1.6 %fusion.161 = f32[2,512,256]{2,1,0:T(8,128)} fusion(f32[2,512,256]{2,1,0:T(8,128)} %get-tuple-element.272, s32[]{:T(128)} %get-tuple-element.270, bf16[1024,256]{1,0:T(8,128)(2,1)S(1)} %copy-done.54, f32[512,1024]{1,0:T(8,128)S(1)} %get-tuple-element.257), kind=kOutput, calls=%fused_computation.13.clone.1 | convolution fusion | flops 273154048 | bytes 3146240 | tf_op jit(solution)/shard_map/while/body/eval_jaxpr/dot_general | solution.py:124
  33.4 3.0 %bitcast_dynamic-update-slice_fusion.4 = (bf16[2,512,1024]{2,1,0:T(8,128)(2,1)}, f32[512,1024]{1,0:T(8,128)S(1)}) fusion(bf16[2,512,1024]{2,1,0:T(8,128)(2,1)} %get-tuple-element.271, s32[]{:T(128)} %get-tuple-element.270, bf16[256,1024]{1,0:T(8,128)(2,1)S(1)} %get-tuple-element.286, bf16[2,512,256]{2,1,0:T(8,128)(2,1)} %get-tuple-element.285), kind=kOutput, calls=%fused_computation.15.clone.1 | convolution fusion | flops 273154048 | bytes 3933184 | tf_op jit(solution)/shard_map/while/body/eval_jaxpr/dot_general | solution.py:122
  36.4 1.4 %bitcast_dynamic-update-slice_fusion.5 = (bf16[2,512,1024]{2,1,0:T(8,128)(2,1)S(1)}, bf16[512,1024]{1,0:T(8,128)(2,1)S(1)}) fusion(bf16[2,512,1024]{2,1,0:T(8,128)(2,1)S(1)} %copy-done.9, s32[]{:T(128)} %get-tuple-element.270, f32[512,1024]{1,0:T(8,128)S(1)} %get-tuple-element.257, bf16[1024,256]{1,0:T(8,128)(2,1)S(1)} %copy-done.54, ...), kind=kOutput, calls=%fused_computation.14.clone.1 | convolution fusion | flops 278396928 | bytes 4981760 | tf_op jit(solution)/shard_map/while/body/eval_jaxpr/dot_general | solution.py:125
  38.4 1.6 %fusion.161 = f32[2,512,256]{2,1,0:T(8,128)} fusion(f32[2,512,256]{2,1,0:T(8,128)} %get-tuple-element.272, s32[]{:T(128)} %get-tuple-element.270, bf16[1024,256]{1,0:T(8,128)(2,1)S(1)} %copy-done.54, f32[512,1024]{1,0:T(8,128)S(1)} %get-tuple-element.257), kind=kOutput, calls=%fused_computation.13.clone.1 | convolution fusion | flops 273154048 | bytes 3146240 | tf_op jit(solution)/shard_map/while/body/eval_jaxpr/dot_general | solution.py:124
  40.0 1.4 %copy.26 = f32[1,2,4,128,256]{4,3,1,2,0:T(8,128)S(1)} copy(f32[1,2,4,128,256]{4,3,2,1,0:T(8,128)} %bitcast.202) | data formatting | bytes 2097152 | tf_op jit(solution)/shard_map/reshape | solution.py:99
  42.4 1.7 %fusion.65 = (f32[256]{0:T(256)S(1)}, f32[256]{0:T(256)S(1)}, f32[256]{0:T(256)S(1)}, f32[256]{0:T(256)S(1)}, f32[256]{0:T(256)S(1)}, /*index=5*/f32[256]{0:T(25...) fusion(f32[10,256,256]{2,1,0:T(8,128)S(1)} %maximum_convert_fusion, ...), kind=kLoop, calls=%fused_computation.127 | loop fusion | flops 7075584 | bytes 6318080 | tf_op jit(solution)/shard_map/reduce_sum | solution.py:76
  44.1 1.6 %fusion.66 = (f32[256]{0:T(256)S(1)}, f32[256]{0:T(256)S(1)}, f32[256]{0:T(256)S(1)}, f32[256]{0:T(256)S(1)}, f32[256]{0:T(256)S(1)}, /*index=5*/f32[256]{0:T(25...) fusion(bf16[4,256,256]{2,1,0:T(8,128)(2,1)S(1)} %get-tuple-element.129, ...), kind=kLoop, calls=%fused_computation.128 | loop fusion | flops 5502464 | bytes 5253120 | tf_op jit(solution)/shard_map/reduce_sum | solution.py:76
  45.8 2.5 %copy.25 = f32[1,2,4,128,256]{4,3,1,2,0:T(8,128)} copy(f32[1,2,4,128,256]{4,3,2,1,0:T(8,128)} %bitcast.63) | data formatting | bytes 2097152 | tf_op jit(solution)/shard_map/reshape | solution.py:99
  48.2 1.7 %fusion.138 = f32[256,1024]{1,0:T(8,128)} fusion(bf16[1024,256]{1,0:T(8,128)(2,1)S(1)} %bitcast.207, bf16[1024,1024]{1,0:T(8,128)(2,1)S(1)} %bitcast.205), kind=kOutput, calls=%fused_computation.253 | convolution fusion | flops 536870912 | bytes 3670016 | tf_op jit(solution)/shard_map/dot_general | solution.py:140
  50.0 3.1 %concatenate.19 = f32[8,2,16384]{2,1,0:T(2,128)} reshape(f32[256,1024]{1,0:T(8,128)} %fusion.138) | data formatting | bytes 2097152 | tf_op jit(solution)/shard_map/concatenate | solution.py:164
  53.0 2.3 %constant_dynamic-update-slice_fusion.1 = f32[8,2,32768]{2,1,0:T(2,128)} fusion(f32[8,2,16384]{2,1,0:T(2,128)} %concatenate.19), kind=kLoop, calls=%fused_computation.232 | loop fusion | bytes 2097152
  55.4 3.3 %fusion.139 = f32[1024,256]{1,0:T(8,128)} fusion(bf16[1024,1024]{1,0:T(8,128)(2,1)} %bitcast.363, bf16[1024,256]{1,0:T(8,128)(2,1)S(1)} %bitcast.212), kind=kOutput, calls=%fused_computation.254 | convolution fusion | flops 536870912 | bytes 3670016 | tf_op jit(solution)/shard_map/dot_general | solution.py:143
  58.7 2.9 %concatenate.20 = f32[8,2,16384]{2,1,0:T(2,128)} reshape(f32[1024,256]{1,0:T(8,128)} %fusion.139) | data formatting | bytes 2097152 | tf_op jit(solution)/shard_map/concatenate | solution.py:164
  61.6 2.3 %constant_dynamic-update-slice_fusion = f32[8,2,32768]{2,1,0:T(2,128)} fusion(f32[8,2,32768]{2,1,0:T(2,128)} %constant_dynamic-update-slice_fusion.1, f32[8,2,16384]{2,1,0:T(2,128)} %concatenate.20), kind=kLoop, calls=%fused_computation.231 | loop fusion | bytes 2097152 | tf_op jit(solution)/shard_map/concatenate | solution.py:164
  63.9 4.4 %constant_dynamic-slice_fusion.6 = (f32[8,1,32768]{2,1,0:T(1,128)S(1)}, f32[8,1,32768]{2,1,0:T(1,128)S(1)}) fusion(f32[8,2,32768]{2,1,0:T(2,128)} %constant_dynamic-update-slice_fusion, s32[]{:T(128)S(6)} %select_n.28, s32[]{:T(128)S(6)} %select_n.29), kind=kLoop, calls=%fused_computation.244 | loop fusion | bytes 4194312 | tf_op jit(solution)/shard_map/jit(dynamic_index_in_dim)/dynamic_slice | solution.py:39
  68.9 4.7 %collective-permute-start.4 = (f32[8,32768]{1,0:T(8,128)S(1)}, f32[8,32768]{1,0:T(8,128)S(1)}, u32[]{:S(2)}, u32[]{:S(2)}) collective-permute-start(f32[8,32768]{1,0:T(8,128)S(1)} %bitcast.210), channel_id=1, source_target_pairs={{0,1},{1,0},{2,3},{3,2},{4,5},{5,4},{6,7},{7,6},{8,9},{9,8},{10,11... | collective-permute-start | bytes 3145736 | tf_op jit(solution)/shard_map/ppermute | solution.py:41
  73.6 1.3 fusion.67
  74.9 1.4 fusion.68
  76.3 1.6 %fusion.69 = (f32[256]{0:T(256)S(1)}, f32[256]{0:T(256)S(1)}, f32[256]{0:T(256)S(1)}, f32[256]{0:T(256)S(1)}, f32[256]{0:T(256)S(1)}, /*index=5*/f32[256]{0:T(25...) fusion(bf16[4,256,256]{2,1,0:T(8,128)(2,1)S(1)} %get-tuple-element.129, ...), kind=kLoop, calls=%fused_computation.131 | loop fusion | flops 5502464 | bytes 5253120 | tf_op jit(solution)/shard_map/reduce_sum | solution.py:76
  77.9 1.6 %bitcast_add_fusion = f32[8,32768]{1,0:T(8,128)} fusion(f32[8,32768]{1,0:T(8,128)S(1)} %collective-permute-done.4, f32[8,1,32768]{2,1,0:T(1,128)S(1)} %get-tuple-element.136), kind=kLoop, calls=%fused_computation.186 | loop fusion | flops 262144 | bytes 3145728 | tf_op jit(solution)/shard_map/add | solution.py:42
  79.5 2.9 %reshape.103 = f32[4,2,32768]{2,1,0:T(2,128)} reshape(f32[8,32768]{1,0:T(8,128)} %bitcast_add_fusion) | data formatting | bytes 2097152 | tf_op jit(solution)/shard_map/reshape | solution.py:38
  82.4 3.6 %constant_dynamic-slice_fusion.4 = (f32[4,1,32768]{2,1,0:T(1,128)}, f32[4,1,32768]{2,1,0:T(1,128)S(1)}) fusion(f32[4,2,32768]{2,1,0:T(2,128)} %reshape.103, s32[]{:T(128)S(6)} %select_n.30, s32[]{:T(128)S(6)} %select_n.31), kind=kLoop, calls=%fused_computation.242 | loop fusion | bytes 2097160 | tf_op jit(solution)/shard_map/jit(dynamic_index_in_dim)/dynamic_slice | solution.py:39
  87.1 2.4 %collective-permute-start.5 = (f32[4,32768]{1,0:T(4,128)}, f32[4,32768]{1,0:T(4,128)}, u32[]{:S(2)}, u32[]{:S(2)}) collective-permute-start(f32[4,32768]{1,0:T(4,128)} %bitcast.175), channel_id=1, source_target_pairs={{0,2},{1,3},{2,0},{3,1},{4,6},{5,7},{6,4},{7,5},{8,10},{9,11},{10,... | collective-permute-start | bytes 1572872 | tf_op jit(solution)/shard_map/ppermute | solution.py:41
  89.6 1.1 fusion.20
  91.2 1.2 collective-permute-done.8
  92.6 2.0 %collective-permute-start.2 = (bf16[3,256,256]{2,1,0:T(8,128)(2,1)S(1)}, bf16[3,256,256]{2,1,0:T(8,128)(2,1)S(1)}, u32[]{:S(2)}, u32[]{:S(2)}) collective-permute-start(bf16[3,256,256]{2,1,0:T(8,128)(2,1)S(1)} %get-tuple-element.144), channel_id=1, source_target_pairs={{0,1},{1,2},{2,3},{3,4},{4,5},{5,6},{6,7},{7,8},{8,9},{9,10},{10,1... | collective-permute-start | bytes 1179656 | tf_op jit(solution)/shard_map/ppermute | solution.py:21
  94.6 1.3 collective-permute-start.3
  95.9 11.6 %collective-permute-done.9 = f32[51,256]{1,0:T(8,128)S(1)} collective-permute-done((f32[51,256]{1,0:T(8,128)S(1)}, f32[51,256]{1,0:T(8,128)S(1)}, u32[]{:S(2)}, u32[]{:S(2)}) %collective-permute-start.9) | collective-permute-done | bytes 52256 | tf_op jit(solution)/shard_map/ppermute | solution.py:41
  107.5 2.2 %collective-permute-start.10 = (f32[51,256]{1,0:T(8,128)S(1)}, f32[51,256]{1,0:T(8,128)S(1)}, u32[]{:S(2)}, u32[]{:S(2)}) collective-permute-start(f32[51,256]{1,0:T(8,128)S(1)} %add.495), channel_id=1, source_target_pairs={{0,4},{1,5},{2,6},{3,7},{4,0},{5,1},{6,2},{7,3},{8,12},{9,13},{10,... | collective-permute-start | bytes 156680 | tf_op jit(solution)/shard_map/ppermute | solution.py:41
  109.7 1.4 %bitcast_add_fusion.1 = f32[4,32768]{1,0:T(4,128)S(1)} fusion(f32[4,32768]{1,0:T(4,128)} %collective-permute-done.5, f32[4,1,32768]{2,1,0:T(1,128)S(1)} %copy-done.13), kind=kLoop, calls=%fused_computation.225 | loop fusion | flops 131072 | bytes 1572864 | tf_op jit(solution)/shard_map/add | solution.py:42
  113.0 3.1 %collective-permute-start.11 = (f32[51,256]{1,0:T(8,128)S(1)}, f32[51,256]{1,0:T(8,128)S(1)}, u32[]{:S(2)}, u32[]{:S(2)}) collective-permute-start(f32[51,256]{1,0:T(8,128)S(1)} %add.496), channel_id=1, source_target_pairs={{0,8},{1,9},{2,10},{3,11},{4,12},{5,13},{6,14},{7,15},{8,0},{9,1},... | collective-permute-start | bytes 156680 | tf_op jit(solution)/shard_map/ppermute | solution.py:41
  116.0 3.4 %collective-permute-done.11 = f32[51,256]{1,0:T(8,128)S(1)} collective-permute-done((f32[51,256]{1,0:T(8,128)S(1)}, f32[51,256]{1,0:T(8,128)S(1)}, u32[]{:S(2)}, u32[]{:S(2)}) %collective-permute-start.11) | collective-permute-done | bytes 52256 | tf_op jit(solution)/shard_map/ppermute | solution.py:41
  121.1 1.3 maximum_convert_fusion.1
  122.4 1.2 bitcast_add_fusion.2
  123.8 3.4 %collective-permute-start.7 = (f32[1,32768]{1,0:T(1,128)S(1)}, f32[1,32768]{1,0:T(1,128)S(1)}, u32[]{:S(2)}, u32[]{:S(2)}) collective-permute-start(f32[1,32768]{1,0:T(1,128)S(1)} %constant_dynamic-slice_fusion), channel_id=1, source_target_pairs={{0,8},{1,9},{2,10},{3,11},{4,12},{5,13},{6,14},{7,15},{8,0},{9,1},... | collective-permute-start | bytes 393224 | tf_op jit(solution)/shard_map/ppermute | solution.py:41
  127.5 9.6 %fusion.19 = bf16[4,256,256]{2,1,0:T(8,128)(2,1)} fusion(bf16[4,256,256]{2,1,0:T(8,128)(2,1)} %param.17, f32[10,256,256]{2,1,0:T(8,128)S(1)} %maximum_convert_fusion.1, f32[256]{0:T(256)S(1)} %bitcast.271, f32[256]{0:T(256)S(1)} %bitcast.273, f32[256]{0:T(256)S(1)} %bitcast.277, f32[256]{0:T(256)S(1)} %bitcast.279, f32[256]{0:T(256)S(1)} %bitcast.281, ...), kind=kLoop, calls=%fused_computation.81 | loop fusion | flops 26214400 | bytes 11060224 | tf_op jit(solution)/shard_map/convert_element_type | solution.py:174
  (170 shorter events, 13.3 us)
Async XLA Ops:
  0.6 10.8 %copy-start.2 = (bf16[4,256,256]{2,1,0:T(8,128)(2,1)S(1)}, bf16[4,256,256]{2,1,0:T(8,128)(2,1)}, u32[]{:S(2)}) copy-start(bf16[4,256,256]{2,1,0:T(8,128)(2,1)} %param.10) | copy-start | bytes 1572868
  0.6 9.4 %copy-start.17 = (f32[7,7,256]{2,1,0:T(8,128)S(1)}, f32[7,7,256]{2,1,0:T(8,128)}, u32[]{:S(2)}) copy-start(f32[7,7,256]{2,1,0:T(8,128)} %param.12) | copy-start | bytes 150532
  1.9 9.5 %collective-permute-start = (bf16[3,256,256]{2,1,0:T(8,128)(2,1)S(1)}, bf16[3,256,256]{2,1,0:T(8,128)(2,1)S(1)}, u32[]{:S(2)}, u32[]{:S(2)}) collective-permute-start(bf16[3,256,256]{2,1,0:T(8,128)(2,1)S(1)} %get-tuple-element.146), channel_id=1, source_target_pairs={{0,1},{1,2},{2,3},{3,4},{4,5},{5,6},{6,7},{7,8},{8,9},{9,10},{10,1... | collective-permute-start | bytes 1179656 | tf_op jit(solution)/shard_map/ppermute | solution.py:21
  4.3 7.1 %collective-permute-start.1 = (bf16[3,256,256]{2,1,0:T(8,128)(2,1)S(1)}, bf16[3,256,256]{2,1,0:T(8,128)(2,1)}, u32[]{:S(2)}, u32[]{:S(2)}) collective-permute-start(bf16[3,256,256]{2,1,0:T(8,128)(2,1)S(1)} %get-tuple-element.147), channel_id=1, source_target_pairs={{1,0},{2,1},{3,2},{4,3},{5,4},{6,5},{7,6},{8,7},{9,8},{10,9},{11,1... | collective-permute-start | bytes 1179656 | tf_op jit(solution)/shard_map/ppermute | solution.py:24
  12.6 11.9 %copy-start.18 = (f32[256]{0:T(256)S(1)}, f32[256]{0:T(256)}, u32[]{:S(2)}) copy-start(f32[256]{0:T(256)} %param.13) | copy-start | bytes 3076
  68.9 9.0 %collective-permute-start.4 = (f32[8,32768]{1,0:T(8,128)S(1)}, f32[8,32768]{1,0:T(8,128)S(1)}, u32[]{:S(2)}, u32[]{:S(2)}) collective-permute-start(f32[8,32768]{1,0:T(8,128)S(1)} %bitcast.210), channel_id=1, source_target_pairs={{0,1},{1,0},{2,3},{3,2},{4,5},{5,4},{6,7},{7,6},{8,9},{9,8},{10,11... | collective-permute-start | bytes 3145736 | tf_op jit(solution)/shard_map/ppermute | solution.py:41
  87.1 22.6 %collective-permute-start.5 = (f32[4,32768]{1,0:T(4,128)}, f32[4,32768]{1,0:T(4,128)}, u32[]{:S(2)}, u32[]{:S(2)}) collective-permute-start(f32[4,32768]{1,0:T(4,128)} %bitcast.175), channel_id=1, source_target_pairs={{0,2},{1,3},{2,0},{3,1},{4,6},{5,7},{6,4},{7,5},{8,10},{9,11},{10,... | collective-permute-start | bytes 1572872 | tf_op jit(solution)/shard_map/ppermute | solution.py:41
  91.0 18.8 %copy-start.13 = (f32[4,1,32768]{2,1,0:T(1,128)S(1)}, f32[4,1,32768]{2,1,0:T(1,128)}, u32[]{:S(2)}) copy-start(f32[4,1,32768]{2,1,0:T(1,128)} %get-tuple-element.140) | copy-start | bytes 1572868
  91.1 1.3 collective-permute-start.8
  92.4 15.1 %collective-permute-start.9 = (f32[51,256]{1,0:T(8,128)S(1)}, f32[51,256]{1,0:T(8,128)S(1)}, u32[]{:S(2)}, u32[]{:S(2)}) collective-permute-start(f32[51,256]{1,0:T(8,128)S(1)} %add.494), channel_id=1, source_target_pairs={{0,2},{1,3},{2,0},{3,1},{4,6},{5,7},{6,4},{7,5},{8,10},{9,11},{10,... | collective-permute-start | bytes 156680 | tf_op jit(solution)/shard_map/ppermute | solution.py:41
  92.6 27.8 %collective-permute-start.2 = (bf16[3,256,256]{2,1,0:T(8,128)(2,1)S(1)}, bf16[3,256,256]{2,1,0:T(8,128)(2,1)S(1)}, u32[]{:S(2)}, u32[]{:S(2)}) collective-permute-start(bf16[3,256,256]{2,1,0:T(8,128)(2,1)S(1)} %get-tuple-element.144), channel_id=1, source_target_pairs={{0,1},{1,2},{2,3},{3,4},{4,5},{5,6},{6,7},{7,8},{8,9},{9,10},{10,1... | collective-permute-start | bytes 1179656 | tf_op jit(solution)/shard_map/ppermute | solution.py:21
  94.6 26.5 %collective-permute-start.3 = (bf16[3,256,256]{2,1,0:T(8,128)(2,1)S(1)}, bf16[3,256,256]{2,1,0:T(8,128)(2,1)}, u32[]{:S(2)}, u32[]{:S(2)}) collective-permute-start(bf16[3,256,256]{2,1,0:T(8,128)(2,1)S(1)} %get-tuple-element.145), channel_id=1, source_target_pairs={{1,0},{2,1},{3,2},{4,3},{5,4},{6,5},{7,6},{8,7},{9,8},{10,9},{11,1... | collective-permute-start | bytes 1179656 | tf_op jit(solution)/shard_map/ppermute | solution.py:24
  107.5 5.4 %collective-permute-start.10 = (f32[51,256]{1,0:T(8,128)S(1)}, f32[51,256]{1,0:T(8,128)S(1)}, u32[]{:S(2)}, u32[]{:S(2)}) collective-permute-start(f32[51,256]{1,0:T(8,128)S(1)} %add.495), channel_id=1, source_target_pairs={{0,4},{1,5},{2,6},{3,7},{4,0},{5,1},{6,2},{7,3},{8,12},{9,13},{10,... | collective-permute-start | bytes 156680 | tf_op jit(solution)/shard_map/ppermute | solution.py:41
  112.9 9.5 %collective-permute-start.6 = (f32[2,32768]{1,0:T(2,128)}, f32[2,32768]{1,0:T(2,128)}, u32[]{:S(2)}, u32[]{:S(2)}) collective-permute-start(f32[2,32768]{1,0:T(2,128)} %bitcast.176), channel_id=1, source_target_pairs={{0,4},{1,5},{2,6},{3,7},{4,0},{5,1},{6,2},{7,3},{8,12},{9,13},{10,... | collective-permute-start | bytes 786440 | tf_op jit(solution)/shard_map/ppermute | solution.py:41
  113.0 6.4 %collective-permute-start.11 = (f32[51,256]{1,0:T(8,128)S(1)}, f32[51,256]{1,0:T(8,128)S(1)}, u32[]{:S(2)}, u32[]{:S(2)}) collective-permute-start(f32[51,256]{1,0:T(8,128)S(1)} %add.496), channel_id=1, source_target_pairs={{0,8},{1,9},{2,10},{3,11},{4,12},{5,13},{6,14},{7,15},{8,0},{9,1},... | collective-permute-start | bytes 156680 | tf_op jit(solution)/shard_map/ppermute | solution.py:41
  120.1 7.2 %copy-start.19 = (f32[1,1,256]{2,1,0:T(1,128)S(1)}, f32[1,1,256]{2,1,0:T(1,128)}, u32[]{:S(2)}) copy-start(f32[1,1,256]{2,1,0:T(1,128)} %get-tuple-element.171) | copy-start | bytes 3076
  120.1 7.2 %copy-start.20 = (f32[1,1,256]{2,1,0:T(1,128)S(1)}, f32[1,1,256]{2,1,0:T(1,128)}, u32[]{:S(2)}) copy-start(f32[1,1,256]{2,1,0:T(1,128)} %get-tuple-element.172) | copy-start | bytes 3076
  120.1 7.2 %copy-start.21 = (f32[1,1,256]{2,1,0:T(1,128)S(1)}, f32[1,1,256]{2,1,0:T(1,128)}, u32[]{:S(2)}) copy-start(f32[1,1,256]{2,1,0:T(1,128)} %get-tuple-element.173) | copy-start | bytes 3076
  120.1 7.2 %copy-start.22 = (f32[1,1,256]{2,1,0:T(1,128)S(1)}, f32[1,1,256]{2,1,0:T(1,128)}, u32[]{:S(2)}) copy-start(f32[1,1,256]{2,1,0:T(1,128)} %get-tuple-element.174) | copy-start | bytes 3076
  120.1 7.2 %copy-start.23 = (f32[1,1,256]{2,1,0:T(1,128)S(1)}, f32[1,1,256]{2,1,0:T(1,128)}, u32[]{:S(2)}) copy-start(f32[1,1,256]{2,1,0:T(1,128)} %get-tuple-element.175) | copy-start | bytes 3076
  120.1 7.2 %copy-start.24 = (f32[1,1,256]{2,1,0:T(1,128)S(1)}, f32[1,1,256]{2,1,0:T(1,128)}, u32[]{:S(2)}) copy-start(f32[1,1,256]{2,1,0:T(1,128)} %get-tuple-element.176) | copy-start | bytes 3076
  120.1 7.2 %copy-start.25 = (f32[1,1,256]{2,1,0:T(1,128)S(1)}, f32[1,1,256]{2,1,0:T(1,128)}, u32[]{:S(2)}) copy-start(f32[1,1,256]{2,1,0:T(1,128)} %get-tuple-element.177) | copy-start | bytes 3076
  120.1 7.2 %copy-start.26 = (f32[1,1,256]{2,1,0:T(1,128)S(1)}, f32[1,1,256]{2,1,0:T(1,128)}, u32[]{:S(2)}) copy-start(f32[1,1,256]{2,1,0:T(1,128)} %get-tuple-element.178) | copy-start | bytes 3076
  120.1 7.2 %copy-start.27 = (f32[1,1,256]{2,1,0:T(1,128)S(1)}, f32[1,1,256]{2,1,0:T(1,128)}, u32[]{:S(2)}) copy-start(f32[1,1,256]{2,1,0:T(1,128)} %get-tuple-element.179) | copy-start | bytes 3076
  120.1 7.2 %copy-start.28 = (f32[1,1,256]{2,1,0:T(1,128)S(1)}, f32[1,1,256]{2,1,0:T(1,128)}, u32[]{:S(2)}) copy-start(f32[1,1,256]{2,1,0:T(1,128)} %get-tuple-element.180) | copy-start | bytes 3076
  120.1 7.2 %copy-start.29 = (f32[1,1,256]{2,1,0:T(1,128)S(1)}, f32[1,1,256]{2,1,0:T(1,128)}, u32[]{:S(2)}) copy-start(f32[1,1,256]{2,1,0:T(1,128)} %get-tuple-element.181) | copy-start | bytes 3076
  120.1 7.2 %copy-start.30 = (f32[1,1,256]{2,1,0:T(1,128)S(1)}, f32[1,1,256]{2,1,0:T(1,128)}, u32[]{:S(2)}) copy-start(f32[1,1,256]{2,1,0:T(1,128)} %get-tuple-element.182) | copy-start | bytes 3076
  120.1 7.2 %copy-start.31 = (f32[1,1,256]{2,1,0:T(1,128)S(1)}, f32[1,1,256]{2,1,0:T(1,128)}, u32[]{:S(2)}) copy-start(f32[1,1,256]{2,1,0:T(1,128)} %get-tuple-element.183) | copy-start | bytes 3076
  120.2 7.2 %copy-start.32 = (f32[1,1,256]{2,1,0:T(1,128)S(1)}, f32[1,1,256]{2,1,0:T(1,128)}, u32[]{:S(2)}) copy-start(f32[1,1,256]{2,1,0:T(1,128)} %get-tuple-element.184) | copy-start | bytes 3076
  120.2 7.2 %copy-start.33 = (f32[1,1,256]{2,1,0:T(1,128)S(1)}, f32[1,1,256]{2,1,0:T(1,128)}, u32[]{:S(2)}) copy-start(f32[1,1,256]{2,1,0:T(1,128)} %get-tuple-element.185) | copy-start | bytes 3076
  120.2 7.2 %copy-start.34 = (f32[1,1,256]{2,1,0:T(1,128)S(1)}, f32[1,1,256]{2,1,0:T(1,128)}, u32[]{:S(2)}) copy-start(f32[1,1,256]{2,1,0:T(1,128)} %get-tuple-element.186) | copy-start | bytes 3076
  120.2 7.2 %copy-start.35 = (f32[1,1,256]{2,1,0:T(1,128)S(1)}, f32[1,1,256]{2,1,0:T(1,128)}, u32[]{:S(2)}) copy-start(f32[1,1,256]{2,1,0:T(1,128)} %get-tuple-element.187) | copy-start | bytes 3076
  120.2 7.2 %copy-start.36 = (f32[1,1,256]{2,1,0:T(1,128)S(1)}, f32[1,1,256]{2,1,0:T(1,128)}, u32[]{:S(2)}) copy-start(f32[1,1,256]{2,1,0:T(1,128)} %get-tuple-element.188) | copy-start | bytes 3076
  120.2 7.2 %copy-start.37 = (f32[1,1,256]{2,1,0:T(1,128)S(1)}, f32[1,1,256]{2,1,0:T(1,128)}, u32[]{:S(2)}) copy-start(f32[1,1,256]{2,1,0:T(1,128)} %get-tuple-element.189) | copy-start | bytes 3076
  120.2 7.2 %copy-start.38 = (f32[1,1,256]{2,1,0:T(1,128)S(1)}, f32[1,1,256]{2,1,0:T(1,128)}, u32[]{:S(2)}) copy-start(f32[1,1,256]{2,1,0:T(1,128)} %get-tuple-element.190) | copy-start | bytes 3076
  120.2 7.2 %copy-start.39 = (f32[1,1,256]{2,1,0:T(1,128)S(1)}, f32[1,1,256]{2,1,0:T(1,128)}, u32[]{:S(2)}) copy-start(f32[1,1,256]{2,1,0:T(1,128)} %get-tuple-element.191) | copy-start | bytes 3076
  120.2 7.2 %copy-start.40 = (f32[1,1,256]{2,1,0:T(1,128)S(1)}, f32[1,1,256]{2,1,0:T(1,128)}, u32[]{:S(2)}) copy-start(f32[1,1,256]{2,1,0:T(1,128)} %get-tuple-element.192) | copy-start | bytes 3076
  120.2 7.2 %copy-start.41 = (f32[1,1,256]{2,1,0:T(1,128)S(1)}, f32[1,1,256]{2,1,0:T(1,128)}, u32[]{:S(2)}) copy-start(f32[1,1,256]{2,1,0:T(1,128)} %get-tuple-element.193) | copy-start | bytes 3076
  120.3 7.2 %copy-start.42 = (f32[1,1,256]{2,1,0:T(1,128)S(1)}, f32[1,1,256]{2,1,0:T(1,128)}, u32[]{:S(2)}) copy-start(f32[1,1,256]{2,1,0:T(1,128)} %get-tuple-element.194) | copy-start | bytes 3076
  120.3 7.2 %copy-start.43 = (f32[1,1,256]{2,1,0:T(1,128)S(1)}, f32[1,1,256]{2,1,0:T(1,128)}, u32[]{:S(2)}) copy-start(f32[1,1,256]{2,1,0:T(1,128)} %get-tuple-element.195) | copy-start | bytes 3076
  120.3 7.2 %copy-start.44 = (f32[1,1,256]{2,1,0:T(1,128)S(1)}, f32[1,1,256]{2,1,0:T(1,128)}, u32[]{:S(2)}) copy-start(f32[1,1,256]{2,1,0:T(1,128)} %get-tuple-element.196) | copy-start | bytes 3076
  120.3 7.2 %copy-start.45 = (f32[1,1,256]{2,1,0:T(1,128)S(1)}, f32[1,1,256]{2,1,0:T(1,128)}, u32[]{:S(2)}) copy-start(f32[1,1,256]{2,1,0:T(1,128)} %get-tuple-element.148) | copy-start | bytes 3076
  120.3 7.2 %copy-start.46 = (f32[1,1,256]{2,1,0:T(1,128)S(1)}, f32[1,1,256]{2,1,0:T(1,128)}, u32[]{:S(2)}) copy-start(f32[1,1,256]{2,1,0:T(1,128)} %get-tuple-element.149) | copy-start | bytes 3076
  120.3 7.2 %copy-start.47 = (f32[1,1,256]{2,1,0:T(1,128)S(1)}, f32[1,1,256]{2,1,0:T(1,128)}, u32[]{:S(2)}) copy-start(f32[1,1,256]{2,1,0:T(1,128)} %get-tuple-element.150) | copy-start | bytes 3076
  120.3 7.2 %copy-start.48 = (f32[1,1,256]{2,1,0:T(1,128)S(1)}, f32[1,1,256]{2,1,0:T(1,128)}, u32[]{:S(2)}) copy-start(f32[1,1,256]{2,1,0:T(1,128)} %get-tuple-element.151) | copy-start | bytes 3076
  120.3 7.2 %copy-start.49 = (f32[1,1,256]{2,1,0:T(1,128)S(1)}, f32[1,1,256]{2,1,0:T(1,128)}, u32[]{:S(2)}) copy-start(f32[1,1,256]{2,1,0:T(1,128)} %get-tuple-element.152) | copy-start | bytes 3076
  120.3 7.2 %copy-start.50 = (f32[1,1,256]{2,1,0:T(1,128)S(1)}, f32[1,1,256]{2,1,0:T(1,128)}, u32[]{:S(2)}) copy-start(f32[1,1,256]{2,1,0:T(1,128)} %get-tuple-element.153) | copy-start | bytes 3076
  123.8 13.4 %collective-permute-start.7 = (f32[1,32768]{1,0:T(1,128)S(1)}, f32[1,32768]{1,0:T(1,128)S(1)}, u32[]{:S(2)}, u32[]{:S(2)}) collective-permute-start(f32[1,32768]{1,0:T(1,128)S(1)} %constant_dynamic-slice_fusion), channel_id=1, source_target_pairs={{0,8},{1,9},{2,10},{3,11},{4,12},{5,13},{6,14},{7,15},{8,0},{9,1},... | collective-permute-start | bytes 393224 | tf_op jit(solution)/shard_map/ppermute | solution.py:41
  (25 other events, 84.6 us)

commit v2 on v1

--- a/solution.py
+++ b/solution.py
@@ -26,22 +26,33 @@
     return block
 
 
-def halving_reduce(blocks, whole, axis):
+def bit_reversed(values, count, steps):
+    rest = values.shape[1:]
+    values = values.reshape((2,) * steps + (values.shape[0] // count,) + rest)
+    order = tuple(reversed(range(steps))) + tuple(range(steps, values.ndim))
+    return values.transpose(order).reshape((-1,) + rest)
+
+
+def halving_reduce(parts, whole, axis):
     count = lax.axis_size(axis)
     steps = count.bit_length() - 1
     if (1 << steps) != count:
-        return lax.psum_scatter(blocks, axis, scatter_dimension=0, tiled=True), lax.psum(whole, axis)
+        owned = [lax.psum_scatter(p, axis, scatter_dimension=0, tiled=True) for p in parts]
+        return owned, lax.psum(whole, axis)
     me = lax.axis_index(axis)
+    parts = [bit_reversed(p, count, steps) for p in parts]
     for step in range(steps):
         bit = (me >> step) & 1
         pairs = [(i, i ^ (1 << step)) for i in range(count)]
-        halves = blocks.reshape(blocks.shape[0] // 2, 2, -1)
-        keep = lax.dynamic_index_in_dim(halves, bit, axis=1, keepdims=False)
-        give = lax.dynamic_index_in_dim(halves, 1 - bit, axis=1, keepdims=False)
-        got, got_whole = lax.ppermute((give, whole), axis, pairs)
-        blocks = keep + got
+        keeps, gives = [], []
+        for p in parts:
+            half = p.shape[0] // 2
+            keeps.append(lax.dynamic_slice_in_dim(p, bit * half, half, axis=0))
+            gives.append(lax.dynamic_slice_in_dim(p, (1 - bit) * half, half, axis=0))
+        got, got_whole = lax.ppermute((gives, whole), axis, pairs)
+        parts = [k + g for k, g in zip(keeps, got)]
         whole = whole + got_whole
-    return blocks, whole
+    return parts, whole
 
 
 def gelu_value(inputs):
@@ -160,14 +171,7 @@
     grad_float = grad_conv.astype(jnp.float32)
     kernel_grad = kernel_terms(padded, grad_float, image_rows, image_cols)
     packed = jnp.concatenate([kernel_grad, gain_grad[None], scale_grad[None]], axis=0)
-    count = lax.axis_size("row")
-    merged = jnp.concatenate(
-        [partial_in.reshape(count, -1), partial_out.reshape(count, -1)], axis=1
-    )
-    owned, small_grads = halving_reduce(merged, packed, "row")
-    split_at = partial_in.size // count
-    grad_w_in = owned[0, :split_at].reshape(-1, hidden)
-    grad_w_out = owned[0, split_at:].reshape(-1, channels)
+    (grad_w_in, grad_w_out), small_grads = halving_reduce([partial_in, partial_out], packed, "row")
     grad_ext = padded_2(grad_conv, (("row", 0),), half_width)
     grad_padded = jnp.pad(grad_ext.astype(jnp.float32), ((0, 0), (half_width, half_width), (0, 0)))
     conv_back = depthwise(grad_padded, kernel[::-1, ::-1], image_rows, image_cols)

time: 140 us -> 122 us (0.87)
  local copies, waits for them, and re-layouts: 37.9 us -> 14.8 us
  waiting for transfers between devices: 16.2 us -> 23 us
  starting transfers between devices: 23 us -> 26.3 us
  other arithmetic: 42.2 us -> 39.6 us
  matrix products: 18 us -> 16 us
    concatenate x3 -> x0, local copies, waits for them, and re-layouts: 8.25 us -> none  [shards(): jnp.concatenate([partial_in.reshape(count, -1), partial_out.reshape(count...]
    ppermute x8 -> x12, waiting for transfers between devices: 16.2 us -> 23 us  [halving_reduce(): got, got_whole = lax.ppermute((gives, whole), axis, pairs)]
    dynamic_slice x3 -> x8, local copies, waits for them, and re-layouts: 8.42 us -> 1.83 us  [halving_reduce(): gives.append(lax.dynamic_slice_in_dim(p, (1 - bit) * half, half, axis=0))]
    unnamed x103 -> x115, local copies, waits for them, and re-layouts: 6.1 us -> 0.48 us
    dot_general x0 -> x2, local copies, waits for them, and re-layouts: none -> 3.3 us  [the longest x1 3.09 us: shards(): lax.dot_general(act_flat, grad_flat, (((0,), (0,)), ((), ())), preferred_...]
    reshape x2 -> x0, local copies, waits for them, and re-layouts: 3.28 us -> none  [halving_reduce(): halves = blocks.reshape(blocks.shape[0] // 2, 2, -1)]
    ppermute x8 -> x12, starting transfers between devices: 16 us -> 18.9 us  [halving_reduce(): got, got_whole = lax.ppermute((gives, whole), axis, pairs)]
    dot_general x1, matrix products: 3.34 us -> 0.71 us  [shards(): lax.dot_general(act_flat, grad_flat, (((0,), (0,)), ((), ())), preferred_...]
  transfers between devices with their start and end apart: 12 -> 16, of which waited for: 3 -> 8; matrix products, arithmetic and copies ran while one was open for 19% -> 22% of each run, Pallas kernels for 0% -> 0%
where the time goes in v2:
time: 122 us
  other arithmetic  39.6 us (32%)
  starting transfers between devices  26.3 us (22%)
  waiting for transfers between devices  23 us (19%)
  matrix products  16 us (13%)
  local copies, waits for them, and re-layouts  14.8 us (12%)
  between operations  1.81 us (1%)
    ppermute x12, waiting for transfers between devices, halving_reduce(): got, got_whole = lax.ppermute((gives, whole), axis, pairs)  23 us
    ppermute x12, starting transfers between devices, halving_reduce(): got, got_whole = lax.ppermute((gives, whole), axis, pairs)  18.9 us
    reduce_sum x1, other arithmetic, shards(): centre = jnp.mean(filtered, axis=-1, keepdims=True)  10.2 us
    convert_element_type x1, other arithmetic, shards(): grad_image = (upstream + conv_back).astype(jnp.bfloat16)  9.53 us
    reduce_sum x6, other arithmetic, kernel_terms(): jnp.sum(padded[row_tap:row_tap + image_rows, col_tap:col_tap + image_cols...  7.39 us
    dot_general x2, matrix products, tile_work(): pre_act = jnp.dot(normed_blk, w_in, preferred_element_type=jnp.float32)  5.87 us
    ppermute x2, starting transfers between devices, padded_2(): lax.ppermute(lax.slice_in_dim(block, block.shape[dim] - width, None, axis...  4.82 us
    add x8, other arithmetic, halving_reduce(): parts = [k + g for k, g in zip(keeps, got)]  3.84 us
  transfers between devices with their start and end apart: 16, of which 8 were waited for; matrix products, arithmetic and copies ran while one was open for 22% of the time, Pallas kernels for 0%

profile of v2, /device:TPU:0, one launch (start us, length us, event | category | flops | bytes accessed | tf_op | source)
XLA Modules:
  0.0 121.6 jit_solution(3477053745123195985)
XLA Ops:
  0.7 1.2 %fusion.134 = (bf16[3,256,256]{2,1,0:T(8,128)(2,1)S(1)}, bf16[3,256,256]{2,1,0:T(8,128)(2,1)S(1)}) fusion(bf16[4,256,256]{2,1,0:T(8,128)(2,1)} %param.10), kind=kLoop, calls=%fused_computation.249 | loop fusion | bytes 1572864 | tf_op jit(solution)/shard_map/slice | solution.py:22
  1.9 2.4 %collective-permute-start = (bf16[3,256,256]{2,1,0:T(8,128)(2,1)S(1)}, bf16[3,256,256]{2,1,0:T(8,128)(2,1)S(1)}, u32[]{:S(2)}, u32[]{:S(2)}) collective-permute-start(bf16[3,256,256]{2,1,0:T(8,128)(2,1)S(1)} %get-tuple-element.138), channel_id=1, source_target_pairs={{0,1},{1,2},{2,3},{3,4},{4,5},{5,6},{6,7},{7,8},{8,9},{9,10},{10,1... | collective-permute-start | bytes 1179656 | tf_op jit(solution)/shard_map/ppermute | solution.py:21
  4.3 1.3 %collective-permute-start.1 = (bf16[3,256,256]{2,1,0:T(8,128)(2,1)S(1)}, bf16[3,256,256]{2,1,0:T(8,128)(2,1)}, u32[]{:S(2)}, u32[]{:S(2)}) collective-permute-start(bf16[3,256,256]{2,1,0:T(8,128)(2,1)S(1)} %get-tuple-element.139), channel_id=1, source_target_pairs={{1,0},{2,1},{3,2},{4,3},{5,4},{6,5},{7,6},{8,7},{9,8},{10,9},{11,1... | collective-permute-start | bytes 1179656 | tf_op jit(solution)/shard_map/ppermute | solution.py:24
  5.7 1.7 %fusion.136 = (f32[1,1,256]{2,1,0:T(1,128)S(1)}, f32[1,1,256]{2,1,0:T(1,128)S(1)}, f32[1,1,256]{2,1,0:T(1,128)S(1)}, f32[1,1,256]{2,1,0:T(1,128)S(1)}, f32[1,1,2...) fusion(f32[7,7,256]{2,1,0:T(8,128)} %param.12), kind=kLoop, calls=%fused_computation.251 | loop fusion | bytes 38912 | tf_op jit(solution)/shard_map/slice | solution.py:77
  8.1 0.8 fusion.18
  11.1 1.2 maximum_convert_fusion
  12.3 10.2 %fusion.132 = (f32[4,256]{1,0:T(4,128)S(1)}, f32[4,256,256]{2,1,0:T(8,128)}) fusion(f32[256]{0:T(256)} %bitcast.280, f32[256]{0:T(256)} %bitcast.282, f32[256]{0:T(256)} %bitcast.286, f32[256]{0:T(256)} %bitcast.288, f32[10,256,256]{2,1,0:T(8,128)S(1)} %maximum_convert_fusion, f32[256]{0:T(256)} %bitcast.290, f32[256]{0:T(256)} %bitcast.292, ...), kind=kLoop, calls=%fused_computation.247 | loop fusion | flops 25689088 | bytes 11064320 | tf_op jit(solution)/shard_map/reduce_sum | solution.py:118
  22.5 1.7 %multiply_reduce_fusion.2 = f32[4,256]{1,0:T(4,128)S(1)} fusion(f32[4,256,256]{2,1,0:T(8,128)} %get-tuple-element.129, f32[4,256]{1,0:T(4,128)S(1)} %broadcast_multiply_fusion.1), kind=kLoop, calls=%fused_computation.221 | loop fusion | flops 785408 | bytes 1056768 | tf_op jit(solution)/shard_map/reduce_sum | solution.py:120
  24.1 1.6 %multiply_convert_fusion.3 = bf16[4,256,256]{2,1,0:T(8,128)(2,1)S(1)} fusion(f32[4,256,256]{2,1,0:T(8,128)} %get-tuple-element.129, f32[256]{0:T(256)S(1)} %copy-done.16, f32[4,256]{1,0:T(4,128)S(1)} %add_rsqrt_fusion, f32[4,256]{1,0:T(4,128)S(1)} %broadcast_multiply_fusion.1), kind=kLoop, calls=%fused_computation.220 | loop fusion | flops 1048576 | bytes 1582080 | tf_op jit(solution)/shard_map/convert_element_type | solution.py:122
  26.5 13.1 %while.16 = (s32[]{:T(128)}, bf16[2,512,1024]{2,1,0:T(8,128)(2,1)}, f32[2,512,256]{2,1,0:T(8,128)}, bf16[2,512,1024]{2,1,0:T(8,128)(2,1)}, f32[2,512,256]{2,1,0:...) while((s32[]{:T(128)}, bf16[2,512,1024]{2,1,0:T(8,128)(2,1)}, ...), condition=%wide.region_3.4_spmd, body=%wide.region_2.3_spmd.sunk | while | flops 1093140480 | bytes 43518736 | solution.py:144
  26.6 2.9 %bitcast_dynamic-update-slice_fusion.4 = (bf16[2,512,1024]{2,1,0:T(8,128)(2,1)}, f32[512,1024]{1,0:T(8,128)S(1)}) fusion(bf16[2,512,1024]{2,1,0:T(8,128)(2,1)} %get-tuple-element.263, s32[]{:T(128)} %get-tuple-element.262, bf16[256,1024]{1,0:T(8,128)(2,1)S(1)} %get-tuple-element.278, bf16[2,512,256]{2,1,0:T(8,128)(2,1)} %get-tuple-element.277), kind=kOutput, calls=%fused_computation.15.clone.1 | convolution fusion | flops 273154048 | bytes 3933184 | tf_op jit(solution)/shard_map/while/body/eval_jaxpr/dot_general | solution.py:133
  29.5 1.4 %bitcast_dynamic-update-slice_fusion.5 = (bf16[2,512,1024]{2,1,0:T(8,128)(2,1)S(1)}, bf16[512,1024]{1,0:T(8,128)(2,1)S(1)}) fusion(bf16[2,512,1024]{2,1,0:T(8,128)(2,1)S(1)} %copy-done.61, s32[]{:T(128)} %get-tuple-element.262, f32[512,1024]{1,0:T(8,128)S(1)} %get-tuple-element.249, bf16[1024,256]{1,0:T(8,128)(2,1)S(1)} %copy-done.60, ...), kind=kOutput, calls=%fused_computation.14.clone.1 | convolution fusion | flops 278396928 | bytes 4981760 | tf_op jit(solution)/shard_map/while/body/eval_jaxpr/dot_general | solution.py:136
  31.5 1.6 %fusion.159 = f32[2,512,256]{2,1,0:T(8,128)} fusion(f32[2,512,256]{2,1,0:T(8,128)} %get-tuple-element.264, s32[]{:T(128)} %get-tuple-element.262, bf16[1024,256]{1,0:T(8,128)(2,1)S(1)} %copy-done.60, f32[512,1024]{1,0:T(8,128)S(1)} %get-tuple-element.249), kind=kOutput, calls=%fused_computation.13.clone.1 | convolution fusion | flops 273154048 | bytes 3146240 | tf_op jit(solution)/shard_map/while/body/eval_jaxpr/dot_general | solution.py:135
  33.1 3.0 %bitcast_dynamic-update-slice_fusion.4 = (bf16[2,512,1024]{2,1,0:T(8,128)(2,1)}, f32[512,1024]{1,0:T(8,128)S(1)}) fusion(bf16[2,512,1024]{2,1,0:T(8,128)(2,1)} %get-tuple-element.263, s32[]{:T(128)} %get-tuple-element.262, bf16[256,1024]{1,0:T(8,128)(2,1)S(1)} %get-tuple-element.278, bf16[2,512,256]{2,1,0:T(8,128)(2,1)} %get-tuple-element.277), kind=kOutput, calls=%fused_computation.15.clone.1 | convolution fusion | flops 273154048 | bytes 3933184 | tf_op jit(solution)/shard_map/while/body/eval_jaxpr/dot_general | solution.py:133
  36.1 1.4 %bitcast_dynamic-update-slice_fusion.5 = (bf16[2,512,1024]{2,1,0:T(8,128)(2,1)S(1)}, bf16[512,1024]{1,0:T(8,128)(2,1)S(1)}) fusion(bf16[2,512,1024]{2,1,0:T(8,128)(2,1)S(1)} %copy-done.61, s32[]{:T(128)} %get-tuple-element.262, f32[512,1024]{1,0:T(8,128)S(1)} %get-tuple-element.249, bf16[1024,256]{1,0:T(8,128)(2,1)S(1)} %copy-done.60, ...), kind=kOutput, calls=%fused_computation.14.clone.1 | convolution fusion | flops 278396928 | bytes 4981760 | tf_op jit(solution)/shard_map/while/body/eval_jaxpr/dot_general | solution.py:136
  38.0 1.6 %fusion.159 = f32[2,512,256]{2,1,0:T(8,128)} fusion(f32[2,512,256]{2,1,0:T(8,128)} %get-tuple-element.264, s32[]{:T(128)} %get-tuple-element.262, bf16[1024,256]{1,0:T(8,128)(2,1)S(1)} %copy-done.60, f32[512,1024]{1,0:T(8,128)S(1)} %get-tuple-element.249), kind=kOutput, calls=%fused_computation.13.clone.1 | convolution fusion | flops 273154048 | bytes 3146240 | tf_op jit(solution)/shard_map/while/body/eval_jaxpr/dot_general | solution.py:135
  39.7 1.4 %copy.39 = f32[1,2,4,128,256]{4,3,1,2,0:T(8,128)S(1)} copy(f32[1,2,4,128,256]{4,3,2,1,0:T(8,128)} %bitcast.208) | data formatting | bytes 2097152 | tf_op jit(solution)/shard_map/reshape | solution.py:110
  42.1 1.7 %fusion.65 = (f32[256]{0:T(256)S(1)}, f32[256]{0:T(256)S(1)}, f32[256]{0:T(256)S(1)}, f32[256]{0:T(256)S(1)}, f32[256]{0:T(256)S(1)}, /*index=5*/f32[256]{0:T(25...) fusion(f32[10,256,256]{2,1,0:T(8,128)S(1)} %maximum_convert_fusion, ...), kind=kLoop, calls=%fused_computation.129 | loop fusion | flops 7075584 | bytes 6318080 | tf_op jit(solution)/shard_map/reduce_sum | solution.py:87
  43.8 1.4 %fusion.68 = (f32[256]{0:T(256)S(1)}, f32[256]{0:T(256)S(1)}, f32[256]{0:T(256)S(1)}, f32[256]{0:T(256)S(1)}, f32[256]{0:T(256)S(1)}, /*index=5*/f32[256]{0:T(25...) fusion(bf16[4,256,256]{2,1,0:T(8,128)(2,1)S(1)} %get-tuple-element.127, ...), kind=kLoop, calls=%fused_computation.132 | loop fusion | flops 5502464 | bytes 5253120 | tf_op jit(solution)/shard_map/reduce_sum | solution.py:87
  45.2 1.4 %fusion.66 = (f32[256]{0:T(256)S(1)}, f32[256]{0:T(256)S(1)}, f32[256]{0:T(256)S(1)}, f32[256]{0:T(256)S(1)}, f32[256]{0:T(256)S(1)}, /*index=5*/f32[256]{0:T(25...) fusion(bf16[4,256,256]{2,1,0:T(8,128)(2,1)S(1)} %get-tuple-element.127, ...), kind=kLoop, calls=%fused_computation.130 | loop fusion | flops 5502464 | bytes 5253120 | tf_op jit(solution)/shard_map/reduce_sum | solution.py:87
  46.6 1.3 %fusion.69 = (f32[256]{0:T(256)S(1)}, f32[256]{0:T(256)S(1)}, f32[256]{0:T(256)S(1)}, f32[256]{0:T(256)S(1)}, f32[256]{0:T(256)S(1)}, /*index=5*/f32[256]{0:T(25...) fusion(bf16[4,256,256]{2,1,0:T(8,128)(2,1)S(1)} %get-tuple-element.127, ...), kind=kLoop, calls=%fused_computation.133 | loop fusion | flops 5502464 | bytes 5253120 | tf_op jit(solution)/shard_map/reduce_sum | solution.py:87
  47.9 1.3 %fusion.67 = (f32[256]{0:T(256)S(1)}, f32[256]{0:T(256)S(1)}, f32[256]{0:T(256)S(1)}, f32[256]{0:T(256)S(1)}, f32[256]{0:T(256)S(1)}, /*index=5*/f32[256]{0:T(25...) fusion(bf16[4,256,256]{2,1,0:T(8,128)(2,1)S(1)} %get-tuple-element.127, f32[10,256,256]{2,1,0:T(8,128)S(1)} %maximum_convert_fusion), kind=kLoop, calls=%fused_computation.131 | loop fusion | flops 4978432 | bytes 3154944 | tf_op jit(solution)/shard_map/reduce_sum | solution.py:87
  49.5 1.4 %copy.38 = f32[1,2,4,128,256]{4,3,1,2,0:T(8,128)S(1)} copy(f32[1,2,4,128,256]{4,3,2,1,0:T(8,128)} %bitcast.63) | data formatting | bytes 2097152 | tf_op jit(solution)/shard_map/reshape | solution.py:110
  50.9 1.1 fusion.20
  52.2 5.1 %collective-permute-start.12 = (f32[51,256]{1,0:T(8,128)S(1)}, f32[51,256]{1,0:T(8,128)S(1)}, u32[]{:S(2)}, u32[]{:S(2)}) collective-permute-start(f32[51,256]{1,0:T(8,128)S(1)} %concatenate.11), channel_id=1, source_target_pairs={{0,1},{1,0},{2,3},{3,2},{4,5},{5,4},{6,7},{7,6},{8,9},{9,8},{10,11... | collective-permute-start | bytes 156680 | tf_op jit(solution)/shard_map/ppermute | solution.py:52
  57.3 3.1 %copy.43 = bf16[1024,1024]{1,0:T(8,128)(2,1)S(1)} copy(bf16[1024,1024]{0,1:T(8,128)(2,1)} %bitcast.217) | data formatting | bytes 4194304 | tf_op jit(solution)/shard_map/dot_general | solution.py:154
  61.4 2.5 %collective-permute-start.13 = (f32[51,256]{1,0:T(8,128)S(1)}, f32[51,256]{1,0:T(8,128)S(1)}, u32[]{:S(2)}, u32[]{:S(2)}) collective-permute-start(f32[51,256]{1,0:T(8,128)S(1)} %add.534), channel_id=1, source_target_pairs={{0,2},{1,3},{2,0},{3,1},{4,6},{5,7},{6,4},{7,5},{8,10},{9,11},{10,... | collective-permute-start | bytes 156680 | tf_op jit(solution)/shard_map/ppermute | solution.py:52
  63.9 0.9 constant_dynamic-slice_fusion.3
  65.0 2.4 %collective-permute-start.2 = (bf16[3,256,256]{2,1,0:T(8,128)(2,1)S(1)}, bf16[3,256,256]{2,1,0:T(8,128)(2,1)S(1)}, u32[]{:S(2)}, u32[]{:S(2)}) collective-permute-start(bf16[3,256,256]{2,1,0:T(8,128)(2,1)S(1)} %get-tuple-element.136), channel_id=1, source_target_pairs={{0,1},{1,2},{2,3},{3,4},{4,5},{5,6},{6,7},{7,8},{8,9},{9,10},{10,1... | collective-permute-start | bytes 1179656 | tf_op jit(solution)/shard_map/ppermute | solution.py:21
  67.4 1.3 %collective-permute-start.3 = (bf16[3,256,256]{2,1,0:T(8,128)(2,1)S(1)}, bf16[3,256,256]{2,1,0:T(8,128)(2,1)S(1)}, u32[]{:S(2)}, u32[]{:S(2)}) collective-permute-start(bf16[3,256,256]{2,1,0:T(8,128)(2,1)S(1)} %get-tuple-element.137), channel_id=1, source_target_pairs={{1,0},{2,1},{3,2},{4,3},{5,4},{6,5},{7,6},{8,7},{9,8},{10,9},{11,1... | collective-permute-start | bytes 1179656 | tf_op jit(solution)/shard_map/ppermute | solution.py:24
  68.7 4.4 %collective-permute-start.14 = (f32[51,256]{1,0:T(8,128)S(1)}, f32[51,256]{1,0:T(8,128)S(1)}, u32[]{:S(2)}, u32[]{:S(2)}) collective-permute-start(f32[51,256]{1,0:T(8,128)S(1)} %add.535), channel_id=1, source_target_pairs={{0,4},{1,5},{2,6},{3,7},{4,0},{5,1},{6,2},{7,3},{8,12},{9,13},{10,... | collective-permute-start | bytes 156680 | tf_op jit(solution)/shard_map/ppermute | solution.py:52
  73.1 2.3 %convolution_bitcast_fusion.3 = f32[2,2,2,2,16,1024]{5,4,0,1,2,3:T(8,128)S(1)} fusion(bf16[2,2,2,2,16,1024]{5,4,3,2,1,0:T(8,128)(2,1)S(1)} %bitcast.222, bf16[1024,1024,1,1,1,1]{1,0,5,4,3,2:T(8,128)(2,1)} %bitcast.373), kind=kOutput, calls=%fused_computation.77 | convolution fusion | flops 536870912 | bytes 3670016 | tf_op jit(solution)/shard_map/dot_general | solution.py:151
  75.5 4.4 %collective-permute-done.14 = f32[51,256]{1,0:T(8,128)S(1)} collective-permute-done((f32[51,256]{1,0:T(8,128)S(1)}, f32[51,256]{1,0:T(8,128)S(1)}, u32[]{:S(2)}, u32[]{:S(2)}) %collective-permute-start.14) | collective-permute-done | bytes 52256 | tf_op jit(solution)/shard_map/ppermute | solution.py:52
  80.0 2.5 %collective-permute-start.15 = (f32[51,256]{1,0:T(8,128)S(1)}, f32[51,256]{1,0:T(8,128)S(1)}, u32[]{:S(2)}, u32[]{:S(2)}) collective-permute-start(f32[51,256]{1,0:T(8,128)S(1)} %add.536), channel_id=1, source_target_pairs={{0,8},{1,9},{2,10},{3,11},{4,12},{5,13},{6,14},{7,15},{8,0},{9,1},... | collective-permute-start | bytes 156680 | tf_op jit(solution)/shard_map/ppermute | solution.py:52
  82.5 0.9 constant_dynamic-slice_fusion.7
  83.8 1.3 %collective-permute-done.15 = f32[51,256]{1,0:T(8,128)S(1)} collective-permute-done((f32[51,256]{1,0:T(8,128)S(1)}, f32[51,256]{1,0:T(8,128)S(1)}, u32[]{:S(2)}, u32[]{:S(2)}) %collective-permute-start.15) | collective-permute-done | bytes 52256 | tf_op jit(solution)/shard_map/ppermute | solution.py:52
  86.4 9.5 %fusion.19 = bf16[4,256,256]{2,1,0:T(8,128)(2,1)} fusion(bf16[4,256,256]{2,1,0:T(8,128)(2,1)} %param.17, f32[10,256,256]{2,1,0:T(8,128)S(1)} %maximum_convert_fusion.1, f32[256]{0:T(256)S(1)} %bitcast.281, f32[256]{0:T(256)S(1)} %bitcast.283, f32[256]{0:T(256)S(1)} %bitcast.287, f32[256]{0:T(256)S(1)} %bitcast.289, f32[256]{0:T(256)S(1)} %bitcast.291, ...), kind=kLoop, calls=%fused_computation.83 | loop fusion | flops 26214400 | bytes 11060224 | tf_op jit(solution)/shard_map/convert_element_type | solution.py:178
  95.9 1.4 %dynamic-slice_add_fusion = f32[512,256]{1,0:T(8,128)S(1)} fusion(f32[512,256]{1,0:T(8,128)} %collective-permute-done.8, f32[1024,256]{1,0:T(8,128)} %bitcast.211, s32[]{:T(128)S(6)} %select_n.56), kind=kLoop, calls=%fused_computation.224 | loop fusion | flops 131072 | bytes 1572868 | tf_op jit(solution)/shard_map/add | solution.py:53
  97.4 1.1 dynamic-slice_add_fusion.1
  98.6 2.0 %collective-permute-start.5 = (f32[64,1024]{1,0:T(8,128)S(1)}, f32[64,1024]{1,0:T(8,128)S(1)}, u32[]{:S(2)}, u32[]{:S(2)}) collective-permute-start(f32[64,1024]{1,0:T(8,128)S(1)} %constant_dynamic-slice_fusion.6), channel_id=1, source_target_pairs={{0,2},{1,3},{2,0},{3,1},{4,6},{5,7},{6,4},{7,5},{8,10},{9,11},{10,... | collective-permute-start | bytes 786440 | tf_op jit(solution)/shard_map/ppermute | solution.py:52
  100.6 6.0 %collective-permute-done.9 = f32[256,256]{1,0:T(8,128)S(1)} collective-permute-done((f32[256,256]{1,0:T(8,128)S(1)}, f32[256,256]{1,0:T(8,128)S(1)}, u32[]{:S(2)}, u32[]{:S(2)}) %collective-permute-start.9) | collective-permute-done | bytes 262176 | tf_op jit(solution)/shard_map/ppermute | solution.py:52
  106.8 3.6 %collective-permute-done.5 = f32[64,1024]{1,0:T(8,128)S(1)} collective-permute-done((f32[64,1024]{1,0:T(8,128)S(1)}, f32[64,1024]{1,0:T(8,128)S(1)}, u32[]{:S(2)}, u32[]{:S(2)}) %collective-permute-start.5) | collective-permute-done | bytes 262176 | tf_op jit(solution)/shard_map/ppermute | solution.py:52
  110.5 1.5 %collective-permute-done.10 = f32[128,256]{1,0:T(8,128)S(1)} collective-permute-done((f32[128,256]{1,0:T(8,128)S(1)}, f32[128,256]{1,0:T(8,128)S(1)}, u32[]{:S(2)}, u32[]{:S(2)}) %collective-permute-start.10) | collective-permute-done | bytes 131104 | tf_op jit(solution)/shard_map/ppermute | solution.py:52
  112.0 1.2 collective-permute-start.11
  113.3 2.2 %collective-permute-done.6 = f32[32,1024]{1,0:T(8,128)S(1)} collective-permute-done((f32[32,1024]{1,0:T(8,128)S(1)}, f32[32,1024]{1,0:T(8,128)S(1)}, u32[]{:S(2)}, u32[]{:S(2)}) %collective-permute-start.6) | collective-permute-done | bytes 131104 | tf_op jit(solution)/shard_map/ppermute | solution.py:52
  115.5 0.8 collective-permute-start.7
  116.4 2.9 %collective-permute-done.11 = f32[64,256]{1,0:T(8,128)S(1)} collective-permute-done((f32[64,256]{1,0:T(8,128)S(1)}, f32[64,256]{1,0:T(8,128)S(1)}, u32[]{:S(2)}, u32[]{:S(2)}) %collective-permute-start.11) | collective-permute-done | bytes 65568 | tf_op jit(solution)/shard_map/ppermute | solution.py:52
  119.9 1.0 collective-permute-done.7
  (194 shorter events, 10.1 us)
Async XLA Ops:
  0.6 10.4 %copy-start.2 = (bf16[4,256,256]{2,1,0:T(8,128)(2,1)S(1)}, bf16[4,256,256]{2,1,0:T(8,128)(2,1)}, u32[]{:S(2)}) copy-start(bf16[4,256,256]{2,1,0:T(8,128)(2,1)} %param.10) | copy-start | bytes 1572868
  0.6 9.1 %copy-start.15 = (f32[7,7,256]{2,1,0:T(8,128)S(1)}, f32[7,7,256]{2,1,0:T(8,128)}, u32[]{:S(2)}) copy-start(f32[7,7,256]{2,1,0:T(8,128)} %param.12) | copy-start | bytes 150532
  0.7 7.4 %copy-start.4 = (bf16[4,256,256]{2,1,0:T(8,128)(2,1)S(1)}, bf16[4,256,256]{2,1,0:T(8,128)(2,1)}, u32[]{:S(2)}) copy-start(bf16[4,256,256]{2,1,0:T(8,128)(2,1)} %param.17) | copy-start | bytes 1572868
  1.9 9.1 %collective-permute-start = (bf16[3,256,256]{2,1,0:T(8,128)(2,1)S(1)}, bf16[3,256,256]{2,1,0:T(8,128)(2,1)S(1)}, u32[]{:S(2)}, u32[]{:S(2)}) collective-permute-start(bf16[3,256,256]{2,1,0:T(8,128)(2,1)S(1)} %get-tuple-element.138), channel_id=1, source_target_pairs={{0,1},{1,2},{2,3},{3,4},{4,5},{5,6},{6,7},{7,8},{8,9},{9,10},{10,1... | collective-permute-start | bytes 1179656 | tf_op jit(solution)/shard_map/ppermute | solution.py:21
  4.3 6.7 %collective-permute-start.1 = (bf16[3,256,256]{2,1,0:T(8,128)(2,1)S(1)}, bf16[3,256,256]{2,1,0:T(8,128)(2,1)}, u32[]{:S(2)}, u32[]{:S(2)}) collective-permute-start(bf16[3,256,256]{2,1,0:T(8,128)(2,1)S(1)} %get-tuple-element.139), channel_id=1, source_target_pairs={{1,0},{2,1},{3,2},{4,3},{5,4},{6,5},{7,6},{8,7},{9,8},{10,9},{11,1... | collective-permute-start | bytes 1179656 | tf_op jit(solution)/shard_map/ppermute | solution.py:24
  8.1 3.0 %copy-start.58 = (f32[256]{0:T(256)}, f32[256]{0:T(256)S(1)}, u32[]{:S(2)}) copy-start(f32[256]{0:T(256)S(1)} %broadcast_bitcast_fusion) | copy-start | bytes 3076
  12.3 11.9 %copy-start.16 = (f32[256]{0:T(256)S(1)}, f32[256]{0:T(256)}, u32[]{:S(2)}) copy-start(f32[256]{0:T(256)} %param.13) | copy-start | bytes 3076
  22.4 4.1 %copy-start.1 = (bf16[256,1024]{1,0:T(8,128)(2,1)S(1)}, bf16[256,1024]{1,0:T(8,128)(2,1)}, u32[]{:S(2)}) copy-start(bf16[256,1024]{1,0:T(8,128)(2,1)} %param.14) | copy-start | bytes 1572868
  26.5 2.9 %copy-start.12 = (bf16[2,512,256]{2,1,0:T(8,128)(2,1)S(1)}, bf16[2,512,256]{2,1,0:T(8,128)(2,1)}, u32[]{:S(2)}) copy-start(bf16[2,512,256]{2,1,0:T(8,128)(2,1)} %get-tuple-element.280) | copy-start | bytes 1572868 | tf_op jit(solution)/shard_map/while
  26.6 2.9 %copy-start.60 = (bf16[1024,256]{1,0:T(8,128)(2,1)S(1)}, bf16[1024,256]{1,0:T(8,128)(2,1)}, u32[]{:S(2)}) copy-start(bf16[1024,256]{1,0:T(8,128)(2,1)} %get-tuple-element.279) | copy-start | bytes 1572868 | tf_op jit(solution)/shard_map/while
  26.6 2.9 %copy-start.61 = (bf16[2,512,1024]{2,1,0:T(8,128)(2,1)S(1)}, bf16[2,512,1024]{2,1,0:T(8,128)(2,1)}, u32[]{:S(2)}) copy-start(bf16[2,512,1024]{2,1,0:T(8,128)(2,1)} %get-tuple-element.265) | copy-start | bytes 6291460 | tf_op jit(solution)/shard_map/while
  33.1 3.0 %copy-start.12 = (bf16[2,512,256]{2,1,0:T(8,128)(2,1)S(1)}, bf16[2,512,256]{2,1,0:T(8,128)(2,1)}, u32[]{:S(2)}) copy-start(bf16[2,512,256]{2,1,0:T(8,128)(2,1)} %get-tuple-element.280) | copy-start | bytes 1572868 | tf_op jit(solution)/shard_map/while
  33.1 3.0 %copy-start.60 = (bf16[1024,256]{1,0:T(8,128)(2,1)S(1)}, bf16[1024,256]{1,0:T(8,128)(2,1)}, u32[]{:S(2)}) copy-start(bf16[1024,256]{1,0:T(8,128)(2,1)} %get-tuple-element.279) | copy-start | bytes 1572868 | tf_op jit(solution)/shard_map/while
  33.1 3.0 %copy-start.61 = (bf16[2,512,1024]{2,1,0:T(8,128)(2,1)S(1)}, bf16[2,512,1024]{2,1,0:T(8,128)(2,1)}, u32[]{:S(2)}) copy-start(bf16[2,512,1024]{2,1,0:T(8,128)(2,1)} %get-tuple-element.265) | copy-start | bytes 6291460 | tf_op jit(solution)/shard_map/while
  52.2 9.1 %collective-permute-start.12 = (f32[51,256]{1,0:T(8,128)S(1)}, f32[51,256]{1,0:T(8,128)S(1)}, u32[]{:S(2)}, u32[]{:S(2)}) collective-permute-start(f32[51,256]{1,0:T(8,128)S(1)} %concatenate.11), channel_id=1, source_target_pairs={{0,1},{1,0},{2,3},{3,2},{4,5},{5,4},{6,7},{7,6},{8,9},{9,8},{10,11... | collective-permute-start | bytes 156680 | tf_op jit(solution)/shard_map/ppermute | solution.py:52
  57.3 3.1 %copy-start.13 = (bf16[2,512,256]{2,1,0:T(8,128)(2,1)S(1)}, bf16[2,512,256]{2,1,0:T(8,128)(2,1)}, u32[]{:S(2)}) copy-start(bf16[2,512,256]{2,1,0:T(8,128)(2,1)} %get-tuple-element.282) | copy-start | bytes 1572868
  61.2 3.6 %copy-start.14 = (bf16[2,512,256]{2,1,0:T(8,128)(2,1)S(1)}, bf16[2,512,256]{2,1,0:T(8,128)(2,1)}, u32[]{:S(2)}) copy-start(bf16[2,512,256]{2,1,0:T(8,128)(2,1)} %get-tuple-element.283) | copy-start | bytes 1572868
  61.4 7.3 %collective-permute-start.13 = (f32[51,256]{1,0:T(8,128)S(1)}, f32[51,256]{1,0:T(8,128)S(1)}, u32[]{:S(2)}, u32[]{:S(2)}) collective-permute-start(f32[51,256]{1,0:T(8,128)S(1)} %add.534), channel_id=1, source_target_pairs={{0,2},{1,3},{2,0},{3,1},{4,6},{5,7},{6,4},{7,5},{8,10},{9,11},{10,... | collective-permute-start | bytes 156680 | tf_op jit(solution)/shard_map/ppermute | solution.py:52
  64.7 31.2 %collective-permute-start.8 = (f32[512,256]{1,0:T(8,128)}, f32[512,256]{1,0:T(8,128)}, u32[]{:S(2)}, u32[]{:S(2)}) collective-permute-start(f32[512,256]{1,0:T(8,128)} %constant_dynamic-slice_fusion.3), channel_id=1, source_target_pairs={{0,1},{1,0},{2,3},{3,2},{4,5},{5,4},{6,7},{7,6},{8,9},{9,8},{10,11... | collective-permute-start | bytes 1572872 | tf_op jit(solution)/shard_map/ppermute | solution.py:52
  65.0 20.8 %collective-permute-start.2 = (bf16[3,256,256]{2,1,0:T(8,128)(2,1)S(1)}, bf16[3,256,256]{2,1,0:T(8,128)(2,1)S(1)}, u32[]{:S(2)}, u32[]{:S(2)}) collective-permute-start(bf16[3,256,256]{2,1,0:T(8,128)(2,1)S(1)} %get-tuple-element.136), channel_id=1, source_target_pairs={{0,1},{1,2},{2,3},{3,4},{4,5},{5,6},{6,7},{7,8},{8,9},{9,10},{10,1... | collective-permute-start | bytes 1179656 | tf_op jit(solution)/shard_map/ppermute | solution.py:21
  67.4 18.4 %collective-permute-start.3 = (bf16[3,256,256]{2,1,0:T(8,128)(2,1)S(1)}, bf16[3,256,256]{2,1,0:T(8,128)(2,1)S(1)}, u32[]{:S(2)}, u32[]{:S(2)}) collective-permute-start(bf16[3,256,256]{2,1,0:T(8,128)(2,1)S(1)} %get-tuple-element.137), channel_id=1, source_target_pairs={{1,0},{2,1},{3,2},{4,3},{5,4},{6,5},{7,6},{8,7},{9,8},{10,9},{11,1... | collective-permute-start | bytes 1179656 | tf_op jit(solution)/shard_map/ppermute | solution.py:24
  68.7 11.2 %collective-permute-start.14 = (f32[51,256]{1,0:T(8,128)S(1)}, f32[51,256]{1,0:T(8,128)S(1)}, u32[]{:S(2)}, u32[]{:S(2)}) collective-permute-start(f32[51,256]{1,0:T(8,128)S(1)} %add.535), channel_id=1, source_target_pairs={{0,4},{1,5},{2,6},{3,7},{4,0},{5,1},{6,2},{7,3},{8,12},{9,13},{10,... | collective-permute-start | bytes 156680 | tf_op jit(solution)/shard_map/ppermute | solution.py:52
  75.5 10.2 %copy-start.10 = (f32[2,2,2,2,16,1024]{5,4,3,2,1,0:T(8,128)}, f32[2,2,2,2,16,1024]{5,4,3,2,1,0:T(8,128)S(1)}, u32[]{:S(2)}) copy-start(f32[2,2,2,2,16,1024]{5,4,3,2,1,0:T(8,128)S(1)} %copy.42) | copy-start | bytes 3145732
  80.0 5.1 %collective-permute-start.15 = (f32[51,256]{1,0:T(8,128)S(1)}, f32[51,256]{1,0:T(8,128)S(1)}, u32[]{:S(2)}, u32[]{:S(2)}) collective-permute-start(f32[51,256]{1,0:T(8,128)S(1)} %add.536), channel_id=1, source_target_pairs={{0,8},{1,9},{2,10},{3,11},{4,12},{5,13},{6,14},{7,15},{8,0},{9,1},... | collective-permute-start | bytes 156680 | tf_op jit(solution)/shard_map/ppermute | solution.py:52
  83.4 2.6 %copy-start.21 = (f32[1,1,256]{2,1,0:T(1,128)S(1)}, f32[1,1,256]{2,1,0:T(1,128)}, u32[]{:S(2)}) copy-start(f32[1,1,256]{2,1,0:T(1,128)} %get-tuple-element.167) | copy-start | bytes 3076
  83.4 2.6 %copy-start.22 = (f32[1,1,256]{2,1,0:T(1,128)S(1)}, f32[1,1,256]{2,1,0:T(1,128)}, u32[]{:S(2)}) copy-start(f32[1,1,256]{2,1,0:T(1,128)} %get-tuple-element.168) | copy-start | bytes 3076
  83.4 2.6 %copy-start.23 = (f32[1,1,256]{2,1,0:T(1,128)S(1)}, f32[1,1,256]{2,1,0:T(1,128)}, u32[]{:S(2)}) copy-start(f32[1,1,256]{2,1,0:T(1,128)} %get-tuple-element.169) | copy-start | bytes 3076
  83.4 2.6 %copy-start.24 = (f32[1,1,256]{2,1,0:T(1,128)S(1)}, f32[1,1,256]{2,1,0:T(1,128)}, u32[]{:S(2)}) copy-start(f32[1,1,256]{2,1,0:T(1,128)} %get-tuple-element.170) | copy-start | bytes 3076
  83.4 2.6 %copy-start.25 = (f32[1,1,256]{2,1,0:T(1,128)S(1)}, f32[1,1,256]{2,1,0:T(1,128)}, u32[]{:S(2)}) copy-start(f32[1,1,256]{2,1,0:T(1,128)} %get-tuple-element.171) | copy-start | bytes 3076
  83.4 2.6 %copy-start.26 = (f32[1,1,256]{2,1,0:T(1,128)S(1)}, f32[1,1,256]{2,1,0:T(1,128)}, u32[]{:S(2)}) copy-start(f32[1,1,256]{2,1,0:T(1,128)} %get-tuple-element.172) | copy-start | bytes 3076
  83.4 2.6 %copy-start.27 = (f32[1,1,256]{2,1,0:T(1,128)S(1)}, f32[1,1,256]{2,1,0:T(1,128)}, u32[]{:S(2)}) copy-start(f32[1,1,256]{2,1,0:T(1,128)} %get-tuple-element.173) | copy-start | bytes 3076
  83.5 2.6 %copy-start.28 = (f32[1,1,256]{2,1,0:T(1,128)S(1)}, f32[1,1,256]{2,1,0:T(1,128)}, u32[]{:S(2)}) copy-start(f32[1,1,256]{2,1,0:T(1,128)} %get-tuple-element.174) | copy-start | bytes 3076
  83.5 2.6 %copy-start.29 = (f32[1,1,256]{2,1,0:T(1,128)S(1)}, f32[1,1,256]{2,1,0:T(1,128)}, u32[]{:S(2)}) copy-start(f32[1,1,256]{2,1,0:T(1,128)} %get-tuple-element.175) | copy-start | bytes 3076
  83.5 2.6 %copy-start.30 = (f32[1,1,256]{2,1,0:T(1,128)S(1)}, f32[1,1,256]{2,1,0:T(1,128)}, u32[]{:S(2)}) copy-start(f32[1,1,256]{2,1,0:T(1,128)} %get-tuple-element.176) | copy-start | bytes 3076
  83.5 2.6 %copy-start.31 = (f32[1,1,256]{2,1,0:T(1,128)S(1)}, f32[1,1,256]{2,1,0:T(1,128)}, u32[]{:S(2)}) copy-start(f32[1,1,256]{2,1,0:T(1,128)} %get-tuple-element.177) | copy-start | bytes 3076
  83.5 2.6 %copy-start.32 = (f32[1,1,256]{2,1,0:T(1,128)S(1)}, f32[1,1,256]{2,1,0:T(1,128)}, u32[]{:S(2)}) copy-start(f32[1,1,256]{2,1,0:T(1,128)} %get-tuple-element.178) | copy-start | bytes 3076
  83.5 2.6 %copy-start.33 = (f32[1,1,256]{2,1,0:T(1,128)S(1)}, f32[1,1,256]{2,1,0:T(1,128)}, u32[]{:S(2)}) copy-start(f32[1,1,256]{2,1,0:T(1,128)} %get-tuple-element.179) | copy-start | bytes 3076
  83.5 2.6 %copy-start.34 = (f32[1,1,256]{2,1,0:T(1,128)S(1)}, f32[1,1,256]{2,1,0:T(1,128)}, u32[]{:S(2)}) copy-start(f32[1,1,256]{2,1,0:T(1,128)} %get-tuple-element.180) | copy-start | bytes 3076
  83.5 2.6 %copy-start.35 = (f32[1,1,256]{2,1,0:T(1,128)S(1)}, f32[1,1,256]{2,1,0:T(1,128)}, u32[]{:S(2)}) copy-start(f32[1,1,256]{2,1,0:T(1,128)} %get-tuple-element.181) | copy-start | bytes 3076
  83.5 2.6 %copy-start.36 = (f32[1,1,256]{2,1,0:T(1,128)S(1)}, f32[1,1,256]{2,1,0:T(1,128)}, u32[]{:S(2)}) copy-start(f32[1,1,256]{2,1,0:T(1,128)} %get-tuple-element.182) | copy-start | bytes 3076
  83.6 2.6 %copy-start.37 = (f32[1,1,256]{2,1,0:T(1,128)S(1)}, f32[1,1,256]{2,1,0:T(1,128)}, u32[]{:S(2)}) copy-start(f32[1,1,256]{2,1,0:T(1,128)} %get-tuple-element.183) | copy-start | bytes 3076
  83.8 13.6 %collective-permute-start.4 = (f32[128,1024]{1,0:T(8,128)}, f32[128,1024]{1,0:T(8,128)}, u32[]{:S(2)}, u32[]{:S(2)}) collective-permute-start(f32[128,1024]{1,0:T(8,128)} %constant_dynamic-slice_fusion.7), channel_id=1, source_target_pairs={{0,1},{1,0},{2,3},{3,2},{4,5},{5,4},{6,7},{7,6},{8,9},{9,8},{10,11... | collective-permute-start | bytes 1572872 | tf_op jit(solution)/shard_map/ppermute | solution.py:52
  97.3 9.3 %collective-permute-start.9 = (f32[256,256]{1,0:T(8,128)S(1)}, f32[256,256]{1,0:T(8,128)S(1)}, u32[]{:S(2)}, u32[]{:S(2)}) collective-permute-start(f32[256,256]{1,0:T(8,128)S(1)} %constant_dynamic-slice_fusion.2), channel_id=1, source_target_pairs={{0,2},{1,3},{2,0},{3,1},{4,6},{5,7},{6,4},{7,5},{8,10},{9,11},{10,... | collective-permute-start | bytes 786440 | tf_op jit(solution)/shard_map/ppermute | solution.py:52
  98.6 11.8 %collective-permute-start.5 = (f32[64,1024]{1,0:T(8,128)S(1)}, f32[64,1024]{1,0:T(8,128)S(1)}, u32[]{:S(2)}, u32[]{:S(2)}) collective-permute-start(f32[64,1024]{1,0:T(8,128)S(1)} %constant_dynamic-slice_fusion.6), channel_id=1, source_target_pairs={{0,2},{1,3},{2,0},{3,1},{4,6},{5,7},{6,4},{7,5},{8,10},{9,11},{10,... | collective-permute-start | bytes 786440 | tf_op jit(solution)/shard_map/ppermute | solution.py:52
  106.7 5.3 %collective-permute-start.10 = (f32[128,256]{1,0:T(8,128)S(1)}, f32[128,256]{1,0:T(8,128)S(1)}, u32[]{:S(2)}, u32[]{:S(2)}) collective-permute-start(f32[128,256]{1,0:T(8,128)S(1)} %constant_dynamic-slice_fusion.1), channel_id=1, source_target_pairs={{0,4},{1,5},{2,6},{3,7},{4,0},{5,1},{6,2},{7,3},{8,12},{9,13},{10,... | collective-permute-start | bytes 393224 | tf_op jit(solution)/shard_map/ppermute | solution.py:52
  110.5 5.0 %collective-permute-start.6 = (f32[32,1024]{1,0:T(8,128)S(1)}, f32[32,1024]{1,0:T(8,128)S(1)}, u32[]{:S(2)}, u32[]{:S(2)}) collective-permute-start(f32[32,1024]{1,0:T(8,128)S(1)} %constant_dynamic-slice_fusion.5), channel_id=1, source_target_pairs={{0,4},{1,5},{2,6},{3,7},{4,0},{5,1},{6,2},{7,3},{8,12},{9,13},{10,... | collective-permute-start | bytes 393224 | tf_op jit(solution)/shard_map/ppermute | solution.py:52
  112.0 7.2 %collective-permute-start.11 = (f32[64,256]{1,0:T(8,128)S(1)}, f32[64,256]{1,0:T(8,128)S(1)}, u32[]{:S(2)}, u32[]{:S(2)}) collective-permute-start(f32[64,256]{1,0:T(8,128)S(1)} %constant_dynamic-slice_fusion), channel_id=1, source_target_pairs={{0,8},{1,9},{2,10},{3,11},{4,12},{5,13},{6,14},{7,15},{8,0},{9,1},... | collective-permute-start | bytes 196616 | tf_op jit(solution)/shard_map/ppermute | solution.py:52
  115.5 5.4 %collective-permute-start.7 = (f32[16,1024]{1,0:T(8,128)S(1)}, f32[16,1024]{1,0:T(8,128)S(1)}, u32[]{:S(2)}, u32[]{:S(2)}) collective-permute-start(f32[16,1024]{1,0:T(8,128)S(1)} %constant_dynamic-slice_fusion.4), channel_id=1, source_target_pairs={{0,8},{1,9},{2,10},{3,11},{4,12},{5,13},{6,14},{7,15},{8,0},{9,1},... | collective-permute-start | bytes 196616 | tf_op jit(solution)/shard_map/ppermute | solution.py:52
  (37 other events, 84.8 us)

commit v3 on v2

--- a/solution.py
+++ b/solution.py
@@ -96,71 +96,44 @@
     half_width = KERNEL // 2
     image_rows, image_cols, channels = image.shape
     hidden = w_in.shape[1]
-    tile_size = TILE_ROWS * TILE_COLS
+    span = TILE_COLS + 2 * half_width
 
-    def to_tiles(values):
-        depth_last = values.shape[-1]
-        values = values.reshape(
-            image_rows // TILE_ROWS, TILE_ROWS, image_cols // TILE_COLS, TILE_COLS, depth_last
-        )
-        return values.transpose(0, 2, 1, 3, 4).reshape(-1, tile_size, depth_last)
-
-    def from_tiles(values):
-        depth_last = values.shape[-1]
-        values = values.reshape(
-            image_rows // TILE_ROWS, image_cols // TILE_COLS, TILE_ROWS, TILE_COLS, depth_last
-        )
-        return values.transpose(0, 2, 1, 3, 4).reshape(image_rows, image_cols, depth_last)
-
+    first_col = jnp.argmax(tissue.reshape(-1)).astype(jnp.int32) * TILE_COLS
     extended = padded_2(image, (("row", 0),), half_width)
-    padded = jnp.pad(extended.astype(jnp.float32), ((0, 0), (half_width, half_width), (0, 0)))
-    filtered = depthwise(padded, kernel, image_rows, image_cols)
+    padded = jnp.pad(extended, ((0, 0), (half_width, half_width), (0, 0)))
+    window = lax.dynamic_slice_in_dim(padded, first_col, span, axis=1).astype(jnp.float32)
+    filtered = depthwise(window, kernel, image_rows, TILE_COLS)
     centre = jnp.mean(filtered, axis=-1, keepdims=True)
     centered = filtered - centre
     inv_std = lax.rsqrt(jnp.mean(centered * centered, axis=-1, keepdims=True) + EPSILON)
     standard = centered * inv_std
     normed = (standard * ln_gain).astype(jnp.bfloat16)
-    tissue_at = jnp.repeat(jnp.repeat(tissue, TILE_ROWS, axis=0), TILE_COLS, axis=1).astype(
-        jnp.float32
-    )[:, :, None]
-    upstream = cotangent.astype(jnp.float32)
-    grad_out = (tissue_at * layer_scale * upstream).astype(jnp.bfloat16)
-    normed_tiles = to_tiles(normed)
-    grad_tiles = to_tiles(grad_out)
-    has_tissue = tissue.reshape(-1)
+    upstream = lax.dynamic_slice_in_dim(cotangent, first_col, TILE_COLS, axis=1).astype(jnp.float32)
+    grad_out = (1.0 * layer_scale * upstream).astype(jnp.bfloat16)
 
-    def tile_work(normed_blk, grad_blk):
-        pre_act = jnp.dot(normed_blk, w_in, preferred_element_type=jnp.float32)
-        activation = gelu_value(pre_act).astype(jnp.bfloat16)
-        branch = jnp.dot(activation, w_out, preferred_element_type=jnp.float32)
-        grad_act = jnp.dot(grad_blk, w_out.T, preferred_element_type=jnp.float32)
-        grad_pre = (grad_act * gelu_slope(pre_act)).astype(jnp.bfloat16)
-        grad_norm = jnp.dot(grad_pre, w_in.T, preferred_element_type=jnp.float32)
-        return (activation, branch, grad_pre, grad_norm)
-
-    def per_tile(record):
-        return tile_work(record[0], record[1])
-
-    act_tiles, branch_tiles, pre_tiles, norm_tiles = lax.map(
-        per_tile, (normed_tiles, grad_tiles, has_tissue)
-    )
-    normed_flat = normed_tiles.reshape(-1, channels)
-    grad_flat = grad_tiles.reshape(-1, channels)
-    act_flat = act_tiles.reshape(-1, hidden)
-    pre_flat = pre_tiles.reshape(-1, hidden)
+    normed_flat = normed.reshape(-1, channels)
+    grad_flat = grad_out.reshape(-1, channels)
+    pre_act = jnp.dot(normed_flat, w_in, preferred_element_type=jnp.float32)
+    act_flat = gelu_value(pre_act).astype(jnp.bfloat16)
+    branch = jnp.dot(act_flat, w_out, preferred_element_type=jnp.float32)
+    grad_act = jnp.dot(grad_flat, w_out.T, preferred_element_type=jnp.float32)
+    pre_flat = (grad_act * gelu_slope(pre_act)).astype(jnp.bfloat16)
+    grad_norm = jnp.dot(pre_flat, w_in.T, preferred_element_type=jnp.float32)
     partial_in = lax.dot_general(
         normed_flat, pre_flat, (((0,), (0,)), ((), ())), preferred_element_type=jnp.float32
     )
     partial_out = lax.dot_general(
         act_flat, grad_flat, (((0,), (0,)), ((), ())), preferred_element_type=jnp.float32
     )
-    branch = from_tiles(branch_tiles)
-    grad_norm = from_tiles(norm_tiles)
-    block_out = (image.astype(jnp.float32) + tissue_at * layer_scale * branch).astype(jnp.bfloat16)
-    scale_grad = jnp.sum(tissue_at * branch * upstream, axis=(0, 1))
+    branch = branch.reshape(image_rows, TILE_COLS, channels)
+    grad_norm = grad_norm.reshape(image_rows, TILE_COLS, channels)
+    image_tile = lax.dynamic_slice_in_dim(image, first_col, TILE_COLS, axis=1)
+    out_tile = (image_tile.astype(jnp.float32) + 1.0 * layer_scale * branch).astype(jnp.bfloat16)
+    block_out = lax.dynamic_update_slice_in_dim(image, out_tile, first_col, axis=1)
+    scale_grad = jnp.sum(1.0 * branch * upstream, axis=(0, 1))
     gain_grad = jnp.sum(grad_norm * standard, axis=(0, 1))
     grad_std = grad_norm * ln_gain
-    grad_conv = (
+    grad_tile = (
         inv_std
         * (
             grad_std
@@ -168,14 +141,16 @@
             - standard * jnp.mean(grad_std * standard, axis=-1, keepdims=True)
         )
     ).astype(jnp.bfloat16)
-    grad_float = grad_conv.astype(jnp.float32)
-    kernel_grad = kernel_terms(padded, grad_float, image_rows, image_cols)
+    kernel_grad = kernel_terms(window, grad_tile.astype(jnp.float32), image_rows, TILE_COLS)
     packed = jnp.concatenate([kernel_grad, gain_grad[None], scale_grad[None]], axis=0)
     (grad_w_in, grad_w_out), small_grads = halving_reduce([partial_in, partial_out], packed, "row")
+    grad_conv = lax.dynamic_update_slice_in_dim(
+        jnp.zeros_like(image), grad_tile, first_col, axis=1
+    )
     grad_ext = padded_2(grad_conv, (("row", 0),), half_width)
     grad_padded = jnp.pad(grad_ext.astype(jnp.float32), ((0, 0), (half_width, half_width), (0, 0)))
     conv_back = depthwise(grad_padded, kernel[::-1, ::-1], image_rows, image_cols)
-    grad_image = (upstream + conv_back).astype(jnp.bfloat16)
+    grad_image = (cotangent.astype(jnp.float32) + conv_back).astype(jnp.bfloat16)
     return (block_out, grad_image, grad_w_in, grad_w_out, small_grads)
 
 

time: 122 us -> 98.1 us (0.80)
  other arithmetic: 39.6 us -> 24.6 us
  matrix products: 16 us -> 6.74 us
  local copies, waits for them, and re-layouts: 14.8 us -> 7.26 us
  starting transfers between devices: 26.3 us -> 31.2 us
  waiting for transfers between devices: 23 us -> 24.7 us
  between operations: 1.81 us -> 3.28 us
    dot_general x8 -> x4, matrix products: 13 us -> 4.65 us  [the longest x1 1.81 us: shards(): pre_act = jnp.dot(normed_flat, w_in, preferred_element_type=jnp.float32)]
    reduce_sum x1, other arithmetic: 10.2 us -> 4.55 us  [shards(): centre = jnp.mean(filtered, axis=-1, keepdims=True)]
    ppermute x12, starting transfers between devices: 18.9 us -> 23.6 us  [halving_reduce(): got, got_whole = lax.ppermute((gives, whole), axis, pairs)]
    reduce_sum x6 -> x3, other arithmetic: 7.39 us -> 3.93 us  [kernel_terms(): jnp.sum(padded[row_tap:row_tap + image_rows, col_tap:col_tap + image_cols...]
    dot_general x1 -> x0, local copies, waits for them, and re-layouts: 3.09 us -> none  [shards(): lax.dot_general(act_flat, grad_flat, (((0,), (0,)), ((), ())), preferred_...]
    reshape x2 -> x0, local copies, waits for them, and re-layouts: 2.8 us -> none  [from_tiles(): values.reshape(image_rows // TILE_ROWS, image_cols // TILE_COLS, TILE_ROW...]
    slice x3, local copies, waits for them, and re-layouts: 2.95 us -> 0.62 us  [depthwise(): kernel[row_tap, col_tap]]
    convert_element_type x4 -> x2, other arithmetic: 12.2 us -> 9.9 us  [the longest x1 9.56 us: shards(): (cotangent.astype(jnp.float32) + conv_back).astype(jnp.bfloat16)]
  transfers between devices with their start and end apart: 16 -> 16, of which waited for: 8 -> 9; matrix products, arithmetic and copies ran while one was open for 22% -> 21% of each run, Pallas kernels for 0% -> 0%
where the time goes in v3:
time: 98.1 us; the launch traced here: 97.7 us
  starting transfers between devices  31.2 us (32%)
  waiting for transfers between devices  24.7 us (25%)
  other arithmetic  24.6 us (25%)
  local copies, waits for them, and re-layouts  7.26 us (7%)
  matrix products  6.74 us (7%)
  between operations  3.28 us (3%)
    ppermute x12, starting transfers between devices, halving_reduce(): got, got_whole = lax.ppermute((gives, whole), axis, pairs)  23.6 us
    ppermute x12, waiting for transfers between devices, halving_reduce(): got, got_whole = lax.ppermute((gives, whole), axis, pairs)  22.7 us
    convert_element_type x1, other arithmetic, shards(): (cotangent.astype(jnp.float32) + conv_back).astype(jnp.bfloat16)  9.56 us
    ppermute x2, starting transfers between devices, padded_2(): lax.ppermute(lax.slice_in_dim(block, block.shape[dim] - width, None, axis...  4.81 us
    reduce_sum x1, other arithmetic, shards(): centre = jnp.mean(filtered, axis=-1, keepdims=True)  4.55 us
    reduce_sum x3, other arithmetic, kernel_terms(): jnp.sum(padded[row_tap:row_tap + image_rows, col_tap:col_tap + image_cols...  3.93 us
    add x8, other arithmetic, halving_reduce(): parts = [k + g for k, g in zip(keeps, got)]  3.84 us
    ppermute x2, starting transfers between devices, padded_2(): lax.ppermute(lax.slice_in_dim(block, 0, width, axis=dim), axis, backward)  2.76 us
  transfers between devices with their start and end apart: 16, of which 9 were waited for; matrix products, arithmetic and copies ran while one was open for 21% of the time, Pallas kernels for 0%

profile of v3, /device:TPU:0, one launch (start us, length us, event | category | flops | bytes accessed | tf_op | source)
XLA Modules:
  0.0 97.7 jit_solution(8711763303527567346)
XLA Ops:
  0.7 1.1 %copy.24 = bf16[4,256,256]{2,1,0:T(8,128)(2,1)S(1)} copy(bf16[4,256,256]{2,1,0:T(8,128)(2,1)} %param.8) | data formatting | bytes 1048576
  1.8 2.4 %collective-permute-start = (bf16[3,256,256]{2,1,0:T(8,128)(2,1)S(1)}, bf16[3,256,256]{2,1,0:T(8,128)(2,1)S(1)}, u32[]{:S(2)}, u32[]{:S(2)}) collective-permute-start(bf16[3,256,256]{2,1,0:T(8,128)(2,1)S(1)} %get-tuple-element.66), channel_id=1, source_target_pairs={{0,1},{1,2},{2,3},{3,4},{4,5},{5,6},{6,7},{7,8},{8,9},{9,10},{10,1... | collective-permute-start | bytes 1179656 | tf_op jit(solution)/shard_map/ppermute | solution.py:21
  4.2 1.3 %collective-permute-start.1 = (bf16[3,256,256]{2,1,0:T(8,128)(2,1)S(1)}, bf16[3,256,256]{2,1,0:T(8,128)(2,1)S(1)}, u32[]{:S(2)}, u32[]{:S(2)}) collective-permute-start(bf16[3,256,256]{2,1,0:T(8,128)(2,1)S(1)} %get-tuple-element.65), channel_id=1, source_target_pairs={{1,0},{2,1},{3,2},{4,3},{5,4},{6,5},{7,6},{8,7},{9,8},{10,9},{11,1... | collective-permute-start | bytes 1179656 | tf_op jit(solution)/shard_map/ppermute | solution.py:24
  5.5 0.7 bitcast_reduce_fusion
  7.1 0.6 fusion.146
  7.9 2.0 %collective-permute-done.1 = bf16[3,256,256]{2,1,0:T(8,128)(2,1)S(1)} collective-permute-done((bf16[3,256,256]{2,1,0:T(8,128)(2,1)S(1)}, bf16[3,256,256]{2,1,0:T(8,128)(2,1)S(1)}, u32[]{:S(2)}, u32[]{:S(2)}) %collective-permute-start.1) | collective-permute-done | bytes 393248 | tf_op jit(solution)/shard_map/ppermute | solution.py:24
  9.9 0.3 fusion.83
  10.3 4.5 %fusion.142 = (f32[4,128]{1,0:T(4,128)S(1)}, f32[4,128,256]{2,1,0:T(8,128)S(1)}) fusion(f32[256]{0:T(256)S(1)} %bitcast.214, f32[10,134,256]{2,1,0:T(8,128)S(1)} %fusion.83, f32[256]{0:T(256)S(1)} %bitcast.216, f32[256]{0:T(256)S(1)} %bitcast.160, f32[256]{0:T(256)S(1)} %bitcast.162, f32[256]{0:T(256)S(1)} %bitcast.164, f32[256]{0:T(256)S(1)} %bitcast.166, ...), kind=kLoop, calls=%fused_computation.256 | loop fusion | flops 12844544 | bytes 26266624 | tf_op jit(solution)/shard_map/reduce_sum | solution.py:106
  15.2 0.2 multiply_reduce_fusion.3
  15.7 1.8 %fusion.11 = (bf16[1024,512]{0,1:T(8,128)(2,1)}, f32[512,1024]{1,0:T(8,128)S(1)}) fusion(bf16[512,256]{1,0:T(8,128)(2,1)S(1)} %bitcast.156, bf16[256,1024]{1,0:T(8,128)(2,1)S(1)} %copy-done), kind=kOutput, calls=%fused_computation.63 | convolution fusion | flops 273154048 | bytes 3932160 | tf_op jit(solution)/shard_map/dot_general | solution.py:116
  17.6 0.8 fusion.87
  18.4 1.4 %fusion.6 = bf16[512,1024]{1,0:T(8,128)(2,1)S(1)} fusion(f32[512,1024]{1,0:T(8,128)S(1)} %get-tuple-element.120, bf16[512,256]{1,0:T(8,128)(2,1)S(1)} %bitcast.153, bf16[1024,256]{1,0:T(8,128)(2,1)S(1)} %copy-done.9), kind=kOutput, calls=%fused_computation.58 | convolution fusion | flops 278396928 | bytes 3932160 | tf_op jit(solution)/shard_map/dot_general | solution.py:119
  19.9 0.6 multiply_reduce_fusion.2
  20.4 0.3 multiply_reduce_fusion
  20.8 2.2 %fusion.135 = (f32[256]{0:T(256)}, f32[256]{0:T(256)}, f32[256]{0:T(256)}, f32[256]{0:T(256)}, f32[256]{0:T(256)}, /*index=5*/f32[256]{0:T(256)}, f32[256]{0:T(2...) fusion(f32[10,134,256]{2,1,0:T(8,128)S(1)} %fusion.83, ...), kind=kLoop, calls=%fused_computation.218 | loop fusion | flops 5893632 | bytes 10775552 | tf_op jit(solution)/shard_map/reduce_sum | solution.py:87
  23.0 1.0 %fusion.136 = (f32[256]{0:T(256)S(1)}, f32[256]{0:T(256)S(1)}, f32[256]{0:T(256)S(1)}, f32[256]{0:T(256)S(1)}, f32[256]{0:T(256)S(1)}, /*index=5*/f32[256]{0:T(2...) fusion(bf16[4,128,256]{2,1,0:T(8,128)(2,1)S(1)} %get-tuple-elem, ...), kind=kLoop, calls=%fused_computation.219 | loop fusion | flops 4845056 | bytes 9717760 | tf_op jit(solution)/shard_map/reduce_sum | solution.py:87
  24.2 0.7 fusion.134
  25.3 6.0 %collective-permute-start.12 = (f32[51,256]{1,0:T(8,128)S(1)}, f32[51,256]{1,0:T(8,128)S(1)}, u32[]{:S(2)}, u32[]{:S(2)}) collective-permute-start(f32[51,256]{1,0:T(8,128)S(1)} %concatenate.11), channel_id=1, source_target_pairs={{0,1},{1,0},{2,3},{3,2},{4,5},{5,4},{6,7},{7,6},{8,9},{9,8},{10,11... | collective-permute-start | bytes 156680 | tf_op jit(solution)/shard_map/ppermute | solution.py:52
  31.3 1.5 %copy.17 = bf16[1024,512]{1,0:T(8,128)(2,1)S(1)} copy(bf16[1024,512]{0,1:T(8,128)(2,1)} %get-tuple-element.119) | data formatting | bytes 2097152 | tf_op jit(solution)/shard_map/convert_element_type | solution.py:117
  32.8 0.4 convolution_bitcast_fusion
  33.3 0.9 constant_dynamic-slice_fusion.2
  34.6 0.8 copy-done.2
  35.6 2.4 %collective-permute-start.2 = (bf16[3,256,256]{2,1,0:T(8,128)(2,1)S(1)}, bf16[3,256,256]{2,1,0:T(8,128)(2,1)S(1)}, u32[]{:S(2)}, u32[]{:S(2)}) collective-permute-start(bf16[3,256,256]{2,1,0:T(8,128)(2,1)S(1)} %get-tuple-element.63), channel_id=1, source_target_pairs={{0,1},{1,2},{2,3},{3,4},{4,5},{5,6},{6,7},{7,8},{8,9},{9,10},{10,1... | collective-permute-start | bytes 1179656 | tf_op jit(solution)/shard_map/ppermute | solution.py:21
  38.0 1.5 %collective-permute-start.3 = (bf16[3,256,256]{2,1,0:T(8,128)(2,1)S(1)}, bf16[3,256,256]{2,1,0:T(8,128)(2,1)S(1)}, u32[]{:S(2)}, u32[]{:S(2)}) collective-permute-start(bf16[3,256,256]{2,1,0:T(8,128)(2,1)S(1)} %get-tuple-element.64), channel_id=1, source_target_pairs={{1,0},{2,1},{3,2},{4,3},{5,4},{6,5},{7,6},{8,7},{9,8},{10,9},{11,1... | collective-permute-start | bytes 1179656 | tf_op jit(solution)/shard_map/ppermute | solution.py:24
  39.5 4.4 %collective-permute-start.13 = (f32[51,256]{1,0:T(8,128)S(1)}, f32[51,256]{1,0:T(8,128)S(1)}, u32[]{:S(2)}, u32[]{:S(2)}) collective-permute-start(f32[51,256]{1,0:T(8,128)S(1)} %add.554), channel_id=1, source_target_pairs={{0,2},{1,3},{2,0},{3,1},{4,6},{5,7},{6,4},{7,5},{8,10},{9,11},{10,... | collective-permute-start | bytes 156680 | tf_op jit(solution)/shard_map/ppermute | solution.py:52
  43.9 1.7 %convolution_bitcast_fusion.1 = f32[2,2,2,2,16,1024]{5,4,0,1,2,3:T(8,128)S(1)} fusion(bf16[2,2,2,2,16,512]{5,4,3,2,1,0:T(8,128)(2,1)S(1)} %bitcast.155, bf16[512,1024]{1,0:T(8,128)(2,1)} %copy-done.8), kind=kOutput, calls=%fused_computation.71 | convolution fusion | flops 268435456 | bytes 2359296 | tf_op jit(solution)/shard_map/dot_general | solution.py:122
  45.7 4.8 %collective-permute-done.13 = f32[51,256]{1,0:T(8,128)S(1)} collective-permute-done((f32[51,256]{1,0:T(8,128)S(1)}, f32[51,256]{1,0:T(8,128)S(1)}, u32[]{:S(2)}, u32[]{:S(2)}) %collective-permute-start.13) | collective-permute-done | bytes 52256 | tf_op jit(solution)/shard_map/ppermute | solution.py:52
  50.6 3.5 %collective-permute-start.14 = (f32[51,256]{1,0:T(8,128)S(1)}, f32[51,256]{1,0:T(8,128)S(1)}, u32[]{:S(2)}, u32[]{:S(2)}) collective-permute-start(f32[51,256]{1,0:T(8,128)S(1)} %add.555), channel_id=1, source_target_pairs={{0,4},{1,5},{2,6},{3,7},{4,0},{5,1},{6,2},{7,3},{8,12},{9,13},{10,... | collective-permute-start | bytes 156680 | tf_op jit(solution)/shard_map/ppermute | solution.py:52
  54.1 0.9 constant_dynamic-slice_fusion.6
  54.9 1.3 %collective-permute-done.14 = f32[51,256]{1,0:T(8,128)S(1)} collective-permute-done((f32[51,256]{1,0:T(8,128)S(1)}, f32[51,256]{1,0:T(8,128)S(1)}, u32[]{:S(2)}, u32[]{:S(2)}) %collective-permute-start.14) | collective-permute-done | bytes 52256 | tf_op jit(solution)/shard_map/ppermute | solution.py:52
  56.2 3.1 %collective-permute-start.15 = (f32[51,256]{1,0:T(8,128)S(1)}, f32[51,256]{1,0:T(8,128)S(1)}, u32[]{:S(2)}, u32[]{:S(2)}) collective-permute-start(f32[51,256]{1,0:T(8,128)S(1)} %add.556), channel_id=1, source_target_pairs={{0,8},{1,9},{2,10},{3,11},{4,12},{5,13},{6,14},{7,15},{8,0},{9,1},... | collective-permute-start | bytes 156680 | tf_op jit(solution)/shard_map/ppermute | solution.py:52
  59.8 1.7 %collective-permute-done.15 = f32[51,256]{1,0:T(8,128)S(1)} collective-permute-done((f32[51,256]{1,0:T(8,128)S(1)}, f32[51,256]{1,0:T(8,128)S(1)}, u32[]{:S(2)}, u32[]{:S(2)}) %collective-permute-start.15) | collective-permute-done | bytes 52256 | tf_op jit(solution)/shard_map/ppermute | solution.py:52
  61.5 0.6 add.557
  62.7 9.6 %fusion.20 = bf16[4,256,256]{2,1,0:T(8,128)(2,1)} fusion(f32[10,256,256]{2,1,0:T(8,128)S(1)} %maximum_convert_fusion, bf16[4,256,256]{2,1,0:T(8,128)(2,1)} %param.15, f32[256]{0:T(256)S(1)} %bitcast.159, f32[256]{0:T(256)S(1)} %bitcast.219, f32[256]{0:T(256)S(1)} %bitcast.197, f32[256]{0:T(256)S(1)} %bitcast.213, f32[256]{0:T(256)S(1)} %bitcast.211, ...), kind=kLoop, calls=%fused_computation.82 | loop fusion | flops 26214400 | bytes 11060224 | tf_op jit(solution)/shard_map/convert_element_type | solution.py:153
  72.3 1.4 %dynamic-slice_add_fusion = f32[512,256]{1,0:T(8,128)S(1)} fusion(f32[512,256]{1,0:T(8,128)} %collective-permute-done.8, f32[1024,256]{1,0:T(8,128)} %bitcast.148, s32[]{:T(128)S(6)} %select_n.71), kind=kLoop, calls=%fused_computation.221 | loop fusion | flops 131072 | bytes 1572868 | tf_op jit(solution)/shard_map/add | solution.py:53
  73.7 0.5 collective-permute-start.9
  74.2 1.1 %dynamic-slice_add_fusion.1 = f32[128,1024]{1,0:T(8,128)S(1)} fusion(f32[128,1024]{1,0:T(8,128)} %collective-permute-done.4, f32[256,1024]{1,0:T(8,128)S(1)} %bitcast.150, s32[]{:T(128)S(6)} %select_n.63), kind=kLoop, calls=%fused_computation.222 | loop fusion | flops 131072 | bytes 1572868 | tf_op jit(solution)/shard_map/add | solution.py:53
  75.4 1.6 %collective-permute-start.5 = (f32[64,1024]{1,0:T(8,128)S(1)}, f32[64,1024]{1,0:T(8,128)S(1)}, u32[]{:S(2)}, u32[]{:S(2)}) collective-permute-start(f32[64,1024]{1,0:T(8,128)S(1)} %constant_dynamic-slice_fusion.5), channel_id=1, source_target_pairs={{0,2},{1,3},{2,0},{3,1},{4,6},{5,7},{6,4},{7,5},{8,10},{9,11},{10,... | collective-permute-start | bytes 786440 | tf_op jit(solution)/shard_map/ppermute | solution.py:52
  77.0 6.0 %collective-permute-done.9 = f32[256,256]{1,0:T(8,128)S(1)} collective-permute-done((f32[256,256]{1,0:T(8,128)S(1)}, f32[256,256]{1,0:T(8,128)S(1)}, u32[]{:S(2)}, u32[]{:S(2)}) %collective-permute-start.9) | collective-permute-done | bytes 262176 | tf_op jit(solution)/shard_map/ppermute | solution.py:52
  83.1 0.2 collective-permute-start.10
  83.3 2.7 %collective-permute-done.5 = f32[64,1024]{1,0:T(8,128)S(1)} collective-permute-done((f32[64,1024]{1,0:T(8,128)S(1)}, f32[64,1024]{1,0:T(8,128)S(1)}, u32[]{:S(2)}, u32[]{:S(2)}) %collective-permute-start.5) | collective-permute-done | bytes 262176 | tf_op jit(solution)/shard_map/ppermute | solution.py:52
  86.1 3.6 %collective-permute-done.10 = f32[128,256]{1,0:T(8,128)S(1)} collective-permute-done((f32[128,256]{1,0:T(8,128)S(1)}, f32[128,256]{1,0:T(8,128)S(1)}, u32[]{:S(2)}, u32[]{:S(2)}) %collective-permute-start.10) | collective-permute-done | bytes 131104 | tf_op jit(solution)/shard_map/ppermute | solution.py:52
  89.8 1.4 %collective-permute-start.11 = (f32[64,256]{1,0:T(8,128)S(1)}, f32[64,256]{1,0:T(8,128)S(1)}, u32[]{:S(2)}, u32[]{:S(2)}) collective-permute-start(f32[64,256]{1,0:T(8,128)S(1)} %constant_dynamic-slice_fusion.7), channel_id=1, source_target_pairs={{0,8},{1,9},{2,10},{3,11},{4,12},{5,13},{6,14},{7,15},{8,0},{9,1},... | collective-permute-start | bytes 196616 | tf_op jit(solution)/shard_map/ppermute | solution.py:52
  91.2 2.7 %collective-permute-start.7 = (f32[16,1024]{1,0:T(8,128)S(1)}, f32[16,1024]{1,0:T(8,128)S(1)}, u32[]{:S(2)}, u32[]{:S(2)}) collective-permute-start(f32[16,1024]{1,0:T(8,128)S(1)} %constant_dynamic-slice_fusion.3), channel_id=1, source_target_pairs={{0,8},{1,9},{2,10},{3,11},{4,12},{5,13},{6,14},{7,15},{8,0},{9,1},... | collective-permute-start | bytes 196616 | tf_op jit(solution)/shard_map/ppermute | solution.py:52
  93.9 1.5 %collective-permute-done.11 = f32[64,256]{1,0:T(8,128)S(1)} collective-permute-done((f32[64,256]{1,0:T(8,128)S(1)}, f32[64,256]{1,0:T(8,128)S(1)}, u32[]{:S(2)}, u32[]{:S(2)}) %collective-permute-start.11) | collective-permute-done | bytes 65568 | tf_op jit(solution)/shard_map/ppermute | solution.py:52
  95.4 0.6 dynamic-slice_add_fusion.6
  96.0 1.1 %collective-permute-done.7 = f32[16,1024]{1,0:T(8,128)S(1)} collective-permute-done((f32[16,1024]{1,0:T(8,128)S(1)}, f32[16,1024]{1,0:T(8,128)S(1)}, u32[]{:S(2)}, u32[]{:S(2)}) %collective-permute-start.7) | collective-permute-done | bytes 65568 | tf_op jit(solution)/shard_map/ppermute | solution.py:52
  97.1 0.6 dynamic-slice_add_fusion.7
  (261 shorter events, 2.3 us)
Async XLA Ops:
  0.6 15.1 %copy-start = (bf16[256,1024]{1,0:T(8,128)(2,1)S(1)}, bf16[256,1024]{1,0:T(8,128)(2,1)}, u32[]{:S(2)}) copy-start(bf16[256,1024]{1,0:T(8,128)(2,1)} %param.12) | copy-start | bytes 1572868
  1.8 6.1 %collective-permute-start = (bf16[3,256,256]{2,1,0:T(8,128)(2,1)S(1)}, bf16[3,256,256]{2,1,0:T(8,128)(2,1)S(1)}, u32[]{:S(2)}, u32[]{:S(2)}) collective-permute-start(bf16[3,256,256]{2,1,0:T(8,128)(2,1)S(1)} %get-tuple-element.66), channel_id=1, source_target_pairs={{0,1},{1,2},{2,3},{3,4},{4,5},{5,6},{6,7},{7,8},{8,9},{9,10},{10,1... | collective-permute-start | bytes 1179656 | tf_op jit(solution)/shard_map/ppermute | solution.py:21
  4.2 5.7 %collective-permute-start.1 = (bf16[3,256,256]{2,1,0:T(8,128)(2,1)S(1)}, bf16[3,256,256]{2,1,0:T(8,128)(2,1)S(1)}, u32[]{:S(2)}, u32[]{:S(2)}) collective-permute-start(bf16[3,256,256]{2,1,0:T(8,128)(2,1)S(1)} %get-tuple-element.65), channel_id=1, source_target_pairs={{1,0},{2,1},{3,2},{4,3},{5,4},{6,5},{7,6},{8,7},{9,8},{10,9},{11,1... | collective-permute-start | bytes 1179656 | tf_op jit(solution)/shard_map/ppermute | solution.py:24
  6.9 7.9 %copy-start.11 = (f32[1,1,256]{2,1,0:T(1,128)}, f32[1,1,256]{2,1,0:T(1,128)S(1)}, u32[]{:S(2)}) copy-start(f32[1,1,256]{2,1,0:T(1,128)S(1)} %get-tuple-element.75) | copy-start | bytes 3076
  6.9 7.9 %copy-start.13 = (f32[1,1,256]{2,1,0:T(1,128)}, f32[1,1,256]{2,1,0:T(1,128)S(1)}, u32[]{:S(2)}) copy-start(f32[1,1,256]{2,1,0:T(1,128)S(1)} %get-tuple-element.76) | copy-start | bytes 3076
  6.9 7.9 %copy-start.15 = (f32[1,1,256]{2,1,0:T(1,128)}, f32[1,1,256]{2,1,0:T(1,128)S(1)}, u32[]{:S(2)}) copy-start(f32[1,1,256]{2,1,0:T(1,128)S(1)} %get-tuple-element.77) | copy-start | bytes 3076
  6.9 7.9 %copy-start.17 = (f32[1,1,256]{2,1,0:T(1,128)}, f32[1,1,256]{2,1,0:T(1,128)S(1)}, u32[]{:S(2)}) copy-start(f32[1,1,256]{2,1,0:T(1,128)S(1)} %get-tuple-element.78) | copy-start | bytes 3076
  6.9 7.9 %copy-start.19 = (f32[1,1,256]{2,1,0:T(1,128)}, f32[1,1,256]{2,1,0:T(1,128)S(1)}, u32[]{:S(2)}) copy-start(f32[1,1,256]{2,1,0:T(1,128)S(1)} %get-tuple-element.79) | copy-start | bytes 3076
  6.9 7.9 %copy-start.21 = (f32[1,1,256]{2,1,0:T(1,128)}, f32[1,1,256]{2,1,0:T(1,128)S(1)}, u32[]{:S(2)}) copy-start(f32[1,1,256]{2,1,0:T(1,128)S(1)} %get-tuple-element.80) | copy-start | bytes 3076
  7.0 7.9 %copy-start.23 = (f32[1,1,256]{2,1,0:T(1,128)}, f32[1,1,256]{2,1,0:T(1,128)S(1)}, u32[]{:S(2)}) copy-start(f32[1,1,256]{2,1,0:T(1,128)S(1)} %get-tuple-element.81) | copy-start | bytes 3076
  7.0 7.9 %copy-start.25 = (f32[1,1,256]{2,1,0:T(1,128)}, f32[1,1,256]{2,1,0:T(1,128)S(1)}, u32[]{:S(2)}) copy-start(f32[1,1,256]{2,1,0:T(1,128)S(1)} %get-tuple-element.82) | copy-start | bytes 3076
  7.0 7.9 %copy-start.27 = (f32[1,1,256]{2,1,0:T(1,128)}, f32[1,1,256]{2,1,0:T(1,128)S(1)}, u32[]{:S(2)}) copy-start(f32[1,1,256]{2,1,0:T(1,128)S(1)} %get-tuple-element.83) | copy-start | bytes 3076
  7.0 7.9 %copy-start.29 = (f32[1,1,256]{2,1,0:T(1,128)}, f32[1,1,256]{2,1,0:T(1,128)S(1)}, u32[]{:S(2)}) copy-start(f32[1,1,256]{2,1,0:T(1,128)S(1)} %get-tuple-element.84) | copy-start | bytes 3076
  7.0 7.9 %copy-start.31 = (f32[1,1,256]{2,1,0:T(1,128)}, f32[1,1,256]{2,1,0:T(1,128)S(1)}, u32[]{:S(2)}) copy-start(f32[1,1,256]{2,1,0:T(1,128)S(1)} %get-tuple-element.85) | copy-start | bytes 3076
  7.0 7.9 %copy-start.33 = (f32[1,1,256]{2,1,0:T(1,128)}, f32[1,1,256]{2,1,0:T(1,128)S(1)}, u32[]{:S(2)}) copy-start(f32[1,1,256]{2,1,0:T(1,128)S(1)} %get-tuple-element.105) | copy-start | bytes 3076
  7.0 7.9 %copy-start.35 = (f32[1,1,256]{2,1,0:T(1,128)}, f32[1,1,256]{2,1,0:T(1,128)S(1)}, u32[]{:S(2)}) copy-start(f32[1,1,256]{2,1,0:T(1,128)S(1)} %get-tuple-element.106) | copy-start | bytes 3076
  7.1 7.9 %copy-start.37 = (f32[1,1,256]{2,1,0:T(1,128)}, f32[1,1,256]{2,1,0:T(1,128)S(1)}, u32[]{:S(2)}) copy-start(f32[1,1,256]{2,1,0:T(1,128)S(1)} %get-tuple-element.107) | copy-start | bytes 3076
  7.1 7.9 %copy-start.39 = (f32[1,1,256]{2,1,0:T(1,128)}, f32[1,1,256]{2,1,0:T(1,128)S(1)}, u32[]{:S(2)}) copy-start(f32[1,1,256]{2,1,0:T(1,128)S(1)} %get-tuple-element.108) | copy-start | bytes 3076
  7.1 7.9 %copy-start.41 = (f32[1,1,256]{2,1,0:T(1,128)}, f32[1,1,256]{2,1,0:T(1,128)S(1)}, u32[]{:S(2)}) copy-start(f32[1,1,256]{2,1,0:T(1,128)S(1)} %get-tuple-element.109) | copy-start | bytes 3076
  7.1 7.9 %copy-start.43 = (f32[1,1,256]{2,1,0:T(1,128)}, f32[1,1,256]{2,1,0:T(1,128)S(1)}, u32[]{:S(2)}) copy-start(f32[1,1,256]{2,1,0:T(1,128)S(1)} %get-tuple-element.110) | copy-start | bytes 3076
  7.1 7.9 %copy-start.45 = (f32[1,1,256]{2,1,0:T(1,128)}, f32[1,1,256]{2,1,0:T(1,128)S(1)}, u32[]{:S(2)}) copy-start(f32[1,1,256]{2,1,0:T(1,128)S(1)} %get-tuple-element.111) | copy-start | bytes 3076
  7.1 7.9 %copy-start.47 = (f32[1,1,256]{2,1,0:T(1,128)}, f32[1,1,256]{2,1,0:T(1,128)S(1)}, u32[]{:S(2)}) copy-start(f32[1,1,256]{2,1,0:T(1,128)S(1)} %get-tuple-element.112) | copy-start | bytes 3076
  7.1 7.9 %copy-start.49 = (f32[1,1,256]{2,1,0:T(1,128)}, f32[1,1,256]{2,1,0:T(1,128)S(1)}, u32[]{:S(2)}) copy-start(f32[1,1,256]{2,1,0:T(1,128)S(1)} %get-tuple-element.113) | copy-start | bytes 3076
  7.1 7.9 %copy-start.51 = (f32[1,1,256]{2,1,0:T(1,128)}, f32[1,1,256]{2,1,0:T(1,128)S(1)}, u32[]{:S(2)}) copy-start(f32[1,1,256]{2,1,0:T(1,128)S(1)} %get-tuple-element.114) | copy-start | bytes 3076
  7.1 7.9 %copy-start.53 = (f32[1,1,256]{2,1,0:T(1,128)}, f32[1,1,256]{2,1,0:T(1,128)S(1)}, u32[]{:S(2)}) copy-start(f32[1,1,256]{2,1,0:T(1,128)S(1)} %get-tuple-element.115) | copy-start | bytes 3076
  7.7 7.3 %copy-start.63 = (f32[1,1,256]{2,1,0:T(1,128)}, f32[1,1,256]{2,1,0:T(1,128)S(1)}, u32[]{:S(2)}) copy-start(f32[1,1,256]{2,1,0:T(1,128)S(1)} %get-tuple-element.90) | copy-start | bytes 3076
  7.7 7.3 %copy-start.65 = (f32[1,1,256]{2,1,0:T(1,128)}, f32[1,1,256]{2,1,0:T(1,128)S(1)}, u32[]{:S(2)}) copy-start(f32[1,1,256]{2,1,0:T(1,128)S(1)} %get-tuple-element.91) | copy-start | bytes 3076
  7.8 7.3 %copy-start.67 = (f32[1,1,256]{2,1,0:T(1,128)}, f32[1,1,256]{2,1,0:T(1,128)S(1)}, u32[]{:S(2)}) copy-start(f32[1,1,256]{2,1,0:T(1,128)S(1)} %get-tuple-element.92) | copy-start | bytes 3076
  7.8 7.3 %copy-start.69 = (f32[1,1,256]{2,1,0:T(1,128)}, f32[1,1,256]{2,1,0:T(1,128)S(1)}, u32[]{:S(2)}) copy-start(f32[1,1,256]{2,1,0:T(1,128)S(1)} %get-tuple-element.93) | copy-start | bytes 3076
  7.8 7.3 %copy-start.71 = (f32[1,1,256]{2,1,0:T(1,128)}, f32[1,1,256]{2,1,0:T(1,128)S(1)}, u32[]{:S(2)}) copy-start(f32[1,1,256]{2,1,0:T(1,128)S(1)} %get-tuple-element.94) | copy-start | bytes 3076
  7.8 7.3 %copy-start.73 = (f32[1,1,256]{2,1,0:T(1,128)}, f32[1,1,256]{2,1,0:T(1,128)S(1)}, u32[]{:S(2)}) copy-start(f32[1,1,256]{2,1,0:T(1,128)S(1)} %get-tuple-element.95) | copy-start | bytes 3076
  25.3 14.2 %collective-permute-start.12 = (f32[51,256]{1,0:T(8,128)S(1)}, f32[51,256]{1,0:T(8,128)S(1)}, u32[]{:S(2)}, u32[]{:S(2)}) collective-permute-start(f32[51,256]{1,0:T(8,128)S(1)} %concatenate.11), channel_id=1, source_target_pairs={{0,1},{1,0},{2,3},{3,2},{4,5},{5,4},{6,7},{7,6},{8,9},{9,8},{10,11... | collective-permute-start | bytes 156680 | tf_op jit(solution)/shard_map/ppermute | solution.py:52
  34.5 37.8 %collective-permute-start.8 = (f32[512,256]{1,0:T(8,128)}, f32[512,256]{1,0:T(8,128)}, u32[]{:S(2)}, u32[]{:S(2)}) collective-permute-start(f32[512,256]{1,0:T(8,128)} %constant_dynamic-slice_fusion.2), channel_id=1, source_target_pairs={{0,1},{1,0},{2,3},{3,2},{4,5},{5,4},{6,7},{7,6},{8,9},{9,8},{10,11... | collective-permute-start | bytes 1572872 | tf_op jit(solution)/shard_map/ppermute | solution.py:52
  35.6 26.6 %collective-permute-start.2 = (bf16[3,256,256]{2,1,0:T(8,128)(2,1)S(1)}, bf16[3,256,256]{2,1,0:T(8,128)(2,1)S(1)}, u32[]{:S(2)}, u32[]{:S(2)}) collective-permute-start(bf16[3,256,256]{2,1,0:T(8,128)(2,1)S(1)} %get-tuple-element.63), channel_id=1, source_target_pairs={{0,1},{1,2},{2,3},{3,4},{4,5},{5,6},{6,7},{7,8},{8,9},{9,10},{10,1... | collective-permute-start | bytes 1179656 | tf_op jit(solution)/shard_map/ppermute | solution.py:21
  38.0 24.1 %collective-permute-start.3 = (bf16[3,256,256]{2,1,0:T(8,128)(2,1)S(1)}, bf16[3,256,256]{2,1,0:T(8,128)(2,1)S(1)}, u32[]{:S(2)}, u32[]{:S(2)}) collective-permute-start(bf16[3,256,256]{2,1,0:T(8,128)(2,1)S(1)} %get-tuple-element.64), channel_id=1, source_target_pairs={{1,0},{2,1},{3,2},{4,3},{5,4},{6,5},{7,6},{8,7},{9,8},{10,9},{11,1... | collective-permute-start | bytes 1179656 | tf_op jit(solution)/shard_map/ppermute | solution.py:24
  39.5 11.0 %collective-permute-start.13 = (f32[51,256]{1,0:T(8,128)S(1)}, f32[51,256]{1,0:T(8,128)S(1)}, u32[]{:S(2)}, u32[]{:S(2)}) collective-permute-start(f32[51,256]{1,0:T(8,128)S(1)} %add.554), channel_id=1, source_target_pairs={{0,2},{1,3},{2,0},{3,1},{4,6},{5,7},{6,4},{7,5},{8,10},{9,11},{10,... | collective-permute-start | bytes 156680 | tf_op jit(solution)/shard_map/ppermute | solution.py:52
  45.6 13.8 %copy-start.91 = (f32[256]{0:T(256)S(1)}, f32[256]{0:T(256)}, u32[]{:S(2)}) copy-start(f32[256]{0:T(256)} %param.14) | copy-start | bytes 3076
  45.6 16.6 %copy-start.3 = (bf16[4,256,256]{2,1,0:T(8,128)(2,1)S(1)}, bf16[4,256,256]{2,1,0:T(8,128)(2,1)}, u32[]{:S(2)}) copy-start(bf16[4,256,256]{2,1,0:T(8,128)(2,1)} %copy-done.2) | copy-start | bytes 1572868
  45.7 16.4 %copy-start.5 = (f32[2,2,2,2,16,1024]{5,4,3,2,1,0:T(8,128)}, f32[2,2,2,2,16,1024]{5,4,3,2,1,0:T(8,128)S(1)}, u32[]{:S(2)}) copy-start(f32[2,2,2,2,16,1024]{5,4,3,2,1,0:T(8,128)S(1)} %copy.16) | copy-start | bytes 3145732
  50.6 5.7 %collective-permute-start.14 = (f32[51,256]{1,0:T(8,128)S(1)}, f32[51,256]{1,0:T(8,128)S(1)}, u32[]{:S(2)}, u32[]{:S(2)}) collective-permute-start(f32[51,256]{1,0:T(8,128)S(1)} %add.555), channel_id=1, source_target_pairs={{0,4},{1,5},{2,6},{3,7},{4,0},{5,1},{6,2},{7,3},{8,12},{9,13},{10,... | collective-permute-start | bytes 156680 | tf_op jit(solution)/shard_map/ppermute | solution.py:52
  54.9 19.3 %collective-permute-start.4 = (f32[128,1024]{1,0:T(8,128)}, f32[128,1024]{1,0:T(8,128)}, u32[]{:S(2)}, u32[]{:S(2)}) collective-permute-start(f32[128,1024]{1,0:T(8,128)} %constant_dynamic-slice_fusion.6), channel_id=1, source_target_pairs={{0,1},{1,0},{2,3},{3,2},{4,5},{5,4},{6,7},{7,6},{8,9},{9,8},{10,11... | collective-permute-start | bytes 1572872 | tf_op jit(solution)/shard_map/ppermute | solution.py:52
  56.2 5.2 %collective-permute-start.15 = (f32[51,256]{1,0:T(8,128)S(1)}, f32[51,256]{1,0:T(8,128)S(1)}, u32[]{:S(2)}, u32[]{:S(2)}) collective-permute-start(f32[51,256]{1,0:T(8,128)S(1)} %add.556), channel_id=1, source_target_pairs={{0,8},{1,9},{2,10},{3,11},{4,12},{5,13},{6,14},{7,15},{8,0},{9,1},... | collective-permute-start | bytes 156680 | tf_op jit(solution)/shard_map/ppermute | solution.py:52
  73.7 9.3 %collective-permute-start.9 = (f32[256,256]{1,0:T(8,128)S(1)}, f32[256,256]{1,0:T(8,128)S(1)}, u32[]{:S(2)}, u32[]{:S(2)}) collective-permute-start(f32[256,256]{1,0:T(8,128)S(1)} %constant_dynamic-slice_fusion.1), channel_id=1, source_target_pairs={{0,2},{1,3},{2,0},{3,1},{4,6},{5,7},{6,4},{7,5},{8,10},{9,11},{10,... | collective-permute-start | bytes 786440 | tf_op jit(solution)/shard_map/ppermute | solution.py:52
  75.4 10.6 %collective-permute-start.5 = (f32[64,1024]{1,0:T(8,128)S(1)}, f32[64,1024]{1,0:T(8,128)S(1)}, u32[]{:S(2)}, u32[]{:S(2)}) collective-permute-start(f32[64,1024]{1,0:T(8,128)S(1)} %constant_dynamic-slice_fusion.5), channel_id=1, source_target_pairs={{0,2},{1,3},{2,0},{3,1},{4,6},{5,7},{6,4},{7,5},{8,10},{9,11},{10,... | collective-permute-start | bytes 786440 | tf_op jit(solution)/shard_map/ppermute | solution.py:52
  83.1 6.6 %collective-permute-start.10 = (f32[128,256]{1,0:T(8,128)S(1)}, f32[128,256]{1,0:T(8,128)S(1)}, u32[]{:S(2)}, u32[]{:S(2)}) collective-permute-start(f32[128,256]{1,0:T(8,128)S(1)} %constant_dynamic-slice_fusion), channel_id=1, source_target_pairs={{0,4},{1,5},{2,6},{3,7},{4,0},{5,1},{6,2},{7,3},{8,12},{9,13},{10,... | collective-permute-start | bytes 393224 | tf_op jit(solution)/shard_map/ppermute | solution.py:52
  86.1 5.1 %collective-permute-start.6 = (f32[32,1024]{1,0:T(8,128)S(1)}, f32[32,1024]{1,0:T(8,128)S(1)}, u32[]{:S(2)}, u32[]{:S(2)}) collective-permute-start(f32[32,1024]{1,0:T(8,128)S(1)} %constant_dynamic-slice_fusion.4), channel_id=1, source_target_pairs={{0,4},{1,5},{2,6},{3,7},{4,0},{5,1},{6,2},{7,3},{8,12},{9,13},{10,... | collective-permute-start | bytes 393224 | tf_op jit(solution)/shard_map/ppermute | solution.py:52
  89.8 5.6 %collective-permute-start.11 = (f32[64,256]{1,0:T(8,128)S(1)}, f32[64,256]{1,0:T(8,128)S(1)}, u32[]{:S(2)}, u32[]{:S(2)}) collective-permute-start(f32[64,256]{1,0:T(8,128)S(1)} %constant_dynamic-slice_fusion.7), channel_id=1, source_target_pairs={{0,8},{1,9},{2,10},{3,11},{4,12},{5,13},{6,14},{7,15},{8,0},{9,1},... | collective-permute-start | bytes 196616 | tf_op jit(solution)/shard_map/ppermute | solution.py:52
  91.2 5.9 %collective-permute-start.7 = (f32[16,1024]{1,0:T(8,128)S(1)}, f32[16,1024]{1,0:T(8,128)S(1)}, u32[]{:S(2)}, u32[]{:S(2)}) collective-permute-start(f32[16,1024]{1,0:T(8,128)S(1)} %constant_dynamic-slice_fusion.3), channel_id=1, source_target_pairs={{0,8},{1,9},{2,10},{3,11},{4,12},{5,13},{6,14},{7,15},{8,0},{9,1},... | collective-permute-start | bytes 196616 | tf_op jit(solution)/shard_map/ppermute | solution.py:52
  (79 other events, 243.4 us)

commit v4 on v3

--- a/solution.py
+++ b/solution.py
@@ -49,9 +49,12 @@
             half = p.shape[0] // 2
             keeps.append(lax.dynamic_slice_in_dim(p, bit * half, half, axis=0))
             gives.append(lax.dynamic_slice_in_dim(p, (1 - bit) * half, half, axis=0))
-        got, got_whole = lax.ppermute((gives, whole), axis, pairs)
-        parts = [k + g for k, g in zip(keeps, got)]
-        whole = whole + got_whole
+        got = lax.ppermute(jnp.concatenate(gives + [whole], axis=0), axis, pairs)
+        parts, offset = [], 0
+        for k in keeps:
+            parts.append(k + got[offset : offset + k.shape[0]])
+            offset += k.shape[0]
+        whole = whole + got[offset:]
     return parts, whole
 
 
@@ -143,7 +146,10 @@
     ).astype(jnp.bfloat16)
     kernel_grad = kernel_terms(window, grad_tile.astype(jnp.float32), image_rows, TILE_COLS)
     packed = jnp.concatenate([kernel_grad, gain_grad[None], scale_grad[None]], axis=0)
-    (grad_w_in, grad_w_out), small_grads = halving_reduce([partial_in, partial_out], packed, "row")
+    (owned_in, grad_w_out), small_grads = halving_reduce(
+        [partial_in.reshape(-1, channels), partial_out], packed, "row"
+    )
+    grad_w_in = owned_in.reshape(-1, hidden)
     grad_conv = lax.dynamic_update_slice_in_dim(
         jnp.zeros_like(image), grad_tile, first_col, axis=1
     )

time: 98.1 us -> 108 us (1.10)
  local copies, waits for them, and re-layouts: 7.26 us -> 26.6 us
  starting transfers between devices: 31.2 us -> 19.9 us
  other arithmetic: 24.6 us -> 27.9 us
  waiting for transfers between devices: 24.7 us -> 22.7 us
    concatenate x0 -> x1, local copies, waits for them, and re-layouts: none -> 11.8 us  [halving_reduce(): got = lax.ppermute(jnp.concatenate(gives + [whole], axis=0), axis, pairs)]
    ppermute x12 -> x4, starting transfers between devices: 23.6 us -> 13.2 us  [halving_reduce(): got = lax.ppermute(jnp.concatenate(gives + [whole], axis=0), axis, pairs)]
    concatenate x1, local copies, waits for them, and re-layouts: 0.18 us -> 4.97 us  [shards(): jnp.concatenate([kernel_grad, gain_grad[None], scale_grad[None]], axis=0)]
    ppermute x12 -> x4, waiting for transfers between devices: 22.7 us -> 20.6 us  [halving_reduce(): got = lax.ppermute(jnp.concatenate(gives + [whole], axis=0), axis, pairs)]
    concatenate x0 -> x3, other arithmetic: none -> 1.55 us  [halving_reduce(): got = lax.ppermute(jnp.concatenate(gives + [whole], axis=0), axis, pairs)]
    another operation x0 -> x1, local copies, waits for them, and re-layouts: none -> 1.29 us  [bit_reversed(): values = values.reshape((2,) * steps + (values.shape[0] // count,) + rest)]
    transpose x2, local copies, waits for them, and re-layouts: 0.19 us -> 1.41 us  [bit_reversed(): return values.transpose(order).reshape((-1,) + rest)]
    dot_general x1, matrix products: 1.66 us -> 0.46 us  [shards(): lax.dot_general(normed_flat, pre_flat, (((0,), (0,)), ((), ())), preferre...]
  transfers between devices with their start and end apart: 16 -> 8, of which waited for: 9 -> 3; matrix products, arithmetic and copies ran while one was open for 21% -> 16% of each run, Pallas kernels for 0% -> 0%
where the time goes in v4:
time: 108 us; the launch traced here: 107 us
  other arithmetic  27.9 us (26%)
  local copies, waits for them, and re-layouts  26.6 us (25%)
  waiting for transfers between devices  22.7 us (21%)
  starting transfers between devices  19.9 us (18%)
  matrix products  7.27 us (7%)
  between operations  2.71 us (3%)
    ppermute x4, waiting for transfers between devices, halving_reduce(): got = lax.ppermute(jnp.concatenate(gives + [whole], axis=0), axis, pairs)  20.6 us
    ppermute x4, starting transfers between devices, halving_reduce(): got = lax.ppermute(jnp.concatenate(gives + [whole], axis=0), axis, pairs)  13.2 us
    concatenate x1, local copies, waits for them, and re-layouts, halving_reduce(): got = lax.ppermute(jnp.concatenate(gives + [whole], axis=0), axis, pairs)  11.8 us
    convert_element_type x1, other arithmetic, shards(): (cotangent.astype(jnp.float32) + conv_back).astype(jnp.bfloat16)  9.86 us
    concatenate x1, local copies, waits for them, and re-layouts, shards(): jnp.concatenate([kernel_grad, gain_grad[None], scale_grad[None]], axis=0)  4.97 us
    reduce_sum x1, other arithmetic, shards(): centre = jnp.mean(filtered, axis=-1, keepdims=True)  4.57 us
    reduce_sum x3, other arithmetic, kernel_terms(): jnp.sum(padded[row_tap:row_tap + image_rows, col_tap:col_tap + image_cols...  4.5 us
    ppermute x2, starting transfers between devices, padded_2(): lax.ppermute(lax.slice_in_dim(block, block.shape[dim] - width, None, axis...  4.16 us
  transfers between devices with their start and end apart: 8, of which 3 were waited for; matrix products, arithmetic and copies ran while one was open for 16% of the time, Pallas kernels for 0%

profile of v4, /device:TPU:0, one launch (start us, length us, event | category | flops | bytes accessed | tf_op | source)
XLA Modules:
  0.0 107.0 jit_solution(13341227777949243819)
XLA Ops:
  0.7 1.1 %copy.22 = bf16[4,256,256]{2,1,0:T(8,128)(2,1)S(1)} copy(bf16[4,256,256]{2,1,0:T(8,128)(2,1)} %param.8) | data formatting | bytes 1048576
  1.8 2.4 %collective-permute-start = (bf16[3,256,256]{2,1,0:T(8,128)(2,1)S(1)}, bf16[3,256,256]{2,1,0:T(8,128)(2,1)S(1)}, u32[]{:S(2)}, u32[]{:S(2)}) collective-permute-start(bf16[3,256,256]{2,1,0:T(8,128)(2,1)S(1)} %get-tuple-element.70), channel_id=1, source_target_pairs={{0,1},{1,2},{2,3},{3,4},{4,5},{5,6},{6,7},{7,8},{8,9},{9,10},{10,1... | collective-permute-start | bytes 1179656 | tf_op jit(solution)/shard_map/ppermute | solution.py:21
  4.2 1.3 %collective-permute-start.1 = (bf16[3,256,256]{2,1,0:T(8,128)(2,1)S(1)}, bf16[3,256,256]{2,1,0:T(8,128)(2,1)S(1)}, u32[]{:S(2)}, u32[]{:S(2)}) collective-permute-start(bf16[3,256,256]{2,1,0:T(8,128)(2,1)S(1)} %get-tuple-element.69), channel_id=1, source_target_pairs={{1,0},{2,1},{3,2},{4,3},{5,4},{6,5},{7,6},{8,7},{9,8},{10,9},{11,1... | collective-permute-start | bytes 1179656 | tf_op jit(solution)/shard_map/ppermute | solution.py:24
  5.5 0.7 bitcast_reduce_fusion
  7.1 0.6 fusion.145
  7.9 2.0 %collective-permute-done.1 = bf16[3,256,256]{2,1,0:T(8,128)(2,1)S(1)} collective-permute-done((bf16[3,256,256]{2,1,0:T(8,128)(2,1)S(1)}, bf16[3,256,256]{2,1,0:T(8,128)(2,1)S(1)}, u32[]{:S(2)}, u32[]{:S(2)}) %collective-permute-start.1) | collective-permute-done | bytes 393248 | tf_op jit(solution)/shard_map/ppermute | solution.py:24
  9.9 0.3 fusion.82
  10.3 4.6 %fusion.141 = (f32[4,128]{1,0:T(4,128)S(1)}, f32[4,128,256]{2,1,0:T(8,128)S(1)}) fusion(f32[256]{0:T(256)S(1)} %bitcast.236, f32[10,134,256]{2,1,0:T(8,128)S(1)} %fusion.82, f32[256]{0:T(256)S(1)} %bitcast.238, f32[256]{0:T(256)S(1)} %bitcast.182, f32[256]{0:T(256)S(1)} %bitcast.184, f32[256]{0:T(256)S(1)} %bitcast.186, f32[256]{0:T(256)S(1)} %bitcast.188, ...), kind=kLoop, calls=%fused_computation.261 | loop fusion | flops 12844544 | bytes 26266624 | tf_op jit(solution)/shard_map/reduce_sum | solution.py:109
  15.2 0.2 multiply_reduce_fusion.3
  15.5 0.2 multiply_convert_fusion.3
  15.8 1.8 %fusion.11 = (bf16[1024,512]{0,1:T(8,128)(2,1)}, f32[512,1024]{1,0:T(8,128)S(1)}) fusion(bf16[512,256]{1,0:T(8,128)(2,1)S(1)} %bitcast.148, bf16[256,1024]{1,0:T(8,128)(2,1)S(1)} %copy-done), kind=kOutput, calls=%fused_computation.63 | convolution fusion | flops 273154048 | bytes 3932160 | tf_op jit(solution)/shard_map/dot_general | solution.py:119
  17.6 1.6 %fusion.86 = (f32[256]{0:T(256)S(1)}, bf16[4,128,256]{2,1,0:T(8,128)(2,1)S(1)}, f32[512,256]{1,0:T(8,128)}) fusion(bf16[4,256,256]{2,1,0:T(8,128)(2,1)S(1)} %copy-done.7, s32[]{:T(128)S(6)} %select_n.24, f32[256]{0:T(256)S(1)} %copy-done.80, bf16[1024,256]{1,0:T(8,128)(2,1)S(1)} %copy-done.9, f32[512,1024]{1,0:T(8,128)S(1)} %get-tuple-element.128), kind=kOutput, calls=%fused_computation.169 | convolution fusion | flops 273809152 | bytes 3672068 | tf_op jit(solution)/shard_map/dot_general | solution.py:121
  19.2 1.4 %fusion.6 = bf16[512,1024]{1,0:T(8,128)(2,1)S(1)} fusion(f32[512,1024]{1,0:T(8,128)S(1)} %get-tuple-element.128, bf16[512,256]{1,0:T(8,128)(2,1)S(1)} %bitcast.146, bf16[1024,256]{1,0:T(8,128)(2,1)S(1)} %copy-done.9), kind=kOutput, calls=%fused_computation.58 | convolution fusion | flops 278396928 | bytes 3932160 | tf_op jit(solution)/shard_map/dot_general | solution.py:122
  20.7 0.5 fusion.147
  21.1 0.6 multiply_reduce_fusion.2
  21.7 0.3 multiply_reduce_fusion
  22.0 2.1 %fusion.134 = (f32[256]{0:T(256)S(1)}, f32[256]{0:T(256)S(1)}, f32[256]{0:T(256)S(1)}, f32[256]{0:T(256)S(1)}, f32[256]{0:T(256)S(1)}, /*index=5*/f32[256]{0:T(2...) fusion(f32[10,134,256]{2,1,0:T(8,128)S(1)} %fusion.82, ...), kind=kLoop, calls=%fused_computation.217 | loop fusion | flops 5893632 | bytes 10775552 | tf_op jit(solution)/shard_map/reduce_sum | solution.py:90
  24.3 1.6 %fusion.135 = (f32[256]{0:T(256)}, f32[256]{0:T(256)}, f32[256]{0:T(256)}, f32[256]{0:T(256)}, f32[256]{0:T(256)}, /*index=5*/f32[256]{0:T(256)}, f32[256]{0:T(2...) fusion(bf16[4,128,256]{2,1,0:T(8,128)(2,1)S(1)} %get-tuple-elem, ...), kind=kLoop, calls=%fused_computation.218 | loop fusion | flops 4845056 | bytes 9717760 | tf_op jit(solution)/shard_map/reduce_sum | solution.py:90
  25.9 0.7 fusion.133
  26.6 1.5 %copy.16 = bf16[1024,512]{1,0:T(8,128)(2,1)S(1)} copy(bf16[1024,512]{0,1:T(8,128)(2,1)} %get-tuple-element.127) | data formatting | bytes 2097152 | tf_op jit(solution)/shard_map/convert_element_type | solution.py:120
  28.1 1.4 %convolution_bitcast_fusion = f32[2,2,2,2,64,256]{5,4,0,1,2,3:T(8,128)S(1)} fusion(bf16[2,2,2,2,64,512]{5,4,3,2,1,0:T(8,128)(2,1)S(1)} %bitcast.143, bf16[512,256,1,1,1,1]{1,0,5,4,3,2:T(8,128)(2,1)} %bitcast.147), kind=kOutput, calls=%fused_computation.70 | convolution fusion | flops 268435456 | bytes 2359296 | tf_op jit(solution)/shard_map/dot_general | solution.py:128
  29.5 0.1 copy.17
  29.6 1.3 %reshape_reshape.3 = f32[2,2,2,2,64,256]{5,4,3,2,1,0:T(8,128)} reshape(f32[256,1024]{1,0:T(8,128)S(1)} %fusion.147) | data formatting | bytes 2097152 | tf_op jit(solution)/shard_map/reshape;reshape | solution.py:31
  30.9 1.3 %copy.15 = f32[2,2,2,2,64,256]{5,4,3,2,1,0:T(8,128)S(1)} copy(f32[2,2,2,2,64,256]{5,4,0,1,2,3:T(8,128)} %bitcast.144) | data formatting | bytes 2097152 | tf_op jit(solution)/shard_map/transpose | solution.py:33
  32.3 1.1 constant_dynamic-slice_fusion.6
  33.4 11.8 %concatenate.24 = f32[1075,256]{1,0:T(8,128)} concatenate(f32[512,256]{1,0:T(8,128)} %get-tuple-element.130, f32[512,256]{1,0:T(8,128)} %get-tuple-element.129, f32[1,256]{1,0:T(1,128)S(1)} %bitcast.178, f32[1,256]{1,0:T(1,128)} %bitcast.310, f32[1,256]{1,0:T(1,128)} %bitcast.312, f32[1,256]{1,0:T(1,128)} %bitcast.314, f32[1,256]{1,0:T(1,128)} %bitcast.316, f32[1,256]{1,0:T(1,128)} %bitcast.318, ...), dimensions={0} | concatenate | bytes 2201600 | tf_op jit(solution)/shard_map/concatenate | solution.py:52
  45.3 6.0 %collective-permute-start.4 = (f32[1075,256]{1,0:T(8,128)}, f32[1075,256]{1,0:T(8,128)}, u32[]{:S(2)}, u32[]{:S(2)}) collective-permute-start(f32[1075,256]{1,0:T(8,128)} %concatenate.24), channel_id=1, source_target_pairs={{0,1},{1,0},{2,3},{3,2},{4,5},{5,4},{6,7},{7,6},{8,9},{9,8},{10,11... | collective-permute-start | bytes 3302408 | tf_op jit(solution)/shard_map/ppermute | solution.py:52
  51.3 5.0 %concatenate.25 = f32[51,256]{1,0:T(8,128)S(1)} concatenate(f32[1,256]{1,0:T(1,128)S(1)} %bitcast.179, f32[1,256]{1,0:T(1,128)} %bitcast.311, f32[1,256]{1,0:T(1,128)} %bitcast.313, f32[1,256]{1,0:T(1,128)} %bitcast.315, f32[1,256]{1,0:T(1,128)} %bitcast.317, f32[1,256]{1,0:T(1,128)} %bitcast.319, f32[1,256]{1,0:T(1,128)} %bitcast.321, f32[1,256]{1,0:T(1,128)} %bitcast.323, ...), dimensions={0} | concatenate | bytes 104448 | tf_op jit(solution)/shard_map/concatenate | solution.py:148
  56.2 1.3 %slice_add_fusion.1 = (f32[512,256]{1,0:T(8,128)S(1)}, f32[512,256]{1,0:T(8,128)S(1)}) fusion(f32[1075,256]{1,0:T(8,128)} %collective-permute-done.4, f32[1024,256]{1,0:T(8,128)S(1)} %bitcast.142, s32[]{:T(128)S(6)} %select_n.47, f32[1024,256]{1,0:T(8,128)S(1)} %bitcast.140), kind=kLoop, calls=%fused_computation.220 | loop fusion | flops 262144 | bytes 3145732 | tf_op jit(solution)/shard_map/add | solution.py:55
  57.6 0.8 copy-done.3
  58.4 0.1 copy-done.5
  58.6 0.9 slice_add_fusion.11
  59.5 0.8 pad_maximum_fusion
  60.3 2.5 %collective-permute-start.5 = (f32[563,256]{1,0:T(8,128)}, f32[563,256]{1,0:T(8,128)S(1)}, u32[]{:S(2)}, u32[]{:S(2)}) collective-permute-start(f32[563,256]{1,0:T(8,128)} %pad_maximum_fusion), channel_id=1, source_target_pairs={{0,2},{1,3},{2,0},{3,1},{4,6},{5,7},{6,4},{7,5},{8,10},{9,11},{10,... | collective-permute-start | bytes 1729544 | tf_op jit(solution)/shard_map/ppermute | solution.py:52
  62.9 1.8 %collective-permute-start.2 = (bf16[3,256,256]{2,1,0:T(8,128)(2,1)S(1)}, bf16[3,256,256]{2,1,0:T(8,128)(2,1)S(1)}, u32[]{:S(2)}, u32[]{:S(2)}) collective-permute-start(bf16[3,256,256]{2,1,0:T(8,128)(2,1)S(1)} %get-tuple-element.67), channel_id=1, source_target_pairs={{0,1},{1,2},{2,3},{3,4},{4,5},{5,6},{6,7},{7,8},{8,9},{9,10},{10,1... | collective-permute-start | bytes 1179656 | tf_op jit(solution)/shard_map/ppermute | solution.py:21
  64.7 1.3 %collective-permute-start.3 = (bf16[3,256,256]{2,1,0:T(8,128)(2,1)S(1)}, bf16[3,256,256]{2,1,0:T(8,128)(2,1)S(1)}, u32[]{:S(2)}, u32[]{:S(2)}) collective-permute-start(bf16[3,256,256]{2,1,0:T(8,128)(2,1)S(1)} %get-tuple-element.68), channel_id=1, source_target_pairs={{1,0},{2,1},{3,2},{4,3},{5,4},{6,5},{7,6},{8,7},{9,8},{10,9},{11,1... | collective-permute-start | bytes 1179656 | tf_op jit(solution)/shard_map/ppermute | solution.py:24
  66.0 14.8 %collective-permute-done.5 = f32[563,256]{1,0:T(8,128)S(1)} collective-permute-done((f32[563,256]{1,0:T(8,128)}, f32[563,256]{1,0:T(8,128)S(1)}, u32[]{:S(2)}, u32[]{:S(2)}) %collective-permute-start.5) | collective-permute-done | bytes 576544 | tf_op jit(solution)/shard_map/ppermute | solution.py:52
  80.9 0.1 slice_add_fusion.3
  81.0 2.0 %collective-permute-start.6 = (f32[307,256]{1,0:T(8,128)S(1)}, f32[307,256]{1,0:T(8,128)S(1)}, u32[]{:S(2)}, u32[]{:S(2)}) collective-permute-start(f32[307,256]{1,0:T(8,128)S(1)} %pad_maximum_fusion.1), channel_id=1, source_target_pairs={{0,4},{1,5},{2,6},{3,7},{4,0},{5,1},{6,2},{7,3},{8,12},{9,13},{10,... | collective-permute-start | bytes 943112 | tf_op jit(solution)/shard_map/ppermute | solution.py:52
  83.3 0.6 copy-done.1
  83.9 0.2 maximum_convert_fusion
  84.1 5.8 %collective-permute-done.6 = f32[307,256]{1,0:T(8,128)S(1)} collective-permute-done((f32[307,256]{1,0:T(8,128)S(1)}, f32[307,256]{1,0:T(8,128)S(1)}, u32[]{:S(2)}, u32[]{:S(2)}) %collective-permute-start.6) | collective-permute-done | bytes 314400 | tf_op jit(solution)/shard_map/ppermute | solution.py:52
  90.0 0.7 pad_maximum_fusion.2
  90.7 2.7 %collective-permute-start.7 = (f32[179,256]{1,0:T(8,128)}, f32[179,256]{1,0:T(8,128)}, u32[]{:S(2)}, u32[]{:S(2)}) collective-permute-start(f32[179,256]{1,0:T(8,128)} %pad_maximum_fusion.2), channel_id=1, source_target_pairs={{0,8},{1,9},{2,10},{3,11},{4,12},{5,13},{6,14},{7,15},{8,0},{9,1},... | collective-permute-start | bytes 549896 | tf_op jit(solution)/shard_map/ppermute | solution.py:52
  93.6 9.9 %fusion.20 = bf16[4,256,256]{2,1,0:T(8,128)(2,1)} fusion(f32[10,256,256]{2,1,0:T(8,128)S(1)} %maximum_convert_fusion, bf16[4,256,256]{2,1,0:T(8,128)(2,1)} %param.15, f32[256]{0:T(256)S(1)} %bitcast.181, f32[256]{0:T(256)} %bitcast.241, f32[256]{0:T(256)S(1)} %bitcast.219, f32[256]{0:T(256)} %bitcast.235, f32[256]{0:T(256)} %bitcast.233, f32[256]{0:T(256)} %bitcast.231, ...), kind=kLoop, calls=%fused_computation.81 | loop fusion | flops 26214400 | bytes 11060224 | tf_op jit(solution)/shard_map/convert_element_type | solution.py:159
  103.4 1.5 %slice_add_fusion.6 = (f32[64,256]{1,0:T(8,128)}, f32[64,256]{1,0:T(8,128)S(1)}) fusion(f32[179,256]{1,0:T(8,128)} %collective-permute-done.7, f32[128,256]{1,0:T(8,128)S(1)} %get-tuple-element.72, s32[]{:T(128)S(6)} %select_n.53, f32[128,256]{1,0:T(8,128)S(1)} %get-tuple-element.71), kind=kLoop, calls=%fused_computation.237 | loop fusion | flops 32768 | bytes 393220 | tf_op jit(solution)/shard_map/add | solution.py:55
  104.9 0.6 reshape.71
  105.6 1.4 %slice_add_fusion.8 = f32[51,256]{1,0:T(8,128)} fusion(f32[51,256]{1,0:T(8,128)S(1)} %slice_add_fusion.9, f32[179,256]{1,0:T(8,128)} %collective-permute-done.7), kind=kLoop, calls=%fused_computation.239 | loop fusion | flops 13056 | bytes 156672 | tf_op jit(solution)/shard_map/add | solution.py:57
  (189 shorter events, 0.8 us)
Async XLA Ops:
  0.6 15.1 %copy-start = (bf16[256,1024]{1,0:T(8,128)(2,1)S(1)}, bf16[256,1024]{1,0:T(8,128)(2,1)}, u32[]{:S(2)}) copy-start(bf16[256,1024]{1,0:T(8,128)(2,1)} %param.12) | copy-start | bytes 1572868
  1.8 6.0 %collective-permute-start = (bf16[3,256,256]{2,1,0:T(8,128)(2,1)S(1)}, bf16[3,256,256]{2,1,0:T(8,128)(2,1)S(1)}, u32[]{:S(2)}, u32[]{:S(2)}) collective-permute-start(bf16[3,256,256]{2,1,0:T(8,128)(2,1)S(1)} %get-tuple-element.70), channel_id=1, source_target_pairs={{0,1},{1,2},{2,3},{3,4},{4,5},{5,6},{6,7},{7,8},{8,9},{9,10},{10,1... | collective-permute-start | bytes 1179656 | tf_op jit(solution)/shard_map/ppermute | solution.py:21
  4.2 5.7 %collective-permute-start.1 = (bf16[3,256,256]{2,1,0:T(8,128)(2,1)S(1)}, bf16[3,256,256]{2,1,0:T(8,128)(2,1)S(1)}, u32[]{:S(2)}, u32[]{:S(2)}) collective-permute-start(bf16[3,256,256]{2,1,0:T(8,128)(2,1)S(1)} %get-tuple-element.69), channel_id=1, source_target_pairs={{1,0},{2,1},{3,2},{4,3},{5,4},{6,5},{7,6},{8,7},{9,8},{10,9},{11,1... | collective-permute-start | bytes 1179656 | tf_op jit(solution)/shard_map/ppermute | solution.py:24
  6.9 8.0 %copy-start.11 = (f32[1,1,256]{2,1,0:T(1,128)}, f32[1,1,256]{2,1,0:T(1,128)S(1)}, u32[]{:S(2)}) copy-start(f32[1,1,256]{2,1,0:T(1,128)S(1)} %get-tuple-element.82) | copy-start | bytes 3076
  6.9 8.0 %copy-start.13 = (f32[1,1,256]{2,1,0:T(1,128)}, f32[1,1,256]{2,1,0:T(1,128)S(1)}, u32[]{:S(2)}) copy-start(f32[1,1,256]{2,1,0:T(1,128)S(1)} %get-tuple-element.83) | copy-start | bytes 3076
  6.9 8.0 %copy-start.15 = (f32[1,1,256]{2,1,0:T(1,128)}, f32[1,1,256]{2,1,0:T(1,128)S(1)}, u32[]{:S(2)}) copy-start(f32[1,1,256]{2,1,0:T(1,128)S(1)} %get-tuple-element.84) | copy-start | bytes 3076
  6.9 8.0 %copy-start.17 = (f32[1,1,256]{2,1,0:T(1,128)}, f32[1,1,256]{2,1,0:T(1,128)S(1)}, u32[]{:S(2)}) copy-start(f32[1,1,256]{2,1,0:T(1,128)S(1)} %get-tuple-element.85) | copy-start | bytes 3076
  6.9 8.0 %copy-start.19 = (f32[1,1,256]{2,1,0:T(1,128)}, f32[1,1,256]{2,1,0:T(1,128)S(1)}, u32[]{:S(2)}) copy-start(f32[1,1,256]{2,1,0:T(1,128)S(1)} %get-tuple-element.86) | copy-start | bytes 3076
  6.9 8.0 %copy-start.21 = (f32[1,1,256]{2,1,0:T(1,128)}, f32[1,1,256]{2,1,0:T(1,128)S(1)}, u32[]{:S(2)}) copy-start(f32[1,1,256]{2,1,0:T(1,128)S(1)} %get-tuple-element.87) | copy-start | bytes 3076
  24.2 9.1 %copy-start.66 = (f32[256]{0:T(256)}, f32[256]{0:T(256)S(1)}, u32[]{:S(2)}) copy-start(f32[256]{0:T(256)S(1)} %get-tuple-element.25) | copy-start | bytes 3076
  24.2 9.1 %copy-start.67 = (f32[256]{0:T(256)}, f32[256]{0:T(256)S(1)}, u32[]{:S(2)}) copy-start(f32[256]{0:T(256)S(1)} %get-tuple-element.26) | copy-start | bytes 3076
  24.2 9.1 %copy-start.68 = (f32[256]{0:T(256)}, f32[256]{0:T(256)S(1)}, u32[]{:S(2)}) copy-start(f32[256]{0:T(256)S(1)} %get-tuple-element.27) | copy-start | bytes 3076
  24.2 9.1 %copy-start.69 = (f32[256]{0:T(256)}, f32[256]{0:T(256)S(1)}, u32[]{:S(2)}) copy-start(f32[256]{0:T(256)S(1)} %get-tuple-element.28) | copy-start | bytes 3076
  24.2 9.2 %copy-start.70 = (f32[256]{0:T(256)}, f32[256]{0:T(256)S(1)}, u32[]{:S(2)}) copy-start(f32[256]{0:T(256)S(1)} %get-tuple-element.29) | copy-start | bytes 3076
  24.2 9.2 %copy-start.71 = (f32[256]{0:T(256)}, f32[256]{0:T(256)S(1)}, u32[]{:S(2)}) copy-start(f32[256]{0:T(256)S(1)} %get-tuple-element.30) | copy-start | bytes 3076
  24.2 9.2 %copy-start.72 = (f32[256]{0:T(256)}, f32[256]{0:T(256)S(1)}, u32[]{:S(2)}) copy-start(f32[256]{0:T(256)S(1)} %get-tuple-element.31) | copy-start | bytes 3076
  24.2 9.2 %copy-start.73 = (f32[256]{0:T(256)}, f32[256]{0:T(256)S(1)}, u32[]{:S(2)}) copy-start(f32[256]{0:T(256)S(1)} %get-tuple-element.32) | copy-start | bytes 3076
  24.2 9.2 %copy-start.74 = (f32[256]{0:T(256)}, f32[256]{0:T(256)S(1)}, u32[]{:S(2)}) copy-start(f32[256]{0:T(256)S(1)} %get-tuple-element.33) | copy-start | bytes 3076
  24.2 9.2 %copy-start.75 = (f32[256]{0:T(256)}, f32[256]{0:T(256)S(1)}, u32[]{:S(2)}) copy-start(f32[256]{0:T(256)S(1)} %get-tuple-element.34) | copy-start | bytes 3076
  24.2 9.2 %copy-start.76 = (f32[256]{0:T(256)}, f32[256]{0:T(256)S(1)}, u32[]{:S(2)}) copy-start(f32[256]{0:T(256)S(1)} %get-tuple-element.35) | copy-start | bytes 3076
  24.2 9.2 %copy-start.77 = (f32[256]{0:T(256)}, f32[256]{0:T(256)S(1)}, u32[]{:S(2)}) copy-start(f32[256]{0:T(256)S(1)} %get-tuple-element.36) | copy-start | bytes 3076
  24.3 9.2 %copy-start.78 = (f32[256]{0:T(256)}, f32[256]{0:T(256)S(1)}, u32[]{:S(2)}) copy-start(f32[256]{0:T(256)S(1)} %get-tuple-element.37) | copy-start | bytes 3076
  24.3 9.2 %copy-start.79 = (f32[256]{0:T(256)}, f32[256]{0:T(256)S(1)}, u32[]{:S(2)}) copy-start(f32[256]{0:T(256)S(1)} %get-tuple-element.38) | copy-start | bytes 3076
  45.3 10.9 %collective-permute-start.4 = (f32[1075,256]{1,0:T(8,128)}, f32[1075,256]{1,0:T(8,128)}, u32[]{:S(2)}, u32[]{:S(2)}) collective-permute-start(f32[1075,256]{1,0:T(8,128)} %concatenate.24), channel_id=1, source_target_pairs={{0,1},{1,0},{2,3},{3,2},{4,5},{5,4},{6,7},{7,6},{8,9},{9,8},{10,11... | collective-permute-start | bytes 3302408 | tf_op jit(solution)/shard_map/ppermute | solution.py:52
  58.5 22.3 %copy-start.4 = (f32[512,256]{1,0:T(8,128)S(1)}, f32[512,256]{1,0:T(8,128)}, u32[]{:S(2)}) copy-start(f32[512,256]{1,0:T(8,128)} %copy-done.3) | copy-start | bytes 1572868
  58.6 22.3 %copy-start.6 = (f32[512,256]{1,0:T(8,128)S(1)}, f32[512,256]{1,0:T(8,128)}, u32[]{:S(2)}) copy-start(f32[512,256]{1,0:T(8,128)} %copy-done.5) | copy-start | bytes 1572868
  60.3 20.5 %collective-permute-start.5 = (f32[563,256]{1,0:T(8,128)}, f32[563,256]{1,0:T(8,128)S(1)}, u32[]{:S(2)}, u32[]{:S(2)}) collective-permute-start(f32[563,256]{1,0:T(8,128)} %pad_maximum_fusion), channel_id=1, source_target_pairs={{0,2},{1,3},{2,0},{3,1},{4,6},{5,7},{6,4},{7,5},{8,10},{9,11},{10,... | collective-permute-start | bytes 1729544 | tf_op jit(solution)/shard_map/ppermute | solution.py:52
  62.9 20.2 %copy-start.2 = (f32[512,256]{1,0:T(8,128)S(1)}, f32[512,256]{1,0:T(8,128)}, u32[]{:S(2)}) copy-start(f32[512,256]{1,0:T(8,128)} %get-tuple-element.124) | copy-start | bytes 1572868
  62.9 20.2 %copy-start.81 = (f32[256]{0:T(256)S(1)}, f32[256]{0:T(256)}, u32[]{:S(2)}) copy-start(f32[256]{0:T(256)} %param.14) | copy-start | bytes 3076
  62.9 20.4 %collective-permute-start.2 = (bf16[3,256,256]{2,1,0:T(8,128)(2,1)S(1)}, bf16[3,256,256]{2,1,0:T(8,128)(2,1)S(1)}, u32[]{:S(2)}, u32[]{:S(2)}) collective-permute-start(bf16[3,256,256]{2,1,0:T(8,128)(2,1)S(1)} %get-tuple-element.67), channel_id=1, source_target_pairs={{0,1},{1,2},{2,3},{3,4},{4,5},{5,6},{6,7},{7,8},{8,9},{9,10},{10,1... | collective-permute-start | bytes 1179656 | tf_op jit(solution)/shard_map/ppermute | solution.py:21
  64.7 19.2 %collective-permute-start.3 = (bf16[3,256,256]{2,1,0:T(8,128)(2,1)S(1)}, bf16[3,256,256]{2,1,0:T(8,128)(2,1)S(1)}, u32[]{:S(2)}, u32[]{:S(2)}) collective-permute-start(bf16[3,256,256]{2,1,0:T(8,128)(2,1)S(1)} %get-tuple-element.68), channel_id=1, source_target_pairs={{1,0},{2,1},{3,2},{4,3},{5,4},{6,5},{7,6},{8,7},{9,8},{10,9},{11,1... | collective-permute-start | bytes 1179656 | tf_op jit(solution)/shard_map/ppermute | solution.py:24
  81.0 8.9 %collective-permute-start.6 = (f32[307,256]{1,0:T(8,128)S(1)}, f32[307,256]{1,0:T(8,128)S(1)}, u32[]{:S(2)}, u32[]{:S(2)}) collective-permute-start(f32[307,256]{1,0:T(8,128)S(1)} %pad_maximum_fusion.1), channel_id=1, source_target_pairs={{0,4},{1,5},{2,6},{3,7},{4,0},{5,1},{6,2},{7,3},{8,12},{9,13},{10,... | collective-permute-start | bytes 943112 | tf_op jit(solution)/shard_map/ppermute | solution.py:52
  83.1 10.3 %copy-start.12 = (f32[1,1,256]{2,1,0:T(1,128)S(1)}, f32[1,1,256]{2,1,0:T(1,128)}, u32[]{:S(2)}) copy-start(f32[1,1,256]{2,1,0:T(1,128)} %copy-done.11) | copy-start | bytes 3076
  83.2 10.3 %copy-start.14 = (f32[1,1,256]{2,1,0:T(1,128)S(1)}, f32[1,1,256]{2,1,0:T(1,128)}, u32[]{:S(2)}) copy-start(f32[1,1,256]{2,1,0:T(1,128)} %copy-done.13) | copy-start | bytes 3076
  83.2 10.3 %copy-start.16 = (f32[1,1,256]{2,1,0:T(1,128)S(1)}, f32[1,1,256]{2,1,0:T(1,128)}, u32[]{:S(2)}) copy-start(f32[1,1,256]{2,1,0:T(1,128)} %copy-done.15) | copy-start | bytes 3076
  83.2 10.3 %copy-start.18 = (f32[1,1,256]{2,1,0:T(1,128)S(1)}, f32[1,1,256]{2,1,0:T(1,128)}, u32[]{:S(2)}) copy-start(f32[1,1,256]{2,1,0:T(1,128)} %copy-done.17) | copy-start | bytes 3076
  83.2 10.3 %copy-start.20 = (f32[1,1,256]{2,1,0:T(1,128)S(1)}, f32[1,1,256]{2,1,0:T(1,128)}, u32[]{:S(2)}) copy-start(f32[1,1,256]{2,1,0:T(1,128)} %copy-done.19) | copy-start | bytes 3076
  83.2 10.3 %copy-start.22 = (f32[1,1,256]{2,1,0:T(1,128)S(1)}, f32[1,1,256]{2,1,0:T(1,128)}, u32[]{:S(2)}) copy-start(f32[1,1,256]{2,1,0:T(1,128)} %copy-done.21) | copy-start | bytes 3076
  83.2 10.3 %copy-start.24 = (f32[1,1,256]{2,1,0:T(1,128)S(1)}, f32[1,1,256]{2,1,0:T(1,128)}, u32[]{:S(2)}) copy-start(f32[1,1,256]{2,1,0:T(1,128)} %copy-done.23) | copy-start | bytes 3076
  83.2 10.3 %copy-start.26 = (f32[1,1,256]{2,1,0:T(1,128)S(1)}, f32[1,1,256]{2,1,0:T(1,128)}, u32[]{:S(2)}) copy-start(f32[1,1,256]{2,1,0:T(1,128)} %copy-done.25) | copy-start | bytes 3076
  83.2 10.3 %copy-start.28 = (f32[1,1,256]{2,1,0:T(1,128)S(1)}, f32[1,1,256]{2,1,0:T(1,128)}, u32[]{:S(2)}) copy-start(f32[1,1,256]{2,1,0:T(1,128)} %copy-done.27) | copy-start | bytes 3076
  83.2 10.3 %copy-start.30 = (f32[1,1,256]{2,1,0:T(1,128)S(1)}, f32[1,1,256]{2,1,0:T(1,128)}, u32[]{:S(2)}) copy-start(f32[1,1,256]{2,1,0:T(1,128)} %copy-done.29) | copy-start | bytes 3076
  83.2 10.3 %copy-start.32 = (f32[1,1,256]{2,1,0:T(1,128)S(1)}, f32[1,1,256]{2,1,0:T(1,128)}, u32[]{:S(2)}) copy-start(f32[1,1,256]{2,1,0:T(1,128)} %copy-done.31) | copy-start | bytes 3076
  83.3 10.3 %copy-start.34 = (f32[1,1,256]{2,1,0:T(1,128)S(1)}, f32[1,1,256]{2,1,0:T(1,128)}, u32[]{:S(2)}) copy-start(f32[1,1,256]{2,1,0:T(1,128)} %copy-done.33) | copy-start | bytes 3076
  83.3 10.3 %copy-start.36 = (f32[1,1,256]{2,1,0:T(1,128)S(1)}, f32[1,1,256]{2,1,0:T(1,128)}, u32[]{:S(2)}) copy-start(f32[1,1,256]{2,1,0:T(1,128)} %copy-done.35) | copy-start | bytes 3076
  83.3 10.3 %copy-start.38 = (f32[1,1,256]{2,1,0:T(1,128)S(1)}, f32[1,1,256]{2,1,0:T(1,128)}, u32[]{:S(2)}) copy-start(f32[1,1,256]{2,1,0:T(1,128)} %copy-done.37) | copy-start | bytes 3076
  83.3 10.3 %copy-start.40 = (f32[1,1,256]{2,1,0:T(1,128)S(1)}, f32[1,1,256]{2,1,0:T(1,128)}, u32[]{:S(2)}) copy-start(f32[1,1,256]{2,1,0:T(1,128)} %copy-done.39) | copy-start | bytes 3076
  90.7 12.7 %collective-permute-start.7 = (f32[179,256]{1,0:T(8,128)}, f32[179,256]{1,0:T(8,128)}, u32[]{:S(2)}, u32[]{:S(2)}) collective-permute-start(f32[179,256]{1,0:T(8,128)} %pad_maximum_fusion.2), channel_id=1, source_target_pairs={{0,8},{1,9},{2,10},{3,11},{4,12},{5,13},{6,14},{7,15},{8,0},{9,1},... | collective-permute-start | bytes 549896 | tf_op jit(solution)/shard_map/ppermute | solution.py:52
  (43 other events, 279.0 us)

commit v5 on v3

--- a/solution.py
+++ b/solution.py
@@ -53,6 +53,18 @@
         parts = [k + g for k, g in zip(keeps, got)]
         whole = whole + got_whole
     return parts, whole
+
+
+def exchange_reduce(parts, whole, axis):
+    count = lax.axis_size(axis)
+    blocks = [p.reshape((count, p.shape[0] // count) + p.shape[1:]) for p in parts]
+    copies = jnp.broadcast_to(whole[None], (count,) + whole.shape)
+    arrived = [
+        lax.all_to_all(b, axis, split_axis=0, concat_axis=0, tiled=False)
+        for b in blocks + [copies]
+    ]
+    summed = [jnp.sum(a, axis=0) for a in arrived]
+    return summed[:-1], summed[-1]
 
 
 def gelu_value(inputs):
@@ -143,7 +155,7 @@
     ).astype(jnp.bfloat16)
     kernel_grad = kernel_terms(window, grad_tile.astype(jnp.float32), image_rows, TILE_COLS)
     packed = jnp.concatenate([kernel_grad, gain_grad[None], scale_grad[None]], axis=0)
-    (grad_w_in, grad_w_out), small_grads = halving_reduce([partial_in, partial_out], packed, "row")
+    (grad_w_in, grad_w_out), small_grads = exchange_reduce([partial_in, partial_out], packed, "row")
     grad_conv = lax.dynamic_update_slice_in_dim(
         jnp.zeros_like(image), grad_tile, first_col, axis=1
     )

time: 98.1 us -> 140 us (1.43)
  the two profiles are of different devices: /device:TPU:0 before, /device:TPU:15 now
where the time goes in v5:
time: 140 us; the launch traced here: 139 us
  waiting for transfers between devices  69.1 us (49%)
  starting transfers between devices  26.3 us (19%)
  other arithmetic  25.2 us (18%)
  matrix products  9.5 us (7%)
  local copies, waits for them, and re-layouts  6.06 us (4%)
  between operations  2.82 us (2%)
    all_to_all x3, waiting for transfers between devices, exchange_reduce(): lax.all_to_all(b, axis, split_axis=0, concat_axis=0, tiled=False)  40.3 us
    ppermute x2, waiting for transfers between devices, padded_2(): lax.ppermute(lax.slice_in_dim(block, block.shape[dim] - width, None, axis...  22 us
    all_to_all x3, starting transfers between devices, exchange_reduce(): lax.all_to_all(b, axis, split_axis=0, concat_axis=0, tiled=False)  15.4 us
    convert_element_type x1, other arithmetic, shards(): (cotangent.astype(jnp.float32) + conv_back).astype(jnp.bfloat16)  9.58 us
    ppermute x2, starting transfers between devices, padded_2(): lax.ppermute(lax.slice_in_dim(block, block.shape[dim] - width, None, axis...  7.08 us
    ppermute x2, waiting for transfers between devices, padded_2(): lax.ppermute(lax.slice_in_dim(block, 0, width, axis=dim), axis, backward)  6.92 us
    reduce_sum x3, other arithmetic, exchange_reduce(): summed = [jnp.sum(a, axis=0) for a in arrived]  5.69 us
    reduce_sum x1, other arithmetic, shards(): centre = jnp.mean(filtered, axis=-1, keepdims=True)  4.59 us
  transfers between devices with their start and end apart: 7, of which 6 were waited for; matrix products, arithmetic and copies ran while one was open for 16% of the time, Pallas kernels for 0%

profile of v5, /device:TPU:15, one launch (start us, length us, event | category | flops | bytes accessed | tf_op | source)
XLA Modules:
  0.0 139.1 jit_solution(11437909810341114204)
XLA Ops:
  0.6 0.0 copy-start
  0.7 1.1 copy.26
  1.8 0.1 fusion.145
  1.8 3.7 %collective-permute-start = (bf16[3,256,256]{2,1,0:T(8,128)(2,1)S(1)}, bf16[3,256,256]{2,1,0:T(8,128)(2,1)S(1)}, u32[]{:S(2)}, u32[]{:S(2)}) collective-permute-start(bf16[3,256,256]{2,1,0:T(8,128)(2,1)S(1)} %get-tuple-element.66), channel_id=1, source_target_pairs={{0,1},{1,2},{2,3},{3,4},{4,5},{5,6},{6,7},{7,8},{8,9},{9,10},{10,1... | collective-permute-start | bytes 1179656 | tf_op jit(solution)/shard_map/ppermute | solution.py:21
  5.6 1.9 %collective-permute-start.1 = (bf16[3,256,256]{2,1,0:T(8,128)(2,1)S(1)}, bf16[3,256,256]{2,1,0:T(8,128)(2,1)S(1)}, u32[]{:S(2)}, u32[]{:S(2)}) collective-permute-start(bf16[3,256,256]{2,1,0:T(8,128)(2,1)S(1)} %get-tuple-element.65), channel_id=1, source_target_pairs={{1,0},{2,1},{3,2},{4,3},{5,4},{6,5},{7,6},{8,7},{9,8},{10,9},{11,1... | collective-permute-start | bytes 1179656 | tf_op jit(solution)/shard_map/ppermute | solution.py:24
  7.5 0.7 bitcast_reduce_fusion
  9.1 0.6 fusion.147
  9.9 0.4 collective-permute-done
  10.3 5.3 %collective-permute-done.1 = bf16[3,256,256]{2,1,0:T(8,128)(2,1)S(1)} collective-permute-done((bf16[3,256,256]{2,1,0:T(8,128)(2,1)S(1)}, bf16[3,256,256]{2,1,0:T(8,128)(2,1)S(1)}, u32[]{:S(2)}, u32[]{:S(2)}) %collective-permute-start.1) | collective-permute-done | bytes 393248 | tf_op jit(solution)/shard_map/ppermute | solution.py:24
  15.6 0.3 fusion.84
  15.9 0.0 copy-start.88
  15.9 4.6 %fusion.143 = (f32[4,128]{1,0:T(4,128)S(1)}, f32[4,128,256]{2,1,0:T(8,128)S(1)}) fusion(f32[256]{0:T(256)S(1)} %bitcast.200, f32[10,134,256]{2,1,0:T(8,128)S(1)} %fusion.84, f32[256]{0:T(256)S(1)} %bitcast.202, f32[256]{0:T(256)S(1)} %bitcast.146, f32[256]{0:T(256)S(1)} %bitcast.148, f32[256]{0:T(256)S(1)} %bitcast.150, f32[256]{0:T(256)S(1)} %bitcast.152, ...), kind=kLoop, calls=%fused_computation.239 | loop fusion | flops 12844544 | bytes 26266624 | tf_op jit(solution)/shard_map/reduce_sum | solution.py:118
  20.9 0.2 multiply_reduce_fusion.3
  21.2 0.2 multiply_convert_fusion.3
  21.4 0.0 copy-start.7
  21.4 0.0 copy-start.5
  21.4 0.0 copy-start.8
  21.4 0.0 copy-start.89
  21.5 1.8 %fusion.11 = (bf16[1024,512]{0,1:T(8,128)(2,1)}, f32[512,1024]{1,0:T(8,128)S(1)}) fusion(bf16[512,256]{1,0:T(8,128)(2,1)S(1)} %bitcast.142, bf16[256,1024]{1,0:T(8,128)(2,1)S(1)} %copy-done), kind=kOutput, calls=%fused_computation.63 | convolution fusion | flops 273154048 | bytes 3932160 | tf_op jit(solution)/shard_map/dot_general | solution.py:128
  23.3 1.6 %fusion.88 = (f32[256]{0:T(256)S(1)}, bf16[4,128,256]{2,1,0:T(8,128)(2,1)S(1)}, f32[512,256]{1,0:T(8,128)}) fusion(bf16[4,256,256]{2,1,0:T(8,128)(2,1)S(1)} %copy-done.5, s32[]{:T(128)S(6)} %select_n.8, f32[256]{0:T(256)S(1)} %copy-done.89, bf16[1024,256]{1,0:T(8,128)(2,1)S(1)} %copy-done.8, f32[512,1024]{1,0:T(8,128)S(1)} %get-tuple-element.120), kind=kOutput, calls=%fused_computation.169 | convolution fusion | flops 273809152 | bytes 3672068 | tf_op jit(solution)/shard_map/dot_general | solution.py:130
  24.9 1.4 %fusion.6 = bf16[512,1024]{1,0:T(8,128)(2,1)S(1)} fusion(f32[512,1024]{1,0:T(8,128)S(1)} %get-tuple-element.120, bf16[512,256]{1,0:T(8,128)(2,1)S(1)} %bitcast.139, bf16[1024,256]{1,0:T(8,128)(2,1)S(1)} %copy-done.8), kind=kOutput, calls=%fused_computation.58 | convolution fusion | flops 278396928 | bytes 3932160 | tf_op jit(solution)/shard_map/dot_general | solution.py:131
  26.3 0.6 multiply_reduce_fusion.2
  26.9 0.3 multiply_reduce_fusion
  27.3 1.5 %fusion.136 = (f32[256]{0:T(256)S(1)}, f32[256]{0:T(256)S(1)}, f32[256]{0:T(256)S(1)}, f32[256]{0:T(256)S(1)}, f32[256]{0:T(256)S(1)}, /*index=5*/f32[256]{0:T(2...) fusion(f32[10,134,256]{2,1,0:T(8,128)S(1)} %fusion.84, ...), kind=kLoop, calls=%fused_computation.217 | loop fusion | flops 5893632 | bytes 10775552 | tf_op jit(solution)/shard_map/reduce_sum | solution.py:99
  28.8 1.0 fusion.137
  29.8 0.7 fusion.135
  30.6 0.2 concatenate.11
  30.8 1.0 broadcast_in_dim.11
  31.7 5.5 %all-to-all-start.2 = ((f32[16,51,256]{2,1,0:T(8,128)}), f32[16,51,256]{2,1,0:T(8,128)S(1)}, u32[]{:S(2)}, u32[]{:S(2)}) async-start(f32[16,51,256]{2,1,0:T(8,128)} %broadcast_in_dim.11), calls=%async_computation.2 | async-start | bytes 1835008 | tf_op jit(solution)/shard_map/all_to_all | solution.py:63
  37.3 1.5 %copy.20 = bf16[1024,512]{1,0:T(8,128)(2,1)S(1)} copy(bf16[1024,512]{0,1:T(8,128)(2,1)} %get-tuple-element.119) | data formatting | bytes 2097152 | tf_op jit(solution)/shard_map/convert_element_type | solution.py:129
  38.8 1.4 %fusion.149 = f32[16,64,256]{2,1,0:T(8,128)} fusion(bf16[16,64,512]{2,1,0:T(8,128)(2,1)S(1)} %bitcast.137, bf16[512,256,1]{1,0,2:T(8,128)(2,1)S(1)} %bitcast.140), kind=kOutput, calls=%fused_computation.245 | convolution fusion | flops 268435456 | bytes 2359296 | tf_op jit(solution)/shard_map/dot_general | solution.py:137
  40.2 19.1 %all-to-all-done.2 = f32[16,51,256]{2,1,0:T(8,128)S(1)} async-done(((f32[16,51,256]{2,1,0:T(8,128)}), f32[16,51,256]{2,1,0:T(8,128)S(1)}, u32[]{:S(2)}, u32[]{:S(2)}) %all-to-all-start.2) | async-done | bytes 835616 | tf_op jit(solution)/shard_map/all_to_all | solution.py:63
  59.3 5.0 %all-to-all-start.1 = ((f32[16,64,256]{2,1,0:T(8,128)}), f32[16,64,256]{2,1,0:T(8,128)S(1)}, u32[]{:S(2)}, u32[]{:S(2)}) async-start(f32[16,64,256]{2,1,0:T(8,128)} %fusion.149), calls=%async_computation.1 | async-start | bytes 2097152 | tf_op jit(solution)/shard_map/all_to_all | solution.py:63
  64.3 1.1 copy.19
  65.4 2.7 %fusion.63 = f32[16,16,1024]{2,1,0:T(8,128)} fusion(bf16[16,16,512]{2,1,0:T(8,128)(2,1)S(1)} %bitcast.141, bf16[512,1024]{1,0:T(8,128)(2,1)} %copy-done.6), kind=kOutput, calls=%fused_computation.129 | convolution fusion | flops 268435456 | bytes 2359296 | tf_op jit(solution)/shard_map/dot_general | solution.py:134
  68.0 21.1 %all-to-all-done.1 = f32[16,64,256]{2,1,0:T(8,128)S(1)} async-done(((f32[16,64,256]{2,1,0:T(8,128)}), f32[16,64,256]{2,1,0:T(8,128)S(1)}, u32[]{:S(2)}, u32[]{:S(2)}) %all-to-all-start.1) | async-done | bytes 1048608 | tf_op jit(solution)/shard_map/all_to_all | solution.py:63
  89.1 4.9 %all-to-all-start = ((f32[16,16,1024]{2,1,0:T(8,128)}), f32[16,16,1024]{2,1,0:T(8,128)}, u32[]{:S(2)}, u32[]{:S(2)}) async-start(f32[16,16,1024]{2,1,0:T(8,128)} %fusion.63), calls=%async_computation | async-start | bytes 2097152 | tf_op jit(solution)/shard_map/all_to_all | solution.py:63
  94.2 0.1 fusion.144
  94.2 3.3 %collective-permute-start.2 = (bf16[3,256,256]{2,1,0:T(8,128)(2,1)S(1)}, bf16[3,256,256]{2,1,0:T(8,128)(2,1)S(1)}, u32[]{:S(2)}, u32[]{:S(2)}) collective-permute-start(bf16[3,256,256]{2,1,0:T(8,128)(2,1)S(1)} %get-tuple-element.63), channel_id=1, source_target_pairs={{0,1},{1,2},{2,3},{3,4},{4,5},{5,6},{6,7},{7,8},{8,9},{9,10},{10,1... | collective-permute-start | bytes 1179656 | tf_op jit(solution)/shard_map/ppermute | solution.py:21
  97.6 1.9 %collective-permute-start.3 = (bf16[3,256,256]{2,1,0:T(8,128)(2,1)S(1)}, bf16[3,256,256]{2,1,0:T(8,128)(2,1)S(1)}, u32[]{:S(2)}, u32[]{:S(2)}) collective-permute-start(bf16[3,256,256]{2,1,0:T(8,128)(2,1)S(1)} %get-tuple-element.64), channel_id=1, source_target_pairs={{1,0},{2,1},{3,2},{4,3},{5,4},{6,5},{7,6},{8,7},{9,8},{10,9},{11,1... | collective-permute-start | bytes 1179656 | tf_op jit(solution)/shard_map/ppermute | solution.py:24
  99.5 0.1 fusion.138
  100.0 21.6 %collective-permute-done.2 = bf16[3,256,256]{2,1,0:T(8,128)(2,1)S(1)} collective-permute-done((bf16[3,256,256]{2,1,0:T(8,128)(2,1)S(1)}, bf16[3,256,256]{2,1,0:T(8,128)(2,1)S(1)}, u32[]{:S(2)}, u32[]{:S(2)}) %collective-permute-start.2) | collective-permute-done | bytes 393248 | tf_op jit(solution)/shard_map/ppermute | solution.py:21
  121.6 1.6 %collective-permute-done.3 = bf16[3,256,256]{2,1,0:T(8,128)(2,1)S(1)} collective-permute-done((bf16[3,256,256]{2,1,0:T(8,128)(2,1)S(1)}, bf16[3,256,256]{2,1,0:T(8,128)(2,1)S(1)}, u32[]{:S(2)}, u32[]{:S(2)}) %collective-permute-start.3) | collective-permute-done | bytes 393248 | tf_op jit(solution)/shard_map/ppermute | solution.py:24
  123.2 0.2 maximum_convert_fusion
  123.8 9.6 %fusion.20 = bf16[4,256,256]{2,1,0:T(8,128)(2,1)} fusion(f32[10,256,256]{2,1,0:T(8,128)S(1)} %maximum_convert_fusion, bf16[4,256,256]{2,1,0:T(8,128)(2,1)} %param.15, f32[256]{0:T(256)S(1)} %bitcast.145, f32[256]{0:T(256)S(1)} %bitcast.205, f32[256]{0:T(256)S(1)} %bitcast.183, f32[256]{0:T(256)S(1)} %bitcast.199, f32[256]{0:T(256)S(1)} %bitcast.197, ...), kind=kLoop, calls=%fused_computation.80 | loop fusion | flops 26214400 | bytes 11060224 | tf_op jit(solution)/shard_map/convert_element_type | solution.py:165
  133.4 1.9 %reduce_sum.579 = f32[51,256]{1,0:T(8,128)} reduce(f32[16,51,256]{2,1,0:T(8,128)} %copy-done.3, f32[]{:T(128)} %constant.13.clone.1), dimensions={0}, to_apply=%region_58.59 | reduce | flops 195840 | bytes 887812 | tf_op jit(solution)/shard_map/reduce_sum | solution.py:66
  135.2 1.9 %reduce_sum.527 = f32[64,256]{1,0:T(8,128)} reduce(f32[16,64,256]{2,1,0:T(8,128)} %copy-done.2, f32[]{:T(128)} %constant.13.clone.1), dimensions={0}, to_apply=%region_6.7 | reduce | flops 245760 | bytes 1114116 | tf_op jit(solution)/shard_map/reduce_sum | solution.py:66
  137.1 1.9 %reduce_sum.526 = f32[16,1024]{1,0:T(8,128)} reduce(f32[16,16,1024]{2,1,0:T(8,128)} %all-to-all-done, f32[]{:T(128)} %constant.13.clone.1), dimensions={0}, to_apply=%region_5.6 | reduce | flops 245760 | bytes 1114116 | tf_op jit(solution)/shard_map/reduce_sum | solution.py:66
  (187 shorter events, 0.5 us)
Async XLA Ops:
  1.8 8.4 %collective-permute-start = (bf16[3,256,256]{2,1,0:T(8,128)(2,1)S(1)}, bf16[3,256,256]{2,1,0:T(8,128)(2,1)S(1)}, u32[]{:S(2)}, u32[]{:S(2)}) collective-permute-start(bf16[3,256,256]{2,1,0:T(8,128)(2,1)S(1)} %get-tuple-element.66), channel_id=1, source_target_pairs={{0,1},{1,2},{2,3},{3,4},{4,5},{5,6},{6,7},{7,8},{8,9},{9,10},{10,1... | collective-permute-start | bytes 1179656 | tf_op jit(solution)/shard_map/ppermute | solution.py:21
  5.6 10.0 %collective-permute-start.1 = (bf16[3,256,256]{2,1,0:T(8,128)(2,1)S(1)}, bf16[3,256,256]{2,1,0:T(8,128)(2,1)S(1)}, u32[]{:S(2)}, u32[]{:S(2)}) collective-permute-start(bf16[3,256,256]{2,1,0:T(8,128)(2,1)S(1)} %get-tuple-element.65), channel_id=1, source_target_pairs={{1,0},{2,1},{3,2},{4,3},{5,4},{6,5},{7,6},{8,7},{9,8},{10,9},{11,1... | collective-permute-start | bytes 1179656 | tf_op jit(solution)/shard_map/ppermute | solution.py:24
  31.7 27.6 %all-to-all-start.2 = ((f32[16,51,256]{2,1,0:T(8,128)}), f32[16,51,256]{2,1,0:T(8,128)S(1)}, u32[]{:S(2)}, u32[]{:S(2)}) async-start(f32[16,51,256]{2,1,0:T(8,128)} %broadcast_in_dim.11), calls=%async_computation.2 | async-start | bytes 1835008 | tf_op jit(solution)/shard_map/all_to_all | solution.py:63
  59.3 62.3 %copy-start.3 = (f32[16,51,256]{2,1,0:T(8,128)}, f32[16,51,256]{2,1,0:T(8,128)S(1)}, u32[]{:S(2)}) copy-start(f32[16,51,256]{2,1,0:T(8,128)S(1)} %all-to-all-done.2) | copy-start | bytes 2506756
  59.3 29.8 %all-to-all-start.1 = ((f32[16,64,256]{2,1,0:T(8,128)}), f32[16,64,256]{2,1,0:T(8,128)S(1)}, u32[]{:S(2)}, u32[]{:S(2)}) async-start(f32[16,64,256]{2,1,0:T(8,128)} %fusion.149), calls=%async_computation.1 | async-start | bytes 2097152 | tf_op jit(solution)/shard_map/all_to_all | solution.py:63
  68.0 31.5 %copy-start.90 = (f32[256]{0:T(256)S(1)}, f32[256]{0:T(256)}, u32[]{:S(2)}) copy-start(f32[256]{0:T(256)} %param.14) | copy-start | bytes 3076
  89.1 32.4 %copy-start.2 = (f32[16,64,256]{2,1,0:T(8,128)}, f32[16,64,256]{2,1,0:T(8,128)S(1)}, u32[]{:S(2)}) copy-start(f32[16,64,256]{2,1,0:T(8,128)S(1)} %all-to-all-done.1) | copy-start | bytes 3145732
  89.1 48.0 %all-to-all-start = ((f32[16,16,1024]{2,1,0:T(8,128)}), f32[16,16,1024]{2,1,0:T(8,128)}, u32[]{:S(2)}, u32[]{:S(2)}) async-start(f32[16,16,1024]{2,1,0:T(8,128)} %fusion.63), calls=%async_computation | async-start | bytes 2097152 | tf_op jit(solution)/shard_map/all_to_all | solution.py:63
  94.2 27.3 %collective-permute-start.2 = (bf16[3,256,256]{2,1,0:T(8,128)(2,1)S(1)}, bf16[3,256,256]{2,1,0:T(8,128)(2,1)S(1)}, u32[]{:S(2)}, u32[]{:S(2)}) collective-permute-start(bf16[3,256,256]{2,1,0:T(8,128)(2,1)S(1)} %get-tuple-element.63), channel_id=1, source_target_pairs={{0,1},{1,2},{2,3},{3,4},{4,5},{5,6},{6,7},{7,8},{8,9},{9,10},{10,1... | collective-permute-start | bytes 1179656 | tf_op jit(solution)/shard_map/ppermute | solution.py:21
  97.6 25.6 %collective-permute-start.3 = (bf16[3,256,256]{2,1,0:T(8,128)(2,1)S(1)}, bf16[3,256,256]{2,1,0:T(8,128)(2,1)S(1)}, u32[]{:S(2)}, u32[]{:S(2)}) collective-permute-start(bf16[3,256,256]{2,1,0:T(8,128)(2,1)S(1)} %get-tuple-element.64), channel_id=1, source_target_pairs={{1,0},{2,1},{3,2},{4,3},{5,4},{6,5},{7,6},{8,7},{9,8},{10,9},{11,1... | collective-permute-start | bytes 1179656 | tf_op jit(solution)/shard_map/ppermute | solution.py:24
  99.6 23.8 %copy-start.11 = (f32[1,1,256]{2,1,0:T(1,128)S(1)}, f32[1,1,256]{2,1,0:T(1,128)}, u32[]{:S(2)}) copy-start(f32[1,1,256]{2,1,0:T(1,128)} %copy-done.10) | copy-start | bytes 3076
  99.6 23.8 %copy-start.13 = (f32[1,1,256]{2,1,0:T(1,128)S(1)}, f32[1,1,256]{2,1,0:T(1,128)}, u32[]{:S(2)}) copy-start(f32[1,1,256]{2,1,0:T(1,128)} %copy-done.12) | copy-start | bytes 3076
  99.6 23.8 %copy-start.15 = (f32[1,1,256]{2,1,0:T(1,128)S(1)}, f32[1,1,256]{2,1,0:T(1,128)}, u32[]{:S(2)}) copy-start(f32[1,1,256]{2,1,0:T(1,128)} %copy-done.14) | copy-start | bytes 3076
  99.6 23.8 %copy-start.17 = (f32[1,1,256]{2,1,0:T(1,128)S(1)}, f32[1,1,256]{2,1,0:T(1,128)}, u32[]{:S(2)}) copy-start(f32[1,1,256]{2,1,0:T(1,128)} %copy-done.16) | copy-start | bytes 3076
  99.7 23.8 %copy-start.19 = (f32[1,1,256]{2,1,0:T(1,128)S(1)}, f32[1,1,256]{2,1,0:T(1,128)}, u32[]{:S(2)}) copy-start(f32[1,1,256]{2,1,0:T(1,128)} %copy-done.18) | copy-start | bytes 3076
  99.7 23.8 %copy-start.21 = (f32[1,1,256]{2,1,0:T(1,128)S(1)}, f32[1,1,256]{2,1,0:T(1,128)}, u32[]{:S(2)}) copy-start(f32[1,1,256]{2,1,0:T(1,128)} %copy-done.20) | copy-start | bytes 3076
  99.7 23.8 %copy-start.23 = (f32[1,1,256]{2,1,0:T(1,128)S(1)}, f32[1,1,256]{2,1,0:T(1,128)}, u32[]{:S(2)}) copy-start(f32[1,1,256]{2,1,0:T(1,128)} %copy-done.22) | copy-start | bytes 3076
  99.7 23.8 %copy-start.25 = (f32[1,1,256]{2,1,0:T(1,128)S(1)}, f32[1,1,256]{2,1,0:T(1,128)}, u32[]{:S(2)}) copy-start(f32[1,1,256]{2,1,0:T(1,128)} %copy-done.24) | copy-start | bytes 3076
  99.7 23.8 %copy-start.27 = (f32[1,1,256]{2,1,0:T(1,128)S(1)}, f32[1,1,256]{2,1,0:T(1,128)}, u32[]{:S(2)}) copy-start(f32[1,1,256]{2,1,0:T(1,128)} %copy-done.26) | copy-start | bytes 3076
  99.7 23.8 %copy-start.29 = (f32[1,1,256]{2,1,0:T(1,128)S(1)}, f32[1,1,256]{2,1,0:T(1,128)}, u32[]{:S(2)}) copy-start(f32[1,1,256]{2,1,0:T(1,128)} %copy-done.28) | copy-start | bytes 3076
  99.7 23.8 %copy-start.31 = (f32[1,1,256]{2,1,0:T(1,128)S(1)}, f32[1,1,256]{2,1,0:T(1,128)}, u32[]{:S(2)}) copy-start(f32[1,1,256]{2,1,0:T(1,128)} %copy-done.30) | copy-start | bytes 3076
  99.7 23.8 %copy-start.33 = (f32[1,1,256]{2,1,0:T(1,128)S(1)}, f32[1,1,256]{2,1,0:T(1,128)}, u32[]{:S(2)}) copy-start(f32[1,1,256]{2,1,0:T(1,128)} %copy-done.32) | copy-start | bytes 3076
  99.7 23.8 %copy-start.35 = (f32[1,1,256]{2,1,0:T(1,128)S(1)}, f32[1,1,256]{2,1,0:T(1,128)}, u32[]{:S(2)}) copy-start(f32[1,1,256]{2,1,0:T(1,128)} %copy-done.34) | copy-start | bytes 3076
  99.7 23.8 %copy-start.37 = (f32[1,1,256]{2,1,0:T(1,128)S(1)}, f32[1,1,256]{2,1,0:T(1,128)}, u32[]{:S(2)}) copy-start(f32[1,1,256]{2,1,0:T(1,128)} %copy-done.36) | copy-start | bytes 3076
  99.8 23.8 %copy-start.39 = (f32[1,1,256]{2,1,0:T(1,128)S(1)}, f32[1,1,256]{2,1,0:T(1,128)}, u32[]{:S(2)}) copy-start(f32[1,1,256]{2,1,0:T(1,128)} %copy-done.38) | copy-start | bytes 3076
  99.8 23.8 %copy-start.41 = (f32[1,1,256]{2,1,0:T(1,128)S(1)}, f32[1,1,256]{2,1,0:T(1,128)}, u32[]{:S(2)}) copy-start(f32[1,1,256]{2,1,0:T(1,128)} %copy-done.40) | copy-start | bytes 3076
  99.8 23.8 %copy-start.43 = (f32[1,1,256]{2,1,0:T(1,128)S(1)}, f32[1,1,256]{2,1,0:T(1,128)}, u32[]{:S(2)}) copy-start(f32[1,1,256]{2,1,0:T(1,128)} %copy-done.42) | copy-start | bytes 3076
  99.8 23.8 %copy-start.45 = (f32[1,1,256]{2,1,0:T(1,128)S(1)}, f32[1,1,256]{2,1,0:T(1,128)}, u32[]{:S(2)}) copy-start(f32[1,1,256]{2,1,0:T(1,128)} %copy-done.44) | copy-start | bytes 3076
  99.8 23.8 %copy-start.47 = (f32[1,1,256]{2,1,0:T(1,128)S(1)}, f32[1,1,256]{2,1,0:T(1,128)}, u32[]{:S(2)}) copy-start(f32[1,1,256]{2,1,0:T(1,128)} %copy-done.46) | copy-start | bytes 3076
  99.8 23.8 %copy-start.49 = (f32[1,1,256]{2,1,0:T(1,128)S(1)}, f32[1,1,256]{2,1,0:T(1,128)}, u32[]{:S(2)}) copy-start(f32[1,1,256]{2,1,0:T(1,128)} %copy-done.48) | copy-start | bytes 3076
  99.8 23.8 %copy-start.51 = (f32[1,1,256]{2,1,0:T(1,128)S(1)}, f32[1,1,256]{2,1,0:T(1,128)}, u32[]{:S(2)}) copy-start(f32[1,1,256]{2,1,0:T(1,128)} %copy-done.50) | copy-start | bytes 3076
  99.8 23.8 %copy-start.53 = (f32[1,1,256]{2,1,0:T(1,128)S(1)}, f32[1,1,256]{2,1,0:T(1,128)}, u32[]{:S(2)}) copy-start(f32[1,1,256]{2,1,0:T(1,128)} %copy-done.52) | copy-start | bytes 3076
  99.8 23.8 %copy-start.55 = (f32[1,1,256]{2,1,0:T(1,128)S(1)}, f32[1,1,256]{2,1,0:T(1,128)}, u32[]{:S(2)}) copy-start(f32[1,1,256]{2,1,0:T(1,128)} %copy-done.54) | copy-start | bytes 3076
  99.8 23.8 %copy-start.57 = (f32[1,1,256]{2,1,0:T(1,128)S(1)}, f32[1,1,256]{2,1,0:T(1,128)}, u32[]{:S(2)}) copy-start(f32[1,1,256]{2,1,0:T(1,128)} %copy-done.56) | copy-start | bytes 3076
  99.9 23.8 %copy-start.59 = (f32[1,1,256]{2,1,0:T(1,128)S(1)}, f32[1,1,256]{2,1,0:T(1,128)}, u32[]{:S(2)}) copy-start(f32[1,1,256]{2,1,0:T(1,128)} %copy-done.58) | copy-start | bytes 3076
  99.9 23.8 %copy-start.61 = (f32[1,1,256]{2,1,0:T(1,128)S(1)}, f32[1,1,256]{2,1,0:T(1,128)}, u32[]{:S(2)}) copy-start(f32[1,1,256]{2,1,0:T(1,128)} %copy-done.60) | copy-start | bytes 3076
  99.9 23.8 %copy-start.63 = (f32[1,1,256]{2,1,0:T(1,128)S(1)}, f32[1,1,256]{2,1,0:T(1,128)}, u32[]{:S(2)}) copy-start(f32[1,1,256]{2,1,0:T(1,128)} %copy-done.62) | copy-start | bytes 3076
  99.9 23.8 %copy-start.65 = (f32[1,1,256]{2,1,0:T(1,128)S(1)}, f32[1,1,256]{2,1,0:T(1,128)}, u32[]{:S(2)}) copy-start(f32[1,1,256]{2,1,0:T(1,128)} %copy-done.64) | copy-start | bytes 3076
  99.9 23.8 %copy-start.67 = (f32[1,1,256]{2,1,0:T(1,128)S(1)}, f32[1,1,256]{2,1,0:T(1,128)}, u32[]{:S(2)}) copy-start(f32[1,1,256]{2,1,0:T(1,128)} %copy-done.66) | copy-start | bytes 3076
  99.9 23.8 %copy-start.69 = (f32[1,1,256]{2,1,0:T(1,128)S(1)}, f32[1,1,256]{2,1,0:T(1,128)}, u32[]{:S(2)}) copy-start(f32[1,1,256]{2,1,0:T(1,128)} %copy-done.68) | copy-start | bytes 3076
  99.9 23.8 %copy-start.71 = (f32[1,1,256]{2,1,0:T(1,128)S(1)}, f32[1,1,256]{2,1,0:T(1,128)}, u32[]{:S(2)}) copy-start(f32[1,1,256]{2,1,0:T(1,128)} %copy-done.70) | copy-start | bytes 3076
  99.9 23.8 %copy-start.73 = (f32[1,1,256]{2,1,0:T(1,128)S(1)}, f32[1,1,256]{2,1,0:T(1,128)}, u32[]{:S(2)}) copy-start(f32[1,1,256]{2,1,0:T(1,128)} %copy-done.72) | copy-start | bytes 3076
  99.9 23.8 %copy-start.75 = (f32[1,1,256]{2,1,0:T(1,128)S(1)}, f32[1,1,256]{2,1,0:T(1,128)}, u32[]{:S(2)}) copy-start(f32[1,1,256]{2,1,0:T(1,128)} %copy-done.74) | copy-start | bytes 3076
  99.9 23.8 %copy-start.77 = (f32[1,1,256]{2,1,0:T(1,128)S(1)}, f32[1,1,256]{2,1,0:T(1,128)}, u32[]{:S(2)}) copy-start(f32[1,1,256]{2,1,0:T(1,128)} %copy-done.76) | copy-start | bytes 3076
  100.0 23.8 %copy-start.79 = (f32[1,1,256]{2,1,0:T(1,128)S(1)}, f32[1,1,256]{2,1,0:T(1,128)}, u32[]{:S(2)}) copy-start(f32[1,1,256]{2,1,0:T(1,128)} %copy-done.78) | copy-start | bytes 3076
  100.0 23.8 %copy-start.81 = (f32[1,1,256]{2,1,0:T(1,128)S(1)}, f32[1,1,256]{2,1,0:T(1,128)}, u32[]{:S(2)}) copy-start(f32[1,1,256]{2,1,0:T(1,128)} %copy-done.80) | copy-start | bytes 3076
  100.0 23.8 %copy-start.83 = (f32[1,1,256]{2,1,0:T(1,128)S(1)}, f32[1,1,256]{2,1,0:T(1,128)}, u32[]{:S(2)}) copy-start(f32[1,1,256]{2,1,0:T(1,128)} %copy-done.82) | copy-start | bytes 3076
  100.0 23.8 %copy-start.85 = (f32[1,1,256]{2,1,0:T(1,128)S(1)}, f32[1,1,256]{2,1,0:T(1,128)}, u32[]{:S(2)}) copy-start(f32[1,1,256]{2,1,0:T(1,128)} %copy-done.84) | copy-start | bytes 3076
  (51 other events, 548.6 us)

commit v6 on v3

--- a/solution.py
+++ b/solution.py
@@ -26,33 +26,46 @@
     return block
 
 
-def bit_reversed(values, count, steps):
-    rest = values.shape[1:]
-    values = values.reshape((2,) * steps + (values.shape[0] // count,) + rest)
-    order = tuple(reversed(range(steps))) + tuple(range(steps, values.ndim))
-    return values.transpose(order).reshape((-1,) + rest)
-
-
-def halving_reduce(parts, whole, axis):
+def bit_reversed(values, count, steps, axis):
+    shape = values.shape
+    values = values.reshape(shape[:axis] + (2,) * steps + (shape[axis] // count,) + shape[axis + 1 :])
+    order = (
+        tuple(range(axis))
+        + tuple(axis + steps - 1 - i for i in range(steps))
+        + tuple(range(axis + steps, values.ndim))
+    )
+    return values.transpose(order).reshape(shape)
+
+
+def halving_reduce(quartered, rows, whole, axis):
     count = lax.axis_size(axis)
     steps = count.bit_length() - 1
     if (1 << steps) != count:
-        owned = [lax.psum_scatter(p, axis, scatter_dimension=0, tiled=True) for p in parts]
-        return owned, lax.psum(whole, axis)
+        return (
+            lax.psum_scatter(quartered, axis, scatter_dimension=1, tiled=True),
+            lax.psum_scatter(rows, axis, scatter_dimension=0, tiled=True),
+            lax.psum(whole, axis),
+        )
     me = lax.axis_index(axis)
-    parts = [bit_reversed(p, count, steps) for p in parts]
+    quartered = bit_reversed(quartered, count, steps, 1)
+    rows = bit_reversed(rows, count, steps, 0)
+    quarters, width = quartered.shape[0], quartered.shape[2]
     for step in range(steps):
         bit = (me >> step) & 1
         pairs = [(i, i ^ (1 << step)) for i in range(count)]
-        keeps, gives = [], []
-        for p in parts:
-            half = p.shape[0] // 2
-            keeps.append(lax.dynamic_slice_in_dim(p, bit * half, half, axis=0))
-            gives.append(lax.dynamic_slice_in_dim(p, (1 - bit) * half, half, axis=0))
-        got, got_whole = lax.ppermute((gives, whole), axis, pairs)
-        parts = [k + g for k, g in zip(keeps, got)]
-        whole = whole + got_whole
-    return parts, whole
+        half_q = quartered.shape[1] // 2
+        half_r = rows.shape[0] // 2
+        keep_q = lax.dynamic_slice_in_dim(quartered, bit * half_q, half_q, axis=1)
+        give_q = lax.dynamic_slice_in_dim(quartered, (1 - bit) * half_q, half_q, axis=1)
+        keep_r = lax.dynamic_slice_in_dim(rows, bit * half_r, half_r, axis=0)
+        give_r = lax.dynamic_slice_in_dim(rows, (1 - bit) * half_r, half_r, axis=0)
+        sent = jnp.concatenate([give_q.reshape(-1, width), give_r, whole], axis=0)
+        got = lax.ppermute(sent, axis, pairs)
+        cut_q = quarters * half_q
+        quartered = keep_q + got[:cut_q].reshape(quarters, half_q, width)
+        rows = keep_r + got[cut_q : cut_q + half_r]
+        whole = whole + got[cut_q + half_r :]
+    return quartered, rows, whole
 
 
 def gelu_value(inputs):
@@ -119,8 +132,17 @@
     grad_act = jnp.dot(grad_flat, w_out.T, preferred_element_type=jnp.float32)
     pre_flat = (grad_act * gelu_slope(pre_act)).astype(jnp.bfloat16)
     grad_norm = jnp.dot(pre_flat, w_in.T, preferred_element_type=jnp.float32)
-    partial_in = lax.dot_general(
-        normed_flat, pre_flat, (((0,), (0,)), ((), ())), preferred_element_type=jnp.float32
+    quarters = hidden // channels
+    partial_in = jnp.stack(
+        [
+            lax.dot_general(
+                normed_flat,
+                pre_flat[:, q * channels : (q + 1) * channels],
+                (((0,), (0,)), ((), ())),
+                preferred_element_type=jnp.float32,
+            )
+            for q in range(quarters)
+        ]
     )
     partial_out = lax.dot_general(
         act_flat, grad_flat, (((0,), (0,)), ((), ())), preferred_element_type=jnp.float32
@@ -143,7 +165,8 @@
     ).astype(jnp.bfloat16)
     kernel_grad = kernel_terms(window, grad_tile.astype(jnp.float32), image_rows, TILE_COLS)
     packed = jnp.concatenate([kernel_grad, gain_grad[None], scale_grad[None]], axis=0)
-    (grad_w_in, grad_w_out), small_grads = halving_reduce([partial_in, partial_out], packed, "row")
+    owned_in, grad_w_out, small_grads = halving_reduce(partial_in, partial_out, packed, "row")
+    grad_w_in = owned_in.transpose(1, 0, 2).reshape(-1, hidden)
     grad_conv = lax.dynamic_update_slice_in_dim(
         jnp.zeros_like(image), grad_tile, first_col, axis=1
     )

time: 98.1 us -> 107 us (1.091)
  starting transfers between devices: 31.2 us -> 20.8 us
  local copies, waits for them, and re-layouts: 7.26 us -> 16.3 us
  matrix products: 6.74 us -> 11.9 us
  other arithmetic: 24.6 us -> 28.6 us
    ppermute x12 -> x4, starting transfers between devices: 23.6 us -> 13.7 us  [halving_reduce(): got = lax.ppermute(sent, axis, pairs)]
    concatenate x0 -> x1, local copies, waits for them, and re-layouts: none -> 6.92 us  [halving_reduce(): sent = jnp.concatenate([give_q.reshape(-1, width), give_r, whole], axis=0)]
    slice x0 -> x3, other arithmetic: none -> 2.56 us  [halving_reduce(): quartered = keep_q + got[:cut_q].reshape(quarters, half_q, width)]
    dot_general x1 -> x4, matrix products: 1.66 us -> 3.86 us  [shards(): lax.dot_general(normed_flat, pre_flat[:, q * channels:(q + 1) * channels]...]
    concatenate x0 -> x3, other arithmetic: none -> 1.56 us  [halving_reduce(): sent = jnp.concatenate([give_q.reshape(-1, width), give_r, whole], axis=0)]
    unnamed x223 -> x165, local copies, waits for them, and re-layouts: 2.6 us -> 3.84 us
    dot_general x1, matrix products: 0.44 us -> 1.65 us  [shards(): lax.dot_general(act_flat, grad_flat, (((0,), (0,)), ((), ())), preferred_...]
    ppermute x12 -> x4, waiting for transfers between devices: 22.7 us -> 23.1 us  [halving_reduce(): got = lax.ppermute(sent, axis, pairs)]
  transfers between devices with their start and end apart: 16 -> 8, of which waited for: 9 -> 4; matrix products, arithmetic and copies ran while one was open for 21% -> 12% of each run, Pallas kernels for 0% -> 0%
where the time goes in v6:
time: 107 us; the launch traced here: 106 us
  other arithmetic  28.6 us (27%)
  waiting for transfers between devices  25.7 us (24%)
  starting transfers between devices  20.8 us (19%)
  local copies, waits for them, and re-layouts  16.3 us (15%)
  matrix products  11.9 us (11%)
  between operations  2.81 us (3%)
    ppermute x4, waiting for transfers between devices, halving_reduce(): got = lax.ppermute(sent, axis, pairs)  23.1 us
    ppermute x4, starting transfers between devices, halving_reduce(): got = lax.ppermute(sent, axis, pairs)  13.7 us
    convert_element_type x1, other arithmetic, shards(): (cotangent.astype(jnp.float32) + conv_back).astype(jnp.bfloat16)  9.87 us
    concatenate x1, local copies, waits for them, and re-layouts, halving_reduce(): sent = jnp.concatenate([give_q.reshape(-1, width), give_r, whole], axis=0)  6.92 us
    ppermute x2, starting transfers between devices, padded_2(): lax.ppermute(lax.slice_in_dim(block, block.shape[dim] - width, None, axis...  4.52 us
    reduce_sum x3, other arithmetic, kernel_terms(): jnp.sum(padded[row_tap:row_tap + image_rows, col_tap:col_tap + image_cols...  3.89 us
    dot_general x4, matrix products, shards(): lax.dot_general(normed_flat, pre_flat[:, q * channels:(q + 1) * channels]...  3.86 us
    reduce_sum x1, other arithmetic, shards(): centre = jnp.mean(filtered, axis=-1, keepdims=True)  3.86 us
  transfers between devices with their start and end apart: 8, of which 4 were waited for; matrix products, arithmetic and copies ran while one was open for 12% of the time, Pallas kernels for 0%

profile of v6, /device:TPU:0, one launch (start us, length us, event | category | flops | bytes accessed | tf_op | source)
XLA Modules:
  0.0 106.2 jit_solution(3783788157529765835)
XLA Ops:
  0.7 1.1 %copy.34 = bf16[4,256,256]{2,1,0:T(8,128)(2,1)S(1)} copy(bf16[4,256,256]{2,1,0:T(8,128)(2,1)} %param.8) | data formatting | bytes 1048576
  1.8 2.4 %collective-permute-start = (bf16[3,256,256]{2,1,0:T(8,128)(2,1)S(1)}, bf16[3,256,256]{2,1,0:T(8,128)(2,1)S(1)}, u32[]{:S(2)}, u32[]{:S(2)}) collective-permute-start(bf16[3,256,256]{2,1,0:T(8,128)(2,1)S(1)} %get-tuple-element.70), channel_id=1, source_target_pairs={{0,1},{1,2},{2,3},{3,4},{4,5},{5,6},{6,7},{7,8},{8,9},{9,10},{10,1... | collective-permute-start | bytes 1179656 | tf_op jit(solution)/shard_map/ppermute | solution.py:21
  4.2 1.3 %collective-permute-start.1 = (bf16[3,256,256]{2,1,0:T(8,128)(2,1)S(1)}, bf16[3,256,256]{2,1,0:T(8,128)(2,1)S(1)}, u32[]{:S(2)}, u32[]{:S(2)}) collective-permute-start(bf16[3,256,256]{2,1,0:T(8,128)(2,1)S(1)} %get-tuple-element.69), channel_id=1, source_target_pairs={{1,0},{2,1},{3,2},{4,3},{5,4},{6,5},{7,6},{8,7},{9,8},{10,9},{11,1... | collective-permute-start | bytes 1179656 | tf_op jit(solution)/shard_map/ppermute | solution.py:24
  5.5 0.7 bitcast_reduce_fusion
  7.3 2.6 %collective-permute-done.1 = bf16[3,256,256]{2,1,0:T(8,128)(2,1)S(1)} collective-permute-done((bf16[3,256,256]{2,1,0:T(8,128)(2,1)S(1)}, bf16[3,256,256]{2,1,0:T(8,128)(2,1)S(1)}, u32[]{:S(2)}, u32[]{:S(2)}) %collective-permute-start.1) | collective-permute-done | bytes 393248 | tf_op jit(solution)/shard_map/ppermute | solution.py:24
  9.9 0.3 fusion.82
  10.3 3.9 %fusion.141 = (f32[4,128]{1,0:T(4,128)S(1)}, f32[4,128,256]{2,1,0:T(8,128)S(1)}) fusion(f32[256]{0:T(256)S(1)} %bitcast.294, f32[10,134,256]{2,1,0:T(8,128)S(1)} %fusion.82, f32[256]{0:T(256)S(1)} %bitcast.296, f32[256]{0:T(256)S(1)} %bitcast.240, f32[256]{0:T(256)S(1)} %bitcast.242, f32[256]{0:T(256)S(1)} %bitcast.244, f32[256]{0:T(256)S(1)} %bitcast.246, ...), kind=kLoop, calls=%fused_computation.270 | loop fusion | flops 12844544 | bytes 26266624 | tf_op jit(solution)/shard_map/reduce_sum | solution.py:119
  14.5 0.2 multiply_reduce_fusion.3
  14.8 0.2 multiply_convert_fusion.3
  15.0 1.8 %fusion.11 = (bf16[1024,512]{0,1:T(8,128)(2,1)}, f32[512,1024]{1,0:T(8,128)S(1)}) fusion(bf16[512,256]{1,0:T(8,128)(2,1)S(1)} %bitcast.199, bf16[256,1024]{1,0:T(8,128)(2,1)S(1)} %copy-done), kind=kOutput, calls=%fused_computation.63 | convolution fusion | flops 273154048 | bytes 3932160 | tf_op jit(solution)/shard_map/dot_general | solution.py:129
  16.9 1.6 %fusion.86 = (f32[256]{0:T(256)S(1)}, bf16[4,128,256]{2,1,0:T(8,128)(2,1)S(1)}, f32[512,256]{1,0:T(8,128)}) fusion(bf16[4,256,256]{2,1,0:T(8,128)(2,1)S(1)} %copy-done.6, s32[]{:T(128)S(6)} %select_n.61, f32[256]{0:T(256)S(1)} %copy-done.79, bf16[1024,256]{1,0:T(8,128)(2,1)S(1)} %copy-done.9, f32[512,1024]{1,0:T(8,128)S(1)} %get-tuple-element.128), kind=kOutput, calls=%fused_computation.174 | convolution fusion | flops 273809152 | bytes 3672068 | tf_op jit(solution)/shard_map/dot_general | solution.py:131
  18.5 2.4 %fusion.6 = bf16[512,1024]{1,0:T(8,128)(2,1)} fusion(f32[512,1024]{1,0:T(8,128)S(1)} %get-tuple-element.128, bf16[512,256]{1,0:T(8,128)(2,1)S(1)} %bitcast.197, bf16[1024,256]{1,0:T(8,128)(2,1)S(1)} %copy-done.9), kind=kOutput, calls=%fused_computation.58 | convolution fusion | flops 278396928 | bytes 3932160 | tf_op jit(solution)/shard_map/dot_general | solution.py:132
  20.9 1.1 %copy.20 = bf16[256,512]{1,0:T(8,128)(2,1)S(1)} copy(bf16[256,512]{0,1:T(8,128)(2,1)} %bitcast.200) | data formatting | bytes 524288 | tf_op jit(solution)/shard_map/dot_general | solution.py:138
  22.0 1.3 %convolution_bitcast_fusion.1 = f32[1,2,2,2,2,16,256]{6,5,4,3,2,1,0:T(8,128)S(1)} fusion(bf16[2,2,2,2,16,512]{5,4,3,2,1,0:T(8,128)(2,1)S(1)} %bitcast.184, bf16[512,1024]{1,0:T(8,128)(2,1)} %fusion.6), kind=kOutput, calls=%fused_computation.75 | convolution fusion | flops 67108864 | bytes 786432 | tf_op jit(solution)/shard_map/dot_general | solution.py:138
  23.3 1.2 %convolution_bitcast_fusion.2 = f32[1,2,2,2,2,16,256]{6,5,4,3,2,1,0:T(8,128)S(1)} fusion(bf16[2,2,2,2,16,512]{5,4,3,2,1,0:T(8,128)(2,1)S(1)} %bitcast.185, bf16[512,1024]{1,0:T(8,128)(2,1)} %fusion.6), kind=kOutput, calls=%fused_computation.76 | convolution fusion | flops 67108864 | bytes 786432 | tf_op jit(solution)/shard_map/dot_general | solution.py:138
  24.5 1.2 %convolution_bitcast_fusion.3 = f32[1,2,2,2,2,16,256]{6,5,4,3,2,1,0:T(8,128)S(1)} fusion(bf16[2,2,2,2,16,512]{5,4,3,2,1,0:T(8,128)(2,1)S(1)} %bitcast.186, bf16[512,1024]{1,0:T(8,128)(2,1)} %fusion.6), kind=kOutput, calls=%fused_computation.77 | convolution fusion | flops 67108864 | bytes 786432 | tf_op jit(solution)/shard_map/dot_general | solution.py:138
  25.7 0.2 convolution_bitcast_fusion.4
  25.9 0.6 multiply_reduce_fusion.2
  26.5 0.3 multiply_reduce_fusion
  26.8 2.2 %fusion.134 = (f32[256]{0:T(256)}, f32[256]{0:T(256)}, f32[256]{0:T(256)}, f32[256]{0:T(256)}, f32[256]{0:T(256)}, /*index=5*/f32[256]{0:T(256)}, f32[256]{0:T(2...) fusion(f32[10,134,256]{2,1,0:T(8,128)S(1)} %fusion.82, ...), kind=kLoop, calls=%fused_computation.222 | loop fusion | flops 5893632 | bytes 10775552 | tf_op jit(solution)/shard_map/reduce_sum | solution.py:100
  29.0 1.0 fusion.135
  30.0 0.7 fusion.133
  30.9 2.3 %copy.22 = bf16[1024,512]{1,0:T(8,128)(2,1)} copy(bf16[1024,512]{0,1:T(8,128)(2,1)} %get-tuple-element.127) | data formatting | bytes 2097152 | tf_op jit(solution)/shard_map/convert_element_type | solution.py:130
  33.2 1.7 %convolution_bitcast_fusion = f32[2,2,2,2,64,256]{5,4,0,1,2,3:T(8,128)S(1)} fusion(bf16[2,2,2,2,64,512]{5,4,3,2,1,0:T(8,128)(2,1)} %bitcast.191, bf16[512,256,1,1,1,1]{1,0,5,4,3,2:T(8,128)(2,1)S(1)} %bitcast.198), kind=kOutput, calls=%fused_computation.70 | convolution fusion | flops 268435456 | bytes 2359296 | tf_op jit(solution)/shard_map/dot_general | solution.py:147
  35.2 0.9 copy-done.2
  36.1 0.8 constant_dynamic-slice_fusion.6
  37.1 6.9 %concatenate.25 = f32[1075,256]{1,0:T(8,128)} concatenate(f32[512,256]{1,0:T(8,128)S(1)} %bitcast.195, f32[512,256]{1,0:T(8,128)} %constant_dynamic-slice_fusion.6, f32[1,256]{1,0:T(1,128)S(1)} %bitcast.236, f32[1,256]{1,0:T(1,128)S(1)} %bitcast.374, f32[1,256]{1,0:T(1,128)S(1)} %bitcast.376, f32[1,256]{1,0:T(1,128)S(1)} %bitcast.378, f32[1,256]{1,0:T(1,128)S(1)} %bitcast.380, ...), dimensions={0} | concatenate | bytes 2201600 | tf_op jit(solution)/shard_map/concatenate | solution.py:62
  44.0 6.0 %collective-permute-start.4 = (f32[1075,256]{1,0:T(8,128)}, f32[1075,256]{1,0:T(8,128)}, u32[]{:S(2)}, u32[]{:S(2)}) collective-permute-start(f32[1075,256]{1,0:T(8,128)} %concatenate.25), channel_id=1, source_target_pairs={{0,1},{1,0},{2,3},{3,2},{4,5},{5,4},{6,7},{7,6},{8,9},{9,8},{10,11... | collective-permute-start | bytes 3302408 | tf_op jit(solution)/shard_map/ppermute | solution.py:63
  50.2 2.5 %collective-permute-done.4 = f32[1075,256]{1,0:T(8,128)} collective-permute-done((f32[1075,256]{1,0:T(8,128)}, f32[1075,256]{1,0:T(8,128)}, u32[]{:S(2)}, u32[]{:S(2)}) %collective-permute-start.4) | collective-permute-done | bytes 1100832 | tf_op jit(solution)/shard_map/ppermute | solution.py:63
  52.7 1.5 %fusion.142 = (f32[512,256]{1,0:T(8,128)S(1)}, f32[512,256]{1,0:T(8,128)S(1)}) fusion(f32[1075,256]{1,0:T(8,128)} %collective-permute-done.4, f32[1024,256]{1,0:T(8,128)} %bitcast.193, s32[]{:T(128)S(6)} %select_n.68), kind=kLoop, calls=%fused_computation.271 | loop fusion | flops 131072 | bytes 2621444 | tf_op jit(solution)/shard_map/slice | solution.py:65
  54.2 0.8 copy-done.4
  55.1 0.8 slice_add_fusion.7
  55.9 0.9 pad_maximum_fusion
  56.8 2.5 %collective-permute-start.5 = (f32[563,256]{1,0:T(8,128)}, f32[563,256]{1,0:T(8,128)}, u32[]{:S(2)}, u32[]{:S(2)}) collective-permute-start(f32[563,256]{1,0:T(8,128)} %pad_maximum_fusion), channel_id=1, source_target_pairs={{0,2},{1,3},{2,0},{3,1},{4,6},{5,7},{6,4},{7,5},{8,10},{9,11},{10,... | collective-permute-start | bytes 1729544 | tf_op jit(solution)/shard_map/ppermute | solution.py:63
  59.4 2.1 %collective-permute-start.2 = (bf16[3,256,256]{2,1,0:T(8,128)(2,1)S(1)}, bf16[3,256,256]{2,1,0:T(8,128)(2,1)S(1)}, u32[]{:S(2)}, u32[]{:S(2)}) collective-permute-start(bf16[3,256,256]{2,1,0:T(8,128)(2,1)S(1)} %get-tuple-element.67), channel_id=1, source_target_pairs={{0,1},{1,2},{2,3},{3,4},{4,5},{5,6},{6,7},{7,8},{8,9},{9,10},{10,1... | collective-permute-start | bytes 1179656 | tf_op jit(solution)/shard_map/ppermute | solution.py:21
  61.5 1.3 %collective-permute-start.3 = (bf16[3,256,256]{2,1,0:T(8,128)(2,1)S(1)}, bf16[3,256,256]{2,1,0:T(8,128)(2,1)S(1)}, u32[]{:S(2)}, u32[]{:S(2)}) collective-permute-start(bf16[3,256,256]{2,1,0:T(8,128)(2,1)S(1)} %get-tuple-element.68), channel_id=1, source_target_pairs={{1,0},{2,1},{3,2},{4,3},{5,4},{6,5},{7,6},{8,7},{9,8},{10,9},{11,1... | collective-permute-start | bytes 1179656 | tf_op jit(solution)/shard_map/ppermute | solution.py:24
  62.8 14.4 %collective-permute-done.5 = f32[563,256]{1,0:T(8,128)} collective-permute-done((f32[563,256]{1,0:T(8,128)}, f32[563,256]{1,0:T(8,128)}, u32[]{:S(2)}, u32[]{:S(2)}) %collective-permute-start.5) | collective-permute-done | bytes 576544 | tf_op jit(solution)/shard_map/ppermute | solution.py:63
  77.2 1.1 %fusion.143 = (f32[256,256]{1,0:T(8,128)S(1)}, f32[256,256]{1,0:T(8,128)S(1)}) fusion(f32[563,256]{1,0:T(8,128)} %collective-permute-done.5, f32[512,256]{1,0:T(8,128)S(1)} %get-tuple-element.62, s32[]{:T(128)S(6)} %select_n.72), kind=kLoop, calls=%fused_computation.272 | loop fusion | flops 65536 | bytes 1310724 | tf_op jit(solution)/shard_map/slice | solution.py:65
  78.4 0.8 slice_add_fusion.6
  79.3 2.5 %collective-permute-start.6 = (f32[307,256]{1,0:T(8,128)S(1)}, f32[307,256]{1,0:T(8,128)S(1)}, u32[]{:S(2)}, u32[]{:S(2)}) collective-permute-start(f32[307,256]{1,0:T(8,128)S(1)} %pad_maximum_fusion.1), channel_id=1, source_target_pairs={{0,4},{1,5},{2,6},{3,7},{4,0},{5,1},{6,2},{7,3},{8,12},{9,13},{10,... | collective-permute-start | bytes 943112 | tf_op jit(solution)/shard_map/ppermute | solution.py:63
  82.0 0.7 copy-done.1
  82.9 6.2 %collective-permute-done.6 = f32[307,256]{1,0:T(8,128)S(1)} collective-permute-done((f32[307,256]{1,0:T(8,128)S(1)}, f32[307,256]{1,0:T(8,128)S(1)}, u32[]{:S(2)}, u32[]{:S(2)}) %collective-permute-start.6) | collective-permute-done | bytes 314400 | tf_op jit(solution)/shard_map/ppermute | solution.py:63
  89.2 0.7 pad_maximum_fusion.2
  89.9 2.8 %collective-permute-start.7 = (f32[179,256]{1,0:T(8,128)}, f32[179,256]{1,0:T(8,128)}, u32[]{:S(2)}, u32[]{:S(2)}) collective-permute-start(f32[179,256]{1,0:T(8,128)} %pad_maximum_fusion.2), channel_id=1, source_target_pairs={{0,8},{1,9},{2,10},{3,11},{4,12},{5,13},{6,14},{7,15},{8,0},{9,1},... | collective-permute-start | bytes 549896 | tf_op jit(solution)/shard_map/ppermute | solution.py:63
  92.7 9.9 %fusion.20 = bf16[4,256,256]{2,1,0:T(8,128)(2,1)} fusion(f32[10,256,256]{2,1,0:T(8,128)S(1)} %maximum_convert_fusion, bf16[4,256,256]{2,1,0:T(8,128)(2,1)} %param.15, f32[256]{0:T(256)S(1)} %bitcast.239, f32[256]{0:T(256)} %bitcast.299, f32[256]{0:T(256)S(1)} %bitcast.277, f32[256]{0:T(256)} %bitcast.293, f32[256]{0:T(256)} %bitcast.291, f32[256]{0:T(256)} %bitcast.289, ...), kind=kLoop, calls=%fused_computation.85 | loop fusion | flops 26214400 | bytes 11060224 | tf_op jit(solution)/shard_map/convert_element_type | solution.py:176
  102.6 1.5 %slice_add_fusion.3 = (f32[64,256]{1,0:T(8,128)}, f32[64,256]{1,0:T(8,128)S(1)}) fusion(f32[179,256]{1,0:T(8,128)} %collective-permute-done.7, f32[128,256]{1,0:T(8,128)S(1)} %get-tuple-element.72, s32[]{:T(128)S(6)} %select_n.78), kind=kLoop, calls=%fused_computation.246 | loop fusion | flops 16384 | bytes 327684 | tf_op jit(solution)/shard_map/add | solution.py:66
  104.1 0.6 copy.30
  104.8 1.4 %slice_add_fusion.4 = f32[51,256]{1,0:T(8,128)} fusion(f32[51,256]{1,0:T(8,128)S(1)} %slice_add_fusion.5, f32[179,256]{1,0:T(8,128)} %collective-permute-done.7), kind=kLoop, calls=%fused_computation.248 | loop fusion | flops 13056 | bytes 156672 | tf_op jit(solution)/shard_map/add | solution.py:67
  (196 shorter events, 1.7 us)
Async XLA Ops:
  0.6 14.4 %copy-start = (bf16[256,1024]{1,0:T(8,128)(2,1)S(1)}, bf16[256,1024]{1,0:T(8,128)(2,1)}, u32[]{:S(2)}) copy-start(bf16[256,1024]{1,0:T(8,128)(2,1)} %param.12) | copy-start | bytes 1572868
  1.8 5.5 %collective-permute-start = (bf16[3,256,256]{2,1,0:T(8,128)(2,1)S(1)}, bf16[3,256,256]{2,1,0:T(8,128)(2,1)S(1)}, u32[]{:S(2)}, u32[]{:S(2)}) collective-permute-start(bf16[3,256,256]{2,1,0:T(8,128)(2,1)S(1)} %get-tuple-element.70), channel_id=1, source_target_pairs={{0,1},{1,2},{2,3},{3,4},{4,5},{5,6},{6,7},{7,8},{8,9},{9,10},{10,1... | collective-permute-start | bytes 1179656 | tf_op jit(solution)/shard_map/ppermute | solution.py:21
  4.2 5.7 %collective-permute-start.1 = (bf16[3,256,256]{2,1,0:T(8,128)(2,1)S(1)}, bf16[3,256,256]{2,1,0:T(8,128)(2,1)S(1)}, u32[]{:S(2)}, u32[]{:S(2)}) collective-permute-start(bf16[3,256,256]{2,1,0:T(8,128)(2,1)S(1)} %get-tuple-element.69), channel_id=1, source_target_pairs={{1,0},{2,1},{3,2},{4,3},{5,4},{6,5},{7,6},{8,7},{9,8},{10,9},{11,1... | collective-permute-start | bytes 1179656 | tf_op jit(solution)/shard_map/ppermute | solution.py:24
  6.9 7.3 %copy-start.11 = (f32[1,1,256]{2,1,0:T(1,128)}, f32[1,1,256]{2,1,0:T(1,128)S(1)}, u32[]{:S(2)}) copy-start(f32[1,1,256]{2,1,0:T(1,128)S(1)} %get-tuple-element.87) | copy-start | bytes 3076
  6.9 7.3 %copy-start.13 = (f32[1,1,256]{2,1,0:T(1,128)}, f32[1,1,256]{2,1,0:T(1,128)S(1)}, u32[]{:S(2)}) copy-start(f32[1,1,256]{2,1,0:T(1,128)S(1)} %get-tuple-element.88) | copy-start | bytes 3076
  6.9 7.3 %copy-start.15 = (f32[1,1,256]{2,1,0:T(1,128)}, f32[1,1,256]{2,1,0:T(1,128)S(1)}, u32[]{:S(2)}) copy-start(f32[1,1,256]{2,1,0:T(1,128)S(1)} %get-tuple-element.89) | copy-start | bytes 3076
  6.9 7.3 %copy-start.17 = (f32[1,1,256]{2,1,0:T(1,128)}, f32[1,1,256]{2,1,0:T(1,128)S(1)}, u32[]{:S(2)}) copy-start(f32[1,1,256]{2,1,0:T(1,128)S(1)} %get-tuple-element.90) | copy-start | bytes 3076
  6.9 7.3 %copy-start.19 = (f32[1,1,256]{2,1,0:T(1,128)}, f32[1,1,256]{2,1,0:T(1,128)S(1)}, u32[]{:S(2)}) copy-start(f32[1,1,256]{2,1,0:T(1,128)S(1)} %get-tuple-element.91) | copy-start | bytes 3076
  6.9 7.3 %copy-start.21 = (f32[1,1,256]{2,1,0:T(1,128)}, f32[1,1,256]{2,1,0:T(1,128)S(1)}, u32[]{:S(2)}) copy-start(f32[1,1,256]{2,1,0:T(1,128)S(1)} %get-tuple-element.92) | copy-start | bytes 3076
  6.9 7.3 %copy-start.23 = (f32[1,1,256]{2,1,0:T(1,128)}, f32[1,1,256]{2,1,0:T(1,128)S(1)}, u32[]{:S(2)}) copy-start(f32[1,1,256]{2,1,0:T(1,128)S(1)} %get-tuple-element.93) | copy-start | bytes 3076
  7.0 7.2 %copy-start.25 = (f32[1,1,256]{2,1,0:T(1,128)}, f32[1,1,256]{2,1,0:T(1,128)S(1)}, u32[]{:S(2)}) copy-start(f32[1,1,256]{2,1,0:T(1,128)S(1)} %get-tuple-element.113) | copy-start | bytes 3076
  7.0 7.2 %copy-start.27 = (f32[1,1,256]{2,1,0:T(1,128)}, f32[1,1,256]{2,1,0:T(1,128)S(1)}, u32[]{:S(2)}) copy-start(f32[1,1,256]{2,1,0:T(1,128)S(1)} %get-tuple-element.114) | copy-start | bytes 3076
  7.0 7.2 %copy-start.29 = (f32[1,1,256]{2,1,0:T(1,128)}, f32[1,1,256]{2,1,0:T(1,128)S(1)}, u32[]{:S(2)}) copy-start(f32[1,1,256]{2,1,0:T(1,128)S(1)} %get-tuple-element.115) | copy-start | bytes 3076
  7.0 7.2 %copy-start.31 = (f32[1,1,256]{2,1,0:T(1,128)}, f32[1,1,256]{2,1,0:T(1,128)S(1)}, u32[]{:S(2)}) copy-start(f32[1,1,256]{2,1,0:T(1,128)S(1)} %get-tuple-element.116) | copy-start | bytes 3076
  7.0 7.2 %copy-start.32 = (f32[1,1,256]{2,1,0:T(1,128)}, f32[1,1,256]{2,1,0:T(1,128)S(1)}, u32[]{:S(2)}) copy-start(f32[1,1,256]{2,1,0:T(1,128)S(1)} %get-tuple-element.117) | copy-start | bytes 3076
  7.0 7.2 %copy-start.33 = (f32[1,1,256]{2,1,0:T(1,128)}, f32[1,1,256]{2,1,0:T(1,128)S(1)}, u32[]{:S(2)}) copy-start(f32[1,1,256]{2,1,0:T(1,128)S(1)} %get-tuple-element.118) | copy-start | bytes 3076
  7.0 7.2 %copy-start.34 = (f32[1,1,256]{2,1,0:T(1,128)}, f32[1,1,256]{2,1,0:T(1,128)S(1)}, u32[]{:S(2)}) copy-start(f32[1,1,256]{2,1,0:T(1,128)S(1)} %get-tuple-element.119) | copy-start | bytes 3076
  7.0 7.2 %copy-start.35 = (f32[1,1,256]{2,1,0:T(1,128)}, f32[1,1,256]{2,1,0:T(1,128)S(1)}, u32[]{:S(2)}) copy-start(f32[1,1,256]{2,1,0:T(1,128)S(1)} %get-tuple-element.120) | copy-start | bytes 3076
  7.1 7.2 %copy-start.36 = (f32[1,1,256]{2,1,0:T(1,128)}, f32[1,1,256]{2,1,0:T(1,128)S(1)}, u32[]{:S(2)}) copy-start(f32[1,1,256]{2,1,0:T(1,128)S(1)} %get-tuple-element.121) | copy-start | bytes 3076
  7.1 7.2 %copy-start.37 = (f32[1,1,256]{2,1,0:T(1,128)}, f32[1,1,256]{2,1,0:T(1,128)S(1)}, u32[]{:S(2)}) copy-start(f32[1,1,256]{2,1,0:T(1,128)S(1)} %get-tuple-element.122) | copy-start | bytes 3076
  7.1 7.2 %copy-start.38 = (f32[1,1,256]{2,1,0:T(1,128)}, f32[1,1,256]{2,1,0:T(1,128)S(1)}, u32[]{:S(2)}) copy-start(f32[1,1,256]{2,1,0:T(1,128)S(1)} %get-tuple-element.123) | copy-start | bytes 3076
  7.1 7.2 %copy-start.39 = (f32[1,1,256]{2,1,0:T(1,128)}, f32[1,1,256]{2,1,0:T(1,128)S(1)}, u32[]{:S(2)}) copy-start(f32[1,1,256]{2,1,0:T(1,128)S(1)} %get-tuple-element.94) | copy-start | bytes 3076
  7.1 7.2 %copy-start.40 = (f32[1,1,256]{2,1,0:T(1,128)}, f32[1,1,256]{2,1,0:T(1,128)S(1)}, u32[]{:S(2)}) copy-start(f32[1,1,256]{2,1,0:T(1,128)S(1)} %get-tuple-element.95) | copy-start | bytes 3076
  7.1 7.2 %copy-start.41 = (f32[1,1,256]{2,1,0:T(1,128)}, f32[1,1,256]{2,1,0:T(1,128)S(1)}, u32[]{:S(2)}) copy-start(f32[1,1,256]{2,1,0:T(1,128)S(1)} %get-tuple-element.96) | copy-start | bytes 3076
  7.1 7.2 %copy-start.42 = (f32[1,1,256]{2,1,0:T(1,128)}, f32[1,1,256]{2,1,0:T(1,128)S(1)}, u32[]{:S(2)}) copy-start(f32[1,1,256]{2,1,0:T(1,128)S(1)} %get-tuple-element.97) | copy-start | bytes 3076
  7.2 7.2 %copy-start.43 = (f32[1,1,256]{2,1,0:T(1,128)}, f32[1,1,256]{2,1,0:T(1,128)S(1)}, u32[]{:S(2)}) copy-start(f32[1,1,256]{2,1,0:T(1,128)S(1)} %get-tuple-element.98) | copy-start | bytes 3076
  7.2 7.2 %copy-start.44 = (f32[1,1,256]{2,1,0:T(1,128)}, f32[1,1,256]{2,1,0:T(1,128)S(1)}, u32[]{:S(2)}) copy-start(f32[1,1,256]{2,1,0:T(1,128)S(1)} %get-tuple-element.99) | copy-start | bytes 3076
  7.2 7.2 %copy-start.45 = (f32[1,1,256]{2,1,0:T(1,128)}, f32[1,1,256]{2,1,0:T(1,128)S(1)}, u32[]{:S(2)}) copy-start(f32[1,1,256]{2,1,0:T(1,128)S(1)} %get-tuple-element.100) | copy-start | bytes 3076
  7.2 7.2 %copy-start.46 = (f32[1,1,256]{2,1,0:T(1,128)}, f32[1,1,256]{2,1,0:T(1,128)S(1)}, u32[]{:S(2)}) copy-start(f32[1,1,256]{2,1,0:T(1,128)S(1)} %get-tuple-element.101) | copy-start | bytes 3076
  44.0 8.7 %collective-permute-start.4 = (f32[1075,256]{1,0:T(8,128)}, f32[1075,256]{1,0:T(8,128)}, u32[]{:S(2)}, u32[]{:S(2)}) collective-permute-start(f32[1075,256]{1,0:T(8,128)} %concatenate.25), channel_id=1, source_target_pairs={{0,1},{1,0},{2,3},{3,2},{4,5},{5,4},{6,7},{7,6},{8,9},{9,8},{10,11... | collective-permute-start | bytes 3302408 | tf_op jit(solution)/shard_map/ppermute | solution.py:63
  56.8 21.6 %copy-start.5 = (f32[4,128,256]{2,1,0:T(8,128)S(1)}, f32[4,128,256]{2,1,0:T(8,128)}, u32[]{:S(2)}) copy-start(f32[4,128,256]{2,1,0:T(8,128)} %copy-done.4) | copy-start | bytes 1572868
  56.8 20.5 %collective-permute-start.5 = (f32[563,256]{1,0:T(8,128)}, f32[563,256]{1,0:T(8,128)}, u32[]{:S(2)}, u32[]{:S(2)}) collective-permute-start(f32[563,256]{1,0:T(8,128)} %pad_maximum_fusion), channel_id=1, source_target_pairs={{0,2},{1,3},{2,0},{3,1},{4,6},{5,7},{6,4},{7,5},{8,10},{9,11},{10,... | collective-permute-start | bytes 1729544 | tf_op jit(solution)/shard_map/ppermute | solution.py:63
  59.4 22.5 %copy-start.3 = (f32[512,256]{1,0:T(8,128)S(1)}, f32[512,256]{1,0:T(8,128)}, u32[]{:S(2)}) copy-start(f32[512,256]{1,0:T(8,128)} %get-tuple-element.124) | copy-start | bytes 1572868
  59.4 22.4 %copy-start.80 = (f32[256]{0:T(256)S(1)}, f32[256]{0:T(256)}, u32[]{:S(2)}) copy-start(f32[256]{0:T(256)} %param.14) | copy-start | bytes 3076
  59.4 22.6 %collective-permute-start.2 = (bf16[3,256,256]{2,1,0:T(8,128)(2,1)S(1)}, bf16[3,256,256]{2,1,0:T(8,128)(2,1)S(1)}, u32[]{:S(2)}, u32[]{:S(2)}) collective-permute-start(bf16[3,256,256]{2,1,0:T(8,128)(2,1)S(1)} %get-tuple-element.67), channel_id=1, source_target_pairs={{0,1},{1,2},{2,3},{3,4},{4,5},{5,6},{6,7},{7,8},{8,9},{9,10},{10,1... | collective-permute-start | bytes 1179656 | tf_op jit(solution)/shard_map/ppermute | solution.py:21
  61.5 21.2 %collective-permute-start.3 = (bf16[3,256,256]{2,1,0:T(8,128)(2,1)S(1)}, bf16[3,256,256]{2,1,0:T(8,128)(2,1)S(1)}, u32[]{:S(2)}, u32[]{:S(2)}) collective-permute-start(bf16[3,256,256]{2,1,0:T(8,128)(2,1)S(1)} %get-tuple-element.68), channel_id=1, source_target_pairs={{1,0},{2,1},{3,2},{4,3},{5,4},{6,5},{7,6},{8,7},{9,8},{10,9},{11,1... | collective-permute-start | bytes 1179656 | tf_op jit(solution)/shard_map/ppermute | solution.py:24
  79.3 9.8 %collective-permute-start.6 = (f32[307,256]{1,0:T(8,128)S(1)}, f32[307,256]{1,0:T(8,128)S(1)}, u32[]{:S(2)}, u32[]{:S(2)}) collective-permute-start(f32[307,256]{1,0:T(8,128)S(1)} %pad_maximum_fusion.1), channel_id=1, source_target_pairs={{0,4},{1,5},{2,6},{3,7},{4,0},{5,1},{6,2},{7,3},{8,12},{9,13},{10,... | collective-permute-start | bytes 943112 | tf_op jit(solution)/shard_map/ppermute | solution.py:63
  81.9 10.7 %copy-start.12 = (f32[1,1,256]{2,1,0:T(1,128)S(1)}, f32[1,1,256]{2,1,0:T(1,128)}, u32[]{:S(2)}) copy-start(f32[1,1,256]{2,1,0:T(1,128)} %copy-done.11) | copy-start | bytes 3076
  81.9 10.7 %copy-start.14 = (f32[1,1,256]{2,1,0:T(1,128)S(1)}, f32[1,1,256]{2,1,0:T(1,128)}, u32[]{:S(2)}) copy-start(f32[1,1,256]{2,1,0:T(1,128)} %copy-done.13) | copy-start | bytes 3076
  81.9 10.7 %copy-start.16 = (f32[1,1,256]{2,1,0:T(1,128)S(1)}, f32[1,1,256]{2,1,0:T(1,128)}, u32[]{:S(2)}) copy-start(f32[1,1,256]{2,1,0:T(1,128)} %copy-done.15) | copy-start | bytes 3076
  81.9 10.7 %copy-start.18 = (f32[1,1,256]{2,1,0:T(1,128)S(1)}, f32[1,1,256]{2,1,0:T(1,128)}, u32[]{:S(2)}) copy-start(f32[1,1,256]{2,1,0:T(1,128)} %copy-done.17) | copy-start | bytes 3076
  81.9 10.7 %copy-start.20 = (f32[1,1,256]{2,1,0:T(1,128)S(1)}, f32[1,1,256]{2,1,0:T(1,128)}, u32[]{:S(2)}) copy-start(f32[1,1,256]{2,1,0:T(1,128)} %copy-done.19) | copy-start | bytes 3076
  82.0 10.7 %copy-start.22 = (f32[1,1,256]{2,1,0:T(1,128)S(1)}, f32[1,1,256]{2,1,0:T(1,128)}, u32[]{:S(2)}) copy-start(f32[1,1,256]{2,1,0:T(1,128)} %copy-done.21) | copy-start | bytes 3076
  82.0 10.7 %copy-start.24 = (f32[1,1,256]{2,1,0:T(1,128)S(1)}, f32[1,1,256]{2,1,0:T(1,128)}, u32[]{:S(2)}) copy-start(f32[1,1,256]{2,1,0:T(1,128)} %copy-done.23) | copy-start | bytes 3076
  82.0 10.7 %copy-start.26 = (f32[1,1,256]{2,1,0:T(1,128)S(1)}, f32[1,1,256]{2,1,0:T(1,128)}, u32[]{:S(2)}) copy-start(f32[1,1,256]{2,1,0:T(1,128)} %copy-done.25) | copy-start | bytes 3076
  82.0 10.7 %copy-start.28 = (f32[1,1,256]{2,1,0:T(1,128)S(1)}, f32[1,1,256]{2,1,0:T(1,128)}, u32[]{:S(2)}) copy-start(f32[1,1,256]{2,1,0:T(1,128)} %copy-done.27) | copy-start | bytes 3076
  82.0 10.7 %copy-start.30 = (f32[1,1,256]{2,1,0:T(1,128)S(1)}, f32[1,1,256]{2,1,0:T(1,128)}, u32[]{:S(2)}) copy-start(f32[1,1,256]{2,1,0:T(1,128)} %copy-done.29) | copy-start | bytes 3076
  89.9 12.7 %collective-permute-start.7 = (f32[179,256]{1,0:T(8,128)}, f32[179,256]{1,0:T(8,128)}, u32[]{:S(2)}, u32[]{:S(2)}) collective-permute-start(f32[179,256]{1,0:T(8,128)} %pad_maximum_fusion.2), channel_id=1, source_target_pairs={{0,8},{1,9},{2,10},{3,11},{4,12},{5,13},{6,14},{7,15},{8,0},{9,1},... | collective-permute-start | bytes 549896 | tf_op jit(solution)/shard_map/ppermute | solution.py:63
  (42 other events, 153.7 us)

commit v7 on v3

--- a/solution.py
+++ b/solution.py
@@ -49,8 +49,10 @@
             half = p.shape[0] // 2
             keeps.append(lax.dynamic_slice_in_dim(p, bit * half, half, axis=0))
             gives.append(lax.dynamic_slice_in_dim(p, (1 - bit) * half, half, axis=0))
+        if step > 0:
+            gives = [g.astype(jnp.bfloat16) for g in gives]
         got, got_whole = lax.ppermute((gives, whole), axis, pairs)
-        parts = [k + g for k, g in zip(keeps, got)]
+        parts = [k + g.astype(jnp.float32) for k, g in zip(keeps, got)]
         whole = whole + got_whole
     return parts, whole
 

time: 98.1 us -> 92.5 us (0.943)
  waiting for transfers between devices: 24.7 us -> 15.6 us
  starting transfers between devices: 31.2 us -> 34.7 us
    ppermute x12, waiting for transfers between devices: 22.7 us -> 13.5 us  [halving_reduce(): got, got_whole = lax.ppermute((gives, whole), axis, pairs)]
    ppermute x12, starting transfers between devices: 23.6 us -> 27.1 us  [halving_reduce(): got, got_whole = lax.ppermute((gives, whole), axis, pairs)]
  transfers between devices with their start and end apart: 16 -> 16, of which waited for: 9 -> 8; matrix products, arithmetic and copies ran while one was open for 21% -> 23% of each run, Pallas kernels for 0% -> 0%
where the time goes in v7:
time: 92.5 us; the launch traced here: 92.1 us
  starting transfers between devices  34.7 us (38%)
  other arithmetic  24.6 us (27%)
  waiting for transfers between devices  15.6 us (17%)
  local copies, waits for them, and re-layouts  7.26 us (8%)
  matrix products  6.74 us (7%)
  between operations  3.27 us (4%)
    ppermute x12, starting transfers between devices, halving_reduce(): got, got_whole = lax.ppermute((gives, whole), axis, pairs)  27.1 us
    ppermute x12, waiting for transfers between devices, halving_reduce(): got, got_whole = lax.ppermute((gives, whole), axis, pairs)  13.5 us
    convert_element_type x1, other arithmetic, shards(): (cotangent.astype(jnp.float32) + conv_back).astype(jnp.bfloat16)  9.56 us
    ppermute x2, starting transfers between devices, padded_2(): lax.ppermute(lax.slice_in_dim(block, block.shape[dim] - width, None, axis...  4.81 us
    reduce_sum x1, other arithmetic, shards(): centre = jnp.mean(filtered, axis=-1, keepdims=True)  4.55 us
    reduce_sum x3, other arithmetic, kernel_terms(): jnp.sum(padded[row_tap:row_tap + image_rows, col_tap:col_tap + image_cols...  3.93 us
    add x8, other arithmetic, halving_reduce(): parts = [k + g.astype(jnp.float32) for k, g in zip(keeps, got)]  3.83 us
    ppermute x2, starting transfers between devices, padded_2(): lax.ppermute(lax.slice_in_dim(block, 0, width, axis=dim), axis, backward)  2.76 us
  transfers between devices with their start and end apart: 16, of which 8 were waited for; matrix products, arithmetic and copies ran while one was open for 23% of the time, Pallas kernels for 0%

profile of v7, /device:TPU:0, one launch (start us, length us, event | category | flops | bytes accessed | tf_op | source)
XLA Modules:
  0.0 92.1 jit_solution(15964673515886140507)
XLA Ops:
  0.7 1.1 %copy.24 = bf16[4,256,256]{2,1,0:T(8,128)(2,1)S(1)} copy(bf16[4,256,256]{2,1,0:T(8,128)(2,1)} %param.8) | data formatting | bytes 1048576
  1.8 2.4 %collective-permute-start = (bf16[3,256,256]{2,1,0:T(8,128)(2,1)S(1)}, bf16[3,256,256]{2,1,0:T(8,128)(2,1)S(1)}, u32[]{:S(2)}, u32[]{:S(2)}) collective-permute-start(bf16[3,256,256]{2,1,0:T(8,128)(2,1)S(1)} %get-tuple-element.66), channel_id=1, source_target_pairs={{0,1},{1,2},{2,3},{3,4},{4,5},{5,6},{6,7},{7,8},{8,9},{9,10},{10,1... | collective-permute-start | bytes 1179656 | tf_op jit(solution)/shard_map/ppermute | solution.py:21
  4.2 1.3 %collective-permute-start.1 = (bf16[3,256,256]{2,1,0:T(8,128)(2,1)S(1)}, bf16[3,256,256]{2,1,0:T(8,128)(2,1)S(1)}, u32[]{:S(2)}, u32[]{:S(2)}) collective-permute-start(bf16[3,256,256]{2,1,0:T(8,128)(2,1)S(1)} %get-tuple-element.65), channel_id=1, source_target_pairs={{1,0},{2,1},{3,2},{4,3},{5,4},{6,5},{7,6},{8,7},{9,8},{10,9},{11,1... | collective-permute-start | bytes 1179656 | tf_op jit(solution)/shard_map/ppermute | solution.py:24
  5.5 0.7 bitcast_reduce_fusion
  7.1 0.6 fusion.146
  7.9 2.0 %collective-permute-done.1 = bf16[3,256,256]{2,1,0:T(8,128)(2,1)S(1)} collective-permute-done((bf16[3,256,256]{2,1,0:T(8,128)(2,1)S(1)}, bf16[3,256,256]{2,1,0:T(8,128)(2,1)S(1)}, u32[]{:S(2)}, u32[]{:S(2)}) %collective-permute-start.1) | collective-permute-done | bytes 393248 | tf_op jit(solution)/shard_map/ppermute | solution.py:24
  9.9 0.3 fusion.83
  10.3 4.5 %fusion.142 = (f32[4,128]{1,0:T(4,128)S(1)}, f32[4,128,256]{2,1,0:T(8,128)S(1)}) fusion(f32[256]{0:T(256)S(1)} %bitcast.214, f32[10,134,256]{2,1,0:T(8,128)S(1)} %fusion.83, f32[256]{0:T(256)S(1)} %bitcast.216, f32[256]{0:T(256)S(1)} %bitcast.160, f32[256]{0:T(256)S(1)} %bitcast.162, f32[256]{0:T(256)S(1)} %bitcast.164, f32[256]{0:T(256)S(1)} %bitcast.166, ...), kind=kLoop, calls=%fused_computation.256 | loop fusion | flops 12844544 | bytes 26266624 | tf_op jit(solution)/shard_map/reduce_sum | solution.py:108
  15.2 0.2 multiply_reduce_fusion.3
  15.7 1.8 %fusion.11 = (bf16[1024,512]{0,1:T(8,128)(2,1)}, f32[512,1024]{1,0:T(8,128)S(1)}) fusion(bf16[512,256]{1,0:T(8,128)(2,1)S(1)} %bitcast.156, bf16[256,1024]{1,0:T(8,128)(2,1)S(1)} %copy-done), kind=kOutput, calls=%fused_computation.63 | convolution fusion | flops 273154048 | bytes 3932160 | tf_op jit(solution)/shard_map/dot_general | solution.py:118
  17.6 0.8 fusion.87
  18.4 1.4 %fusion.6 = bf16[512,1024]{1,0:T(8,128)(2,1)S(1)} fusion(f32[512,1024]{1,0:T(8,128)S(1)} %get-tuple-element.120, bf16[512,256]{1,0:T(8,128)(2,1)S(1)} %bitcast.153, bf16[1024,256]{1,0:T(8,128)(2,1)S(1)} %copy-done.9), kind=kOutput, calls=%fused_computation.58 | convolution fusion | flops 278396928 | bytes 3932160 | tf_op jit(solution)/shard_map/dot_general | solution.py:121
  19.9 0.6 multiply_reduce_fusion.2
  20.4 0.3 multiply_reduce_fusion
  20.8 2.2 %fusion.135 = (f32[256]{0:T(256)}, f32[256]{0:T(256)}, f32[256]{0:T(256)}, f32[256]{0:T(256)}, f32[256]{0:T(256)}, /*index=5*/f32[256]{0:T(256)}, f32[256]{0:T(2...) fusion(f32[10,134,256]{2,1,0:T(8,128)S(1)} %fusion.83, ...), kind=kLoop, calls=%fused_computation.218 | loop fusion | flops 5893632 | bytes 10775552 | tf_op jit(solution)/shard_map/reduce_sum | solution.py:89
  23.0 1.0 %fusion.136 = (f32[256]{0:T(256)S(1)}, f32[256]{0:T(256)S(1)}, f32[256]{0:T(256)S(1)}, f32[256]{0:T(256)S(1)}, f32[256]{0:T(256)S(1)}, /*index=5*/f32[256]{0:T(2...) fusion(bf16[4,128,256]{2,1,0:T(8,128)(2,1)S(1)} %get-tuple-elem, ...), kind=kLoop, calls=%fused_computation.219 | loop fusion | flops 4845056 | bytes 9717760 | tf_op jit(solution)/shard_map/reduce_sum | solution.py:89
  24.2 0.7 fusion.134
  25.3 6.0 %collective-permute-start.12 = (f32[51,256]{1,0:T(8,128)S(1)}, f32[51,256]{1,0:T(8,128)S(1)}, u32[]{:S(2)}, u32[]{:S(2)}) collective-permute-start(f32[51,256]{1,0:T(8,128)S(1)} %concatenate.11), channel_id=1, source_target_pairs={{0,1},{1,0},{2,3},{3,2},{4,5},{5,4},{6,7},{7,6},{8,9},{9,8},{10,11... | collective-permute-start | bytes 156680 | tf_op jit(solution)/shard_map/ppermute | solution.py:54
  31.3 1.5 %copy.17 = bf16[1024,512]{1,0:T(8,128)(2,1)S(1)} copy(bf16[1024,512]{0,1:T(8,128)(2,1)} %get-tuple-element.119) | data formatting | bytes 2097152 | tf_op jit(solution)/shard_map/convert_element_type | solution.py:119
  32.8 0.4 convolution_bitcast_fusion
  33.3 0.9 constant_dynamic-slice_fusion
  34.2 0.2 copy-done.4
  34.6 0.8 copy-done.2
  35.6 2.4 %collective-permute-start.2 = (bf16[3,256,256]{2,1,0:T(8,128)(2,1)S(1)}, bf16[3,256,256]{2,1,0:T(8,128)(2,1)S(1)}, u32[]{:S(2)}, u32[]{:S(2)}) collective-permute-start(bf16[3,256,256]{2,1,0:T(8,128)(2,1)S(1)} %get-tuple-element.63), channel_id=1, source_target_pairs={{0,1},{1,2},{2,3},{3,4},{4,5},{5,6},{6,7},{7,8},{8,9},{9,10},{10,1... | collective-permute-start | bytes 1179656 | tf_op jit(solution)/shard_map/ppermute | solution.py:21
  38.0 1.5 %collective-permute-start.3 = (bf16[3,256,256]{2,1,0:T(8,128)(2,1)S(1)}, bf16[3,256,256]{2,1,0:T(8,128)(2,1)S(1)}, u32[]{:S(2)}, u32[]{:S(2)}) collective-permute-start(bf16[3,256,256]{2,1,0:T(8,128)(2,1)S(1)} %get-tuple-element.64), channel_id=1, source_target_pairs={{1,0},{2,1},{3,2},{4,3},{5,4},{6,5},{7,6},{8,7},{9,8},{10,9},{11,1... | collective-permute-start | bytes 1179656 | tf_op jit(solution)/shard_map/ppermute | solution.py:24
  39.5 4.4 %collective-permute-start.13 = (f32[51,256]{1,0:T(8,128)S(1)}, f32[51,256]{1,0:T(8,128)S(1)}, u32[]{:S(2)}, u32[]{:S(2)}) collective-permute-start(f32[51,256]{1,0:T(8,128)S(1)} %add.554), channel_id=1, source_target_pairs={{0,2},{1,3},{2,0},{3,1},{4,6},{5,7},{6,4},{7,5},{8,10},{9,11},{10,... | collective-permute-start | bytes 156680 | tf_op jit(solution)/shard_map/ppermute | solution.py:54
  43.9 1.7 %convolution_bitcast_fusion.1 = f32[2,2,2,2,16,1024]{5,4,0,1,2,3:T(8,128)S(1)} fusion(bf16[2,2,2,2,16,512]{5,4,3,2,1,0:T(8,128)(2,1)S(1)} %bitcast.155, bf16[512,1024]{1,0:T(8,128)(2,1)} %copy-done.8), kind=kOutput, calls=%fused_computation.71 | convolution fusion | flops 268435456 | bytes 2359296 | tf_op jit(solution)/shard_map/dot_general | solution.py:124
  45.7 4.8 %collective-permute-done.13 = f32[51,256]{1,0:T(8,128)S(1)} collective-permute-done((f32[51,256]{1,0:T(8,128)S(1)}, f32[51,256]{1,0:T(8,128)S(1)}, u32[]{:S(2)}, u32[]{:S(2)}) %collective-permute-start.13) | collective-permute-done | bytes 52256 | tf_op jit(solution)/shard_map/ppermute | solution.py:54
  50.6 3.5 %collective-permute-start.14 = (f32[51,256]{1,0:T(8,128)S(1)}, f32[51,256]{1,0:T(8,128)S(1)}, u32[]{:S(2)}, u32[]{:S(2)}) collective-permute-start(f32[51,256]{1,0:T(8,128)S(1)} %add.555), channel_id=1, source_target_pairs={{0,4},{1,5},{2,6},{3,7},{4,0},{5,1},{6,2},{7,3},{8,12},{9,13},{10,... | collective-permute-start | bytes 156680 | tf_op jit(solution)/shard_map/ppermute | solution.py:54
  54.1 0.9 constant_dynamic-slice_fusion.1
  54.9 1.3 %collective-permute-done.14 = f32[51,256]{1,0:T(8,128)S(1)} collective-permute-done((f32[51,256]{1,0:T(8,128)S(1)}, f32[51,256]{1,0:T(8,128)S(1)}, u32[]{:S(2)}, u32[]{:S(2)}) %collective-permute-start.14) | collective-permute-done | bytes 52256 | tf_op jit(solution)/shard_map/ppermute | solution.py:54
  56.2 3.1 %collective-permute-start.15 = (f32[51,256]{1,0:T(8,128)S(1)}, f32[51,256]{1,0:T(8,128)S(1)}, u32[]{:S(2)}, u32[]{:S(2)}) collective-permute-start(f32[51,256]{1,0:T(8,128)S(1)} %add.556), channel_id=1, source_target_pairs={{0,8},{1,9},{2,10},{3,11},{4,12},{5,13},{6,14},{7,15},{8,0},{9,1},... | collective-permute-start | bytes 156680 | tf_op jit(solution)/shard_map/ppermute | solution.py:54
  59.8 1.7 %collective-permute-done.15 = f32[51,256]{1,0:T(8,128)S(1)} collective-permute-done((f32[51,256]{1,0:T(8,128)S(1)}, f32[51,256]{1,0:T(8,128)S(1)}, u32[]{:S(2)}, u32[]{:S(2)}) %collective-permute-start.15) | collective-permute-done | bytes 52256 | tf_op jit(solution)/shard_map/ppermute | solution.py:54
  61.5 0.6 add.557
  62.7 9.6 %fusion.20 = bf16[4,256,256]{2,1,0:T(8,128)(2,1)} fusion(f32[10,256,256]{2,1,0:T(8,128)S(1)} %maximum_convert_fusion, bf16[4,256,256]{2,1,0:T(8,128)(2,1)} %param.15, f32[256]{0:T(256)S(1)} %bitcast.159, f32[256]{0:T(256)S(1)} %bitcast.219, f32[256]{0:T(256)S(1)} %bitcast.197, f32[256]{0:T(256)S(1)} %bitcast.213, f32[256]{0:T(256)S(1)} %bitcast.211, ...), kind=kLoop, calls=%fused_computation.82 | loop fusion | flops 26214400 | bytes 11060224 | tf_op jit(solution)/shard_map/convert_element_type | solution.py:155
  72.3 1.4 %dynamic-slice_add_fusion = f32[512,256]{1,0:T(8,128)S(1)} fusion(f32[512,256]{1,0:T(8,128)} %collective-permute-done.8, f32[1024,256]{1,0:T(8,128)} %bitcast.148, s32[]{:T(128)S(6)} %select_n.71), kind=kLoop, calls=%fused_computation.221 | loop fusion | flops 131072 | bytes 1572868 | tf_op jit(solution)/shard_map/add | solution.py:55
  73.7 0.5 collective-permute-start.9
  74.2 1.1 %dynamic-slice_add_fusion.1 = f32[128,1024]{1,0:T(8,128)S(1)} fusion(f32[128,1024]{1,0:T(8,128)} %collective-permute-done.4, f32[256,1024]{1,0:T(8,128)S(1)} %bitcast.150, s32[]{:T(128)S(6)} %select_n.63), kind=kLoop, calls=%fused_computation.222 | loop fusion | flops 131072 | bytes 1572868 | tf_op jit(solution)/shard_map/add | solution.py:55
  75.4 1.6 %collective-permute-start.5 = (bf16[64,1024]{1,0:T(8,128)(2,1)S(1)}, bf16[64,1024]{1,0:T(8,128)(2,1)S(1)}, u32[]{:S(2)}, u32[]{:S(2)}) collective-permute-start(bf16[64,1024]{1,0:T(8,128)(2,1)S(1)} %dynamic-slice_convert_fusion.1), channel_id=1, source_target_pairs={{0,2},{1,3},{2,0},{3,1},{4,6},{5,7},{6,4},{7,5},{8,10},{9,11},{10,... | collective-permute-start | bytes 393224 | tf_op jit(solution)/shard_map/ppermute | solution.py:54
  77.0 2.0 %collective-permute-done.9 = bf16[256,256]{1,0:T(8,128)(2,1)S(1)} collective-permute-done((bf16[256,256]{1,0:T(8,128)(2,1)S(1)}, bf16[256,256]{1,0:T(8,128)(2,1)S(1)}, u32[]{:S(2)}, u32[]{:S(2)}) %collective-permute-start.9) | collective-permute-done | bytes 131104 | tf_op jit(solution)/shard_map/ppermute | solution.py:54
  79.0 1.7 %collective-permute-start.10 = (bf16[128,256]{1,0:T(8,128)(2,1)S(1)}, bf16[128,256]{1,0:T(8,128)(2,1)S(1)}, u32[]{:S(2)}, u32[]{:S(2)}) collective-permute-start(bf16[128,256]{1,0:T(8,128)(2,1)S(1)} %dynamic-slice_convert_fusion.2), channel_id=1, source_target_pairs={{0,4},{1,5},{2,6},{3,7},{4,0},{5,1},{6,2},{7,3},{8,12},{9,13},{10,... | collective-permute-start | bytes 196616 | tf_op jit(solution)/shard_map/ppermute | solution.py:54
  80.8 1.3 %collective-permute-start.6 = (bf16[32,1024]{1,0:T(8,128)(2,1)S(1)}, bf16[32,1024]{1,0:T(8,128)(2,1)S(1)}, u32[]{:S(2)}, u32[]{:S(2)}) collective-permute-start(bf16[32,1024]{1,0:T(8,128)(2,1)S(1)} %dynamic-slice_convert_fusion.3), channel_id=1, source_target_pairs={{0,4},{1,5},{2,6},{3,7},{4,0},{5,1},{6,2},{7,3},{8,12},{9,13},{10,... | collective-permute-start | bytes 196616 | tf_op jit(solution)/shard_map/ppermute | solution.py:54
  82.2 1.2 %collective-permute-done.10 = bf16[128,256]{1,0:T(8,128)(2,1)S(1)} collective-permute-done((bf16[128,256]{1,0:T(8,128)(2,1)S(1)}, bf16[128,256]{1,0:T(8,128)(2,1)S(1)}, u32[]{:S(2)}, u32[]{:S(2)}) %collective-permute-start.10) | collective-permute-done | bytes 65568 | tf_op jit(solution)/shard_map/ppermute | solution.py:54
  83.4 3.1 %collective-permute-start.11 = (bf16[64,256]{1,0:T(8,128)(2,1)S(1)}, bf16[64,256]{1,0:T(8,128)(2,1)S(1)}, u32[]{:S(2)}, u32[]{:S(2)}) collective-permute-start(bf16[64,256]{1,0:T(8,128)(2,1)S(1)} %dynamic-slice_convert_fusion.4), channel_id=1, source_target_pairs={{0,8},{1,9},{2,10},{3,11},{4,12},{5,13},{6,14},{7,15},{8,0},{9,1},... | collective-permute-start | bytes 98312 | tf_op jit(solution)/shard_map/ppermute | solution.py:54
  86.6 1.7 %collective-permute-start.7 = (bf16[16,1024]{1,0:T(8,128)(2,1)S(1)}, bf16[16,1024]{1,0:T(8,128)(2,1)S(1)}, u32[]{:S(2)}, u32[]{:S(2)}) collective-permute-start(bf16[16,1024]{1,0:T(8,128)(2,1)S(1)} %dynamic-slice_convert_fusion.5), channel_id=1, source_target_pairs={{0,8},{1,9},{2,10},{3,11},{4,12},{5,13},{6,14},{7,15},{8,0},{9,1},... | collective-permute-start | bytes 98312 | tf_op jit(solution)/shard_map/ppermute | solution.py:54
  88.4 0.6 convert_add_fusion.4
  89.1 2.4 %collective-permute-done.7 = bf16[16,1024]{1,0:T(8,128)(2,1)S(1)} collective-permute-done((bf16[16,1024]{1,0:T(8,128)(2,1)S(1)}, bf16[16,1024]{1,0:T(8,128)(2,1)S(1)}, u32[]{:S(2)}, u32[]{:S(2)}) %collective-permute-start.7) | collective-permute-done | bytes 32800 | tf_op jit(solution)/shard_map/ppermute | solution.py:54
  91.5 0.6 convert_add_fusion.5
  (261 shorter events, 2.0 us)
Async XLA Ops:
  0.6 15.1 %copy-start = (bf16[256,1024]{1,0:T(8,128)(2,1)S(1)}, bf16[256,1024]{1,0:T(8,128)(2,1)}, u32[]{:S(2)}) copy-start(bf16[256,1024]{1,0:T(8,128)(2,1)} %param.12) | copy-start | bytes 1572868
  1.8 6.1 %collective-permute-start = (bf16[3,256,256]{2,1,0:T(8,128)(2,1)S(1)}, bf16[3,256,256]{2,1,0:T(8,128)(2,1)S(1)}, u32[]{:S(2)}, u32[]{:S(2)}) collective-permute-start(bf16[3,256,256]{2,1,0:T(8,128)(2,1)S(1)} %get-tuple-element.66), channel_id=1, source_target_pairs={{0,1},{1,2},{2,3},{3,4},{4,5},{5,6},{6,7},{7,8},{8,9},{9,10},{10,1... | collective-permute-start | bytes 1179656 | tf_op jit(solution)/shard_map/ppermute | solution.py:21
  4.2 5.7 %collective-permute-start.1 = (bf16[3,256,256]{2,1,0:T(8,128)(2,1)S(1)}, bf16[3,256,256]{2,1,0:T(8,128)(2,1)S(1)}, u32[]{:S(2)}, u32[]{:S(2)}) collective-permute-start(bf16[3,256,256]{2,1,0:T(8,128)(2,1)S(1)} %get-tuple-element.65), channel_id=1, source_target_pairs={{1,0},{2,1},{3,2},{4,3},{5,4},{6,5},{7,6},{8,7},{9,8},{10,9},{11,1... | collective-permute-start | bytes 1179656 | tf_op jit(solution)/shard_map/ppermute | solution.py:24
  6.9 7.9 %copy-start.11 = (f32[1,1,256]{2,1,0:T(1,128)}, f32[1,1,256]{2,1,0:T(1,128)S(1)}, u32[]{:S(2)}) copy-start(f32[1,1,256]{2,1,0:T(1,128)S(1)} %get-tuple-element.75) | copy-start | bytes 3076
  6.9 7.9 %copy-start.13 = (f32[1,1,256]{2,1,0:T(1,128)}, f32[1,1,256]{2,1,0:T(1,128)S(1)}, u32[]{:S(2)}) copy-start(f32[1,1,256]{2,1,0:T(1,128)S(1)} %get-tuple-element.76) | copy-start | bytes 3076
  6.9 7.9 %copy-start.15 = (f32[1,1,256]{2,1,0:T(1,128)}, f32[1,1,256]{2,1,0:T(1,128)S(1)}, u32[]{:S(2)}) copy-start(f32[1,1,256]{2,1,0:T(1,128)S(1)} %get-tuple-element.77) | copy-start | bytes 3076
  6.9 7.9 %copy-start.17 = (f32[1,1,256]{2,1,0:T(1,128)}, f32[1,1,256]{2,1,0:T(1,128)S(1)}, u32[]{:S(2)}) copy-start(f32[1,1,256]{2,1,0:T(1,128)S(1)} %get-tuple-element.78) | copy-start | bytes 3076
  6.9 7.9 %copy-start.19 = (f32[1,1,256]{2,1,0:T(1,128)}, f32[1,1,256]{2,1,0:T(1,128)S(1)}, u32[]{:S(2)}) copy-start(f32[1,1,256]{2,1,0:T(1,128)S(1)} %get-tuple-element.79) | copy-start | bytes 3076
  6.9 7.9 %copy-start.21 = (f32[1,1,256]{2,1,0:T(1,128)}, f32[1,1,256]{2,1,0:T(1,128)S(1)}, u32[]{:S(2)}) copy-start(f32[1,1,256]{2,1,0:T(1,128)S(1)} %get-tuple-element.80) | copy-start | bytes 3076
  7.0 7.9 %copy-start.23 = (f32[1,1,256]{2,1,0:T(1,128)}, f32[1,1,256]{2,1,0:T(1,128)S(1)}, u32[]{:S(2)}) copy-start(f32[1,1,256]{2,1,0:T(1,128)S(1)} %get-tuple-element.81) | copy-start | bytes 3076
  7.0 7.9 %copy-start.25 = (f32[1,1,256]{2,1,0:T(1,128)}, f32[1,1,256]{2,1,0:T(1,128)S(1)}, u32[]{:S(2)}) copy-start(f32[1,1,256]{2,1,0:T(1,128)S(1)} %get-tuple-element.82) | copy-start | bytes 3076
  7.0 7.9 %copy-start.27 = (f32[1,1,256]{2,1,0:T(1,128)}, f32[1,1,256]{2,1,0:T(1,128)S(1)}, u32[]{:S(2)}) copy-start(f32[1,1,256]{2,1,0:T(1,128)S(1)} %get-tuple-element.83) | copy-start | bytes 3076
  7.0 7.9 %copy-start.29 = (f32[1,1,256]{2,1,0:T(1,128)}, f32[1,1,256]{2,1,0:T(1,128)S(1)}, u32[]{:S(2)}) copy-start(f32[1,1,256]{2,1,0:T(1,128)S(1)} %get-tuple-element.84) | copy-start | bytes 3076
  7.0 7.9 %copy-start.31 = (f32[1,1,256]{2,1,0:T(1,128)}, f32[1,1,256]{2,1,0:T(1,128)S(1)}, u32[]{:S(2)}) copy-start(f32[1,1,256]{2,1,0:T(1,128)S(1)} %get-tuple-element.85) | copy-start | bytes 3076
  7.0 7.9 %copy-start.33 = (f32[1,1,256]{2,1,0:T(1,128)}, f32[1,1,256]{2,1,0:T(1,128)S(1)}, u32[]{:S(2)}) copy-start(f32[1,1,256]{2,1,0:T(1,128)S(1)} %get-tuple-element.105) | copy-start | bytes 3076
  7.0 7.9 %copy-start.35 = (f32[1,1,256]{2,1,0:T(1,128)}, f32[1,1,256]{2,1,0:T(1,128)S(1)}, u32[]{:S(2)}) copy-start(f32[1,1,256]{2,1,0:T(1,128)S(1)} %get-tuple-element.106) | copy-start | bytes 3076
  7.1 7.9 %copy-start.37 = (f32[1,1,256]{2,1,0:T(1,128)}, f32[1,1,256]{2,1,0:T(1,128)S(1)}, u32[]{:S(2)}) copy-start(f32[1,1,256]{2,1,0:T(1,128)S(1)} %get-tuple-element.107) | copy-start | bytes 3076
  7.1 7.9 %copy-start.39 = (f32[1,1,256]{2,1,0:T(1,128)}, f32[1,1,256]{2,1,0:T(1,128)S(1)}, u32[]{:S(2)}) copy-start(f32[1,1,256]{2,1,0:T(1,128)S(1)} %get-tuple-element.108) | copy-start | bytes 3076
  7.1 7.9 %copy-start.41 = (f32[1,1,256]{2,1,0:T(1,128)}, f32[1,1,256]{2,1,0:T(1,128)S(1)}, u32[]{:S(2)}) copy-start(f32[1,1,256]{2,1,0:T(1,128)S(1)} %get-tuple-element.109) | copy-start | bytes 3076
  7.1 7.9 %copy-start.43 = (f32[1,1,256]{2,1,0:T(1,128)}, f32[1,1,256]{2,1,0:T(1,128)S(1)}, u32[]{:S(2)}) copy-start(f32[1,1,256]{2,1,0:T(1,128)S(1)} %get-tuple-element.110) | copy-start | bytes 3076
  7.1 7.9 %copy-start.45 = (f32[1,1,256]{2,1,0:T(1,128)}, f32[1,1,256]{2,1,0:T(1,128)S(1)}, u32[]{:S(2)}) copy-start(f32[1,1,256]{2,1,0:T(1,128)S(1)} %get-tuple-element.111) | copy-start | bytes 3076
  7.1 7.9 %copy-start.47 = (f32[1,1,256]{2,1,0:T(1,128)}, f32[1,1,256]{2,1,0:T(1,128)S(1)}, u32[]{:S(2)}) copy-start(f32[1,1,256]{2,1,0:T(1,128)S(1)} %get-tuple-element.112) | copy-start | bytes 3076
  7.1 7.9 %copy-start.49 = (f32[1,1,256]{2,1,0:T(1,128)}, f32[1,1,256]{2,1,0:T(1,128)S(1)}, u32[]{:S(2)}) copy-start(f32[1,1,256]{2,1,0:T(1,128)S(1)} %get-tuple-element.113) | copy-start | bytes 3076
  7.1 7.9 %copy-start.51 = (f32[1,1,256]{2,1,0:T(1,128)}, f32[1,1,256]{2,1,0:T(1,128)S(1)}, u32[]{:S(2)}) copy-start(f32[1,1,256]{2,1,0:T(1,128)S(1)} %get-tuple-element.114) | copy-start | bytes 3076
  7.1 7.9 %copy-start.53 = (f32[1,1,256]{2,1,0:T(1,128)}, f32[1,1,256]{2,1,0:T(1,128)S(1)}, u32[]{:S(2)}) copy-start(f32[1,1,256]{2,1,0:T(1,128)S(1)} %get-tuple-element.115) | copy-start | bytes 3076
  7.7 7.3 %copy-start.63 = (f32[1,1,256]{2,1,0:T(1,128)}, f32[1,1,256]{2,1,0:T(1,128)S(1)}, u32[]{:S(2)}) copy-start(f32[1,1,256]{2,1,0:T(1,128)S(1)} %get-tuple-element.90) | copy-start | bytes 3076
  7.7 7.3 %copy-start.65 = (f32[1,1,256]{2,1,0:T(1,128)}, f32[1,1,256]{2,1,0:T(1,128)S(1)}, u32[]{:S(2)}) copy-start(f32[1,1,256]{2,1,0:T(1,128)S(1)} %get-tuple-element.91) | copy-start | bytes 3076
  7.8 7.3 %copy-start.67 = (f32[1,1,256]{2,1,0:T(1,128)}, f32[1,1,256]{2,1,0:T(1,128)S(1)}, u32[]{:S(2)}) copy-start(f32[1,1,256]{2,1,0:T(1,128)S(1)} %get-tuple-element.92) | copy-start | bytes 3076
  7.8 7.3 %copy-start.69 = (f32[1,1,256]{2,1,0:T(1,128)}, f32[1,1,256]{2,1,0:T(1,128)S(1)}, u32[]{:S(2)}) copy-start(f32[1,1,256]{2,1,0:T(1,128)S(1)} %get-tuple-element.93) | copy-start | bytes 3076
  7.8 7.3 %copy-start.71 = (f32[1,1,256]{2,1,0:T(1,128)}, f32[1,1,256]{2,1,0:T(1,128)S(1)}, u32[]{:S(2)}) copy-start(f32[1,1,256]{2,1,0:T(1,128)S(1)} %get-tuple-element.94) | copy-start | bytes 3076
  7.8 7.3 %copy-start.73 = (f32[1,1,256]{2,1,0:T(1,128)}, f32[1,1,256]{2,1,0:T(1,128)S(1)}, u32[]{:S(2)}) copy-start(f32[1,1,256]{2,1,0:T(1,128)S(1)} %get-tuple-element.95) | copy-start | bytes 3076
  25.3 14.2 %collective-permute-start.12 = (f32[51,256]{1,0:T(8,128)S(1)}, f32[51,256]{1,0:T(8,128)S(1)}, u32[]{:S(2)}, u32[]{:S(2)}) collective-permute-start(f32[51,256]{1,0:T(8,128)S(1)} %concatenate.11), channel_id=1, source_target_pairs={{0,1},{1,0},{2,3},{3,2},{4,5},{5,4},{6,7},{7,6},{8,9},{9,8},{10,11... | collective-permute-start | bytes 156680 | tf_op jit(solution)/shard_map/ppermute | solution.py:54
  34.5 37.8 %collective-permute-start.8 = (f32[512,256]{1,0:T(8,128)}, f32[512,256]{1,0:T(8,128)}, u32[]{:S(2)}, u32[]{:S(2)}) collective-permute-start(f32[512,256]{1,0:T(8,128)} %constant_dynamic-slice_fusion), channel_id=1, source_target_pairs={{0,1},{1,0},{2,3},{3,2},{4,5},{5,4},{6,7},{7,6},{8,9},{9,8},{10,11... | collective-permute-start | bytes 1572872 | tf_op jit(solution)/shard_map/ppermute | solution.py:54
  35.6 26.6 %collective-permute-start.2 = (bf16[3,256,256]{2,1,0:T(8,128)(2,1)S(1)}, bf16[3,256,256]{2,1,0:T(8,128)(2,1)S(1)}, u32[]{:S(2)}, u32[]{:S(2)}) collective-permute-start(bf16[3,256,256]{2,1,0:T(8,128)(2,1)S(1)} %get-tuple-element.63), channel_id=1, source_target_pairs={{0,1},{1,2},{2,3},{3,4},{4,5},{5,6},{6,7},{7,8},{8,9},{9,10},{10,1... | collective-permute-start | bytes 1179656 | tf_op jit(solution)/shard_map/ppermute | solution.py:21
  38.0 24.1 %collective-permute-start.3 = (bf16[3,256,256]{2,1,0:T(8,128)(2,1)S(1)}, bf16[3,256,256]{2,1,0:T(8,128)(2,1)S(1)}, u32[]{:S(2)}, u32[]{:S(2)}) collective-permute-start(bf16[3,256,256]{2,1,0:T(8,128)(2,1)S(1)} %get-tuple-element.64), channel_id=1, source_target_pairs={{1,0},{2,1},{3,2},{4,3},{5,4},{6,5},{7,6},{8,7},{9,8},{10,9},{11,1... | collective-permute-start | bytes 1179656 | tf_op jit(solution)/shard_map/ppermute | solution.py:24
  39.5 11.0 %collective-permute-start.13 = (f32[51,256]{1,0:T(8,128)S(1)}, f32[51,256]{1,0:T(8,128)S(1)}, u32[]{:S(2)}, u32[]{:S(2)}) collective-permute-start(f32[51,256]{1,0:T(8,128)S(1)} %add.554), channel_id=1, source_target_pairs={{0,2},{1,3},{2,0},{3,1},{4,6},{5,7},{6,4},{7,5},{8,10},{9,11},{10,... | collective-permute-start | bytes 156680 | tf_op jit(solution)/shard_map/ppermute | solution.py:54
  45.6 13.8 %copy-start.91 = (f32[256]{0:T(256)S(1)}, f32[256]{0:T(256)}, u32[]{:S(2)}) copy-start(f32[256]{0:T(256)} %param.14) | copy-start | bytes 3076
  45.6 16.6 %copy-start.3 = (bf16[4,256,256]{2,1,0:T(8,128)(2,1)S(1)}, bf16[4,256,256]{2,1,0:T(8,128)(2,1)}, u32[]{:S(2)}) copy-start(bf16[4,256,256]{2,1,0:T(8,128)(2,1)} %copy-done.2) | copy-start | bytes 1572868
  45.7 16.4 %copy-start.5 = (f32[2,2,2,2,16,1024]{5,4,3,2,1,0:T(8,128)}, f32[2,2,2,2,16,1024]{5,4,3,2,1,0:T(8,128)S(1)}, u32[]{:S(2)}) copy-start(f32[2,2,2,2,16,1024]{5,4,3,2,1,0:T(8,128)S(1)} %copy.16) | copy-start | bytes 3145732
  50.6 5.7 %collective-permute-start.14 = (f32[51,256]{1,0:T(8,128)S(1)}, f32[51,256]{1,0:T(8,128)S(1)}, u32[]{:S(2)}, u32[]{:S(2)}) collective-permute-start(f32[51,256]{1,0:T(8,128)S(1)} %add.555), channel_id=1, source_target_pairs={{0,4},{1,5},{2,6},{3,7},{4,0},{5,1},{6,2},{7,3},{8,12},{9,13},{10,... | collective-permute-start | bytes 156680 | tf_op jit(solution)/shard_map/ppermute | solution.py:54
  54.9 19.3 %collective-permute-start.4 = (f32[128,1024]{1,0:T(8,128)}, f32[128,1024]{1,0:T(8,128)}, u32[]{:S(2)}, u32[]{:S(2)}) collective-permute-start(f32[128,1024]{1,0:T(8,128)} %constant_dynamic-slice_fusion.1), channel_id=1, source_target_pairs={{0,1},{1,0},{2,3},{3,2},{4,5},{5,4},{6,7},{7,6},{8,9},{9,8},{10,11... | collective-permute-start | bytes 1572872 | tf_op jit(solution)/shard_map/ppermute | solution.py:54
  56.2 5.2 %collective-permute-start.15 = (f32[51,256]{1,0:T(8,128)S(1)}, f32[51,256]{1,0:T(8,128)S(1)}, u32[]{:S(2)}, u32[]{:S(2)}) collective-permute-start(f32[51,256]{1,0:T(8,128)S(1)} %add.556), channel_id=1, source_target_pairs={{0,8},{1,9},{2,10},{3,11},{4,12},{5,13},{6,14},{7,15},{8,0},{9,1},... | collective-permute-start | bytes 156680 | tf_op jit(solution)/shard_map/ppermute | solution.py:54
  73.7 5.3 %collective-permute-start.9 = (bf16[256,256]{1,0:T(8,128)(2,1)S(1)}, bf16[256,256]{1,0:T(8,128)(2,1)S(1)}, u32[]{:S(2)}, u32[]{:S(2)}) collective-permute-start(bf16[256,256]{1,0:T(8,128)(2,1)S(1)} %dynamic-slice_convert_fusion), channel_id=1, source_target_pairs={{0,2},{1,3},{2,0},{3,1},{4,6},{5,7},{6,4},{7,5},{8,10},{9,11},{10,... | collective-permute-start | bytes 393224 | tf_op jit(solution)/shard_map/ppermute | solution.py:54
  75.4 5.4 %collective-permute-start.5 = (bf16[64,1024]{1,0:T(8,128)(2,1)S(1)}, bf16[64,1024]{1,0:T(8,128)(2,1)S(1)}, u32[]{:S(2)}, u32[]{:S(2)}) collective-permute-start(bf16[64,1024]{1,0:T(8,128)(2,1)S(1)} %dynamic-slice_convert_fusion.1), channel_id=1, source_target_pairs={{0,2},{1,3},{2,0},{3,1},{4,6},{5,7},{6,4},{7,5},{8,10},{9,11},{10,... | collective-permute-start | bytes 393224 | tf_op jit(solution)/shard_map/ppermute | solution.py:54
  79.0 4.4 %collective-permute-start.10 = (bf16[128,256]{1,0:T(8,128)(2,1)S(1)}, bf16[128,256]{1,0:T(8,128)(2,1)S(1)}, u32[]{:S(2)}, u32[]{:S(2)}) collective-permute-start(bf16[128,256]{1,0:T(8,128)(2,1)S(1)} %dynamic-slice_convert_fusion.2), channel_id=1, source_target_pairs={{0,4},{1,5},{2,6},{3,7},{4,0},{5,1},{6,2},{7,3},{8,12},{9,13},{10,... | collective-permute-start | bytes 196616 | tf_op jit(solution)/shard_map/ppermute | solution.py:54
  80.8 5.7 %collective-permute-start.6 = (bf16[32,1024]{1,0:T(8,128)(2,1)S(1)}, bf16[32,1024]{1,0:T(8,128)(2,1)S(1)}, u32[]{:S(2)}, u32[]{:S(2)}) collective-permute-start(bf16[32,1024]{1,0:T(8,128)(2,1)S(1)} %dynamic-slice_convert_fusion.3), channel_id=1, source_target_pairs={{0,4},{1,5},{2,6},{3,7},{4,0},{5,1},{6,2},{7,3},{8,12},{9,13},{10,... | collective-permute-start | bytes 196616 | tf_op jit(solution)/shard_map/ppermute | solution.py:54
  83.4 5.0 %collective-permute-start.11 = (bf16[64,256]{1,0:T(8,128)(2,1)S(1)}, bf16[64,256]{1,0:T(8,128)(2,1)S(1)}, u32[]{:S(2)}, u32[]{:S(2)}) collective-permute-start(bf16[64,256]{1,0:T(8,128)(2,1)S(1)} %dynamic-slice_convert_fusion.4), channel_id=1, source_target_pairs={{0,8},{1,9},{2,10},{3,11},{4,12},{5,13},{6,14},{7,15},{8,0},{9,1},... | collective-permute-start | bytes 98312 | tf_op jit(solution)/shard_map/ppermute | solution.py:54
  86.6 4.9 %collective-permute-start.7 = (bf16[16,1024]{1,0:T(8,128)(2,1)S(1)}, bf16[16,1024]{1,0:T(8,128)(2,1)S(1)}, u32[]{:S(2)}, u32[]{:S(2)}) collective-permute-start(bf16[16,1024]{1,0:T(8,128)(2,1)S(1)} %dynamic-slice_convert_fusion.5), channel_id=1, source_target_pairs={{0,8},{1,9},{2,10},{3,11},{4,12},{5,13},{6,14},{7,15},{8,0},{9,1},... | collective-permute-start | bytes 98312 | tf_op jit(solution)/shard_map/ppermute | solution.py:54
  (79 other events, 243.4 us)

commit v8 on v7

--- a/solution.py
+++ b/solution.py
@@ -57,6 +57,15 @@
     return parts, whole
 
 
+def halo_rows(block, axis, width):
+    count = lax.axis_size(axis)
+    forward = [(i, i + 1) for i in range(count - 1)]
+    backward = [(target, source) for source, target in forward]
+    low = lax.ppermute(lax.slice_in_dim(block, block.shape[0] - width, None, axis=0), axis, forward)
+    high = lax.ppermute(lax.slice_in_dim(block, 0, width, axis=0), axis, backward)
+    return low, high
+
+
 def gelu_value(inputs):
     tangent = jnp.tanh(ROOT_TWO_PI * (inputs + CUBIC_TERM * inputs * inputs * inputs))
     return 0.5 * inputs * (1.0 + tangent)
@@ -146,12 +155,40 @@
     kernel_grad = kernel_terms(window, grad_tile.astype(jnp.float32), image_rows, TILE_COLS)
     packed = jnp.concatenate([kernel_grad, gain_grad[None], scale_grad[None]], axis=0)
     (grad_w_in, grad_w_out), small_grads = halving_reduce([partial_in, partial_out], packed, "row")
+    flipped = kernel[::-1, ::-1]
+    tile_padded = jnp.pad(
+        grad_tile.astype(jnp.float32),
+        ((half_width, half_width), (2 * half_width, 2 * half_width), (0, 0)),
+    )
+    own = depthwise(tile_padded, flipped, image_rows, span)
+    own_full = lax.dynamic_update_slice_in_dim(
+        jnp.zeros((image_rows, image_cols + 2 * half_width, channels), jnp.float32),
+        own,
+        first_col,
+        axis=1,
+    )[:, half_width : half_width + image_cols]
     grad_conv = lax.dynamic_update_slice_in_dim(
         jnp.zeros_like(image), grad_tile, first_col, axis=1
     )
-    grad_ext = padded_2(grad_conv, (("row", 0),), half_width)
-    grad_padded = jnp.pad(grad_ext.astype(jnp.float32), ((0, 0), (half_width, half_width), (0, 0)))
-    conv_back = depthwise(grad_padded, kernel[::-1, ::-1], image_rows, image_cols)
+    low, high = halo_rows(grad_conv, "row", half_width)
+    edge = ((0, 0), (half_width, half_width), (0, 0))
+    low = jnp.pad(low.astype(jnp.float32), edge)
+    high = jnp.pad(high.astype(jnp.float32), edge)
+    halo_out = []
+    for out_row in range(image_rows):
+        total = jnp.zeros((image_cols, channels), jnp.float32)
+        for row_tap in range(KERNEL):
+            source = out_row + row_tap
+            if source < half_width:
+                line = low[source]
+            elif source >= half_width + image_rows:
+                line = high[source - half_width - image_rows]
+            else:
+                continue
+            for col_tap in range(KERNEL):
+                total = total + line[col_tap : col_tap + image_cols] * flipped[row_tap, col_tap]
+        halo_out.append(total)
+    conv_back = own_full + jnp.stack(halo_out)
     grad_image = (cotangent.astype(jnp.float32) + conv_back).astype(jnp.bfloat16)
     return (block_out, grad_image, grad_w_in, grad_w_out, small_grads)
 

time: 92.5 us -> 88.4 us (0.956)
  starting transfers between devices: 34.7 us -> 29.2 us
  local copies, waits for them, and re-layouts: 7.26 us -> 11.5 us
  waiting for transfers between devices: 15.6 us -> 12.3 us
    convert_element_type x1, other arithmetic: 9.56 us -> 1.07 us  [shards(): (cotangent.astype(jnp.float32) + conv_back).astype(jnp.bfloat16)]
    add x0 -> x5, other arithmetic: none -> 6.77 us  [the longest x1 4.1 us: depthwise(): total + padded[row_tap:row_tap + image_rows, col_tap:col_tap + image_cols...]
    ppermute x12, starting transfers between devices: 27.1 us -> 21.6 us  [halving_reduce(): got, got_whole = lax.ppermute((gives, whole), axis, pairs)]
    ppermute x0 -> x2, starting transfers between devices: none -> 3.85 us  [the longest x1 2.57 us: halo_rows(): lax.ppermute(lax.slice_in_dim(block, block.shape[0] - width, None, axis=0...]
    ppermute x12, waiting for transfers between devices: 13.5 us -> 10.2 us  [halving_reduce(): got, got_whole = lax.ppermute((gives, whole), axis, pairs)]
    dynamic_update_slice x1, local copies, waits for them, and re-layouts: 0.02 us -> 3.29 us  [shards(): lax.dynamic_update_slice_in_dim(jnp.zeros((image_rows, image_cols + 2 * h...]
    ppermute x2 -> x1, starting transfers between devices: 4.81 us -> 2.38 us  [padded_2(): lax.ppermute(lax.slice_in_dim(block, block.shape[dim] - width, None, axis...]
    convert_element_type x1 -> x2, other arithmetic: 0.2 us -> 2.12 us  [the longest x1 1.06 us: shards(): low = jnp.pad(low.astype(jnp.float32), edge)]
  transfers between devices with their start and end apart: 16 -> 16, of which waited for: 8 -> 8; matrix products, arithmetic and copies ran while one was open for 23% -> 29% of each run, Pallas kernels for 0% -> 0%
where the time goes in v8:
time: 88.4 us; the launch traced here: 87.8 us
  starting transfers between devices  29.2 us (33%)
  other arithmetic  24.6 us (28%)
  waiting for transfers between devices  12.3 us (14%)
  local copies, waits for them, and re-layouts  11.5 us (13%)
  matrix products  6.74 us (8%)
  between operations  3.52 us (4%)
    ppermute x12, starting transfers between devices, halving_reduce(): got, got_whole = lax.ppermute((gives, whole), axis, pairs)  21.6 us
    ppermute x12, waiting for transfers between devices, halving_reduce(): got, got_whole = lax.ppermute((gives, whole), axis, pairs)  10.2 us
    reduce_sum x1, other arithmetic, shards(): centre = jnp.mean(filtered, axis=-1, keepdims=True)  4.54 us
    add x1, other arithmetic, depthwise(): total + padded[row_tap:row_tap + image_rows, col_tap:col_tap + image_cols...  4.1 us
    add x8, other arithmetic, halving_reduce(): parts = [k + g.astype(jnp.float32) for k, g in zip(keeps, got)]  3.58 us
    dynamic_update_slice x1, local copies, waits for them, and re-layouts, shards(): lax.dynamic_update_slice_in_dim(jnp.zeros((image_rows, image_cols + 2 * h...  3.29 us
    reduce_sum x3, other arithmetic, kernel_terms(): jnp.sum(padded[row_tap:row_tap + image_rows, col_tap:col_tap + image_cols...  3.28 us
    unnamed x249, local copies, waits for them, and re-layouts  2.78 us
  transfers between devices with their start and end apart: 16, of which 8 were waited for; matrix products, arithmetic and copies ran while one was open for 29% of the time, Pallas kernels for 0%

profile of v8, /device:TPU:0, one launch (start us, length us, event | category | flops | bytes accessed | tf_op | source)
XLA Modules:
  0.0 87.8 jit_solution(7036700708693839087)
XLA Ops:
  0.7 1.1 %copy.25 = bf16[4,256,256]{2,1,0:T(8,128)(2,1)S(1)} copy(bf16[4,256,256]{2,1,0:T(8,128)(2,1)} %param.8) | data formatting | bytes 1048576
  1.8 2.4 %collective-permute-start = (bf16[3,256,256]{2,1,0:T(8,128)(2,1)S(1)}, bf16[3,256,256]{2,1,0:T(8,128)(2,1)S(1)}, u32[]{:S(2)}, u32[]{:S(2)}) collective-permute-start(bf16[3,256,256]{2,1,0:T(8,128)(2,1)S(1)} %get-tuple-element.66), channel_id=1, source_target_pairs={{0,1},{1,2},{2,3},{3,4},{4,5},{5,6},{6,7},{7,8},{8,9},{9,10},{10,1... | collective-permute-start | bytes 1179656 | tf_op jit(solution)/shard_map/ppermute | solution.py:21
  4.2 1.3 %collective-permute-start.1 = (bf16[3,256,256]{2,1,0:T(8,128)(2,1)S(1)}, bf16[3,256,256]{2,1,0:T(8,128)(2,1)S(1)}, u32[]{:S(2)}, u32[]{:S(2)}) collective-permute-start(bf16[3,256,256]{2,1,0:T(8,128)(2,1)S(1)} %get-tuple-element.65), channel_id=1, source_target_pairs={{1,0},{2,1},{3,2},{4,3},{5,4},{6,5},{7,6},{8,7},{9,8},{10,9},{11,1... | collective-permute-start | bytes 1179656 | tf_op jit(solution)/shard_map/ppermute | solution.py:24
  5.5 0.7 bitcast_reduce_fusion
  7.9 2.0 %collective-permute-done.1 = bf16[3,256,256]{2,1,0:T(8,128)(2,1)S(1)} collective-permute-done((bf16[3,256,256]{2,1,0:T(8,128)(2,1)S(1)}, bf16[3,256,256]{2,1,0:T(8,128)(2,1)S(1)}, u32[]{:S(2)}, u32[]{:S(2)}) %collective-permute-start.1) | collective-permute-done | bytes 393248 | tf_op jit(solution)/shard_map/ppermute | solution.py:24
  10.3 4.5 %fusion.211 = (f32[4,128]{1,0:T(4,128)S(1)}, f32[4,128,256]{2,1,0:T(8,128)S(1)}) fusion(f32[256]{0:T(256)S(1)} %bitcast.213, f32[10,134,256]{2,1,0:T(8,128)S(1)} %fusion.22, f32[256]{0:T(256)S(1)} %bitcast.218, f32[256]{0:T(256)S(1)} %bitcast.163, f32[256]{0:T(256)S(1)} %bitcast.168, f32[256]{0:T(256)S(1)} %bitcast.173, f32[256]{0:T(256)S(1)} %bitcast.178, ...), kind=kLoop, calls=%fused_computation.388 | loop fusion | flops 12844544 | bytes 26266624 | tf_op jit(solution)/shard_map/reduce_sum | solution.py:117
  15.7 1.8 %fusion.11 = (bf16[1024,512]{0,1:T(8,128)(2,1)}, f32[512,1024]{1,0:T(8,128)S(1)}) fusion(bf16[512,256]{1,0:T(8,128)(2,1)S(1)} %bitcast.156, bf16[256,1024]{1,0:T(8,128)(2,1)S(1)} %copy-done), kind=kOutput, calls=%fused_computation.112 | convolution fusion | flops 273154048 | bytes 3932160 | tf_op jit(solution)/shard_map/dot_general | solution.py:127
  17.6 0.8 fusion.123
  18.4 1.4 %fusion.6 = bf16[512,1024]{1,0:T(8,128)(2,1)S(1)} fusion(f32[512,1024]{1,0:T(8,128)S(1)} %get-tuple-element.122, bf16[512,256]{1,0:T(8,128)(2,1)S(1)} %bitcast.153, bf16[1024,256]{1,0:T(8,128)(2,1)S(1)} %copy-done.7), kind=kOutput, calls=%fused_computation.107 | convolution fusion | flops 278396928 | bytes 3932160 | tf_op jit(solution)/shard_map/dot_general | solution.py:130
  20.8 1.3 %fusion.170 = (f32[256]{0:T(256)S(1)}, f32[256]{0:T(256)S(1)}, f32[256]{0:T(256)S(1)}, f32[256]{0:T(256)S(1)}, f32[256]{0:T(256)S(1)}, /*index=5*/f32[256]{0:T(2...) fusion(f32[10,134,256]{2,1,0:T(8,128)S(1)} %fusion.22, ...), kind=kLoop, calls=%fused_computation.282 | loop fusion | flops 4584192 | bytes 8148992 | tf_op jit(solution)/shard_map/reduce_sum | solution.py:98
  22.0 1.0 %fusion.171 = (f32[256]{0:T(256)S(1)}, f32[256]{0:T(256)S(1)}, f32[256]{0:T(256)S(1)}, f32[256]{0:T(256)S(1)}, f32[256]{0:T(256)S(1)}, /*index=5*/f32[256]{0:T(2...) fusion(bf16[4,128,256]{2,1,0:T(8,128)(2,1)S(1)} %get-tuple-elem, ...), kind=kLoop, calls=%fused_computation.283 | loop fusion | flops 4845056 | bytes 9717760 | tf_op jit(solution)/shard_map/reduce_sum | solution.py:98
  23.0 1.0 %fusion.172 = (f32[256]{0:T(256)S(1)}, f32[256]{0:T(256)S(1)}, f32[256]{0:T(256)S(1)}, f32[256]{0:T(256)S(1)}, f32[256]{0:T(256)S(1)}, /*index=5*/f32[256]{0:T(2...) fusion(bf16[4,128,256]{2,1,0:T(8,128)(2,1)S(1)} %get-tuple-elem, ...), kind=kLoop, calls=%fused_computation.284 | loop fusion | flops 4845056 | bytes 9717760 | tf_op jit(solution)/shard_map/reduce_sum | solution.py:98
  24.2 6.0 %collective-permute-start.12 = (f32[51,256]{1,0:T(8,128)S(1)}, f32[51,256]{1,0:T(8,128)S(1)}, u32[]{:S(2)}, u32[]{:S(2)}) collective-permute-start(f32[51,256]{1,0:T(8,128)S(1)} %concatenate.7), channel_id=1, source_target_pairs={{0,1},{1,0},{2,3},{3,2},{4,5},{5,4},{6,7},{7,6},{8,9},{9,8},{10,11... | collective-permute-start | bytes 156680 | tf_op jit(solution)/shard_map/ppermute | solution.py:54
  30.3 1.5 %copy.17 = bf16[1024,512]{1,0:T(8,128)(2,1)S(1)} copy(bf16[1024,512]{0,1:T(8,128)(2,1)} %get-tuple-element.121) | data formatting | bytes 2097152 | tf_op jit(solution)/shard_map/convert_element_type | solution.py:128
  32.3 1.0 %copy-done.2 = f32[2,2,2,2,64,256]{5,4,3,2,1,0:T(8,128)} copy-done((f32[2,2,2,2,64,256]{5,4,3,2,1,0:T(8,128)}, f32[2,2,2,2,64,256]{5,4,3,2,1,0:T(8,128)S(1)}, u32[]{:S(2)}) %copy-start.2) | copy-done | bytes 1048600
  33.3 0.8 constant_dynamic-slice_fusion
  34.3 1.7 %convolution_bitcast_fusion.1 = f32[2,2,2,2,16,1024]{5,4,0,1,2,3:T(8,128)S(1)} fusion(bf16[2,2,2,2,16,512]{5,4,3,2,1,0:T(8,128)(2,1)S(1)} %bitcast.155, bf16[512,1024]{1,0:T(8,128)(2,1)} %copy-done.6), kind=kOutput, calls=%fused_computation.120 | convolution fusion | flops 268435456 | bytes 2359296 | tf_op jit(solution)/shard_map/dot_general | solution.py:133
  36.4 0.8 constant_dynamic-slice_fusion.1
  37.9 2.5 %collective-permute-start.13 = (f32[51,256]{1,0:T(8,128)S(1)}, f32[51,256]{1,0:T(8,128)S(1)}, u32[]{:S(2)}, u32[]{:S(2)}) collective-permute-start(f32[51,256]{1,0:T(8,128)S(1)} %add.963), channel_id=1, source_target_pairs={{0,2},{1,3},{2,0},{3,1},{4,6},{5,7},{6,4},{7,5},{8,10},{9,11},{10,... | collective-permute-start | bytes 156680 | tf_op jit(solution)/shard_map/ppermute | solution.py:54
  40.4 0.9 %fusion.212 = (bf16[3,256,256]{2,1,0:T(8,128)(2,1)}, bf16[3,256,256]{2,1,0:T(8,128)(2,1)}) fusion(bf16[4,256,256]{2,1,0:T(8,128)(2,1)S(1)} %get-tuple-element.67), kind=kLoop, calls=%fused_computation.389 | loop fusion | bytes 1572864 | tf_op jit(solution)/shard_map/slice | solution.py:64
  41.4 2.6 %collective-permute-start.2 = (bf16[3,256,256]{2,1,0:T(8,128)(2,1)}, bf16[3,256,256]{2,1,0:T(8,128)(2,1)}, u32[]{:S(2)}, u32[]{:S(2)}) collective-permute-start(bf16[3,256,256]{2,1,0:T(8,128)(2,1)} %get-tuple-element.63), channel_id=1, source_target_pairs={{0,1},{1,2},{2,3},{3,4},{4,5},{5,6},{6,7},{7,8},{8,9},{9,10},{10,1... | collective-permute-start | bytes 1179656 | tf_op jit(solution)/shard_map/ppermute | solution.py:64
  43.9 1.3 %collective-permute-start.3 = (bf16[3,256,256]{2,1,0:T(8,128)(2,1)}, bf16[3,256,256]{2,1,0:T(8,128)(2,1)}, u32[]{:S(2)}, u32[]{:S(2)}) collective-permute-start(bf16[3,256,256]{2,1,0:T(8,128)(2,1)} %get-tuple-element.64), channel_id=1, source_target_pairs={{1,0},{2,1},{3,2},{4,3},{5,4},{6,5},{7,6},{8,7},{9,8},{10,9},{11,1... | collective-permute-start | bytes 1179656 | tf_op jit(solution)/shard_map/ppermute | solution.py:65
  45.2 4.4 %collective-permute-start.14 = (f32[51,256]{1,0:T(8,128)S(1)}, f32[51,256]{1,0:T(8,128)S(1)}, u32[]{:S(2)}, u32[]{:S(2)}) collective-permute-start(f32[51,256]{1,0:T(8,128)S(1)} %add.964), channel_id=1, source_target_pairs={{0,4},{1,5},{2,6},{3,7},{4,0},{5,1},{6,2},{7,3},{8,12},{9,13},{10,... | collective-permute-start | bytes 156680 | tf_op jit(solution)/shard_map/ppermute | solution.py:54
  50.0 4.1 %fusion.116 = f32[4,134,256]{2,1,0:T(8,128)} fusion(f32[4,128,256]{2,1,0:T(8,128)S(1)} %get-tuple-element.68, f32[256]{0:T(256)S(1)} %bitcast.159, f32[256]{0:T(256)S(1)} %bitcast.224, f32[256]{0:T(256)S(1)} %bitcast.189, f32[256]{0:T(256)S(1)} %bitcast.209, f32[256]{0:T(256)S(1)} %bitcast.204, f32[256]{0:T(256)S(1)} %bitcast.199, f32[256]{0:T(256)S(1)} %bitcast.194, ...), kind=kLoop, calls=%fused_computation.228 | loop fusion | flops 13309952 | bytes 1123328 | tf_op jit(solution)/shard_map/add | solution.py:86
  54.1 2.0 %collective-permute-done.14 = f32[51,256]{1,0:T(8,128)S(1)} collective-permute-done((f32[51,256]{1,0:T(8,128)S(1)}, f32[51,256]{1,0:T(8,128)S(1)}, u32[]{:S(2)}, u32[]{:S(2)}) %collective-permute-start.14) | collective-permute-done | bytes 52256 | tf_op jit(solution)/shard_map/ppermute | solution.py:54
  56.2 2.2 %collective-permute-start.15 = (f32[51,256]{1,0:T(8,128)S(1)}, f32[51,256]{1,0:T(8,128)S(1)}, u32[]{:S(2)}, u32[]{:S(2)}) collective-permute-start(f32[51,256]{1,0:T(8,128)S(1)} %add.965), channel_id=1, source_target_pairs={{0,8},{1,9},{2,10},{3,11},{4,12},{5,13},{6,14},{7,15},{8,0},{9,1},... | collective-permute-start | bytes 156680 | tf_op jit(solution)/shard_map/ppermute | solution.py:54
  58.5 0.8 fusion.173
  59.4 3.3 %dynamic_update_slice.10 = f32[4,262,256]{2,1,0:T(8,128)S(1)} dynamic-update-slice(f32[4,262,256]{2,1,0:T(8,128)S(1)} %broadcast_in_dim.8, f32[4,134,256]{2,1,0:T(8,128)} %fusion.116, s32[]{:T(128)} %constant.23.clone.1, s32[]{:T(128)S(6)} %select_n.63, s32[]{:T(128)} %constant.23.clone.1) | dynamic-update-slice | bytes 1097732 | tf_op jit(solution)/shard_map/dynamic_update_slice | solution.py:164
  63.3 1.1 %convert_element_type.100 = f32[3,256,256]{2,1,0:T(8,128)S(1)} convert(bf16[3,256,256]{2,1,0:T(8,128)(2,1)} %collective-permute-done.2) | non-fusion elementwise | flops 196608 | bytes 1179648 | tf_op jit(solution)/shard_map/convert_element_type | solution.py:175
  64.6 0.7 fusion.195
  65.4 1.1 %convert_element_type.101 = f32[3,256,256]{2,1,0:T(8,128)S(1)} convert(bf16[3,256,256]{2,1,0:T(8,128)(2,1)} %collective-permute-done.3) | non-fusion elementwise | flops 196608 | bytes 1179648 | tf_op jit(solution)/shard_map/convert_element_type | solution.py:176
  66.5 0.7 multiply_add_fusion.4
  67.3 0.7 fusion.177
  68.0 0.7 multiply_add_fusion.3
  68.7 1.1 %fusion.16 = bf16[4,256,256]{2,1,0:T(8,128)(2,1)} fusion(f32[4,262,256]{2,1,0:T(8,128)S(1)} %dynamic_update_slice.10, f32[1,256,256]{2,1,0:T(8,128)S(1)} %fusion.177, f32[1,256,256]{2,1,0:T(8,128)S(1)} %multiply_add_fusion.3, f32[1,256,256]{2,1,0:T(8,128)S(1)} %multiply_add_fusion.4, f32[1,256,256]{2,1,0:T(8,128)S(1)} %fusion.195, ...), kind=kLoop, calls=%fused_computation.126 | loop fusion | flops 1835008 | bytes 3145728 | tf_op jit(solution)/shard_map/convert_element_type | solution.py:192
  69.9 1.1 %dynamic-slice_add_fusion = f32[512,256]{1,0:T(8,128)S(1)} fusion(f32[512,256]{1,0:T(8,128)} %collective-permute-done.8, f32[1024,256]{1,0:T(8,128)S(1)} %bitcast.150, s32[]{:T(128)S(6)} %select_n.72), kind=kLoop, calls=%fused_computation.286 | loop fusion | flops 131072 | bytes 1572868 | tf_op jit(solution)/shard_map/add | solution.py:55
  71.1 1.1 %dynamic-slice_add_fusion.1 = f32[128,1024]{1,0:T(8,128)S(1)} fusion(f32[128,1024]{1,0:T(8,128)} %collective-permute-done.4, f32[256,1024]{1,0:T(8,128)S(1)} %bitcast.148, s32[]{:T(128)S(6)} %select_n.64), kind=kLoop, calls=%fused_computation.287 | loop fusion | flops 131072 | bytes 1572868 | tf_op jit(solution)/shard_map/add | solution.py:55
  72.3 2.1 %collective-permute-start.5 = (bf16[64,1024]{1,0:T(8,128)(2,1)S(1)}, bf16[64,1024]{1,0:T(8,128)(2,1)S(1)}, u32[]{:S(2)}, u32[]{:S(2)}) collective-permute-start(bf16[64,1024]{1,0:T(8,128)(2,1)S(1)} %dynamic-slice_convert_fusion.1), channel_id=1, source_target_pairs={{0,2},{1,3},{2,0},{3,1},{4,6},{5,7},{6,4},{7,5},{8,10},{9,11},{10,... | collective-permute-start | bytes 393224 | tf_op jit(solution)/shard_map/ppermute | solution.py:54
  74.4 1.7 %collective-permute-done.9 = bf16[256,256]{1,0:T(8,128)(2,1)S(1)} collective-permute-done((bf16[256,256]{1,0:T(8,128)(2,1)S(1)}, bf16[256,256]{1,0:T(8,128)(2,1)S(1)}, u32[]{:S(2)}, u32[]{:S(2)}) %collective-permute-start.9) | collective-permute-done | bytes 131104 | tf_op jit(solution)/shard_map/ppermute | solution.py:54
  76.2 1.3 %collective-permute-done.5 = bf16[64,1024]{1,0:T(8,128)(2,1)S(1)} collective-permute-done((bf16[64,1024]{1,0:T(8,128)(2,1)S(1)}, bf16[64,1024]{1,0:T(8,128)(2,1)S(1)}, u32[]{:S(2)}, u32[]{:S(2)}) %collective-permute-start.5) | collective-permute-done | bytes 131104 | tf_op jit(solution)/shard_map/ppermute | solution.py:54
  77.6 0.8 collective-permute-start.6
  78.4 2.1 %collective-permute-done.10 = bf16[128,256]{1,0:T(8,128)(2,1)S(1)} collective-permute-done((bf16[128,256]{1,0:T(8,128)(2,1)S(1)}, bf16[128,256]{1,0:T(8,128)(2,1)S(1)}, u32[]{:S(2)}, u32[]{:S(2)}) %collective-permute-start.10) | collective-permute-done | bytes 65568 | tf_op jit(solution)/shard_map/ppermute | solution.py:54
  80.5 1.2 %collective-permute-start.11 = (bf16[64,256]{1,0:T(8,128)(2,1)S(1)}, bf16[64,256]{1,0:T(8,128)(2,1)S(1)}, u32[]{:S(2)}, u32[]{:S(2)}) collective-permute-start(bf16[64,256]{1,0:T(8,128)(2,1)S(1)} %dynamic-slice_convert_fusion.4), channel_id=1, source_target_pairs={{0,8},{1,9},{2,10},{3,11},{4,12},{5,13},{6,14},{7,15},{8,0},{9,1},... | collective-permute-start | bytes 98312 | tf_op jit(solution)/shard_map/ppermute | solution.py:54
  81.9 1.7 %collective-permute-start.7 = (bf16[16,1024]{1,0:T(8,128)(2,1)S(1)}, bf16[16,1024]{1,0:T(8,128)(2,1)S(1)}, u32[]{:S(2)}, u32[]{:S(2)}) collective-permute-start(bf16[16,1024]{1,0:T(8,128)(2,1)S(1)} %dynamic-slice_convert_fusion.5), channel_id=1, source_target_pairs={{0,8},{1,9},{2,10},{3,11},{4,12},{5,13},{6,14},{7,15},{8,0},{9,1},... | collective-permute-start | bytes 98312 | tf_op jit(solution)/shard_map/ppermute | solution.py:54
  83.6 1.8 %collective-permute-done.11 = bf16[64,256]{1,0:T(8,128)(2,1)S(1)} collective-permute-done((bf16[64,256]{1,0:T(8,128)(2,1)S(1)}, bf16[64,256]{1,0:T(8,128)(2,1)S(1)}, u32[]{:S(2)}, u32[]{:S(2)}) %collective-permute-start.11) | collective-permute-done | bytes 32800 | tf_op jit(solution)/shard_map/ppermute | solution.py:54
  85.4 0.6 convert_add_fusion.4
  86.0 1.1 %collective-permute-done.7 = bf16[16,1024]{1,0:T(8,128)(2,1)S(1)} collective-permute-done((bf16[16,1024]{1,0:T(8,128)(2,1)S(1)}, bf16[16,1024]{1,0:T(8,128)(2,1)S(1)}, u32[]{:S(2)}, u32[]{:S(2)}) %collective-permute-start.7) | collective-permute-done | bytes 32800 | tf_op jit(solution)/shard_map/ppermute | solution.py:54
  87.2 0.6 convert_add_fusion.5
  (295 shorter events, 5.8 us)
Async XLA Ops:
  0.6 15.1 %copy-start = (bf16[256,1024]{1,0:T(8,128)(2,1)S(1)}, bf16[256,1024]{1,0:T(8,128)(2,1)}, u32[]{:S(2)}) copy-start(bf16[256,1024]{1,0:T(8,128)(2,1)} %param.12) | copy-start | bytes 1572868
  1.8 6.1 %collective-permute-start = (bf16[3,256,256]{2,1,0:T(8,128)(2,1)S(1)}, bf16[3,256,256]{2,1,0:T(8,128)(2,1)S(1)}, u32[]{:S(2)}, u32[]{:S(2)}) collective-permute-start(bf16[3,256,256]{2,1,0:T(8,128)(2,1)S(1)} %get-tuple-element.66), channel_id=1, source_target_pairs={{0,1},{1,2},{2,3},{3,4},{4,5},{5,6},{6,7},{7,8},{8,9},{9,10},{10,1... | collective-permute-start | bytes 1179656 | tf_op jit(solution)/shard_map/ppermute | solution.py:21
  4.2 5.7 %collective-permute-start.1 = (bf16[3,256,256]{2,1,0:T(8,128)(2,1)S(1)}, bf16[3,256,256]{2,1,0:T(8,128)(2,1)S(1)}, u32[]{:S(2)}, u32[]{:S(2)}) collective-permute-start(bf16[3,256,256]{2,1,0:T(8,128)(2,1)S(1)} %get-tuple-element.65), channel_id=1, source_target_pairs={{1,0},{2,1},{3,2},{4,3},{5,4},{6,5},{7,6},{8,7},{9,8},{10,9},{11,1... | collective-permute-start | bytes 1179656 | tf_op jit(solution)/shard_map/ppermute | solution.py:24
  24.2 13.7 %collective-permute-start.12 = (f32[51,256]{1,0:T(8,128)S(1)}, f32[51,256]{1,0:T(8,128)S(1)}, u32[]{:S(2)}, u32[]{:S(2)}) collective-permute-start(f32[51,256]{1,0:T(8,128)S(1)} %concatenate.7), channel_id=1, source_target_pairs={{0,1},{1,0},{2,3},{3,2},{4,5},{5,4},{6,7},{7,6},{8,9},{9,8},{10,11... | collective-permute-start | bytes 156680 | tf_op jit(solution)/shard_map/ppermute | solution.py:54
  34.1 35.6 %collective-permute-start.8 = (f32[512,256]{1,0:T(8,128)}, f32[512,256]{1,0:T(8,128)}, u32[]{:S(2)}, u32[]{:S(2)}) collective-permute-start(f32[512,256]{1,0:T(8,128)} %constant_dynamic-slice_fusion), channel_id=1, source_target_pairs={{0,1},{1,0},{2,3},{3,2},{4,5},{5,4},{6,7},{7,6},{8,9},{9,8},{10,11... | collective-permute-start | bytes 1572872 | tf_op jit(solution)/shard_map/ppermute | solution.py:54
  36.0 13.6 %copy-start.10 = (f32[1,1,256]{2,1,0:T(1,128)S(1)}, f32[1,1,256]{2,1,0:T(1,128)}, u32[]{:S(2)}) copy-start(f32[1,1,256]{2,1,0:T(1,128)} %copy-done.9) | copy-start | bytes 3076
  36.0 13.6 %copy-start.13 = (f32[1,1,256]{2,1,0:T(1,128)S(1)}, f32[1,1,256]{2,1,0:T(1,128)}, u32[]{:S(2)}) copy-start(f32[1,1,256]{2,1,0:T(1,128)} %copy-done.12) | copy-start | bytes 3076
  36.1 13.6 %copy-start.16 = (f32[1,1,256]{2,1,0:T(1,128)S(1)}, f32[1,1,256]{2,1,0:T(1,128)}, u32[]{:S(2)}) copy-start(f32[1,1,256]{2,1,0:T(1,128)} %copy-done.15) | copy-start | bytes 3076
  36.1 13.6 %copy-start.19 = (f32[1,1,256]{2,1,0:T(1,128)S(1)}, f32[1,1,256]{2,1,0:T(1,128)}, u32[]{:S(2)}) copy-start(f32[1,1,256]{2,1,0:T(1,128)} %copy-done.18) | copy-start | bytes 3076
  36.1 13.6 %copy-start.22 = (f32[1,1,256]{2,1,0:T(1,128)S(1)}, f32[1,1,256]{2,1,0:T(1,128)}, u32[]{:S(2)}) copy-start(f32[1,1,256]{2,1,0:T(1,128)} %copy-done.21) | copy-start | bytes 3076
  36.1 13.6 %copy-start.25 = (f32[1,1,256]{2,1,0:T(1,128)S(1)}, f32[1,1,256]{2,1,0:T(1,128)}, u32[]{:S(2)}) copy-start(f32[1,1,256]{2,1,0:T(1,128)} %copy-done.24) | copy-start | bytes 3076
  36.1 13.6 %copy-start.28 = (f32[1,1,256]{2,1,0:T(1,128)S(1)}, f32[1,1,256]{2,1,0:T(1,128)}, u32[]{:S(2)}) copy-start(f32[1,1,256]{2,1,0:T(1,128)} %copy-done.27) | copy-start | bytes 3076
  36.1 13.6 %copy-start.31 = (f32[1,1,256]{2,1,0:T(1,128)S(1)}, f32[1,1,256]{2,1,0:T(1,128)}, u32[]{:S(2)}) copy-start(f32[1,1,256]{2,1,0:T(1,128)} %copy-done.30) | copy-start | bytes 3076
  36.1 13.6 %copy-start.34 = (f32[1,1,256]{2,1,0:T(1,128)S(1)}, f32[1,1,256]{2,1,0:T(1,128)}, u32[]{:S(2)}) copy-start(f32[1,1,256]{2,1,0:T(1,128)} %copy-done.33) | copy-start | bytes 3076
  36.1 13.6 %copy-start.37 = (f32[1,1,256]{2,1,0:T(1,128)S(1)}, f32[1,1,256]{2,1,0:T(1,128)}, u32[]{:S(2)}) copy-start(f32[1,1,256]{2,1,0:T(1,128)} %copy-done.36) | copy-start | bytes 3076
  36.1 13.6 %copy-start.40 = (f32[1,1,256]{2,1,0:T(1,128)S(1)}, f32[1,1,256]{2,1,0:T(1,128)}, u32[]{:S(2)}) copy-start(f32[1,1,256]{2,1,0:T(1,128)} %copy-done.39) | copy-start | bytes 3076
  36.1 13.6 %copy-start.43 = (f32[1,1,256]{2,1,0:T(1,128)S(1)}, f32[1,1,256]{2,1,0:T(1,128)}, u32[]{:S(2)}) copy-start(f32[1,1,256]{2,1,0:T(1,128)} %copy-done.42) | copy-start | bytes 3076
  36.2 13.6 %copy-start.46 = (f32[1,1,256]{2,1,0:T(1,128)S(1)}, f32[1,1,256]{2,1,0:T(1,128)}, u32[]{:S(2)}) copy-start(f32[1,1,256]{2,1,0:T(1,128)} %copy-done.45) | copy-start | bytes 3076
  36.2 13.6 %copy-start.49 = (f32[1,1,256]{2,1,0:T(1,128)S(1)}, f32[1,1,256]{2,1,0:T(1,128)}, u32[]{:S(2)}) copy-start(f32[1,1,256]{2,1,0:T(1,128)} %copy-done.48) | copy-start | bytes 3076
  36.2 13.6 %copy-start.52 = (f32[1,1,256]{2,1,0:T(1,128)S(1)}, f32[1,1,256]{2,1,0:T(1,128)}, u32[]{:S(2)}) copy-start(f32[1,1,256]{2,1,0:T(1,128)} %copy-done.51) | copy-start | bytes 3076
  36.2 13.6 %copy-start.55 = (f32[1,1,256]{2,1,0:T(1,128)S(1)}, f32[1,1,256]{2,1,0:T(1,128)}, u32[]{:S(2)}) copy-start(f32[1,1,256]{2,1,0:T(1,128)} %copy-done.54) | copy-start | bytes 3076
  36.2 13.6 %copy-start.58 = (f32[1,1,256]{2,1,0:T(1,128)S(1)}, f32[1,1,256]{2,1,0:T(1,128)}, u32[]{:S(2)}) copy-start(f32[1,1,256]{2,1,0:T(1,128)} %copy-done.57) | copy-start | bytes 3076
  36.2 13.6 %copy-start.61 = (f32[1,1,256]{2,1,0:T(1,128)S(1)}, f32[1,1,256]{2,1,0:T(1,128)}, u32[]{:S(2)}) copy-start(f32[1,1,256]{2,1,0:T(1,128)} %copy-done.60) | copy-start | bytes 3076
  36.2 13.6 %copy-start.64 = (f32[1,1,256]{2,1,0:T(1,128)S(1)}, f32[1,1,256]{2,1,0:T(1,128)}, u32[]{:S(2)}) copy-start(f32[1,1,256]{2,1,0:T(1,128)} %copy-done.63) | copy-start | bytes 3076
  36.2 13.6 %copy-start.67 = (f32[1,1,256]{2,1,0:T(1,128)S(1)}, f32[1,1,256]{2,1,0:T(1,128)}, u32[]{:S(2)}) copy-start(f32[1,1,256]{2,1,0:T(1,128)} %copy-done.66) | copy-start | bytes 3076
  36.2 13.6 %copy-start.70 = (f32[1,1,256]{2,1,0:T(1,128)S(1)}, f32[1,1,256]{2,1,0:T(1,128)}, u32[]{:S(2)}) copy-start(f32[1,1,256]{2,1,0:T(1,128)} %copy-done.69) | copy-start | bytes 3076
  36.2 13.6 %copy-start.73 = (f32[1,1,256]{2,1,0:T(1,128)S(1)}, f32[1,1,256]{2,1,0:T(1,128)}, u32[]{:S(2)}) copy-start(f32[1,1,256]{2,1,0:T(1,128)} %copy-done.72) | copy-start | bytes 3076
  36.3 13.6 %copy-start.76 = (f32[1,1,256]{2,1,0:T(1,128)S(1)}, f32[1,1,256]{2,1,0:T(1,128)}, u32[]{:S(2)}) copy-start(f32[1,1,256]{2,1,0:T(1,128)} %copy-done.75) | copy-start | bytes 3076
  36.3 13.6 %copy-start.79 = (f32[1,1,256]{2,1,0:T(1,128)S(1)}, f32[1,1,256]{2,1,0:T(1,128)}, u32[]{:S(2)}) copy-start(f32[1,1,256]{2,1,0:T(1,128)} %copy-done.78) | copy-start | bytes 3076
  36.3 13.6 %copy-start.82 = (f32[1,1,256]{2,1,0:T(1,128)S(1)}, f32[1,1,256]{2,1,0:T(1,128)}, u32[]{:S(2)}) copy-start(f32[1,1,256]{2,1,0:T(1,128)} %copy-done.81) | copy-start | bytes 3076
  36.3 13.6 %copy-start.85 = (f32[1,1,256]{2,1,0:T(1,128)S(1)}, f32[1,1,256]{2,1,0:T(1,128)}, u32[]{:S(2)}) copy-start(f32[1,1,256]{2,1,0:T(1,128)} %copy-done.84) | copy-start | bytes 3076
  36.3 13.6 %copy-start.88 = (f32[1,1,256]{2,1,0:T(1,128)S(1)}, f32[1,1,256]{2,1,0:T(1,128)}, u32[]{:S(2)}) copy-start(f32[1,1,256]{2,1,0:T(1,128)} %copy-done.87) | copy-start | bytes 3076
  36.3 13.6 %copy-start.91 = (f32[1,1,256]{2,1,0:T(1,128)S(1)}, f32[1,1,256]{2,1,0:T(1,128)}, u32[]{:S(2)}) copy-start(f32[1,1,256]{2,1,0:T(1,128)} %copy-done.90) | copy-start | bytes 3076
  36.3 13.6 %copy-start.94 = (f32[1,1,256]{2,1,0:T(1,128)S(1)}, f32[1,1,256]{2,1,0:T(1,128)}, u32[]{:S(2)}) copy-start(f32[1,1,256]{2,1,0:T(1,128)} %copy-done.93) | copy-start | bytes 3076
  36.3 13.6 %copy-start.97 = (f32[1,1,256]{2,1,0:T(1,128)S(1)}, f32[1,1,256]{2,1,0:T(1,128)}, u32[]{:S(2)}) copy-start(f32[1,1,256]{2,1,0:T(1,128)} %copy-done.96) | copy-start | bytes 3076
  36.3 13.6 %copy-start.100 = (f32[1,1,256]{2,1,0:T(1,128)S(1)}, f32[1,1,256]{2,1,0:T(1,128)}, u32[]{:S(2)}) copy-start(f32[1,1,256]{2,1,0:T(1,128)} %copy-done.99) | copy-start | bytes 3076
  37.3 33.9 %collective-permute-start.4 = (f32[128,1024]{1,0:T(8,128)}, f32[128,1024]{1,0:T(8,128)}, u32[]{:S(2)}, u32[]{:S(2)}) collective-permute-start(f32[128,1024]{1,0:T(8,128)} %constant_dynamic-slice_fusion.1), channel_id=1, source_target_pairs={{0,1},{1,0},{2,3},{3,2},{4,5},{5,4},{6,7},{7,6},{8,9},{9,8},{10,11... | collective-permute-start | bytes 1572872 | tf_op jit(solution)/shard_map/ppermute | solution.py:54
  37.9 7.3 %collective-permute-start.13 = (f32[51,256]{1,0:T(8,128)S(1)}, f32[51,256]{1,0:T(8,128)S(1)}, u32[]{:S(2)}, u32[]{:S(2)}) collective-permute-start(f32[51,256]{1,0:T(8,128)S(1)} %add.963), channel_id=1, source_target_pairs={{0,2},{1,3},{2,0},{3,1},{4,6},{5,7},{6,4},{7,5},{8,10},{9,11},{10,... | collective-permute-start | bytes 156680 | tf_op jit(solution)/shard_map/ppermute | solution.py:54
  41.4 22.0 %collective-permute-start.2 = (bf16[3,256,256]{2,1,0:T(8,128)(2,1)}, bf16[3,256,256]{2,1,0:T(8,128)(2,1)}, u32[]{:S(2)}, u32[]{:S(2)}) collective-permute-start(bf16[3,256,256]{2,1,0:T(8,128)(2,1)} %get-tuple-element.63), channel_id=1, source_target_pairs={{0,1},{1,2},{2,3},{3,4},{4,5},{5,6},{6,7},{7,8},{8,9},{9,10},{10,1... | collective-permute-start | bytes 1179656 | tf_op jit(solution)/shard_map/ppermute | solution.py:64
  43.9 21.5 %collective-permute-start.3 = (bf16[3,256,256]{2,1,0:T(8,128)(2,1)}, bf16[3,256,256]{2,1,0:T(8,128)(2,1)}, u32[]{:S(2)}, u32[]{:S(2)}) collective-permute-start(bf16[3,256,256]{2,1,0:T(8,128)(2,1)} %get-tuple-element.64), channel_id=1, source_target_pairs={{1,0},{2,1},{3,2},{4,3},{5,4},{6,5},{7,6},{8,7},{9,8},{10,9},{11,1... | collective-permute-start | bytes 1179656 | tf_op jit(solution)/shard_map/ppermute | solution.py:65
  45.2 10.9 %collective-permute-start.14 = (f32[51,256]{1,0:T(8,128)S(1)}, f32[51,256]{1,0:T(8,128)S(1)}, u32[]{:S(2)}, u32[]{:S(2)}) collective-permute-start(f32[51,256]{1,0:T(8,128)S(1)} %add.964), channel_id=1, source_target_pairs={{0,4},{1,5},{2,6},{3,7},{4,0},{5,1},{6,2},{7,3},{8,12},{9,13},{10,... | collective-permute-start | bytes 156680 | tf_op jit(solution)/shard_map/ppermute | solution.py:54
  56.2 6.5 %collective-permute-start.15 = (f32[51,256]{1,0:T(8,128)S(1)}, f32[51,256]{1,0:T(8,128)S(1)}, u32[]{:S(2)}, u32[]{:S(2)}) collective-permute-start(f32[51,256]{1,0:T(8,128)S(1)} %add.965), channel_id=1, source_target_pairs={{0,8},{1,9},{2,10},{3,11},{4,12},{5,13},{6,14},{7,15},{8,0},{9,1},... | collective-permute-start | bytes 156680 | tf_op jit(solution)/shard_map/ppermute | solution.py:54
  71.1 5.0 %collective-permute-start.9 = (bf16[256,256]{1,0:T(8,128)(2,1)S(1)}, bf16[256,256]{1,0:T(8,128)(2,1)S(1)}, u32[]{:S(2)}, u32[]{:S(2)}) collective-permute-start(bf16[256,256]{1,0:T(8,128)(2,1)S(1)} %dynamic-slice_convert_fusion), channel_id=1, source_target_pairs={{0,2},{1,3},{2,0},{3,1},{4,6},{5,7},{6,4},{7,5},{8,10},{9,11},{10,... | collective-permute-start | bytes 393224 | tf_op jit(solution)/shard_map/ppermute | solution.py:54
  72.3 5.2 %collective-permute-start.5 = (bf16[64,1024]{1,0:T(8,128)(2,1)S(1)}, bf16[64,1024]{1,0:T(8,128)(2,1)S(1)}, u32[]{:S(2)}, u32[]{:S(2)}) collective-permute-start(bf16[64,1024]{1,0:T(8,128)(2,1)S(1)} %dynamic-slice_convert_fusion.1), channel_id=1, source_target_pairs={{0,2},{1,3},{2,0},{3,1},{4,6},{5,7},{6,4},{7,5},{8,10},{9,11},{10,... | collective-permute-start | bytes 393224 | tf_op jit(solution)/shard_map/ppermute | solution.py:54
  76.1 4.3 %collective-permute-start.10 = (bf16[128,256]{1,0:T(8,128)(2,1)S(1)}, bf16[128,256]{1,0:T(8,128)(2,1)S(1)}, u32[]{:S(2)}, u32[]{:S(2)}) collective-permute-start(bf16[128,256]{1,0:T(8,128)(2,1)S(1)} %dynamic-slice_convert_fusion.2), channel_id=1, source_target_pairs={{0,4},{1,5},{2,6},{3,7},{4,0},{5,1},{6,2},{7,3},{8,12},{9,13},{10,... | collective-permute-start | bytes 196616 | tf_op jit(solution)/shard_map/ppermute | solution.py:54
  77.6 4.3 %collective-permute-start.6 = (bf16[32,1024]{1,0:T(8,128)(2,1)S(1)}, bf16[32,1024]{1,0:T(8,128)(2,1)S(1)}, u32[]{:S(2)}, u32[]{:S(2)}) collective-permute-start(bf16[32,1024]{1,0:T(8,128)(2,1)S(1)} %dynamic-slice_convert_fusion.3), channel_id=1, source_target_pairs={{0,4},{1,5},{2,6},{3,7},{4,0},{5,1},{6,2},{7,3},{8,12},{9,13},{10,... | collective-permute-start | bytes 196616 | tf_op jit(solution)/shard_map/ppermute | solution.py:54
  80.5 4.9 %collective-permute-start.11 = (bf16[64,256]{1,0:T(8,128)(2,1)S(1)}, bf16[64,256]{1,0:T(8,128)(2,1)S(1)}, u32[]{:S(2)}, u32[]{:S(2)}) collective-permute-start(bf16[64,256]{1,0:T(8,128)(2,1)S(1)} %dynamic-slice_convert_fusion.4), channel_id=1, source_target_pairs={{0,8},{1,9},{2,10},{3,11},{4,12},{5,13},{6,14},{7,15},{8,0},{9,1},... | collective-permute-start | bytes 98312 | tf_op jit(solution)/shard_map/ppermute | solution.py:54
  81.9 5.2 %collective-permute-start.7 = (bf16[16,1024]{1,0:T(8,128)(2,1)S(1)}, bf16[16,1024]{1,0:T(8,128)(2,1)S(1)}, u32[]{:S(2)}, u32[]{:S(2)}) collective-permute-start(bf16[16,1024]{1,0:T(8,128)(2,1)S(1)} %dynamic-slice_convert_fusion.5), channel_id=1, source_target_pairs={{0,8},{1,9},{2,10},{3,11},{4,12},{5,13},{6,14},{7,15},{8,0},{9,1},... | collective-permute-start | bytes 98312 | tf_op jit(solution)/shard_map/ppermute | solution.py:54
  (92 other events, 577.3 us)

commit v9 on v8

--- a/solution.py
+++ b/solution.py
@@ -54,6 +54,7 @@
         got, got_whole = lax.ppermute((gives, whole), axis, pairs)
         parts = [k + g.astype(jnp.float32) for k, g in zip(keeps, got)]
         whole = whole + got_whole
+        parts, whole = lax.optimization_barrier((parts, whole))
     return parts, whole
 
 

time: 88.4 us -> 89 us (level)
  starting transfers between devices: 29.2 us -> 30.8 us
  local copies, waits for them, and re-layouts: 11.5 us -> 10.4 us
  other arithmetic: 24.6 us -> 25.5 us
    add x4, other arithmetic: 2.67 us -> 4.03 us  [shards(): total + line[col_tap:col_tap + image_cols] * flipped[row_tap, col_tap]]
    ppermute x12, starting transfers between devices: 21.6 us -> 22.9 us  [halving_reduce(): got, got_whole = lax.ppermute((gives, whole), axis, pairs)]
    unnamed x249 -> x245, local copies, waits for them, and re-layouts: 2.78 us -> 1.63 us
  transfers between devices with their start and end apart: 16 -> 16, of which waited for: 8 -> 7; matrix products, arithmetic and copies ran while one was open for 29% -> 29% of each run, Pallas kernels for 0% -> 0%
where the time goes in v9:
time: 89 us; the launch traced here: 88.7 us
  starting transfers between devices  30.8 us (35%)
  other arithmetic  25.5 us (29%)
  waiting for transfers between devices  11.7 us (13%)
  local copies, waits for them, and re-layouts  10.4 us (12%)
  matrix products  6.78 us (8%)
  between operations  3.51 us (4%)
    ppermute x12, starting transfers between devices, halving_reduce(): got, got_whole = lax.ppermute((gives, whole), axis, pairs)  22.9 us
    ppermute x12, waiting for transfers between devices, halving_reduce(): got, got_whole = lax.ppermute((gives, whole), axis, pairs)  9.72 us
    reduce_sum x1, other arithmetic, shards(): centre = jnp.mean(filtered, axis=-1, keepdims=True)  4.61 us
    add x1, other arithmetic, depthwise(): total + padded[row_tap:row_tap + image_rows, col_tap:col_tap + image_cols...  4.18 us
    add x4, other arithmetic, shards(): total + line[col_tap:col_tap + image_cols] * flipped[row_tap, col_tap]  4.03 us
    add x8, other arithmetic, halving_reduce(): parts = [k + g.astype(jnp.float32) for k, g in zip(keeps, got)]  3.66 us
    dynamic_update_slice x1, local copies, waits for them, and re-layouts, shards(): lax.dynamic_update_slice_in_dim(jnp.zeros((image_rows, image_cols + 2 * h...  3.29 us
    reduce_sum x3, other arithmetic, kernel_terms(): jnp.sum(padded[row_tap:row_tap + image_rows, col_tap:col_tap + image_cols...  3.27 us
  transfers between devices with their start and end apart: 16, of which 7 were waited for; matrix products, arithmetic and copies ran while one was open for 29% of the time, Pallas kernels for 0%

profile of v9, /device:TPU:0, one launch (start us, length us, event | category | flops | bytes accessed | tf_op | source)
XLA Modules:
  0.0 88.7 jit_solution(13490775291946693853)
XLA Ops:
  0.7 1.1 %copy.25 = bf16[4,256,256]{2,1,0:T(8,128)(2,1)S(1)} copy(bf16[4,256,256]{2,1,0:T(8,128)(2,1)} %param.8) | data formatting | bytes 1048576
  1.8 2.4 %collective-permute-start = (bf16[3,256,256]{2,1,0:T(8,128)(2,1)S(1)}, bf16[3,256,256]{2,1,0:T(8,128)(2,1)S(1)}, u32[]{:S(2)}, u32[]{:S(2)}) collective-permute-start(bf16[3,256,256]{2,1,0:T(8,128)(2,1)S(1)} %get-tuple-element.90), channel_id=1, source_target_pairs={{0,1},{1,2},{2,3},{3,4},{4,5},{5,6},{6,7},{7,8},{8,9},{9,10},{10,1... | collective-permute-start | bytes 1179656 | tf_op jit(solution)/shard_map/ppermute | solution.py:21
  4.2 1.3 %collective-permute-start.1 = (bf16[3,256,256]{2,1,0:T(8,128)(2,1)S(1)}, bf16[3,256,256]{2,1,0:T(8,128)(2,1)S(1)}, u32[]{:S(2)}, u32[]{:S(2)}) collective-permute-start(bf16[3,256,256]{2,1,0:T(8,128)(2,1)S(1)} %get-tuple-element.89), channel_id=1, source_target_pairs={{1,0},{2,1},{3,2},{4,3},{5,4},{6,5},{7,6},{8,7},{9,8},{10,9},{11,1... | collective-permute-start | bytes 1179656 | tf_op jit(solution)/shard_map/ppermute | solution.py:24
  5.5 0.7 bitcast_reduce_fusion
  7.2 0.6 fusion.215
  7.9 2.0 %collective-permute-done.1 = bf16[3,256,256]{2,1,0:T(8,128)(2,1)S(1)} collective-permute-done((bf16[3,256,256]{2,1,0:T(8,128)(2,1)S(1)}, bf16[3,256,256]{2,1,0:T(8,128)(2,1)S(1)}, u32[]{:S(2)}, u32[]{:S(2)}) %collective-permute-start.1) | collective-permute-done | bytes 393248 | tf_op jit(solution)/shard_map/ppermute | solution.py:24
  10.3 4.6 %fusion.211 = (f32[4,128]{1,0:T(4,128)S(1)}, f32[4,128,256]{2,1,0:T(8,128)S(1)}) fusion(f32[256]{0:T(256)S(1)} %bitcast.213, f32[10,134,256]{2,1,0:T(8,128)S(1)} %fusion.22, f32[256]{0:T(256)S(1)} %bitcast.218, f32[256]{0:T(256)S(1)} %bitcast.163, f32[256]{0:T(256)S(1)} %bitcast.168, f32[256]{0:T(256)S(1)} %bitcast.173, f32[256]{0:T(256)S(1)} %bitcast.178, ...), kind=kLoop, calls=%fused_computation.388 | loop fusion | flops 12844544 | bytes 26266624 | tf_op jit(solution)/shard_map/reduce_sum | solution.py:118
  15.7 1.9 %fusion.11 = (bf16[1024,512]{0,1:T(8,128)(2,1)}, f32[512,1024]{1,0:T(8,128)S(1)}) fusion(bf16[512,256]{1,0:T(8,128)(2,1)S(1)} %bitcast.156, bf16[256,1024]{1,0:T(8,128)(2,1)S(1)} %copy-done), kind=kOutput, calls=%fused_computation.112 | convolution fusion | flops 273154048 | bytes 3932160 | tf_op jit(solution)/shard_map/dot_general | solution.py:128
  17.6 0.8 fusion.123
  18.4 1.4 %fusion.6 = bf16[512,1024]{1,0:T(8,128)(2,1)S(1)} fusion(f32[512,1024]{1,0:T(8,128)S(1)} %get-tuple-element.146, bf16[512,256]{1,0:T(8,128)(2,1)S(1)} %bitcast.153, bf16[1024,256]{1,0:T(8,128)(2,1)S(1)} %copy-done.7), kind=kOutput, calls=%fused_computation.107 | convolution fusion | flops 278396928 | bytes 3932160 | tf_op jit(solution)/shard_map/dot_general | solution.py:131
  19.9 0.6 multiply_reduce_fusion.2
  20.8 1.3 %fusion.170 = (f32[256]{0:T(256)S(1)}, f32[256]{0:T(256)S(1)}, f32[256]{0:T(256)S(1)}, f32[256]{0:T(256)S(1)}, f32[256]{0:T(256)S(1)}, /*index=5*/f32[256]{0:T(2...) fusion(f32[10,134,256]{2,1,0:T(8,128)S(1)} %fusion.22, ...), kind=kLoop, calls=%fused_computation.282 | loop fusion | flops 4584192 | bytes 8148992 | tf_op jit(solution)/shard_map/reduce_sum | solution.py:99
  22.1 1.0 %fusion.171 = (f32[256]{0:T(256)S(1)}, f32[256]{0:T(256)S(1)}, f32[256]{0:T(256)S(1)}, f32[256]{0:T(256)S(1)}, f32[256]{0:T(256)S(1)}, /*index=5*/f32[256]{0:T(2...) fusion(bf16[4,128,256]{2,1,0:T(8,128)(2,1)S(1)} %get-tuple-elem, ...), kind=kLoop, calls=%fused_computation.283 | loop fusion | flops 4845056 | bytes 9717760 | tf_op jit(solution)/shard_map/reduce_sum | solution.py:99
  23.1 1.0 %fusion.172 = (f32[256]{0:T(256)S(1)}, f32[256]{0:T(256)S(1)}, f32[256]{0:T(256)S(1)}, f32[256]{0:T(256)S(1)}, f32[256]{0:T(256)S(1)}, /*index=5*/f32[256]{0:T(2...) fusion(bf16[4,128,256]{2,1,0:T(8,128)(2,1)S(1)} %get-tuple-elem, ...), kind=kLoop, calls=%fused_computation.284 | loop fusion | flops 4845056 | bytes 9717760 | tf_op jit(solution)/shard_map/reduce_sum | solution.py:99
  24.3 6.0 %collective-permute-start.6 = (f32[51,256]{1,0:T(8,128)S(1)}, f32[51,256]{1,0:T(8,128)S(1)}, u32[]{:S(2)}, u32[]{:S(2)}) collective-permute-start(f32[51,256]{1,0:T(8,128)S(1)} %concatenate.7), channel_id=1, source_target_pairs={{0,1},{1,0},{2,3},{3,2},{4,5},{5,4},{6,7},{7,6},{8,9},{9,8},{10,11... | collective-permute-start | bytes 156680 | tf_op jit(solution)/shard_map/ppermute | solution.py:54
  30.3 1.5 %copy.17 = bf16[1024,512]{1,0:T(8,128)(2,1)S(1)} copy(bf16[1024,512]{0,1:T(8,128)(2,1)} %get-tuple-element.145) | data formatting | bytes 2097152 | tf_op jit(solution)/shard_map/convert_element_type | solution.py:129
  32.3 0.8 constant_dynamic-slice_fusion
  33.3 1.7 %convolution_bitcast_fusion.1 = f32[2,2,2,2,16,1024]{5,4,0,1,2,3:T(8,128)S(1)} fusion(bf16[2,2,2,2,16,512]{5,4,3,2,1,0:T(8,128)(2,1)S(1)} %bitcast.155, bf16[512,1024]{1,0:T(8,128)(2,1)} %copy-done.6), kind=kOutput, calls=%fused_computation.120 | convolution fusion | flops 268435456 | bytes 2359296 | tf_op jit(solution)/shard_map/dot_general | solution.py:134
  35.4 0.8 constant_dynamic-slice_fusion.1
  36.9 0.9 %fusion.212 = (bf16[3,256,256]{2,1,0:T(8,128)(2,1)}, bf16[3,256,256]{2,1,0:T(8,128)(2,1)}) fusion(bf16[4,256,256]{2,1,0:T(8,128)(2,1)S(1)} %get-tuple-element.91), kind=kLoop, calls=%fused_computation.389 | loop fusion | bytes 1572864 | tf_op jit(solution)/shard_map/slice | solution.py:65
  37.8 2.7 %collective-permute-start.2 = (bf16[3,256,256]{2,1,0:T(8,128)(2,1)}, bf16[3,256,256]{2,1,0:T(8,128)(2,1)}, u32[]{:S(2)}, u32[]{:S(2)}) collective-permute-start(bf16[3,256,256]{2,1,0:T(8,128)(2,1)} %get-tuple-element.87), channel_id=1, source_target_pairs={{0,1},{1,2},{2,3},{3,4},{4,5},{5,6},{6,7},{7,8},{8,9},{9,10},{10,1... | collective-permute-start | bytes 1179656 | tf_op jit(solution)/shard_map/ppermute | solution.py:65
  40.5 1.5 %collective-permute-start.3 = (bf16[3,256,256]{2,1,0:T(8,128)(2,1)}, bf16[3,256,256]{2,1,0:T(8,128)(2,1)}, u32[]{:S(2)}, u32[]{:S(2)}) collective-permute-start(bf16[3,256,256]{2,1,0:T(8,128)(2,1)} %get-tuple-element.88), channel_id=1, source_target_pairs={{1,0},{2,1},{3,2},{4,3},{5,4},{6,5},{7,6},{8,7},{9,8},{10,9},{11,1... | collective-permute-start | bytes 1179656 | tf_op jit(solution)/shard_map/ppermute | solution.py:66
  42.4 4.2 %fusion.116 = f32[4,134,256]{2,1,0:T(8,128)} fusion(f32[4,128,256]{2,1,0:T(8,128)S(1)} %get-tuple-element.92, f32[256]{0:T(256)S(1)} %bitcast.159, f32[256]{0:T(256)S(1)} %bitcast.224, f32[256]{0:T(256)S(1)} %bitcast.189, f32[256]{0:T(256)S(1)} %bitcast.209, f32[256]{0:T(256)S(1)} %bitcast.204, f32[256]{0:T(256)S(1)} %bitcast.199, f32[256]{0:T(256)S(1)} %bitcast.194, ...), kind=kLoop, calls=%fused_computation.228 | loop fusion | flops 13309952 | bytes 1123328 | tf_op jit(solution)/shard_map/add | solution.py:87
  46.9 3.3 %dynamic_update_slice.10 = f32[4,262,256]{2,1,0:T(8,128)S(1)} dynamic-update-slice(f32[4,262,256]{2,1,0:T(8,128)S(1)} %broadcast_in_dim.8, f32[4,134,256]{2,1,0:T(8,128)} %fusion.116, s32[]{:T(128)} %constant.23.clone.1, s32[]{:T(128)S(6)} %select_n.63, s32[]{:T(128)} %constant.23.clone.1) | dynamic-update-slice | bytes 1097732 | tf_op jit(solution)/shard_map/dynamic_update_slice | solution.py:165
  50.3 1.1 %convert_element_type.100 = f32[3,256,256]{2,1,0:T(8,128)S(1)} convert(bf16[3,256,256]{2,1,0:T(8,128)(2,1)} %collective-permute-done.2) | non-fusion elementwise | flops 196608 | bytes 1179648 | tf_op jit(solution)/shard_map/convert_element_type | solution.py:176
  51.4 1.1 %convert_element_type.101 = f32[3,256,256]{2,1,0:T(8,128)S(1)} convert(bf16[3,256,256]{2,1,0:T(8,128)(2,1)} %collective-permute-done.3) | non-fusion elementwise | flops 196608 | bytes 1179648 | tf_op jit(solution)/shard_map/convert_element_type | solution.py:177
  52.8 0.7 multiply_add_fusion.4
  53.5 1.4 %fusion.195 = f32[1,256,256]{2,1,0:T(8,128)S(1)} fusion(f32[3,256,256]{2,1,0:T(8,128)S(1)} %convert_element_type.100, f32[256]{0:T(256)} %bitcast.29, f32[256]{0:T(256)S(1)} %bitcast.301, f32[256]{0:T(256)S(1)} %bitcast.298, f32[256]{0:T(256)S(1)} %bitcast.295, f32[256]{0:T(256)S(1)} %bitcast.292, f32[256]{0:T(256)S(1)} %bitcast.289, f32[256]{0:T(256)S(1)} %bitcast.286, ...), kind=kLoop, calls=%fused_computation.320 | loop fusion | flops 2686976 | bytes 1856512 | tf_op jit(solution)/shard_map/add | solution.py:190
  55.0 1.3 %fusion.177 = f32[1,256,256]{2,1,0:T(8,128)S(1)} fusion(f32[3,256,256]{2,1,0:T(8,128)S(1)} %convert_element_type.101, f32[256]{0:T(256)} %bitcast.15, f32[256]{0:T(256)} %bitcast.16, f32[256]{0:T(256)S(1)} %bitcast.316, f32[256]{0:T(256)S(1)} %bitcast.313, f32[256]{0:T(256)S(1)} %bitcast.310, f32[256]{0:T(256)S(1)} %bitcast.307, f32[256]{0:T(256)S(1)} %bitcast.304, ...), kind=kLoop, calls=%fused_computation.301 | loop fusion | flops 2686976 | bytes 1856512 | tf_op jit(solution)/shard_map/add | solution.py:190
  56.4 0.7 multiply_add_fusion.3
  57.1 1.2 %dynamic-slice_add_fusion = f32[512,256]{1,0:T(8,128)S(1)} fusion(f32[512,256]{1,0:T(8,128)} %collective-permute-done.5, f32[1024,256]{1,0:T(8,128)S(1)} %bitcast.148, s32[]{:T(128)S(6)} %select_n.66), kind=kLoop, calls=%fused_computation.286 | loop fusion | flops 131072 | bytes 1572868 | tf_op jit(solution)/shard_map/add | solution.py:55
  58.2 1.1 %dynamic-slice_add_fusion.1 = f32[128,1024]{1,0:T(8,128)S(1)} fusion(f32[128,1024]{1,0:T(8,128)} %collective-permute-done.4, f32[256,1024]{1,0:T(8,128)S(1)} %bitcast.150, s32[]{:T(128)S(6)} %select_n.64), kind=kLoop, calls=%fused_computation.287 | loop fusion | flops 131072 | bytes 1572868 | tf_op jit(solution)/shard_map/add | solution.py:55
  59.4 4.1 %collective-permute-start.8 = (bf16[256,256]{1,0:T(8,128)(2,1)S(1)}, bf16[256,256]{1,0:T(8,128)(2,1)S(1)}, u32[]{:S(2)}, u32[]{:S(2)}) collective-permute-start(bf16[256,256]{1,0:T(8,128)(2,1)S(1)} %dynamic-slice_convert_fusion), channel_id=1, source_target_pairs={{0,2},{1,3},{2,0},{3,1},{4,6},{5,7},{6,4},{7,5},{8,10},{9,11},{10,... | collective-permute-start | bytes 393224 | tf_op jit(solution)/shard_map/ppermute | solution.py:54
  63.5 1.1 %fusion.16 = bf16[4,256,256]{2,1,0:T(8,128)(2,1)} fusion(f32[4,262,256]{2,1,0:T(8,128)S(1)} %dynamic_update_slice.10, f32[1,256,256]{2,1,0:T(8,128)S(1)} %fusion.177, f32[1,256,256]{2,1,0:T(8,128)S(1)} %multiply_add_fusion.3, f32[1,256,256]{2,1,0:T(8,128)S(1)} %multiply_add_fusion.4, f32[1,256,256]{2,1,0:T(8,128)S(1)} %fusion.195, ...), kind=kLoop, calls=%fused_computation.126 | loop fusion | flops 1835008 | bytes 3145728 | tf_op jit(solution)/shard_map/convert_element_type | solution.py:193
  64.6 2.1 %collective-permute-start.7 = (bf16[64,1024]{1,0:T(8,128)(2,1)S(1)}, bf16[64,1024]{1,0:T(8,128)(2,1)S(1)}, u32[]{:S(2)}, u32[]{:S(2)}) collective-permute-start(bf16[64,1024]{1,0:T(8,128)(2,1)S(1)} %dynamic-slice_convert_fusion.1), channel_id=1, source_target_pairs={{0,2},{1,3},{2,0},{3,1},{4,6},{5,7},{6,4},{7,5},{8,10},{9,11},{10,... | collective-permute-start | bytes 393224 | tf_op jit(solution)/shard_map/ppermute | solution.py:54
  66.7 2.7 %collective-permute-done.9 = f32[51,256]{1,0:T(8,128)S(1)} collective-permute-done((f32[51,256]{1,0:T(8,128)S(1)}, f32[51,256]{1,0:T(8,128)S(1)}, u32[]{:S(2)}, u32[]{:S(2)}) %collective-permute-start.9) | collective-permute-done | bytes 52256 | tf_op jit(solution)/shard_map/ppermute | solution.py:54
  69.5 1.9 %collective-permute-done.7 = bf16[64,1024]{1,0:T(8,128)(2,1)S(1)} collective-permute-done((bf16[64,1024]{1,0:T(8,128)(2,1)S(1)}, bf16[64,1024]{1,0:T(8,128)(2,1)S(1)}, u32[]{:S(2)}, u32[]{:S(2)}) %collective-permute-start.7) | collective-permute-done | bytes 131104 | tf_op jit(solution)/shard_map/ppermute | solution.py:54
  71.4 2.4 %collective-permute-start.12 = (f32[51,256]{1,0:T(8,128)S(1)}, f32[51,256]{1,0:T(8,128)S(1)}, u32[]{:S(2)}, u32[]{:S(2)}) collective-permute-start(f32[51,256]{1,0:T(8,128)S(1)} %add.952), channel_id=1, source_target_pairs={{0,4},{1,5},{2,6},{3,7},{4,0},{5,1},{6,2},{7,3},{8,12},{9,13},{10,... | collective-permute-start | bytes 156680 | tf_op jit(solution)/shard_map/ppermute | solution.py:54
  74.0 2.1 %collective-permute-start.10 = (bf16[32,1024]{1,0:T(8,128)(2,1)S(1)}, bf16[32,1024]{1,0:T(8,128)(2,1)S(1)}, u32[]{:S(2)}, u32[]{:S(2)}) collective-permute-start(bf16[32,1024]{1,0:T(8,128)(2,1)S(1)} %dynamic-slice_convert_fusion.3), channel_id=1, source_target_pairs={{0,4},{1,5},{2,6},{3,7},{4,0},{5,1},{6,2},{7,3},{8,12},{9,13},{10,... | collective-permute-start | bytes 196616 | tf_op jit(solution)/shard_map/ppermute | solution.py:54
  76.0 0.6 collective-permute-done.12
  76.6 1.6 %collective-permute-done.11 = bf16[128,256]{1,0:T(8,128)(2,1)S(1)} collective-permute-done((bf16[128,256]{1,0:T(8,128)(2,1)S(1)}, bf16[128,256]{1,0:T(8,128)(2,1)S(1)}, u32[]{:S(2)}, u32[]{:S(2)}) %collective-permute-start.11) | collective-permute-done | bytes 65568 | tf_op jit(solution)/shard_map/ppermute | solution.py:54
  78.2 0.7 collective-permute-done.10
  78.9 2.7 %collective-permute-start.15 = (f32[51,256]{1,0:T(8,128)S(1)}, f32[51,256]{1,0:T(8,128)S(1)}, u32[]{:S(2)}, u32[]{:S(2)}) collective-permute-start(f32[51,256]{1,0:T(8,128)S(1)} %add.959), channel_id=1, source_target_pairs={{0,8},{1,9},{2,10},{3,11},{4,12},{5,13},{6,14},{7,15},{8,0},{9,1},... | collective-permute-start | bytes 156680 | tf_op jit(solution)/shard_map/ppermute | solution.py:54
  81.9 2.6 %collective-permute-start.13 = (bf16[16,1024]{1,0:T(8,128)(2,1)S(1)}, bf16[16,1024]{1,0:T(8,128)(2,1)S(1)}, u32[]{:S(2)}, u32[]{:S(2)}) collective-permute-start(bf16[16,1024]{1,0:T(8,128)(2,1)S(1)} %dynamic-slice_convert_fusion.5), channel_id=1, source_target_pairs={{0,8},{1,9},{2,10},{3,11},{4,12},{5,13},{6,14},{7,15},{8,0},{9,1},... | collective-permute-start | bytes 98312 | tf_op jit(solution)/shard_map/ppermute | solution.py:54
  84.5 2.2 %collective-permute-done.14 = bf16[64,256]{1,0:T(8,128)(2,1)S(1)} collective-permute-done((bf16[64,256]{1,0:T(8,128)(2,1)S(1)}, bf16[64,256]{1,0:T(8,128)(2,1)S(1)}, u32[]{:S(2)}, u32[]{:S(2)}) %collective-permute-start.14) | collective-permute-done | bytes 32800 | tf_op jit(solution)/shard_map/ppermute | solution.py:54
  86.8 0.6 convert_add_fusion.4
  87.4 0.6 convert_add_fusion.5
  88.1 0.6 add.966
  (291 shorter events, 4.1 us)
Async XLA Ops:
  0.6 15.0 %copy-start = (bf16[256,1024]{1,0:T(8,128)(2,1)S(1)}, bf16[256,1024]{1,0:T(8,128)(2,1)}, u32[]{:S(2)}) copy-start(bf16[256,1024]{1,0:T(8,128)(2,1)} %param.12) | copy-start | bytes 1572868
  1.8 6.1 %collective-permute-start = (bf16[3,256,256]{2,1,0:T(8,128)(2,1)S(1)}, bf16[3,256,256]{2,1,0:T(8,128)(2,1)S(1)}, u32[]{:S(2)}, u32[]{:S(2)}) collective-permute-start(bf16[3,256,256]{2,1,0:T(8,128)(2,1)S(1)} %get-tuple-element.90), channel_id=1, source_target_pairs={{0,1},{1,2},{2,3},{3,4},{4,5},{5,6},{6,7},{7,8},{8,9},{9,10},{10,1... | collective-permute-start | bytes 1179656 | tf_op jit(solution)/shard_map/ppermute | solution.py:21
  4.2 5.7 %collective-permute-start.1 = (bf16[3,256,256]{2,1,0:T(8,128)(2,1)S(1)}, bf16[3,256,256]{2,1,0:T(8,128)(2,1)S(1)}, u32[]{:S(2)}, u32[]{:S(2)}) collective-permute-start(bf16[3,256,256]{2,1,0:T(8,128)(2,1)S(1)} %get-tuple-element.89), channel_id=1, source_target_pairs={{1,0},{2,1},{3,2},{4,3},{5,4},{6,5},{7,6},{8,7},{9,8},{10,9},{11,1... | collective-permute-start | bytes 1179656 | tf_op jit(solution)/shard_map/ppermute | solution.py:24
  6.9 8.0 %copy-start.43 = (f32[1,1,256]{2,1,0:T(1,128)}, f32[1,1,256]{2,1,0:T(1,128)S(1)}, u32[]{:S(2)}) copy-start(f32[1,1,256]{2,1,0:T(1,128)S(1)} %get-tuple-element.99) | copy-start | bytes 3076
  6.9 8.0 %copy-start.46 = (f32[1,1,256]{2,1,0:T(1,128)}, f32[1,1,256]{2,1,0:T(1,128)S(1)}, u32[]{:S(2)}) copy-start(f32[1,1,256]{2,1,0:T(1,128)S(1)} %get-tuple-element.100) | copy-start | bytes 3076
  6.9 8.0 %copy-start.49 = (f32[1,1,256]{2,1,0:T(1,128)}, f32[1,1,256]{2,1,0:T(1,128)S(1)}, u32[]{:S(2)}) copy-start(f32[1,1,256]{2,1,0:T(1,128)S(1)} %get-tuple-element.101) | copy-start | bytes 3076
  6.9 8.0 %copy-start.52 = (f32[1,1,256]{2,1,0:T(1,128)}, f32[1,1,256]{2,1,0:T(1,128)S(1)}, u32[]{:S(2)}) copy-start(f32[1,1,256]{2,1,0:T(1,128)S(1)} %get-tuple-element.102) | copy-start | bytes 3076
  6.9 8.0 %copy-start.55 = (f32[1,1,256]{2,1,0:T(1,128)}, f32[1,1,256]{2,1,0:T(1,128)S(1)}, u32[]{:S(2)}) copy-start(f32[1,1,256]{2,1,0:T(1,128)S(1)} %get-tuple-element.103) | copy-start | bytes 3076
  6.9 8.0 %copy-start.58 = (f32[1,1,256]{2,1,0:T(1,128)}, f32[1,1,256]{2,1,0:T(1,128)S(1)}, u32[]{:S(2)}) copy-start(f32[1,1,256]{2,1,0:T(1,128)S(1)} %get-tuple-element.104) | copy-start | bytes 3076
  6.9 8.0 %copy-start.61 = (f32[1,1,256]{2,1,0:T(1,128)}, f32[1,1,256]{2,1,0:T(1,128)S(1)}, u32[]{:S(2)}) copy-start(f32[1,1,256]{2,1,0:T(1,128)S(1)} %get-tuple-element.105) | copy-start | bytes 3076
  7.0 8.0 %copy-start.85 = (f32[1,1,256]{2,1,0:T(1,128)}, f32[1,1,256]{2,1,0:T(1,128)S(1)}, u32[]{:S(2)}) copy-start(f32[1,1,256]{2,1,0:T(1,128)S(1)} %get-tuple-element.106) | copy-start | bytes 3076
  7.0 8.0 %copy-start.88 = (f32[1,1,256]{2,1,0:T(1,128)}, f32[1,1,256]{2,1,0:T(1,128)S(1)}, u32[]{:S(2)}) copy-start(f32[1,1,256]{2,1,0:T(1,128)S(1)} %get-tuple-element.107) | copy-start | bytes 3076
  7.0 8.0 %copy-start.91 = (f32[1,1,256]{2,1,0:T(1,128)}, f32[1,1,256]{2,1,0:T(1,128)S(1)}, u32[]{:S(2)}) copy-start(f32[1,1,256]{2,1,0:T(1,128)S(1)} %get-tuple-element.108) | copy-start | bytes 3076
  7.0 8.0 %copy-start.94 = (f32[1,1,256]{2,1,0:T(1,128)}, f32[1,1,256]{2,1,0:T(1,128)S(1)}, u32[]{:S(2)}) copy-start(f32[1,1,256]{2,1,0:T(1,128)S(1)} %get-tuple-element.109) | copy-start | bytes 3076
  7.0 8.0 %copy-start.97 = (f32[1,1,256]{2,1,0:T(1,128)}, f32[1,1,256]{2,1,0:T(1,128)S(1)}, u32[]{:S(2)}) copy-start(f32[1,1,256]{2,1,0:T(1,128)S(1)} %get-tuple-element.110) | copy-start | bytes 3076
  7.0 8.0 %copy-start.100 = (f32[1,1,256]{2,1,0:T(1,128)}, f32[1,1,256]{2,1,0:T(1,128)S(1)}, u32[]{:S(2)}) copy-start(f32[1,1,256]{2,1,0:T(1,128)S(1)} %get-tuple-element.111) | copy-start | bytes 3076
  7.0 35.0 %copy-start.9 = (f32[1,1,256]{2,1,0:T(1,128)}, f32[1,1,256]{2,1,0:T(1,128)S(1)}, u32[]{:S(2)}) copy-start(f32[1,1,256]{2,1,0:T(1,128)S(1)} %get-tuple-element.93) | copy-start | bytes 3076
  7.0 35.0 %copy-start.11 = (f32[1,1,256]{2,1,0:T(1,128)}, f32[1,1,256]{2,1,0:T(1,128)S(1)}, u32[]{:S(2)}) copy-start(f32[1,1,256]{2,1,0:T(1,128)S(1)} %get-tuple-element.94) | copy-start | bytes 3076
  7.0 35.0 %copy-start.13 = (f32[1,1,256]{2,1,0:T(1,128)}, f32[1,1,256]{2,1,0:T(1,128)S(1)}, u32[]{:S(2)}) copy-start(f32[1,1,256]{2,1,0:T(1,128)S(1)} %get-tuple-element.95) | copy-start | bytes 3076
  7.0 35.0 %copy-start.15 = (f32[1,1,256]{2,1,0:T(1,128)}, f32[1,1,256]{2,1,0:T(1,128)S(1)}, u32[]{:S(2)}) copy-start(f32[1,1,256]{2,1,0:T(1,128)S(1)} %get-tuple-element.96) | copy-start | bytes 3076
  7.1 35.0 %copy-start.17 = (f32[1,1,256]{2,1,0:T(1,128)}, f32[1,1,256]{2,1,0:T(1,128)S(1)}, u32[]{:S(2)}) copy-start(f32[1,1,256]{2,1,0:T(1,128)S(1)} %get-tuple-element.97) | copy-start | bytes 3076
  7.1 35.0 %copy-start.19 = (f32[1,1,256]{2,1,0:T(1,128)}, f32[1,1,256]{2,1,0:T(1,128)S(1)}, u32[]{:S(2)}) copy-start(f32[1,1,256]{2,1,0:T(1,128)S(1)} %get-tuple-element.98) | copy-start | bytes 3076
  7.1 7.9 %copy-start.25 = (f32[1,1,256]{2,1,0:T(1,128)}, f32[1,1,256]{2,1,0:T(1,128)S(1)}, u32[]{:S(2)}) copy-start(f32[1,1,256]{2,1,0:T(1,128)S(1)} %get-tuple-element.137) | copy-start | bytes 3076
  7.1 7.9 %copy-start.28 = (f32[1,1,256]{2,1,0:T(1,128)}, f32[1,1,256]{2,1,0:T(1,128)S(1)}, u32[]{:S(2)}) copy-start(f32[1,1,256]{2,1,0:T(1,128)S(1)} %get-tuple-element.138) | copy-start | bytes 3076
  7.1 7.9 %copy-start.31 = (f32[1,1,256]{2,1,0:T(1,128)}, f32[1,1,256]{2,1,0:T(1,128)S(1)}, u32[]{:S(2)}) copy-start(f32[1,1,256]{2,1,0:T(1,128)S(1)} %get-tuple-element.139) | copy-start | bytes 3076
  7.1 7.9 %copy-start.34 = (f32[1,1,256]{2,1,0:T(1,128)}, f32[1,1,256]{2,1,0:T(1,128)S(1)}, u32[]{:S(2)}) copy-start(f32[1,1,256]{2,1,0:T(1,128)S(1)} %get-tuple-element.140) | copy-start | bytes 3076
  7.1 7.9 %copy-start.37 = (f32[1,1,256]{2,1,0:T(1,128)}, f32[1,1,256]{2,1,0:T(1,128)S(1)}, u32[]{:S(2)}) copy-start(f32[1,1,256]{2,1,0:T(1,128)S(1)} %get-tuple-element.141) | copy-start | bytes 3076
  7.2 7.9 %copy-start.64 = (f32[1,1,256]{2,1,0:T(1,128)}, f32[1,1,256]{2,1,0:T(1,128)S(1)}, u32[]{:S(2)}) copy-start(f32[1,1,256]{2,1,0:T(1,128)S(1)} %get-tuple-element.132) | copy-start | bytes 3076
  7.2 7.9 %copy-start.67 = (f32[1,1,256]{2,1,0:T(1,128)}, f32[1,1,256]{2,1,0:T(1,128)S(1)}, u32[]{:S(2)}) copy-start(f32[1,1,256]{2,1,0:T(1,128)S(1)} %get-tuple-element.133) | copy-start | bytes 3076
  7.2 7.9 %copy-start.70 = (f32[1,1,256]{2,1,0:T(1,128)}, f32[1,1,256]{2,1,0:T(1,128)S(1)}, u32[]{:S(2)}) copy-start(f32[1,1,256]{2,1,0:T(1,128)S(1)} %get-tuple-element.134) | copy-start | bytes 3076
  7.2 7.9 %copy-start.73 = (f32[1,1,256]{2,1,0:T(1,128)}, f32[1,1,256]{2,1,0:T(1,128)S(1)}, u32[]{:S(2)}) copy-start(f32[1,1,256]{2,1,0:T(1,128)S(1)} %get-tuple-element.135) | copy-start | bytes 3076
  7.2 34.8 %copy-start.21 = (f32[1,1,256]{2,1,0:T(1,128)}, f32[1,1,256]{2,1,0:T(1,128)S(1)}, u32[]{:S(2)}) copy-start(f32[1,1,256]{2,1,0:T(1,128)S(1)} %get-tuple-element.131) | copy-start | bytes 3076
  7.2 34.8 %copy-start.23 = (f32[1,1,256]{2,1,0:T(1,128)}, f32[1,1,256]{2,1,0:T(1,128)S(1)}, u32[]{:S(2)}) copy-start(f32[1,1,256]{2,1,0:T(1,128)S(1)} %get-tuple-element.136) | copy-start | bytes 3076
  24.3 26.0 %collective-permute-start.6 = (f32[51,256]{1,0:T(8,128)S(1)}, f32[51,256]{1,0:T(8,128)S(1)}, u32[]{:S(2)}, u32[]{:S(2)}) collective-permute-start(f32[51,256]{1,0:T(8,128)S(1)} %concatenate.7), channel_id=1, source_target_pairs={{0,1},{1,0},{2,3},{3,2},{4,5},{5,4},{6,7},{7,6},{8,9},{9,8},{10,11... | collective-permute-start | bytes 156680 | tf_op jit(solution)/shard_map/ppermute | solution.py:54
  33.2 23.9 %collective-permute-start.5 = (f32[512,256]{1,0:T(8,128)}, f32[512,256]{1,0:T(8,128)}, u32[]{:S(2)}, u32[]{:S(2)}) collective-permute-start(f32[512,256]{1,0:T(8,128)} %constant_dynamic-slice_fusion), channel_id=1, source_target_pairs={{0,1},{1,0},{2,3},{3,2},{4,5},{5,4},{6,7},{7,6},{8,9},{9,8},{10,11... | collective-permute-start | bytes 1572872 | tf_op jit(solution)/shard_map/ppermute | solution.py:54
  36.3 10.3 %copy-start.120 = (f32[256]{0:T(256)S(1)}, f32[256]{0:T(256)}, u32[]{:S(2)}) copy-start(f32[256]{0:T(256)} %param.14) | copy-start | bytes 3076
  36.3 21.9 %collective-permute-start.4 = (f32[128,1024]{1,0:T(8,128)}, f32[128,1024]{1,0:T(8,128)}, u32[]{:S(2)}, u32[]{:S(2)}) collective-permute-start(f32[128,1024]{1,0:T(8,128)} %constant_dynamic-slice_fusion.1), channel_id=1, source_target_pairs={{0,1},{1,0},{2,3},{3,2},{4,5},{5,4},{6,7},{7,6},{8,9},{9,8},{10,11... | collective-permute-start | bytes 1572872 | tf_op jit(solution)/shard_map/ppermute | solution.py:54
  37.8 12.4 %collective-permute-start.2 = (bf16[3,256,256]{2,1,0:T(8,128)(2,1)}, bf16[3,256,256]{2,1,0:T(8,128)(2,1)}, u32[]{:S(2)}, u32[]{:S(2)}) collective-permute-start(bf16[3,256,256]{2,1,0:T(8,128)(2,1)} %get-tuple-element.87), channel_id=1, source_target_pairs={{0,1},{1,2},{2,3},{3,4},{4,5},{5,6},{6,7},{7,8},{8,9},{9,10},{10,1... | collective-permute-start | bytes 1179656 | tf_op jit(solution)/shard_map/ppermute | solution.py:65
  40.5 10.9 %collective-permute-start.3 = (bf16[3,256,256]{2,1,0:T(8,128)(2,1)}, bf16[3,256,256]{2,1,0:T(8,128)(2,1)}, u32[]{:S(2)}, u32[]{:S(2)}) collective-permute-start(bf16[3,256,256]{2,1,0:T(8,128)(2,1)} %get-tuple-element.88), channel_id=1, source_target_pairs={{1,0},{2,1},{3,2},{4,3},{5,4},{6,5},{7,6},{8,7},{9,8},{10,9},{11,1... | collective-permute-start | bytes 1179656 | tf_op jit(solution)/shard_map/ppermute | solution.py:66
  59.4 10.0 %collective-permute-start.8 = (bf16[256,256]{1,0:T(8,128)(2,1)S(1)}, bf16[256,256]{1,0:T(8,128)(2,1)S(1)}, u32[]{:S(2)}, u32[]{:S(2)}) collective-permute-start(bf16[256,256]{1,0:T(8,128)(2,1)S(1)} %dynamic-slice_convert_fusion), channel_id=1, source_target_pairs={{0,2},{1,3},{2,0},{3,1},{4,6},{5,7},{6,4},{7,5},{8,10},{9,11},{10,... | collective-permute-start | bytes 393224 | tf_op jit(solution)/shard_map/ppermute | solution.py:54
  64.6 4.8 %collective-permute-start.9 = (f32[51,256]{1,0:T(8,128)S(1)}, f32[51,256]{1,0:T(8,128)S(1)}, u32[]{:S(2)}, u32[]{:S(2)}) collective-permute-start(f32[51,256]{1,0:T(8,128)S(1)} %add.945), channel_id=1, source_target_pairs={{0,2},{1,3},{2,0},{3,1},{4,6},{5,7},{6,4},{7,5},{8,10},{9,11},{10,... | collective-permute-start | bytes 156680 | tf_op jit(solution)/shard_map/ppermute | solution.py:54
  64.6 6.8 %collective-permute-start.7 = (bf16[64,1024]{1,0:T(8,128)(2,1)S(1)}, bf16[64,1024]{1,0:T(8,128)(2,1)S(1)}, u32[]{:S(2)}, u32[]{:S(2)}) collective-permute-start(bf16[64,1024]{1,0:T(8,128)(2,1)S(1)} %dynamic-slice_convert_fusion.1), channel_id=1, source_target_pairs={{0,2},{1,3},{2,0},{3,1},{4,6},{5,7},{6,4},{7,5},{8,10},{9,11},{10,... | collective-permute-start | bytes 393224 | tf_op jit(solution)/shard_map/ppermute | solution.py:54
  71.4 5.2 %collective-permute-start.12 = (f32[51,256]{1,0:T(8,128)S(1)}, f32[51,256]{1,0:T(8,128)S(1)}, u32[]{:S(2)}, u32[]{:S(2)}) collective-permute-start(f32[51,256]{1,0:T(8,128)S(1)} %add.952), channel_id=1, source_target_pairs={{0,4},{1,5},{2,6},{3,7},{4,0},{5,1},{6,2},{7,3},{8,12},{9,13},{10,... | collective-permute-start | bytes 156680 | tf_op jit(solution)/shard_map/ppermute | solution.py:54
  73.9 4.3 %collective-permute-start.11 = (bf16[128,256]{1,0:T(8,128)(2,1)S(1)}, bf16[128,256]{1,0:T(8,128)(2,1)S(1)}, u32[]{:S(2)}, u32[]{:S(2)}) collective-permute-start(bf16[128,256]{1,0:T(8,128)(2,1)S(1)} %dynamic-slice_convert_fusion.2), channel_id=1, source_target_pairs={{0,4},{1,5},{2,6},{3,7},{4,0},{5,1},{6,2},{7,3},{8,12},{9,13},{10,... | collective-permute-start | bytes 196616 | tf_op jit(solution)/shard_map/ppermute | solution.py:54
  74.0 4.9 %collective-permute-start.10 = (bf16[32,1024]{1,0:T(8,128)(2,1)S(1)}, bf16[32,1024]{1,0:T(8,128)(2,1)S(1)}, u32[]{:S(2)}, u32[]{:S(2)}) collective-permute-start(bf16[32,1024]{1,0:T(8,128)(2,1)S(1)} %dynamic-slice_convert_fusion.3), channel_id=1, source_target_pairs={{0,4},{1,5},{2,6},{3,7},{4,0},{5,1},{6,2},{7,3},{8,12},{9,13},{10,... | collective-permute-start | bytes 196616 | tf_op jit(solution)/shard_map/ppermute | solution.py:54
  78.9 9.1 %collective-permute-start.15 = (f32[51,256]{1,0:T(8,128)S(1)}, f32[51,256]{1,0:T(8,128)S(1)}, u32[]{:S(2)}, u32[]{:S(2)}) collective-permute-start(f32[51,256]{1,0:T(8,128)S(1)} %add.959), channel_id=1, source_target_pairs={{0,8},{1,9},{2,10},{3,11},{4,12},{5,13},{6,14},{7,15},{8,0},{9,1},... | collective-permute-start | bytes 156680 | tf_op jit(solution)/shard_map/ppermute | solution.py:54
  81.6 5.2 %collective-permute-start.14 = (bf16[64,256]{1,0:T(8,128)(2,1)S(1)}, bf16[64,256]{1,0:T(8,128)(2,1)S(1)}, u32[]{:S(2)}, u32[]{:S(2)}) collective-permute-start(bf16[64,256]{1,0:T(8,128)(2,1)S(1)} %dynamic-slice_convert_fusion.4), channel_id=1, source_target_pairs={{0,8},{1,9},{2,10},{3,11},{4,12},{5,13},{6,14},{7,15},{8,0},{9,1},... | collective-permute-start | bytes 98312 | tf_op jit(solution)/shard_map/ppermute | solution.py:54
  81.9 5.5 %collective-permute-start.13 = (bf16[16,1024]{1,0:T(8,128)(2,1)S(1)}, bf16[16,1024]{1,0:T(8,128)(2,1)S(1)}, u32[]{:S(2)}, u32[]{:S(2)}) collective-permute-start(bf16[16,1024]{1,0:T(8,128)(2,1)S(1)} %dynamic-slice_convert_fusion.5), channel_id=1, source_target_pairs={{0,8},{1,9},{2,10},{3,11},{4,12},{5,13},{6,14},{7,15},{8,0},{9,1},... | collective-permute-start | bytes 98312 | tf_op jit(solution)/shard_map/ppermute | solution.py:54
  (90 other events, 483.1 us)

commit v10 on v6

--- a/solution.py
+++ b/solution.py
@@ -35,6 +35,12 @@
         + tuple(range(axis + steps, values.ndim))
     )
     return values.transpose(order).reshape(shape)
+
+
+def split_pair(values):
+    high = values.astype(jnp.bfloat16)
+    low = (values - high.astype(jnp.float32)).astype(jnp.bfloat16)
+    return high, low
 
 
 def halving_reduce(quartered, rows, whole, axis):
@@ -59,13 +65,39 @@
         give_q = lax.dynamic_slice_in_dim(quartered, (1 - bit) * half_q, half_q, axis=1)
         keep_r = lax.dynamic_slice_in_dim(rows, bit * half_r, half_r, axis=0)
         give_r = lax.dynamic_slice_in_dim(rows, (1 - bit) * half_r, half_r, axis=0)
-        sent = jnp.concatenate([give_q.reshape(-1, width), give_r, whole], axis=0)
-        got = lax.ppermute(sent, axis, pairs)
-        cut_q = quarters * half_q
-        quartered = keep_q + got[:cut_q].reshape(quarters, half_q, width)
-        rows = keep_r + got[cut_q : cut_q + half_r]
-        whole = whole + got[cut_q + half_r :]
+        if step == 0:
+            got_q, got_r, got_whole = lax.ppermute((give_q, give_r, whole), axis, pairs)
+            whole = whole + got_whole
+        else:
+            high, low = split_pair(whole)
+            sent = jnp.concatenate(
+                [give_q.astype(jnp.bfloat16).reshape(-1, width), give_r.astype(jnp.bfloat16), high, low],
+                axis=0,
+            )
+            got = lax.ppermute(sent, axis, pairs)
+            cut_q = quarters * half_q
+            cut_r = cut_q + half_r
+            size = whole.shape[0]
+            got_q = got[:cut_q].reshape(quarters, half_q, width)
+            got_r = got[cut_q:cut_r]
+            mine = high.astype(jnp.float32) + low.astype(jnp.float32)
+            theirs = got[cut_r : cut_r + size].astype(jnp.float32) + got[cut_r + size :].astype(
+                jnp.float32
+            )
+            whole = mine + theirs
+        quartered = keep_q + got_q.astype(jnp.float32)
+        rows = keep_r + got_r.astype(jnp.float32)
+        quartered, rows, whole = lax.optimization_barrier((quartered, rows, whole))
     return quartered, rows, whole
+
+
+def halo_rows(block, axis, width):
+    count = lax.axis_size(axis)
+    forward = [(i, i + 1) for i in range(count - 1)]
+    backward = [(target, source) for source, target in forward]
+    low = lax.ppermute(lax.slice_in_dim(block, block.shape[0] - width, None, axis=0), axis, forward)
+    high = lax.ppermute(lax.slice_in_dim(block, 0, width, axis=0), axis, backward)
+    return low, high
 
 
 def gelu_value(inputs):
@@ -167,12 +199,40 @@
     packed = jnp.concatenate([kernel_grad, gain_grad[None], scale_grad[None]], axis=0)
     owned_in, grad_w_out, small_grads = halving_reduce(partial_in, partial_out, packed, "row")
     grad_w_in = owned_in.transpose(1, 0, 2).reshape(-1, hidden)
+    flipped = kernel[::-1, ::-1]
+    tile_padded = jnp.pad(
+        grad_tile.astype(jnp.float32),
+        ((half_width, half_width), (2 * half_width, 2 * half_width), (0, 0)),
+    )
+    own = depthwise(tile_padded, flipped, image_rows, span)
+    own_full = lax.dynamic_update_slice_in_dim(
+        jnp.zeros((image_rows, image_cols + 2 * half_width, channels), jnp.float32),
+        own,
+        first_col,
+        axis=1,
+    )[:, half_width : half_width + image_cols]
     grad_conv = lax.dynamic_update_slice_in_dim(
         jnp.zeros_like(image), grad_tile, first_col, axis=1
     )
-    grad_ext = padded_2(grad_conv, (("row", 0),), half_width)
-    grad_padded = jnp.pad(grad_ext.astype(jnp.float32), ((0, 0), (half_width, half_width), (0, 0)))
-    conv_back = depthwise(grad_padded, kernel[::-1, ::-1], image_rows, image_cols)
+    low, high = halo_rows(grad_conv, "row", half_width)
+    edge = ((0, 0), (half_width, half_width), (0, 0))
+    low = jnp.pad(low.astype(jnp.float32), edge)
+    high = jnp.pad(high.astype(jnp.float32), edge)
+    halo_out = []
+    for out_row in range(image_rows):
+        total = jnp.zeros((image_cols, channels), jnp.float32)
+        for row_tap in range(KERNEL):
+            source = out_row + row_tap
+            if source < half_width:
+                line = low[source]
+            elif source >= half_width + image_rows:
+                line = high[source - half_width - image_rows]
+            else:
+                continue
+            for col_tap in range(KERNEL):
+                total = total + line[col_tap : col_tap + image_cols] * flipped[row_tap, col_tap]
+        halo_out.append(total)
+    conv_back = own_full + jnp.stack(halo_out)
     grad_image = (cotangent.astype(jnp.float32) + conv_back).astype(jnp.bfloat16)
     return (block_out, grad_image, grad_w_in, grad_w_out, small_grads)
 

time: 107 us -> 86 us (0.80)
  waiting for transfers between devices: 25.7 us -> 15.5 us
  local copies, waits for them, and re-layouts: 16.3 us -> 11.5 us
  other arithmetic: 28.6 us -> 25 us
  matrix products: 11.9 us -> 8.89 us
    ppermute x0 -> x5, starting transfers between devices: none -> 10.5 us  [the longest x3 6.24 us: halving_reduce(): got_q, got_r, got_whole = lax.ppermute((give_q, give_r, whole), axis, pairs)]
    ppermute x4 -> x3, waiting for transfers between devices: 23.1 us -> 13.6 us  [halving_reduce(): got = lax.ppermute(sent, axis, pairs)]
    convert_element_type x1, other arithmetic: 9.87 us -> 1.07 us  [shards(): (cotangent.astype(jnp.float32) + conv_back).astype(jnp.bfloat16)]
    add x8 -> x17, other arithmetic: 4.77 us -> 11.9 us  [the longest x1 4.17 us: depthwise(): total + padded[row_tap:row_tap + image_rows, col_tap:col_tap + image_cols...]
    concatenate x1 -> x0, local copies, waits for them, and re-layouts: 6.92 us -> none  [halving_reduce(): sent = jnp.concatenate([give_q.reshape(-1, width), give_r, whole], axis=0)]
    ppermute x4 -> x3, starting transfers between devices: 13.7 us -> 7.26 us  [halving_reduce(): got = lax.ppermute(sent, axis, pairs)]
    dynamic_update_slice x1, local copies, waits for them, and re-layouts: 0.02 us -> 3.29 us  [shards(): lax.dynamic_update_slice_in_dim(jnp.zeros((image_rows, image_cols + 2 * h...]
    slice x3 -> x0, other arithmetic: 2.56 us -> none  [halving_reduce(): quartered = keep_q + got[:cut_q].reshape(quarters, half_q, width)]
  transfers between devices with their start and end apart: 8 -> 10, of which waited for: 4 -> 4; matrix products, arithmetic and copies ran while one was open for 12% -> 26% of each run, Pallas kernels for 0% -> 0%
where the time goes in v10:
time: 86 us; the launch traced here: 85.5 us
  other arithmetic  25 us (29%)
  starting transfers between devices  21.5 us (25%)
  waiting for transfers between devices  15.5 us (18%)
  local copies, waits for them, and re-layouts  11.5 us (13%)
  matrix products  8.89 us (10%)
  between operations  3.12 us (4%)
    ppermute x3, waiting for transfers between devices, halving_reduce(): got = lax.ppermute(sent, axis, pairs)  13.6 us
    ppermute x3, starting transfers between devices, halving_reduce(): got = lax.ppermute(sent, axis, pairs)  7.26 us
    ppermute x3, starting transfers between devices, halving_reduce(): got_q, got_r, got_whole = lax.ppermute((give_q, give_r, whole), axis, pairs)  6.24 us
    reduce_sum x1, other arithmetic, shards(): centre = jnp.mean(filtered, axis=-1, keepdims=True)  4.6 us
    add x1, other arithmetic, depthwise(): total + padded[row_tap:row_tap + image_rows, col_tap:col_tap + image_cols...  4.17 us
    add x4, other arithmetic, shards(): total + line[col_tap:col_tap + image_cols] * flipped[row_tap, col_tap]  4.02 us
    dynamic_update_slice x1, local copies, waits for them, and re-layouts, shards(): lax.dynamic_update_slice_in_dim(jnp.zeros((image_rows, image_cols + 2 * h...  3.29 us
    reduce_sum x3, other arithmetic, kernel_terms(): jnp.sum(padded[row_tap:row_tap + image_rows, col_tap:col_tap + image_cols...  3.28 us
  transfers between devices with their start and end apart: 10, of which 4 were waited for; matrix products, arithmetic and copies ran while one was open for 26% of the time, Pallas kernels for 0%

profile of v10, /device:TPU:0, one launch (start us, length us, event | category | flops | bytes accessed | tf_op | source)
XLA Modules:
  0.0 85.5 jit_solution(11017149165648974913)
XLA Ops:
  0.7 1.1 %copy.35 = bf16[4,256,256]{2,1,0:T(8,128)(2,1)S(1)} copy(bf16[4,256,256]{2,1,0:T(8,128)(2,1)} %param.8) | data formatting | bytes 1048576
  1.8 2.4 %collective-permute-start = (bf16[3,256,256]{2,1,0:T(8,128)(2,1)S(1)}, bf16[3,256,256]{2,1,0:T(8,128)(2,1)S(1)}, u32[]{:S(2)}, u32[]{:S(2)}) collective-permute-start(bf16[3,256,256]{2,1,0:T(8,128)(2,1)S(1)} %get-tuple-element.90), channel_id=1, source_target_pairs={{0,1},{1,2},{2,3},{3,4},{4,5},{5,6},{6,7},{7,8},{8,9},{9,10},{10,1... | collective-permute-start | bytes 1179656 | tf_op jit(solution)/shard_map/ppermute | solution.py:21
  4.2 1.3 %collective-permute-start.1 = (bf16[3,256,256]{2,1,0:T(8,128)(2,1)S(1)}, bf16[3,256,256]{2,1,0:T(8,128)(2,1)S(1)}, u32[]{:S(2)}, u32[]{:S(2)}) collective-permute-start(bf16[3,256,256]{2,1,0:T(8,128)(2,1)S(1)} %get-tuple-element.89), channel_id=1, source_target_pairs={{1,0},{2,1},{3,2},{4,3},{5,4},{6,5},{7,6},{8,7},{9,8},{10,9},{11,1... | collective-permute-start | bytes 1179656 | tf_op jit(solution)/shard_map/ppermute | solution.py:24
  5.5 0.7 bitcast_reduce_fusion
  7.2 0.6 fusion.223
  7.9 2.0 %collective-permute-done.1 = bf16[3,256,256]{2,1,0:T(8,128)(2,1)S(1)} collective-permute-done((bf16[3,256,256]{2,1,0:T(8,128)(2,1)S(1)}, bf16[3,256,256]{2,1,0:T(8,128)(2,1)S(1)}, u32[]{:S(2)}, u32[]{:S(2)}) %collective-permute-start.1) | collective-permute-done | bytes 393248 | tf_op jit(solution)/shard_map/ppermute | solution.py:24
  9.9 0.3 fusion.21
  10.3 4.6 %fusion.216 = (f32[4,128]{1,0:T(4,128)S(1)}, f32[4,128,256]{2,1,0:T(8,128)S(1)}) fusion(f32[256]{0:T(256)S(1)} %bitcast.267, f32[10,134,256]{2,1,0:T(8,128)S(1)} %fusion.21, f32[256]{0:T(256)S(1)} %bitcast.272, f32[256]{0:T(256)S(1)} %bitcast.212, f32[256]{0:T(256)S(1)} %bitcast.217, f32[256]{0:T(256)S(1)} %bitcast.222, f32[256]{0:T(256)S(1)} %bitcast.227, ...), kind=kLoop, calls=%fused_computation.410 | loop fusion | flops 12844544 | bytes 26266624 | tf_op jit(solution)/shard_map/reduce_sum | solution.py:151
  15.8 1.8 %fusion.11 = (bf16[1024,512]{0,1:T(8,128)(2,1)}, f32[512,1024]{1,0:T(8,128)S(1)}) fusion(bf16[512,256]{1,0:T(8,128)(2,1)S(1)} %bitcast.197, bf16[256,1024]{1,0:T(8,128)(2,1)S(1)} %copy-done), kind=kOutput, calls=%fused_computation.112 | convolution fusion | flops 273154048 | bytes 3932160 | tf_op jit(solution)/shard_map/dot_general | solution.py:161
  17.6 1.6 %fusion.122 = (f32[256]{0:T(256)S(1)}, bf16[4,128,256]{2,1,0:T(8,128)(2,1)S(1)}, f32[512,256]{1,0:T(8,128)}) fusion(bf16[4,256,256]{2,1,0:T(8,128)(2,1)S(1)} %copy-done.5, s32[]{:T(128)S(6)} %select_n.62, f32[256]{0:T(256)S(1)} %copy-done.91, bf16[1024,256]{1,0:T(8,128)(2,1)S(1)} %copy-done.10, f32[512,1024]{1,0:T(8,128)S(1)} %get-tuple-element.152), kind=kOutput, calls=%fused_computation.238 | convolution fusion | flops 273809152 | bytes 3672068 | tf_op jit(solution)/shard_map/dot_general | solution.py:163
  19.2 1.4 %fusion.6 = bf16[512,1024]{1,0:T(8,128)(2,1)S(1)} fusion(f32[512,1024]{1,0:T(8,128)S(1)} %get-tuple-element.152, bf16[512,256]{1,0:T(8,128)(2,1)S(1)} %bitcast.195, bf16[1024,256]{1,0:T(8,128)(2,1)S(1)} %copy-done.10), kind=kOutput, calls=%fused_computation.107 | convolution fusion | flops 278396928 | bytes 3932160 | tf_op jit(solution)/shard_map/dot_general | solution.py:164
  20.7 0.6 multiply_reduce_fusion.2
  21.2 0.3 multiply_reduce_fusion
  21.6 1.3 %fusion.169 = (f32[256]{0:T(256)S(1)}, f32[256]{0:T(256)S(1)}, f32[256]{0:T(256)S(1)}, f32[256]{0:T(256)S(1)}, f32[256]{0:T(256)S(1)}, /*index=5*/f32[256]{0:T(2...) fusion(f32[10,134,256]{2,1,0:T(8,128)S(1)} %fusion.21, ...), kind=kLoop, calls=%fused_computation.285 | loop fusion | flops 4584192 | bytes 8148992 | tf_op jit(solution)/shard_map/reduce_sum | solution.py:132
  22.9 1.0 %fusion.170 = (f32[256]{0:T(256)S(1)}, f32[256]{0:T(256)S(1)}, f32[256]{0:T(256)S(1)}, f32[256]{0:T(256)S(1)}, f32[256]{0:T(256)S(1)}, /*index=5*/f32[256]{0:T(2...) fusion(bf16[4,128,256]{2,1,0:T(8,128)(2,1)S(1)} %get-tuple-elem, ...), kind=kLoop, calls=%fused_computation.286 | loop fusion | flops 4845056 | bytes 9717760 | tf_op jit(solution)/shard_map/reduce_sum | solution.py:132
  23.9 1.0 %fusion.171 = (f32[256]{0:T(256)S(1)}, f32[256]{0:T(256)S(1)}, f32[256]{0:T(256)S(1)}, f32[256]{0:T(256)S(1)}, f32[256]{0:T(256)S(1)}, /*index=5*/f32[256]{0:T(2...) fusion(bf16[4,128,256]{2,1,0:T(8,128)(2,1)S(1)} %get-tuple-elem, ...), kind=kLoop, calls=%fused_computation.287 | loop fusion | flops 4845056 | bytes 9717760 | tf_op jit(solution)/shard_map/reduce_sum | solution.py:132
  25.3 0.9 %convolution_bitcast_fusion.2 = f32[1,2,2,2,2,16,256]{6,5,4,3,2,1,0:T(8,128)} fusion(bf16[2,2,2,2,16,512]{5,4,3,2,1,0:T(8,128)(2,1)S(1)} %bitcast.185, bf16[512,1024]{1,0:T(8,128)(2,1)S(1)} %fusion.6), kind=kOutput, calls=%fused_computation.124 | convolution fusion | flops 67108864 | bytes 786432 | tf_op jit(solution)/shard_map/dot_general | solution.py:170
  26.2 0.9 %convolution_bitcast_fusion.3 = f32[1,2,2,2,2,16,256]{6,5,4,3,2,1,0:T(8,128)} fusion(bf16[2,2,2,2,16,512]{5,4,3,2,1,0:T(8,128)(2,1)S(1)} %bitcast.186, bf16[512,1024]{1,0:T(8,128)(2,1)S(1)} %fusion.6), kind=kOutput, calls=%fused_computation.125 | convolution fusion | flops 67108864 | bytes 786432 | tf_op jit(solution)/shard_map/dot_general | solution.py:170
  27.1 0.9 %convolution_bitcast_fusion.4 = f32[1,2,2,2,2,16,256]{6,5,4,3,2,1,0:T(8,128)} fusion(bf16[2,2,2,2,16,512]{5,4,3,2,1,0:T(8,128)(2,1)S(1)} %bitcast.187, bf16[512,1024]{1,0:T(8,128)(2,1)S(1)} %fusion.6), kind=kOutput, calls=%fused_computation.126 | convolution fusion | flops 67108864 | bytes 786432 | tf_op jit(solution)/shard_map/dot_general | solution.py:170
  28.2 6.0 %collective-permute-start.6 = (f32[51,256]{1,0:T(8,128)S(1)}, f32[51,256]{1,0:T(8,128)S(1)}, u32[]{:S(2)}, u32[]{:S(2)}) collective-permute-start(f32[51,256]{1,0:T(8,128)S(1)} %concatenate.17), channel_id=1, source_target_pairs={{0,1},{1,0},{2,3},{3,2},{4,5},{5,4},{6,7},{7,6},{8,9},{9,8},{10,11... | collective-permute-start | bytes 156680 | tf_op jit(solution)/shard_map/ppermute | solution.py:69
  34.3 1.7 %copy.22 = bf16[1024,512]{1,0:T(8,128)(2,1)S(1)} copy(bf16[1024,512]{0,1:T(8,128)(2,1)} %get-tuple-element.151) | data formatting | bytes 2097152 | tf_op jit(solution)/shard_map/convert_element_type | solution.py:162
  36.0 0.4 convolution_bitcast_fusion
  36.5 0.8 constant_dynamic-slice_fusion
  37.4 0.2 copy-done.9
  38.3 0.8 constant_dynamic-slice_fusion.1
  39.4 0.9 %fusion.217 = (bf16[3,256,256]{2,1,0:T(8,128)(2,1)}, bf16[3,256,256]{2,1,0:T(8,128)(2,1)}) fusion(bf16[4,256,256]{2,1,0:T(8,128)(2,1)S(1)} %get-tuple-element.91), kind=kLoop, calls=%fused_computation.411 | loop fusion | bytes 1572864 | tf_op jit(solution)/shard_map/slice | solution.py:98
  40.4 3.0 %collective-permute-start.2 = (bf16[3,256,256]{2,1,0:T(8,128)(2,1)}, bf16[3,256,256]{2,1,0:T(8,128)(2,1)}, u32[]{:S(2)}, u32[]{:S(2)}) collective-permute-start(bf16[3,256,256]{2,1,0:T(8,128)(2,1)} %get-tuple-element.87), channel_id=1, source_target_pairs={{0,1},{1,2},{2,3},{3,4},{4,5},{5,6},{6,7},{7,8},{8,9},{9,10},{10,1... | collective-permute-start | bytes 1179656 | tf_op jit(solution)/shard_map/ppermute | solution.py:98
  43.4 1.3 %collective-permute-start.3 = (bf16[3,256,256]{2,1,0:T(8,128)(2,1)}, bf16[3,256,256]{2,1,0:T(8,128)(2,1)}, u32[]{:S(2)}, u32[]{:S(2)}) collective-permute-start(bf16[3,256,256]{2,1,0:T(8,128)(2,1)} %get-tuple-element.88), channel_id=1, source_target_pairs={{1,0},{2,1},{3,2},{4,3},{5,4},{6,5},{7,6},{8,7},{9,8},{10,9},{11,1... | collective-permute-start | bytes 1179656 | tf_op jit(solution)/shard_map/ppermute | solution.py:99
  45.0 4.2 %fusion.115 = f32[4,134,256]{2,1,0:T(8,128)} fusion(f32[4,128,256]{2,1,0:T(8,128)S(1)} %get-tuple-element.92, f32[256]{0:T(256)S(1)} %bitcast.208, f32[256]{0:T(256)S(1)} %bitcast.263, f32[256]{0:T(256)S(1)} %bitcast.238, f32[256]{0:T(256)S(1)} %bitcast.258, f32[256]{0:T(256)S(1)} %bitcast.253, f32[256]{0:T(256)S(1)} %bitcast.248, f32[256]{0:T(256)S(1)} %bitcast.243, ...), kind=kLoop, calls=%fused_computation.231 | loop fusion | flops 13309952 | bytes 1123328 | tf_op jit(solution)/shard_map/add | solution.py:120
  49.4 3.3 %dynamic_update_slice.10 = f32[4,262,256]{2,1,0:T(8,128)S(1)} dynamic-update-slice(f32[4,262,256]{2,1,0:T(8,128)S(1)} %broadcast_in_dim.8, f32[4,134,256]{2,1,0:T(8,128)} %fusion.115, s32[]{:T(128)} %constant.23.clone.1, s32[]{:T(128)S(6)} %select_n.63, s32[]{:T(128)} %constant.23.clone.1) | dynamic-update-slice | bytes 1097732 | tf_op jit(solution)/shard_map/dynamic_update_slice | solution.py:208
  52.7 1.1 %convert_element_type.166 = f32[3,256,256]{2,1,0:T(8,128)S(1)} convert(bf16[3,256,256]{2,1,0:T(8,128)(2,1)} %collective-permute-done.2) | non-fusion elementwise | flops 196608 | bytes 1179648 | tf_op jit(solution)/shard_map/convert_element_type | solution.py:219
  53.8 1.1 %convert_element_type.167 = f32[3,256,256]{2,1,0:T(8,128)S(1)} convert(bf16[3,256,256]{2,1,0:T(8,128)(2,1)} %collective-permute-done.3) | non-fusion elementwise | flops 196608 | bytes 1179648 | tf_op jit(solution)/shard_map/convert_element_type | solution.py:220
  54.9 0.7 multiply_add_fusion.4
  55.6 1.1 %dynamic-slice_add_fusion = f32[512,256]{1,0:T(8,128)S(1)} fusion(f32[512,256]{1,0:T(8,128)} %collective-permute-done.5, f32[1024,256]{1,0:T(8,128)S(1)} %bitcast.190, s32[]{:T(128)S(6)} %select_n.66), kind=kLoop, calls=%fused_computation.289 | loop fusion | flops 131072 | bytes 1572868 | tf_op jit(solution)/shard_map/add | solution.py:89
  56.7 1.1 %dynamic-slice_add_fusion.1 = f32[4,128,256]{2,1,0:T(8,128)S(1)} fusion(f32[4,128,256]{2,1,0:T(8,128)} %collective-permute-done.4, f32[4,256,256]{2,1,0:T(8,128)S(1)} %bitcast.192, s32[]{:T(128)S(6)} %select_n.64), kind=kLoop, calls=%fused_computation.290 | loop fusion | flops 131072 | bytes 1572868 | tf_op jit(solution)/shard_map/add | solution.py:88
  57.9 3.8 %collective-permute-start.7 = (bf16[614,256]{1,0:T(8,128)(2,1)S(1)}, bf16[614,256]{1,0:T(8,128)(2,1)S(1)}, u32[]{:S(2)}, u32[]{:S(2)}) collective-permute-start(bf16[614,256]{1,0:T(8,128)(2,1)S(1)} %pad_maximum_fusion), channel_id=1, source_target_pairs={{0,2},{1,3},{2,0},{3,1},{4,6},{5,7},{6,4},{7,5},{8,10},{9,11},{10,... | collective-permute-start | bytes 943112 | tf_op jit(solution)/shard_map/ppermute | solution.py:77
  61.8 1.3 %fusion.194 = f32[1,256,256]{2,1,0:T(8,128)S(1)} fusion(f32[3,256,256]{2,1,0:T(8,128)S(1)} %convert_element_type.166, f32[256]{0:T(256)} %bitcast.29, f32[256]{0:T(256)S(1)} %bitcast.350, f32[256]{0:T(256)S(1)} %bitcast.347, f32[256]{0:T(256)S(1)} %bitcast.344, f32[256]{0:T(256)S(1)} %bitcast.341, f32[256]{0:T(256)S(1)} %bitcast.338, f32[256]{0:T(256)S(1)} %bitcast.335, ...), kind=kLoop, calls=%fused_computation.328 | loop fusion | flops 2686976 | bytes 1856512 | tf_op jit(solution)/shard_map/add | solution.py:233
  63.1 0.7 multiply_add_fusion.3
  63.8 6.0 %collective-permute-done.7 = bf16[614,256]{1,0:T(8,128)(2,1)S(1)} collective-permute-done((bf16[614,256]{1,0:T(8,128)(2,1)S(1)}, bf16[614,256]{1,0:T(8,128)(2,1)S(1)}, u32[]{:S(2)}, u32[]{:S(2)}) %collective-permute-start.7) | collective-permute-done | bytes 314400 | tf_op jit(solution)/shard_map/ppermute | solution.py:77
  69.9 1.6 %collective-permute-start.8 = (bf16[358,256]{1,0:T(8,128)(2,1)S(1)}, bf16[358,256]{1,0:T(8,128)(2,1)S(1)}, u32[]{:S(2)}, u32[]{:S(2)}) collective-permute-start(bf16[358,256]{1,0:T(8,128)(2,1)S(1)} %pad_maximum_fusion.1), channel_id=1, source_target_pairs={{0,4},{1,5},{2,6},{3,7},{4,0},{5,1},{6,2},{7,3},{8,12},{9,13},{10,... | collective-permute-start | bytes 549896 | tf_op jit(solution)/shard_map/ppermute | solution.py:77
  71.5 1.3 %fusion.176 = f32[1,256,256]{2,1,0:T(8,128)S(1)} fusion(f32[3,256,256]{2,1,0:T(8,128)S(1)} %convert_element_type.167, f32[256]{0:T(256)} %bitcast.15, f32[256]{0:T(256)} %bitcast.16, f32[256]{0:T(256)S(1)} %bitcast.365, f32[256]{0:T(256)S(1)} %bitcast.362, f32[256]{0:T(256)S(1)} %bitcast.359, f32[256]{0:T(256)S(1)} %bitcast.356, f32[256]{0:T(256)S(1)} %bitcast.353, ...), kind=kLoop, calls=%fused_computation.309 | loop fusion | flops 2686976 | bytes 1856512 | tf_op jit(solution)/shard_map/add | solution.py:233
  72.9 3.5 %collective-permute-done.8 = bf16[358,256]{1,0:T(8,128)(2,1)S(1)} collective-permute-done((bf16[358,256]{1,0:T(8,128)(2,1)S(1)}, bf16[358,256]{1,0:T(8,128)(2,1)S(1)}, u32[]{:S(2)}, u32[]{:S(2)}) %collective-permute-start.8) | collective-permute-done | bytes 183328 | tf_op jit(solution)/shard_map/ppermute | solution.py:77
  76.5 1.9 %collective-permute-start.9 = (bf16[230,256]{1,0:T(8,128)(2,1)S(1)}, bf16[230,256]{1,0:T(8,128)(2,1)S(1)}, u32[]{:S(2)}, u32[]{:S(2)}) collective-permute-start(bf16[230,256]{1,0:T(8,128)(2,1)S(1)} %pad_maximum_fusion.2), channel_id=1, source_target_pairs={{0,8},{1,9},{2,10},{3,11},{4,12},{5,13},{6,14},{7,15},{8,0},{9,1},... | collective-permute-start | bytes 353288 | tf_op jit(solution)/shard_map/ppermute | solution.py:77
  78.4 1.1 %fusion.16 = bf16[4,256,256]{2,1,0:T(8,128)(2,1)} fusion(f32[4,262,256]{2,1,0:T(8,128)S(1)} %dynamic_update_slice.10, f32[1,256,256]{2,1,0:T(8,128)S(1)} %fusion.176, f32[1,256,256]{2,1,0:T(8,128)S(1)} %multiply_add_fusion.3, f32[1,256,256]{2,1,0:T(8,128)S(1)} %multiply_add_fusion.4, f32[1,256,256]{2,1,0:T(8,128)S(1)} %fusion.194, ...), kind=kLoop, calls=%fused_computation.129 | loop fusion | flops 1835008 | bytes 3145728 | tf_op jit(solution)/shard_map/convert_element_type | solution.py:236
  79.4 4.1 %collective-permute-done.9 = bf16[230,256]{1,0:T(8,128)(2,1)S(1)} collective-permute-done((bf16[230,256]{1,0:T(8,128)(2,1)S(1)}, bf16[230,256]{1,0:T(8,128)(2,1)S(1)}, u32[]{:S(2)}, u32[]{:S(2)}) %collective-permute-start.9) | collective-permute-done | bytes 117792 | tf_op jit(solution)/shard_map/ppermute | solution.py:77
  83.6 0.6 fusion.211
  84.2 0.6 convert_add_fusion.8
  84.9 0.6 copy.30
  (235 shorter events, 2.7 us)
Async XLA Ops:
  0.6 15.1 %copy-start = (bf16[256,1024]{1,0:T(8,128)(2,1)S(1)}, bf16[256,1024]{1,0:T(8,128)(2,1)}, u32[]{:S(2)}) copy-start(bf16[256,1024]{1,0:T(8,128)(2,1)} %param.12) | copy-start | bytes 1572868
  1.8 6.1 %collective-permute-start = (bf16[3,256,256]{2,1,0:T(8,128)(2,1)S(1)}, bf16[3,256,256]{2,1,0:T(8,128)(2,1)S(1)}, u32[]{:S(2)}, u32[]{:S(2)}) collective-permute-start(bf16[3,256,256]{2,1,0:T(8,128)(2,1)S(1)} %get-tuple-element.90), channel_id=1, source_target_pairs={{0,1},{1,2},{2,3},{3,4},{4,5},{5,6},{6,7},{7,8},{8,9},{9,10},{10,1... | collective-permute-start | bytes 1179656 | tf_op jit(solution)/shard_map/ppermute | solution.py:21
  4.2 5.7 %collective-permute-start.1 = (bf16[3,256,256]{2,1,0:T(8,128)(2,1)S(1)}, bf16[3,256,256]{2,1,0:T(8,128)(2,1)S(1)}, u32[]{:S(2)}, u32[]{:S(2)}) collective-permute-start(bf16[3,256,256]{2,1,0:T(8,128)(2,1)S(1)} %get-tuple-element.89), channel_id=1, source_target_pairs={{1,0},{2,1},{3,2},{4,3},{5,4},{6,5},{7,6},{8,7},{9,8},{10,9},{11,1... | collective-permute-start | bytes 1179656 | tf_op jit(solution)/shard_map/ppermute | solution.py:24
  6.9 8.0 %copy-start.12 = (f32[1,1,256]{2,1,0:T(1,128)}, f32[1,1,256]{2,1,0:T(1,128)S(1)}, u32[]{:S(2)}) copy-start(f32[1,1,256]{2,1,0:T(1,128)S(1)} %get-tuple-element.99) | copy-start | bytes 3076
  6.9 8.0 %copy-start.14 = (f32[1,1,256]{2,1,0:T(1,128)}, f32[1,1,256]{2,1,0:T(1,128)S(1)}, u32[]{:S(2)}) copy-start(f32[1,1,256]{2,1,0:T(1,128)S(1)} %get-tuple-element.100) | copy-start | bytes 3076
  6.9 8.0 %copy-start.16 = (f32[1,1,256]{2,1,0:T(1,128)}, f32[1,1,256]{2,1,0:T(1,128)S(1)}, u32[]{:S(2)}) copy-start(f32[1,1,256]{2,1,0:T(1,128)S(1)} %get-tuple-element.101) | copy-start | bytes 3076
  6.9 8.0 %copy-start.18 = (f32[1,1,256]{2,1,0:T(1,128)}, f32[1,1,256]{2,1,0:T(1,128)S(1)}, u32[]{:S(2)}) copy-start(f32[1,1,256]{2,1,0:T(1,128)S(1)} %get-tuple-element.102) | copy-start | bytes 3076
  6.9 8.0 %copy-start.20 = (f32[1,1,256]{2,1,0:T(1,128)}, f32[1,1,256]{2,1,0:T(1,128)S(1)}, u32[]{:S(2)}) copy-start(f32[1,1,256]{2,1,0:T(1,128)S(1)} %get-tuple-element.103) | copy-start | bytes 3076
  6.9 8.0 %copy-start.22 = (f32[1,1,256]{2,1,0:T(1,128)}, f32[1,1,256]{2,1,0:T(1,128)S(1)}, u32[]{:S(2)}) copy-start(f32[1,1,256]{2,1,0:T(1,128)S(1)} %get-tuple-element.104) | copy-start | bytes 3076
  6.9 8.0 %copy-start.40 = (f32[1,1,256]{2,1,0:T(1,128)}, f32[1,1,256]{2,1,0:T(1,128)S(1)}, u32[]{:S(2)}) copy-start(f32[1,1,256]{2,1,0:T(1,128)S(1)} %get-tuple-element.105) | copy-start | bytes 3076
  7.0 8.0 %copy-start.42 = (f32[1,1,256]{2,1,0:T(1,128)}, f32[1,1,256]{2,1,0:T(1,128)S(1)}, u32[]{:S(2)}) copy-start(f32[1,1,256]{2,1,0:T(1,128)S(1)} %get-tuple-element.106) | copy-start | bytes 3076
  7.0 8.0 %copy-start.44 = (f32[1,1,256]{2,1,0:T(1,128)}, f32[1,1,256]{2,1,0:T(1,128)S(1)}, u32[]{:S(2)}) copy-start(f32[1,1,256]{2,1,0:T(1,128)S(1)} %get-tuple-element.107) | copy-start | bytes 3076
  7.0 8.0 %copy-start.46 = (f32[1,1,256]{2,1,0:T(1,128)}, f32[1,1,256]{2,1,0:T(1,128)S(1)}, u32[]{:S(2)}) copy-start(f32[1,1,256]{2,1,0:T(1,128)S(1)} %get-tuple-element.108) | copy-start | bytes 3076
  7.0 8.0 %copy-start.48 = (f32[1,1,256]{2,1,0:T(1,128)}, f32[1,1,256]{2,1,0:T(1,128)S(1)}, u32[]{:S(2)}) copy-start(f32[1,1,256]{2,1,0:T(1,128)S(1)} %get-tuple-element.109) | copy-start | bytes 3076
  7.0 8.0 %copy-start.50 = (f32[1,1,256]{2,1,0:T(1,128)}, f32[1,1,256]{2,1,0:T(1,128)S(1)}, u32[]{:S(2)}) copy-start(f32[1,1,256]{2,1,0:T(1,128)S(1)} %get-tuple-element.110) | copy-start | bytes 3076
  7.0 8.0 %copy-start.52 = (f32[1,1,256]{2,1,0:T(1,128)}, f32[1,1,256]{2,1,0:T(1,128)S(1)}, u32[]{:S(2)}) copy-start(f32[1,1,256]{2,1,0:T(1,128)S(1)} %get-tuple-element.111) | copy-start | bytes 3076
  7.0 8.0 %copy-start.68 = (f32[1,1,256]{2,1,0:T(1,128)}, f32[1,1,256]{2,1,0:T(1,128)S(1)}, u32[]{:S(2)}) copy-start(f32[1,1,256]{2,1,0:T(1,128)S(1)} %get-tuple-element.112) | copy-start | bytes 3076
  7.0 8.0 %copy-start.70 = (f32[1,1,256]{2,1,0:T(1,128)}, f32[1,1,256]{2,1,0:T(1,128)S(1)}, u32[]{:S(2)}) copy-start(f32[1,1,256]{2,1,0:T(1,128)S(1)} %get-tuple-element.113) | copy-start | bytes 3076
  7.0 8.0 %copy-start.72 = (f32[1,1,256]{2,1,0:T(1,128)}, f32[1,1,256]{2,1,0:T(1,128)S(1)}, u32[]{:S(2)}) copy-start(f32[1,1,256]{2,1,0:T(1,128)S(1)} %get-tuple-element.114) | copy-start | bytes 3076
  7.0 8.0 %copy-start.74 = (f32[1,1,256]{2,1,0:T(1,128)}, f32[1,1,256]{2,1,0:T(1,128)S(1)}, u32[]{:S(2)}) copy-start(f32[1,1,256]{2,1,0:T(1,128)S(1)} %get-tuple-element.115) | copy-start | bytes 3076
  7.1 8.0 %copy-start.76 = (f32[1,1,256]{2,1,0:T(1,128)}, f32[1,1,256]{2,1,0:T(1,128)S(1)}, u32[]{:S(2)}) copy-start(f32[1,1,256]{2,1,0:T(1,128)S(1)} %get-tuple-element.116) | copy-start | bytes 3076
  7.1 8.0 %copy-start.78 = (f32[1,1,256]{2,1,0:T(1,128)}, f32[1,1,256]{2,1,0:T(1,128)S(1)}, u32[]{:S(2)}) copy-start(f32[1,1,256]{2,1,0:T(1,128)S(1)} %get-tuple-element.117) | copy-start | bytes 3076
  7.1 8.0 %copy-start.24 = (f32[1,1,256]{2,1,0:T(1,128)}, f32[1,1,256]{2,1,0:T(1,128)S(1)}, u32[]{:S(2)}) copy-start(f32[1,1,256]{2,1,0:T(1,128)S(1)} %get-tuple-element.137) | copy-start | bytes 3076
  7.1 8.0 %copy-start.26 = (f32[1,1,256]{2,1,0:T(1,128)}, f32[1,1,256]{2,1,0:T(1,128)S(1)}, u32[]{:S(2)}) copy-start(f32[1,1,256]{2,1,0:T(1,128)S(1)} %get-tuple-element.142) | copy-start | bytes 3076
  7.1 8.0 %copy-start.28 = (f32[1,1,256]{2,1,0:T(1,128)}, f32[1,1,256]{2,1,0:T(1,128)S(1)}, u32[]{:S(2)}) copy-start(f32[1,1,256]{2,1,0:T(1,128)S(1)} %get-tuple-element.143) | copy-start | bytes 3076
  7.1 8.0 %copy-start.30 = (f32[1,1,256]{2,1,0:T(1,128)}, f32[1,1,256]{2,1,0:T(1,128)S(1)}, u32[]{:S(2)}) copy-start(f32[1,1,256]{2,1,0:T(1,128)S(1)} %get-tuple-element.144) | copy-start | bytes 3076
  7.1 8.0 %copy-start.32 = (f32[1,1,256]{2,1,0:T(1,128)}, f32[1,1,256]{2,1,0:T(1,128)S(1)}, u32[]{:S(2)}) copy-start(f32[1,1,256]{2,1,0:T(1,128)S(1)} %get-tuple-element.145) | copy-start | bytes 3076
  7.2 8.0 %copy-start.36 = (f32[1,1,256]{2,1,0:T(1,128)}, f32[1,1,256]{2,1,0:T(1,128)S(1)}, u32[]{:S(2)}) copy-start(f32[1,1,256]{2,1,0:T(1,128)S(1)} %get-tuple-element.146) | copy-start | bytes 3076
  7.2 8.0 %copy-start.38 = (f32[1,1,256]{2,1,0:T(1,128)}, f32[1,1,256]{2,1,0:T(1,128)S(1)}, u32[]{:S(2)}) copy-start(f32[1,1,256]{2,1,0:T(1,128)S(1)} %get-tuple-element.147) | copy-start | bytes 3076
  7.2 8.0 %copy-start.54 = (f32[1,1,256]{2,1,0:T(1,128)}, f32[1,1,256]{2,1,0:T(1,128)S(1)}, u32[]{:S(2)}) copy-start(f32[1,1,256]{2,1,0:T(1,128)S(1)} %get-tuple-element.138) | copy-start | bytes 3076
  7.2 8.0 %copy-start.56 = (f32[1,1,256]{2,1,0:T(1,128)}, f32[1,1,256]{2,1,0:T(1,128)S(1)}, u32[]{:S(2)}) copy-start(f32[1,1,256]{2,1,0:T(1,128)S(1)} %get-tuple-element.139) | copy-start | bytes 3076
  7.2 8.0 %copy-start.58 = (f32[1,1,256]{2,1,0:T(1,128)}, f32[1,1,256]{2,1,0:T(1,128)S(1)}, u32[]{:S(2)}) copy-start(f32[1,1,256]{2,1,0:T(1,128)S(1)} %get-tuple-element.140) | copy-start | bytes 3076
  7.2 8.0 %copy-start.60 = (f32[1,1,256]{2,1,0:T(1,128)}, f32[1,1,256]{2,1,0:T(1,128)S(1)}, u32[]{:S(2)}) copy-start(f32[1,1,256]{2,1,0:T(1,128)S(1)} %get-tuple-element.141) | copy-start | bytes 3076
  7.9 7.3 %copy-start.66 = (f32[1,1,256]{2,1,0:T(1,128)}, f32[1,1,256]{2,1,0:T(1,128)S(1)}, u32[]{:S(2)}) copy-start(f32[1,1,256]{2,1,0:T(1,128)S(1)} %get-tuple-element.136) | copy-start | bytes 3076
  7.9 7.3 %copy-start.80 = (f32[1,1,256]{2,1,0:T(1,128)}, f32[1,1,256]{2,1,0:T(1,128)S(1)}, u32[]{:S(2)}) copy-start(f32[1,1,256]{2,1,0:T(1,128)S(1)} %get-tuple-element.127) | copy-start | bytes 3076
  7.9 7.3 %copy-start.82 = (f32[1,1,256]{2,1,0:T(1,128)}, f32[1,1,256]{2,1,0:T(1,128)S(1)}, u32[]{:S(2)}) copy-start(f32[1,1,256]{2,1,0:T(1,128)S(1)} %get-tuple-element.128) | copy-start | bytes 3076
  7.9 7.3 %copy-start.84 = (f32[1,1,256]{2,1,0:T(1,128)}, f32[1,1,256]{2,1,0:T(1,128)S(1)}, u32[]{:S(2)}) copy-start(f32[1,1,256]{2,1,0:T(1,128)S(1)} %get-tuple-element.129) | copy-start | bytes 3076
  7.9 7.3 %copy-start.86 = (f32[1,1,256]{2,1,0:T(1,128)}, f32[1,1,256]{2,1,0:T(1,128)S(1)}, u32[]{:S(2)}) copy-start(f32[1,1,256]{2,1,0:T(1,128)S(1)} %get-tuple-element.130) | copy-start | bytes 3076
  28.2 24.5 %collective-permute-start.6 = (f32[51,256]{1,0:T(8,128)S(1)}, f32[51,256]{1,0:T(8,128)S(1)}, u32[]{:S(2)}, u32[]{:S(2)}) collective-permute-start(f32[51,256]{1,0:T(8,128)S(1)} %concatenate.17), channel_id=1, source_target_pairs={{0,1},{1,0},{2,3},{3,2},{4,5},{5,4},{6,7},{7,6},{8,9},{9,8},{10,11... | collective-permute-start | bytes 156680 | tf_op jit(solution)/shard_map/ppermute | solution.py:69
  37.4 18.2 %collective-permute-start.5 = (f32[512,256]{1,0:T(8,128)}, f32[512,256]{1,0:T(8,128)}, u32[]{:S(2)}, u32[]{:S(2)}) collective-permute-start(f32[512,256]{1,0:T(8,128)} %constant_dynamic-slice_fusion), channel_id=1, source_target_pairs={{0,1},{1,0},{2,3},{3,2},{4,5},{5,4},{6,7},{7,6},{8,9},{9,8},{10,11... | collective-permute-start | bytes 1572872 | tf_op jit(solution)/shard_map/ppermute | solution.py:69
  39.1 10.1 %copy-start.4 = (f32[512,256]{1,0:T(8,128)S(1)}, f32[512,256]{1,0:T(8,128)}, u32[]{:S(2)}) copy-start(f32[512,256]{1,0:T(8,128)} %get-tuple-element.148) | copy-start | bytes 1572868
  39.1 17.6 %collective-permute-start.4 = (f32[4,128,256]{2,1,0:T(8,128)}, f32[4,128,256]{2,1,0:T(8,128)}, u32[]{:S(2)}, u32[]{:S(2)}) collective-permute-start(f32[4,128,256]{2,1,0:T(8,128)} %constant_dynamic-slice_fusion.1), channel_id=1, source_target_pairs={{0,1},{1,0},{2,3},{3,2},{4,5},{5,4},{6,7},{7,6},{8,9},{9,8},{10,11... | collective-permute-start | bytes 1572872 | tf_op jit(solution)/shard_map/ppermute | solution.py:69
  40.4 12.3 %collective-permute-start.2 = (bf16[3,256,256]{2,1,0:T(8,128)(2,1)}, bf16[3,256,256]{2,1,0:T(8,128)(2,1)}, u32[]{:S(2)}, u32[]{:S(2)}) collective-permute-start(bf16[3,256,256]{2,1,0:T(8,128)(2,1)} %get-tuple-element.87), channel_id=1, source_target_pairs={{0,1},{1,2},{2,3},{3,4},{4,5},{5,6},{6,7},{7,8},{8,9},{9,10},{10,1... | collective-permute-start | bytes 1179656 | tf_op jit(solution)/shard_map/ppermute | solution.py:98
  43.4 10.4 %collective-permute-start.3 = (bf16[3,256,256]{2,1,0:T(8,128)(2,1)}, bf16[3,256,256]{2,1,0:T(8,128)(2,1)}, u32[]{:S(2)}, u32[]{:S(2)}) collective-permute-start(bf16[3,256,256]{2,1,0:T(8,128)(2,1)} %get-tuple-element.88), channel_id=1, source_target_pairs={{1,0},{2,1},{3,2},{4,3},{5,4},{6,5},{7,6},{8,7},{9,8},{10,9},{11,1... | collective-permute-start | bytes 1179656 | tf_op jit(solution)/shard_map/ppermute | solution.py:99
  57.9 11.8 %collective-permute-start.7 = (bf16[614,256]{1,0:T(8,128)(2,1)S(1)}, bf16[614,256]{1,0:T(8,128)(2,1)S(1)}, u32[]{:S(2)}, u32[]{:S(2)}) collective-permute-start(bf16[614,256]{1,0:T(8,128)(2,1)S(1)} %pad_maximum_fusion), channel_id=1, source_target_pairs={{0,2},{1,3},{2,0},{3,1},{4,6},{5,7},{6,4},{7,5},{8,10},{9,11},{10,... | collective-permute-start | bytes 943112 | tf_op jit(solution)/shard_map/ppermute | solution.py:77
  69.8 8.5 %copy-start.6 = (bf16[4,256,256]{2,1,0:T(8,128)(2,1)S(1)}, bf16[4,256,256]{2,1,0:T(8,128)(2,1)}, u32[]{:S(2)}) copy-start(bf16[4,256,256]{2,1,0:T(8,128)(2,1)} %param.15) | copy-start | bytes 1572868
  69.9 6.4 %collective-permute-start.8 = (bf16[358,256]{1,0:T(8,128)(2,1)S(1)}, bf16[358,256]{1,0:T(8,128)(2,1)S(1)}, u32[]{:S(2)}, u32[]{:S(2)}) collective-permute-start(bf16[358,256]{1,0:T(8,128)(2,1)S(1)} %pad_maximum_fusion.1), channel_id=1, source_target_pairs={{0,4},{1,5},{2,6},{3,7},{4,0},{5,1},{6,2},{7,3},{8,12},{9,13},{10,... | collective-permute-start | bytes 549896 | tf_op jit(solution)/shard_map/ppermute | solution.py:77
  76.5 7.1 %collective-permute-start.9 = (bf16[230,256]{1,0:T(8,128)(2,1)S(1)}, bf16[230,256]{1,0:T(8,128)(2,1)S(1)}, u32[]{:S(2)}, u32[]{:S(2)}) collective-permute-start(bf16[230,256]{1,0:T(8,128)(2,1)S(1)} %pad_maximum_fusion.2), channel_id=1, source_target_pairs={{0,8},{1,9},{2,10},{3,11},{4,12},{5,13},{6,14},{7,15},{8,0},{9,1},... | collective-permute-start | bytes 353288 | tf_op jit(solution)/shard_map/ppermute | solution.py:77
  (55 other events, 328.5 us)

commit v11 on v10

--- a/solution.py
+++ b/solution.py
@@ -43,7 +43,7 @@
     return high, low
 
 
-def halving_reduce(quartered, rows, whole, axis):
+def halving_reduce(quartered, rows, whole, axis, riders):
     count = lax.axis_size(axis)
     steps = count.bit_length() - 1
     if (1 << steps) != count:
@@ -51,8 +51,10 @@
             lax.psum_scatter(quartered, axis, scatter_dimension=1, tiled=True),
             lax.psum_scatter(rows, axis, scatter_dimension=0, tiled=True),
             lax.psum(whole, axis),
+            riders,
         )
     me = lax.axis_index(axis)
+    riders = list(riders)
     quartered = bit_reversed(quartered, count, steps, 1)
     rows = bit_reversed(rows, count, steps, 0)
     quarters, width = quartered.shape[0], quartered.shape[2]
@@ -87,8 +89,11 @@
             whole = mine + theirs
         quartered = keep_q + got_q.astype(jnp.float32)
         rows = keep_r + got_r.astype(jnp.float32)
-        quartered, rows, whole = lax.optimization_barrier((quartered, rows, whole))
-    return quartered, rows, whole
+        if step < len(riders):
+            quartered, rows, whole, riders[step] = lax.optimization_barrier(
+                (quartered, rows, whole, riders[step])
+            )
+    return quartered, rows, whole, riders
 
 
 def halo_rows(block, axis, width):
@@ -197,11 +202,17 @@
     ).astype(jnp.bfloat16)
     kernel_grad = kernel_terms(window, grad_tile.astype(jnp.float32), image_rows, TILE_COLS)
     packed = jnp.concatenate([kernel_grad, gain_grad[None], scale_grad[None]], axis=0)
-    owned_in, grad_w_out, small_grads = halving_reduce(partial_in, partial_out, packed, "row")
+    grad_conv = lax.dynamic_update_slice_in_dim(
+        jnp.zeros_like(image), grad_tile, first_col, axis=1
+    )
+    low, high = halo_rows(grad_conv, "row", half_width)
+    owned_in, grad_w_out, small_grads, (conv_tile, (low, high)) = halving_reduce(
+        partial_in, partial_out, packed, "row", [grad_tile, (low, high)]
+    )
     grad_w_in = owned_in.transpose(1, 0, 2).reshape(-1, hidden)
     flipped = kernel[::-1, ::-1]
     tile_padded = jnp.pad(
-        grad_tile.astype(jnp.float32),
+        conv_tile.astype(jnp.float32),
         ((half_width, half_width), (2 * half_width, 2 * half_width), (0, 0)),
     )
     own = depthwise(tile_padded, flipped, image_rows, span)
@@ -211,10 +222,6 @@
         first_col,
         axis=1,
     )[:, half_width : half_width + image_cols]
-    grad_conv = lax.dynamic_update_slice_in_dim(
-        jnp.zeros_like(image), grad_tile, first_col, axis=1
-    )
-    low, high = halo_rows(grad_conv, "row", half_width)
     edge = ((0, 0), (half_width, half_width), (0, 0))
     low = jnp.pad(low.astype(jnp.float32), edge)
     high = jnp.pad(high.astype(jnp.float32), edge)

time: 86 us -> 92 us (1.070)
  the two profiles are of different devices: /device:TPU:0 before, /device:TPU:6 now
where the time goes in v11:
time: 92 us; the launch traced here: 91.4 us
  other arithmetic  26.1 us (28%)
  waiting for transfers between devices  18.9 us (21%)
  starting transfers between devices  18.3 us (20%)
  local copies, waits for them, and re-layouts  15.2 us (17%)
  matrix products  9.63 us (10%)
  between operations  3.14 us (3%)
    ppermute x3, waiting for transfers between devices, halving_reduce(): got = lax.ppermute(sent, axis, pairs)  16 us
    concatenate x1, local copies, waits for them, and re-layouts, shards(): jnp.concatenate([kernel_grad, gain_grad[None], scale_grad[None]], axis=0)  4.99 us
    add x1, other arithmetic, depthwise(): total + padded[row_tap:row_tap + image_rows, col_tap:col_tap + image_cols...  4.62 us
    reduce_sum x3, other arithmetic, kernel_terms(): jnp.sum(padded[row_tap:row_tap + image_rows, col_tap:col_tap + image_cols...  4.54 us
    reduce_sum x1, other arithmetic, shards(): centre = jnp.mean(filtered, axis=-1, keepdims=True)  4.54 us
    ppermute x3, starting transfers between devices, halving_reduce(): got = lax.ppermute(sent, axis, pairs)  4.29 us
    dot_general x4, matrix products, shards(): lax.dot_general(normed_flat, pre_flat[:, q * channels:(q + 1) * channels]...  3.77 us
    ppermute x1, starting transfers between devices, padded_2(): lax.ppermute(lax.slice_in_dim(block, 0, width, axis=dim), axis, backward)  3.64 us
  transfers between devices with their start and end apart: 10, of which 5 were waited for; matrix products, arithmetic and copies ran while one was open for 18% of the time, Pallas kernels for 0%

profile of v11, /device:TPU:6, one launch (start us, length us, event | category | flops | bytes accessed | tf_op | source)
XLA Modules:
  0.0 91.4 jit_solution(13997240841393259127)
XLA Ops:
  0.7 1.1 %copy.35 = bf16[4,256,256]{2,1,0:T(8,128)(2,1)S(1)} copy(bf16[4,256,256]{2,1,0:T(8,128)(2,1)} %param.8) | data formatting | bytes 1048576
  1.8 1.9 %collective-permute-start = (bf16[3,256,256]{2,1,0:T(8,128)(2,1)S(1)}, bf16[3,256,256]{2,1,0:T(8,128)(2,1)S(1)}, u32[]{:S(2)}, u32[]{:S(2)}) collective-permute-start(bf16[3,256,256]{2,1,0:T(8,128)(2,1)S(1)} %get-tuple-element.89), channel_id=1, source_target_pairs={{0,1},{1,2},{2,3},{3,4},{4,5},{5,6},{6,7},{7,8},{8,9},{9,10},{10,1... | collective-permute-start | bytes 1179656 | tf_op jit(solution)/shard_map/ppermute | solution.py:21
  3.7 3.6 %collective-permute-start.1 = (bf16[3,256,256]{2,1,0:T(8,128)(2,1)S(1)}, bf16[3,256,256]{2,1,0:T(8,128)(2,1)S(1)}, u32[]{:S(2)}, u32[]{:S(2)}) collective-permute-start(bf16[3,256,256]{2,1,0:T(8,128)(2,1)S(1)} %get-tuple-element.88), channel_id=1, source_target_pairs={{1,0},{2,1},{3,2},{4,3},{5,4},{6,5},{7,6},{8,7},{9,8},{10,9},{11,1... | collective-permute-start | bytes 1179656 | tf_op jit(solution)/shard_map/ppermute | solution.py:24
  7.4 0.7 bitcast_reduce_fusion
  9.0 0.6 fusion.175
  9.8 1.2 %collective-permute-done = bf16[3,256,256]{2,1,0:T(8,128)(2,1)S(1)} collective-permute-done((bf16[3,256,256]{2,1,0:T(8,128)(2,1)S(1)}, bf16[3,256,256]{2,1,0:T(8,128)(2,1)S(1)}, u32[]{:S(2)}, u32[]{:S(2)}) %collective-permute-start) | collective-permute-done | bytes 393248 | tf_op jit(solution)/shard_map/ppermute | solution.py:21
  10.9 1.8 %collective-permute-done.1 = bf16[3,256,256]{2,1,0:T(8,128)(2,1)S(1)} collective-permute-done((bf16[3,256,256]{2,1,0:T(8,128)(2,1)S(1)}, bf16[3,256,256]{2,1,0:T(8,128)(2,1)S(1)}, u32[]{:S(2)}, u32[]{:S(2)}) %collective-permute-start.1) | collective-permute-done | bytes 393248 | tf_op jit(solution)/shard_map/ppermute | solution.py:24
  13.0 4.5 %fusion.170 = (f32[4,128]{1,0:T(4,128)S(1)}, f32[4,128,256]{2,1,0:T(8,128)S(1)}) fusion(f32[256]{0:T(256)S(1)} %bitcast.267, f32[10,134,256]{2,1,0:T(8,128)S(1)} %fusion.21, f32[256]{0:T(256)S(1)} %bitcast.272, f32[256]{0:T(256)S(1)} %bitcast.212, f32[256]{0:T(256)S(1)} %bitcast.217, f32[256]{0:T(256)S(1)} %bitcast.222, f32[256]{0:T(256)S(1)} %bitcast.227, ...), kind=kLoop, calls=%fused_computation.364 | loop fusion | flops 12844544 | bytes 26266624 | tf_op jit(solution)/shard_map/reduce_sum | solution.py:156
  18.5 1.8 %fusion.11 = (bf16[1024,512]{0,1:T(8,128)(2,1)}, f32[512,1024]{1,0:T(8,128)S(1)}) fusion(bf16[512,256]{1,0:T(8,128)(2,1)S(1)} %bitcast.198, bf16[256,1024]{1,0:T(8,128)(2,1)S(1)} %copy-done), kind=kOutput, calls=%fused_computation.63 | convolution fusion | flops 273154048 | bytes 3932160 | tf_op jit(solution)/shard_map/dot_general | solution.py:166
  20.3 1.6 %fusion.73 = (f32[256]{0:T(256)S(1)}, bf16[4,128,256]{2,1,0:T(8,128)(2,1)S(1)}, f32[512,256]{1,0:T(8,128)}) fusion(bf16[4,256,256]{2,1,0:T(8,128)(2,1)S(1)} %copy-done.3, s32[]{:T(128)S(6)} %select_n.62, f32[256]{0:T(256)S(1)} %copy-done.91, bf16[1024,256]{1,0:T(8,128)(2,1)S(1)} %copy-done.10, f32[512,1024]{1,0:T(8,128)S(1)} %get-tuple-element.143), kind=kOutput, calls=%fused_computation.190 | convolution fusion | flops 273809152 | bytes 3672068 | tf_op jit(solution)/shard_map/dot_general | solution.py:168
  21.9 1.4 %fusion.6 = bf16[512,1024]{1,0:T(8,128)(2,1)S(1)} fusion(f32[512,1024]{1,0:T(8,128)S(1)} %get-tuple-element.143, bf16[512,256]{1,0:T(8,128)(2,1)S(1)} %bitcast.196, bf16[1024,256]{1,0:T(8,128)(2,1)S(1)} %copy-done.10), kind=kOutput, calls=%fused_computation.58 | convolution fusion | flops 278396928 | bytes 3932160 | tf_op jit(solution)/shard_map/dot_general | solution.py:169
  23.4 0.6 multiply_reduce_fusion.2
  24.7 1.6 %fusion.121 = (f32[256]{0:T(256)}, f32[256]{0:T(256)}, f32[256]{0:T(256)}, f32[256]{0:T(256)}, f32[256]{0:T(256)}, /*index=5*/f32[256]{0:T(256)}, f32[256]{0:T(2...) fusion(bf16[4,128,256]{2,1,0:T(8,128)(2,1)S(1)} %get-tuple-elem, ...), kind=kLoop, calls=%fused_computation.238 | loop fusion | flops 4845056 | bytes 9717760 | tf_op jit(solution)/shard_map/reduce_sum | solution.py:137
  26.3 1.6 %fusion.122 = (f32[256]{0:T(256)}, f32[256]{0:T(256)}, f32[256]{0:T(256)}, f32[256]{0:T(256)}, f32[256]{0:T(256)}, /*index=5*/f32[256]{0:T(256)}, f32[256]{0:T(2...) fusion(bf16[4,128,256]{2,1,0:T(8,128)(2,1)S(1)} %get-tuple-elem, ...), kind=kLoop, calls=%fused_computation.239 | loop fusion | flops 4845056 | bytes 9717760 | tf_op jit(solution)/shard_map/reduce_sum | solution.py:137
  27.9 1.3 %fusion.120 = (f32[256]{0:T(256)S(1)}, f32[256]{0:T(256)S(1)}, f32[256]{0:T(256)S(1)}, f32[256]{0:T(256)S(1)}, f32[256]{0:T(256)S(1)}, /*index=5*/f32[256]{0:T(2...) fusion(bf16[4,128,256]{2,1,0:T(8,128)(2,1)S(1)} %get-tuple-elem, ...), kind=kLoop, calls=%fused_computation.237 | loop fusion | flops 3535616 | bytes 7091200 | tf_op jit(solution)/shard_map/reduce_sum | solution.py:137
  29.2 1.1 %copy.20 = bf16[256,512]{1,0:T(8,128)(2,1)S(1)} copy(bf16[256,512]{0,1:T(8,128)(2,1)} %bitcast.199) | data formatting | bytes 524288 | tf_op jit(solution)/shard_map/dot_general | solution.py:175
  30.3 0.9 %convolution_bitcast_fusion.4 = f32[1,2,2,2,2,16,256]{6,5,4,3,2,1,0:T(8,128)} fusion(bf16[2,2,2,2,16,512]{5,4,3,2,1,0:T(8,128)(2,1)S(1)} %bitcast.185, bf16[512,1024]{1,0:T(8,128)(2,1)S(1)} %fusion.6), kind=kOutput, calls=%fused_computation.77 | convolution fusion | flops 67108864 | bytes 786432 | tf_op jit(solution)/shard_map/dot_general | solution.py:175
  31.3 0.9 %convolution_bitcast_fusion.3 = f32[1,2,2,2,2,16,256]{6,5,4,3,2,1,0:T(8,128)} fusion(bf16[2,2,2,2,16,512]{5,4,3,2,1,0:T(8,128)(2,1)S(1)} %bitcast.186, bf16[512,1024]{1,0:T(8,128)(2,1)S(1)} %fusion.6), kind=kOutput, calls=%fused_computation.76 | convolution fusion | flops 67108864 | bytes 786432 | tf_op jit(solution)/shard_map/dot_general | solution.py:175
  32.2 1.0 %convolution_bitcast_fusion.2 = f32[1,2,2,2,2,16,256]{6,5,4,3,2,1,0:T(8,128)} fusion(bf16[2,2,2,2,16,512]{5,4,3,2,1,0:T(8,128)(2,1)S(1)} %bitcast.187, bf16[512,1024]{1,0:T(8,128)(2,1)S(1)} %fusion.6), kind=kOutput, calls=%fused_computation.75 | convolution fusion | flops 67108864 | bytes 786432 | tf_op jit(solution)/shard_map/dot_general | solution.py:175
  33.2 0.9 %convolution_bitcast_fusion.1 = f32[1,2,2,2,2,16,256]{6,5,4,3,2,1,0:T(8,128)} fusion(bf16[2,2,2,2,16,512]{5,4,3,2,1,0:T(8,128)(2,1)S(1)} %bitcast.188, bf16[512,1024]{1,0:T(8,128)(2,1)S(1)} %fusion.6), kind=kOutput, calls=%fused_computation.74 | convolution fusion | flops 67108864 | bytes 786432 | tf_op jit(solution)/shard_map/dot_general | solution.py:175
  34.1 5.0 %concatenate.17 = f32[51,256]{1,0:T(8,128)S(1)} concatenate(f32[1,256]{1,0:T(1,128)} %bitcast.399, f32[1,256]{1,0:T(1,128)} %bitcast.419, f32[1,256]{1,0:T(1,128)} %bitcast.420, f32[1,256]{1,0:T(1,128)} %bitcast.421, f32[1,256]{1,0:T(1,128)} %bitcast.422, f32[1,256]{1,0:T(1,128)} %bitcast.423, f32[1,256]{1,0:T(1,128)} %bitcast.424, f32[1,256]{1,0:T(1,128)} %bitcast.425, ...), dimensions={0} | concatenate | bytes 104448 | tf_op jit(solution)/shard_map/concatenate | solution.py:204
  39.1 2.8 %collective-permute-start.4 = (f32[51,256]{1,0:T(8,128)S(1)}, f32[51,256]{1,0:T(8,128)S(1)}, u32[]{:S(2)}, u32[]{:S(2)}) collective-permute-start(f32[51,256]{1,0:T(8,128)S(1)} %concatenate.17), channel_id=1, source_target_pairs={{0,1},{1,0},{2,3},{3,2},{4,5},{5,4},{6,7},{7,6},{8,9},{9,8},{10,11... | collective-permute-start | bytes 156680 | tf_op jit(solution)/shard_map/ppermute | solution.py:71
  41.9 1.7 %copy.22 = bf16[1024,512]{1,0:T(8,128)(2,1)S(1)} copy(bf16[1024,512]{0,1:T(8,128)(2,1)} %get-tuple-element.142) | data formatting | bytes 2097152 | tf_op jit(solution)/shard_map/convert_element_type | solution.py:167
  44.3 0.7 copy-done.6
  45.5 0.9 %fusion.171 = (bf16[3,256,256]{2,1,0:T(8,128)(2,1)}, bf16[3,256,256]{2,1,0:T(8,128)(2,1)}) fusion(bf16[4,256,256]{2,1,0:T(8,128)(2,1)S(1)} %get-tuple-element.80), kind=kLoop, calls=%fused_computation.365 | loop fusion | bytes 1572864 | tf_op jit(solution)/shard_map/slice | solution.py:104
  46.5 2.4 %collective-permute-start.6 = (bf16[3,256,256]{2,1,0:T(8,128)(2,1)}, bf16[3,256,256]{2,1,0:T(8,128)(2,1)}, u32[]{:S(2)}, u32[]{:S(2)}) collective-permute-start(bf16[3,256,256]{2,1,0:T(8,128)(2,1)} %get-tuple-element.85), channel_id=1, source_target_pairs={{0,1},{1,2},{2,3},{3,4},{4,5},{5,6},{6,7},{7,8},{8,9},{9,10},{10,1... | collective-permute-start | bytes 1179656 | tf_op jit(solution)/shard_map/ppermute | solution.py:103
  48.9 3.2 %collective-permute-start.7 = (bf16[3,256,256]{2,1,0:T(8,128)(2,1)}, bf16[3,256,256]{2,1,0:T(8,128)(2,1)}, u32[]{:S(2)}, u32[]{:S(2)}) collective-permute-start(bf16[3,256,256]{2,1,0:T(8,128)(2,1)} %get-tuple-element.84), channel_id=1, source_target_pairs={{1,0},{2,1},{3,2},{4,3},{5,4},{6,5},{7,6},{8,7},{9,8},{10,9},{11,1... | collective-permute-start | bytes 1179656 | tf_op jit(solution)/shard_map/ppermute | solution.py:104
  52.8 0.7 pad_maximum_fusion
  54.1 4.6 %fusion.24 = f32[4,134,256]{2,1,0:T(8,128)S(1)} fusion(f32[10,140,256]{2,1,0:T(8,128)S(1)} %pad_convert_fusion, f32[256]{0:T(256)S(1)} %bitcast.208, f32[256]{0:T(256)S(1)} %bitcast.263, f32[256]{0:T(256)S(1)} %bitcast.238, f32[256]{0:T(256)S(1)} %bitcast.258, f32[256]{0:T(256)S(1)} %bitcast.253, f32[256]{0:T(256)S(1)} %bitcast.248, f32[256]{0:T(256)S(1)} %bitcast.243, ...), kind=kLoop, calls=%fused_computation.93 | loop fusion | flops 13309952 | bytes 27493376 | tf_op jit(solution)/shard_map/add | solution.py:125
  58.8 1.4 %dynamic_update_slice.10 = f32[4,262,256]{2,1,0:T(8,128)S(1)} dynamic-update-slice(f32[4,262,256]{2,1,0:T(8,128)S(1)} %broadcast_in_dim.8, f32[4,134,256]{2,1,0:T(8,128)S(1)} %fusion.24, s32[]{:T(128)} %constant.23.clone.1, s32[]{:T(128)S(6)} %select_n.63, s32[]{:T(128)} %constant.23.clone.1) | dynamic-update-slice | bytes 1097732 | tf_op jit(solution)/shard_map/dynamic_update_slice | solution.py:219
  60.2 7.5 %collective-permute-done.5 = bf16[614,256]{1,0:T(8,128)(2,1)} collective-permute-done((bf16[614,256]{1,0:T(8,128)(2,1)}, bf16[614,256]{1,0:T(8,128)(2,1)}, u32[]{:S(2)}, u32[]{:S(2)}) %collective-permute-start.5) | collective-permute-done | bytes 314400 | tf_op jit(solution)/shard_map/ppermute | solution.py:79
  67.7 0.9 slice.1318
  68.7 0.8 fusion.159
  69.5 0.9 %convert_add_fusion.1 = f32[256,256]{1,0:T(8,128)S(1)} fusion(f32[512,256]{1,0:T(8,128)S(1)} %dynamic-slice_add_fusion, s32[]{:T(128)S(6)} %select_n.71, bf16[614,256]{1,0:T(8,128)(2,1)} %collective-permute-done.5), kind=kLoop, calls=%fused_computation.325 | loop fusion | flops 131072 | bytes 655364 | tf_op jit(solution)/shard_map/add | solution.py:91
  70.5 1.1 %convert_element_type.178 = f32[3,256,256]{2,1,0:T(8,128)S(1)} convert(bf16[3,256,256]{2,1,0:T(8,128)(2,1)} %collective-permute-done.6) | non-fusion elementwise | flops 196608 | bytes 1179648 | tf_op jit(solution)/shard_map/convert_element_type | solution.py:226
  71.6 1.1 %convert_element_type.179 = f32[3,256,256]{2,1,0:T(8,128)S(1)} convert(bf16[3,256,256]{2,1,0:T(8,128)(2,1)} %collective-permute-done.7) | non-fusion elementwise | flops 196608 | bytes 1179648 | tf_op jit(solution)/shard_map/convert_element_type | solution.py:227
  72.6 0.7 multiply_add_fusion.4
  73.3 0.7 multiply_add_fusion.3
  74.0 0.7 fusion.145
  74.8 1.6 %collective-permute-start.8 = (bf16[358,256]{1,0:T(8,128)(2,1)S(1)}, bf16[358,256]{1,0:T(8,128)(2,1)S(1)}, u32[]{:S(2)}, u32[]{:S(2)}) collective-permute-start(bf16[358,256]{1,0:T(8,128)(2,1)S(1)} %pad_maximum_fusion.1), channel_id=1, source_target_pairs={{0,4},{1,5},{2,6},{3,7},{4,0},{5,1},{6,2},{7,3},{8,12},{9,13},{10,... | collective-permute-start | bytes 549896 | tf_op jit(solution)/shard_map/ppermute | solution.py:79
  76.4 0.7 fusion.127
  77.0 4.4 %collective-permute-done.8 = bf16[358,256]{1,0:T(8,128)(2,1)S(1)} collective-permute-done((bf16[358,256]{1,0:T(8,128)(2,1)S(1)}, bf16[358,256]{1,0:T(8,128)(2,1)S(1)}, u32[]{:S(2)}, u32[]{:S(2)}) %collective-permute-start.8) | collective-permute-done | bytes 183328 | tf_op jit(solution)/shard_map/ppermute | solution.py:79
  81.6 2.7 %collective-permute-start.9 = (bf16[230,256]{1,0:T(8,128)(2,1)S(1)}, bf16[230,256]{1,0:T(8,128)(2,1)S(1)}, u32[]{:S(2)}, u32[]{:S(2)}) collective-permute-start(bf16[230,256]{1,0:T(8,128)(2,1)S(1)} %pad_maximum_fusion.2), channel_id=1, source_target_pairs={{0,8},{1,9},{2,10},{3,11},{4,12},{5,13},{6,14},{7,15},{8,0},{9,1},... | collective-permute-start | bytes 353288 | tf_op jit(solution)/shard_map/ppermute | solution.py:79
  84.2 1.1 %fusion.16 = bf16[4,256,256]{2,1,0:T(8,128)(2,1)} fusion(f32[4,262,256]{2,1,0:T(8,128)S(1)} %dynamic_update_slice.10, f32[1,256,256]{2,1,0:T(8,128)S(1)} %fusion.127, f32[1,256,256]{2,1,0:T(8,128)S(1)} %multiply_add_fusion.3, f32[1,256,256]{2,1,0:T(8,128)S(1)} %multiply_add_fusion.4, f32[1,256,256]{2,1,0:T(8,128)S(1)} %fusion.145, ...), kind=kLoop, calls=%fused_computation.80 | loop fusion | flops 1835008 | bytes 3145728 | tf_op jit(solution)/shard_map/convert_element_type | solution.py:243
  85.3 4.1 %collective-permute-done.9 = bf16[230,256]{1,0:T(8,128)(2,1)S(1)} collective-permute-done((bf16[230,256]{1,0:T(8,128)(2,1)S(1)}, bf16[230,256]{1,0:T(8,128)(2,1)S(1)}, u32[]{:S(2)}, u32[]{:S(2)}) %collective-permute-start.9) | collective-permute-done | bytes 117792 | tf_op jit(solution)/shard_map/ppermute | solution.py:79
  89.5 0.6 copy.30
  90.1 0.6 fusion.163
  90.7 0.6 convert_add_fusion.8
  (237 shorter events, 3.9 us)
Async XLA Ops:
  0.6 17.8 %copy-start = (bf16[256,1024]{1,0:T(8,128)(2,1)S(1)}, bf16[256,1024]{1,0:T(8,128)(2,1)}, u32[]{:S(2)}) copy-start(bf16[256,1024]{1,0:T(8,128)(2,1)} %param.12) | copy-start | bytes 1572868
  1.8 9.1 %collective-permute-start = (bf16[3,256,256]{2,1,0:T(8,128)(2,1)S(1)}, bf16[3,256,256]{2,1,0:T(8,128)(2,1)S(1)}, u32[]{:S(2)}, u32[]{:S(2)}) collective-permute-start(bf16[3,256,256]{2,1,0:T(8,128)(2,1)S(1)} %get-tuple-element.89), channel_id=1, source_target_pairs={{0,1},{1,2},{2,3},{3,4},{4,5},{5,6},{6,7},{7,8},{8,9},{9,10},{10,1... | collective-permute-start | bytes 1179656 | tf_op jit(solution)/shard_map/ppermute | solution.py:21
  3.7 8.9 %collective-permute-start.1 = (bf16[3,256,256]{2,1,0:T(8,128)(2,1)S(1)}, bf16[3,256,256]{2,1,0:T(8,128)(2,1)S(1)}, u32[]{:S(2)}, u32[]{:S(2)}) collective-permute-start(bf16[3,256,256]{2,1,0:T(8,128)(2,1)S(1)} %get-tuple-element.88), channel_id=1, source_target_pairs={{1,0},{2,1},{3,2},{4,3},{5,4},{6,5},{7,6},{8,7},{9,8},{10,9},{11,1... | collective-permute-start | bytes 1179656 | tf_op jit(solution)/shard_map/ppermute | solution.py:24
  8.8 8.8 %copy-start.24 = (f32[1,1,256]{2,1,0:T(1,128)}, f32[1,1,256]{2,1,0:T(1,128)S(1)}, u32[]{:S(2)}) copy-start(f32[1,1,256]{2,1,0:T(1,128)S(1)} %get-tuple-element.98) | copy-start | bytes 3076
  8.8 8.8 %copy-start.26 = (f32[1,1,256]{2,1,0:T(1,128)}, f32[1,1,256]{2,1,0:T(1,128)S(1)}, u32[]{:S(2)}) copy-start(f32[1,1,256]{2,1,0:T(1,128)S(1)} %get-tuple-element.99) | copy-start | bytes 3076
  8.8 8.8 %copy-start.28 = (f32[1,1,256]{2,1,0:T(1,128)}, f32[1,1,256]{2,1,0:T(1,128)S(1)}, u32[]{:S(2)}) copy-start(f32[1,1,256]{2,1,0:T(1,128)S(1)} %get-tuple-element.100) | copy-start | bytes 3076
  8.8 8.8 %copy-start.30 = (f32[1,1,256]{2,1,0:T(1,128)}, f32[1,1,256]{2,1,0:T(1,128)S(1)}, u32[]{:S(2)}) copy-start(f32[1,1,256]{2,1,0:T(1,128)S(1)} %get-tuple-element.101) | copy-start | bytes 3076
  8.8 8.8 %copy-start.32 = (f32[1,1,256]{2,1,0:T(1,128)}, f32[1,1,256]{2,1,0:T(1,128)S(1)}, u32[]{:S(2)}) copy-start(f32[1,1,256]{2,1,0:T(1,128)S(1)} %get-tuple-element.102) | copy-start | bytes 3076
  8.8 8.8 %copy-start.34 = (f32[1,1,256]{2,1,0:T(1,128)}, f32[1,1,256]{2,1,0:T(1,128)S(1)}, u32[]{:S(2)}) copy-start(f32[1,1,256]{2,1,0:T(1,128)S(1)} %get-tuple-element.103) | copy-start | bytes 3076
  8.8 8.8 %copy-start.36 = (f32[1,1,256]{2,1,0:T(1,128)}, f32[1,1,256]{2,1,0:T(1,128)S(1)}, u32[]{:S(2)}) copy-start(f32[1,1,256]{2,1,0:T(1,128)S(1)} %get-tuple-element.104) | copy-start | bytes 3076
  8.8 8.8 %copy-start.52 = (f32[1,1,256]{2,1,0:T(1,128)}, f32[1,1,256]{2,1,0:T(1,128)S(1)}, u32[]{:S(2)}) copy-start(f32[1,1,256]{2,1,0:T(1,128)S(1)} %get-tuple-element.105) | copy-start | bytes 3076
  8.9 8.8 %copy-start.54 = (f32[1,1,256]{2,1,0:T(1,128)}, f32[1,1,256]{2,1,0:T(1,128)S(1)}, u32[]{:S(2)}) copy-start(f32[1,1,256]{2,1,0:T(1,128)S(1)} %get-tuple-element.106) | copy-start | bytes 3076
  8.9 8.8 %copy-start.56 = (f32[1,1,256]{2,1,0:T(1,128)}, f32[1,1,256]{2,1,0:T(1,128)S(1)}, u32[]{:S(2)}) copy-start(f32[1,1,256]{2,1,0:T(1,128)S(1)} %get-tuple-element.107) | copy-start | bytes 3076
  8.9 8.8 %copy-start.58 = (f32[1,1,256]{2,1,0:T(1,128)}, f32[1,1,256]{2,1,0:T(1,128)S(1)}, u32[]{:S(2)}) copy-start(f32[1,1,256]{2,1,0:T(1,128)S(1)} %get-tuple-element.108) | copy-start | bytes 3076
  8.9 8.8 %copy-start.60 = (f32[1,1,256]{2,1,0:T(1,128)}, f32[1,1,256]{2,1,0:T(1,128)S(1)}, u32[]{:S(2)}) copy-start(f32[1,1,256]{2,1,0:T(1,128)S(1)} %get-tuple-element.109) | copy-start | bytes 3076
  8.9 8.8 %copy-start.62 = (f32[1,1,256]{2,1,0:T(1,128)}, f32[1,1,256]{2,1,0:T(1,128)S(1)}, u32[]{:S(2)}) copy-start(f32[1,1,256]{2,1,0:T(1,128)S(1)} %get-tuple-element.110) | copy-start | bytes 3076
  8.9 8.8 %copy-start.12 = (f32[1,1,256]{2,1,0:T(1,128)}, f32[1,1,256]{2,1,0:T(1,128)S(1)}, u32[]{:S(2)}) copy-start(f32[1,1,256]{2,1,0:T(1,128)S(1)} %get-tuple-element.136) | copy-start | bytes 3076
  8.9 8.8 %copy-start.14 = (f32[1,1,256]{2,1,0:T(1,128)}, f32[1,1,256]{2,1,0:T(1,128)S(1)}, u32[]{:S(2)}) copy-start(f32[1,1,256]{2,1,0:T(1,128)S(1)} %get-tuple-element.137) | copy-start | bytes 3076
  9.0 8.8 %copy-start.16 = (f32[1,1,256]{2,1,0:T(1,128)}, f32[1,1,256]{2,1,0:T(1,128)S(1)}, u32[]{:S(2)}) copy-start(f32[1,1,256]{2,1,0:T(1,128)S(1)} %get-tuple-element.138) | copy-start | bytes 3076
  9.0 8.8 %copy-start.20 = (f32[1,1,256]{2,1,0:T(1,128)}, f32[1,1,256]{2,1,0:T(1,128)S(1)}, u32[]{:S(2)}) copy-start(f32[1,1,256]{2,1,0:T(1,128)S(1)} %get-tuple-element.139) | copy-start | bytes 3076
  9.0 8.8 %copy-start.22 = (f32[1,1,256]{2,1,0:T(1,128)}, f32[1,1,256]{2,1,0:T(1,128)S(1)}, u32[]{:S(2)}) copy-start(f32[1,1,256]{2,1,0:T(1,128)S(1)} %get-tuple-element.140) | copy-start | bytes 3076
  9.0 8.8 %copy-start.38 = (f32[1,1,256]{2,1,0:T(1,128)}, f32[1,1,256]{2,1,0:T(1,128)S(1)}, u32[]{:S(2)}) copy-start(f32[1,1,256]{2,1,0:T(1,128)S(1)} %get-tuple-element.131) | copy-start | bytes 3076
  9.0 8.8 %copy-start.40 = (f32[1,1,256]{2,1,0:T(1,128)}, f32[1,1,256]{2,1,0:T(1,128)S(1)}, u32[]{:S(2)}) copy-start(f32[1,1,256]{2,1,0:T(1,128)S(1)} %get-tuple-element.132) | copy-start | bytes 3076
  9.0 8.8 %copy-start.42 = (f32[1,1,256]{2,1,0:T(1,128)}, f32[1,1,256]{2,1,0:T(1,128)S(1)}, u32[]{:S(2)}) copy-start(f32[1,1,256]{2,1,0:T(1,128)S(1)} %get-tuple-element.133) | copy-start | bytes 3076
  9.0 8.8 %copy-start.44 = (f32[1,1,256]{2,1,0:T(1,128)}, f32[1,1,256]{2,1,0:T(1,128)S(1)}, u32[]{:S(2)}) copy-start(f32[1,1,256]{2,1,0:T(1,128)S(1)} %get-tuple-element.134) | copy-start | bytes 3076
  9.6 8.2 %copy-start.50 = (f32[1,1,256]{2,1,0:T(1,128)}, f32[1,1,256]{2,1,0:T(1,128)S(1)}, u32[]{:S(2)}) copy-start(f32[1,1,256]{2,1,0:T(1,128)S(1)} %get-tuple-element.129) | copy-start | bytes 3076
  9.6 8.2 %copy-start.64 = (f32[1,1,256]{2,1,0:T(1,128)}, f32[1,1,256]{2,1,0:T(1,128)S(1)}, u32[]{:S(2)}) copy-start(f32[1,1,256]{2,1,0:T(1,128)S(1)} %get-tuple-element.120) | copy-start | bytes 3076
  9.6 8.2 %copy-start.66 = (f32[1,1,256]{2,1,0:T(1,128)}, f32[1,1,256]{2,1,0:T(1,128)S(1)}, u32[]{:S(2)}) copy-start(f32[1,1,256]{2,1,0:T(1,128)S(1)} %get-tuple-element.121) | copy-start | bytes 3076
  9.6 8.2 %copy-start.68 = (f32[1,1,256]{2,1,0:T(1,128)}, f32[1,1,256]{2,1,0:T(1,128)S(1)}, u32[]{:S(2)}) copy-start(f32[1,1,256]{2,1,0:T(1,128)S(1)} %get-tuple-element.122) | copy-start | bytes 3076
  9.7 8.2 %copy-start.70 = (f32[1,1,256]{2,1,0:T(1,128)}, f32[1,1,256]{2,1,0:T(1,128)S(1)}, u32[]{:S(2)}) copy-start(f32[1,1,256]{2,1,0:T(1,128)S(1)} %get-tuple-element.123) | copy-start | bytes 3076
  9.7 8.2 %copy-start.72 = (f32[1,1,256]{2,1,0:T(1,128)}, f32[1,1,256]{2,1,0:T(1,128)S(1)}, u32[]{:S(2)}) copy-start(f32[1,1,256]{2,1,0:T(1,128)S(1)} %get-tuple-element.124) | copy-start | bytes 3076
  9.7 8.2 %copy-start.74 = (f32[1,1,256]{2,1,0:T(1,128)}, f32[1,1,256]{2,1,0:T(1,128)S(1)}, u32[]{:S(2)}) copy-start(f32[1,1,256]{2,1,0:T(1,128)S(1)} %get-tuple-element.125) | copy-start | bytes 3076
  9.7 8.2 %copy-start.76 = (f32[1,1,256]{2,1,0:T(1,128)}, f32[1,1,256]{2,1,0:T(1,128)S(1)}, u32[]{:S(2)}) copy-start(f32[1,1,256]{2,1,0:T(1,128)S(1)} %get-tuple-element.126) | copy-start | bytes 3076
  9.7 8.2 %copy-start.78 = (f32[1,1,256]{2,1,0:T(1,128)}, f32[1,1,256]{2,1,0:T(1,128)S(1)}, u32[]{:S(2)}) copy-start(f32[1,1,256]{2,1,0:T(1,128)S(1)} %get-tuple-element.112) | copy-start | bytes 3076
  9.7 8.2 %copy-start.81 = (f32[1,1,256]{2,1,0:T(1,128)}, f32[1,1,256]{2,1,0:T(1,128)S(1)}, u32[]{:S(2)}) copy-start(f32[1,1,256]{2,1,0:T(1,128)S(1)} %get-tuple-element.113) | copy-start | bytes 3076
  9.7 8.2 %copy-start.83 = (f32[1,1,256]{2,1,0:T(1,128)}, f32[1,1,256]{2,1,0:T(1,128)S(1)}, u32[]{:S(2)}) copy-start(f32[1,1,256]{2,1,0:T(1,128)S(1)} %get-tuple-element.114) | copy-start | bytes 3076
  9.7 8.2 %copy-start.85 = (f32[1,1,256]{2,1,0:T(1,128)}, f32[1,1,256]{2,1,0:T(1,128)S(1)}, u32[]{:S(2)}) copy-start(f32[1,1,256]{2,1,0:T(1,128)S(1)} %get-tuple-element.115) | copy-start | bytes 3076
  9.7 8.2 %copy-start.87 = (f32[1,1,256]{2,1,0:T(1,128)}, f32[1,1,256]{2,1,0:T(1,128)S(1)}, u32[]{:S(2)}) copy-start(f32[1,1,256]{2,1,0:T(1,128)S(1)} %get-tuple-element.116) | copy-start | bytes 3076
  9.7 8.2 %copy-start.89 = (f32[1,1,256]{2,1,0:T(1,128)}, f32[1,1,256]{2,1,0:T(1,128)S(1)}, u32[]{:S(2)}) copy-start(f32[1,1,256]{2,1,0:T(1,128)S(1)} %get-tuple-element.117) | copy-start | bytes 3076
  39.1 13.0 %collective-permute-start.4 = (f32[51,256]{1,0:T(8,128)S(1)}, f32[51,256]{1,0:T(8,128)S(1)}, u32[]{:S(2)}, u32[]{:S(2)}) collective-permute-start(f32[51,256]{1,0:T(8,128)S(1)} %concatenate.17), channel_id=1, source_target_pairs={{0,1},{1,0},{2,3},{3,2},{4,5},{5,4},{6,7},{7,6},{8,9},{9,8},{10,11... | collective-permute-start | bytes 156680 | tf_op jit(solution)/shard_map/ppermute | solution.py:71
  44.2 8.0 %collective-permute-start.3 = (f32[512,256]{1,0:T(8,128)S(1)}, f32[512,256]{1,0:T(8,128)S(1)}, u32[]{:S(2)}, u32[]{:S(2)}) collective-permute-start(f32[512,256]{1,0:T(8,128)S(1)} %constant_dynamic-slice_fusion), channel_id=1, source_target_pairs={{0,1},{1,0},{2,3},{3,2},{4,5},{5,4},{6,7},{7,6},{8,9},{9,8},{10,11... | collective-permute-start | bytes 1572872 | tf_op jit(solution)/shard_map/ppermute | solution.py:71
  45.5 7.2 %collective-permute-start.2 = (f32[4,128,256]{2,1,0:T(8,128)S(1)}, f32[4,128,256]{2,1,0:T(8,128)S(1)}, u32[]{:S(2)}, u32[]{:S(2)}) collective-permute-start(f32[4,128,256]{2,1,0:T(8,128)S(1)} %constant_dynamic-slice_fusion.1), channel_id=1, source_target_pairs={{0,1},{1,0},{2,3},{3,2},{4,5},{5,4},{6,7},{7,6},{8,9},{9,8},{10,11... | collective-permute-start | bytes 1572872 | tf_op jit(solution)/shard_map/ppermute | solution.py:71
  46.5 24.0 %collective-permute-start.6 = (bf16[3,256,256]{2,1,0:T(8,128)(2,1)}, bf16[3,256,256]{2,1,0:T(8,128)(2,1)}, u32[]{:S(2)}, u32[]{:S(2)}) collective-permute-start(bf16[3,256,256]{2,1,0:T(8,128)(2,1)} %get-tuple-element.85), channel_id=1, source_target_pairs={{0,1},{1,2},{2,3},{3,4},{4,5},{5,6},{6,7},{7,8},{8,9},{9,10},{10,1... | collective-permute-start | bytes 1179656 | tf_op jit(solution)/shard_map/ppermute | solution.py:103
  48.9 21.6 %collective-permute-start.7 = (bf16[3,256,256]{2,1,0:T(8,128)(2,1)}, bf16[3,256,256]{2,1,0:T(8,128)(2,1)}, u32[]{:S(2)}, u32[]{:S(2)}) collective-permute-start(bf16[3,256,256]{2,1,0:T(8,128)(2,1)} %get-tuple-element.84), channel_id=1, source_target_pairs={{1,0},{2,1},{3,2},{4,3},{5,4},{6,5},{7,6},{8,7},{9,8},{10,9},{11,1... | collective-permute-start | bytes 1179656 | tf_op jit(solution)/shard_map/ppermute | solution.py:104
  53.6 14.2 %collective-permute-start.5 = (bf16[614,256]{1,0:T(8,128)(2,1)}, bf16[614,256]{1,0:T(8,128)(2,1)}, u32[]{:S(2)}, u32[]{:S(2)}) collective-permute-start(bf16[614,256]{1,0:T(8,128)(2,1)} %pad_maximum_fusion), channel_id=1, source_target_pairs={{0,2},{1,3},{2,0},{3,1},{4,6},{5,7},{6,4},{7,5},{8,10},{9,11},{10,... | collective-permute-start | bytes 943112 | tf_op jit(solution)/shard_map/ppermute | solution.py:79
  74.6 9.6 %copy-start.4 = (bf16[4,256,256]{2,1,0:T(8,128)(2,1)S(1)}, bf16[4,256,256]{2,1,0:T(8,128)(2,1)}, u32[]{:S(2)}) copy-start(bf16[4,256,256]{2,1,0:T(8,128)(2,1)} %param.15) | copy-start | bytes 1572868
  74.8 6.7 %collective-permute-start.8 = (bf16[358,256]{1,0:T(8,128)(2,1)S(1)}, bf16[358,256]{1,0:T(8,128)(2,1)S(1)}, u32[]{:S(2)}, u32[]{:S(2)}) collective-permute-start(bf16[358,256]{1,0:T(8,128)(2,1)S(1)} %pad_maximum_fusion.1), channel_id=1, source_target_pairs={{0,4},{1,5},{2,6},{3,7},{4,0},{5,1},{6,2},{7,3},{8,12},{9,13},{10,... | collective-permute-start | bytes 549896 | tf_op jit(solution)/shard_map/ppermute | solution.py:79
  81.6 7.9 %collective-permute-start.9 = (bf16[230,256]{1,0:T(8,128)(2,1)S(1)}, bf16[230,256]{1,0:T(8,128)(2,1)S(1)}, u32[]{:S(2)}, u32[]{:S(2)}) collective-permute-start(bf16[230,256]{1,0:T(8,128)(2,1)S(1)} %pad_maximum_fusion.2), channel_id=1, source_target_pairs={{0,8},{1,9},{2,10},{3,11},{4,12},{5,13},{6,14},{7,15},{8,0},{9,1},... | collective-permute-start | bytes 353288 | tf_op jit(solution)/shard_map/ppermute | solution.py:79
  (56 other events, 130.8 us)

commit v12 on v10

--- a/solution.py
+++ b/solution.py
@@ -100,6 +100,20 @@
     return low, high
 
 
+def row_taps(line_of, kernel, out_rows, out_cols):
+    rows = []
+    for out_row in range(out_rows):
+        total = jnp.zeros((out_cols, kernel.shape[-1]), jnp.float32)
+        for row_tap in range(KERNEL):
+            line = line_of(out_row + row_tap)
+            if line is None:
+                continue
+            for col_tap in range(KERNEL):
+                total = total + line[col_tap : col_tap + out_cols] * kernel[row_tap, col_tap]
+        rows.append(total)
+    return jnp.stack(rows)
+
+
 def gelu_value(inputs):
     tangent = jnp.tanh(ROOT_TWO_PI * (inputs + CUBIC_TERM * inputs * inputs * inputs))
     return 0.5 * inputs * (1.0 + tangent)
@@ -144,10 +158,36 @@
     span = TILE_COLS + 2 * half_width
 
     first_col = jnp.argmax(tissue.reshape(-1)).astype(jnp.int32) * TILE_COLS
-    extended = padded_2(image, (("row", 0),), half_width)
+    image_low, image_high = halo_rows(image, "row", half_width)
+    extended = jnp.concatenate([image_low, image, image_high], axis=0)
     padded = jnp.pad(extended, ((0, 0), (half_width, half_width), (0, 0)))
     window = lax.dynamic_slice_in_dim(padded, first_col, span, axis=1).astype(jnp.float32)
-    filtered = depthwise(window, kernel, image_rows, TILE_COLS)
+    own_window = lax.dynamic_slice_in_dim(
+        jnp.pad(image, ((0, 0), (half_width, half_width), (0, 0))), first_col, span, axis=1
+    ).astype(jnp.float32)
+    low_window = lax.dynamic_slice_in_dim(
+        jnp.pad(image_low, ((0, 0), (half_width, half_width), (0, 0))), first_col, span, axis=1
+    ).astype(jnp.float32)
+    high_window = lax.dynamic_slice_in_dim(
+        jnp.pad(image_high, ((0, 0), (half_width, half_width), (0, 0))), first_col, span, axis=1
+    ).astype(jnp.float32)
+    own_part = row_taps(
+        lambda source: own_window[source - half_width]
+        if half_width <= source < half_width + image_rows
+        else None,
+        kernel,
+        image_rows,
+        TILE_COLS,
+    )
+    halo_part = row_taps(
+        lambda source: low_window[source]
+        if source < half_width
+        else (high_window[source - half_width - image_rows] if source >= half_width + image_rows else None),
+        kernel,
+        image_rows,
+        TILE_COLS,
+    )
+    filtered = own_part + halo_part
     centre = jnp.mean(filtered, axis=-1, keepdims=True)
     centered = filtered - centre
     inv_std = lax.rsqrt(jnp.mean(centered * centered, axis=-1, keepdims=True) + EPSILON)

time: 86 us -> 91.5 us (1.064)
  local copies, waits for them, and re-layouts: 11.5 us -> 16 us
  starting transfers between devices: 21.5 us -> 24.1 us
  other arithmetic: 25 us -> 22.8 us
    concatenate x1, local copies, waits for them, and re-layouts: 0.18 us -> 5.06 us  [shards(): jnp.concatenate([kernel_grad, gain_grad[None], scale_grad[None]], axis=0)]
    reduce_sum x1, other arithmetic: 4.6 us -> 0.16 us  [shards(): centre = jnp.mean(filtered, axis=-1, keepdims=True)]
    ppermute x2 -> x0, starting transfers between devices: 3.67 us -> none  [the longest x1 2.38 us: padded_2(): lax.ppermute(lax.slice_in_dim(block, block.shape[dim] - width, None, axis...]
    add x0 -> x8, other arithmetic: none -> 3.26 us  [row_taps(): total = total + line[col_tap:col_tap + out_cols] * kernel[row_tap, col_tap]]
    ppermute x3, starting transfers between devices: 7.26 us -> 9.93 us  [halving_reduce(): got = lax.ppermute(sent, axis, pairs)]
    ppermute x1 -> x2, starting transfers between devices: 3 us -> 5.51 us  [halo_rows(): lax.ppermute(lax.slice_in_dim(block, block.shape[0] - width, None, axis=0...]
    reduce_sum x3, other arithmetic: 3.28 us -> 5.27 us  [kernel_terms(): jnp.sum(padded[row_tap:row_tap + image_rows, col_tap:col_tap + image_cols...]
    ppermute x2 -> x0, waiting for transfers between devices: 1.98 us -> none  [the longest x1 1.97 us: padded_2(): lax.ppermute(lax.slice_in_dim(block, 0, width, axis=dim), axis, backward)]
  transfers between devices with their start and end apart: 10 -> 10, of which waited for: 4 -> 4; matrix products, arithmetic and copies ran while one was open for 26% -> 22% of each run, Pallas kernels for 0% -> 0%
where the time goes in v12:
time: 91.5 us; the launch traced here: 90.9 us
  starting transfers between devices  24.1 us (26%)
  other arithmetic  22.8 us (25%)
  local copies, waits for them, and re-layouts  16 us (17%)
  waiting for transfers between devices  15.2 us (17%)
  matrix products  9.42 us (10%)
  between operations  3.49 us (4%)
    ppermute x3, waiting for transfers between devices, halving_reduce(): got = lax.ppermute(sent, axis, pairs)  14.7 us
    ppermute x3, starting transfers between devices, halving_reduce(): got = lax.ppermute(sent, axis, pairs)  9.93 us
    ppermute x3, starting transfers between devices, halving_reduce(): got_q, got_r, got_whole = lax.ppermute((give_q, give_r, whole), axis, pairs)  6.05 us
    ppermute x2, starting transfers between devices, halo_rows(): lax.ppermute(lax.slice_in_dim(block, block.shape[0] - width, None, axis=0...  5.51 us
    reduce_sum x3, other arithmetic, kernel_terms(): jnp.sum(padded[row_tap:row_tap + image_rows, col_tap:col_tap + image_cols...  5.27 us
    concatenate x1, local copies, waits for them, and re-layouts, shards(): jnp.concatenate([kernel_grad, gain_grad[None], scale_grad[None]], axis=0)  5.06 us
    dot_general x4, matrix products, shards(): lax.dot_general(normed_flat, pre_flat[:, q * channels:(q + 1) * channels]...  3.77 us
    add x8, other arithmetic, row_taps(): total = total + line[col_tap:col_tap + out_cols] * kernel[row_tap, col_tap]  3.26 us
  transfers between devices with their start and end apart: 10, of which 4 were waited for; matrix products, arithmetic and copies ran while one was open for 22% of the time, Pallas kernels for 0%

profile of v12, /device:TPU:0, one launch (start us, length us, event | category | flops | bytes accessed | tf_op | source)
XLA Modules:
  0.0 90.9 jit_solution(6208970295725235199)
XLA Ops:
  0.7 1.1 %copy.38 = bf16[4,256,256]{2,1,0:T(8,128)(2,1)S(1)} copy(bf16[4,256,256]{2,1,0:T(8,128)(2,1)} %param.8) | data formatting | bytes 1048576
  1.8 0.8 fusion.251
  2.6 2.4 %collective-permute-start = (bf16[3,256,256]{2,1,0:T(8,128)(2,1)}, bf16[3,256,256]{2,1,0:T(8,128)(2,1)S(1)}, u32[]{:S(2)}, u32[]{:S(2)}) collective-permute-start(bf16[3,256,256]{2,1,0:T(8,128)(2,1)} %get-tuple-element.90), channel_id=1, source_target_pairs={{0,1},{1,2},{2,3},{3,4},{4,5},{5,6},{6,7},{7,8},{8,9},{9,10},{10,1... | collective-permute-start | bytes 1179656 | tf_op jit(solution)/shard_map/ppermute | solution.py:98
  5.0 1.3 %collective-permute-start.1 = (bf16[3,256,256]{2,1,0:T(8,128)(2,1)S(1)}, bf16[3,256,256]{2,1,0:T(8,128)(2,1)S(1)}, u32[]{:S(2)}, u32[]{:S(2)}) collective-permute-start(bf16[3,256,256]{2,1,0:T(8,128)(2,1)S(1)} %get-tuple-element.91), channel_id=1, source_target_pairs={{1,0},{2,1},{3,2},{4,3},{5,4},{6,5},{7,6},{8,7},{9,8},{10,9},{11,1... | collective-permute-start | bytes 1179656 | tf_op jit(solution)/shard_map/ppermute | solution.py:99
  6.7 0.7 bitcast_reduce_fusion
  8.1 0.5 multiply_add_fusion.6
  8.6 0.5 multiply_add_fusion.7
  9.0 0.5 multiply_add_fusion.8
  10.2 0.5 collective-permute-done.1
  13.1 1.8 %fusion.11 = (bf16[1024,512]{0,1:T(8,128)(2,1)}, f32[512,1024]{1,0:T(8,128)S(1)}) fusion(bf16[512,256]{1,0:T(8,128)(2,1)S(1)} %multiply_convert_fusion.3, bf16[256,1024]{1,0:T(8,128)(2,1)S(1)} %copy-done), kind=kOutput, calls=%fused_computation.112 | convolution fusion | flops 273154048 | bytes 3932160 | tf_op jit(solution)/shard_map/dot_general | solution.py:201
  14.9 0.8 fusion.122
  15.8 1.4 %fusion.6 = bf16[512,1024]{1,0:T(8,128)(2,1)S(1)} fusion(f32[512,1024]{1,0:T(8,128)S(1)} %get-tuple-element.156, bf16[512,256]{1,0:T(8,128)(2,1)S(1)} %bitcast.206, bf16[1024,256]{1,0:T(8,128)(2,1)S(1)} %copy-done.18), kind=kOutput, calls=%fused_computation.107 | convolution fusion | flops 278396928 | bytes 3932160 | tf_op jit(solution)/shard_map/dot_general | solution.py:204
  17.2 1.1 %multiply_reduce_fusion = (f32[256]{0:T(256)}, f32[512]{0:T(512)S(1)}, f32[512]{0:T(512)S(1)}, f32[512,256]{1,0:T(8,128)S(1)}) fusion(f32[4,128,256]{2,1,0:T(8,128)S(1)} %get-tuple-element.85, f32[512]{0:T(512)S(1)} %get-tuple-element.150, f32[512]{0:T(512)S(1)} %get-tuple-element.151, f32[256]{0:T(256)S(1)} %copy-done.118, ...), kind=kOutput, calls=%fused_computation.292 | convolution fusion | flops 269482752 | bytes 2631680 | tf_op jit(solution)/shard_map/dot_general | solution.py:206
  18.7 2.1 %fusion.169 = (f32[256]{0:T(256)S(1)}, f32[256]{0:T(256)S(1)}, f32[256]{0:T(256)S(1)}, f32[256]{0:T(256)S(1)}, f32[256]{0:T(256)S(1)}, /*index=5*/f32[256]{0:T(2...) fusion(f32[10,134,256]{2,1,0:T(8,128)S(1)} %fusion.21, ...), kind=kLoop, calls=%fused_computation.286 | loop fusion | flops 4584192 | bytes 8148992 | tf_op jit(solution)/shard_map/reduce_sum | solution.py:146
  20.8 1.6 %fusion.170 = (f32[256]{0:T(256)}, f32[256]{0:T(256)}, f32[256]{0:T(256)}, f32[256]{0:T(256)}, f32[256]{0:T(256)}, /*index=5*/f32[256]{0:T(256)}, f32[256]{0:T(2...) fusion(bf16[4,128,256]{2,1,0:T(8,128)(2,1)S(1)} %get-tuple-elem, ...), kind=kLoop, calls=%fused_computation.287 | loop fusion | flops 4845056 | bytes 9717760 | tf_op jit(solution)/shard_map/reduce_sum | solution.py:146
  22.4 1.6 %fusion.171 = (f32[256]{0:T(256)}, f32[256]{0:T(256)}, f32[256]{0:T(256)}, f32[256]{0:T(256)}, f32[256]{0:T(256)}, /*index=5*/f32[256]{0:T(256)}, f32[256]{0:T(2...) fusion(bf16[4,128,256]{2,1,0:T(8,128)(2,1)S(1)} %get-tuple-elem, ...), kind=kLoop, calls=%fused_computation.288 | loop fusion | flops 4845056 | bytes 9717760 | tf_op jit(solution)/shard_map/reduce_sum | solution.py:146
  24.2 0.9 %convolution_bitcast_fusion.1 = f32[1,2,2,2,2,16,256]{6,5,4,3,2,1,0:T(8,128)} fusion(bf16[2,2,2,2,16,512]{5,4,3,2,1,0:T(8,128)(2,1)S(1)} %bitcast.196, bf16[512,1024]{1,0:T(8,128)(2,1)S(1)} %copy-done.9), kind=kOutput, calls=%fused_computation.123 | convolution fusion | flops 67108864 | bytes 786432 | tf_op jit(solution)/shard_map/dot_general | solution.py:210
  25.1 1.0 %convolution_bitcast_fusion.2 = f32[1,2,2,2,2,16,256]{6,5,4,3,2,1,0:T(8,128)} fusion(bf16[2,2,2,2,16,512]{5,4,3,2,1,0:T(8,128)(2,1)S(1)} %bitcast.197, bf16[512,1024]{1,0:T(8,128)(2,1)S(1)} %copy-done.9), kind=kOutput, calls=%fused_computation.124 | convolution fusion | flops 67108864 | bytes 786432 | tf_op jit(solution)/shard_map/dot_general | solution.py:210
  26.1 0.9 %convolution_bitcast_fusion.3 = f32[1,2,2,2,2,16,256]{6,5,4,3,2,1,0:T(8,128)} fusion(bf16[2,2,2,2,16,512]{5,4,3,2,1,0:T(8,128)(2,1)S(1)} %bitcast.198, bf16[512,1024]{1,0:T(8,128)(2,1)S(1)} %copy-done.9), kind=kOutput, calls=%fused_computation.125 | convolution fusion | flops 67108864 | bytes 786432 | tf_op jit(solution)/shard_map/dot_general | solution.py:210
  27.0 0.9 %convolution_bitcast_fusion.4 = f32[1,2,2,2,2,16,256]{6,5,4,3,2,1,0:T(8,128)} fusion(bf16[2,2,2,2,16,512]{5,4,3,2,1,0:T(8,128)(2,1)S(1)} %bitcast.199, bf16[512,1024]{1,0:T(8,128)(2,1)S(1)} %copy-done.9), kind=kOutput, calls=%fused_computation.126 | convolution fusion | flops 67108864 | bytes 786432 | tf_op jit(solution)/shard_map/dot_general | solution.py:210
  27.9 5.1 %concatenate.17 = f32[51,256]{1,0:T(8,128)S(1)} concatenate(f32[1,256]{1,0:T(1,128)} %bitcast.579, f32[1,256]{1,0:T(1,128)} %bitcast.580, f32[1,256]{1,0:T(1,128)} %bitcast.581, f32[1,256]{1,0:T(1,128)} %bitcast.582, f32[1,256]{1,0:T(1,128)} %bitcast.583, f32[1,256]{1,0:T(1,128)} %bitcast.584, f32[1,256]{1,0:T(1,128)} %bitcast.585, f32[1,256]{1,0:T(1,128)} %bitcast.586, ...), dimensions={0} | concatenate | bytes 104448 | tf_op jit(solution)/shard_map/concatenate | solution.py:239
  33.0 6.0 %collective-permute-start.6 = (f32[51,256]{1,0:T(8,128)S(1)}, f32[51,256]{1,0:T(8,128)}, u32[]{:S(2)}, u32[]{:S(2)}) collective-permute-start(f32[51,256]{1,0:T(8,128)S(1)} %concatenate.17), channel_id=1, source_target_pairs={{0,1},{1,0},{2,3},{3,2},{4,5},{5,4},{6,7},{7,6},{8,9},{9,8},{10,11... | collective-permute-start | bytes 156680 | tf_op jit(solution)/shard_map/ppermute | solution.py:69
  39.0 1.5 %copy.25 = bf16[1024,512]{1,0:T(8,128)(2,1)S(1)} copy(bf16[1024,512]{0,1:T(8,128)(2,1)} %get-tuple-element.155) | data formatting | bytes 2097152 | tf_op jit(solution)/shard_map/convert_element_type | solution.py:202
  41.1 0.8 constant_dynamic-slice_fusion
  43.1 0.9 constant_dynamic-slice_fusion.1
  44.1 0.9 %fusion.250 = (bf16[3,256,256]{2,1,0:T(8,128)(2,1)}, bf16[3,256,256]{2,1,0:T(8,128)(2,1)}) fusion(bf16[4,256,256]{2,1,0:T(8,128)(2,1)S(1)} %get-tuple-element.92), kind=kLoop, calls=%fused_computation.467 | loop fusion | bytes 1572864 | tf_op jit(solution)/shard_map/slice | solution.py:98
  45.1 3.1 %collective-permute-start.2 = (bf16[3,256,256]{2,1,0:T(8,128)(2,1)}, bf16[3,256,256]{2,1,0:T(8,128)(2,1)}, u32[]{:S(2)}, u32[]{:S(2)}) collective-permute-start(bf16[3,256,256]{2,1,0:T(8,128)(2,1)} %get-tuple-element.88), channel_id=1, source_target_pairs={{0,1},{1,2},{2,3},{3,4},{4,5},{5,6},{6,7},{7,8},{8,9},{9,10},{10,1... | collective-permute-start | bytes 1179656 | tf_op jit(solution)/shard_map/ppermute | solution.py:98
  48.2 1.3 %collective-permute-start.3 = (bf16[3,256,256]{2,1,0:T(8,128)(2,1)}, bf16[3,256,256]{2,1,0:T(8,128)(2,1)}, u32[]{:S(2)}, u32[]{:S(2)}) collective-permute-start(bf16[3,256,256]{2,1,0:T(8,128)(2,1)} %get-tuple-element.89), channel_id=1, source_target_pairs={{1,0},{2,1},{3,2},{4,3},{5,4},{6,5},{7,6},{8,7},{9,8},{10,9},{11,1... | collective-permute-start | bytes 1179656 | tf_op jit(solution)/shard_map/ppermute | solution.py:99
  49.8 2.7 %fusion.115 = f32[4,134,256]{2,1,0:T(8,128)S(1)} fusion(f32[4,128,256]{2,1,0:T(8,128)S(1)} %get-tuple-element.93, f32[256]{0:T(256)S(1)} %bitcast.308, f32[256]{0:T(256)S(1)} %bitcast.300, f32[256]{0:T(256)S(1)} %bitcast.292, f32[256]{0:T(256)S(1)} %bitcast.284, f32[256]{0:T(256)S(1)} %bitcast.276, f32[256]{0:T(256)S(1)} %bitcast.324, f32[256]{0:T(256)S(1)} %bitcast.316, ...), kind=kLoop, calls=%fused_computation.231 | loop fusion | flops 13309952 | bytes 1123328 | tf_op jit(solution)/shard_map/add | solution.py:134
  52.8 2.2 %dynamic_update_slice.10 = f32[4,262,256]{2,1,0:T(8,128)S(1)} dynamic-update-slice(f32[4,262,256]{2,1,0:T(8,128)S(1)} %broadcast_in_dim.8, f32[4,134,256]{2,1,0:T(8,128)S(1)} %fusion.115, s32[]{:T(128)} %constant.23.clone.1, s32[]{:T(128)S(6)} %select_n.66, s32[]{:T(128)} %constant.23.clone.1) | dynamic-update-slice | bytes 1097732 | tf_op jit(solution)/shard_map/dynamic_update_slice | solution.py:248
  55.0 0.8 add.1733
  55.9 1.1 %convert_element_type.183 = f32[3,256,256]{2,1,0:T(8,128)S(1)} convert(bf16[3,256,256]{2,1,0:T(8,128)(2,1)} %collective-permute-done.2) | non-fusion elementwise | flops 196608 | bytes 1179648 | tf_op jit(solution)/shard_map/convert_element_type | solution.py:259
  56.9 1.1 %convert_element_type.184 = f32[3,256,256]{2,1,0:T(8,128)S(1)} convert(bf16[3,256,256]{2,1,0:T(8,128)(2,1)} %collective-permute-done.3) | non-fusion elementwise | flops 196608 | bytes 1179648 | tf_op jit(solution)/shard_map/convert_element_type | solution.py:260
  58.2 0.7 multiply_add_fusion.3
  59.4 1.1 %dynamic-slice_add_fusion.1 = f32[4,128,256]{2,1,0:T(8,128)S(1)} fusion(f32[4,128,256]{2,1,0:T(8,128)} %collective-permute-done.4, f32[4,256,256]{2,1,0:T(8,128)S(1)} %bitcast.203, s32[]{:T(128)S(6)} %select_n.67), kind=kLoop, calls=%fused_computation.294 | loop fusion | flops 131072 | bytes 1572868 | tf_op jit(solution)/shard_map/add | solution.py:88
  60.7 3.7 %collective-permute-start.7 = (bf16[614,256]{1,0:T(8,128)(2,1)S(1)}, bf16[614,256]{1,0:T(8,128)(2,1)S(1)}, u32[]{:S(2)}, u32[]{:S(2)}) collective-permute-start(bf16[614,256]{1,0:T(8,128)(2,1)S(1)} %pad_maximum_fusion), channel_id=1, source_target_pairs={{0,2},{1,3},{2,0},{3,1},{4,6},{5,7},{6,4},{7,5},{8,10},{9,11},{10,... | collective-permute-start | bytes 943112 | tf_op jit(solution)/shard_map/ppermute | solution.py:77
  64.4 0.7 fusion.178
  65.2 0.7 multiply_add_fusion.2
  65.8 6.1 %collective-permute-done.7 = bf16[614,256]{1,0:T(8,128)(2,1)S(1)} collective-permute-done((bf16[614,256]{1,0:T(8,128)(2,1)S(1)}, bf16[614,256]{1,0:T(8,128)(2,1)S(1)}, u32[]{:S(2)}, u32[]{:S(2)}) %collective-permute-start.7) | collective-permute-done | bytes 314400 | tf_op jit(solution)/shard_map/ppermute | solution.py:77
  72.2 3.4 %collective-permute-start.8 = (bf16[358,256]{1,0:T(8,128)(2,1)S(1)}, bf16[358,256]{1,0:T(8,128)(2,1)S(1)}, u32[]{:S(2)}, u32[]{:S(2)}) collective-permute-start(bf16[358,256]{1,0:T(8,128)(2,1)S(1)} %pad_maximum_fusion.1), channel_id=1, source_target_pairs={{0,4},{1,5},{2,6},{3,7},{4,0},{5,1},{6,2},{7,3},{8,12},{9,13},{10,... | collective-permute-start | bytes 549896 | tf_op jit(solution)/shard_map/ppermute | solution.py:77
  75.7 0.7 fusion.196
  76.3 4.2 %collective-permute-done.8 = bf16[358,256]{1,0:T(8,128)(2,1)S(1)} collective-permute-done((bf16[358,256]{1,0:T(8,128)(2,1)S(1)}, bf16[358,256]{1,0:T(8,128)(2,1)S(1)}, u32[]{:S(2)}, u32[]{:S(2)}) %collective-permute-start.8) | collective-permute-done | bytes 183328 | tf_op jit(solution)/shard_map/ppermute | solution.py:77
  80.7 2.8 %collective-permute-start.9 = (bf16[230,256]{1,0:T(8,128)(2,1)S(1)}, bf16[230,256]{1,0:T(8,128)(2,1)S(1)}, u32[]{:S(2)}, u32[]{:S(2)}) collective-permute-start(bf16[230,256]{1,0:T(8,128)(2,1)S(1)} %pad_maximum_fusion.2), channel_id=1, source_target_pairs={{0,8},{1,9},{2,10},{3,11},{4,12},{5,13},{6,14},{7,15},{8,0},{9,1},... | collective-permute-start | bytes 353288 | tf_op jit(solution)/shard_map/ppermute | solution.py:77
  83.5 1.1 %fusion.16 = bf16[4,256,256]{2,1,0:T(8,128)(2,1)} fusion(f32[4,262,256]{2,1,0:T(8,128)S(1)} %dynamic_update_slice.10, f32[1,256,256]{2,1,0:T(8,128)S(1)} %fusion.178, f32[1,256,256]{2,1,0:T(8,128)S(1)} %multiply_add_fusion.2, f32[1,256,256]{2,1,0:T(8,128)S(1)} %multiply_add_fusion.3, f32[1,256,256]{2,1,0:T(8,128)S(1)} %fusion.196, ...), kind=kLoop, calls=%fused_computation.129 | loop fusion | flops 1835008 | bytes 3145728 | tf_op jit(solution)/shard_map/convert_element_type | solution.py:276
  84.6 4.3 %collective-permute-done.9 = bf16[230,256]{1,0:T(8,128)(2,1)S(1)} collective-permute-done((bf16[230,256]{1,0:T(8,128)(2,1)S(1)}, bf16[230,256]{1,0:T(8,128)(2,1)S(1)}, u32[]{:S(2)}, u32[]{:S(2)}) %collective-permute-start.9) | collective-permute-done | bytes 117792 | tf_op jit(solution)/shard_map/ppermute | solution.py:77
  89.0 0.6 fusion.242
  89.6 0.6 convert_add_fusion.8
  90.3 0.6 copy.33
  (302 shorter events, 6.0 us)
Async XLA Ops:
  0.6 12.4 %copy-start = (bf16[256,1024]{1,0:T(8,128)(2,1)S(1)}, bf16[256,1024]{1,0:T(8,128)(2,1)}, u32[]{:S(2)}) copy-start(bf16[256,1024]{1,0:T(8,128)(2,1)} %param.12) | copy-start | bytes 1572868
  2.6 7.5 %collective-permute-start = (bf16[3,256,256]{2,1,0:T(8,128)(2,1)}, bf16[3,256,256]{2,1,0:T(8,128)(2,1)S(1)}, u32[]{:S(2)}, u32[]{:S(2)}) collective-permute-start(bf16[3,256,256]{2,1,0:T(8,128)(2,1)} %get-tuple-element.90), channel_id=1, source_target_pairs={{0,1},{1,2},{2,3},{3,4},{4,5},{5,6},{6,7},{7,8},{8,9},{9,10},{10,1... | collective-permute-start | bytes 1179656 | tf_op jit(solution)/shard_map/ppermute | solution.py:98
  5.0 5.7 %collective-permute-start.1 = (bf16[3,256,256]{2,1,0:T(8,128)(2,1)S(1)}, bf16[3,256,256]{2,1,0:T(8,128)(2,1)S(1)}, u32[]{:S(2)}, u32[]{:S(2)}) collective-permute-start(bf16[3,256,256]{2,1,0:T(8,128)(2,1)S(1)} %get-tuple-element.91), channel_id=1, source_target_pairs={{1,0},{2,1},{3,2},{4,3},{5,4},{6,5},{7,6},{8,7},{9,8},{10,9},{11,1... | collective-permute-start | bytes 1179656 | tf_op jit(solution)/shard_map/ppermute | solution.py:99
  26.1 14.5 %copy-start.11 = (bf16[4,128,256]{2,1,0:T(8,128)(2,1)S(1)}, bf16[4,128,256]{2,1,0:T(8,128)(2,1)}, u32[]{:S(2)}) copy-start(bf16[4,128,256]{2,1,0:T(8,128)(2,1)} %copy-done.10) | copy-start | bytes 786436
  33.0 22.0 %collective-permute-start.6 = (f32[51,256]{1,0:T(8,128)S(1)}, f32[51,256]{1,0:T(8,128)}, u32[]{:S(2)}, u32[]{:S(2)}) collective-permute-start(f32[51,256]{1,0:T(8,128)S(1)} %concatenate.17), channel_id=1, source_target_pairs={{0,1},{1,0},{2,3},{3,2},{4,5},{5,4},{6,7},{7,6},{8,9},{9,8},{10,11... | collective-permute-start | bytes 156680 | tf_op jit(solution)/shard_map/ppermute | solution.py:69
  42.0 17.0 %collective-permute-start.5 = (f32[512,256]{1,0:T(8,128)}, f32[512,256]{1,0:T(8,128)S(1)}, u32[]{:S(2)}, u32[]{:S(2)}) collective-permute-start(f32[512,256]{1,0:T(8,128)} %constant_dynamic-slice_fusion), channel_id=1, source_target_pairs={{0,1},{1,0},{2,3},{3,2},{4,5},{5,4},{6,7},{7,6},{8,9},{9,8},{10,11... | collective-permute-start | bytes 1572872 | tf_op jit(solution)/shard_map/ppermute | solution.py:69
  42.8 6.7 %copy-start.20 = (f32[1,1,256]{2,1,0:T(1,128)S(1)}, f32[1,1,256]{2,1,0:T(1,128)}, u32[]{:S(2)}) copy-start(f32[1,1,256]{2,1,0:T(1,128)} %copy-done.19) | copy-start | bytes 3076
  42.8 6.7 %copy-start.23 = (f32[1,1,256]{2,1,0:T(1,128)S(1)}, f32[1,1,256]{2,1,0:T(1,128)}, u32[]{:S(2)}) copy-start(f32[1,1,256]{2,1,0:T(1,128)} %copy-done.22) | copy-start | bytes 3076
  42.8 6.7 %copy-start.26 = (f32[1,1,256]{2,1,0:T(1,128)S(1)}, f32[1,1,256]{2,1,0:T(1,128)}, u32[]{:S(2)}) copy-start(f32[1,1,256]{2,1,0:T(1,128)} %copy-done.25) | copy-start | bytes 3076
  42.8 6.7 %copy-start.29 = (f32[1,1,256]{2,1,0:T(1,128)S(1)}, f32[1,1,256]{2,1,0:T(1,128)}, u32[]{:S(2)}) copy-start(f32[1,1,256]{2,1,0:T(1,128)} %copy-done.28) | copy-start | bytes 3076
  42.8 6.7 %copy-start.32 = (f32[1,1,256]{2,1,0:T(1,128)S(1)}, f32[1,1,256]{2,1,0:T(1,128)}, u32[]{:S(2)}) copy-start(f32[1,1,256]{2,1,0:T(1,128)} %copy-done.31) | copy-start | bytes 3076
  42.8 6.7 %copy-start.35 = (f32[1,1,256]{2,1,0:T(1,128)S(1)}, f32[1,1,256]{2,1,0:T(1,128)}, u32[]{:S(2)}) copy-start(f32[1,1,256]{2,1,0:T(1,128)} %copy-done.34) | copy-start | bytes 3076
  42.8 6.7 %copy-start.38 = (f32[1,1,256]{2,1,0:T(1,128)S(1)}, f32[1,1,256]{2,1,0:T(1,128)}, u32[]{:S(2)}) copy-start(f32[1,1,256]{2,1,0:T(1,128)} %copy-done.37) | copy-start | bytes 3076
  42.8 6.7 %copy-start.41 = (f32[1,1,256]{2,1,0:T(1,128)S(1)}, f32[1,1,256]{2,1,0:T(1,128)}, u32[]{:S(2)}) copy-start(f32[1,1,256]{2,1,0:T(1,128)} %copy-done.40) | copy-start | bytes 3076
  42.9 6.7 %copy-start.44 = (f32[1,1,256]{2,1,0:T(1,128)S(1)}, f32[1,1,256]{2,1,0:T(1,128)}, u32[]{:S(2)}) copy-start(f32[1,1,256]{2,1,0:T(1,128)} %copy-done.43) | copy-start | bytes 3076
  42.9 6.7 %copy-start.47 = (f32[1,1,256]{2,1,0:T(1,128)S(1)}, f32[1,1,256]{2,1,0:T(1,128)}, u32[]{:S(2)}) copy-start(f32[1,1,256]{2,1,0:T(1,128)} %copy-done.46) | copy-start | bytes 3076
  42.9 6.7 %copy-start.50 = (f32[1,1,256]{2,1,0:T(1,128)S(1)}, f32[1,1,256]{2,1,0:T(1,128)}, u32[]{:S(2)}) copy-start(f32[1,1,256]{2,1,0:T(1,128)} %copy-done.49) | copy-start | bytes 3076
  42.9 6.7 %copy-start.53 = (f32[1,1,256]{2,1,0:T(1,128)S(1)}, f32[1,1,256]{2,1,0:T(1,128)}, u32[]{:S(2)}) copy-start(f32[1,1,256]{2,1,0:T(1,128)} %copy-done.52) | copy-start | bytes 3076
  42.9 6.7 %copy-start.56 = (f32[1,1,256]{2,1,0:T(1,128)S(1)}, f32[1,1,256]{2,1,0:T(1,128)}, u32[]{:S(2)}) copy-start(f32[1,1,256]{2,1,0:T(1,128)} %copy-done.55) | copy-start | bytes 3076
  42.9 6.7 %copy-start.59 = (f32[1,1,256]{2,1,0:T(1,128)S(1)}, f32[1,1,256]{2,1,0:T(1,128)}, u32[]{:S(2)}) copy-start(f32[1,1,256]{2,1,0:T(1,128)} %copy-done.58) | copy-start | bytes 3076
  42.9 6.7 %copy-start.62 = (f32[1,1,256]{2,1,0:T(1,128)S(1)}, f32[1,1,256]{2,1,0:T(1,128)}, u32[]{:S(2)}) copy-start(f32[1,1,256]{2,1,0:T(1,128)} %copy-done.61) | copy-start | bytes 3076
  42.9 6.7 %copy-start.65 = (f32[1,1,256]{2,1,0:T(1,128)S(1)}, f32[1,1,256]{2,1,0:T(1,128)}, u32[]{:S(2)}) copy-start(f32[1,1,256]{2,1,0:T(1,128)} %copy-done.64) | copy-start | bytes 3076
  42.9 6.7 %copy-start.68 = (f32[1,1,256]{2,1,0:T(1,128)S(1)}, f32[1,1,256]{2,1,0:T(1,128)}, u32[]{:S(2)}) copy-start(f32[1,1,256]{2,1,0:T(1,128)} %copy-done.67) | copy-start | bytes 3076
  42.9 6.7 %copy-start.71 = (f32[1,1,256]{2,1,0:T(1,128)S(1)}, f32[1,1,256]{2,1,0:T(1,128)}, u32[]{:S(2)}) copy-start(f32[1,1,256]{2,1,0:T(1,128)} %copy-done.70) | copy-start | bytes 3076
  43.0 6.7 %copy-start.74 = (f32[1,1,256]{2,1,0:T(1,128)S(1)}, f32[1,1,256]{2,1,0:T(1,128)}, u32[]{:S(2)}) copy-start(f32[1,1,256]{2,1,0:T(1,128)} %copy-done.73) | copy-start | bytes 3076
  43.0 6.7 %copy-start.77 = (f32[1,1,256]{2,1,0:T(1,128)S(1)}, f32[1,1,256]{2,1,0:T(1,128)}, u32[]{:S(2)}) copy-start(f32[1,1,256]{2,1,0:T(1,128)} %copy-done.76) | copy-start | bytes 3076
  43.0 6.7 %copy-start.80 = (f32[1,1,256]{2,1,0:T(1,128)S(1)}, f32[1,1,256]{2,1,0:T(1,128)}, u32[]{:S(2)}) copy-start(f32[1,1,256]{2,1,0:T(1,128)} %copy-done.79) | copy-start | bytes 3076
  43.0 6.7 %copy-start.83 = (f32[1,1,256]{2,1,0:T(1,128)S(1)}, f32[1,1,256]{2,1,0:T(1,128)}, u32[]{:S(2)}) copy-start(f32[1,1,256]{2,1,0:T(1,128)} %copy-done.82) | copy-start | bytes 3076
  43.0 6.7 %copy-start.86 = (f32[1,1,256]{2,1,0:T(1,128)S(1)}, f32[1,1,256]{2,1,0:T(1,128)}, u32[]{:S(2)}) copy-start(f32[1,1,256]{2,1,0:T(1,128)} %copy-done.85) | copy-start | bytes 3076
  43.0 6.7 %copy-start.89 = (f32[1,1,256]{2,1,0:T(1,128)S(1)}, f32[1,1,256]{2,1,0:T(1,128)}, u32[]{:S(2)}) copy-start(f32[1,1,256]{2,1,0:T(1,128)} %copy-done.88) | copy-start | bytes 3076
  43.0 6.7 %copy-start.92 = (f32[1,1,256]{2,1,0:T(1,128)S(1)}, f32[1,1,256]{2,1,0:T(1,128)}, u32[]{:S(2)}) copy-start(f32[1,1,256]{2,1,0:T(1,128)} %copy-done.91) | copy-start | bytes 3076
  43.0 6.7 %copy-start.95 = (f32[1,1,256]{2,1,0:T(1,128)S(1)}, f32[1,1,256]{2,1,0:T(1,128)}, u32[]{:S(2)}) copy-start(f32[1,1,256]{2,1,0:T(1,128)} %copy-done.94) | copy-start | bytes 3076
  43.0 6.7 %copy-start.98 = (f32[1,1,256]{2,1,0:T(1,128)S(1)}, f32[1,1,256]{2,1,0:T(1,128)}, u32[]{:S(2)}) copy-start(f32[1,1,256]{2,1,0:T(1,128)} %copy-done.97) | copy-start | bytes 3076
  44.0 8.6 %copy-start.120 = (f32[256]{0:T(256)S(1)}, f32[256]{0:T(256)}, u32[]{:S(2)}) copy-start(f32[256]{0:T(256)} %param.14) | copy-start | bytes 3076
  44.0 15.1 %collective-permute-start.4 = (f32[4,128,256]{2,1,0:T(8,128)}, f32[4,128,256]{2,1,0:T(8,128)}, u32[]{:S(2)}, u32[]{:S(2)}) collective-permute-start(f32[4,128,256]{2,1,0:T(8,128)} %constant_dynamic-slice_fusion.1), channel_id=1, source_target_pairs={{0,1},{1,0},{2,3},{3,2},{4,5},{5,4},{6,7},{7,6},{8,9},{9,8},{10,11... | collective-permute-start | bytes 1572872 | tf_op jit(solution)/shard_map/ppermute | solution.py:69
  45.1 10.8 %collective-permute-start.2 = (bf16[3,256,256]{2,1,0:T(8,128)(2,1)}, bf16[3,256,256]{2,1,0:T(8,128)(2,1)}, u32[]{:S(2)}, u32[]{:S(2)}) collective-permute-start(bf16[3,256,256]{2,1,0:T(8,128)(2,1)} %get-tuple-element.88), channel_id=1, source_target_pairs={{0,1},{1,2},{2,3},{3,4},{4,5},{5,6},{6,7},{7,8},{8,9},{9,10},{10,1... | collective-permute-start | bytes 1179656 | tf_op jit(solution)/shard_map/ppermute | solution.py:98
  48.2 8.7 %collective-permute-start.3 = (bf16[3,256,256]{2,1,0:T(8,128)(2,1)}, bf16[3,256,256]{2,1,0:T(8,128)(2,1)}, u32[]{:S(2)}, u32[]{:S(2)}) collective-permute-start(bf16[3,256,256]{2,1,0:T(8,128)(2,1)} %get-tuple-element.89), channel_id=1, source_target_pairs={{1,0},{2,1},{3,2},{4,3},{5,4},{6,5},{7,6},{8,7},{9,8},{10,9},{11,1... | collective-permute-start | bytes 1179656 | tf_op jit(solution)/shard_map/ppermute | solution.py:99
  60.7 11.3 %collective-permute-start.7 = (bf16[614,256]{1,0:T(8,128)(2,1)S(1)}, bf16[614,256]{1,0:T(8,128)(2,1)S(1)}, u32[]{:S(2)}, u32[]{:S(2)}) collective-permute-start(bf16[614,256]{1,0:T(8,128)(2,1)S(1)} %pad_maximum_fusion), channel_id=1, source_target_pairs={{0,2},{1,3},{2,0},{3,1},{4,6},{5,7},{6,4},{7,5},{8,10},{9,11},{10,... | collective-permute-start | bytes 943112 | tf_op jit(solution)/shard_map/ppermute | solution.py:77
  65.1 10.5 %copy-start.63 = (f32[1,1,256]{2,1,0:T(1,128)S(1)}, f32[1,1,256]{2,1,0:T(1,128)}, u32[]{:S(2)}) copy-start(f32[1,1,256]{2,1,0:T(1,128)} %copy-done.61) | copy-start | bytes 3076
  65.1 10.5 %copy-start.66 = (f32[1,1,256]{2,1,0:T(1,128)S(1)}, f32[1,1,256]{2,1,0:T(1,128)}, u32[]{:S(2)}) copy-start(f32[1,1,256]{2,1,0:T(1,128)} %copy-done.64) | copy-start | bytes 3076
  65.1 10.5 %copy-start.69 = (f32[1,1,256]{2,1,0:T(1,128)S(1)}, f32[1,1,256]{2,1,0:T(1,128)}, u32[]{:S(2)}) copy-start(f32[1,1,256]{2,1,0:T(1,128)} %copy-done.67) | copy-start | bytes 3076
  65.1 10.5 %copy-start.72 = (f32[1,1,256]{2,1,0:T(1,128)S(1)}, f32[1,1,256]{2,1,0:T(1,128)}, u32[]{:S(2)}) copy-start(f32[1,1,256]{2,1,0:T(1,128)} %copy-done.70) | copy-start | bytes 3076
  65.2 10.5 %copy-start.75 = (f32[1,1,256]{2,1,0:T(1,128)S(1)}, f32[1,1,256]{2,1,0:T(1,128)}, u32[]{:S(2)}) copy-start(f32[1,1,256]{2,1,0:T(1,128)} %copy-done.73) | copy-start | bytes 3076
  65.2 10.5 %copy-start.78 = (f32[1,1,256]{2,1,0:T(1,128)S(1)}, f32[1,1,256]{2,1,0:T(1,128)}, u32[]{:S(2)}) copy-start(f32[1,1,256]{2,1,0:T(1,128)} %copy-done.76) | copy-start | bytes 3076
  65.2 10.5 %copy-start.81 = (f32[1,1,256]{2,1,0:T(1,128)S(1)}, f32[1,1,256]{2,1,0:T(1,128)}, u32[]{:S(2)}) copy-start(f32[1,1,256]{2,1,0:T(1,128)} %copy-done.79) | copy-start | bytes 3076
  72.1 11.5 %copy-start.7 = (bf16[4,256,256]{2,1,0:T(8,128)(2,1)S(1)}, bf16[4,256,256]{2,1,0:T(8,128)(2,1)}, u32[]{:S(2)}) copy-start(bf16[4,256,256]{2,1,0:T(8,128)(2,1)} %param.15) | copy-start | bytes 1572868
  72.2 8.4 %collective-permute-start.8 = (bf16[358,256]{1,0:T(8,128)(2,1)S(1)}, bf16[358,256]{1,0:T(8,128)(2,1)S(1)}, u32[]{:S(2)}, u32[]{:S(2)}) collective-permute-start(bf16[358,256]{1,0:T(8,128)(2,1)S(1)} %pad_maximum_fusion.1), channel_id=1, source_target_pairs={{0,4},{1,5},{2,6},{3,7},{4,0},{5,1},{6,2},{7,3},{8,12},{9,13},{10,... | collective-permute-start | bytes 549896 | tf_op jit(solution)/shard_map/ppermute | solution.py:77
  80.7 8.2 %collective-permute-start.9 = (bf16[230,256]{1,0:T(8,128)(2,1)S(1)}, bf16[230,256]{1,0:T(8,128)(2,1)S(1)}, u32[]{:S(2)}, u32[]{:S(2)}) collective-permute-start(bf16[230,256]{1,0:T(8,128)(2,1)S(1)} %pad_maximum_fusion.2), channel_id=1, source_target_pairs={{0,8},{1,9},{2,10},{3,11},{4,12},{5,13},{6,14},{7,15},{8,0},{9,1},... | collective-permute-start | bytes 353288 | tf_op jit(solution)/shard_map/ppermute | solution.py:77
  (84 other events, 379.8 us)

commit v13 on v10

--- a/solution.py
+++ b/solution.py
@@ -43,7 +43,7 @@
     return high, low
 
 
-def halving_reduce(quartered, rows, whole, axis):
+def halving_reduce(quartered, rows, whole, axis, rider):
     count = lax.axis_size(axis)
     steps = count.bit_length() - 1
     if (1 << steps) != count:
@@ -51,6 +51,7 @@
             lax.psum_scatter(quartered, axis, scatter_dimension=1, tiled=True),
             lax.psum_scatter(rows, axis, scatter_dimension=0, tiled=True),
             lax.psum(whole, axis),
+            rider,
         )
     me = lax.axis_index(axis)
     quartered = bit_reversed(quartered, count, steps, 1)
@@ -87,8 +88,11 @@
             whole = mine + theirs
         quartered = keep_q + got_q.astype(jnp.float32)
         rows = keep_r + got_r.astype(jnp.float32)
-        quartered, rows, whole = lax.optimization_barrier((quartered, rows, whole))
-    return quartered, rows, whole
+        if step == 0:
+            quartered, rows, whole, rider = lax.optimization_barrier((quartered, rows, whole, rider))
+        else:
+            quartered, rows, whole = lax.optimization_barrier((quartered, rows, whole))
+    return quartered, rows, whole, rider
 
 
 def halo_rows(block, axis, width):
@@ -197,9 +201,10 @@
     ).astype(jnp.bfloat16)
     kernel_grad = kernel_terms(window, grad_tile.astype(jnp.float32), image_rows, TILE_COLS)
     packed = jnp.concatenate([kernel_grad, gain_grad[None], scale_grad[None]], axis=0)
-    owned_in, grad_w_out, small_grads = halving_reduce(partial_in, partial_out, packed, "row")
+    owned_in, grad_w_out, small_grads, flipped = halving_reduce(
+        partial_in, partial_out, packed, "row", kernel[::-1, ::-1]
+    )
     grad_w_in = owned_in.transpose(1, 0, 2).reshape(-1, hidden)
-    flipped = kernel[::-1, ::-1]
     tile_padded = jnp.pad(
         grad_tile.astype(jnp.float32),
         ((half_width, half_width), (2 * half_width, 2 * half_width), (0, 0)),

time: 86 us -> 100 us (1.16)
  matrix products: 8.89 us -> 14.6 us
  starting transfers between devices: 21.5 us -> 26.9 us
  local copies, waits for them, and re-layouts: 11.5 us -> 15.4 us
  waiting for transfers between devices: 15.5 us -> 12.1 us
  other arithmetic: 25 us -> 27.3 us
    dot_general x4, matrix products: 3.04 us -> 7.55 us  [shards(): lax.dot_general(normed_flat, pre_flat[:, q * channels:(q + 1) * channels]...]
    ppermute x3, waiting for transfers between devices: 13.6 us -> 9.24 us  [halving_reduce(): got = lax.ppermute(sent, axis, pairs)]
    ppermute x3, starting transfers between devices: 7.26 us -> 10.1 us  [halving_reduce(): got = lax.ppermute(sent, axis, pairs)]
    ppermute x3, starting transfers between devices: 6.24 us -> 9.03 us  [halving_reduce(): got_q, got_r, got_whole = lax.ppermute((give_q, give_r, whole), axis, pairs)]
    unnamed x187 -> x165, local copies, waits for them, and re-layouts: 1.81 us -> 3.68 us
    dot_general x1, matrix products: 0.44 us -> 1.65 us  [shards(): lax.dot_general(act_flat, grad_flat, (((0,), (0,)), ((), ())), preferred_...]
    dynamic_update_slice x1, other arithmetic: 0.07 us -> 1.2 us  [shards(): lax.dynamic_update_slice_in_dim(image, out_tile, first_col, axis=1)]
  transfers between devices with their start and end apart: 10 -> 10, of which waited for: 4 -> 3; matrix products, arithmetic and copies ran while one was open for 26% -> 20% of each run, Pallas kernels for 0% -> 0%
where the time goes in v13:
time: 100 us; the launch traced here: 99.2 us
  other arithmetic  27.3 us (27%)
  starting transfers between devices  26.9 us (27%)
  local copies, waits for them, and re-layouts  15.4 us (15%)
  matrix products  14.6 us (15%)
  waiting for transfers between devices  12.1 us (12%)
  between operations  2.87 us (3%)
    ppermute x3, starting transfers between devices, halving_reduce(): got = lax.ppermute(sent, axis, pairs)  10.1 us
    ppermute x3, waiting for transfers between devices, halving_reduce(): got = lax.ppermute(sent, axis, pairs)  9.24 us
    ppermute x3, starting transfers between devices, halving_reduce(): got_q, got_r, got_whole = lax.ppermute((give_q, give_r, whole), axis, pairs)  9.03 us
    dot_general x4, matrix products, shards(): lax.dot_general(normed_flat, pre_flat[:, q * channels:(q + 1) * channels]...  7.55 us
    add x4, other arithmetic, shards(): total + line[col_tap:col_tap + image_cols] * flipped[row_tap, col_tap]  4.14 us
    reduce_sum x1, other arithmetic, shards(): centre = jnp.mean(filtered, axis=-1, keepdims=True)  3.86 us
    unnamed x165, local copies, waits for them, and re-layouts  3.68 us
    add x1, other arithmetic, depthwise(): total + padded[row_tap:row_tap + image_rows, col_tap:col_tap + image_cols...  3.38 us
  transfers between devices with their start and end apart: 10, of which 3 were waited for; matrix products, arithmetic and copies ran while one was open for 20% of the time, Pallas kernels for 0%

profile of v13, /device:TPU:0, one launch (start us, length us, event | category | flops | bytes accessed | tf_op | source)
XLA Modules:
  0.0 99.2 jit_solution(16123617656714300460)
XLA Ops:
  0.7 1.1 %copy.35 = bf16[4,256,256]{2,1,0:T(8,128)(2,1)S(1)} copy(bf16[4,256,256]{2,1,0:T(8,128)(2,1)} %param.8) | data formatting | bytes 1048576
  1.8 2.4 %collective-permute-start = (bf16[3,256,256]{2,1,0:T(8,128)(2,1)S(1)}, bf16[3,256,256]{2,1,0:T(8,128)(2,1)S(1)}, u32[]{:S(2)}, u32[]{:S(2)}) collective-permute-start(bf16[3,256,256]{2,1,0:T(8,128)(2,1)S(1)} %get-tuple-element.93), channel_id=1, source_target_pairs={{0,1},{1,2},{2,3},{3,4},{4,5},{5,6},{6,7},{7,8},{8,9},{9,10},{10,1... | collective-permute-start | bytes 1179656 | tf_op jit(solution)/shard_map/ppermute | solution.py:21
  4.2 1.3 %collective-permute-start.1 = (bf16[3,256,256]{2,1,0:T(8,128)(2,1)S(1)}, bf16[3,256,256]{2,1,0:T(8,128)(2,1)S(1)}, u32[]{:S(2)}, u32[]{:S(2)}) collective-permute-start(bf16[3,256,256]{2,1,0:T(8,128)(2,1)S(1)} %get-tuple-element.92), channel_id=1, source_target_pairs={{1,0},{2,1},{3,2},{4,3},{5,4},{6,5},{7,6},{8,7},{9,8},{10,9},{11,1... | collective-permute-start | bytes 1179656 | tf_op jit(solution)/shard_map/ppermute | solution.py:24
  7.1 2.8 %collective-permute-done.1 = bf16[3,256,256]{2,1,0:T(8,128)(2,1)S(1)} collective-permute-done((bf16[3,256,256]{2,1,0:T(8,128)(2,1)S(1)}, bf16[3,256,256]{2,1,0:T(8,128)(2,1)S(1)}, u32[]{:S(2)}, u32[]{:S(2)}) %collective-permute-start.1) | collective-permute-done | bytes 393248 | tf_op jit(solution)/shard_map/ppermute | solution.py:24
  10.3 3.9 %fusion.216 = (f32[4,128]{1,0:T(4,128)S(1)}, f32[4,128,256]{2,1,0:T(8,128)S(1)}) fusion(f32[256]{0:T(256)S(1)} %bitcast.426, f32[10,134,256]{2,1,0:T(8,128)S(1)} %fusion.21, f32[256]{0:T(256)S(1)} %bitcast.398, f32[256]{0:T(256)S(1)} %bitcast.399, f32[256]{0:T(256)S(1)} %bitcast.400, f32[256]{0:T(256)S(1)} %bitcast.401, f32[256]{0:T(256)S(1)} %bitcast.402, ...), kind=kLoop, calls=%fused_computation.410 | loop fusion | flops 12844544 | bytes 26266624 | tf_op jit(solution)/shard_map/reduce_sum | solution.py:155
  14.7 1.8 %fusion.11 = (bf16[1024,512]{0,1:T(8,128)(2,1)}, f32[512,1024]{1,0:T(8,128)S(1)}) fusion(bf16[512,256]{1,0:T(8,128)(2,1)S(1)} %bitcast.246, bf16[256,1024]{1,0:T(8,128)(2,1)S(1)} %copy-done), kind=kOutput, calls=%fused_computation.112 | convolution fusion | flops 273154048 | bytes 3932160 | tf_op jit(solution)/shard_map/dot_general | solution.py:165
  16.5 1.6 %fusion.122 = (f32[256]{0:T(256)S(1)}, bf16[4,128,256]{2,1,0:T(8,128)(2,1)S(1)}, f32[512,256]{1,0:T(8,128)}) fusion(bf16[4,256,256]{2,1,0:T(8,128)(2,1)S(1)} %copy-done.12, s32[]{:T(128)S(6)} %select_n.62, f32[256]{0:T(256)S(1)} %copy-done.80, bf16[1024,256]{1,0:T(8,128)(2,1)S(1)} %copy-done.21, f32[512,1024]{1,0:T(8,128)S(1)} %get-tuple-element.202), kind=kOutput, calls=%fused_computation.238 | convolution fusion | flops 273809152 | bytes 3672068 | tf_op jit(solution)/shard_map/dot_general | solution.py:167
  18.1 1.4 %fusion.6 = bf16[512,1024]{1,0:T(8,128)(2,1)S(1)} fusion(f32[512,1024]{1,0:T(8,128)S(1)} %get-tuple-element.202, bf16[512,256]{1,0:T(8,128)(2,1)S(1)} %bitcast.244, bf16[1024,256]{1,0:T(8,128)(2,1)S(1)} %copy-done.21), kind=kOutput, calls=%fused_computation.107 | convolution fusion | flops 278396928 | bytes 3932160 | tf_op jit(solution)/shard_map/dot_general | solution.py:168
  20.9 0.8 copy-done.6
  21.7 1.0 fusion.170
  22.7 1.0 %fusion.171 = (f32[256]{0:T(256)S(1)}, f32[256]{0:T(256)S(1)}, f32[256]{0:T(256)S(1)}, f32[256]{0:T(256)S(1)}, f32[256]{0:T(256)S(1)}, /*index=5*/f32[256]{0:T(2...) fusion(bf16[4,128,256]{2,1,0:T(8,128)(2,1)S(1)} %get-tuple-elem, ...), kind=kLoop, calls=%fused_computation.287 | loop fusion | flops 4845056 | bytes 9717760 | tf_op jit(solution)/shard_map/reduce_sum | solution.py:136
  23.7 1.1 %copy.20 = bf16[256,512]{1,0:T(8,128)(2,1)S(1)} copy(bf16[256,512]{0,1:T(8,128)(2,1)} %bitcast.247) | data formatting | bytes 524288 | tf_op jit(solution)/shard_map/dot_general | solution.py:174
  24.8 1.9 %convolution_bitcast_fusion.4 = f32[1,2,2,2,2,16,256]{6,5,4,3,2,1,0:T(8,128)} fusion(bf16[2,2,2,2,16,512]{5,4,3,2,1,0:T(8,128)(2,1)S(1)} %bitcast.233, bf16[512,1024]{1,0:T(8,128)(2,1)} %copy-done.14), kind=kOutput, calls=%fused_computation.126 | convolution fusion | flops 67108864 | bytes 786432 | tf_op jit(solution)/shard_map/dot_general | solution.py:174
  26.7 1.9 %convolution_bitcast_fusion.3 = f32[1,2,2,2,2,16,256]{6,5,4,3,2,1,0:T(8,128)} fusion(bf16[2,2,2,2,16,512]{5,4,3,2,1,0:T(8,128)(2,1)S(1)} %bitcast.234, bf16[512,1024]{1,0:T(8,128)(2,1)} %copy-done.14), kind=kOutput, calls=%fused_computation.125 | convolution fusion | flops 67108864 | bytes 786432 | tf_op jit(solution)/shard_map/dot_general | solution.py:174
  28.6 1.9 %convolution_bitcast_fusion.2 = f32[1,2,2,2,2,16,256]{6,5,4,3,2,1,0:T(8,128)} fusion(bf16[2,2,2,2,16,512]{5,4,3,2,1,0:T(8,128)(2,1)S(1)} %bitcast.235, bf16[512,1024]{1,0:T(8,128)(2,1)} %copy-done.14), kind=kOutput, calls=%fused_computation.124 | convolution fusion | flops 67108864 | bytes 786432 | tf_op jit(solution)/shard_map/dot_general | solution.py:174
  30.4 1.9 %convolution_bitcast_fusion.1 = f32[1,2,2,2,2,16,256]{6,5,4,3,2,1,0:T(8,128)} fusion(bf16[2,2,2,2,16,512]{5,4,3,2,1,0:T(8,128)(2,1)S(1)} %bitcast.236, bf16[512,1024]{1,0:T(8,128)(2,1)} %copy-done.14), kind=kOutput, calls=%fused_computation.123 | convolution fusion | flops 67108864 | bytes 786432 | tf_op jit(solution)/shard_map/dot_general | solution.py:174
  32.3 2.3 %copy.22 = bf16[1024,512]{1,0:T(8,128)(2,1)} copy(bf16[1024,512]{0,1:T(8,128)(2,1)} %get-tuple-element.201) | data formatting | bytes 2097152 | tf_op jit(solution)/shard_map/convert_element_type | solution.py:166
  34.6 1.7 %convolution_bitcast_fusion = f32[2,2,2,2,64,256]{5,4,0,1,2,3:T(8,128)S(1)} fusion(bf16[2,2,2,2,64,512]{5,4,3,2,1,0:T(8,128)(2,1)} %bitcast.242, bf16[512,256,1,1,1,1]{1,0,5,4,3,2:T(8,128)(2,1)S(1)} %bitcast.245), kind=kOutput, calls=%fused_computation.119 | convolution fusion | flops 268435456 | bytes 2359296 | tf_op jit(solution)/shard_map/dot_general | solution.py:183
  36.4 0.9 constant_dynamic-slice_fusion
  37.3 6.0 %collective-permute-start.3 = (f32[512,256]{1,0:T(8,128)}, f32[512,256]{1,0:T(8,128)}, u32[]{:S(2)}, u32[]{:S(2)}) collective-permute-start(f32[512,256]{1,0:T(8,128)} %constant_dynamic-slice_fusion), channel_id=1, source_target_pairs={{0,1},{1,0},{2,3},{3,2},{4,5},{5,4},{6,7},{7,6},{8,9},{9,8},{10,11... | collective-permute-start | bytes 1572872 | tf_op jit(solution)/shard_map/ppermute | solution.py:70
  43.5 1.0 %copy-done.4 = f32[4,2,2,2,2,16,256]{6,5,4,3,2,1,0:T(8,128)} copy-done((f32[4,2,2,2,2,16,256]{6,5,4,3,2,1,0:T(8,128)}, f32[4,2,2,2,2,16,256]{6,5,4,3,2,1,0:T(8,128)S(1)}, u32[]{:S(2)}) %copy-start.4) | copy-done | bytes 1048600
  44.6 0.8 constant_dynamic-slice_fusion.1
  46.0 0.9 fusion.217
  46.9 2.7 %collective-permute-start.5 = (bf16[3,256,256]{2,1,0:T(8,128)(2,1)}, bf16[3,256,256]{2,1,0:T(8,128)(2,1)}, u32[]{:S(2)}, u32[]{:S(2)}) collective-permute-start(bf16[3,256,256]{2,1,0:T(8,128)(2,1)} %get-tuple-element.88), channel_id=1, source_target_pairs={{0,1},{1,2},{2,3},{3,4},{4,5},{5,6},{6,7},{7,8},{8,9},{9,10},{10,1... | collective-permute-start | bytes 1179656 | tf_op jit(solution)/shard_map/ppermute | solution.py:102
  49.6 1.5 %collective-permute-start.6 = (bf16[3,256,256]{2,1,0:T(8,128)(2,1)}, bf16[3,256,256]{2,1,0:T(8,128)(2,1)}, u32[]{:S(2)}, u32[]{:S(2)}) collective-permute-start(bf16[3,256,256]{2,1,0:T(8,128)(2,1)} %get-tuple-element.89), channel_id=1, source_target_pairs={{1,0},{2,1},{3,2},{4,3},{5,4},{6,5},{7,6},{8,7},{9,8},{10,9},{11,1... | collective-permute-start | bytes 1179656 | tf_op jit(solution)/shard_map/ppermute | solution.py:103
  51.0 0.7 fusion.169
  52.0 2.5 %collective-permute-start.4 = (f32[51,256]{1,0:T(8,128)S(1)}, f32[51,256]{1,0:T(8,128)S(1)}, u32[]{:S(2)}, u32[]{:S(2)}) collective-permute-start(f32[51,256]{1,0:T(8,128)S(1)} %concatenate.17), channel_id=1, source_target_pairs={{0,1},{1,0},{2,3},{3,2},{4,5},{5,4},{6,7},{7,6},{8,9},{9,8},{10,11... | collective-permute-start | bytes 156680 | tf_op jit(solution)/shard_map/ppermute | solution.py:70
  54.4 1.2 %fusion.172 = bf16[4,256,256]{2,1,0:T(8,128)(2,1)S(1)} fusion(bf16[4,256,256]{2,1,0:T(8,128)(2,1)S(1)} %copy.35, s32[]{:T(128)S(6)} %select_n.62, f32[4,128,256]{2,1,0:T(8,128)} %bitcast.243, f32[256]{0:T(256)S(1)} %copy-done.80), kind=kLoop, calls=%fused_computation.300 | loop fusion | flops 524288 | bytes 1049604 | tf_op jit(solution)/shard_map/dynamic_update_slice | solution.py:190
  55.8 1.2 %convert_element_type.167 = f32[3,256,256]{2,1,0:T(8,128)S(1)} convert(bf16[3,256,256]{2,1,0:T(8,128)(2,1)} %collective-permute-done.5) | non-fusion elementwise | flops 196608 | bytes 1179648 | tf_op jit(solution)/shard_map/convert_element_type | solution.py:224
  57.0 1.1 %convert_element_type.168 = f32[3,256,256]{2,1,0:T(8,128)S(1)} convert(bf16[3,256,256]{2,1,0:T(8,128)(2,1)} %collective-permute-done.6) | non-fusion elementwise | flops 196608 | bytes 1179648 | tf_op jit(solution)/shard_map/convert_element_type | solution.py:225
  58.1 1.1 %dynamic-slice_add_fusion = f32[512,256]{1,0:T(8,128)S(1)} fusion(f32[512,256]{1,0:T(8,128)} %collective-permute-done.3, f32[1024,256]{1,0:T(8,128)S(1)} %bitcast.239, s32[]{:T(128)S(6)} %select_n.66), kind=kLoop, calls=%fused_computation.289 | loop fusion | flops 131072 | bytes 1572868 | tf_op jit(solution)/shard_map/add | solution.py:90
  59.3 1.3 %dynamic-slice_add_fusion.1 = f32[4,128,256]{2,1,0:T(8,128)S(1)} fusion(f32[4,128,256]{2,1,0:T(8,128)} %collective-permute-done.2, f32[4,256,256]{2,1,0:T(8,128)S(1)} %bitcast.241, s32[]{:T(128)S(6)} %select_n.64), kind=kLoop, calls=%fused_computation.290 | loop fusion | flops 131072 | bytes 1572868 | tf_op jit(solution)/shard_map/add | solution.py:89
  61.4 0.7 pad_maximum_fusion
  62.1 3.5 %collective-permute-start.7 = (bf16[614,256]{1,0:T(8,128)(2,1)}, bf16[614,256]{1,0:T(8,128)(2,1)}, u32[]{:S(2)}, u32[]{:S(2)}) collective-permute-start(bf16[614,256]{1,0:T(8,128)(2,1)} %pad_maximum_fusion), channel_id=1, source_target_pairs={{0,2},{1,3},{2,0},{3,1},{4,6},{5,7},{6,4},{7,5},{8,10},{9,11},{10,... | collective-permute-start | bytes 943112 | tf_op jit(solution)/shard_map/ppermute | solution.py:78
  65.6 0.7 multiply_add_fusion.4
  66.3 3.4 %fusion.115 = f32[4,134,256]{2,1,0:T(8,128)} fusion(f32[4,128,256]{2,1,0:T(8,128)S(1)} %convert_element_type.165, f32[256]{0:T(256)S(1)} %bitcast.257, f32[256]{0:T(256)S(1)} %bitcast.261, f32[256]{0:T(256)S(1)} %bitcast.265, f32[256]{0:T(256)S(1)} %bitcast.269, f32[256]{0:T(256)S(1)} %bitcast.273, f32[256]{0:T(256)S(1)} %bitcast.277, f32[256]{0:T(256)S(1)} %bitcast.281, ...), kind=kLoop, calls=%fused_computation.231 | loop fusion | flops 13309952 | bytes 1123328 | tf_op jit(solution)/shard_map/add | solution.py:124
  69.9 1.4 %fusion.194 = f32[1,256,256]{2,1,0:T(8,128)} fusion(f32[3,256,256]{2,1,0:T(8,128)S(1)} %convert_element_type.167, f32[256]{0:T(256)S(1)} %bitcast.369, f32[256]{0:T(256)S(1)} %bitcast.371, f32[256]{0:T(256)S(1)} %bitcast.373, f32[256]{0:T(256)S(1)} %bitcast.375, f32[256]{0:T(256)S(1)} %bitcast.377, f32[256]{0:T(256)S(1)} %bitcast.379, f32[256]{0:T(256)S(1)} %bitcast.381, ...), kind=kLoop, calls=%fused_computation.324 | loop fusion | flops 2686976 | bytes 1856512 | tf_op jit(solution)/shard_map/add | solution.py:238
  71.5 3.3 %dynamic_update_slice.10 = f32[4,262,256]{2,1,0:T(8,128)S(1)} dynamic-update-slice(f32[4,262,256]{2,1,0:T(8,128)S(1)} %broadcast_in_dim.8, f32[4,134,256]{2,1,0:T(8,128)} %fusion.115, s32[]{:T(128)} %constant.23.clone.1, s32[]{:T(128)S(6)} %select_n.63, s32[]{:T(128)} %constant.23.clone.1) | dynamic-update-slice | bytes 1097732 | tf_op jit(solution)/shard_map/dynamic_update_slice | solution.py:213
  75.1 1.4 %multiply_add_fusion.3 = f32[1,256,256]{2,1,0:T(8,128)S(1)} fusion(f32[3,256,256]{2,1,0:T(8,128)S(1)} %convert_element_type.168, f32[3,256,256]{2,1,0:T(8,128)S(1)} %convert_element_type.167, f32[256]{0:T(256)} %bitcast.313, f32[256]{0:T(256)} %bitcast.316, f32[256]{0:T(256)} %bitcast.319, f32[256]{0:T(256)} %bitcast.322, f32[256]{0:T(256)} %bitcast.325, ...), kind=kLoop, calls=%fused_computation.354 | loop fusion | flops 2686976 | bytes 2642944 | tf_op jit(solution)/shard_map/add | solution.py:238
  76.5 0.9 slice.1375
  77.5 0.8 fusion.207
  78.4 0.9 convert_add_fusion.1
  79.4 3.3 %collective-permute-start.8 = (bf16[358,256]{1,0:T(8,128)(2,1)S(1)}, bf16[358,256]{1,0:T(8,128)(2,1)S(1)}, u32[]{:S(2)}, u32[]{:S(2)}) collective-permute-start(bf16[358,256]{1,0:T(8,128)(2,1)S(1)} %pad_maximum_fusion.1), channel_id=1, source_target_pairs={{0,4},{1,5},{2,6},{3,7},{4,0},{5,1},{6,2},{7,3},{8,12},{9,13},{10,... | collective-permute-start | bytes 549896 | tf_op jit(solution)/shard_map/ppermute | solution.py:78
  82.8 0.7 fusion.176
  83.5 4.2 %collective-permute-done.8 = bf16[358,256]{1,0:T(8,128)(2,1)S(1)} collective-permute-done((bf16[358,256]{1,0:T(8,128)(2,1)S(1)}, bf16[358,256]{1,0:T(8,128)(2,1)S(1)}, u32[]{:S(2)}, u32[]{:S(2)}) %collective-permute-start.8) | collective-permute-done | bytes 183328 | tf_op jit(solution)/shard_map/ppermute | solution.py:78
  87.9 3.3 %collective-permute-start.9 = (bf16[230,256]{1,0:T(8,128)(2,1)S(1)}, bf16[230,256]{1,0:T(8,128)(2,1)S(1)}, u32[]{:S(2)}, u32[]{:S(2)}) collective-permute-start(bf16[230,256]{1,0:T(8,128)(2,1)S(1)} %pad_maximum_fusion.2), channel_id=1, source_target_pairs={{0,8},{1,9},{2,10},{3,11},{4,12},{5,13},{6,14},{7,15},{8,0},{9,1},... | collective-permute-start | bytes 353288 | tf_op jit(solution)/shard_map/ppermute | solution.py:78
  91.2 1.0 %fusion.16 = bf16[4,256,256]{2,1,0:T(8,128)(2,1)} fusion(f32[4,262,256]{2,1,0:T(8,128)S(1)} %dynamic_update_slice.10, f32[1,256,256]{2,1,0:T(8,128)S(1)} %fusion.176, f32[1,256,256]{2,1,0:T(8,128)S(1)} %multiply_add_fusion.3, f32[1,256,256]{2,1,0:T(8,128)S(1)} %multiply_add_fusion.4, f32[1,256,256]{2,1,0:T(8,128)S(1)} %copy-done.15, ...), kind=kLoop, calls=%fused_computation.129 | loop fusion | flops 1835008 | bytes 3145728 | tf_op jit(solution)/shard_map/convert_element_type | solution.py:241
  92.3 5.0 %collective-permute-done.9 = bf16[230,256]{1,0:T(8,128)(2,1)S(1)} collective-permute-done((bf16[230,256]{1,0:T(8,128)(2,1)S(1)}, bf16[230,256]{1,0:T(8,128)(2,1)S(1)}, u32[]{:S(2)}, u32[]{:S(2)}) %collective-permute-start.9) | collective-permute-done | bytes 117792 | tf_op jit(solution)/shard_map/ppermute | solution.py:78
  (218 shorter events, 7.1 us)
Async XLA Ops:
  0.6 14.0 %copy-start = (bf16[256,1024]{1,0:T(8,128)(2,1)S(1)}, bf16[256,1024]{1,0:T(8,128)(2,1)}, u32[]{:S(2)}) copy-start(bf16[256,1024]{1,0:T(8,128)(2,1)} %param.12) | copy-start | bytes 1572868
  1.8 5.2 %collective-permute-start = (bf16[3,256,256]{2,1,0:T(8,128)(2,1)S(1)}, bf16[3,256,256]{2,1,0:T(8,128)(2,1)S(1)}, u32[]{:S(2)}, u32[]{:S(2)}) collective-permute-start(bf16[3,256,256]{2,1,0:T(8,128)(2,1)S(1)} %get-tuple-element.93), channel_id=1, source_target_pairs={{0,1},{1,2},{2,3},{3,4},{4,5},{5,6},{6,7},{7,8},{8,9},{9,10},{10,1... | collective-permute-start | bytes 1179656 | tf_op jit(solution)/shard_map/ppermute | solution.py:21
  4.2 5.7 %collective-permute-start.1 = (bf16[3,256,256]{2,1,0:T(8,128)(2,1)S(1)}, bf16[3,256,256]{2,1,0:T(8,128)(2,1)S(1)}, u32[]{:S(2)}, u32[]{:S(2)}) collective-permute-start(bf16[3,256,256]{2,1,0:T(8,128)(2,1)S(1)} %get-tuple-element.92), channel_id=1, source_target_pairs={{1,0},{2,1},{3,2},{4,3},{5,4},{6,5},{7,6},{8,7},{9,8},{10,9},{11,1... | collective-permute-start | bytes 1179656 | tf_op jit(solution)/shard_map/ppermute | solution.py:24
  37.3 20.8 %collective-permute-start.3 = (f32[512,256]{1,0:T(8,128)}, f32[512,256]{1,0:T(8,128)}, u32[]{:S(2)}, u32[]{:S(2)}) collective-permute-start(f32[512,256]{1,0:T(8,128)} %constant_dynamic-slice_fusion), channel_id=1, source_target_pairs={{0,1},{1,0},{2,3},{3,2},{4,5},{5,4},{6,7},{7,6},{8,9},{9,8},{10,11... | collective-permute-start | bytes 1572872 | tf_op jit(solution)/shard_map/ppermute | solution.py:70
  45.4 13.8 %collective-permute-start.2 = (f32[4,128,256]{2,1,0:T(8,128)}, f32[4,128,256]{2,1,0:T(8,128)}, u32[]{:S(2)}, u32[]{:S(2)}) collective-permute-start(f32[4,128,256]{2,1,0:T(8,128)} %constant_dynamic-slice_fusion.1), channel_id=1, source_target_pairs={{0,1},{1,0},{2,3},{3,2},{4,5},{5,4},{6,7},{7,6},{8,9},{9,8},{10,11... | collective-permute-start | bytes 1572872 | tf_op jit(solution)/shard_map/ppermute | solution.py:70
  46.9 8.8 %collective-permute-start.5 = (bf16[3,256,256]{2,1,0:T(8,128)(2,1)}, bf16[3,256,256]{2,1,0:T(8,128)(2,1)}, u32[]{:S(2)}, u32[]{:S(2)}) collective-permute-start(bf16[3,256,256]{2,1,0:T(8,128)(2,1)} %get-tuple-element.88), channel_id=1, source_target_pairs={{0,1},{1,2},{2,3},{3,4},{4,5},{5,6},{6,7},{7,8},{8,9},{9,10},{10,1... | collective-permute-start | bytes 1179656 | tf_op jit(solution)/shard_map/ppermute | solution.py:102
  49.6 7.4 %collective-permute-start.6 = (bf16[3,256,256]{2,1,0:T(8,128)(2,1)}, bf16[3,256,256]{2,1,0:T(8,128)(2,1)}, u32[]{:S(2)}, u32[]{:S(2)}) collective-permute-start(bf16[3,256,256]{2,1,0:T(8,128)(2,1)} %get-tuple-element.89), channel_id=1, source_target_pairs={{1,0},{2,1},{3,2},{4,3},{5,4},{6,5},{7,6},{8,7},{9,8},{10,9},{11,1... | collective-permute-start | bytes 1179656 | tf_op jit(solution)/shard_map/ppermute | solution.py:103
  52.0 3.8 %collective-permute-start.4 = (f32[51,256]{1,0:T(8,128)S(1)}, f32[51,256]{1,0:T(8,128)S(1)}, u32[]{:S(2)}, u32[]{:S(2)}) collective-permute-start(f32[51,256]{1,0:T(8,128)S(1)} %concatenate.17), channel_id=1, source_target_pairs={{0,1},{1,0},{2,3},{3,2},{4,5},{5,4},{6,7},{7,6},{8,9},{9,8},{10,11... | collective-permute-start | bytes 156680 | tf_op jit(solution)/shard_map/ppermute | solution.py:70
  60.6 9.1 %copy-start.23 = (f32[1,1,256]{2,1,0:T(1,128)}, f32[1,1,256]{2,1,0:T(1,128)S(1)}, u32[]{:S(2)}) copy-start(f32[1,1,256]{2,1,0:T(1,128)S(1)} %get-tuple-element.101) | copy-start | bytes 3076
  60.6 9.1 %copy-start.25 = (f32[1,1,256]{2,1,0:T(1,128)}, f32[1,1,256]{2,1,0:T(1,128)S(1)}, u32[]{:S(2)}) copy-start(f32[1,1,256]{2,1,0:T(1,128)S(1)} %get-tuple-element.102) | copy-start | bytes 3076
  60.6 9.1 %copy-start.27 = (f32[1,1,256]{2,1,0:T(1,128)}, f32[1,1,256]{2,1,0:T(1,128)S(1)}, u32[]{:S(2)}) copy-start(f32[1,1,256]{2,1,0:T(1,128)S(1)} %get-tuple-element.103) | copy-start | bytes 3076
  60.6 9.1 %copy-start.29 = (f32[1,1,256]{2,1,0:T(1,128)}, f32[1,1,256]{2,1,0:T(1,128)S(1)}, u32[]{:S(2)}) copy-start(f32[1,1,256]{2,1,0:T(1,128)S(1)} %get-tuple-element.104) | copy-start | bytes 3076
  60.6 9.1 %copy-start.31 = (f32[1,1,256]{2,1,0:T(1,128)}, f32[1,1,256]{2,1,0:T(1,128)S(1)}, u32[]{:S(2)}) copy-start(f32[1,1,256]{2,1,0:T(1,128)S(1)} %get-tuple-element.105) | copy-start | bytes 3076
  60.6 9.1 %copy-start.33 = (f32[1,1,256]{2,1,0:T(1,128)}, f32[1,1,256]{2,1,0:T(1,128)S(1)}, u32[]{:S(2)}) copy-start(f32[1,1,256]{2,1,0:T(1,128)S(1)} %get-tuple-element.106) | copy-start | bytes 3076
  60.6 9.1 %copy-start.35 = (f32[1,1,256]{2,1,0:T(1,128)}, f32[1,1,256]{2,1,0:T(1,128)S(1)}, u32[]{:S(2)}) copy-start(f32[1,1,256]{2,1,0:T(1,128)S(1)} %get-tuple-element.107) | copy-start | bytes 3076
  60.7 9.1 %copy-start.37 = (f32[1,1,256]{2,1,0:T(1,128)}, f32[1,1,256]{2,1,0:T(1,128)S(1)}, u32[]{:S(2)}) copy-start(f32[1,1,256]{2,1,0:T(1,128)S(1)} %get-tuple-element.100) | copy-start | bytes 3076
  60.7 9.1 %copy-start.51 = (f32[1,1,256]{2,1,0:T(1,128)}, f32[1,1,256]{2,1,0:T(1,128)S(1)}, u32[]{:S(2)}) copy-start(f32[1,1,256]{2,1,0:T(1,128)S(1)} %get-tuple-element.108) | copy-start | bytes 3076
  60.7 9.1 %copy-start.53 = (f32[1,1,256]{2,1,0:T(1,128)}, f32[1,1,256]{2,1,0:T(1,128)S(1)}, u32[]{:S(2)}) copy-start(f32[1,1,256]{2,1,0:T(1,128)S(1)} %get-tuple-element.109) | copy-start | bytes 3076
  60.7 9.1 %copy-start.55 = (f32[1,1,256]{2,1,0:T(1,128)}, f32[1,1,256]{2,1,0:T(1,128)S(1)}, u32[]{:S(2)}) copy-start(f32[1,1,256]{2,1,0:T(1,128)S(1)} %get-tuple-element.110) | copy-start | bytes 3076
  60.7 9.1 %copy-start.57 = (f32[1,1,256]{2,1,0:T(1,128)}, f32[1,1,256]{2,1,0:T(1,128)S(1)}, u32[]{:S(2)}) copy-start(f32[1,1,256]{2,1,0:T(1,128)S(1)} %get-tuple-element.111) | copy-start | bytes 3076
  60.7 9.1 %copy-start.59 = (f32[1,1,256]{2,1,0:T(1,128)}, f32[1,1,256]{2,1,0:T(1,128)S(1)}, u32[]{:S(2)}) copy-start(f32[1,1,256]{2,1,0:T(1,128)S(1)} %get-tuple-element.112) | copy-start | bytes 3076
  60.7 9.1 %copy-start.61 = (f32[1,1,256]{2,1,0:T(1,128)}, f32[1,1,256]{2,1,0:T(1,128)S(1)}, u32[]{:S(2)}) copy-start(f32[1,1,256]{2,1,0:T(1,128)S(1)} %get-tuple-element.113) | copy-start | bytes 3076
  60.7 9.1 %copy-start.63 = (f32[1,1,256]{2,1,0:T(1,128)}, f32[1,1,256]{2,1,0:T(1,128)S(1)}, u32[]{:S(2)}) copy-start(f32[1,1,256]{2,1,0:T(1,128)S(1)} %get-tuple-element.114) | copy-start | bytes 3076
  60.7 9.1 %copy-start.66 = (f32[1,1,256]{2,1,0:T(1,128)}, f32[1,1,256]{2,1,0:T(1,128)S(1)}, u32[]{:S(2)}) copy-start(f32[1,1,256]{2,1,0:T(1,128)S(1)} %get-tuple-element.115) | copy-start | bytes 3076
  60.8 9.1 %copy-start.68 = (f32[1,1,256]{2,1,0:T(1,128)}, f32[1,1,256]{2,1,0:T(1,128)S(1)}, u32[]{:S(2)}) copy-start(f32[1,1,256]{2,1,0:T(1,128)S(1)} %get-tuple-element.116) | copy-start | bytes 3076
  60.8 9.1 %copy-start.70 = (f32[1,1,256]{2,1,0:T(1,128)}, f32[1,1,256]{2,1,0:T(1,128)S(1)}, u32[]{:S(2)}) copy-start(f32[1,1,256]{2,1,0:T(1,128)S(1)} %get-tuple-element.117) | copy-start | bytes 3076
  60.8 9.1 %copy-start.72 = (f32[1,1,256]{2,1,0:T(1,128)}, f32[1,1,256]{2,1,0:T(1,128)S(1)}, u32[]{:S(2)}) copy-start(f32[1,1,256]{2,1,0:T(1,128)S(1)} %get-tuple-element.118) | copy-start | bytes 3076
  60.8 9.0 %copy-start.39 = (f32[1,1,256]{2,1,0:T(1,128)}, f32[1,1,256]{2,1,0:T(1,128)S(1)}, u32[]{:S(2)}) copy-start(f32[1,1,256]{2,1,0:T(1,128)S(1)} %get-tuple-element.119) | copy-start | bytes 3076
  60.8 9.0 %copy-start.74 = (f32[1,1,256]{2,1,0:T(1,128)}, f32[1,1,256]{2,1,0:T(1,128)S(1)}, u32[]{:S(2)}) copy-start(f32[1,1,256]{2,1,0:T(1,128)S(1)} %get-tuple-element.120) | copy-start | bytes 3076
  60.8 9.0 %copy-start.76 = (f32[1,1,256]{2,1,0:T(1,128)}, f32[1,1,256]{2,1,0:T(1,128)S(1)}, u32[]{:S(2)}) copy-start(f32[1,1,256]{2,1,0:T(1,128)S(1)} %get-tuple-element.121) | copy-start | bytes 3076
  60.8 9.0 %copy-start.78 = (f32[1,1,256]{2,1,0:T(1,128)}, f32[1,1,256]{2,1,0:T(1,128)S(1)}, u32[]{:S(2)}) copy-start(f32[1,1,256]{2,1,0:T(1,128)S(1)} %get-tuple-element.122) | copy-start | bytes 3076
  60.9 9.0 %copy-start.41 = (f32[1,1,256]{2,1,0:T(1,128)}, f32[1,1,256]{2,1,0:T(1,128)S(1)}, u32[]{:S(2)}) copy-start(f32[1,1,256]{2,1,0:T(1,128)S(1)} %get-tuple-element.138) | copy-start | bytes 3076
  60.9 9.0 %copy-start.43 = (f32[1,1,256]{2,1,0:T(1,128)}, f32[1,1,256]{2,1,0:T(1,128)S(1)}, u32[]{:S(2)}) copy-start(f32[1,1,256]{2,1,0:T(1,128)S(1)} %get-tuple-element.145) | copy-start | bytes 3076
  60.9 9.0 %copy-start.45 = (f32[1,1,256]{2,1,0:T(1,128)}, f32[1,1,256]{2,1,0:T(1,128)S(1)}, u32[]{:S(2)}) copy-start(f32[1,1,256]{2,1,0:T(1,128)S(1)} %get-tuple-element.146) | copy-start | bytes 3076
  60.9 9.0 %copy-start.47 = (f32[1,1,256]{2,1,0:T(1,128)}, f32[1,1,256]{2,1,0:T(1,128)S(1)}, u32[]{:S(2)}) copy-start(f32[1,1,256]{2,1,0:T(1,128)S(1)} %get-tuple-element.147) | copy-start | bytes 3076
  60.9 9.0 %copy-start.49 = (f32[1,1,256]{2,1,0:T(1,128)}, f32[1,1,256]{2,1,0:T(1,128)S(1)}, u32[]{:S(2)}) copy-start(f32[1,1,256]{2,1,0:T(1,128)S(1)} %get-tuple-element.148) | copy-start | bytes 3076
  62.1 14.4 %collective-permute-start.7 = (bf16[614,256]{1,0:T(8,128)(2,1)}, bf16[614,256]{1,0:T(8,128)(2,1)}, u32[]{:S(2)}, u32[]{:S(2)}) collective-permute-start(bf16[614,256]{1,0:T(8,128)(2,1)} %pad_maximum_fusion), channel_id=1, source_target_pairs={{0,2},{1,3},{2,0},{3,1},{4,6},{5,7},{6,4},{7,5},{8,10},{9,11},{10,... | collective-permute-start | bytes 943112 | tf_op jit(solution)/shard_map/ppermute | solution.py:78
  74.9 7.8 %copy-start.52 = (f32[1,1,256]{2,1,0:T(1,128)S(1)}, f32[1,1,256]{2,1,0:T(1,128)}, u32[]{:S(2)}) copy-start(f32[1,1,256]{2,1,0:T(1,128)} %copy-done.51) | copy-start | bytes 3076
  75.0 7.8 %copy-start.54 = (f32[1,1,256]{2,1,0:T(1,128)S(1)}, f32[1,1,256]{2,1,0:T(1,128)}, u32[]{:S(2)}) copy-start(f32[1,1,256]{2,1,0:T(1,128)} %copy-done.53) | copy-start | bytes 3076
  75.0 7.8 %copy-start.56 = (f32[1,1,256]{2,1,0:T(1,128)S(1)}, f32[1,1,256]{2,1,0:T(1,128)}, u32[]{:S(2)}) copy-start(f32[1,1,256]{2,1,0:T(1,128)} %copy-done.55) | copy-start | bytes 3076
  75.0 7.8 %copy-start.58 = (f32[1,1,256]{2,1,0:T(1,128)S(1)}, f32[1,1,256]{2,1,0:T(1,128)}, u32[]{:S(2)}) copy-start(f32[1,1,256]{2,1,0:T(1,128)} %copy-done.57) | copy-start | bytes 3076
  75.0 7.8 %copy-start.60 = (f32[1,1,256]{2,1,0:T(1,128)S(1)}, f32[1,1,256]{2,1,0:T(1,128)}, u32[]{:S(2)}) copy-start(f32[1,1,256]{2,1,0:T(1,128)} %copy-done.59) | copy-start | bytes 3076
  75.0 7.8 %copy-start.62 = (f32[1,1,256]{2,1,0:T(1,128)S(1)}, f32[1,1,256]{2,1,0:T(1,128)}, u32[]{:S(2)}) copy-start(f32[1,1,256]{2,1,0:T(1,128)} %copy-done.61) | copy-start | bytes 3076
  75.0 7.8 %copy-start.64 = (f32[1,1,256]{2,1,0:T(1,128)S(1)}, f32[1,1,256]{2,1,0:T(1,128)}, u32[]{:S(2)}) copy-start(f32[1,1,256]{2,1,0:T(1,128)} %copy-done.63) | copy-start | bytes 3076
  79.3 11.9 %copy-start.13 = (bf16[4,256,256]{2,1,0:T(8,128)(2,1)S(1)}, bf16[4,256,256]{2,1,0:T(8,128)(2,1)}, u32[]{:S(2)}) copy-start(bf16[4,256,256]{2,1,0:T(8,128)(2,1)} %param.15) | copy-start | bytes 1572868
  79.3 11.9 %copy-start.15 = (f32[1,256,256]{2,1,0:T(8,128)S(1)}, f32[1,256,256]{2,1,0:T(8,128)}, u32[]{:S(2)}) copy-start(f32[1,256,256]{2,1,0:T(8,128)} %fusion.194) | copy-start | bytes 786436
  79.4 8.3 %collective-permute-start.8 = (bf16[358,256]{1,0:T(8,128)(2,1)S(1)}, bf16[358,256]{1,0:T(8,128)(2,1)S(1)}, u32[]{:S(2)}, u32[]{:S(2)}) collective-permute-start(bf16[358,256]{1,0:T(8,128)(2,1)S(1)} %pad_maximum_fusion.1), channel_id=1, source_target_pairs={{0,4},{1,5},{2,6},{3,7},{4,0},{5,1},{6,2},{7,3},{8,12},{9,13},{10,... | collective-permute-start | bytes 549896 | tf_op jit(solution)/shard_map/ppermute | solution.py:78
  87.9 9.4 %collective-permute-start.9 = (bf16[230,256]{1,0:T(8,128)(2,1)S(1)}, bf16[230,256]{1,0:T(8,128)(2,1)S(1)}, u32[]{:S(2)}, u32[]{:S(2)}) collective-permute-start(bf16[230,256]{1,0:T(8,128)(2,1)S(1)} %pad_maximum_fusion.2), channel_id=1, source_target_pairs={{0,8},{1,9},{2,10},{3,11},{4,12},{5,13},{6,14},{7,15},{8,0},{9,1},... | collective-permute-start | bytes 353288 | tf_op jit(solution)/shard_map/ppermute | solution.py:78
  (44 other events, 186.4 us)

commit v14 on v10

--- a/solution.py
+++ b/solution.py
@@ -205,19 +205,20 @@
         ((half_width, half_width), (2 * half_width, 2 * half_width), (0, 0)),
     )
     own = depthwise(tile_padded, flipped, image_rows, span)
-    own_full = lax.dynamic_update_slice_in_dim(
-        jnp.zeros((image_rows, image_cols + 2 * half_width, channels), jnp.float32),
-        own,
-        first_col,
-        axis=1,
-    )[:, half_width : half_width + image_cols]
+    tile_index = first_col // TILE_COLS
+    own_full = jnp.zeros((image_rows, image_cols, channels), jnp.float32)
+    for tile in range(image_cols // TILE_COLS):
+        left = tile * TILE_COLS - half_width
+        lo, hi = max(left, 0), min(left + span, image_cols)
+        placed = jnp.pad(own[:, lo - left : hi - left], ((0, 0), (lo, image_cols - hi), (0, 0)))
+        own_full = jnp.where(tile_index == tile, placed, own_full)
     grad_conv = lax.dynamic_update_slice_in_dim(
         jnp.zeros_like(image), grad_tile, first_col, axis=1
     )
     low, high = halo_rows(grad_conv, "row", half_width)
     edge = ((0, 0), (half_width, half_width), (0, 0))
-    low = jnp.pad(low.astype(jnp.float32), edge)
-    high = jnp.pad(high.astype(jnp.float32), edge)
+    low = jnp.pad(low, edge)
+    high = jnp.pad(high, edge)
     halo_out = []
     for out_row in range(image_rows):
         total = jnp.zeros((image_cols, channels), jnp.float32)

time: 86 us -> 96.3 us (1.12)
  matrix products: 8.89 us -> 13.7 us
  local copies, waits for them, and re-layouts: 11.5 us -> 14.7 us
  starting transfers between devices: 21.5 us -> 23.5 us
    ppermute x1, starting transfers between devices: 3 us -> 8.72 us  [halo_rows(): lax.ppermute(lax.slice_in_dim(block, block.shape[0] - width, None, axis=0...]
    concatenate x1, local copies, waits for them, and re-layouts: 0.18 us -> 5.11 us  [shards(): jnp.concatenate([kernel_grad, gain_grad[None], scale_grad[None]], axis=0)]
    ppermute x3, starting transfers between devices: 6.24 us -> 2.27 us  [halving_reduce(): got_q, got_r, got_whole = lax.ppermute((give_q, give_r, whole), axis, pairs)]
    dynamic_update_slice x1 -> x0, local copies, waits for them, and re-layouts: 3.29 us -> none  [shards(): lax.dynamic_update_slice_in_dim(jnp.zeros((image_rows, image_cols + 2 * h...]
    convert_element_type x2 -> x1, other arithmetic: 2.11 us -> 0.06 us  [shards(): grad_tile.astype(jnp.float32)]
    reduce_sum x3, other arithmetic: 3.28 us -> 5.11 us  [kernel_terms(): jnp.sum(padded[row_tap:row_tap + image_rows, col_tap:col_tap + image_cols...]
    dot_general x4, matrix products: 3.04 us -> 4.77 us  [shards(): lax.dot_general(normed_flat, pre_flat[:, q * channels:(q + 1) * channels]...]
    add x1, other arithmetic: 4.17 us -> 2.69 us  [depthwise(): total + padded[row_tap:row_tap + image_rows, col_tap:col_tap + image_cols...]
  transfers between devices with their start and end apart: 10 -> 10, of which waited for: 4 -> 4; matrix products, arithmetic and copies ran while one was open for 26% -> 23% of each run, Pallas kernels for 0% -> 0%
where the time goes in v14:
time: 96.3 us; the launch traced here: 95.7 us
  other arithmetic  24.4 us (25%)
  starting transfers between devices  23.5 us (24%)
  waiting for transfers between devices  16 us (17%)
  local copies, waits for them, and re-layouts  14.7 us (15%)
  matrix products  13.7 us (14%)
  between operations  3.4 us (4%)
    ppermute x3, waiting for transfers between devices, halving_reduce(): got = lax.ppermute(sent, axis, pairs)  13.4 us
    ppermute x1, starting transfers between devices, halo_rows(): lax.ppermute(lax.slice_in_dim(block, block.shape[0] - width, None, axis=0...  8.72 us
    ppermute x3, starting transfers between devices, halving_reduce(): got = lax.ppermute(sent, axis, pairs)  7.58 us
    concatenate x1, local copies, waits for them, and re-layouts, shards(): jnp.concatenate([kernel_grad, gain_grad[None], scale_grad[None]], axis=0)  5.11 us
    reduce_sum x3, other arithmetic, kernel_terms(): jnp.sum(padded[row_tap:row_tap + image_rows, col_tap:col_tap + image_cols...  5.11 us
    dot_general x4, matrix products, shards(): lax.dot_general(normed_flat, pre_flat[:, q * channels:(q + 1) * channels]...  4.77 us
    reduce_sum x1, other arithmetic, shards(): centre = jnp.mean(filtered, axis=-1, keepdims=True)  3.86 us
    add x4, other arithmetic, shards(): total + line[col_tap:col_tap + image_cols] * flipped[row_tap, col_tap]  3.54 us
  transfers between devices with their start and end apart: 10, of which 4 were waited for; matrix products, arithmetic and copies ran while one was open for 23% of the time, Pallas kernels for 0%

profile of v14, /device:TPU:0, one launch (start us, length us, event | category | flops | bytes accessed | tf_op | source)
XLA Modules:
  0.0 95.7 jit_solution(329175972623265273)
XLA Ops:
  0.7 1.1 %copy.34 = bf16[4,256,256]{2,1,0:T(8,128)(2,1)S(1)} copy(bf16[4,256,256]{2,1,0:T(8,128)(2,1)} %param.8) | data formatting | bytes 1048576
  1.8 2.4 %collective-permute-start = (bf16[3,256,256]{2,1,0:T(8,128)(2,1)S(1)}, bf16[3,256,256]{2,1,0:T(8,128)(2,1)S(1)}, u32[]{:S(2)}, u32[]{:S(2)}) collective-permute-start(bf16[3,256,256]{2,1,0:T(8,128)(2,1)S(1)} %get-tuple-element.92), channel_id=1, source_target_pairs={{0,1},{1,2},{2,3},{3,4},{4,5},{5,6},{6,7},{7,8},{8,9},{9,10},{10,1... | collective-permute-start | bytes 1179656 | tf_op jit(solution)/shard_map/ppermute | solution.py:21
  4.2 1.3 %collective-permute-start.1 = (bf16[3,256,256]{2,1,0:T(8,128)(2,1)S(1)}, bf16[3,256,256]{2,1,0:T(8,128)(2,1)S(1)}, u32[]{:S(2)}, u32[]{:S(2)}) collective-permute-start(bf16[3,256,256]{2,1,0:T(8,128)(2,1)S(1)} %get-tuple-element.91), channel_id=1, source_target_pairs={{1,0},{2,1},{3,2},{4,3},{5,4},{6,5},{7,6},{8,7},{9,8},{10,9},{11,1... | collective-permute-start | bytes 1179656 | tf_op jit(solution)/shard_map/ppermute | solution.py:24
  5.5 0.7 bitcast_reduce_fusion
  7.3 2.6 %collective-permute-done.1 = bf16[3,256,256]{2,1,0:T(8,128)(2,1)S(1)} collective-permute-done((bf16[3,256,256]{2,1,0:T(8,128)(2,1)S(1)}, bf16[3,256,256]{2,1,0:T(8,128)(2,1)S(1)}, u32[]{:S(2)}, u32[]{:S(2)}) %collective-permute-start.1) | collective-permute-done | bytes 393248 | tf_op jit(solution)/shard_map/ppermute | solution.py:24
  10.3 3.9 %fusion.257 = (f32[4,128]{1,0:T(4,128)S(1)}, f32[4,128,256]{2,1,0:T(8,128)S(1)}) fusion(f32[256]{0:T(256)S(1)} %bitcast.237, f32[10,134,256]{2,1,0:T(8,128)S(1)} %fusion.21, f32[256]{0:T(256)S(1)} %bitcast.242, f32[256]{0:T(256)S(1)} %bitcast.207, f32[256]{0:T(256)S(1)} %bitcast.212, f32[256]{0:T(256)S(1)} %bitcast.217, f32[256]{0:T(256)S(1)} %bitcast.222, ...), kind=kLoop, calls=%fused_computation.499 | loop fusion | flops 12844544 | bytes 26266624 | tf_op jit(solution)/shard_map/reduce_sum | solution.py:151
  15.0 1.8 %fusion.11 = (bf16[1024,512]{0,1:T(8,128)(2,1)}, f32[512,1024]{1,0:T(8,128)S(1)}) fusion(bf16[512,256]{1,0:T(8,128)(2,1)S(1)} %bitcast.197, bf16[256,1024]{1,0:T(8,128)(2,1)S(1)} %copy-done), kind=kOutput, calls=%fused_computation.112 | convolution fusion | flops 273154048 | bytes 3932160 | tf_op jit(solution)/shard_map/dot_general | solution.py:161
  16.8 2.2 %fusion.122 = (f32[256]{0:T(256)}, bf16[4,128,256]{2,1,0:T(8,128)(2,1)S(1)}, f32[512,256]{1,0:T(8,128)}) fusion(bf16[4,256,256]{2,1,0:T(8,128)(2,1)S(1)} %copy-done.6, s32[]{:T(128)S(6)} %select_n.80, f32[256]{0:T(256)S(1)} %copy-done.112, bf16[1024,256]{1,0:T(8,128)(2,1)S(1)} %copy-done.10, f32[512,1024]{1,0:T(8,128)S(1)} %get-tuple-element.154), kind=kOutput, calls=%fused_computation.238 | convolution fusion | flops 273809152 | bytes 3672068 | tf_op jit(solution)/shard_map/dot_general | solution.py:163
  19.0 1.4 %fusion.6 = bf16[512,1024]{1,0:T(8,128)(2,1)S(1)} fusion(f32[512,1024]{1,0:T(8,128)S(1)} %get-tuple-element.154, bf16[512,256]{1,0:T(8,128)(2,1)S(1)} %bitcast.195, bf16[1024,256]{1,0:T(8,128)(2,1)S(1)} %copy-done.10), kind=kOutput, calls=%fused_computation.107 | convolution fusion | flops 278396928 | bytes 3932160 | tf_op jit(solution)/shard_map/dot_general | solution.py:164
  20.5 1.9 %multiply_reduce_fusion.2 = (f32[512]{0:T(512)}, f32[512,256]{1,0:T(8,128)}) fusion(f32[256]{0:T(256)S(1)} %copy-done.96, bf16[512,1024]{1,0:T(8,128)(2,1)S(1)} %fusion.6, bf16[256,1024]{1,0:T(8,128)(2,1)S(1)} %copy-done), kind=kOutput, calls=%fused_computation.293 | convolution fusion | flops 268697088 | bytes 2100224 | tf_op jit(solution)/shard_map/dot_general | solution.py:166
  22.5 1.2 %convolution_bitcast_fusion.1 = f32[1,2,2,2,2,16,256]{6,5,4,3,2,1,0:T(8,128)S(1)} fusion(bf16[2,2,2,2,16,512]{5,4,3,2,1,0:T(8,128)(2,1)S(1)} %bitcast.184, bf16[512,1024]{1,0:T(8,128)(2,1)} %copy-done.8), kind=kOutput, calls=%fused_computation.123 | convolution fusion | flops 67108864 | bytes 786432 | tf_op jit(solution)/shard_map/dot_general | solution.py:170
  23.8 1.2 %convolution_bitcast_fusion.2 = f32[1,2,2,2,2,16,256]{6,5,4,3,2,1,0:T(8,128)S(1)} fusion(bf16[2,2,2,2,16,512]{5,4,3,2,1,0:T(8,128)(2,1)S(1)} %bitcast.185, bf16[512,1024]{1,0:T(8,128)(2,1)} %copy-done.8), kind=kOutput, calls=%fused_computation.124 | convolution fusion | flops 67108864 | bytes 786432 | tf_op jit(solution)/shard_map/dot_general | solution.py:170
  24.9 1.2 %convolution_bitcast_fusion.3 = f32[1,2,2,2,2,16,256]{6,5,4,3,2,1,0:T(8,128)S(1)} fusion(bf16[2,2,2,2,16,512]{5,4,3,2,1,0:T(8,128)(2,1)S(1)} %bitcast.186, bf16[512,1024]{1,0:T(8,128)(2,1)} %copy-done.8), kind=kOutput, calls=%fused_computation.125 | convolution fusion | flops 67108864 | bytes 786432 | tf_op jit(solution)/shard_map/dot_general | solution.py:170
  26.1 1.2 %convolution_bitcast_fusion.4 = f32[1,2,2,2,2,16,256]{6,5,4,3,2,1,0:T(8,128)S(1)} fusion(bf16[2,2,2,2,16,512]{5,4,3,2,1,0:T(8,128)(2,1)S(1)} %bitcast.187, bf16[512,1024]{1,0:T(8,128)(2,1)} %copy-done.8), kind=kOutput, calls=%fused_computation.126 | convolution fusion | flops 67108864 | bytes 786432 | tf_op jit(solution)/shard_map/dot_general | solution.py:170
  27.3 1.6 %multiply_reduce_fusion = (f32[256]{0:T(256)}, f32[4,128]{1,0:T(4,128)S(1)}) fusion(f32[4,128,256]{2,1,0:T(8,128)S(1)} %get-tuple-element.84, f32[4,128]{1,0:T(4,128)S(1)} %add_rsqrt_fusion, f32[4,128]{1,0:T(4,128)S(1)} %broadcast_multiply_fusion.1, f32[512,256]{1,0:T(8,128)S(1)} %copy-done.2, f32[4,128,256]{2,1,0:T(8,128)S(1)} %bitcast.188, f32[256]{0:T(256)} %param.11), kind=kLoop, calls=%fused_computation.288 | loop fusion | flops 916736 | bytes 1581056 | tf_op jit(solution)/shard_map/reduce_sum | solution.py:188
  28.9 1.9 %fusion.169 = (f32[256]{0:T(256)}, f32[256]{0:T(256)}, f32[256]{0:T(256)}, f32[256]{0:T(256)}, f32[256]{0:T(256)}, /*index=5*/f32[256]{0:T(256)}, f32[256]{0:T(2...) fusion(f32[10,134,256]{2,1,0:T(8,128)S(1)} %fusion.21, ...), kind=kLoop, calls=%fused_computation.285 | loop fusion | flops 4584192 | bytes 8148992 | tf_op jit(solution)/shard_map/reduce_sum | solution.py:132
  30.8 1.6 %fusion.171 = (f32[256]{0:T(256)}, f32[256]{0:T(256)}, f32[256]{0:T(256)}, f32[256]{0:T(256)}, f32[256]{0:T(256)}, /*index=5*/f32[256]{0:T(256)}, f32[256]{0:T(2...) fusion(bf16[4,128,256]{2,1,0:T(8,128)(2,1)S(1)} %get-tuple-elem, ...), kind=kLoop, calls=%fused_computation.287 | loop fusion | flops 4845056 | bytes 9717760 | tf_op jit(solution)/shard_map/reduce_sum | solution.py:132
  32.4 1.6 %fusion.170 = (f32[256]{0:T(256)}, f32[256]{0:T(256)}, f32[256]{0:T(256)}, f32[256]{0:T(256)}, f32[256]{0:T(256)}, /*index=5*/f32[256]{0:T(256)}, f32[256]{0:T(2...) fusion(bf16[4,128,256]{2,1,0:T(8,128)(2,1)S(1)} %get-tuple-elem, ...), kind=kLoop, calls=%fused_computation.286 | loop fusion | flops 4845056 | bytes 9717760 | tf_op jit(solution)/shard_map/reduce_sum | solution.py:132
  34.4 0.9 fusion.259
  35.4 1.3 %collective-permute-start.3 = (bf16[3,256,256]{2,1,0:T(8,128)(2,1)}, bf16[3,256,256]{2,1,0:T(8,128)(2,1)S(1)}, u32[]{:S(2)}, u32[]{:S(2)}) collective-permute-start(bf16[3,256,256]{2,1,0:T(8,128)(2,1)} %get-tuple-element.90), channel_id=1, source_target_pairs={{1,0},{2,1},{3,2},{4,3},{5,4},{6,5},{7,6},{8,7},{9,8},{10,9},{11,1... | collective-permute-start | bytes 1179656 | tf_op jit(solution)/shard_map/ppermute | solution.py:99
  36.7 8.7 %collective-permute-start.2 = (bf16[3,256,256]{2,1,0:T(8,128)(2,1)}, bf16[3,256,256]{2,1,0:T(8,128)(2,1)S(1)}, u32[]{:S(2)}, u32[]{:S(2)}) collective-permute-start(bf16[3,256,256]{2,1,0:T(8,128)(2,1)} %get-tuple-element.89), channel_id=1, source_target_pairs={{0,1},{1,2},{2,3},{3,4},{4,5},{5,6},{6,7},{7,8},{8,9},{9,10},{10,1... | collective-permute-start | bytes 1179656 | tf_op jit(solution)/shard_map/ppermute | solution.py:98
  45.8 2.7 %fusion.115 = f32[4,134,256]{2,1,0:T(8,128)S(1)} fusion(f32[4,128,256]{2,1,0:T(8,128)S(1)} %get-tuple-element.93, f32[256]{0:T(256)S(1)} %bitcast.233, f32[256]{0:T(256)S(1)} %bitcast.273, f32[256]{0:T(256)S(1)} %bitcast.248, f32[256]{0:T(256)S(1)} %bitcast.268, f32[256]{0:T(256)S(1)} %bitcast.263, f32[256]{0:T(256)S(1)} %bitcast.258, f32[256]{0:T(256)S(1)} %bitcast.253, ...), kind=kLoop, calls=%fused_computation.231 | loop fusion | flops 13309952 | bytes 1123328 | tf_op jit(solution)/shard_map/add | solution.py:120
  48.4 0.9 fusion.258
  49.5 0.8 constant_dynamic-slice_fusion.1
  50.4 1.7 %collective-permute-start.4 = (f32[4,128,256]{2,1,0:T(8,128)}, f32[4,128,256]{2,1,0:T(8,128)}, u32[]{:S(2)}, u32[]{:S(2)}) collective-permute-start(f32[4,128,256]{2,1,0:T(8,128)} %constant_dynamic-slice_fusion.1), channel_id=1, source_target_pairs={{0,1},{1,0},{2,3},{3,2},{4,5},{5,4},{6,7},{7,6},{8,9},{9,8},{10,11... | collective-permute-start | bytes 1572872 | tf_op jit(solution)/shard_map/ppermute | solution.py:69
  52.1 2.3 %copy.22 = bf16[1024,512]{1,0:T(8,128)(2,1)} copy(bf16[1024,512]{0,1:T(8,128)(2,1)} %get-tuple-element.153) | data formatting | bytes 2097152 | tf_op jit(solution)/shard_map/convert_element_type | solution.py:162
  54.4 1.7 %convolution_bitcast_fusion = f32[2,2,2,2,64,256]{5,4,0,1,2,3:T(8,128)S(1)} fusion(bf16[2,2,2,2,64,512]{5,4,3,2,1,0:T(8,128)(2,1)} %bitcast.193, bf16[512,256,1,1,1,1]{1,0,5,4,3,2:T(8,128)(2,1)} %bitcast.196), kind=kOutput, calls=%fused_computation.119 | convolution fusion | flops 268435456 | bytes 2359296 | tf_op jit(solution)/shard_map/dot_general | solution.py:179
  56.2 1.0 %copy-done.3 = f32[2,2,2,2,64,256]{5,4,3,2,1,0:T(8,128)} copy-done((f32[2,2,2,2,64,256]{5,4,3,2,1,0:T(8,128)}, f32[2,2,2,2,64,256]{5,4,3,2,1,0:T(8,128)S(1)}, u32[]{:S(2)}) %copy-start.3) | copy-done | bytes 1048600
  57.2 0.8 constant_dynamic-slice_fusion
  58.0 5.1 %concatenate.17 = f32[51,256]{1,0:T(8,128)S(1)} concatenate(f32[1,256]{1,0:T(1,128)} %bitcast.405, f32[1,256]{1,0:T(1,128)} %bitcast.406, f32[1,256]{1,0:T(1,128)} %bitcast.407, f32[1,256]{1,0:T(1,128)} %bitcast.408, f32[1,256]{1,0:T(1,128)} %bitcast.409, f32[1,256]{1,0:T(1,128)} %bitcast.410, f32[1,256]{1,0:T(1,128)} %bitcast.411, f32[1,256]{1,0:T(1,128)} %bitcast.412, ...), dimensions={0} | concatenate | bytes 104448 | tf_op jit(solution)/shard_map/concatenate | solution.py:199
  63.1 0.6 collective-permute-start.6
  63.7 1.2 %fusion.246 = bf16[4,256,256]{2,1,0:T(8,128)(2,1)S(1)} fusion(bf16[4,256,256]{2,1,0:T(8,128)(2,1)S(1)} %copy.34, s32[]{:T(128)S(6)} %select_n.80, f32[4,128,256]{2,1,0:T(8,128)} %bitcast.194, f32[256]{0:T(256)} %param.14), kind=kLoop, calls=%fused_computation.444 | loop fusion | flops 524288 | bytes 1049604 | tf_op jit(solution)/shard_map/dynamic_update_slice | solution.py:186
  65.0 1.5 %fusion.212 = f32[1,256,256]{2,1,0:T(8,128)S(1)} fusion(f32[256]{0:T(256)} %bitcast.318, f32[256]{0:T(256)} %bitcast.314, f32[256]{0:T(256)} %bitcast.310, f32[256]{0:T(256)} %bitcast.306, f32[256]{0:T(256)} %bitcast.330, f32[256]{0:T(256)} %bitcast.326, f32[256]{0:T(256)} %bitcast.322, f32[256]{0:T(256)S(1)} %bitcast.234, f32[256]{0:T(256)S(1)} %bitcast.274, ...), kind=kLoop, calls=%fused_computation.410 | loop fusion | flops 4063232 | bytes 1463296 | tf_op jit(solution)/shard_map/add | solution.py:234
  66.6 1.1 %dynamic-slice_add_fusion.1 = f32[4,128,256]{2,1,0:T(8,128)S(1)} fusion(f32[4,128,256]{2,1,0:T(8,128)} %collective-permute-done.4, f32[4,256,256]{2,1,0:T(8,128)S(1)} %bitcast.190, s32[]{:T(128)S(6)} %select_n.87), kind=kLoop, calls=%fused_computation.290 | loop fusion | flops 131072 | bytes 1572868 | tf_op jit(solution)/shard_map/add | solution.py:88
  67.8 1.1 %dynamic-slice_add_fusion = f32[512,256]{1,0:T(8,128)S(1)} fusion(f32[512,256]{1,0:T(8,128)} %collective-permute-done.5, f32[1024,256]{1,0:T(8,128)S(1)} %bitcast.192, s32[]{:T(128)S(6)} %select_n.89), kind=kLoop, calls=%fused_computation.289 | loop fusion | flops 131072 | bytes 1572868 | tf_op jit(solution)/shard_map/add | solution.py:89
  69.0 3.4 %collective-permute-start.7 = (bf16[614,256]{1,0:T(8,128)(2,1)S(1)}, bf16[614,256]{1,0:T(8,128)(2,1)S(1)}, u32[]{:S(2)}, u32[]{:S(2)}) collective-permute-start(bf16[614,256]{1,0:T(8,128)(2,1)S(1)} %pad_maximum_fusion), channel_id=1, source_target_pairs={{0,2},{1,3},{2,0},{3,1},{4,6},{5,7},{6,4},{7,5},{8,10},{9,11},{10,... | collective-permute-start | bytes 943112 | tf_op jit(solution)/shard_map/ppermute | solution.py:77
  72.6 0.7 fusion.226
  73.4 0.7 fusion.205
  74.1 6.0 %collective-permute-done.7 = bf16[614,256]{1,0:T(8,128)(2,1)S(1)} collective-permute-done((bf16[614,256]{1,0:T(8,128)(2,1)S(1)}, bf16[614,256]{1,0:T(8,128)(2,1)S(1)}, u32[]{:S(2)}, u32[]{:S(2)}) %collective-permute-start.7) | collective-permute-done | bytes 314400 | tf_op jit(solution)/shard_map/ppermute | solution.py:77
  80.3 1.6 %collective-permute-start.8 = (bf16[358,256]{1,0:T(8,128)(2,1)S(1)}, bf16[358,256]{1,0:T(8,128)(2,1)S(1)}, u32[]{:S(2)}, u32[]{:S(2)}) collective-permute-start(bf16[358,256]{1,0:T(8,128)(2,1)S(1)} %pad_maximum_fusion.1), channel_id=1, source_target_pairs={{0,4},{1,5},{2,6},{3,7},{4,0},{5,1},{6,2},{7,3},{8,12},{9,13},{10,... | collective-permute-start | bytes 549896 | tf_op jit(solution)/shard_map/ppermute | solution.py:77
  82.0 0.7 fusion.185
  82.7 3.7 %collective-permute-done.8 = bf16[358,256]{1,0:T(8,128)(2,1)S(1)} collective-permute-done((bf16[358,256]{1,0:T(8,128)(2,1)S(1)}, bf16[358,256]{1,0:T(8,128)(2,1)S(1)}, u32[]{:S(2)}, u32[]{:S(2)}) %collective-permute-start.8) | collective-permute-done | bytes 183328 | tf_op jit(solution)/shard_map/ppermute | solution.py:77
  86.6 2.5 %collective-permute-start.9 = (bf16[230,256]{1,0:T(8,128)(2,1)S(1)}, bf16[230,256]{1,0:T(8,128)(2,1)S(1)}, u32[]{:S(2)}, u32[]{:S(2)}) collective-permute-start(bf16[230,256]{1,0:T(8,128)(2,1)S(1)} %pad_maximum_fusion.2), channel_id=1, source_target_pairs={{0,8},{1,9},{2,10},{3,11},{4,12},{5,13},{6,14},{7,15},{8,0},{9,1},... | collective-permute-start | bytes 353288 | tf_op jit(solution)/shard_map/ppermute | solution.py:77
  89.1 1.0 %fusion.16 = bf16[4,256,256]{2,1,0:T(8,128)(2,1)} fusion(f32[1,256,256]{2,1,0:T(8,128)S(1)} %fusion.226, f32[1,256,256]{2,1,0:T(8,128)S(1)} %fusion.212, f32[1,256,256]{2,1,0:T(8,128)S(1)} %fusion.205, f32[1,256,256]{2,1,0:T(8,128)S(1)} %fusion.185, f32[4,131,256]{2,1,0:T(8,128)S(1)} %copy-done.5, f32[4,131,256]{2,1,0:T(8,128)S(1)} %get-tuple-element.85, ...), kind=kLoop, calls=%fused_computation.129 | loop fusion | flops 2359296 | bytes 3170306 | tf_op jit(solution)/shard_map/convert_element_type | solution.py:237
  90.2 3.6 %collective-permute-done.9 = bf16[230,256]{1,0:T(8,128)(2,1)S(1)} collective-permute-done((bf16[230,256]{1,0:T(8,128)(2,1)S(1)}, bf16[230,256]{1,0:T(8,128)(2,1)S(1)}, u32[]{:S(2)}, u32[]{:S(2)}) %collective-permute-start.9) | collective-permute-done | bytes 117792 | tf_op jit(solution)/shard_map/ppermute | solution.py:77
  93.8 0.6 fusion.252
  94.5 0.6 convert_add_fusion.8
  95.1 0.6 copy.30
  (276 shorter events, 2.3 us)
Async XLA Ops:
  0.6 14.3 %copy-start = (bf16[256,1024]{1,0:T(8,128)(2,1)S(1)}, bf16[256,1024]{1,0:T(8,128)(2,1)}, u32[]{:S(2)}) copy-start(bf16[256,1024]{1,0:T(8,128)(2,1)} %param.12) | copy-start | bytes 1572868
  1.8 5.5 %collective-permute-start = (bf16[3,256,256]{2,1,0:T(8,128)(2,1)S(1)}, bf16[3,256,256]{2,1,0:T(8,128)(2,1)S(1)}, u32[]{:S(2)}, u32[]{:S(2)}) collective-permute-start(bf16[3,256,256]{2,1,0:T(8,128)(2,1)S(1)} %get-tuple-element.92), channel_id=1, source_target_pairs={{0,1},{1,2},{2,3},{3,4},{4,5},{5,6},{6,7},{7,8},{8,9},{9,10},{10,1... | collective-permute-start | bytes 1179656 | tf_op jit(solution)/shard_map/ppermute | solution.py:21
  4.2 5.7 %collective-permute-start.1 = (bf16[3,256,256]{2,1,0:T(8,128)(2,1)S(1)}, bf16[3,256,256]{2,1,0:T(8,128)(2,1)S(1)}, u32[]{:S(2)}, u32[]{:S(2)}) collective-permute-start(bf16[3,256,256]{2,1,0:T(8,128)(2,1)S(1)} %get-tuple-element.91), channel_id=1, source_target_pairs={{1,0},{2,1},{3,2},{4,3},{5,4},{6,5},{7,6},{8,7},{9,8},{10,9},{11,1... | collective-permute-start | bytes 1179656 | tf_op jit(solution)/shard_map/ppermute | solution.py:24
  34.0 11.4 %copy-start.13 = (f32[1,1,256]{2,1,0:T(1,128)S(1)}, f32[1,1,256]{2,1,0:T(1,128)}, u32[]{:S(2)}) copy-start(f32[1,1,256]{2,1,0:T(1,128)} %copy-done.12) | copy-start | bytes 3076
  34.0 11.4 %copy-start.16 = (f32[1,1,256]{2,1,0:T(1,128)S(1)}, f32[1,1,256]{2,1,0:T(1,128)}, u32[]{:S(2)}) copy-start(f32[1,1,256]{2,1,0:T(1,128)} %copy-done.15) | copy-start | bytes 3076
  34.0 11.4 %copy-start.19 = (f32[1,1,256]{2,1,0:T(1,128)S(1)}, f32[1,1,256]{2,1,0:T(1,128)}, u32[]{:S(2)}) copy-start(f32[1,1,256]{2,1,0:T(1,128)} %copy-done.18) | copy-start | bytes 3076
  34.0 11.4 %copy-start.22 = (f32[1,1,256]{2,1,0:T(1,128)S(1)}, f32[1,1,256]{2,1,0:T(1,128)}, u32[]{:S(2)}) copy-start(f32[1,1,256]{2,1,0:T(1,128)} %copy-done.21) | copy-start | bytes 3076
  34.0 11.4 %copy-start.25 = (f32[1,1,256]{2,1,0:T(1,128)S(1)}, f32[1,1,256]{2,1,0:T(1,128)}, u32[]{:S(2)}) copy-start(f32[1,1,256]{2,1,0:T(1,128)} %copy-done.24) | copy-start | bytes 3076
  34.0 11.4 %copy-start.28 = (f32[1,1,256]{2,1,0:T(1,128)S(1)}, f32[1,1,256]{2,1,0:T(1,128)}, u32[]{:S(2)}) copy-start(f32[1,1,256]{2,1,0:T(1,128)} %copy-done.27) | copy-start | bytes 3076
  34.0 11.4 %copy-start.31 = (f32[1,1,256]{2,1,0:T(1,128)S(1)}, f32[1,1,256]{2,1,0:T(1,128)}, u32[]{:S(2)}) copy-start(f32[1,1,256]{2,1,0:T(1,128)} %copy-done.30) | copy-start | bytes 3076
  34.1 11.4 %copy-start.34 = (f32[1,1,256]{2,1,0:T(1,128)S(1)}, f32[1,1,256]{2,1,0:T(1,128)}, u32[]{:S(2)}) copy-start(f32[1,1,256]{2,1,0:T(1,128)} %copy-done.33) | copy-start | bytes 3076
  34.1 11.4 %copy-start.37 = (f32[1,1,256]{2,1,0:T(1,128)S(1)}, f32[1,1,256]{2,1,0:T(1,128)}, u32[]{:S(2)}) copy-start(f32[1,1,256]{2,1,0:T(1,128)} %copy-done.36) | copy-start | bytes 3076
  34.1 11.4 %copy-start.40 = (f32[1,1,256]{2,1,0:T(1,128)S(1)}, f32[1,1,256]{2,1,0:T(1,128)}, u32[]{:S(2)}) copy-start(f32[1,1,256]{2,1,0:T(1,128)} %copy-done.39) | copy-start | bytes 3076
  34.1 11.4 %copy-start.43 = (f32[1,1,256]{2,1,0:T(1,128)S(1)}, f32[1,1,256]{2,1,0:T(1,128)}, u32[]{:S(2)}) copy-start(f32[1,1,256]{2,1,0:T(1,128)} %copy-done.42) | copy-start | bytes 3076
  34.1 11.4 %copy-start.46 = (f32[1,1,256]{2,1,0:T(1,128)S(1)}, f32[1,1,256]{2,1,0:T(1,128)}, u32[]{:S(2)}) copy-start(f32[1,1,256]{2,1,0:T(1,128)} %copy-done.45) | copy-start | bytes 3076
  34.1 11.4 %copy-start.49 = (f32[1,1,256]{2,1,0:T(1,128)S(1)}, f32[1,1,256]{2,1,0:T(1,128)}, u32[]{:S(2)}) copy-start(f32[1,1,256]{2,1,0:T(1,128)} %copy-done.48) | copy-start | bytes 3076
  34.1 11.4 %copy-start.52 = (f32[1,1,256]{2,1,0:T(1,128)S(1)}, f32[1,1,256]{2,1,0:T(1,128)}, u32[]{:S(2)}) copy-start(f32[1,1,256]{2,1,0:T(1,128)} %copy-done.51) | copy-start | bytes 3076
  34.1 11.4 %copy-start.55 = (f32[1,1,256]{2,1,0:T(1,128)S(1)}, f32[1,1,256]{2,1,0:T(1,128)}, u32[]{:S(2)}) copy-start(f32[1,1,256]{2,1,0:T(1,128)} %copy-done.54) | copy-start | bytes 3076
  34.1 11.4 %copy-start.58 = (f32[1,1,256]{2,1,0:T(1,128)S(1)}, f32[1,1,256]{2,1,0:T(1,128)}, u32[]{:S(2)}) copy-start(f32[1,1,256]{2,1,0:T(1,128)} %copy-done.57) | copy-start | bytes 3076
  34.1 11.4 %copy-start.61 = (f32[1,1,256]{2,1,0:T(1,128)S(1)}, f32[1,1,256]{2,1,0:T(1,128)}, u32[]{:S(2)}) copy-start(f32[1,1,256]{2,1,0:T(1,128)} %copy-done.60) | copy-start | bytes 3076
  34.2 11.4 %copy-start.64 = (f32[1,1,256]{2,1,0:T(1,128)S(1)}, f32[1,1,256]{2,1,0:T(1,128)}, u32[]{:S(2)}) copy-start(f32[1,1,256]{2,1,0:T(1,128)} %copy-done.63) | copy-start | bytes 3076
  34.2 11.4 %copy-start.67 = (f32[1,1,256]{2,1,0:T(1,128)S(1)}, f32[1,1,256]{2,1,0:T(1,128)}, u32[]{:S(2)}) copy-start(f32[1,1,256]{2,1,0:T(1,128)} %copy-done.66) | copy-start | bytes 3076
  34.2 11.4 %copy-start.70 = (f32[1,1,256]{2,1,0:T(1,128)S(1)}, f32[1,1,256]{2,1,0:T(1,128)}, u32[]{:S(2)}) copy-start(f32[1,1,256]{2,1,0:T(1,128)} %copy-done.69) | copy-start | bytes 3076
  34.2 11.4 %copy-start.73 = (f32[1,1,256]{2,1,0:T(1,128)S(1)}, f32[1,1,256]{2,1,0:T(1,128)}, u32[]{:S(2)}) copy-start(f32[1,1,256]{2,1,0:T(1,128)} %copy-done.72) | copy-start | bytes 3076
  34.2 11.4 %copy-start.76 = (f32[1,1,256]{2,1,0:T(1,128)S(1)}, f32[1,1,256]{2,1,0:T(1,128)}, u32[]{:S(2)}) copy-start(f32[1,1,256]{2,1,0:T(1,128)} %copy-done.75) | copy-start | bytes 3076
  34.2 11.4 %copy-start.79 = (f32[1,1,256]{2,1,0:T(1,128)S(1)}, f32[1,1,256]{2,1,0:T(1,128)}, u32[]{:S(2)}) copy-start(f32[1,1,256]{2,1,0:T(1,128)} %copy-done.78) | copy-start | bytes 3076
  34.2 11.4 %copy-start.82 = (f32[1,1,256]{2,1,0:T(1,128)S(1)}, f32[1,1,256]{2,1,0:T(1,128)}, u32[]{:S(2)}) copy-start(f32[1,1,256]{2,1,0:T(1,128)} %copy-done.81) | copy-start | bytes 3076
  34.2 11.4 %copy-start.85 = (f32[1,1,256]{2,1,0:T(1,128)S(1)}, f32[1,1,256]{2,1,0:T(1,128)}, u32[]{:S(2)}) copy-start(f32[1,1,256]{2,1,0:T(1,128)} %copy-done.84) | copy-start | bytes 3076
  34.2 11.4 %copy-start.88 = (f32[1,1,256]{2,1,0:T(1,128)S(1)}, f32[1,1,256]{2,1,0:T(1,128)}, u32[]{:S(2)}) copy-start(f32[1,1,256]{2,1,0:T(1,128)} %copy-done.87) | copy-start | bytes 3076
  34.2 11.4 %copy-start.91 = (f32[1,1,256]{2,1,0:T(1,128)S(1)}, f32[1,1,256]{2,1,0:T(1,128)}, u32[]{:S(2)}) copy-start(f32[1,1,256]{2,1,0:T(1,128)} %copy-done.90) | copy-start | bytes 3076
  34.3 11.4 %copy-start.94 = (f32[1,1,256]{2,1,0:T(1,128)S(1)}, f32[1,1,256]{2,1,0:T(1,128)}, u32[]{:S(2)}) copy-start(f32[1,1,256]{2,1,0:T(1,128)} %copy-done.93) | copy-start | bytes 3076
  34.3 11.4 %copy-start.99 = (f32[1,1,256]{2,1,0:T(1,128)S(1)}, f32[1,1,256]{2,1,0:T(1,128)}, u32[]{:S(2)}) copy-start(f32[1,1,256]{2,1,0:T(1,128)} %copy-done.98) | copy-start | bytes 3076
  34.3 11.4 %copy-start.101 = (f32[1,1,256]{2,1,0:T(1,128)S(1)}, f32[1,1,256]{2,1,0:T(1,128)}, u32[]{:S(2)}) copy-start(f32[1,1,256]{2,1,0:T(1,128)} %copy-done.100) | copy-start | bytes 3076
  34.3 11.4 %copy-start.103 = (f32[1,1,256]{2,1,0:T(1,128)S(1)}, f32[1,1,256]{2,1,0:T(1,128)}, u32[]{:S(2)}) copy-start(f32[1,1,256]{2,1,0:T(1,128)} %copy-done.102) | copy-start | bytes 3076
  34.3 11.4 %copy-start.105 = (f32[1,1,256]{2,1,0:T(1,128)S(1)}, f32[1,1,256]{2,1,0:T(1,128)}, u32[]{:S(2)}) copy-start(f32[1,1,256]{2,1,0:T(1,128)} %copy-done.104) | copy-start | bytes 3076
  34.3 11.4 %copy-start.107 = (f32[1,1,256]{2,1,0:T(1,128)S(1)}, f32[1,1,256]{2,1,0:T(1,128)}, u32[]{:S(2)}) copy-start(f32[1,1,256]{2,1,0:T(1,128)} %copy-done.106) | copy-start | bytes 3076
  34.3 11.4 %copy-start.109 = (f32[1,1,256]{2,1,0:T(1,128)S(1)}, f32[1,1,256]{2,1,0:T(1,128)}, u32[]{:S(2)}) copy-start(f32[1,1,256]{2,1,0:T(1,128)} %copy-done.108) | copy-start | bytes 3076
  34.3 11.4 %copy-start.111 = (f32[1,1,256]{2,1,0:T(1,128)S(1)}, f32[1,1,256]{2,1,0:T(1,128)}, u32[]{:S(2)}) copy-start(f32[1,1,256]{2,1,0:T(1,128)} %copy-done.110) | copy-start | bytes 3076
  35.4 29.6 %collective-permute-start.3 = (bf16[3,256,256]{2,1,0:T(8,128)(2,1)}, bf16[3,256,256]{2,1,0:T(8,128)(2,1)S(1)}, u32[]{:S(2)}, u32[]{:S(2)}) collective-permute-start(bf16[3,256,256]{2,1,0:T(8,128)(2,1)} %get-tuple-element.90), channel_id=1, source_target_pairs={{1,0},{2,1},{3,2},{4,3},{5,4},{6,5},{7,6},{8,7},{9,8},{10,9},{11,1... | collective-permute-start | bytes 1179656 | tf_op jit(solution)/shard_map/ppermute | solution.py:99
  36.7 28.3 %collective-permute-start.2 = (bf16[3,256,256]{2,1,0:T(8,128)(2,1)}, bf16[3,256,256]{2,1,0:T(8,128)(2,1)S(1)}, u32[]{:S(2)}, u32[]{:S(2)}) collective-permute-start(bf16[3,256,256]{2,1,0:T(8,128)(2,1)} %get-tuple-element.89), channel_id=1, source_target_pairs={{0,1},{1,2},{2,3},{3,4},{4,5},{5,6},{6,7},{7,8},{8,9},{9,10},{10,1... | collective-permute-start | bytes 1179656 | tf_op jit(solution)/shard_map/ppermute | solution.py:98
  50.4 16.2 %collective-permute-start.4 = (f32[4,128,256]{2,1,0:T(8,128)}, f32[4,128,256]{2,1,0:T(8,128)}, u32[]{:S(2)}, u32[]{:S(2)}) collective-permute-start(f32[4,128,256]{2,1,0:T(8,128)} %constant_dynamic-slice_fusion.1), channel_id=1, source_target_pairs={{0,1},{1,0},{2,3},{3,2},{4,5},{5,4},{6,7},{7,6},{8,9},{9,8},{10,11... | collective-permute-start | bytes 1572872 | tf_op jit(solution)/shard_map/ppermute | solution.py:69
  58.0 9.7 %collective-permute-start.5 = (f32[512,256]{1,0:T(8,128)}, f32[512,256]{1,0:T(8,128)}, u32[]{:S(2)}, u32[]{:S(2)}) collective-permute-start(f32[512,256]{1,0:T(8,128)} %constant_dynamic-slice_fusion), channel_id=1, source_target_pairs={{0,1},{1,0},{2,3},{3,2},{4,5},{5,4},{6,7},{7,6},{8,9},{9,8},{10,11... | collective-permute-start | bytes 1572872 | tf_op jit(solution)/shard_map/ppermute | solution.py:69
  63.1 1.8 %collective-permute-start.6 = (f32[51,256]{1,0:T(8,128)S(1)}, f32[51,256]{1,0:T(8,128)S(1)}, u32[]{:S(2)}, u32[]{:S(2)}) collective-permute-start(f32[51,256]{1,0:T(8,128)S(1)} %concatenate.17), channel_id=1, source_target_pairs={{0,1},{1,0},{2,3},{3,2},{4,5},{5,4},{6,7},{7,6},{8,9},{9,8},{10,11... | collective-permute-start | bytes 156680 | tf_op jit(solution)/shard_map/ppermute | solution.py:69
  69.0 11.0 %collective-permute-start.7 = (bf16[614,256]{1,0:T(8,128)(2,1)S(1)}, bf16[614,256]{1,0:T(8,128)(2,1)S(1)}, u32[]{:S(2)}, u32[]{:S(2)}) collective-permute-start(bf16[614,256]{1,0:T(8,128)(2,1)S(1)} %pad_maximum_fusion), channel_id=1, source_target_pairs={{0,2},{1,3},{2,0},{3,1},{4,6},{5,7},{6,4},{7,5},{8,10},{9,11},{10,... | collective-permute-start | bytes 943112 | tf_op jit(solution)/shard_map/ppermute | solution.py:77
  80.1 9.0 %copy-start.5 = (f32[4,131,256]{2,1,0:T(8,128)S(1)}, f32[4,131,256]{2,1,0:T(8,128)}, u32[]{:S(2)}) copy-start(f32[4,131,256]{2,1,0:T(8,128)} %get-tuple-element.86) | copy-start | bytes 1609732
  80.1 9.0 %copy-start.7 = (bf16[4,256,256]{2,1,0:T(8,128)(2,1)S(1)}, bf16[4,256,256]{2,1,0:T(8,128)(2,1)}, u32[]{:S(2)}) copy-start(bf16[4,256,256]{2,1,0:T(8,128)(2,1)} %param.15) | copy-start | bytes 1572868
  80.3 6.1 %collective-permute-start.8 = (bf16[358,256]{1,0:T(8,128)(2,1)S(1)}, bf16[358,256]{1,0:T(8,128)(2,1)S(1)}, u32[]{:S(2)}, u32[]{:S(2)}) collective-permute-start(bf16[358,256]{1,0:T(8,128)(2,1)S(1)} %pad_maximum_fusion.1), channel_id=1, source_target_pairs={{0,4},{1,5},{2,6},{3,7},{4,0},{5,1},{6,2},{7,3},{8,12},{9,13},{10,... | collective-permute-start | bytes 549896 | tf_op jit(solution)/shard_map/ppermute | solution.py:77
  86.6 7.2 %collective-permute-start.9 = (bf16[230,256]{1,0:T(8,128)(2,1)S(1)}, bf16[230,256]{1,0:T(8,128)(2,1)S(1)}, u32[]{:S(2)}, u32[]{:S(2)}) collective-permute-start(bf16[230,256]{1,0:T(8,128)(2,1)S(1)} %pad_maximum_fusion.2), channel_id=1, source_target_pairs={{0,8},{1,9},{2,10},{3,11},{4,12},{5,13},{6,14},{7,15},{8,0},{9,1},... | collective-permute-start | bytes 353288 | tf_op jit(solution)/shard_map/ppermute | solution.py:77
  (77 other events, 483.4 us)

commit v15 on v14

--- a/solution.py
+++ b/solution.py
@@ -165,16 +165,14 @@
     pre_flat = (grad_act * gelu_slope(pre_act)).astype(jnp.bfloat16)
     grad_norm = jnp.dot(pre_flat, w_in.T, preferred_element_type=jnp.float32)
     quarters = hidden // channels
-    partial_in = jnp.stack(
-        [
-            lax.dot_general(
-                normed_flat,
-                pre_flat[:, q * channels : (q + 1) * channels],
-                (((0,), (0,)), ((), ())),
-                preferred_element_type=jnp.float32,
-            )
-            for q in range(quarters)
-        ]
+    positions = pre_flat.shape[0]
+    pre_quarters = pre_flat.reshape(positions, quarters, channels).transpose(1, 0, 2)
+    normed_copies = jnp.broadcast_to(normed_flat[None], (quarters, positions, channels))
+    partial_in = lax.dot_general(
+        normed_copies,
+        pre_quarters,
+        (((1,), (1,)), ((0,), (0,))),
+        preferred_element_type=jnp.float32,
     )
     partial_out = lax.dot_general(
         act_flat, grad_flat, (((0,), (0,)), ((), ())), preferred_element_type=jnp.float32

time: 96.3 us -> 90.2 us (0.937)
  matrix products: 13.7 us -> 8.1 us
  other arithmetic: 24.4 us -> 23.4 us
    dot_general x4 -> x1, matrix products: 4.77 us -> 0.43 us  [shards(): lax.dot_general(normed_copies, pre_quarters, (((1,), (1,)), ((0,), (0,)))...]
    dot_general x1, matrix products: 1.86 us -> 0.56 us  [shards(): grad_norm = jnp.dot(pre_flat, w_in.T, preferred_element_type=jnp.float32)]
    unnamed x231 -> x225, local copies, waits for them, and re-layouts: 2.58 us -> 3.26 us
  transfers between devices with their start and end apart: 10 -> 10, of which waited for: 4 -> 4; matrix products, arithmetic and copies ran while one was open for 23% -> 25% of each run, Pallas kernels for 0% -> 0%
where the time goes in v15:
time: 90.2 us; the launch traced here: 89.8 us
  starting transfers between devices  23.6 us (26%)
  other arithmetic  23.4 us (26%)
  waiting for transfers between devices  15.9 us (18%)
  local copies, waits for them, and re-layouts  15.4 us (17%)
  matrix products  8.1 us (9%)
  between operations  3.33 us (4%)
    ppermute x3, waiting for transfers between devices, halving_reduce(): got = lax.ppermute(sent, axis, pairs)  13.3 us
    ppermute x1, starting transfers between devices, halo_rows(): lax.ppermute(lax.slice_in_dim(block, block.shape[0] - width, None, axis=0...  8.71 us
    ppermute x3, starting transfers between devices, halving_reduce(): got = lax.ppermute(sent, axis, pairs)  7.65 us
    concatenate x1, local copies, waits for them, and re-layouts, shards(): jnp.concatenate([kernel_grad, gain_grad[None], scale_grad[None]], axis=0)  5.1 us
    reduce_sum x3, other arithmetic, kernel_terms(): jnp.sum(padded[row_tap:row_tap + image_rows, col_tap:col_tap + image_cols...  5.06 us
    reduce_sum x1, other arithmetic, shards(): centre = jnp.mean(filtered, axis=-1, keepdims=True)  3.85 us
    add x4, other arithmetic, shards(): total + line[col_tap:col_tap + image_cols] * flipped[row_tap, col_tap]  3.52 us
    unnamed x225, local copies, waits for them, and re-layouts  3.26 us
  transfers between devices with their start and end apart: 10, of which 4 were waited for; matrix products, arithmetic and copies ran while one was open for 25% of the time, Pallas kernels for 0%

profile of v15, /device:TPU:0, one launch (start us, length us, event | category | flops | bytes accessed | tf_op | source)
XLA Modules:
  0.0 89.8 jit_solution(11058051824216095506)
XLA Ops:
  0.7 1.1 %copy.38 = bf16[4,256,256]{2,1,0:T(8,128)(2,1)S(1)} copy(bf16[4,256,256]{2,1,0:T(8,128)(2,1)} %param.8) | data formatting | bytes 1048576
  1.8 2.4 %collective-permute-start = (bf16[3,256,256]{2,1,0:T(8,128)(2,1)S(1)}, bf16[3,256,256]{2,1,0:T(8,128)(2,1)S(1)}, u32[]{:S(2)}, u32[]{:S(2)}) collective-permute-start(bf16[3,256,256]{2,1,0:T(8,128)(2,1)S(1)} %get-tuple-element.92), channel_id=1, source_target_pairs={{0,1},{1,2},{2,3},{3,4},{4,5},{5,6},{6,7},{7,8},{8,9},{9,10},{10,1... | collective-permute-start | bytes 1179656 | tf_op jit(solution)/shard_map/ppermute | solution.py:21
  4.2 1.3 %collective-permute-start.1 = (bf16[3,256,256]{2,1,0:T(8,128)(2,1)S(1)}, bf16[3,256,256]{2,1,0:T(8,128)(2,1)S(1)}, u32[]{:S(2)}, u32[]{:S(2)}) collective-permute-start(bf16[3,256,256]{2,1,0:T(8,128)(2,1)S(1)} %get-tuple-element.91), channel_id=1, source_target_pairs={{1,0},{2,1},{3,2},{4,3},{5,4},{6,5},{7,6},{8,7},{9,8},{10,9},{11,1... | collective-permute-start | bytes 1179656 | tf_op jit(solution)/shard_map/ppermute | solution.py:24
  5.5 0.7 bitcast_reduce_fusion
  7.3 2.6 %collective-permute-done.1 = bf16[3,256,256]{2,1,0:T(8,128)(2,1)S(1)} collective-permute-done((bf16[3,256,256]{2,1,0:T(8,128)(2,1)S(1)}, bf16[3,256,256]{2,1,0:T(8,128)(2,1)S(1)}, u32[]{:S(2)}, u32[]{:S(2)}) %collective-permute-start.1) | collective-permute-done | bytes 393248 | tf_op jit(solution)/shard_map/ppermute | solution.py:24
  9.9 0.3 fusion.23
  10.3 3.9 %fusion.260 = (f32[4,128]{1,0:T(4,128)S(1)}, f32[4,128,256]{2,1,0:T(8,128)S(1)}) fusion(f32[256]{0:T(256)S(1)} %bitcast.207, f32[10,134,256]{2,1,0:T(8,128)S(1)} %fusion.23, f32[256]{0:T(256)S(1)} %bitcast.212, f32[256]{0:T(256)S(1)} %bitcast.177, f32[256]{0:T(256)S(1)} %bitcast.182, f32[256]{0:T(256)S(1)} %bitcast.187, f32[256]{0:T(256)S(1)} %bitcast.192, ...), kind=kLoop, calls=%fused_computation.494 | loop fusion | flops 12844544 | bytes 26266624 | tf_op jit(solution)/shard_map/reduce_sum | solution.py:151
  14.5 0.2 multiply_reduce_fusion.3
  15.2 1.8 %fusion.11 = (bf16[1024,512]{0,1:T(8,128)(2,1)}, f32[512,1024]{1,0:T(8,128)S(1)}) fusion(bf16[512,256]{1,0:T(8,128)(2,1)S(1)} %bitcast.168, bf16[256,1024]{1,0:T(8,128)(2,1)S(1)} %copy-done), kind=kOutput, calls=%fused_computation.112 | convolution fusion | flops 273154048 | bytes 3932160 | tf_op jit(solution)/shard_map/dot_general | solution.py:161
  17.0 2.2 %fusion.124 = (f32[256]{0:T(256)}, bf16[4,128,256]{2,1,0:T(8,128)(2,1)S(1)}, f32[512,256]{1,0:T(8,128)}) fusion(bf16[4,256,256]{2,1,0:T(8,128)(2,1)S(1)} %copy-done.5, s32[]{:T(128)S(6)} %select_n.80, f32[256]{0:T(256)S(1)} %copy-done.110, bf16[1024,256]{1,0:T(8,128)(2,1)S(1)} %copy-done.8, f32[512,1024]{1,0:T(8,128)S(1)} %get-tuple-element.154), kind=kOutput, calls=%fused_computation.236 | convolution fusion | flops 273809152 | bytes 3672068 | tf_op jit(solution)/shard_map/dot_general | solution.py:163
  19.1 0.7 copy-done.7
  19.9 1.4 %fusion.6 = bf16[512,1024]{1,0:T(8,128)(2,1)S(1)} fusion(f32[512,1024]{1,0:T(8,128)S(1)} %get-tuple-element.154, bf16[512,256]{1,0:T(8,128)(2,1)S(1)} %bitcast.164, bf16[1024,256]{1,0:T(8,128)(2,1)S(1)} %copy-done.8), kind=kOutput, calls=%fused_computation.107 | convolution fusion | flops 278396928 | bytes 3932160 | tf_op jit(solution)/shard_map/dot_general | solution.py:164
  21.3 0.6 multiply_reduce_fusion.2
  21.9 0.8 multiply_reduce_fusion
  22.7 1.8 %fusion.171 = (f32[256]{0:T(256)}, f32[256]{0:T(256)}, f32[256]{0:T(256)}, f32[256]{0:T(256)}, f32[256]{0:T(256)}, /*index=5*/f32[256]{0:T(256)}, f32[256]{0:T(2...) fusion(f32[10,134,256]{2,1,0:T(8,128)S(1)} %fusion.23, ...), kind=kLoop, calls=%fused_computation.283 | loop fusion | flops 4584192 | bytes 8148992 | tf_op jit(solution)/shard_map/reduce_sum | solution.py:132
  24.5 1.6 %fusion.173 = (f32[256]{0:T(256)}, f32[256]{0:T(256)}, f32[256]{0:T(256)}, f32[256]{0:T(256)}, f32[256]{0:T(256)}, /*index=5*/f32[256]{0:T(256)}, f32[256]{0:T(2...) fusion(bf16[4,128,256]{2,1,0:T(8,128)(2,1)S(1)} %get-tuple-elem, ...), kind=kLoop, calls=%fused_computation.285 | loop fusion | flops 4845056 | bytes 9717760 | tf_op jit(solution)/shard_map/reduce_sum | solution.py:132
  26.1 1.6 %fusion.172 = (f32[256]{0:T(256)}, f32[256]{0:T(256)}, f32[256]{0:T(256)}, f32[256]{0:T(256)}, f32[256]{0:T(256)}, /*index=5*/f32[256]{0:T(256)}, f32[256]{0:T(2...) fusion(bf16[4,128,256]{2,1,0:T(8,128)(2,1)S(1)} %get-tuple-elem, ...), kind=kLoop, calls=%fused_computation.284 | loop fusion | flops 4845056 | bytes 9717760 | tf_op jit(solution)/shard_map/reduce_sum | solution.py:132
  28.2 0.9 %fusion.262 = (bf16[3,256,256]{2,1,0:T(8,128)(2,1)}, bf16[3,256,256]{2,1,0:T(8,128)(2,1)}) fusion(bf16[4,256,256]{2,1,0:T(8,128)(2,1)S(1)} %get-tuple-element.94), kind=kLoop, calls=%fused_computation.496 | loop fusion | bytes 1572864 | tf_op jit(solution)/shard_map/slice | solution.py:98
  29.1 1.3 %collective-permute-start.3 = (bf16[3,256,256]{2,1,0:T(8,128)(2,1)}, bf16[3,256,256]{2,1,0:T(8,128)(2,1)S(1)}, u32[]{:S(2)}, u32[]{:S(2)}) collective-permute-start(bf16[3,256,256]{2,1,0:T(8,128)(2,1)} %get-tuple-element.90), channel_id=1, source_target_pairs={{1,0},{2,1},{3,2},{4,3},{5,4},{6,5},{7,6},{8,7},{9,8},{10,9},{11,1... | collective-permute-start | bytes 1179656 | tf_op jit(solution)/shard_map/ppermute | solution.py:99
  30.4 8.7 %collective-permute-start.2 = (bf16[3,256,256]{2,1,0:T(8,128)(2,1)}, bf16[3,256,256]{2,1,0:T(8,128)(2,1)S(1)}, u32[]{:S(2)}, u32[]{:S(2)}) collective-permute-start(bf16[3,256,256]{2,1,0:T(8,128)(2,1)} %get-tuple-element.89), channel_id=1, source_target_pairs={{0,1},{1,2},{2,3},{3,4},{4,5},{5,6},{6,7},{7,8},{8,9},{9,10},{10,1... | collective-permute-start | bytes 1179656 | tf_op jit(solution)/shard_map/ppermute | solution.py:98
  39.5 2.7 %fusion.117 = f32[4,134,256]{2,1,0:T(8,128)S(1)} fusion(f32[4,128,256]{2,1,0:T(8,128)S(1)} %get-tuple-element.93, f32[256]{0:T(256)S(1)} %bitcast.203, f32[256]{0:T(256)S(1)} %bitcast.243, f32[256]{0:T(256)S(1)} %bitcast.218, f32[256]{0:T(256)S(1)} %bitcast.238, f32[256]{0:T(256)S(1)} %bitcast.233, f32[256]{0:T(256)S(1)} %bitcast.228, f32[256]{0:T(256)S(1)} %bitcast.223, ...), kind=kLoop, calls=%fused_computation.229 | loop fusion | flops 13309952 | bytes 1123328 | tf_op jit(solution)/shard_map/add | solution.py:120
  42.2 0.9 fusion.261
  43.0 0.4 fusion.15
  43.6 0.8 constant_dynamic-slice_fusion.1
  44.4 1.7 %collective-permute-start.4 = (f32[4,128,256]{2,1,0:T(8,128)}, f32[4,128,256]{2,1,0:T(8,128)}, u32[]{:S(2)}, u32[]{:S(2)}) collective-permute-start(f32[4,128,256]{2,1,0:T(8,128)} %constant_dynamic-slice_fusion.1), channel_id=1, source_target_pairs={{0,1},{1,0},{2,3},{3,2},{4,5},{5,4},{6,7},{7,6},{8,9},{9,8},{10,11... | collective-permute-start | bytes 1572872 | tf_op jit(solution)/shard_map/ppermute | solution.py:69
  46.1 2.3 %copy.25 = bf16[1024,512]{1,0:T(8,128)(2,1)} copy(bf16[1024,512]{0,1:T(8,128)(2,1)} %get-tuple-element.153) | data formatting | bytes 2097152 | tf_op jit(solution)/shard_map/convert_element_type | solution.py:162
  48.4 1.7 %convolution_bitcast_fusion = f32[2,2,2,2,64,256]{5,4,0,1,2,3:T(8,128)S(1)} fusion(bf16[2,2,2,2,64,512]{5,4,3,2,1,0:T(8,128)(2,1)} %bitcast.162, bf16[512,256,1,1,1,1]{1,0,5,4,3,2:T(8,128)(2,1)} %bitcast.165), kind=kOutput, calls=%fused_computation.119 | convolution fusion | flops 268435456 | bytes 2359296 | tf_op jit(solution)/shard_map/dot_general | solution.py:177
  50.2 1.0 %copy-done.2 = f32[2,2,2,2,64,256]{5,4,3,2,1,0:T(8,128)} copy-done((f32[2,2,2,2,64,256]{5,4,3,2,1,0:T(8,128)}, f32[2,2,2,2,64,256]{5,4,3,2,1,0:T(8,128)S(1)}, u32[]{:S(2)}) %copy-start.2) | copy-done | bytes 1048600
  51.2 0.8 constant_dynamic-slice_fusion
  52.1 5.1 %concatenate.16 = f32[51,256]{1,0:T(8,128)S(1)} concatenate(f32[1,256]{1,0:T(1,128)} %bitcast.375, f32[1,256]{1,0:T(1,128)} %bitcast.376, f32[1,256]{1,0:T(1,128)} %bitcast.377, f32[1,256]{1,0:T(1,128)} %bitcast.378, f32[1,256]{1,0:T(1,128)} %bitcast.379, f32[1,256]{1,0:T(1,128)} %bitcast.380, f32[1,256]{1,0:T(1,128)} %bitcast.381, f32[1,256]{1,0:T(1,128)} %bitcast.382, ...), dimensions={0} | concatenate | bytes 104448 | tf_op jit(solution)/shard_map/concatenate | solution.py:197
  57.2 0.6 collective-permute-start.6
  57.7 1.2 %fusion.249 = bf16[4,256,256]{2,1,0:T(8,128)(2,1)S(1)} fusion(bf16[4,256,256]{2,1,0:T(8,128)(2,1)S(1)} %copy.38, s32[]{:T(128)S(6)} %select_n.80, f32[4,128,256]{2,1,0:T(8,128)} %bitcast.163, f32[256]{0:T(256)} %param.14), kind=kLoop, calls=%fused_computation.443 | loop fusion | flops 524288 | bytes 1049604 | tf_op jit(solution)/shard_map/dynamic_update_slice | solution.py:184
  59.0 1.4 %fusion.215 = f32[1,256,256]{2,1,0:T(8,128)S(1)} fusion(f32[256]{0:T(256)} %bitcast.288, f32[256]{0:T(256)} %bitcast.284, f32[256]{0:T(256)} %bitcast.280, f32[256]{0:T(256)} %bitcast.276, f32[256]{0:T(256)} %bitcast.300, f32[256]{0:T(256)} %bitcast.296, f32[256]{0:T(256)} %bitcast.292, f32[256]{0:T(256)S(1)} %bitcast.204, f32[256]{0:T(256)S(1)} %bitcast.244, ...), kind=kLoop, calls=%fused_computation.409 | loop fusion | flops 4063232 | bytes 1463296 | tf_op jit(solution)/shard_map/add | solution.py:232
  60.6 1.1 %dynamic-slice_add_fusion.1 = f32[4,128,256]{2,1,0:T(8,128)S(1)} fusion(f32[4,128,256]{2,1,0:T(8,128)} %collective-permute-done.4, f32[4,256,256]{2,1,0:T(8,128)S(1)} %bitcast.159, s32[]{:T(128)S(6)} %select_n.87), kind=kLoop, calls=%fused_computation.288 | loop fusion | flops 131072 | bytes 1572868 | tf_op jit(solution)/shard_map/add | solution.py:88
  61.8 1.1 %dynamic-slice_add_fusion = f32[512,256]{1,0:T(8,128)S(1)} fusion(f32[512,256]{1,0:T(8,128)} %collective-permute-done.5, f32[1024,256]{1,0:T(8,128)S(1)} %bitcast.161, s32[]{:T(128)S(6)} %select_n.89), kind=kLoop, calls=%fused_computation.287 | loop fusion | flops 131072 | bytes 1572868 | tf_op jit(solution)/shard_map/add | solution.py:89
  63.0 3.4 %collective-permute-start.7 = (bf16[614,256]{1,0:T(8,128)(2,1)S(1)}, bf16[614,256]{1,0:T(8,128)(2,1)S(1)}, u32[]{:S(2)}, u32[]{:S(2)}) collective-permute-start(bf16[614,256]{1,0:T(8,128)(2,1)S(1)} %pad_maximum_fusion), channel_id=1, source_target_pairs={{0,2},{1,3},{2,0},{3,1},{4,6},{5,7},{6,4},{7,5},{8,10},{9,11},{10,... | collective-permute-start | bytes 943112 | tf_op jit(solution)/shard_map/ppermute | solution.py:77
  66.6 0.7 fusion.229
  67.4 0.7 fusion.208
  68.1 6.0 %collective-permute-done.7 = bf16[614,256]{1,0:T(8,128)(2,1)S(1)} collective-permute-done((bf16[614,256]{1,0:T(8,128)(2,1)S(1)}, bf16[614,256]{1,0:T(8,128)(2,1)S(1)}, u32[]{:S(2)}, u32[]{:S(2)}) %collective-permute-start.7) | collective-permute-done | bytes 314400 | tf_op jit(solution)/shard_map/ppermute | solution.py:77
  74.3 1.6 %collective-permute-start.8 = (bf16[358,256]{1,0:T(8,128)(2,1)S(1)}, bf16[358,256]{1,0:T(8,128)(2,1)S(1)}, u32[]{:S(2)}, u32[]{:S(2)}) collective-permute-start(bf16[358,256]{1,0:T(8,128)(2,1)S(1)} %pad_maximum_fusion.1), channel_id=1, source_target_pairs={{0,4},{1,5},{2,6},{3,7},{4,0},{5,1},{6,2},{7,3},{8,12},{9,13},{10,... | collective-permute-start | bytes 549896 | tf_op jit(solution)/shard_map/ppermute | solution.py:77
  76.0 0.7 fusion.188
  76.7 3.7 %collective-permute-done.8 = bf16[358,256]{1,0:T(8,128)(2,1)S(1)} collective-permute-done((bf16[358,256]{1,0:T(8,128)(2,1)S(1)}, bf16[358,256]{1,0:T(8,128)(2,1)S(1)}, u32[]{:S(2)}, u32[]{:S(2)}) %collective-permute-start.8) | collective-permute-done | bytes 183328 | tf_op jit(solution)/shard_map/ppermute | solution.py:77
  80.6 2.6 %collective-permute-start.9 = (bf16[230,256]{1,0:T(8,128)(2,1)S(1)}, bf16[230,256]{1,0:T(8,128)(2,1)S(1)}, u32[]{:S(2)}, u32[]{:S(2)}) collective-permute-start(bf16[230,256]{1,0:T(8,128)(2,1)S(1)} %pad_maximum_fusion.2), channel_id=1, source_target_pairs={{0,8},{1,9},{2,10},{3,11},{4,12},{5,13},{6,14},{7,15},{8,0},{9,1},... | collective-permute-start | bytes 353288 | tf_op jit(solution)/shard_map/ppermute | solution.py:77
  83.2 1.0 %fusion.18 = bf16[4,256,256]{2,1,0:T(8,128)(2,1)} fusion(f32[1,256,256]{2,1,0:T(8,128)S(1)} %fusion.229, f32[1,256,256]{2,1,0:T(8,128)S(1)} %fusion.215, f32[1,256,256]{2,1,0:T(8,128)S(1)} %fusion.208, f32[1,256,256]{2,1,0:T(8,128)S(1)} %fusion.188, f32[4,131,256]{2,1,0:T(8,128)S(1)} %copy-done.4, f32[4,131,256]{2,1,0:T(8,128)S(1)} %get-tuple-element.85, ...), kind=kLoop, calls=%fused_computation.128 | loop fusion | flops 2359296 | bytes 3170306 | tf_op jit(solution)/shard_map/convert_element_type | solution.py:235
  84.2 3.6 %collective-permute-done.9 = bf16[230,256]{1,0:T(8,128)(2,1)S(1)} collective-permute-done((bf16[230,256]{1,0:T(8,128)(2,1)S(1)}, bf16[230,256]{1,0:T(8,128)(2,1)S(1)}, u32[]{:S(2)}, u32[]{:S(2)}) %collective-permute-start.9) | collective-permute-done | bytes 117792 | tf_op jit(solution)/shard_map/ppermute | solution.py:77
  87.8 0.6 fusion.255
  88.5 0.6 convert_add_fusion.8
  89.1 0.6 copy.30
  (266 shorter events, 1.6 us)
Async XLA Ops:
  0.6 14.5 %copy-start = (bf16[256,1024]{1,0:T(8,128)(2,1)S(1)}, bf16[256,1024]{1,0:T(8,128)(2,1)}, u32[]{:S(2)}) copy-start(bf16[256,1024]{1,0:T(8,128)(2,1)} %param.12) | copy-start | bytes 1572868
  1.8 5.5 %collective-permute-start = (bf16[3,256,256]{2,1,0:T(8,128)(2,1)S(1)}, bf16[3,256,256]{2,1,0:T(8,128)(2,1)S(1)}, u32[]{:S(2)}, u32[]{:S(2)}) collective-permute-start(bf16[3,256,256]{2,1,0:T(8,128)(2,1)S(1)} %get-tuple-element.92), channel_id=1, source_target_pairs={{0,1},{1,2},{2,3},{3,4},{4,5},{5,6},{6,7},{7,8},{8,9},{9,10},{10,1... | collective-permute-start | bytes 1179656 | tf_op jit(solution)/shard_map/ppermute | solution.py:21
  4.2 5.7 %collective-permute-start.1 = (bf16[3,256,256]{2,1,0:T(8,128)(2,1)S(1)}, bf16[3,256,256]{2,1,0:T(8,128)(2,1)S(1)}, u32[]{:S(2)}, u32[]{:S(2)}) collective-permute-start(bf16[3,256,256]{2,1,0:T(8,128)(2,1)S(1)} %get-tuple-element.91), channel_id=1, source_target_pairs={{1,0},{2,1},{3,2},{4,3},{5,4},{6,5},{7,6},{8,7},{9,8},{10,9},{11,1... | collective-permute-start | bytes 1179656 | tf_op jit(solution)/shard_map/ppermute | solution.py:24
  27.7 11.4 %copy-start.11 = (f32[1,1,256]{2,1,0:T(1,128)S(1)}, f32[1,1,256]{2,1,0:T(1,128)}, u32[]{:S(2)}) copy-start(f32[1,1,256]{2,1,0:T(1,128)} %copy-done.10) | copy-start | bytes 3076
  27.7 11.4 %copy-start.14 = (f32[1,1,256]{2,1,0:T(1,128)S(1)}, f32[1,1,256]{2,1,0:T(1,128)}, u32[]{:S(2)}) copy-start(f32[1,1,256]{2,1,0:T(1,128)} %copy-done.13) | copy-start | bytes 3076
  27.8 11.4 %copy-start.17 = (f32[1,1,256]{2,1,0:T(1,128)S(1)}, f32[1,1,256]{2,1,0:T(1,128)}, u32[]{:S(2)}) copy-start(f32[1,1,256]{2,1,0:T(1,128)} %copy-done.16) | copy-start | bytes 3076
  27.8 11.4 %copy-start.20 = (f32[1,1,256]{2,1,0:T(1,128)S(1)}, f32[1,1,256]{2,1,0:T(1,128)}, u32[]{:S(2)}) copy-start(f32[1,1,256]{2,1,0:T(1,128)} %copy-done.19) | copy-start | bytes 3076
  27.8 11.4 %copy-start.23 = (f32[1,1,256]{2,1,0:T(1,128)S(1)}, f32[1,1,256]{2,1,0:T(1,128)}, u32[]{:S(2)}) copy-start(f32[1,1,256]{2,1,0:T(1,128)} %copy-done.22) | copy-start | bytes 3076
  27.8 11.4 %copy-start.26 = (f32[1,1,256]{2,1,0:T(1,128)S(1)}, f32[1,1,256]{2,1,0:T(1,128)}, u32[]{:S(2)}) copy-start(f32[1,1,256]{2,1,0:T(1,128)} %copy-done.25) | copy-start | bytes 3076
  27.8 11.4 %copy-start.29 = (f32[1,1,256]{2,1,0:T(1,128)S(1)}, f32[1,1,256]{2,1,0:T(1,128)}, u32[]{:S(2)}) copy-start(f32[1,1,256]{2,1,0:T(1,128)} %copy-done.28) | copy-start | bytes 3076
  27.8 11.4 %copy-start.32 = (f32[1,1,256]{2,1,0:T(1,128)S(1)}, f32[1,1,256]{2,1,0:T(1,128)}, u32[]{:S(2)}) copy-start(f32[1,1,256]{2,1,0:T(1,128)} %copy-done.31) | copy-start | bytes 3076
  27.8 11.4 %copy-start.35 = (f32[1,1,256]{2,1,0:T(1,128)S(1)}, f32[1,1,256]{2,1,0:T(1,128)}, u32[]{:S(2)}) copy-start(f32[1,1,256]{2,1,0:T(1,128)} %copy-done.34) | copy-start | bytes 3076
  27.8 11.4 %copy-start.38 = (f32[1,1,256]{2,1,0:T(1,128)S(1)}, f32[1,1,256]{2,1,0:T(1,128)}, u32[]{:S(2)}) copy-start(f32[1,1,256]{2,1,0:T(1,128)} %copy-done.37) | copy-start | bytes 3076
  27.8 11.4 %copy-start.41 = (f32[1,1,256]{2,1,0:T(1,128)S(1)}, f32[1,1,256]{2,1,0:T(1,128)}, u32[]{:S(2)}) copy-start(f32[1,1,256]{2,1,0:T(1,128)} %copy-done.40) | copy-start | bytes 3076
  27.8 11.4 %copy-start.44 = (f32[1,1,256]{2,1,0:T(1,128)S(1)}, f32[1,1,256]{2,1,0:T(1,128)}, u32[]{:S(2)}) copy-start(f32[1,1,256]{2,1,0:T(1,128)} %copy-done.43) | copy-start | bytes 3076
  27.8 11.4 %copy-start.47 = (f32[1,1,256]{2,1,0:T(1,128)S(1)}, f32[1,1,256]{2,1,0:T(1,128)}, u32[]{:S(2)}) copy-start(f32[1,1,256]{2,1,0:T(1,128)} %copy-done.46) | copy-start | bytes 3076
  27.8 11.4 %copy-start.50 = (f32[1,1,256]{2,1,0:T(1,128)S(1)}, f32[1,1,256]{2,1,0:T(1,128)}, u32[]{:S(2)}) copy-start(f32[1,1,256]{2,1,0:T(1,128)} %copy-done.49) | copy-start | bytes 3076
  27.9 11.4 %copy-start.53 = (f32[1,1,256]{2,1,0:T(1,128)S(1)}, f32[1,1,256]{2,1,0:T(1,128)}, u32[]{:S(2)}) copy-start(f32[1,1,256]{2,1,0:T(1,128)} %copy-done.52) | copy-start | bytes 3076
  27.9 11.4 %copy-start.56 = (f32[1,1,256]{2,1,0:T(1,128)S(1)}, f32[1,1,256]{2,1,0:T(1,128)}, u32[]{:S(2)}) copy-start(f32[1,1,256]{2,1,0:T(1,128)} %copy-done.55) | copy-start | bytes 3076
  27.9 11.4 %copy-start.59 = (f32[1,1,256]{2,1,0:T(1,128)S(1)}, f32[1,1,256]{2,1,0:T(1,128)}, u32[]{:S(2)}) copy-start(f32[1,1,256]{2,1,0:T(1,128)} %copy-done.58) | copy-start | bytes 3076
  27.9 11.4 %copy-start.62 = (f32[1,1,256]{2,1,0:T(1,128)S(1)}, f32[1,1,256]{2,1,0:T(1,128)}, u32[]{:S(2)}) copy-start(f32[1,1,256]{2,1,0:T(1,128)} %copy-done.61) | copy-start | bytes 3076
  27.9 11.4 %copy-start.65 = (f32[1,1,256]{2,1,0:T(1,128)S(1)}, f32[1,1,256]{2,1,0:T(1,128)}, u32[]{:S(2)}) copy-start(f32[1,1,256]{2,1,0:T(1,128)} %copy-done.64) | copy-start | bytes 3076
  27.9 11.4 %copy-start.68 = (f32[1,1,256]{2,1,0:T(1,128)S(1)}, f32[1,1,256]{2,1,0:T(1,128)}, u32[]{:S(2)}) copy-start(f32[1,1,256]{2,1,0:T(1,128)} %copy-done.67) | copy-start | bytes 3076
  27.9 11.4 %copy-start.71 = (f32[1,1,256]{2,1,0:T(1,128)S(1)}, f32[1,1,256]{2,1,0:T(1,128)}, u32[]{:S(2)}) copy-start(f32[1,1,256]{2,1,0:T(1,128)} %copy-done.70) | copy-start | bytes 3076
  27.9 11.4 %copy-start.74 = (f32[1,1,256]{2,1,0:T(1,128)S(1)}, f32[1,1,256]{2,1,0:T(1,128)}, u32[]{:S(2)}) copy-start(f32[1,1,256]{2,1,0:T(1,128)} %copy-done.73) | copy-start | bytes 3076
  27.9 11.4 %copy-start.77 = (f32[1,1,256]{2,1,0:T(1,128)S(1)}, f32[1,1,256]{2,1,0:T(1,128)}, u32[]{:S(2)}) copy-start(f32[1,1,256]{2,1,0:T(1,128)} %copy-done.76) | copy-start | bytes 3076
  27.9 11.4 %copy-start.80 = (f32[1,1,256]{2,1,0:T(1,128)S(1)}, f32[1,1,256]{2,1,0:T(1,128)}, u32[]{:S(2)}) copy-start(f32[1,1,256]{2,1,0:T(1,128)} %copy-done.79) | copy-start | bytes 3076
  27.9 11.4 %copy-start.83 = (f32[1,1,256]{2,1,0:T(1,128)S(1)}, f32[1,1,256]{2,1,0:T(1,128)}, u32[]{:S(2)}) copy-start(f32[1,1,256]{2,1,0:T(1,128)} %copy-done.82) | copy-start | bytes 3076
  28.0 11.4 %copy-start.86 = (f32[1,1,256]{2,1,0:T(1,128)S(1)}, f32[1,1,256]{2,1,0:T(1,128)}, u32[]{:S(2)}) copy-start(f32[1,1,256]{2,1,0:T(1,128)} %copy-done.85) | copy-start | bytes 3076
  28.0 11.4 %copy-start.89 = (f32[1,1,256]{2,1,0:T(1,128)S(1)}, f32[1,1,256]{2,1,0:T(1,128)}, u32[]{:S(2)}) copy-start(f32[1,1,256]{2,1,0:T(1,128)} %copy-done.88) | copy-start | bytes 3076
  28.0 11.4 %copy-start.92 = (f32[1,1,256]{2,1,0:T(1,128)S(1)}, f32[1,1,256]{2,1,0:T(1,128)}, u32[]{:S(2)}) copy-start(f32[1,1,256]{2,1,0:T(1,128)} %copy-done.91) | copy-start | bytes 3076
  28.0 11.4 %copy-start.97 = (f32[1,1,256]{2,1,0:T(1,128)S(1)}, f32[1,1,256]{2,1,0:T(1,128)}, u32[]{:S(2)}) copy-start(f32[1,1,256]{2,1,0:T(1,128)} %copy-done.96) | copy-start | bytes 3076
  28.0 11.4 %copy-start.99 = (f32[1,1,256]{2,1,0:T(1,128)S(1)}, f32[1,1,256]{2,1,0:T(1,128)}, u32[]{:S(2)}) copy-start(f32[1,1,256]{2,1,0:T(1,128)} %copy-done.98) | copy-start | bytes 3076
  28.0 11.4 %copy-start.101 = (f32[1,1,256]{2,1,0:T(1,128)S(1)}, f32[1,1,256]{2,1,0:T(1,128)}, u32[]{:S(2)}) copy-start(f32[1,1,256]{2,1,0:T(1,128)} %copy-done.100) | copy-start | bytes 3076
  28.0 11.4 %copy-start.103 = (f32[1,1,256]{2,1,0:T(1,128)S(1)}, f32[1,1,256]{2,1,0:T(1,128)}, u32[]{:S(2)}) copy-start(f32[1,1,256]{2,1,0:T(1,128)} %copy-done.102) | copy-start | bytes 3076
  28.0 11.4 %copy-start.105 = (f32[1,1,256]{2,1,0:T(1,128)S(1)}, f32[1,1,256]{2,1,0:T(1,128)}, u32[]{:S(2)}) copy-start(f32[1,1,256]{2,1,0:T(1,128)} %copy-done.104) | copy-start | bytes 3076
  28.0 11.4 %copy-start.107 = (f32[1,1,256]{2,1,0:T(1,128)S(1)}, f32[1,1,256]{2,1,0:T(1,128)}, u32[]{:S(2)}) copy-start(f32[1,1,256]{2,1,0:T(1,128)} %copy-done.106) | copy-start | bytes 3076
  28.1 11.4 %copy-start.109 = (f32[1,1,256]{2,1,0:T(1,128)S(1)}, f32[1,1,256]{2,1,0:T(1,128)}, u32[]{:S(2)}) copy-start(f32[1,1,256]{2,1,0:T(1,128)} %copy-done.108) | copy-start | bytes 3076
  29.1 29.9 %collective-permute-start.3 = (bf16[3,256,256]{2,1,0:T(8,128)(2,1)}, bf16[3,256,256]{2,1,0:T(8,128)(2,1)S(1)}, u32[]{:S(2)}, u32[]{:S(2)}) collective-permute-start(bf16[3,256,256]{2,1,0:T(8,128)(2,1)} %get-tuple-element.90), channel_id=1, source_target_pairs={{1,0},{2,1},{3,2},{4,3},{5,4},{6,5},{7,6},{8,7},{9,8},{10,9},{11,1... | collective-permute-start | bytes 1179656 | tf_op jit(solution)/shard_map/ppermute | solution.py:99
  30.4 28.6 %collective-permute-start.2 = (bf16[3,256,256]{2,1,0:T(8,128)(2,1)}, bf16[3,256,256]{2,1,0:T(8,128)(2,1)S(1)}, u32[]{:S(2)}, u32[]{:S(2)}) collective-permute-start(bf16[3,256,256]{2,1,0:T(8,128)(2,1)} %get-tuple-element.89), channel_id=1, source_target_pairs={{0,1},{1,2},{2,3},{3,4},{4,5},{5,6},{6,7},{7,8},{8,9},{9,10},{10,1... | collective-permute-start | bytes 1179656 | tf_op jit(solution)/shard_map/ppermute | solution.py:98
  44.4 16.2 %collective-permute-start.4 = (f32[4,128,256]{2,1,0:T(8,128)}, f32[4,128,256]{2,1,0:T(8,128)}, u32[]{:S(2)}, u32[]{:S(2)}) collective-permute-start(f32[4,128,256]{2,1,0:T(8,128)} %constant_dynamic-slice_fusion.1), channel_id=1, source_target_pairs={{0,1},{1,0},{2,3},{3,2},{4,5},{5,4},{6,7},{7,6},{8,9},{9,8},{10,11... | collective-permute-start | bytes 1572872 | tf_op jit(solution)/shard_map/ppermute | solution.py:69
  52.1 9.7 %collective-permute-start.5 = (f32[512,256]{1,0:T(8,128)}, f32[512,256]{1,0:T(8,128)}, u32[]{:S(2)}, u32[]{:S(2)}) collective-permute-start(f32[512,256]{1,0:T(8,128)} %constant_dynamic-slice_fusion), channel_id=1, source_target_pairs={{0,1},{1,0},{2,3},{3,2},{4,5},{5,4},{6,7},{7,6},{8,9},{9,8},{10,11... | collective-permute-start | bytes 1572872 | tf_op jit(solution)/shard_map/ppermute | solution.py:69
  57.2 1.8 %collective-permute-start.6 = (f32[51,256]{1,0:T(8,128)S(1)}, f32[51,256]{1,0:T(8,128)S(1)}, u32[]{:S(2)}, u32[]{:S(2)}) collective-permute-start(f32[51,256]{1,0:T(8,128)S(1)} %concatenate.16), channel_id=1, source_target_pairs={{0,1},{1,0},{2,3},{3,2},{4,5},{5,4},{6,7},{7,6},{8,9},{9,8},{10,11... | collective-permute-start | bytes 156680 | tf_op jit(solution)/shard_map/ppermute | solution.py:69
  63.0 11.1 %collective-permute-start.7 = (bf16[614,256]{1,0:T(8,128)(2,1)S(1)}, bf16[614,256]{1,0:T(8,128)(2,1)S(1)}, u32[]{:S(2)}, u32[]{:S(2)}) collective-permute-start(bf16[614,256]{1,0:T(8,128)(2,1)S(1)} %pad_maximum_fusion), channel_id=1, source_target_pairs={{0,2},{1,3},{2,0},{3,1},{4,6},{5,7},{6,4},{7,5},{8,10},{9,11},{10,... | collective-permute-start | bytes 943112 | tf_op jit(solution)/shard_map/ppermute | solution.py:77
  74.2 9.0 %copy-start.4 = (f32[4,131,256]{2,1,0:T(8,128)S(1)}, f32[4,131,256]{2,1,0:T(8,128)}, u32[]{:S(2)}) copy-start(f32[4,131,256]{2,1,0:T(8,128)} %get-tuple-element.86) | copy-start | bytes 1609732
  74.2 9.0 %copy-start.6 = (bf16[4,256,256]{2,1,0:T(8,128)(2,1)S(1)}, bf16[4,256,256]{2,1,0:T(8,128)(2,1)}, u32[]{:S(2)}) copy-start(bf16[4,256,256]{2,1,0:T(8,128)(2,1)} %param.15) | copy-start | bytes 1572868
  74.3 6.1 %collective-permute-start.8 = (bf16[358,256]{1,0:T(8,128)(2,1)S(1)}, bf16[358,256]{1,0:T(8,128)(2,1)S(1)}, u32[]{:S(2)}, u32[]{:S(2)}) collective-permute-start(bf16[358,256]{1,0:T(8,128)(2,1)S(1)} %pad_maximum_fusion.1), channel_id=1, source_target_pairs={{0,4},{1,5},{2,6},{3,7},{4,0},{5,1},{6,2},{7,3},{8,12},{9,13},{10,... | collective-permute-start | bytes 549896 | tf_op jit(solution)/shard_map/ppermute | solution.py:77
  80.6 7.2 %collective-permute-start.9 = (bf16[230,256]{1,0:T(8,128)(2,1)S(1)}, bf16[230,256]{1,0:T(8,128)(2,1)S(1)}, u32[]{:S(2)}, u32[]{:S(2)}) collective-permute-start(bf16[230,256]{1,0:T(8,128)(2,1)S(1)} %pad_maximum_fusion.2), channel_id=1, source_target_pairs={{0,8},{1,9},{2,10},{3,11},{4,12},{5,13},{6,14},{7,15},{8,0},{9,1},... | collective-permute-start | bytes 353288 | tf_op jit(solution)/shard_map/ppermute | solution.py:77
  (74 other events, 467.2 us)

commit v16 on v15

--- a/solution.py
+++ b/solution.py
@@ -203,20 +203,19 @@
         ((half_width, half_width), (2 * half_width, 2 * half_width), (0, 0)),
     )
     own = depthwise(tile_padded, flipped, image_rows, span)
-    tile_index = first_col // TILE_COLS
-    own_full = jnp.zeros((image_rows, image_cols, channels), jnp.float32)
-    for tile in range(image_cols // TILE_COLS):
-        left = tile * TILE_COLS - half_width
-        lo, hi = max(left, 0), min(left + span, image_cols)
-        placed = jnp.pad(own[:, lo - left : hi - left], ((0, 0), (lo, image_cols - hi), (0, 0)))
-        own_full = jnp.where(tile_index == tile, placed, own_full)
+    own_full = lax.dynamic_update_slice_in_dim(
+        jnp.zeros((image_rows, image_cols + 2 * half_width, channels), jnp.float32),
+        own,
+        first_col,
+        axis=1,
+    )[:, half_width : half_width + image_cols]
     grad_conv = lax.dynamic_update_slice_in_dim(
         jnp.zeros_like(image), grad_tile, first_col, axis=1
     )
     low, high = halo_rows(grad_conv, "row", half_width)
     edge = ((0, 0), (half_width, half_width), (0, 0))
-    low = jnp.pad(low, edge)
-    high = jnp.pad(high, edge)
+    low = jnp.pad(low.astype(jnp.float32), edge)
+    high = jnp.pad(high.astype(jnp.float32), edge)
     halo_out = []
     for out_row in range(image_rows):
         total = jnp.zeros((image_cols, channels), jnp.float32)

time: 90.2 us -> 83.3 us (0.924)
  local copies, waits for them, and re-layouts: 15.4 us -> 11.5 us
  starting transfers between devices: 23.6 us -> 21.6 us
  matrix products: 8.1 us -> 6.29 us
  other arithmetic: 23.4 us -> 24.9 us
    ppermute x1, starting transfers between devices: 8.71 us -> 3.3 us  [halo_rows(): lax.ppermute(lax.slice_in_dim(block, block.shape[0] - width, None, axis=0...]
    concatenate x1, local copies, waits for them, and re-layouts: 5.1 us -> 0.18 us  [shards(): jnp.concatenate([kernel_grad, gain_grad[None], scale_grad[None]], axis=0)]
    ppermute x3, starting transfers between devices: 2.27 us -> 6.11 us  [halving_reduce(): got_q, got_r, got_whole = lax.ppermute((give_q, give_r, whole), axis, pairs)]
    dynamic_update_slice x0 -> x1, local copies, waits for them, and re-layouts: none -> 3.29 us  [shards(): lax.dynamic_update_slice_in_dim(jnp.zeros((image_rows, image_cols + 2 * h...]
    convert_element_type x1 -> x2, other arithmetic: 0.06 us -> 2.11 us  [the longest x1 1.06 us: shards(): high = jnp.pad(high.astype(jnp.float32), edge)]
    reduce_sum x3, other arithmetic: 5.06 us -> 3.25 us  [kernel_terms(): jnp.sum(padded[row_tap:row_tap + image_rows, col_tap:col_tap + image_cols...]
    add x1, other arithmetic: 2.69 us -> 4.18 us  [depthwise(): total + padded[row_tap:row_tap + image_rows, col_tap:col_tap + image_cols...]
    dot_general x1, matrix products: 1.69 us -> 0.43 us  [shards(): lax.dot_general(act_flat, grad_flat, (((0,), (0,)), ((), ())), preferred_...]
  transfers between devices with their start and end apart: 10 -> 10, of which waited for: 4 -> 4; matrix products, arithmetic and copies ran while one was open for 25% -> 27% of each run, Pallas kernels for 0% -> 0%
where the time goes in v16:
time: 83.3 us; the launch traced here: 82.7 us
  other arithmetic  24.9 us (30%)
  starting transfers between devices  21.6 us (26%)
  waiting for transfers between devices  15.3 us (18%)
  local copies, waits for them, and re-layouts  11.5 us (14%)
  matrix products  6.29 us (8%)
  between operations  3.1 us (4%)
    ppermute x3, waiting for transfers between devices, halving_reduce(): got = lax.ppermute(sent, axis, pairs)  13.3 us
    ppermute x3, starting transfers between devices, halving_reduce(): got = lax.ppermute(sent, axis, pairs)  7.19 us
    ppermute x3, starting transfers between devices, halving_reduce(): got_q, got_r, got_whole = lax.ppermute((give_q, give_r, whole), axis, pairs)  6.11 us
    reduce_sum x1, other arithmetic, shards(): centre = jnp.mean(filtered, axis=-1, keepdims=True)  4.62 us
    add x1, other arithmetic, depthwise(): total + padded[row_tap:row_tap + image_rows, col_tap:col_tap + image_cols...  4.18 us
    add x4, other arithmetic, shards(): total + line[col_tap:col_tap + image_cols] * flipped[row_tap, col_tap]  4.02 us
    ppermute x1, starting transfers between devices, halo_rows(): lax.ppermute(lax.slice_in_dim(block, block.shape[0] - width, None, axis=0...  3.3 us
    dynamic_update_slice x1, local copies, waits for them, and re-layouts, shards(): lax.dynamic_update_slice_in_dim(jnp.zeros((image_rows, image_cols + 2 * h...  3.29 us
  transfers between devices with their start and end apart: 10, of which 4 were waited for; matrix products, arithmetic and copies ran while one was open for 27% of the time, Pallas kernels for 0%

profile of v16, /device:TPU:0, one launch (start us, length us, event | category | flops | bytes accessed | tf_op | source)
XLA Modules:
  0.0 82.7 jit_solution(10770511535818411278)
XLA Ops:
  0.7 1.1 %copy.39 = bf16[4,256,256]{2,1,0:T(8,128)(2,1)S(1)} copy(bf16[4,256,256]{2,1,0:T(8,128)(2,1)} %param.8) | data formatting | bytes 1048576
  1.8 2.4 %collective-permute-start = (bf16[3,256,256]{2,1,0:T(8,128)(2,1)S(1)}, bf16[3,256,256]{2,1,0:T(8,128)(2,1)S(1)}, u32[]{:S(2)}, u32[]{:S(2)}) collective-permute-start(bf16[3,256,256]{2,1,0:T(8,128)(2,1)S(1)} %get-tuple-element.90), channel_id=1, source_target_pairs={{0,1},{1,2},{2,3},{3,4},{4,5},{5,6},{6,7},{7,8},{8,9},{9,10},{10,1... | collective-permute-start | bytes 1179656 | tf_op jit(solution)/shard_map/ppermute | solution.py:21
  4.2 1.3 %collective-permute-start.1 = (bf16[3,256,256]{2,1,0:T(8,128)(2,1)S(1)}, bf16[3,256,256]{2,1,0:T(8,128)(2,1)S(1)}, u32[]{:S(2)}, u32[]{:S(2)}) collective-permute-start(bf16[3,256,256]{2,1,0:T(8,128)(2,1)S(1)} %get-tuple-element.89), channel_id=1, source_target_pairs={{1,0},{2,1},{3,2},{4,3},{5,4},{6,5},{7,6},{8,7},{9,8},{10,9},{11,1... | collective-permute-start | bytes 1179656 | tf_op jit(solution)/shard_map/ppermute | solution.py:24
  5.5 0.7 bitcast_reduce_fusion
  7.2 0.6 fusion.226
  7.9 2.0 %collective-permute-done.1 = bf16[3,256,256]{2,1,0:T(8,128)(2,1)S(1)} collective-permute-done((bf16[3,256,256]{2,1,0:T(8,128)(2,1)S(1)}, bf16[3,256,256]{2,1,0:T(8,128)(2,1)S(1)}, u32[]{:S(2)}, u32[]{:S(2)}) %collective-permute-start.1) | collective-permute-done | bytes 393248 | tf_op jit(solution)/shard_map/ppermute | solution.py:24
  9.9 0.3 fusion.23
  10.3 4.6 %fusion.219 = (f32[4,128]{1,0:T(4,128)S(1)}, f32[4,128,256]{2,1,0:T(8,128)S(1)}) fusion(f32[256]{0:T(256)S(1)} %bitcast.237, f32[10,134,256]{2,1,0:T(8,128)S(1)} %fusion.23, f32[256]{0:T(256)S(1)} %bitcast.242, f32[256]{0:T(256)S(1)} %bitcast.182, f32[256]{0:T(256)S(1)} %bitcast.187, f32[256]{0:T(256)S(1)} %bitcast.192, f32[256]{0:T(256)S(1)} %bitcast.197, ...), kind=kLoop, calls=%fused_computation.405 | loop fusion | flops 12844544 | bytes 26266624 | tf_op jit(solution)/shard_map/reduce_sum | solution.py:151
  15.3 0.2 multiply_reduce_fusion.3
  15.6 0.2 multiply_convert_fusion.3
  15.8 1.8 %fusion.11 = (bf16[1024,512]{0,1:T(8,128)(2,1)}, f32[512,1024]{1,0:T(8,128)S(1)}) fusion(bf16[512,256]{1,0:T(8,128)(2,1)S(1)} %bitcast.167, bf16[256,1024]{1,0:T(8,128)(2,1)S(1)} %copy-done), kind=kOutput, calls=%fused_computation.112 | convolution fusion | flops 273154048 | bytes 3932160 | tf_op jit(solution)/shard_map/dot_general | solution.py:161
  17.6 1.6 %fusion.124 = (f32[256]{0:T(256)S(1)}, bf16[4,128,256]{2,1,0:T(8,128)(2,1)S(1)}, f32[512,256]{1,0:T(8,128)}) fusion(bf16[4,256,256]{2,1,0:T(8,128)(2,1)S(1)} %copy-done.5, s32[]{:T(128)S(6)} %select_n.62, f32[256]{0:T(256)S(1)} %copy-done.88, bf16[1024,256]{1,0:T(8,128)(2,1)S(1)} %copy-done.7, f32[512,1024]{1,0:T(8,128)S(1)} %get-tuple-element.152), kind=kOutput, calls=%fused_computation.236 | convolution fusion | flops 273809152 | bytes 3672068 | tf_op jit(solution)/shard_map/dot_general | solution.py:163
  19.2 1.4 %fusion.6 = bf16[512,1024]{1,0:T(8,128)(2,1)S(1)} fusion(f32[512,1024]{1,0:T(8,128)S(1)} %get-tuple-element.152, bf16[512,256]{1,0:T(8,128)(2,1)S(1)} %bitcast.164, bf16[1024,256]{1,0:T(8,128)(2,1)S(1)} %copy-done.7), kind=kOutput, calls=%fused_computation.107 | convolution fusion | flops 278396928 | bytes 3932160 | tf_op jit(solution)/shard_map/dot_general | solution.py:164
  20.7 0.6 multiply_reduce_fusion.2
  21.3 0.3 multiply_reduce_fusion
  21.7 1.2 %fusion.171 = (f32[256]{0:T(256)S(1)}, f32[256]{0:T(256)S(1)}, f32[256]{0:T(256)S(1)}, f32[256]{0:T(256)S(1)}, f32[256]{0:T(256)S(1)}, /*index=5*/f32[256]{0:T(2...) fusion(f32[10,134,256]{2,1,0:T(8,128)S(1)} %fusion.23, ...), kind=kLoop, calls=%fused_computation.283 | loop fusion | flops 4584192 | bytes 8148992 | tf_op jit(solution)/shard_map/reduce_sum | solution.py:132
  22.9 1.0 %fusion.172 = (f32[256]{0:T(256)S(1)}, f32[256]{0:T(256)S(1)}, f32[256]{0:T(256)S(1)}, f32[256]{0:T(256)S(1)}, f32[256]{0:T(256)S(1)}, /*index=5*/f32[256]{0:T(2...) fusion(bf16[4,128,256]{2,1,0:T(8,128)(2,1)S(1)} %get-tuple-elem, ...), kind=kLoop, calls=%fused_computation.284 | loop fusion | flops 4845056 | bytes 9717760 | tf_op jit(solution)/shard_map/reduce_sum | solution.py:132
  23.9 1.0 %fusion.173 = (f32[256]{0:T(256)S(1)}, f32[256]{0:T(256)S(1)}, f32[256]{0:T(256)S(1)}, f32[256]{0:T(256)S(1)}, f32[256]{0:T(256)S(1)}, /*index=5*/f32[256]{0:T(2...) fusion(bf16[4,128,256]{2,1,0:T(8,128)(2,1)S(1)} %get-tuple-elem, ...), kind=kLoop, calls=%fused_computation.285 | loop fusion | flops 4845056 | bytes 9717760 | tf_op jit(solution)/shard_map/reduce_sum | solution.py:132
  25.3 6.0 %collective-permute-start.6 = (f32[51,256]{1,0:T(8,128)S(1)}, f32[51,256]{1,0:T(8,128)S(1)}, u32[]{:S(2)}, u32[]{:S(2)}) collective-permute-start(f32[51,256]{1,0:T(8,128)S(1)} %concatenate.16), channel_id=1, source_target_pairs={{0,1},{1,0},{2,3},{3,2},{4,5},{5,4},{6,7},{7,6},{8,9},{9,8},{10,11... | collective-permute-start | bytes 156680 | tf_op jit(solution)/shard_map/ppermute | solution.py:69
  31.3 1.5 %copy.25 = bf16[1024,512]{1,0:T(8,128)(2,1)S(1)} copy(bf16[1024,512]{0,1:T(8,128)(2,1)} %get-tuple-element.151) | data formatting | bytes 2097152 | tf_op jit(solution)/shard_map/convert_element_type | solution.py:162
  32.8 0.4 convolution_bitcast_fusion
  33.3 0.9 %constant_dynamic-slice_fusion = f32[512,256]{1,0:T(8,128)} fusion(f32[1024,256]{1,0:T(8,128)S(1)} %bitcast.158, s32[]{:T(128)S(6)} %select_n.67), kind=kLoop, calls=%fused_computation.393 | loop fusion | bytes 1048580 | tf_op jit(solution)/shard_map/dynamic_slice | solution.py:67
  34.2 0.4 copy-done.91
  34.7 0.4 fusion.15
  35.6 0.8 %constant_dynamic-slice_fusion.1 = f32[4,128,256]{2,1,0:T(8,128)} fusion(f32[4,256,256]{2,1,0:T(8,128)S(1)} %bitcast.160, s32[]{:T(128)S(6)} %select_n.65), kind=kLoop, calls=%fused_computation.394 | loop fusion | bytes 1048580 | tf_op jit(solution)/shard_map/dynamic_slice | solution.py:65
  36.6 0.9 %fusion.220 = (bf16[3,256,256]{2,1,0:T(8,128)(2,1)}, bf16[3,256,256]{2,1,0:T(8,128)(2,1)}) fusion(bf16[4,256,256]{2,1,0:T(8,128)(2,1)S(1)} %get-tuple-element.91), kind=kLoop, calls=%fused_computation.406 | loop fusion | bytes 1572864 | tf_op jit(solution)/shard_map/slice | solution.py:98
  37.6 3.3 %collective-permute-start.2 = (bf16[3,256,256]{2,1,0:T(8,128)(2,1)}, bf16[3,256,256]{2,1,0:T(8,128)(2,1)}, u32[]{:S(2)}, u32[]{:S(2)}) collective-permute-start(bf16[3,256,256]{2,1,0:T(8,128)(2,1)} %get-tuple-element.87), channel_id=1, source_target_pairs={{0,1},{1,2},{2,3},{3,4},{4,5},{5,6},{6,7},{7,8},{8,9},{9,10},{10,1... | collective-permute-start | bytes 1179656 | tf_op jit(solution)/shard_map/ppermute | solution.py:98
  40.9 1.3 %collective-permute-start.3 = (bf16[3,256,256]{2,1,0:T(8,128)(2,1)}, bf16[3,256,256]{2,1,0:T(8,128)(2,1)}, u32[]{:S(2)}, u32[]{:S(2)}) collective-permute-start(bf16[3,256,256]{2,1,0:T(8,128)(2,1)} %get-tuple-element.88), channel_id=1, source_target_pairs={{1,0},{2,1},{3,2},{4,3},{5,4},{6,5},{7,6},{8,7},{9,8},{10,9},{11,1... | collective-permute-start | bytes 1179656 | tf_op jit(solution)/shard_map/ppermute | solution.py:99
  42.5 4.2 %fusion.117 = f32[4,134,256]{2,1,0:T(8,128)} fusion(f32[4,128,256]{2,1,0:T(8,128)S(1)} %get-tuple-element.92, f32[256]{0:T(256)S(1)} %bitcast.178, f32[256]{0:T(256)S(1)} %bitcast.233, f32[256]{0:T(256)S(1)} %bitcast.208, f32[256]{0:T(256)S(1)} %bitcast.228, f32[256]{0:T(256)S(1)} %bitcast.223, f32[256]{0:T(256)S(1)} %bitcast.218, f32[256]{0:T(256)S(1)} %bitcast.213, ...), kind=kLoop, calls=%fused_computation.229 | loop fusion | flops 13309952 | bytes 1123328 | tf_op jit(solution)/shard_map/add | solution.py:120
  46.9 3.3 %dynamic_update_slice.10 = f32[4,262,256]{2,1,0:T(8,128)S(1)} dynamic-update-slice(f32[4,262,256]{2,1,0:T(8,128)S(1)} %broadcast_in_dim.10, f32[4,134,256]{2,1,0:T(8,128)} %fusion.117, s32[]{:T(128)} %constant.23.clone.1, s32[]{:T(128)S(6)} %select_n.63, s32[]{:T(128)} %constant.23.clone.1) | dynamic-update-slice | bytes 1097732 | tf_op jit(solution)/shard_map/dynamic_update_slice | solution.py:206
  50.2 1.1 %convert_element_type.166 = f32[3,256,256]{2,1,0:T(8,128)S(1)} convert(bf16[3,256,256]{2,1,0:T(8,128)(2,1)} %collective-permute-done.2) | non-fusion elementwise | flops 196608 | bytes 1179648 | tf_op jit(solution)/shard_map/convert_element_type | solution.py:217
  51.3 1.1 %convert_element_type.167 = f32[3,256,256]{2,1,0:T(8,128)S(1)} convert(bf16[3,256,256]{2,1,0:T(8,128)(2,1)} %collective-permute-done.3) | non-fusion elementwise | flops 196608 | bytes 1179648 | tf_op jit(solution)/shard_map/convert_element_type | solution.py:218
  52.4 0.7 multiply_add_fusion.4
  53.1 1.1 %dynamic-slice_add_fusion = f32[512,256]{1,0:T(8,128)S(1)} fusion(f32[512,256]{1,0:T(8,128)} %collective-permute-done.5, f32[1024,256]{1,0:T(8,128)S(1)} %bitcast.159, s32[]{:T(128)S(6)} %select_n.66), kind=kLoop, calls=%fused_computation.287 | loop fusion | flops 131072 | bytes 1572868 | tf_op jit(solution)/shard_map/add | solution.py:89
  54.2 1.1 %dynamic-slice_add_fusion.1 = f32[4,128,256]{2,1,0:T(8,128)S(1)} fusion(f32[4,128,256]{2,1,0:T(8,128)} %collective-permute-done.4, f32[4,256,256]{2,1,0:T(8,128)S(1)} %bitcast.161, s32[]{:T(128)S(6)} %select_n.64), kind=kLoop, calls=%fused_computation.288 | loop fusion | flops 131072 | bytes 1572868 | tf_op jit(solution)/shard_map/add | solution.py:88
  55.4 3.5 %collective-permute-start.7 = (bf16[614,256]{1,0:T(8,128)(2,1)S(1)}, bf16[614,256]{1,0:T(8,128)(2,1)S(1)}, u32[]{:S(2)}, u32[]{:S(2)}) collective-permute-start(bf16[614,256]{1,0:T(8,128)(2,1)S(1)} %pad_maximum_fusion), channel_id=1, source_target_pairs={{0,2},{1,3},{2,0},{3,1},{4,6},{5,7},{6,4},{7,5},{8,10},{9,11},{10,... | collective-permute-start | bytes 943112 | tf_op jit(solution)/shard_map/ppermute | solution.py:77
  58.9 1.3 %fusion.197 = f32[1,256,256]{2,1,0:T(8,128)S(1)} fusion(f32[3,256,256]{2,1,0:T(8,128)S(1)} %convert_element_type.166, f32[256]{0:T(256)} %bitcast.29, f32[256]{0:T(256)S(1)} %bitcast.320, f32[256]{0:T(256)S(1)} %bitcast.317, f32[256]{0:T(256)S(1)} %bitcast.314, f32[256]{0:T(256)S(1)} %bitcast.311, f32[256]{0:T(256)S(1)} %bitcast.308, f32[256]{0:T(256)S(1)} %bitcast.305, ...), kind=kLoop, calls=%fused_computation.323 | loop fusion | flops 2686976 | bytes 1856512 | tf_op jit(solution)/shard_map/add | solution.py:231
  60.3 0.7 multiply_add_fusion.3
  60.9 6.0 %collective-permute-done.7 = bf16[614,256]{1,0:T(8,128)(2,1)S(1)} collective-permute-done((bf16[614,256]{1,0:T(8,128)(2,1)S(1)}, bf16[614,256]{1,0:T(8,128)(2,1)S(1)}, u32[]{:S(2)}, u32[]{:S(2)}) %collective-permute-start.7) | collective-permute-done | bytes 314400 | tf_op jit(solution)/shard_map/ppermute | solution.py:77
  67.1 1.8 %collective-permute-start.8 = (bf16[358,256]{1,0:T(8,128)(2,1)S(1)}, bf16[358,256]{1,0:T(8,128)(2,1)S(1)}, u32[]{:S(2)}, u32[]{:S(2)}) collective-permute-start(bf16[358,256]{1,0:T(8,128)(2,1)S(1)} %pad_maximum_fusion.1), channel_id=1, source_target_pairs={{0,4},{1,5},{2,6},{3,7},{4,0},{5,1},{6,2},{7,3},{8,12},{9,13},{10,... | collective-permute-start | bytes 549896 | tf_op jit(solution)/shard_map/ppermute | solution.py:77
  69.0 1.3 %fusion.179 = f32[1,256,256]{2,1,0:T(8,128)S(1)} fusion(f32[3,256,256]{2,1,0:T(8,128)S(1)} %convert_element_type.167, f32[256]{0:T(256)} %bitcast.15, f32[256]{0:T(256)} %bitcast.16, f32[256]{0:T(256)S(1)} %bitcast.335, f32[256]{0:T(256)S(1)} %bitcast.332, f32[256]{0:T(256)S(1)} %bitcast.329, f32[256]{0:T(256)S(1)} %bitcast.326, f32[256]{0:T(256)S(1)} %bitcast.323, ...), kind=kLoop, calls=%fused_computation.304 | loop fusion | flops 2686976 | bytes 1856512 | tf_op jit(solution)/shard_map/add | solution.py:231
  70.3 3.2 %collective-permute-done.8 = bf16[358,256]{1,0:T(8,128)(2,1)S(1)} collective-permute-done((bf16[358,256]{1,0:T(8,128)(2,1)S(1)}, bf16[358,256]{1,0:T(8,128)(2,1)S(1)}, u32[]{:S(2)}, u32[]{:S(2)}) %collective-permute-start.8) | collective-permute-done | bytes 183328 | tf_op jit(solution)/shard_map/ppermute | solution.py:77
  73.7 1.9 %collective-permute-start.9 = (bf16[230,256]{1,0:T(8,128)(2,1)S(1)}, bf16[230,256]{1,0:T(8,128)(2,1)S(1)}, u32[]{:S(2)}, u32[]{:S(2)}) collective-permute-start(bf16[230,256]{1,0:T(8,128)(2,1)S(1)} %pad_maximum_fusion.2), channel_id=1, source_target_pairs={{0,8},{1,9},{2,10},{3,11},{4,12},{5,13},{6,14},{7,15},{8,0},{9,1},... | collective-permute-start | bytes 353288 | tf_op jit(solution)/shard_map/ppermute | solution.py:77
  75.6 1.1 %fusion.18 = bf16[4,256,256]{2,1,0:T(8,128)(2,1)} fusion(f32[4,262,256]{2,1,0:T(8,128)S(1)} %dynamic_update_slice.10, f32[1,256,256]{2,1,0:T(8,128)S(1)} %fusion.179, f32[1,256,256]{2,1,0:T(8,128)S(1)} %multiply_add_fusion.3, f32[1,256,256]{2,1,0:T(8,128)S(1)} %multiply_add_fusion.4, f32[1,256,256]{2,1,0:T(8,128)S(1)} %fusion.197, ...), kind=kLoop, calls=%fused_computation.128 | loop fusion | flops 1835008 | bytes 3145728 | tf_op jit(solution)/shard_map/convert_element_type | solution.py:234
  76.6 4.1 %collective-permute-done.9 = bf16[230,256]{1,0:T(8,128)(2,1)S(1)} collective-permute-done((bf16[230,256]{1,0:T(8,128)(2,1)S(1)}, bf16[230,256]{1,0:T(8,128)(2,1)S(1)}, u32[]{:S(2)}, u32[]{:S(2)}) %collective-permute-start.9) | collective-permute-done | bytes 117792 | tf_op jit(solution)/shard_map/ppermute | solution.py:77
  80.8 0.6 fusion.214
  81.4 0.6 convert_add_fusion.8
  82.1 0.6 copy.30
  (229 shorter events, 1.8 us)
Async XLA Ops:
  0.6 15.1 %copy-start = (bf16[256,1024]{1,0:T(8,128)(2,1)S(1)}, bf16[256,1024]{1,0:T(8,128)(2,1)}, u32[]{:S(2)}) copy-start(bf16[256,1024]{1,0:T(8,128)(2,1)} %param.12) | copy-start | bytes 1572868
  1.8 6.1 %collective-permute-start = (bf16[3,256,256]{2,1,0:T(8,128)(2,1)S(1)}, bf16[3,256,256]{2,1,0:T(8,128)(2,1)S(1)}, u32[]{:S(2)}, u32[]{:S(2)}) collective-permute-start(bf16[3,256,256]{2,1,0:T(8,128)(2,1)S(1)} %get-tuple-element.90), channel_id=1, source_target_pairs={{0,1},{1,2},{2,3},{3,4},{4,5},{5,6},{6,7},{7,8},{8,9},{9,10},{10,1... | collective-permute-start | bytes 1179656 | tf_op jit(solution)/shard_map/ppermute | solution.py:21
  4.2 5.7 %collective-permute-start.1 = (bf16[3,256,256]{2,1,0:T(8,128)(2,1)S(1)}, bf16[3,256,256]{2,1,0:T(8,128)(2,1)S(1)}, u32[]{:S(2)}, u32[]{:S(2)}) collective-permute-start(bf16[3,256,256]{2,1,0:T(8,128)(2,1)S(1)} %get-tuple-element.89), channel_id=1, source_target_pairs={{1,0},{2,1},{3,2},{4,3},{5,4},{6,5},{7,6},{8,7},{9,8},{10,9},{11,1... | collective-permute-start | bytes 1179656 | tf_op jit(solution)/shard_map/ppermute | solution.py:24
  6.9 8.0 %copy-start.9 = (f32[1,1,256]{2,1,0:T(1,128)}, f32[1,1,256]{2,1,0:T(1,128)S(1)}, u32[]{:S(2)}) copy-start(f32[1,1,256]{2,1,0:T(1,128)S(1)} %get-tuple-element.99) | copy-start | bytes 3076
  6.9 8.0 %copy-start.11 = (f32[1,1,256]{2,1,0:T(1,128)}, f32[1,1,256]{2,1,0:T(1,128)S(1)}, u32[]{:S(2)}) copy-start(f32[1,1,256]{2,1,0:T(1,128)S(1)} %get-tuple-element.100) | copy-start | bytes 3076
  6.9 8.0 %copy-start.13 = (f32[1,1,256]{2,1,0:T(1,128)}, f32[1,1,256]{2,1,0:T(1,128)S(1)}, u32[]{:S(2)}) copy-start(f32[1,1,256]{2,1,0:T(1,128)S(1)} %get-tuple-element.101) | copy-start | bytes 3076
  6.9 8.0 %copy-start.15 = (f32[1,1,256]{2,1,0:T(1,128)}, f32[1,1,256]{2,1,0:T(1,128)S(1)}, u32[]{:S(2)}) copy-start(f32[1,1,256]{2,1,0:T(1,128)S(1)} %get-tuple-element.102) | copy-start | bytes 3076
  6.9 8.0 %copy-start.17 = (f32[1,1,256]{2,1,0:T(1,128)}, f32[1,1,256]{2,1,0:T(1,128)S(1)}, u32[]{:S(2)}) copy-start(f32[1,1,256]{2,1,0:T(1,128)S(1)} %get-tuple-element.103) | copy-start | bytes 3076
  6.9 8.0 %copy-start.19 = (f32[1,1,256]{2,1,0:T(1,128)}, f32[1,1,256]{2,1,0:T(1,128)S(1)}, u32[]{:S(2)}) copy-start(f32[1,1,256]{2,1,0:T(1,128)S(1)} %get-tuple-element.104) | copy-start | bytes 3076
  6.9 8.0 %copy-start.37 = (f32[1,1,256]{2,1,0:T(1,128)}, f32[1,1,256]{2,1,0:T(1,128)S(1)}, u32[]{:S(2)}) copy-start(f32[1,1,256]{2,1,0:T(1,128)S(1)} %get-tuple-element.105) | copy-start | bytes 3076
  7.0 8.0 %copy-start.39 = (f32[1,1,256]{2,1,0:T(1,128)}, f32[1,1,256]{2,1,0:T(1,128)S(1)}, u32[]{:S(2)}) copy-start(f32[1,1,256]{2,1,0:T(1,128)S(1)} %get-tuple-element.106) | copy-start | bytes 3076
  7.0 8.0 %copy-start.41 = (f32[1,1,256]{2,1,0:T(1,128)}, f32[1,1,256]{2,1,0:T(1,128)S(1)}, u32[]{:S(2)}) copy-start(f32[1,1,256]{2,1,0:T(1,128)S(1)} %get-tuple-element.107) | copy-start | bytes 3076
  7.0 8.0 %copy-start.43 = (f32[1,1,256]{2,1,0:T(1,128)}, f32[1,1,256]{2,1,0:T(1,128)S(1)}, u32[]{:S(2)}) copy-start(f32[1,1,256]{2,1,0:T(1,128)S(1)} %get-tuple-element.108) | copy-start | bytes 3076
  7.0 8.0 %copy-start.45 = (f32[1,1,256]{2,1,0:T(1,128)}, f32[1,1,256]{2,1,0:T(1,128)S(1)}, u32[]{:S(2)}) copy-start(f32[1,1,256]{2,1,0:T(1,128)S(1)} %get-tuple-element.109) | copy-start | bytes 3076
  7.0 8.0 %copy-start.47 = (f32[1,1,256]{2,1,0:T(1,128)}, f32[1,1,256]{2,1,0:T(1,128)S(1)}, u32[]{:S(2)}) copy-start(f32[1,1,256]{2,1,0:T(1,128)S(1)} %get-tuple-element.110) | copy-start | bytes 3076
  7.0 8.0 %copy-start.49 = (f32[1,1,256]{2,1,0:T(1,128)}, f32[1,1,256]{2,1,0:T(1,128)S(1)}, u32[]{:S(2)}) copy-start(f32[1,1,256]{2,1,0:T(1,128)S(1)} %get-tuple-element.111) | copy-start | bytes 3076
  7.0 8.0 %copy-start.65 = (f32[1,1,256]{2,1,0:T(1,128)}, f32[1,1,256]{2,1,0:T(1,128)S(1)}, u32[]{:S(2)}) copy-start(f32[1,1,256]{2,1,0:T(1,128)S(1)} %get-tuple-element.112) | copy-start | bytes 3076
  7.0 8.0 %copy-start.67 = (f32[1,1,256]{2,1,0:T(1,128)}, f32[1,1,256]{2,1,0:T(1,128)S(1)}, u32[]{:S(2)}) copy-start(f32[1,1,256]{2,1,0:T(1,128)S(1)} %get-tuple-element.113) | copy-start | bytes 3076
  7.0 8.0 %copy-start.69 = (f32[1,1,256]{2,1,0:T(1,128)}, f32[1,1,256]{2,1,0:T(1,128)S(1)}, u32[]{:S(2)}) copy-start(f32[1,1,256]{2,1,0:T(1,128)S(1)} %get-tuple-element.114) | copy-start | bytes 3076
  7.0 8.0 %copy-start.71 = (f32[1,1,256]{2,1,0:T(1,128)}, f32[1,1,256]{2,1,0:T(1,128)S(1)}, u32[]{:S(2)}) copy-start(f32[1,1,256]{2,1,0:T(1,128)S(1)} %get-tuple-element.115) | copy-start | bytes 3076
  7.1 8.0 %copy-start.73 = (f32[1,1,256]{2,1,0:T(1,128)}, f32[1,1,256]{2,1,0:T(1,128)S(1)}, u32[]{:S(2)}) copy-start(f32[1,1,256]{2,1,0:T(1,128)S(1)} %get-tuple-element.116) | copy-start | bytes 3076
  7.1 8.0 %copy-start.75 = (f32[1,1,256]{2,1,0:T(1,128)}, f32[1,1,256]{2,1,0:T(1,128)S(1)}, u32[]{:S(2)}) copy-start(f32[1,1,256]{2,1,0:T(1,128)S(1)} %get-tuple-element.117) | copy-start | bytes 3076
  7.1 8.0 %copy-start.21 = (f32[1,1,256]{2,1,0:T(1,128)}, f32[1,1,256]{2,1,0:T(1,128)S(1)}, u32[]{:S(2)}) copy-start(f32[1,1,256]{2,1,0:T(1,128)S(1)} %get-tuple-element.137) | copy-start | bytes 3076
  7.1 8.0 %copy-start.23 = (f32[1,1,256]{2,1,0:T(1,128)}, f32[1,1,256]{2,1,0:T(1,128)S(1)}, u32[]{:S(2)}) copy-start(f32[1,1,256]{2,1,0:T(1,128)S(1)} %get-tuple-element.142) | copy-start | bytes 3076
  7.1 8.0 %copy-start.25 = (f32[1,1,256]{2,1,0:T(1,128)}, f32[1,1,256]{2,1,0:T(1,128)S(1)}, u32[]{:S(2)}) copy-start(f32[1,1,256]{2,1,0:T(1,128)S(1)} %get-tuple-element.143) | copy-start | bytes 3076
  7.1 8.0 %copy-start.27 = (f32[1,1,256]{2,1,0:T(1,128)}, f32[1,1,256]{2,1,0:T(1,128)S(1)}, u32[]{:S(2)}) copy-start(f32[1,1,256]{2,1,0:T(1,128)S(1)} %get-tuple-element.144) | copy-start | bytes 3076
  7.1 8.0 %copy-start.29 = (f32[1,1,256]{2,1,0:T(1,128)}, f32[1,1,256]{2,1,0:T(1,128)S(1)}, u32[]{:S(2)}) copy-start(f32[1,1,256]{2,1,0:T(1,128)S(1)} %get-tuple-element.145) | copy-start | bytes 3076
  7.2 8.0 %copy-start.33 = (f32[1,1,256]{2,1,0:T(1,128)}, f32[1,1,256]{2,1,0:T(1,128)S(1)}, u32[]{:S(2)}) copy-start(f32[1,1,256]{2,1,0:T(1,128)S(1)} %get-tuple-element.146) | copy-start | bytes 3076
  7.2 8.0 %copy-start.35 = (f32[1,1,256]{2,1,0:T(1,128)}, f32[1,1,256]{2,1,0:T(1,128)S(1)}, u32[]{:S(2)}) copy-start(f32[1,1,256]{2,1,0:T(1,128)S(1)} %get-tuple-element.147) | copy-start | bytes 3076
  7.2 8.0 %copy-start.51 = (f32[1,1,256]{2,1,0:T(1,128)}, f32[1,1,256]{2,1,0:T(1,128)S(1)}, u32[]{:S(2)}) copy-start(f32[1,1,256]{2,1,0:T(1,128)S(1)} %get-tuple-element.138) | copy-start | bytes 3076
  7.2 8.0 %copy-start.53 = (f32[1,1,256]{2,1,0:T(1,128)}, f32[1,1,256]{2,1,0:T(1,128)S(1)}, u32[]{:S(2)}) copy-start(f32[1,1,256]{2,1,0:T(1,128)S(1)} %get-tuple-element.139) | copy-start | bytes 3076
  7.2 8.0 %copy-start.55 = (f32[1,1,256]{2,1,0:T(1,128)}, f32[1,1,256]{2,1,0:T(1,128)S(1)}, u32[]{:S(2)}) copy-start(f32[1,1,256]{2,1,0:T(1,128)S(1)} %get-tuple-element.140) | copy-start | bytes 3076
  7.2 8.0 %copy-start.57 = (f32[1,1,256]{2,1,0:T(1,128)}, f32[1,1,256]{2,1,0:T(1,128)S(1)}, u32[]{:S(2)}) copy-start(f32[1,1,256]{2,1,0:T(1,128)S(1)} %get-tuple-element.141) | copy-start | bytes 3076
  7.9 7.4 %copy-start.63 = (f32[1,1,256]{2,1,0:T(1,128)}, f32[1,1,256]{2,1,0:T(1,128)S(1)}, u32[]{:S(2)}) copy-start(f32[1,1,256]{2,1,0:T(1,128)S(1)} %get-tuple-element.136) | copy-start | bytes 3076
  7.9 7.4 %copy-start.77 = (f32[1,1,256]{2,1,0:T(1,128)}, f32[1,1,256]{2,1,0:T(1,128)S(1)}, u32[]{:S(2)}) copy-start(f32[1,1,256]{2,1,0:T(1,128)S(1)} %get-tuple-element.127) | copy-start | bytes 3076
  7.9 7.4 %copy-start.79 = (f32[1,1,256]{2,1,0:T(1,128)}, f32[1,1,256]{2,1,0:T(1,128)S(1)}, u32[]{:S(2)}) copy-start(f32[1,1,256]{2,1,0:T(1,128)S(1)} %get-tuple-element.128) | copy-start | bytes 3076
  7.9 7.4 %copy-start.81 = (f32[1,1,256]{2,1,0:T(1,128)}, f32[1,1,256]{2,1,0:T(1,128)S(1)}, u32[]{:S(2)}) copy-start(f32[1,1,256]{2,1,0:T(1,128)S(1)} %get-tuple-element.129) | copy-start | bytes 3076
  7.9 7.4 %copy-start.83 = (f32[1,1,256]{2,1,0:T(1,128)}, f32[1,1,256]{2,1,0:T(1,128)S(1)}, u32[]{:S(2)}) copy-start(f32[1,1,256]{2,1,0:T(1,128)S(1)} %get-tuple-element.130) | copy-start | bytes 3076
  25.3 24.9 %collective-permute-start.6 = (f32[51,256]{1,0:T(8,128)S(1)}, f32[51,256]{1,0:T(8,128)S(1)}, u32[]{:S(2)}, u32[]{:S(2)}) collective-permute-start(f32[51,256]{1,0:T(8,128)S(1)} %concatenate.16), channel_id=1, source_target_pairs={{0,1},{1,0},{2,3},{3,2},{4,5},{5,4},{6,7},{7,6},{8,9},{9,8},{10,11... | collective-permute-start | bytes 156680 | tf_op jit(solution)/shard_map/ppermute | solution.py:69
  34.2 18.9 %collective-permute-start.5 = (f32[512,256]{1,0:T(8,128)}, f32[512,256]{1,0:T(8,128)}, u32[]{:S(2)}, u32[]{:S(2)}) collective-permute-start(f32[512,256]{1,0:T(8,128)} %constant_dynamic-slice_fusion), channel_id=1, source_target_pairs={{0,1},{1,0},{2,3},{3,2},{4,5},{5,4},{6,7},{7,6},{8,9},{9,8},{10,11... | collective-permute-start | bytes 1572872 | tf_op jit(solution)/shard_map/ppermute | solution.py:69
  36.4 10.3 %copy-start.4 = (f32[512,256]{1,0:T(8,128)S(1)}, f32[512,256]{1,0:T(8,128)}, u32[]{:S(2)}) copy-start(f32[512,256]{1,0:T(8,128)} %get-tuple-element.148) | copy-start | bytes 1572868
  36.4 17.8 %collective-permute-start.4 = (f32[4,128,256]{2,1,0:T(8,128)}, f32[4,128,256]{2,1,0:T(8,128)}, u32[]{:S(2)}, u32[]{:S(2)}) collective-permute-start(f32[4,128,256]{2,1,0:T(8,128)} %constant_dynamic-slice_fusion.1), channel_id=1, source_target_pairs={{0,1},{1,0},{2,3},{3,2},{4,5},{5,4},{6,7},{7,6},{8,9},{9,8},{10,11... | collective-permute-start | bytes 1572872 | tf_op jit(solution)/shard_map/ppermute | solution.py:69
  37.6 12.7 %collective-permute-start.2 = (bf16[3,256,256]{2,1,0:T(8,128)(2,1)}, bf16[3,256,256]{2,1,0:T(8,128)(2,1)}, u32[]{:S(2)}, u32[]{:S(2)}) collective-permute-start(bf16[3,256,256]{2,1,0:T(8,128)(2,1)} %get-tuple-element.87), channel_id=1, source_target_pairs={{0,1},{1,2},{2,3},{3,4},{4,5},{5,6},{6,7},{7,8},{8,9},{9,10},{10,1... | collective-permute-start | bytes 1179656 | tf_op jit(solution)/shard_map/ppermute | solution.py:98
  40.9 10.4 %collective-permute-start.3 = (bf16[3,256,256]{2,1,0:T(8,128)(2,1)}, bf16[3,256,256]{2,1,0:T(8,128)(2,1)}, u32[]{:S(2)}, u32[]{:S(2)}) collective-permute-start(bf16[3,256,256]{2,1,0:T(8,128)(2,1)} %get-tuple-element.88), channel_id=1, source_target_pairs={{1,0},{2,1},{3,2},{4,3},{5,4},{6,5},{7,6},{8,7},{9,8},{10,9},{11,1... | collective-permute-start | bytes 1179656 | tf_op jit(solution)/shard_map/ppermute | solution.py:99
  55.4 11.5 %collective-permute-start.7 = (bf16[614,256]{1,0:T(8,128)(2,1)S(1)}, bf16[614,256]{1,0:T(8,128)(2,1)S(1)}, u32[]{:S(2)}, u32[]{:S(2)}) collective-permute-start(bf16[614,256]{1,0:T(8,128)(2,1)S(1)} %pad_maximum_fusion), channel_id=1, source_target_pairs={{0,2},{1,3},{2,0},{3,1},{4,6},{5,7},{6,4},{7,5},{8,10},{9,11},{10,... | collective-permute-start | bytes 943112 | tf_op jit(solution)/shard_map/ppermute | solution.py:77
  67.0 8.5 %copy-start.6 = (bf16[4,256,256]{2,1,0:T(8,128)(2,1)S(1)}, bf16[4,256,256]{2,1,0:T(8,128)(2,1)}, u32[]{:S(2)}) copy-start(bf16[4,256,256]{2,1,0:T(8,128)(2,1)} %param.15) | copy-start | bytes 1572868
  67.1 6.4 %collective-permute-start.8 = (bf16[358,256]{1,0:T(8,128)(2,1)S(1)}, bf16[358,256]{1,0:T(8,128)(2,1)S(1)}, u32[]{:S(2)}, u32[]{:S(2)}) collective-permute-start(bf16[358,256]{1,0:T(8,128)(2,1)S(1)} %pad_maximum_fusion.1), channel_id=1, source_target_pairs={{0,4},{1,5},{2,6},{3,7},{4,0},{5,1},{6,2},{7,3},{8,12},{9,13},{10,... | collective-permute-start | bytes 549896 | tf_op jit(solution)/shard_map/ppermute | solution.py:77
  73.7 7.1 %collective-permute-start.9 = (bf16[230,256]{1,0:T(8,128)(2,1)S(1)}, bf16[230,256]{1,0:T(8,128)(2,1)S(1)}, u32[]{:S(2)}, u32[]{:S(2)}) collective-permute-start(bf16[230,256]{1,0:T(8,128)(2,1)S(1)} %pad_maximum_fusion.2), channel_id=1, source_target_pairs={{0,8},{1,9},{2,10},{3,11},{4,12},{5,13},{6,14},{7,15},{8,0},{9,1},... | collective-permute-start | bytes 353288 | tf_op jit(solution)/shard_map/ppermute | solution.py:77
  (54 other events, 334.5 us)

commit v17 on v16

--- a/solution.py
+++ b/solution.py
@@ -214,8 +214,8 @@
     )
     low, high = halo_rows(grad_conv, "row", half_width)
     edge = ((0, 0), (half_width, half_width), (0, 0))
-    low = jnp.pad(low.astype(jnp.float32), edge)
-    high = jnp.pad(high.astype(jnp.float32), edge)
+    low = jnp.pad(low, edge)
+    high = jnp.pad(high, edge)
     halo_out = []
     for out_row in range(image_rows):
         total = jnp.zeros((image_cols, channels), jnp.float32)

time: 83.3 us -> 84.6 us (1.016)
  starting transfers between devices: 21.6 us -> 24.5 us
  other arithmetic: 24.9 us -> 23.2 us
  local copies, waits for them, and re-layouts: 11.5 us -> 10.2 us
  waiting for transfers between devices: 15.3 us -> 16.4 us
    ppermute x3, starting transfers between devices: 7.19 us -> 10.9 us  [halving_reduce(): got = lax.ppermute(sent, axis, pairs)]
    convert_element_type x2 -> x0, other arithmetic: 2.11 us -> none  [the longest x1 1.06 us: shards(): high = jnp.pad(high.astype(jnp.float32), edge)]
    dynamic_update_slice x1, local copies, waits for them, and re-layouts: 3.29 us -> 1.4 us  [shards(): lax.dynamic_update_slice_in_dim(jnp.zeros((image_rows, image_cols + 2 * h...]
    ppermute x1, starting transfers between devices: 3.3 us -> 1.94 us  [halo_rows(): lax.ppermute(lax.slice_in_dim(block, block.shape[0] - width, None, axis=0...]
    ppermute x3, waiting for transfers between devices: 13.3 us -> 14.3 us  [halving_reduce(): got = lax.ppermute(sent, axis, pairs)]
    add x1, other arithmetic: 0.01 us -> 0.91 us  [halving_reduce(): whole = whole + got_whole]
    unnamed x185 -> x259, local copies, waits for them, and re-layouts: 2.01 us -> 2.64 us
  transfers between devices with their start and end apart: 10 -> 10, of which waited for: 4 -> 4; matrix products, arithmetic and copies ran while one was open for 27% -> 22% of each run, Pallas kernels for 0% -> 0%
where the time goes in v17:
time: 84.6 us; the launch traced here: 84.2 us
  starting transfers between devices  24.5 us (29%)
  other arithmetic  23.2 us (27%)
  waiting for transfers between devices  16.4 us (19%)
  local copies, waits for them, and re-layouts  10.2 us (12%)
  matrix products  6.29 us (7%)
  between operations  3.62 us (4%)
    ppermute x3, waiting for transfers between devices, halving_reduce(): got = lax.ppermute(sent, axis, pairs)  14.3 us
    ppermute x3, starting transfers between devices, halving_reduce(): got = lax.ppermute(sent, axis, pairs)  10.9 us
    ppermute x3, starting transfers between devices, halving_reduce(): got_q, got_r, got_whole = lax.ppermute((give_q, give_r, whole), axis, pairs)  6.54 us
    reduce_sum x1, other arithmetic, shards(): centre = jnp.mean(filtered, axis=-1, keepdims=True)  4.58 us
    add x4, other arithmetic, shards(): total + line[col_tap:col_tap + image_cols] * flipped[row_tap, col_tap]  3.52 us
    add x1, other arithmetic, depthwise(): total + padded[row_tap:row_tap + image_rows, col_tap:col_tap + image_cols...  3.4 us
    reduce_sum x3, other arithmetic, kernel_terms(): jnp.sum(padded[row_tap:row_tap + image_rows, col_tap:col_tap + image_cols...  3.27 us
    unnamed x259, local copies, waits for them, and re-layouts  2.64 us
  transfers between devices with their start and end apart: 10, of which 4 were waited for; matrix products, arithmetic and copies ran while one was open for 22% of the time, Pallas kernels for 0%

profile of v17, /device:TPU:0, one launch (start us, length us, event | category | flops | bytes accessed | tf_op | source)
XLA Modules:
  0.0 84.2 jit_solution(9328064991352379278)
XLA Ops:
  0.7 1.1 %copy.39 = bf16[4,256,256]{2,1,0:T(8,128)(2,1)S(1)} copy(bf16[4,256,256]{2,1,0:T(8,128)(2,1)} %param.8) | data formatting | bytes 1048576
  1.8 2.4 %collective-permute-start = (bf16[3,256,256]{2,1,0:T(8,128)(2,1)S(1)}, bf16[3,256,256]{2,1,0:T(8,128)(2,1)S(1)}, u32[]{:S(2)}, u32[]{:S(2)}) collective-permute-start(bf16[3,256,256]{2,1,0:T(8,128)(2,1)S(1)} %get-tuple-element.90), channel_id=1, source_target_pairs={{0,1},{1,2},{2,3},{3,4},{4,5},{5,6},{6,7},{7,8},{8,9},{9,10},{10,1... | collective-permute-start | bytes 1179656 | tf_op jit(solution)/shard_map/ppermute | solution.py:21
  4.2 1.3 %collective-permute-start.1 = (bf16[3,256,256]{2,1,0:T(8,128)(2,1)S(1)}, bf16[3,256,256]{2,1,0:T(8,128)(2,1)S(1)}, u32[]{:S(2)}, u32[]{:S(2)}) collective-permute-start(bf16[3,256,256]{2,1,0:T(8,128)(2,1)S(1)} %get-tuple-element.89), channel_id=1, source_target_pairs={{1,0},{2,1},{3,2},{4,3},{5,4},{6,5},{7,6},{8,7},{9,8},{10,9},{11,1... | collective-permute-start | bytes 1179656 | tf_op jit(solution)/shard_map/ppermute | solution.py:24
  5.5 0.7 bitcast_reduce_fusion
  7.2 0.6 fusion.267
  7.9 2.0 %collective-permute-done.1 = bf16[3,256,256]{2,1,0:T(8,128)(2,1)S(1)} collective-permute-done((bf16[3,256,256]{2,1,0:T(8,128)(2,1)S(1)}, bf16[3,256,256]{2,1,0:T(8,128)(2,1)S(1)}, u32[]{:S(2)}, u32[]{:S(2)}) %collective-permute-start.1) | collective-permute-done | bytes 393248 | tf_op jit(solution)/shard_map/ppermute | solution.py:24
  9.9 0.3 fusion.23
  10.3 4.6 %fusion.260 = (f32[4,128]{1,0:T(4,128)S(1)}, f32[4,128,256]{2,1,0:T(8,128)S(1)}) fusion(f32[256]{0:T(256)S(1)} %bitcast.237, f32[10,134,256]{2,1,0:T(8,128)S(1)} %fusion.23, f32[256]{0:T(256)S(1)} %bitcast.242, f32[256]{0:T(256)S(1)} %bitcast.182, f32[256]{0:T(256)S(1)} %bitcast.187, f32[256]{0:T(256)S(1)} %bitcast.192, f32[256]{0:T(256)S(1)} %bitcast.197, ...), kind=kLoop, calls=%fused_computation.494 | loop fusion | flops 12844544 | bytes 26266624 | tf_op jit(solution)/shard_map/reduce_sum | solution.py:151
  15.2 0.2 multiply_reduce_fusion.3
  15.8 1.8 %fusion.11 = (bf16[1024,512]{0,1:T(8,128)(2,1)}, f32[512,1024]{1,0:T(8,128)S(1)}) fusion(bf16[512,256]{1,0:T(8,128)(2,1)S(1)} %bitcast.167, bf16[256,1024]{1,0:T(8,128)(2,1)S(1)} %copy-done), kind=kOutput, calls=%fused_computation.112 | convolution fusion | flops 273154048 | bytes 3932160 | tf_op jit(solution)/shard_map/dot_general | solution.py:161
  17.6 1.6 %fusion.124 = (f32[256]{0:T(256)S(1)}, bf16[4,128,256]{2,1,0:T(8,128)(2,1)S(1)}, f32[512,256]{1,0:T(8,128)}) fusion(bf16[4,256,256]{2,1,0:T(8,128)(2,1)S(1)} %copy-done.6, s32[]{:T(128)S(6)} %select_n.62, f32[256]{0:T(256)S(1)} %copy-done.125, bf16[1024,256]{1,0:T(8,128)(2,1)S(1)} %copy-done.8, f32[512,1024]{1,0:T(8,128)S(1)} %get-tuple-element.152), kind=kOutput, calls=%fused_computation.236 | convolution fusion | flops 273809152 | bytes 3672068 | tf_op jit(solution)/shard_map/dot_general | solution.py:163
  19.2 1.4 %fusion.6 = bf16[512,1024]{1,0:T(8,128)(2,1)S(1)} fusion(f32[512,1024]{1,0:T(8,128)S(1)} %get-tuple-element.152, bf16[512,256]{1,0:T(8,128)(2,1)S(1)} %bitcast.164, bf16[1024,256]{1,0:T(8,128)(2,1)S(1)} %copy-done.8), kind=kOutput, calls=%fused_computation.107 | convolution fusion | flops 278396928 | bytes 3932160 | tf_op jit(solution)/shard_map/dot_general | solution.py:164
  20.7 0.6 multiply_reduce_fusion.2
  21.2 0.3 multiply_reduce_fusion
  21.6 1.3 %fusion.171 = (f32[256]{0:T(256)S(1)}, f32[256]{0:T(256)S(1)}, f32[256]{0:T(256)S(1)}, f32[256]{0:T(256)S(1)}, f32[256]{0:T(256)S(1)}, /*index=5*/f32[256]{0:T(2...) fusion(f32[10,134,256]{2,1,0:T(8,128)S(1)} %fusion.23, ...), kind=kLoop, calls=%fused_computation.283 | loop fusion | flops 4584192 | bytes 8148992 | tf_op jit(solution)/shard_map/reduce_sum | solution.py:132
  22.9 1.0 %fusion.172 = (f32[256]{0:T(256)S(1)}, f32[256]{0:T(256)S(1)}, f32[256]{0:T(256)S(1)}, f32[256]{0:T(256)S(1)}, f32[256]{0:T(256)S(1)}, /*index=5*/f32[256]{0:T(2...) fusion(bf16[4,128,256]{2,1,0:T(8,128)(2,1)S(1)} %get-tuple-elem, ...), kind=kLoop, calls=%fused_computation.284 | loop fusion | flops 4845056 | bytes 9717760 | tf_op jit(solution)/shard_map/reduce_sum | solution.py:132
  23.9 1.0 %fusion.173 = (f32[256]{0:T(256)S(1)}, f32[256]{0:T(256)S(1)}, f32[256]{0:T(256)S(1)}, f32[256]{0:T(256)S(1)}, f32[256]{0:T(256)S(1)}, /*index=5*/f32[256]{0:T(2...) fusion(bf16[4,128,256]{2,1,0:T(8,128)(2,1)S(1)} %get-tuple-elem, ...), kind=kLoop, calls=%fused_computation.285 | loop fusion | flops 4845056 | bytes 9717760 | tf_op jit(solution)/shard_map/reduce_sum | solution.py:132
  25.2 6.0 %collective-permute-start.6 = (f32[51,256]{1,0:T(8,128)S(1)}, f32[51,256]{1,0:T(8,128)}, u32[]{:S(2)}, u32[]{:S(2)}) collective-permute-start(f32[51,256]{1,0:T(8,128)S(1)} %concatenate.16), channel_id=1, source_target_pairs={{0,1},{1,0},{2,3},{3,2},{4,5},{5,4},{6,7},{7,6},{8,9},{9,8},{10,11... | collective-permute-start | bytes 156680 | tf_op jit(solution)/shard_map/ppermute | solution.py:69
  31.2 1.5 %copy.25 = bf16[1024,512]{1,0:T(8,128)(2,1)S(1)} copy(bf16[1024,512]{0,1:T(8,128)(2,1)} %get-tuple-element.151) | data formatting | bytes 2097152 | tf_op jit(solution)/shard_map/convert_element_type | solution.py:162
  32.7 0.4 convolution_bitcast_fusion
  33.3 1.0 %copy-done.2 = f32[2,2,2,2,64,256]{5,4,3,2,1,0:T(8,128)} copy-done((f32[2,2,2,2,64,256]{5,4,3,2,1,0:T(8,128)}, f32[2,2,2,2,64,256]{5,4,3,2,1,0:T(8,128)S(1)}, u32[]{:S(2)}) %copy-start.2) | copy-done | bytes 1048600
  34.3 0.8 %constant_dynamic-slice_fusion = f32[512,256]{1,0:T(8,128)} fusion(f32[1024,256]{1,0:T(8,128)S(1)} %bitcast.158, s32[]{:T(128)S(6)} %select_n.67), kind=kLoop, calls=%fused_computation.482 | loop fusion | bytes 1048580 | tf_op jit(solution)/shard_map/dynamic_slice | solution.py:67
  35.1 0.4 fusion.15
  36.1 0.9 %constant_dynamic-slice_fusion.1 = f32[4,128,256]{2,1,0:T(8,128)} fusion(f32[4,256,256]{2,1,0:T(8,128)S(1)} %bitcast.160, s32[]{:T(128)S(6)} %select_n.65), kind=kLoop, calls=%fused_computation.483 | loop fusion | bytes 1048580 | tf_op jit(solution)/shard_map/dynamic_slice | solution.py:65
  36.9 0.5 collective-permute-start.4
  37.5 0.9 %fusion.261 = (bf16[3,256,256]{2,1,0:T(8,128)(2,1)}, bf16[3,256,256]{2,1,0:T(8,128)(2,1)}) fusion(bf16[4,256,256]{2,1,0:T(8,128)(2,1)S(1)} %get-tuple-element.91), kind=kLoop, calls=%fused_computation.495 | loop fusion | bytes 1572864 | tf_op jit(solution)/shard_map/slice | solution.py:98
  38.5 1.9 %collective-permute-start.2 = (bf16[3,256,256]{2,1,0:T(8,128)(2,1)}, bf16[3,256,256]{2,1,0:T(8,128)(2,1)S(1)}, u32[]{:S(2)}, u32[]{:S(2)}) collective-permute-start(bf16[3,256,256]{2,1,0:T(8,128)(2,1)} %get-tuple-element.87), channel_id=1, source_target_pairs={{0,1},{1,2},{2,3},{3,4},{4,5},{5,6},{6,7},{7,8},{8,9},{9,10},{10,1... | collective-permute-start | bytes 1179656 | tf_op jit(solution)/shard_map/ppermute | solution.py:98
  40.4 1.5 %collective-permute-start.3 = (bf16[3,256,256]{2,1,0:T(8,128)(2,1)}, bf16[3,256,256]{2,1,0:T(8,128)(2,1)S(1)}, u32[]{:S(2)}, u32[]{:S(2)}) collective-permute-start(bf16[3,256,256]{2,1,0:T(8,128)(2,1)} %get-tuple-element.88), channel_id=1, source_target_pairs={{1,0},{2,1},{3,2},{4,3},{5,4},{6,5},{7,6},{8,7},{9,8},{10,9},{11,1... | collective-permute-start | bytes 1179656 | tf_op jit(solution)/shard_map/ppermute | solution.py:99
  42.3 3.4 %fusion.117 = f32[4,134,256]{2,1,0:T(8,128)S(1)} fusion(f32[4,128,256]{2,1,0:T(8,128)S(1)} %get-tuple-element.92, f32[256]{0:T(256)S(1)} %bitcast.178, f32[256]{0:T(256)S(1)} %bitcast.234, f32[256]{0:T(256)S(1)} %bitcast.209, f32[256]{0:T(256)S(1)} %bitcast.229, f32[256]{0:T(256)S(1)} %bitcast.224, f32[256]{0:T(256)S(1)} %bitcast.219, f32[256]{0:T(256)S(1)} %bitcast.214, ...), kind=kLoop, calls=%fused_computation.229 | loop fusion | flops 13309952 | bytes 1123328 | tf_op jit(solution)/shard_map/add | solution.py:120
  45.7 0.8 fusion.249
  46.6 1.4 %dynamic_update_slice.10 = f32[4,262,256]{2,1,0:T(8,128)S(1)} dynamic-update-slice(f32[4,262,256]{2,1,0:T(8,128)S(1)} %broadcast_in_dim.10, f32[4,134,256]{2,1,0:T(8,128)S(1)} %fusion.117, s32[]{:T(128)} %constant.23.clone.1, s32[]{:T(128)S(6)} %select_n.63, s32[]{:T(128)} %constant.23.clone.1) | dynamic-update-slice | bytes 1097732 | tf_op jit(solution)/shard_map/dynamic_update_slice | solution.py:206
  48.0 0.9 %add.963 = f32[51,256]{1,0:T(8,128)S(1)} add(f32[51,256]{1,0:T(8,128)S(1)} %concatenate.16, f32[51,256]{1,0:T(8,128)} %collective-permute-done.6) | non-fusion elementwise | flops 13056 | bytes 156672 | tf_op jit(solution)/shard_map/add | solution.py:70
  48.9 1.4 %fusion.208 = f32[1,256,256]{2,1,0:T(8,128)S(1)} fusion(f32[256]{0:T(256)S(1)} %bitcast.179, f32[256]{0:T(256)} %bitcast.233, f32[256]{0:T(256)} %bitcast.208, f32[256]{0:T(256)} %bitcast.228, f32[256]{0:T(256)} %bitcast.223, f32[256]{0:T(256)} %bitcast.218, f32[256]{0:T(256)} %bitcast.213, f32[256]{0:T(256)} %bitcast.272, f32[256]{0:T(256)} %bitcast.268, ...), kind=kLoop, calls=%fused_computation.402 | loop fusion | flops 4063232 | bytes 1463296 | tf_op jit(solution)/shard_map/add | solution.py:231
  50.5 1.3 %dynamic-slice_add_fusion = f32[512,256]{1,0:T(8,128)S(1)} fusion(f32[512,256]{1,0:T(8,128)} %collective-permute-done.5, f32[1024,256]{1,0:T(8,128)} %bitcast.159, s32[]{:T(128)S(6)} %select_n.66), kind=kLoop, calls=%fused_computation.287 | loop fusion | flops 131072 | bytes 1572868 | tf_op jit(solution)/shard_map/add | solution.py:89
  52.0 1.1 %dynamic-slice_add_fusion.1 = f32[4,128,256]{2,1,0:T(8,128)S(1)} fusion(f32[4,128,256]{2,1,0:T(8,128)} %collective-permute-done.4, f32[4,256,256]{2,1,0:T(8,128)S(1)} %bitcast.161, s32[]{:T(128)S(6)} %select_n.64), kind=kLoop, calls=%fused_computation.288 | loop fusion | flops 131072 | bytes 1572868 | tf_op jit(solution)/shard_map/add | solution.py:88
  53.2 5.6 %collective-permute-start.7 = (bf16[614,256]{1,0:T(8,128)(2,1)S(1)}, bf16[614,256]{1,0:T(8,128)(2,1)S(1)}, u32[]{:S(2)}, u32[]{:S(2)}) collective-permute-start(bf16[614,256]{1,0:T(8,128)(2,1)S(1)} %pad_maximum_fusion), channel_id=1, source_target_pairs={{0,2},{1,3},{2,0},{3,1},{4,6},{5,7},{6,4},{7,5},{8,10},{9,11},{10,... | collective-permute-start | bytes 943112 | tf_op jit(solution)/shard_map/ppermute | solution.py:77
  59.0 0.7 fusion.188
  59.9 0.7 fusion.215
  60.6 6.4 %collective-permute-done.7 = bf16[614,256]{1,0:T(8,128)(2,1)S(1)} collective-permute-done((bf16[614,256]{1,0:T(8,128)(2,1)S(1)}, bf16[614,256]{1,0:T(8,128)(2,1)S(1)}, u32[]{:S(2)}, u32[]{:S(2)}) %collective-permute-start.7) | collective-permute-done | bytes 314400 | tf_op jit(solution)/shard_map/ppermute | solution.py:77
  67.2 2.4 %collective-permute-start.8 = (bf16[358,256]{1,0:T(8,128)(2,1)S(1)}, bf16[358,256]{1,0:T(8,128)(2,1)S(1)}, u32[]{:S(2)}, u32[]{:S(2)}) collective-permute-start(bf16[358,256]{1,0:T(8,128)(2,1)S(1)} %pad_maximum_fusion.1), channel_id=1, source_target_pairs={{0,4},{1,5},{2,6},{3,7},{4,0},{5,1},{6,2},{7,3},{8,12},{9,13},{10,... | collective-permute-start | bytes 549896 | tf_op jit(solution)/shard_map/ppermute | solution.py:77
  69.7 0.7 fusion.229
  70.4 3.8 %collective-permute-done.8 = bf16[358,256]{1,0:T(8,128)(2,1)S(1)} collective-permute-done((bf16[358,256]{1,0:T(8,128)(2,1)S(1)}, bf16[358,256]{1,0:T(8,128)(2,1)S(1)}, u32[]{:S(2)}, u32[]{:S(2)}) %collective-permute-start.8) | collective-permute-done | bytes 183328 | tf_op jit(solution)/shard_map/ppermute | solution.py:77
  74.4 2.8 %collective-permute-start.9 = (bf16[230,256]{1,0:T(8,128)(2,1)S(1)}, bf16[230,256]{1,0:T(8,128)(2,1)S(1)}, u32[]{:S(2)}, u32[]{:S(2)}) collective-permute-start(bf16[230,256]{1,0:T(8,128)(2,1)S(1)} %pad_maximum_fusion.2), channel_id=1, source_target_pairs={{0,8},{1,9},{2,10},{3,11},{4,12},{5,13},{6,14},{7,15},{8,0},{9,1},... | collective-permute-start | bytes 353288 | tf_op jit(solution)/shard_map/ppermute | solution.py:77
  77.2 1.0 %fusion.18 = bf16[4,256,256]{2,1,0:T(8,128)(2,1)} fusion(f32[4,262,256]{2,1,0:T(8,128)S(1)} %dynamic_update_slice.10, f32[1,256,256]{2,1,0:T(8,128)S(1)} %fusion.229, f32[1,256,256]{2,1,0:T(8,128)S(1)} %fusion.215, f32[1,256,256]{2,1,0:T(8,128)S(1)} %fusion.208, f32[1,256,256]{2,1,0:T(8,128)S(1)} %fusion.188, bf16[4,256,256]{2,1,0:T(8,128)(2,1)S(1)} %copy-done.7), kind=kLoop, calls=%fused_computation.128 | loop fusion | flops 1835008 | bytes 3145728 | tf_op jit(solution)/shard_map/convert_element_type | solution.py:234
  78.3 4.0 %collective-permute-done.9 = bf16[230,256]{1,0:T(8,128)(2,1)S(1)} collective-permute-done((bf16[230,256]{1,0:T(8,128)(2,1)S(1)}, bf16[230,256]{1,0:T(8,128)(2,1)S(1)}, u32[]{:S(2)}, u32[]{:S(2)}) %collective-permute-start.9) | collective-permute-done | bytes 117792 | tf_op jit(solution)/shard_map/ppermute | solution.py:77
  82.3 0.6 fusion.255
  83.0 0.6 convert_add_fusion.8
  83.6 0.6 copy.30
  (301 shorter events, 1.9 us)
Async XLA Ops:
  0.6 15.1 %copy-start = (bf16[256,1024]{1,0:T(8,128)(2,1)S(1)}, bf16[256,1024]{1,0:T(8,128)(2,1)}, u32[]{:S(2)}) copy-start(bf16[256,1024]{1,0:T(8,128)(2,1)} %param.12) | copy-start | bytes 1572868
  1.8 6.1 %collective-permute-start = (bf16[3,256,256]{2,1,0:T(8,128)(2,1)S(1)}, bf16[3,256,256]{2,1,0:T(8,128)(2,1)S(1)}, u32[]{:S(2)}, u32[]{:S(2)}) collective-permute-start(bf16[3,256,256]{2,1,0:T(8,128)(2,1)S(1)} %get-tuple-element.90), channel_id=1, source_target_pairs={{0,1},{1,2},{2,3},{3,4},{4,5},{5,6},{6,7},{7,8},{8,9},{9,10},{10,1... | collective-permute-start | bytes 1179656 | tf_op jit(solution)/shard_map/ppermute | solution.py:21
  4.2 5.7 %collective-permute-start.1 = (bf16[3,256,256]{2,1,0:T(8,128)(2,1)S(1)}, bf16[3,256,256]{2,1,0:T(8,128)(2,1)S(1)}, u32[]{:S(2)}, u32[]{:S(2)}) collective-permute-start(bf16[3,256,256]{2,1,0:T(8,128)(2,1)S(1)} %get-tuple-element.89), channel_id=1, source_target_pairs={{1,0},{2,1},{3,2},{4,3},{5,4},{6,5},{7,6},{8,7},{9,8},{10,9},{11,1... | collective-permute-start | bytes 1179656 | tf_op jit(solution)/shard_map/ppermute | solution.py:24
  6.9 8.0 %copy-start.34 = (f32[1,1,256]{2,1,0:T(1,128)}, f32[1,1,256]{2,1,0:T(1,128)S(1)}, u32[]{:S(2)}) copy-start(f32[1,1,256]{2,1,0:T(1,128)S(1)} %get-tuple-element.105) | copy-start | bytes 3076
  6.9 8.0 %copy-start.37 = (f32[1,1,256]{2,1,0:T(1,128)}, f32[1,1,256]{2,1,0:T(1,128)S(1)}, u32[]{:S(2)}) copy-start(f32[1,1,256]{2,1,0:T(1,128)S(1)} %get-tuple-element.106) | copy-start | bytes 3076
  6.9 8.0 %copy-start.40 = (f32[1,1,256]{2,1,0:T(1,128)}, f32[1,1,256]{2,1,0:T(1,128)S(1)}, u32[]{:S(2)}) copy-start(f32[1,1,256]{2,1,0:T(1,128)S(1)} %get-tuple-element.107) | copy-start | bytes 3076
  6.9 8.0 %copy-start.43 = (f32[1,1,256]{2,1,0:T(1,128)}, f32[1,1,256]{2,1,0:T(1,128)S(1)}, u32[]{:S(2)}) copy-start(f32[1,1,256]{2,1,0:T(1,128)S(1)} %get-tuple-element.108) | copy-start | bytes 3076
  6.9 8.0 %copy-start.46 = (f32[1,1,256]{2,1,0:T(1,128)}, f32[1,1,256]{2,1,0:T(1,128)S(1)}, u32[]{:S(2)}) copy-start(f32[1,1,256]{2,1,0:T(1,128)S(1)} %get-tuple-element.109) | copy-start | bytes 3076
  6.9 8.0 %copy-start.49 = (f32[1,1,256]{2,1,0:T(1,128)}, f32[1,1,256]{2,1,0:T(1,128)S(1)}, u32[]{:S(2)}) copy-start(f32[1,1,256]{2,1,0:T(1,128)S(1)} %get-tuple-element.110) | copy-start | bytes 3076
  6.9 8.0 %copy-start.52 = (f32[1,1,256]{2,1,0:T(1,128)}, f32[1,1,256]{2,1,0:T(1,128)S(1)}, u32[]{:S(2)}) copy-start(f32[1,1,256]{2,1,0:T(1,128)S(1)} %get-tuple-element.111) | copy-start | bytes 3076
  7.0 8.0 %copy-start.76 = (f32[1,1,256]{2,1,0:T(1,128)}, f32[1,1,256]{2,1,0:T(1,128)S(1)}, u32[]{:S(2)}) copy-start(f32[1,1,256]{2,1,0:T(1,128)S(1)} %get-tuple-element.112) | copy-start | bytes 3076
  7.0 8.0 %copy-start.79 = (f32[1,1,256]{2,1,0:T(1,128)}, f32[1,1,256]{2,1,0:T(1,128)S(1)}, u32[]{:S(2)}) copy-start(f32[1,1,256]{2,1,0:T(1,128)S(1)} %get-tuple-element.113) | copy-start | bytes 3076
  7.0 8.0 %copy-start.82 = (f32[1,1,256]{2,1,0:T(1,128)}, f32[1,1,256]{2,1,0:T(1,128)S(1)}, u32[]{:S(2)}) copy-start(f32[1,1,256]{2,1,0:T(1,128)S(1)} %get-tuple-element.114) | copy-start | bytes 3076
  7.0 8.0 %copy-start.85 = (f32[1,1,256]{2,1,0:T(1,128)}, f32[1,1,256]{2,1,0:T(1,128)S(1)}, u32[]{:S(2)}) copy-start(f32[1,1,256]{2,1,0:T(1,128)S(1)} %get-tuple-element.115) | copy-start | bytes 3076
  7.0 8.0 %copy-start.88 = (f32[1,1,256]{2,1,0:T(1,128)}, f32[1,1,256]{2,1,0:T(1,128)S(1)}, u32[]{:S(2)}) copy-start(f32[1,1,256]{2,1,0:T(1,128)S(1)} %get-tuple-element.116) | copy-start | bytes 3076
  25.2 22.8 %collective-permute-start.6 = (f32[51,256]{1,0:T(8,128)S(1)}, f32[51,256]{1,0:T(8,128)}, u32[]{:S(2)}, u32[]{:S(2)}) collective-permute-start(f32[51,256]{1,0:T(8,128)S(1)} %concatenate.16), channel_id=1, source_target_pairs={{0,1},{1,0},{2,3},{3,2},{4,5},{5,4},{6,7},{7,6},{8,9},{9,8},{10,11... | collective-permute-start | bytes 156680 | tf_op jit(solution)/shard_map/ppermute | solution.py:69
  35.1 15.4 %collective-permute-start.5 = (f32[512,256]{1,0:T(8,128)}, f32[512,256]{1,0:T(8,128)}, u32[]{:S(2)}, u32[]{:S(2)}) collective-permute-start(f32[512,256]{1,0:T(8,128)} %constant_dynamic-slice_fusion), channel_id=1, source_target_pairs={{0,1},{1,0},{2,3},{3,2},{4,5},{5,4},{6,7},{7,6},{8,9},{9,8},{10,11... | collective-permute-start | bytes 1572872 | tf_op jit(solution)/shard_map/ppermute | solution.py:69
  36.9 8.8 %copy-start.5 = (f32[512,256]{1,0:T(8,128)S(1)}, f32[512,256]{1,0:T(8,128)}, u32[]{:S(2)}) copy-start(f32[512,256]{1,0:T(8,128)} %get-tuple-element.148) | copy-start | bytes 1572868
  36.9 15.0 %collective-permute-start.4 = (f32[4,128,256]{2,1,0:T(8,128)}, f32[4,128,256]{2,1,0:T(8,128)}, u32[]{:S(2)}, u32[]{:S(2)}) collective-permute-start(f32[4,128,256]{2,1,0:T(8,128)} %constant_dynamic-slice_fusion.1), channel_id=1, source_target_pairs={{0,1},{1,0},{2,3},{3,2},{4,5},{5,4},{6,7},{7,6},{8,9},{9,8},{10,11... | collective-permute-start | bytes 1572872 | tf_op jit(solution)/shard_map/ppermute | solution.py:69
  38.5 10.4 %collective-permute-start.2 = (bf16[3,256,256]{2,1,0:T(8,128)(2,1)}, bf16[3,256,256]{2,1,0:T(8,128)(2,1)S(1)}, u32[]{:S(2)}, u32[]{:S(2)}) collective-permute-start(bf16[3,256,256]{2,1,0:T(8,128)(2,1)} %get-tuple-element.87), channel_id=1, source_target_pairs={{0,1},{1,2},{2,3},{3,4},{4,5},{5,6},{6,7},{7,8},{8,9},{9,10},{10,1... | collective-permute-start | bytes 1179656 | tf_op jit(solution)/shard_map/ppermute | solution.py:98
  40.4 8.5 %collective-permute-start.3 = (bf16[3,256,256]{2,1,0:T(8,128)(2,1)}, bf16[3,256,256]{2,1,0:T(8,128)(2,1)S(1)}, u32[]{:S(2)}, u32[]{:S(2)}) collective-permute-start(bf16[3,256,256]{2,1,0:T(8,128)(2,1)} %get-tuple-element.88), channel_id=1, source_target_pairs={{1,0},{2,1},{3,2},{4,3},{5,4},{6,5},{7,6},{8,7},{9,8},{10,9},{11,1... | collective-permute-start | bytes 1179656 | tf_op jit(solution)/shard_map/ppermute | solution.py:99
  50.4 8.5 %copy-start.30 = (f32[1,1,256]{2,1,0:T(1,128)S(1)}, f32[1,1,256]{2,1,0:T(1,128)}, u32[]{:S(2)}) copy-start(f32[1,1,256]{2,1,0:T(1,128)} %copy-done.28) | copy-start | bytes 3076
  50.4 8.5 %copy-start.33 = (f32[1,1,256]{2,1,0:T(1,128)S(1)}, f32[1,1,256]{2,1,0:T(1,128)}, u32[]{:S(2)}) copy-start(f32[1,1,256]{2,1,0:T(1,128)} %copy-done.31) | copy-start | bytes 3076
  50.4 8.5 %copy-start.36 = (f32[1,1,256]{2,1,0:T(1,128)S(1)}, f32[1,1,256]{2,1,0:T(1,128)}, u32[]{:S(2)}) copy-start(f32[1,1,256]{2,1,0:T(1,128)} %copy-done.34) | copy-start | bytes 3076
  50.4 8.5 %copy-start.39 = (f32[1,1,256]{2,1,0:T(1,128)S(1)}, f32[1,1,256]{2,1,0:T(1,128)}, u32[]{:S(2)}) copy-start(f32[1,1,256]{2,1,0:T(1,128)} %copy-done.37) | copy-start | bytes 3076
  50.4 8.5 %copy-start.42 = (f32[1,1,256]{2,1,0:T(1,128)S(1)}, f32[1,1,256]{2,1,0:T(1,128)}, u32[]{:S(2)}) copy-start(f32[1,1,256]{2,1,0:T(1,128)} %copy-done.40) | copy-start | bytes 3076
  50.4 8.5 %copy-start.45 = (f32[1,1,256]{2,1,0:T(1,128)S(1)}, f32[1,1,256]{2,1,0:T(1,128)}, u32[]{:S(2)}) copy-start(f32[1,1,256]{2,1,0:T(1,128)} %copy-done.43) | copy-start | bytes 3076
  50.4 8.5 %copy-start.48 = (f32[1,1,256]{2,1,0:T(1,128)S(1)}, f32[1,1,256]{2,1,0:T(1,128)}, u32[]{:S(2)}) copy-start(f32[1,1,256]{2,1,0:T(1,128)} %copy-done.46) | copy-start | bytes 3076
  50.4 8.5 %copy-start.51 = (f32[1,1,256]{2,1,0:T(1,128)S(1)}, f32[1,1,256]{2,1,0:T(1,128)}, u32[]{:S(2)}) copy-start(f32[1,1,256]{2,1,0:T(1,128)} %copy-done.49) | copy-start | bytes 3076
  50.5 8.5 %copy-start.54 = (f32[1,1,256]{2,1,0:T(1,128)S(1)}, f32[1,1,256]{2,1,0:T(1,128)}, u32[]{:S(2)}) copy-start(f32[1,1,256]{2,1,0:T(1,128)} %copy-done.52) | copy-start | bytes 3076
  50.5 8.5 %copy-start.78 = (f32[1,1,256]{2,1,0:T(1,128)S(1)}, f32[1,1,256]{2,1,0:T(1,128)}, u32[]{:S(2)}) copy-start(f32[1,1,256]{2,1,0:T(1,128)} %copy-done.76) | copy-start | bytes 3076
  50.5 8.5 %copy-start.81 = (f32[1,1,256]{2,1,0:T(1,128)S(1)}, f32[1,1,256]{2,1,0:T(1,128)}, u32[]{:S(2)}) copy-start(f32[1,1,256]{2,1,0:T(1,128)} %copy-done.79) | copy-start | bytes 3076
  50.5 8.5 %copy-start.84 = (f32[1,1,256]{2,1,0:T(1,128)S(1)}, f32[1,1,256]{2,1,0:T(1,128)}, u32[]{:S(2)}) copy-start(f32[1,1,256]{2,1,0:T(1,128)} %copy-done.82) | copy-start | bytes 3076
  50.5 8.5 %copy-start.87 = (f32[1,1,256]{2,1,0:T(1,128)S(1)}, f32[1,1,256]{2,1,0:T(1,128)}, u32[]{:S(2)}) copy-start(f32[1,1,256]{2,1,0:T(1,128)} %copy-done.85) | copy-start | bytes 3076
  50.5 8.5 %copy-start.90 = (f32[1,1,256]{2,1,0:T(1,128)S(1)}, f32[1,1,256]{2,1,0:T(1,128)}, u32[]{:S(2)}) copy-start(f32[1,1,256]{2,1,0:T(1,128)} %copy-done.88) | copy-start | bytes 3076
  50.5 8.5 %copy-start.93 = (f32[1,1,256]{2,1,0:T(1,128)S(1)}, f32[1,1,256]{2,1,0:T(1,128)}, u32[]{:S(2)}) copy-start(f32[1,1,256]{2,1,0:T(1,128)} %copy-done.91) | copy-start | bytes 3076
  50.5 8.5 %copy-start.117 = (f32[1,1,256]{2,1,0:T(1,128)S(1)}, f32[1,1,256]{2,1,0:T(1,128)}, u32[]{:S(2)}) copy-start(f32[1,1,256]{2,1,0:T(1,128)} %copy-done.115) | copy-start | bytes 3076
  53.2 13.8 %collective-permute-start.7 = (bf16[614,256]{1,0:T(8,128)(2,1)S(1)}, bf16[614,256]{1,0:T(8,128)(2,1)S(1)}, u32[]{:S(2)}, u32[]{:S(2)}) collective-permute-start(bf16[614,256]{1,0:T(8,128)(2,1)S(1)} %pad_maximum_fusion), channel_id=1, source_target_pairs={{0,2},{1,3},{2,0},{3,1},{4,6},{5,7},{6,4},{7,5},{8,10},{9,11},{10,... | collective-permute-start | bytes 943112 | tf_op jit(solution)/shard_map/ppermute | solution.py:77
  59.8 9.9 %copy-start.96 = (f32[1,1,256]{2,1,0:T(1,128)S(1)}, f32[1,1,256]{2,1,0:T(1,128)}, u32[]{:S(2)}) copy-start(f32[1,1,256]{2,1,0:T(1,128)} %copy-done.94) | copy-start | bytes 3076
  59.8 9.9 %copy-start.99 = (f32[1,1,256]{2,1,0:T(1,128)S(1)}, f32[1,1,256]{2,1,0:T(1,128)}, u32[]{:S(2)}) copy-start(f32[1,1,256]{2,1,0:T(1,128)} %copy-done.97) | copy-start | bytes 3076
  59.8 9.9 %copy-start.102 = (f32[1,1,256]{2,1,0:T(1,128)S(1)}, f32[1,1,256]{2,1,0:T(1,128)}, u32[]{:S(2)}) copy-start(f32[1,1,256]{2,1,0:T(1,128)} %copy-done.100) | copy-start | bytes 3076
  59.8 9.8 %copy-start.105 = (f32[1,1,256]{2,1,0:T(1,128)S(1)}, f32[1,1,256]{2,1,0:T(1,128)}, u32[]{:S(2)}) copy-start(f32[1,1,256]{2,1,0:T(1,128)} %copy-done.103) | copy-start | bytes 3076
  59.9 9.8 %copy-start.108 = (f32[1,1,256]{2,1,0:T(1,128)S(1)}, f32[1,1,256]{2,1,0:T(1,128)}, u32[]{:S(2)}) copy-start(f32[1,1,256]{2,1,0:T(1,128)} %copy-done.106) | copy-start | bytes 3076
  59.9 9.8 %copy-start.111 = (f32[1,1,256]{2,1,0:T(1,128)S(1)}, f32[1,1,256]{2,1,0:T(1,128)}, u32[]{:S(2)}) copy-start(f32[1,1,256]{2,1,0:T(1,128)} %copy-done.109) | copy-start | bytes 3076
  59.9 9.8 %copy-start.114 = (f32[1,1,256]{2,1,0:T(1,128)S(1)}, f32[1,1,256]{2,1,0:T(1,128)}, u32[]{:S(2)}) copy-start(f32[1,1,256]{2,1,0:T(1,128)} %copy-done.112) | copy-start | bytes 3076
  67.1 10.2 %copy-start.7 = (bf16[4,256,256]{2,1,0:T(8,128)(2,1)S(1)}, bf16[4,256,256]{2,1,0:T(8,128)(2,1)}, u32[]{:S(2)}) copy-start(bf16[4,256,256]{2,1,0:T(8,128)(2,1)} %param.15) | copy-start | bytes 1572868
  67.2 7.0 %collective-permute-start.8 = (bf16[358,256]{1,0:T(8,128)(2,1)S(1)}, bf16[358,256]{1,0:T(8,128)(2,1)S(1)}, u32[]{:S(2)}, u32[]{:S(2)}) collective-permute-start(bf16[358,256]{1,0:T(8,128)(2,1)S(1)} %pad_maximum_fusion.1), channel_id=1, source_target_pairs={{0,4},{1,5},{2,6},{3,7},{4,0},{5,1},{6,2},{7,3},{8,12},{9,13},{10,... | collective-permute-start | bytes 549896 | tf_op jit(solution)/shard_map/ppermute | solution.py:77
  74.4 7.9 %collective-permute-start.9 = (bf16[230,256]{1,0:T(8,128)(2,1)S(1)}, bf16[230,256]{1,0:T(8,128)(2,1)S(1)}, u32[]{:S(2)}, u32[]{:S(2)}) collective-permute-start(bf16[230,256]{1,0:T(8,128)(2,1)S(1)} %pad_maximum_fusion.2), channel_id=1, source_target_pairs={{0,8},{1,9},{2,10},{3,11},{4,12},{5,13},{6,14},{7,15},{8,0},{9,1},... | collective-permute-start | bytes 353288 | tf_op jit(solution)/shard_map/ppermute | solution.py:77
  (91 other events, 590.2 us)

commit v18 on v15

--- a/solution.py
+++ b/solution.py
@@ -215,8 +215,8 @@
     )
     low, high = halo_rows(grad_conv, "row", half_width)
     edge = ((0, 0), (half_width, half_width), (0, 0))
-    low = jnp.pad(low, edge)
-    high = jnp.pad(high, edge)
+    low = jnp.pad(low.astype(jnp.float32), edge)
+    high = jnp.pad(high.astype(jnp.float32), edge)
     halo_out = []
     for out_row in range(image_rows):
         total = jnp.zeros((image_cols, channels), jnp.float32)

time: 90.2 us -> 79.8 us (0.88)
  local copies, waits for them, and re-layouts: 15.4 us -> 7.63 us
  other arithmetic: 23.4 us -> 18.6 us
  starting transfers between devices: 23.6 us -> 27.6 us
  matrix products: 8.1 us -> 6.46 us
    ppermute x1, starting transfers between devices: 8.71 us -> 2.42 us  [halo_rows(): lax.ppermute(lax.slice_in_dim(block, block.shape[0] - width, None, axis=0...]
    ppermute x3, starting transfers between devices: 7.65 us -> 13.8 us  [halving_reduce(): got = lax.ppermute(sent, axis, pairs)]
    concatenate x1, local copies, waits for them, and re-layouts: 5.1 us -> 0.18 us  [shards(): jnp.concatenate([kernel_grad, gain_grad[None], scale_grad[None]], axis=0)]
    ppermute x3, starting transfers between devices: 2.27 us -> 6.2 us  [halving_reduce(): got_q, got_r, got_whole = lax.ppermute((give_q, give_r, whole), axis, pairs)]
    reduce_sum x3, other arithmetic: 5.06 us -> 3.28 us  [kernel_terms(): jnp.sum(padded[row_tap:row_tap + image_rows, col_tap:col_tap + image_cols...]
    dot_general x1, matrix products: 2.17 us -> 0.82 us  [shards(): branch = jnp.dot(act_flat, w_out, preferred_element_type=jnp.float32)]
    dynamic_update_slice x1, other arithmetic: 1.2 us -> 0.07 us  [shards(): lax.dynamic_update_slice_in_dim(image, out_tile, first_col, axis=1)]
    add x4, other arithmetic: 1.81 us -> 0.76 us  [halving_reduce(): rows = keep_r + got_r.astype(jnp.float32)]
  transfers between devices with their start and end apart: 10 -> 10, of which waited for: 4 -> 4; matrix products, arithmetic and copies ran while one was open for 25% -> 16% of each run, Pallas kernels for 0% -> 0%
where the time goes in v18:
time: 79.8 us; the launch traced here: 79.5 us
  starting transfers between devices  27.6 us (35%)
  other arithmetic  18.6 us (23%)
  waiting for transfers between devices  16 us (20%)
  local copies, waits for them, and re-layouts  7.63 us (10%)
  matrix products  6.46 us (8%)
  between operations  3.16 us (4%)
    ppermute x3, waiting for transfers between devices, halving_reduce(): got = lax.ppermute(sent, axis, pairs)  14 us
    ppermute x3, starting transfers between devices, halving_reduce(): got = lax.ppermute(sent, axis, pairs)  13.8 us
    ppermute x3, starting transfers between devices, halving_reduce(): got_q, got_r, got_whole = lax.ppermute((give_q, give_r, whole), axis, pairs)  6.2 us
    reduce_sum x1, other arithmetic, shards(): centre = jnp.mean(filtered, axis=-1, keepdims=True)  4.54 us
    add x1, other arithmetic, depthwise(): total + padded[row_tap:row_tap + image_rows, col_tap:col_tap + image_cols...  3.37 us
    reduce_sum x3, other arithmetic, kernel_terms(): jnp.sum(padded[row_tap:row_tap + image_rows, col_tap:col_tap + image_cols...  3.28 us
    unnamed x183, local copies, waits for them, and re-layouts  3.24 us
    add x4, other arithmetic, shards(): total + line[col_tap:col_tap + image_cols] * flipped[row_tap, col_tap]  2.66 us
  transfers between devices with their start and end apart: 10, of which 4 were waited for; matrix products, arithmetic and copies ran while one was open for 16% of the time, Pallas kernels for 0%

profile of v18, /device:TPU:0, one launch (start us, length us, event | category | flops | bytes accessed | tf_op | source)
XLA Modules:
  0.0 79.5 jit_solution(10915418999369374937)
XLA Ops:
  0.7 1.1 %copy.38 = bf16[4,256,256]{2,1,0:T(8,128)(2,1)S(1)} copy(bf16[4,256,256]{2,1,0:T(8,128)(2,1)} %param.8) | data formatting | bytes 1048576
  1.8 2.4 %collective-permute-start = (bf16[3,256,256]{2,1,0:T(8,128)(2,1)S(1)}, bf16[3,256,256]{2,1,0:T(8,128)(2,1)S(1)}, u32[]{:S(2)}, u32[]{:S(2)}) collective-permute-start(bf16[3,256,256]{2,1,0:T(8,128)(2,1)S(1)} %get-tuple-element.92), channel_id=1, source_target_pairs={{0,1},{1,2},{2,3},{3,4},{4,5},{5,6},{6,7},{7,8},{8,9},{9,10},{10,1... | collective-permute-start | bytes 1179656 | tf_op jit(solution)/shard_map/ppermute | solution.py:21
  4.2 1.3 %collective-permute-start.1 = (bf16[3,256,256]{2,1,0:T(8,128)(2,1)S(1)}, bf16[3,256,256]{2,1,0:T(8,128)(2,1)S(1)}, u32[]{:S(2)}, u32[]{:S(2)}) collective-permute-start(bf16[3,256,256]{2,1,0:T(8,128)(2,1)S(1)} %get-tuple-element.91), channel_id=1, source_target_pairs={{1,0},{2,1},{3,2},{4,3},{5,4},{6,5},{7,6},{8,7},{9,8},{10,9},{11,1... | collective-permute-start | bytes 1179656 | tf_op jit(solution)/shard_map/ppermute | solution.py:24
  5.5 0.7 bitcast_reduce_fusion
  7.2 0.6 fusion.228
  7.9 2.0 %collective-permute-done.1 = bf16[3,256,256]{2,1,0:T(8,128)(2,1)S(1)} collective-permute-done((bf16[3,256,256]{2,1,0:T(8,128)(2,1)S(1)}, bf16[3,256,256]{2,1,0:T(8,128)(2,1)S(1)}, u32[]{:S(2)}, u32[]{:S(2)}) %collective-permute-start.1) | collective-permute-done | bytes 393248 | tf_op jit(solution)/shard_map/ppermute | solution.py:24
  9.9 0.3 fusion.23
  10.3 4.5 %fusion.219 = (f32[4,128]{1,0:T(4,128)S(1)}, f32[4,128,256]{2,1,0:T(8,128)S(1)}) fusion(f32[256]{0:T(256)S(1)} %bitcast.237, f32[10,134,256]{2,1,0:T(8,128)S(1)} %fusion.23, f32[256]{0:T(256)S(1)} %bitcast.242, f32[256]{0:T(256)S(1)} %bitcast.182, f32[256]{0:T(256)S(1)} %bitcast.187, f32[256]{0:T(256)S(1)} %bitcast.192, f32[256]{0:T(256)S(1)} %bitcast.197, ...), kind=kLoop, calls=%fused_computation.405 | loop fusion | flops 12844544 | bytes 26266624 | tf_op jit(solution)/shard_map/reduce_sum | solution.py:151
  15.2 0.2 multiply_reduce_fusion.3
  15.5 0.2 multiply_convert_fusion.3
  15.7 1.8 %fusion.11 = (bf16[1024,512]{0,1:T(8,128)(2,1)}, f32[512,1024]{1,0:T(8,128)S(1)}) fusion(bf16[512,256]{1,0:T(8,128)(2,1)S(1)} %bitcast.167, bf16[256,1024]{1,0:T(8,128)(2,1)S(1)} %copy-done), kind=kOutput, calls=%fused_computation.112 | convolution fusion | flops 273154048 | bytes 3932160 | tf_op jit(solution)/shard_map/dot_general | solution.py:161
  17.6 0.8 %fusion.124 = (f32[256]{0:T(256)S(1)}, bf16[4,128,256]{2,1,0:T(8,128)(2,1)S(1)}, f32[512,256]{1,0:T(8,128)S(1)}) fusion(bf16[4,256,256]{2,1,0:T(8,128)(2,1)S(1)} %copy-done.2, s32[]{:T(128)S(6)} %select_n.80, f32[256]{0:T(256)S(1)} %copy-done.86, bf16[1024,256]{1,0:T(8,128)(2,1)S(1)} %copy-done.4, f32[512,1024]{1,0:T(8,128)S(1)} %get-tuple-element.154), kind=kOutput, calls=%fused_computation.236 | convolution fusion | flops 273809152 | bytes 3672068 | tf_op jit(solution)/shard_map/dot_general | solution.py:163
  18.4 0.7 copy-done.3
  19.1 1.4 %fusion.6 = bf16[512,1024]{1,0:T(8,128)(2,1)S(1)} fusion(f32[512,1024]{1,0:T(8,128)S(1)} %get-tuple-element.154, bf16[512,256]{1,0:T(8,128)(2,1)S(1)} %bitcast.164, bf16[1024,256]{1,0:T(8,128)(2,1)S(1)} %copy-done.4), kind=kOutput, calls=%fused_computation.107 | convolution fusion | flops 278396928 | bytes 3932160 | tf_op jit(solution)/shard_map/dot_general | solution.py:164
  20.6 0.6 multiply_reduce_fusion.2
  21.1 0.3 multiply_reduce_fusion
  21.5 1.3 %fusion.171 = (f32[256]{0:T(256)S(1)}, f32[256]{0:T(256)S(1)}, f32[256]{0:T(256)S(1)}, f32[256]{0:T(256)S(1)}, f32[256]{0:T(256)S(1)}, /*index=5*/f32[256]{0:T(2...) fusion(f32[10,134,256]{2,1,0:T(8,128)S(1)} %fusion.23, ...), kind=kLoop, calls=%fused_computation.283 | loop fusion | flops 4584192 | bytes 8148992 | tf_op jit(solution)/shard_map/reduce_sum | solution.py:132
  22.7 1.0 %fusion.172 = (f32[256]{0:T(256)S(1)}, f32[256]{0:T(256)S(1)}, f32[256]{0:T(256)S(1)}, f32[256]{0:T(256)S(1)}, f32[256]{0:T(256)S(1)}, /*index=5*/f32[256]{0:T(2...) fusion(bf16[4,128,256]{2,1,0:T(8,128)(2,1)S(1)} %get-tuple-elem, ...), kind=kLoop, calls=%fused_computation.284 | loop fusion | flops 4845056 | bytes 9717760 | tf_op jit(solution)/shard_map/reduce_sum | solution.py:132
  23.7 1.0 %fusion.173 = (f32[256]{0:T(256)S(1)}, f32[256]{0:T(256)S(1)}, f32[256]{0:T(256)S(1)}, f32[256]{0:T(256)S(1)}, f32[256]{0:T(256)S(1)}, /*index=5*/f32[256]{0:T(2...) fusion(bf16[4,128,256]{2,1,0:T(8,128)(2,1)S(1)} %get-tuple-elem, ...), kind=kLoop, calls=%fused_computation.285 | loop fusion | flops 4845056 | bytes 9717760 | tf_op jit(solution)/shard_map/reduce_sum | solution.py:132
  24.8 0.8 %copy.22 = bf16[512,256]{0,1:T(8,128)(2,1)} copy(bf16[512,256]{1,0:T(8,128)(2,1)S(1)} %bitcast.168) | data formatting | bytes 524288 | tf_op jit(solution)/shard_map/reshape | solution.py:159
  25.6 0.2 concatenate.16
  25.8 6.0 %collective-permute-start.6 = (f32[51,256]{1,0:T(8,128)S(1)}, f32[51,256]{1,0:T(8,128)S(1)}, u32[]{:S(2)}, u32[]{:S(2)}) collective-permute-start(f32[51,256]{1,0:T(8,128)S(1)} %concatenate.16), channel_id=1, source_target_pairs={{0,1},{1,0},{2,3},{3,2},{4,5},{5,4},{6,7},{7,6},{8,9},{9,8},{10,11... | collective-permute-start | bytes 156680 | tf_op jit(solution)/shard_map/ppermute | solution.py:69
  31.8 1.5 %copy.25 = bf16[1024,512]{1,0:T(8,128)(2,1)S(1)} copy(bf16[1024,512]{0,1:T(8,128)(2,1)} %get-tuple-element.153) | data formatting | bytes 2097152 | tf_op jit(solution)/shard_map/convert_element_type | solution.py:162
  33.3 1.4 %convolution_bitcast_fusion = f32[2,2,2,2,64,256]{5,4,0,1,2,3:T(8,128)S(1)} fusion(bf16[2,2,2,2,64,512]{5,4,3,2,1,0:T(8,128)(2,1)S(1)} %bitcast.162, bf16[512,256,1,1,1,1]{1,0,5,4,3,2:T(8,128)(2,1)} %bitcast.165), kind=kOutput, calls=%fused_computation.119 | convolution fusion | flops 268435456 | bytes 2359296 | tf_op jit(solution)/shard_map/dot_general | solution.py:177
  34.7 0.1 copy.26
  34.9 0.1 collective-permute-start.5
  35.0 0.7 copy-done.5
  35.6 0.4 copy-done.90
  36.0 0.4 fusion.15
  36.5 0.1 copy.24
  37.0 0.1 collective-permute-start.4
  37.3 2.4 %collective-permute-start.2 = (bf16[3,256,256]{2,1,0:T(8,128)(2,1)S(1)}, bf16[3,256,256]{2,1,0:T(8,128)(2,1)S(1)}, u32[]{:S(2)}, u32[]{:S(2)}) collective-permute-start(bf16[3,256,256]{2,1,0:T(8,128)(2,1)S(1)} %get-tuple-element.89), channel_id=1, source_target_pairs={{0,1},{1,2},{2,3},{3,4},{4,5},{5,6},{6,7},{7,8},{8,9},{9,10},{10,1... | collective-permute-start | bytes 1179656 | tf_op jit(solution)/shard_map/ppermute | solution.py:98
  39.7 1.5 %collective-permute-start.3 = (bf16[3,256,256]{2,1,0:T(8,128)(2,1)S(1)}, bf16[3,256,256]{2,1,0:T(8,128)(2,1)S(1)}, u32[]{:S(2)}, u32[]{:S(2)}) collective-permute-start(bf16[3,256,256]{2,1,0:T(8,128)(2,1)S(1)} %get-tuple-element.90), channel_id=1, source_target_pairs={{1,0},{2,1},{3,2},{4,3},{5,4},{6,5},{7,6},{8,7},{9,8},{10,9},{11,1... | collective-permute-start | bytes 1179656 | tf_op jit(solution)/shard_map/ppermute | solution.py:99
  41.6 3.4 %fusion.117 = f32[4,134,256]{2,1,0:T(8,128)S(1)} fusion(f32[4,128,256]{2,1,0:T(8,128)S(1)} %get-tuple-element.93, f32[256]{0:T(256)S(1)} %bitcast.178, f32[256]{0:T(256)S(1)} %bitcast.233, f32[256]{0:T(256)S(1)} %bitcast.208, f32[256]{0:T(256)S(1)} %bitcast.228, f32[256]{0:T(256)S(1)} %bitcast.223, f32[256]{0:T(256)S(1)} %bitcast.218, f32[256]{0:T(256)S(1)} %bitcast.213, ...), kind=kLoop, calls=%fused_computation.229 | loop fusion | flops 13309952 | bytes 1123328 | tf_op jit(solution)/shard_map/add | solution.py:120
  45.3 0.7 multiply_add_fusion.4
  46.3 5.6 %collective-permute-start.7 = (bf16[614,256]{1,0:T(8,128)(2,1)S(1)}, bf16[614,256]{1,0:T(8,128)(2,1)S(1)}, u32[]{:S(2)}, u32[]{:S(2)}) collective-permute-start(bf16[614,256]{1,0:T(8,128)(2,1)S(1)} %pad_maximum_fusion), channel_id=1, source_target_pairs={{0,2},{1,3},{2,0},{3,1},{4,6},{5,7},{6,4},{7,5},{8,10},{9,11},{10,... | collective-permute-start | bytes 943112 | tf_op jit(solution)/shard_map/ppermute | solution.py:77
  51.9 0.7 fusion.197
  52.5 0.7 multiply_add_fusion.3
  53.2 4.4 %collective-permute-done.7 = bf16[614,256]{1,0:T(8,128)(2,1)S(1)} collective-permute-done((bf16[614,256]{1,0:T(8,128)(2,1)S(1)}, bf16[614,256]{1,0:T(8,128)(2,1)S(1)}, u32[]{:S(2)}, u32[]{:S(2)}) %collective-permute-start.7) | collective-permute-done | bytes 314400 | tf_op jit(solution)/shard_map/ppermute | solution.py:77
  57.8 4.9 %collective-permute-start.8 = (bf16[358,256]{1,0:T(8,128)(2,1)S(1)}, bf16[358,256]{1,0:T(8,128)(2,1)S(1)}, u32[]{:S(2)}, u32[]{:S(2)}) collective-permute-start(bf16[358,256]{1,0:T(8,128)(2,1)S(1)} %pad_maximum_fusion.1), channel_id=1, source_target_pairs={{0,4},{1,5},{2,6},{3,7},{4,0},{5,1},{6,2},{7,3},{8,12},{9,13},{10,... | collective-permute-start | bytes 549896 | tf_op jit(solution)/shard_map/ppermute | solution.py:77
  62.8 0.7 fusion.179
  63.4 4.6 %collective-permute-done.8 = bf16[358,256]{1,0:T(8,128)(2,1)S(1)} collective-permute-done((bf16[358,256]{1,0:T(8,128)(2,1)S(1)}, bf16[358,256]{1,0:T(8,128)(2,1)S(1)}, u32[]{:S(2)}, u32[]{:S(2)}) %collective-permute-start.8) | collective-permute-done | bytes 183328 | tf_op jit(solution)/shard_map/ppermute | solution.py:77
  68.2 3.3 %collective-permute-start.9 = (bf16[230,256]{1,0:T(8,128)(2,1)S(1)}, bf16[230,256]{1,0:T(8,128)(2,1)S(1)}, u32[]{:S(2)}, u32[]{:S(2)}) collective-permute-start(bf16[230,256]{1,0:T(8,128)(2,1)S(1)} %pad_maximum_fusion.2), channel_id=1, source_target_pairs={{0,8},{1,9},{2,10},{3,11},{4,12},{5,13},{6,14},{7,15},{8,0},{9,1},... | collective-permute-start | bytes 353288 | tf_op jit(solution)/shard_map/ppermute | solution.py:77
  71.5 1.1 %fusion.18 = bf16[4,256,256]{2,1,0:T(8,128)(2,1)} fusion(f32[1,256,256]{2,1,0:T(8,128)S(1)} %fusion.179, f32[1,256,256]{2,1,0:T(8,128)S(1)} %multiply_add_fusion.3, f32[1,256,256]{2,1,0:T(8,128)S(1)} %multiply_add_fusion.4, f32[1,256,256]{2,1,0:T(8,128)S(1)} %fusion.197, f32[4,131,256]{2,1,0:T(8,128)S(1)} %get-tuple-element.86, ...), kind=kLoop, calls=%fused_computation.128 | loop fusion | flops 2359296 | bytes 3170306 | tf_op jit(solution)/shard_map/convert_element_type | solution.py:235
  72.6 5.0 %collective-permute-done.9 = bf16[230,256]{1,0:T(8,128)(2,1)S(1)} collective-permute-done((bf16[230,256]{1,0:T(8,128)(2,1)S(1)}, bf16[230,256]{1,0:T(8,128)(2,1)S(1)}, u32[]{:S(2)}, u32[]{:S(2)}) %collective-permute-start.9) | collective-permute-done | bytes 117792 | tf_op jit(solution)/shard_map/ppermute | solution.py:77
  77.5 0.6 fusion.214
  78.2 0.6 convert_add_fusion.8
  78.8 0.6 copy.30
  (226 shorter events, 1.6 us)
Async XLA Ops:
  0.6 15.1 %copy-start = (bf16[256,1024]{1,0:T(8,128)(2,1)S(1)}, bf16[256,1024]{1,0:T(8,128)(2,1)}, u32[]{:S(2)}) copy-start(bf16[256,1024]{1,0:T(8,128)(2,1)} %param.12) | copy-start | bytes 1572868
  1.8 6.1 %collective-permute-start = (bf16[3,256,256]{2,1,0:T(8,128)(2,1)S(1)}, bf16[3,256,256]{2,1,0:T(8,128)(2,1)S(1)}, u32[]{:S(2)}, u32[]{:S(2)}) collective-permute-start(bf16[3,256,256]{2,1,0:T(8,128)(2,1)S(1)} %get-tuple-element.92), channel_id=1, source_target_pairs={{0,1},{1,2},{2,3},{3,4},{4,5},{5,6},{6,7},{7,8},{8,9},{9,10},{10,1... | collective-permute-start | bytes 1179656 | tf_op jit(solution)/shard_map/ppermute | solution.py:21
  4.2 5.7 %collective-permute-start.1 = (bf16[3,256,256]{2,1,0:T(8,128)(2,1)S(1)}, bf16[3,256,256]{2,1,0:T(8,128)(2,1)S(1)}, u32[]{:S(2)}, u32[]{:S(2)}) collective-permute-start(bf16[3,256,256]{2,1,0:T(8,128)(2,1)S(1)} %get-tuple-element.91), channel_id=1, source_target_pairs={{1,0},{2,1},{3,2},{4,3},{5,4},{6,5},{7,6},{8,7},{9,8},{10,9},{11,1... | collective-permute-start | bytes 1179656 | tf_op jit(solution)/shard_map/ppermute | solution.py:24
  6.9 7.9 %copy-start.19 = (f32[1,1,256]{2,1,0:T(1,128)}, f32[1,1,256]{2,1,0:T(1,128)S(1)}, u32[]{:S(2)}) copy-start(f32[1,1,256]{2,1,0:T(1,128)S(1)} %get-tuple-element.107) | copy-start | bytes 3076
  6.9 7.9 %copy-start.21 = (f32[1,1,256]{2,1,0:T(1,128)}, f32[1,1,256]{2,1,0:T(1,128)S(1)}, u32[]{:S(2)}) copy-start(f32[1,1,256]{2,1,0:T(1,128)S(1)} %get-tuple-element.108) | copy-start | bytes 3076
  6.9 7.9 %copy-start.23 = (f32[1,1,256]{2,1,0:T(1,128)}, f32[1,1,256]{2,1,0:T(1,128)S(1)}, u32[]{:S(2)}) copy-start(f32[1,1,256]{2,1,0:T(1,128)S(1)} %get-tuple-element.109) | copy-start | bytes 3076
  6.9 7.9 %copy-start.25 = (f32[1,1,256]{2,1,0:T(1,128)}, f32[1,1,256]{2,1,0:T(1,128)S(1)}, u32[]{:S(2)}) copy-start(f32[1,1,256]{2,1,0:T(1,128)S(1)} %get-tuple-element.110) | copy-start | bytes 3076
  7.0 7.9 %copy-start.27 = (f32[1,1,256]{2,1,0:T(1,128)}, f32[1,1,256]{2,1,0:T(1,128)S(1)}, u32[]{:S(2)}) copy-start(f32[1,1,256]{2,1,0:T(1,128)S(1)} %get-tuple-element.111) | copy-start | bytes 3076
  7.0 7.9 %copy-start.29 = (f32[1,1,256]{2,1,0:T(1,128)}, f32[1,1,256]{2,1,0:T(1,128)S(1)}, u32[]{:S(2)}) copy-start(f32[1,1,256]{2,1,0:T(1,128)S(1)} %get-tuple-element.112) | copy-start | bytes 3076
  7.0 7.9 %copy-start.31 = (f32[1,1,256]{2,1,0:T(1,128)}, f32[1,1,256]{2,1,0:T(1,128)S(1)}, u32[]{:S(2)}) copy-start(f32[1,1,256]{2,1,0:T(1,128)S(1)} %get-tuple-element.113) | copy-start | bytes 3076
  7.0 7.9 %copy-start.47 = (f32[1,1,256]{2,1,0:T(1,128)}, f32[1,1,256]{2,1,0:T(1,128)S(1)}, u32[]{:S(2)}) copy-start(f32[1,1,256]{2,1,0:T(1,128)S(1)} %get-tuple-element.114) | copy-start | bytes 3076
  7.0 7.9 %copy-start.49 = (f32[1,1,256]{2,1,0:T(1,128)}, f32[1,1,256]{2,1,0:T(1,128)S(1)}, u32[]{:S(2)}) copy-start(f32[1,1,256]{2,1,0:T(1,128)S(1)} %get-tuple-element.115) | copy-start | bytes 3076
  7.0 7.9 %copy-start.51 = (f32[1,1,256]{2,1,0:T(1,128)}, f32[1,1,256]{2,1,0:T(1,128)S(1)}, u32[]{:S(2)}) copy-start(f32[1,1,256]{2,1,0:T(1,128)S(1)} %get-tuple-element.116) | copy-start | bytes 3076
  7.0 7.9 %copy-start.53 = (f32[1,1,256]{2,1,0:T(1,128)}, f32[1,1,256]{2,1,0:T(1,128)S(1)}, u32[]{:S(2)}) copy-start(f32[1,1,256]{2,1,0:T(1,128)S(1)} %get-tuple-element.117) | copy-start | bytes 3076
  7.0 7.9 %copy-start.55 = (f32[1,1,256]{2,1,0:T(1,128)}, f32[1,1,256]{2,1,0:T(1,128)S(1)}, u32[]{:S(2)}) copy-start(f32[1,1,256]{2,1,0:T(1,128)S(1)} %get-tuple-element.118) | copy-start | bytes 3076
  7.0 7.9 %copy-start.57 = (f32[1,1,256]{2,1,0:T(1,128)}, f32[1,1,256]{2,1,0:T(1,128)S(1)}, u32[]{:S(2)}) copy-start(f32[1,1,256]{2,1,0:T(1,128)S(1)} %get-tuple-element.119) | copy-start | bytes 3076
  7.1 7.9 %copy-start.7 = (f32[1,1,256]{2,1,0:T(1,128)}, f32[1,1,256]{2,1,0:T(1,128)S(1)}, u32[]{:S(2)}) copy-start(f32[1,1,256]{2,1,0:T(1,128)S(1)} %get-tuple-element.145) | copy-start | bytes 3076
  7.1 7.9 %copy-start.9 = (f32[1,1,256]{2,1,0:T(1,128)}, f32[1,1,256]{2,1,0:T(1,128)S(1)}, u32[]{:S(2)}) copy-start(f32[1,1,256]{2,1,0:T(1,128)S(1)} %get-tuple-element.146) | copy-start | bytes 3076
  7.1 7.9 %copy-start.11 = (f32[1,1,256]{2,1,0:T(1,128)}, f32[1,1,256]{2,1,0:T(1,128)S(1)}, u32[]{:S(2)}) copy-start(f32[1,1,256]{2,1,0:T(1,128)S(1)} %get-tuple-element.147) | copy-start | bytes 3076
  7.1 7.9 %copy-start.15 = (f32[1,1,256]{2,1,0:T(1,128)}, f32[1,1,256]{2,1,0:T(1,128)S(1)}, u32[]{:S(2)}) copy-start(f32[1,1,256]{2,1,0:T(1,128)S(1)} %get-tuple-element.148) | copy-start | bytes 3076
  7.1 7.9 %copy-start.17 = (f32[1,1,256]{2,1,0:T(1,128)}, f32[1,1,256]{2,1,0:T(1,128)S(1)}, u32[]{:S(2)}) copy-start(f32[1,1,256]{2,1,0:T(1,128)S(1)} %get-tuple-element.149) | copy-start | bytes 3076
  7.1 7.9 %copy-start.33 = (f32[1,1,256]{2,1,0:T(1,128)}, f32[1,1,256]{2,1,0:T(1,128)S(1)}, u32[]{:S(2)}) copy-start(f32[1,1,256]{2,1,0:T(1,128)S(1)} %get-tuple-element.140) | copy-start | bytes 3076
  7.1 7.9 %copy-start.35 = (f32[1,1,256]{2,1,0:T(1,128)}, f32[1,1,256]{2,1,0:T(1,128)S(1)}, u32[]{:S(2)}) copy-start(f32[1,1,256]{2,1,0:T(1,128)S(1)} %get-tuple-element.141) | copy-start | bytes 3076
  7.1 7.9 %copy-start.37 = (f32[1,1,256]{2,1,0:T(1,128)}, f32[1,1,256]{2,1,0:T(1,128)S(1)}, u32[]{:S(2)}) copy-start(f32[1,1,256]{2,1,0:T(1,128)S(1)} %get-tuple-element.142) | copy-start | bytes 3076
  7.2 7.9 %copy-start.39 = (f32[1,1,256]{2,1,0:T(1,128)}, f32[1,1,256]{2,1,0:T(1,128)S(1)}, u32[]{:S(2)}) copy-start(f32[1,1,256]{2,1,0:T(1,128)S(1)} %get-tuple-element.143) | copy-start | bytes 3076
  7.8 7.3 %copy-start.45 = (f32[1,1,256]{2,1,0:T(1,128)}, f32[1,1,256]{2,1,0:T(1,128)S(1)}, u32[]{:S(2)}) copy-start(f32[1,1,256]{2,1,0:T(1,128)S(1)} %get-tuple-element.138) | copy-start | bytes 3076
  7.8 7.3 %copy-start.59 = (f32[1,1,256]{2,1,0:T(1,128)}, f32[1,1,256]{2,1,0:T(1,128)S(1)}, u32[]{:S(2)}) copy-start(f32[1,1,256]{2,1,0:T(1,128)S(1)} %get-tuple-element.129) | copy-start | bytes 3076
  7.8 7.3 %copy-start.61 = (f32[1,1,256]{2,1,0:T(1,128)}, f32[1,1,256]{2,1,0:T(1,128)S(1)}, u32[]{:S(2)}) copy-start(f32[1,1,256]{2,1,0:T(1,128)S(1)} %get-tuple-element.130) | copy-start | bytes 3076
  7.8 7.3 %copy-start.63 = (f32[1,1,256]{2,1,0:T(1,128)}, f32[1,1,256]{2,1,0:T(1,128)S(1)}, u32[]{:S(2)}) copy-start(f32[1,1,256]{2,1,0:T(1,128)S(1)} %get-tuple-element.131) | copy-start | bytes 3076
  7.8 7.3 %copy-start.65 = (f32[1,1,256]{2,1,0:T(1,128)}, f32[1,1,256]{2,1,0:T(1,128)S(1)}, u32[]{:S(2)}) copy-start(f32[1,1,256]{2,1,0:T(1,128)S(1)} %get-tuple-element.132) | copy-start | bytes 3076
  7.8 7.3 %copy-start.67 = (f32[1,1,256]{2,1,0:T(1,128)}, f32[1,1,256]{2,1,0:T(1,128)S(1)}, u32[]{:S(2)}) copy-start(f32[1,1,256]{2,1,0:T(1,128)S(1)} %get-tuple-element.133) | copy-start | bytes 3076
  7.8 7.3 %copy-start.69 = (f32[1,1,256]{2,1,0:T(1,128)}, f32[1,1,256]{2,1,0:T(1,128)S(1)}, u32[]{:S(2)}) copy-start(f32[1,1,256]{2,1,0:T(1,128)S(1)} %get-tuple-element.134) | copy-start | bytes 3076
  7.8 7.3 %copy-start.71 = (f32[1,1,256]{2,1,0:T(1,128)}, f32[1,1,256]{2,1,0:T(1,128)S(1)}, u32[]{:S(2)}) copy-start(f32[1,1,256]{2,1,0:T(1,128)S(1)} %get-tuple-element.135) | copy-start | bytes 3076
  7.8 7.3 %copy-start.73 = (f32[1,1,256]{2,1,0:T(1,128)}, f32[1,1,256]{2,1,0:T(1,128)S(1)}, u32[]{:S(2)}) copy-start(f32[1,1,256]{2,1,0:T(1,128)S(1)} %get-tuple-element.121) | copy-start | bytes 3076
  7.8 7.3 %copy-start.76 = (f32[1,1,256]{2,1,0:T(1,128)}, f32[1,1,256]{2,1,0:T(1,128)S(1)}, u32[]{:S(2)}) copy-start(f32[1,1,256]{2,1,0:T(1,128)S(1)} %get-tuple-element.122) | copy-start | bytes 3076
  7.8 7.3 %copy-start.78 = (f32[1,1,256]{2,1,0:T(1,128)}, f32[1,1,256]{2,1,0:T(1,128)S(1)}, u32[]{:S(2)}) copy-start(f32[1,1,256]{2,1,0:T(1,128)S(1)} %get-tuple-element.123) | copy-start | bytes 3076
  7.9 7.3 %copy-start.80 = (f32[1,1,256]{2,1,0:T(1,128)}, f32[1,1,256]{2,1,0:T(1,128)S(1)}, u32[]{:S(2)}) copy-start(f32[1,1,256]{2,1,0:T(1,128)S(1)} %get-tuple-element.124) | copy-start | bytes 3076
  7.9 7.3 %copy-start.82 = (f32[1,1,256]{2,1,0:T(1,128)}, f32[1,1,256]{2,1,0:T(1,128)S(1)}, u32[]{:S(2)}) copy-start(f32[1,1,256]{2,1,0:T(1,128)S(1)} %get-tuple-element.125) | copy-start | bytes 3076
  7.9 7.3 %copy-start.84 = (f32[1,1,256]{2,1,0:T(1,128)}, f32[1,1,256]{2,1,0:T(1,128)S(1)}, u32[]{:S(2)}) copy-start(f32[1,1,256]{2,1,0:T(1,128)S(1)} %get-tuple-element.126) | copy-start | bytes 3076
  25.8 19.4 %collective-permute-start.6 = (f32[51,256]{1,0:T(8,128)S(1)}, f32[51,256]{1,0:T(8,128)S(1)}, u32[]{:S(2)}, u32[]{:S(2)}) collective-permute-start(f32[51,256]{1,0:T(8,128)S(1)} %concatenate.16), channel_id=1, source_target_pairs={{0,1},{1,0},{2,3},{3,2},{4,5},{5,4},{6,7},{7,6},{8,9},{9,8},{10,11... | collective-permute-start | bytes 156680 | tf_op jit(solution)/shard_map/ppermute | solution.py:69
  34.9 11.1 %collective-permute-start.5 = (f32[512,256]{1,0:T(8,128)S(1)}, f32[512,256]{1,0:T(8,128)S(1)}, u32[]{:S(2)}, u32[]{:S(2)}) collective-permute-start(f32[512,256]{1,0:T(8,128)S(1)} %constant_dynamic-slice_fusion), channel_id=1, source_target_pairs={{0,1},{1,0},{2,3},{3,2},{4,5},{5,4},{6,7},{7,6},{8,9},{9,8},{10,11... | collective-permute-start | bytes 1572872 | tf_op jit(solution)/shard_map/ppermute | solution.py:69
  37.0 9.1 %collective-permute-start.4 = (f32[4,128,256]{2,1,0:T(8,128)S(1)}, f32[4,128,256]{2,1,0:T(8,128)S(1)}, u32[]{:S(2)}, u32[]{:S(2)}) collective-permute-start(f32[4,128,256]{2,1,0:T(8,128)S(1)} %constant_dynamic-slice_fusion.1), channel_id=1, source_target_pairs={{0,1},{1,0},{2,3},{3,2},{4,5},{5,4},{6,7},{7,6},{8,9},{9,8},{10,11... | collective-permute-start | bytes 1572872 | tf_op jit(solution)/shard_map/ppermute | solution.py:69
  37.2 7.8 %copy-start.87 = (f32[256]{0:T(256)S(1)}, f32[256]{0:T(256)}, u32[]{:S(2)}) copy-start(f32[256]{0:T(256)} %param.14) | copy-start | bytes 3076
  37.3 7.9 %collective-permute-start.2 = (bf16[3,256,256]{2,1,0:T(8,128)(2,1)S(1)}, bf16[3,256,256]{2,1,0:T(8,128)(2,1)S(1)}, u32[]{:S(2)}, u32[]{:S(2)}) collective-permute-start(bf16[3,256,256]{2,1,0:T(8,128)(2,1)S(1)} %get-tuple-element.89), channel_id=1, source_target_pairs={{0,1},{1,2},{2,3},{3,4},{4,5},{5,6},{6,7},{7,8},{8,9},{9,10},{10,1... | collective-permute-start | bytes 1179656 | tf_op jit(solution)/shard_map/ppermute | solution.py:98
  39.7 5.5 %collective-permute-start.3 = (bf16[3,256,256]{2,1,0:T(8,128)(2,1)S(1)}, bf16[3,256,256]{2,1,0:T(8,128)(2,1)S(1)}, u32[]{:S(2)}, u32[]{:S(2)}) collective-permute-start(bf16[3,256,256]{2,1,0:T(8,128)(2,1)S(1)} %get-tuple-element.90), channel_id=1, source_target_pairs={{1,0},{2,1},{3,2},{4,3},{5,4},{6,5},{7,6},{8,7},{9,8},{10,9},{11,1... | collective-permute-start | bytes 1179656 | tf_op jit(solution)/shard_map/ppermute | solution.py:99
  46.3 11.3 %collective-permute-start.7 = (bf16[614,256]{1,0:T(8,128)(2,1)S(1)}, bf16[614,256]{1,0:T(8,128)(2,1)S(1)}, u32[]{:S(2)}, u32[]{:S(2)}) collective-permute-start(bf16[614,256]{1,0:T(8,128)(2,1)S(1)} %pad_maximum_fusion), channel_id=1, source_target_pairs={{0,2},{1,3},{2,0},{3,1},{4,6},{5,7},{6,4},{7,5},{8,10},{9,11},{10,... | collective-permute-start | bytes 943112 | tf_op jit(solution)/shard_map/ppermute | solution.py:77
  57.8 10.2 %collective-permute-start.8 = (bf16[358,256]{1,0:T(8,128)(2,1)S(1)}, bf16[358,256]{1,0:T(8,128)(2,1)S(1)}, u32[]{:S(2)}, u32[]{:S(2)}) collective-permute-start(bf16[358,256]{1,0:T(8,128)(2,1)S(1)} %pad_maximum_fusion.1), channel_id=1, source_target_pairs={{0,4},{1,5},{2,6},{3,7},{4,0},{5,1},{6,2},{7,3},{8,12},{9,13},{10,... | collective-permute-start | bytes 549896 | tf_op jit(solution)/shard_map/ppermute | solution.py:77
  68.2 9.3 %collective-permute-start.9 = (bf16[230,256]{1,0:T(8,128)(2,1)S(1)}, bf16[230,256]{1,0:T(8,128)(2,1)S(1)}, u32[]{:S(2)}, u32[]{:S(2)}) collective-permute-start(bf16[230,256]{1,0:T(8,128)(2,1)S(1)} %pad_maximum_fusion.2), channel_id=1, source_target_pairs={{0,8},{1,9},{2,10},{3,11},{4,12},{5,13},{6,14},{7,15},{8,0},{9,1},... | collective-permute-start | bytes 353288 | tf_op jit(solution)/shard_map/ppermute | solution.py:77
  (53 other events, 229.8 us)

commit v19 on v18

--- a/solution.py
+++ b/solution.py
@@ -41,6 +41,41 @@
     high = values.astype(jnp.bfloat16)
     low = (values - high.astype(jnp.float32)).astype(jnp.bfloat16)
     return high, low
+
+
+def four_way(quartered, rows, whole, axis, step):
+    count = lax.axis_size(axis)
+    me = lax.axis_index(axis)
+    quarters, width = quartered.shape[0], quartered.shape[2]
+    part_q = quartered.shape[1] // 4
+    part_r = rows.shape[0] // 4
+    mine = 2 * ((me >> step) & 1) + ((me >> (step + 1)) & 1)
+    high, low = split_pair(whole)
+    size = whole.shape[0]
+    cut_q = quarters * part_q
+    cut_r = cut_q + part_r
+    quartered_new = lax.dynamic_slice_in_dim(quartered, mine * part_q, part_q, axis=1)
+    rows_new = lax.dynamic_slice_in_dim(rows, mine * part_r, part_r, axis=0)
+    decoded = [high.astype(jnp.float32) + low.astype(jnp.float32)]
+    for offset in (1, 2, 3):
+        mask = ((offset >> 1) << step) | ((offset & 1) << (step + 1))
+        pairs = [(i, i ^ mask) for i in range(count)]
+        other = mine ^ offset
+        give_q = lax.dynamic_slice_in_dim(quartered, other * part_q, part_q, axis=1)
+        give_r = lax.dynamic_slice_in_dim(rows, other * part_r, part_r, axis=0)
+        sent = jnp.concatenate(
+            [give_q.astype(jnp.bfloat16).reshape(-1, width), give_r.astype(jnp.bfloat16), high, low],
+            axis=0,
+        )
+        got = lax.ppermute(sent, axis, pairs)
+        quartered_new = quartered_new + got[:cut_q].reshape(quarters, part_q, width).astype(jnp.float32)
+        rows_new = rows_new + got[cut_q:cut_r].astype(jnp.float32)
+        decoded.append(
+            got[cut_r : cut_r + size].astype(jnp.float32) + got[cut_r + size :].astype(jnp.float32)
+        )
+    ordered = jnp.stack(decoded)[jnp.bitwise_xor(jnp.arange(4), mine)]
+    whole = ((ordered[0] + ordered[1]) + ordered[2]) + ordered[3]
+    return lax.optimization_barrier((quartered_new, rows_new, whole))
 
 
 def halving_reduce(quartered, rows, whole, axis):
@@ -56,7 +91,15 @@
     quartered = bit_reversed(quartered, count, steps, 1)
     rows = bit_reversed(rows, count, steps, 0)
     quarters, width = quartered.shape[0], quartered.shape[2]
-    for step in range(steps):
+    rounds, step = [[0]], 1
+    while step < steps:
+        rounds.append([step, step + 1] if step + 1 < steps else [step])
+        step += len(rounds[-1])
+    for bits in rounds:
+        if len(bits) == 2:
+            quartered, rows, whole = four_way(quartered, rows, whole, axis, bits[0])
+            continue
+        step = bits[0]
         bit = (me >> step) & 1
         pairs = [(i, i ^ (1 << step)) for i in range(count)]
         half_q = quartered.shape[1] // 2

time: 79.8 us -> 87.9 us (1.10)
  local copies, waits for them, and re-layouts: 7.63 us -> 13.1 us
  other arithmetic: 18.6 us -> 23.8 us
  starting transfers between devices: 27.6 us -> 25.4 us
  waiting for transfers between devices: 16 us -> 13.8 us
  matrix products: 6.46 us -> 8.04 us
    ppermute x3 -> x1, starting transfers between devices: 13.8 us -> 2.77 us  [halving_reduce(): got = lax.ppermute(sent, axis, pairs)]
    ppermute x3 -> x1, waiting for transfers between devices: 14 us -> 4.96 us  [halving_reduce(): got = lax.ppermute(sent, axis, pairs)]
    ppermute x0 -> x3, starting transfers between devices: none -> 8.84 us  [four_way(): got = lax.ppermute(sent, axis, pairs)]
    ppermute x0 -> x3, waiting for transfers between devices: none -> 7.46 us  [four_way(): got = lax.ppermute(sent, axis, pairs)]
    slice x0 -> x3, local copies, waits for them, and re-layouts: none -> 2.53 us  [four_way(): got[:cut_q].reshape(quarters, part_q, width).astype(jnp.float32)]
    gather x0 -> x1, local copies, waits for them, and re-layouts: none -> 2.3 us  [four_way(): ordered = jnp.stack(decoded)[jnp.bitwise_xor(jnp.arange(4), mine)]]
    add x4, other arithmetic: 2.66 us -> 4.75 us  [shards(): total + line[col_tap:col_tap + image_cols] * flipped[row_tap, col_tap]]
    add x0 -> x3, other arithmetic: none -> 1.96 us  [the longest x1 0.99 us: four_way(): whole = ordered[0] + ordered[1] + ordered[2] + ordered[3]]
  transfers between devices with their start and end apart: 10 -> 11, of which waited for: 4 -> 4; matrix products, arithmetic and copies ran while one was open for 16% -> 17% of each run, Pallas kernels for 0% -> 0%
where the time goes in v19:
time: 87.9 us; the launch traced here: 87.3 us
  starting transfers between devices  25.4 us (29%)
  other arithmetic  23.8 us (27%)
  waiting for transfers between devices  13.8 us (16%)
  local copies, waits for them, and re-layouts  13.1 us (15%)
  matrix products  8.04 us (9%)
  between operations  3.13 us (4%)
    ppermute x3, starting transfers between devices, four_way(): got = lax.ppermute(sent, axis, pairs)  8.84 us
    ppermute x3, waiting for transfers between devices, four_way(): got = lax.ppermute(sent, axis, pairs)  7.46 us
    ppermute x3, starting transfers between devices, halving_reduce(): got_q, got_r, got_whole = lax.ppermute((give_q, give_r, whole), axis, pairs)  6.22 us
    ppermute x1, waiting for transfers between devices, halving_reduce(): got = lax.ppermute(sent, axis, pairs)  4.96 us
    add x4, other arithmetic, shards(): total + line[col_tap:col_tap + image_cols] * flipped[row_tap, col_tap]  4.75 us
    reduce_sum x1, other arithmetic, shards(): centre = jnp.mean(filtered, axis=-1, keepdims=True)  4.54 us
    unnamed x193, local copies, waits for them, and re-layouts  3.89 us
    add x1, other arithmetic, depthwise(): total + padded[row_tap:row_tap + image_rows, col_tap:col_tap + image_cols...  3.36 us
  transfers between devices with their start and end apart: 11, of which 4 were waited for; matrix products, arithmetic and copies ran while one was open for 17% of the time, Pallas kernels for 0%

profile of v19, /device:TPU:0, one launch (start us, length us, event | category | flops | bytes accessed | tf_op | source)
XLA Modules:
  0.0 87.3 jit_solution(11459134266892056809)
XLA Ops:
  0.7 1.1 %copy.38 = bf16[4,256,256]{2,1,0:T(8,128)(2,1)S(1)} copy(bf16[4,256,256]{2,1,0:T(8,128)(2,1)} %param.8) | data formatting | bytes 1048576
  1.8 2.4 %collective-permute-start = (bf16[3,256,256]{2,1,0:T(8,128)(2,1)S(1)}, bf16[3,256,256]{2,1,0:T(8,128)(2,1)S(1)}, u32[]{:S(2)}, u32[]{:S(2)}) collective-permute-start(bf16[3,256,256]{2,1,0:T(8,128)(2,1)S(1)} %get-tuple-element.92), channel_id=1, source_target_pairs={{0,1},{1,2},{2,3},{3,4},{4,5},{5,6},{6,7},{7,8},{8,9},{9,10},{10,1... | collective-permute-start | bytes 1179656 | tf_op jit(solution)/shard_map/ppermute | solution.py:21
  4.2 1.3 %collective-permute-start.1 = (bf16[3,256,256]{2,1,0:T(8,128)(2,1)S(1)}, bf16[3,256,256]{2,1,0:T(8,128)(2,1)S(1)}, u32[]{:S(2)}, u32[]{:S(2)}) collective-permute-start(bf16[3,256,256]{2,1,0:T(8,128)(2,1)S(1)} %get-tuple-element.91), channel_id=1, source_target_pairs={{1,0},{2,1},{3,2},{4,3},{5,4},{6,5},{7,6},{8,7},{9,8},{10,9},{11,1... | collective-permute-start | bytes 1179656 | tf_op jit(solution)/shard_map/ppermute | solution.py:24
  5.5 0.7 bitcast_reduce_fusion
  7.1 0.6 pad_clamp_fusion
  7.8 0.6 fusion.226
  8.5 1.4 %collective-permute-done.1 = bf16[3,256,256]{2,1,0:T(8,128)(2,1)S(1)} collective-permute-done((bf16[3,256,256]{2,1,0:T(8,128)(2,1)S(1)}, bf16[3,256,256]{2,1,0:T(8,128)(2,1)S(1)}, u32[]{:S(2)}, u32[]{:S(2)}) %collective-permute-start.1) | collective-permute-done | bytes 393248 | tf_op jit(solution)/shard_map/ppermute | solution.py:24
  10.3 4.5 %fusion.219 = (f32[4,128]{1,0:T(4,128)S(1)}, f32[4,128,256]{2,1,0:T(8,128)S(1)}) fusion(f32[256]{0:T(256)S(1)} %bitcast.252, f32[10,134,256]{2,1,0:T(8,128)S(1)} %fusion.23, f32[256]{0:T(256)S(1)} %bitcast.257, f32[256]{0:T(256)S(1)} %bitcast.197, f32[256]{0:T(256)S(1)} %bitcast.202, f32[256]{0:T(256)S(1)} %bitcast.207, f32[256]{0:T(256)S(1)} %bitcast.212, ...), kind=kLoop, calls=%fused_computation.419 | loop fusion | flops 12844544 | bytes 26266624 | tf_op jit(solution)/shard_map/reduce_sum | solution.py:194
  15.7 1.8 %fusion.11 = (bf16[1024,512]{0,1:T(8,128)(2,1)}, f32[512,1024]{1,0:T(8,128)S(1)}) fusion(bf16[512,256]{1,0:T(8,128)(2,1)S(1)} %bitcast.180, bf16[256,1024]{1,0:T(8,128)(2,1)S(1)} %copy-done), kind=kOutput, calls=%fused_computation.113 | convolution fusion | flops 273154048 | bytes 3932160 | tf_op jit(solution)/shard_map/dot_general | solution.py:204
  17.6 1.5 %fusion.124 = (f32[256]{0:T(256)S(1)}, bf16[4,128,256]{2,1,0:T(8,128)(2,1)}, f32[512,256]{1,0:T(8,128)S(1)}) fusion(bf16[4,256,256]{2,1,0:T(8,128)(2,1)S(1)} %copy-done.2, s32[]{:T(128)S(6)} %select_n.90, f32[256]{0:T(256)S(1)} %copy-done.91, bf16[1024,256]{1,0:T(8,128)(2,1)S(1)} %copy-done.6, f32[512,1024]{1,0:T(8,128)S(1)} %get-tuple-element.156), kind=kOutput, calls=%fused_computation.237 | convolution fusion | flops 273809152 | bytes 3672068 | tf_op jit(solution)/shard_map/dot_general | solution.py:206
  19.0 2.4 %fusion.6 = bf16[512,1024]{1,0:T(8,128)(2,1)S(1)} fusion(f32[512,1024]{1,0:T(8,128)S(1)} %get-tuple-element.156, bf16[512,256]{1,0:T(8,128)(2,1)} %bitcast.52, bf16[1024,256]{1,0:T(8,128)(2,1)S(1)} %copy-done.6), kind=kOutput, calls=%fused_computation.108 | convolution fusion | flops 278396928 | bytes 3932160 | tf_op jit(solution)/shard_map/dot_general | solution.py:207
  21.4 0.6 multiply_reduce_fusion.2
  22.3 1.3 %fusion.171 = (f32[256]{0:T(256)S(1)}, f32[256]{0:T(256)S(1)}, f32[256]{0:T(256)S(1)}, f32[256]{0:T(256)S(1)}, f32[256]{0:T(256)S(1)}, /*index=5*/f32[256]{0:T(2...) fusion(f32[10,134,256]{2,1,0:T(8,128)S(1)} %fusion.23, ...), kind=kLoop, calls=%fused_computation.284 | loop fusion | flops 4584192 | bytes 8148992 | tf_op jit(solution)/shard_map/reduce_sum | solution.py:175
  23.6 1.0 %fusion.172 = (f32[256]{0:T(256)S(1)}, f32[256]{0:T(256)S(1)}, f32[256]{0:T(256)S(1)}, f32[256]{0:T(256)S(1)}, f32[256]{0:T(256)S(1)}, /*index=5*/f32[256]{0:T(2...) fusion(bf16[4,128,256]{2,1,0:T(8,128)(2,1)S(1)} %get-tuple-elem, ...), kind=kLoop, calls=%fused_computation.285 | loop fusion | flops 4845056 | bytes 9717760 | tf_op jit(solution)/shard_map/reduce_sum | solution.py:175
  24.6 1.0 %fusion.173 = (f32[256]{0:T(256)S(1)}, f32[256]{0:T(256)S(1)}, f32[256]{0:T(256)S(1)}, f32[256]{0:T(256)S(1)}, f32[256]{0:T(256)S(1)}, /*index=5*/f32[256]{0:T(2...) fusion(bf16[4,128,256]{2,1,0:T(8,128)(2,1)S(1)} %get-tuple-elem, ...), kind=kLoop, calls=%fused_computation.286 | loop fusion | flops 4845056 | bytes 9717760 | tf_op jit(solution)/shard_map/reduce_sum | solution.py:175
  25.6 0.8 copy.22
  26.6 6.0 %collective-permute-start.6 = (f32[51,256]{1,0:T(8,128)S(1)}, f32[51,256]{1,0:T(8,128)S(1)}, u32[]{:S(2)}, u32[]{:S(2)}) collective-permute-start(f32[51,256]{1,0:T(8,128)S(1)} %concatenate.19), channel_id=1, source_target_pairs={{0,1},{1,0},{2,3},{3,2},{4,5},{5,4},{6,7},{7,6},{8,9},{9,8},{10,11... | collective-permute-start | bytes 156680 | tf_op jit(solution)/shard_map/ppermute | solution.py:112
  32.7 1.5 %copy.25 = bf16[1024,512]{1,0:T(8,128)(2,1)S(1)} copy(bf16[1024,512]{0,1:T(8,128)(2,1)} %get-tuple-element.155) | data formatting | bytes 2097152 | tf_op jit(solution)/shard_map/convert_element_type | solution.py:205
  34.2 1.4 %convolution_bitcast_fusion = f32[2,2,2,2,64,256]{5,4,0,1,2,3:T(8,128)S(1)} fusion(bf16[2,2,2,2,64,512]{5,4,3,2,1,0:T(8,128)(2,1)S(1)} %bitcast.177, bf16[512,256,1,1,1,1]{1,0,5,4,3,2:T(8,128)(2,1)} %bitcast.63), kind=kOutput, calls=%fused_computation.120 | convolution fusion | flops 268435456 | bytes 2359296 | tf_op jit(solution)/shard_map/dot_general | solution.py:220
  35.9 0.7 copy-done.7
  36.5 0.4 copy-done.95
  36.9 0.4 fusion.15
  38.2 2.6 %collective-permute-start.2 = (bf16[3,256,256]{2,1,0:T(8,128)(2,1)S(1)}, bf16[3,256,256]{2,1,0:T(8,128)(2,1)S(1)}, u32[]{:S(2)}, u32[]{:S(2)}) collective-permute-start(bf16[3,256,256]{2,1,0:T(8,128)(2,1)S(1)} %get-tuple-element.89), channel_id=1, source_target_pairs={{0,1},{1,2},{2,3},{3,4},{4,5},{5,6},{6,7},{7,8},{8,9},{9,10},{10,1... | collective-permute-start | bytes 1179656 | tf_op jit(solution)/shard_map/ppermute | solution.py:141
  40.8 1.3 %collective-permute-start.3 = (bf16[3,256,256]{2,1,0:T(8,128)(2,1)S(1)}, bf16[3,256,256]{2,1,0:T(8,128)(2,1)S(1)}, u32[]{:S(2)}, u32[]{:S(2)}) collective-permute-start(bf16[3,256,256]{2,1,0:T(8,128)(2,1)S(1)} %get-tuple-element.90), channel_id=1, source_target_pairs={{1,0},{2,1},{3,2},{4,3},{5,4},{6,5},{7,6},{8,7},{9,8},{10,9},{11,1... | collective-permute-start | bytes 1179656 | tf_op jit(solution)/shard_map/ppermute | solution.py:142
  42.4 3.4 %fusion.117 = f32[4,134,256]{2,1,0:T(8,128)S(1)} fusion(f32[4,128,256]{2,1,0:T(8,128)S(1)} %get-tuple-element.93, f32[256]{0:T(256)S(1)} %bitcast.193, f32[256]{0:T(256)S(1)} %bitcast.248, f32[256]{0:T(256)S(1)} %bitcast.223, f32[256]{0:T(256)S(1)} %bitcast.243, f32[256]{0:T(256)S(1)} %bitcast.238, f32[256]{0:T(256)S(1)} %bitcast.233, f32[256]{0:T(256)S(1)} %bitcast.228, ...), kind=kLoop, calls=%fused_computation.230 | loop fusion | flops 13309952 | bytes 1123328 | tf_op jit(solution)/shard_map/add | solution.py:163
  46.2 0.7 multiply_add_fusion.4
  46.9 1.4 %fusion.197 = f32[1,256,256]{2,1,0:T(8,128)} fusion(f32[3,256,256]{2,1,0:T(8,128)S(1)} %convert_element_type.178, f32[256]{0:T(256)S(1)} %bitcast.359, f32[256]{0:T(256)S(1)} %bitcast.335, f32[256]{0:T(256)S(1)} %bitcast.332, f32[256]{0:T(256)S(1)} %bitcast.329, f32[256]{0:T(256)S(1)} %bitcast.326, f32[256]{0:T(256)S(1)} %bitcast.323, f32[256]{0:T(256)S(1)} %bitcast.320, ...), kind=kLoop, calls=%fused_computation.329 | loop fusion | flops 2686976 | bytes 1856512 | tf_op jit(solution)/shard_map/add | solution.py:275
  48.2 1.4 %multiply_add_fusion.3 = f32[1,256,256]{2,1,0:T(8,128)} fusion(f32[3,256,256]{2,1,0:T(8,128)S(1)} %convert_element_type.179, f32[3,256,256]{2,1,0:T(8,128)S(1)} %convert_element_type.178, f32[256]{0:T(256)S(1)} %bitcast.304, f32[256]{0:T(256)S(1)} %bitcast.300, f32[256]{0:T(256)S(1)} %bitcast.296, f32[256]{0:T(256)S(1)} %bitcast.292, f32[256]{0:T(256)S(1)} %bitcast.316, ...), kind=kLoop, calls=%fused_computation.351 | loop fusion | flops 2686976 | bytes 2642944 | tf_op jit(solution)/shard_map/add | solution.py:275
  49.9 8.3 %collective-permute-start.9 = (bf16[358,256]{1,0:T(8,128)(2,1)S(1)}, bf16[358,256]{1,0:T(8,128)(2,1)S(1)}, u32[]{:S(2)}, u32[]{:S(2)}) collective-permute-start(bf16[358,256]{1,0:T(8,128)(2,1)S(1)} %get-tuple-element.101), channel_id=1, source_target_pairs={{0,6},{1,7},{2,4},{3,5},{4,2},{5,3},{6,0},{7,1},{8,14},{9,15},{10,... | collective-permute-start | bytes 549896 | tf_op jit(solution)/shard_map/ppermute | solution.py:70
  58.2 1.4 %fusion.179 = f32[1,256,256]{2,1,0:T(8,128)} fusion(f32[3,256,256]{2,1,0:T(8,128)S(1)} %convert_element_type.179, f32[256]{0:T(256)S(1)} %bitcast.356, f32[256]{0:T(256)S(1)} %bitcast.353, f32[256]{0:T(256)S(1)} %bitcast.350, f32[256]{0:T(256)S(1)} %bitcast.347, f32[256]{0:T(256)S(1)} %bitcast.344, f32[256]{0:T(256)S(1)} %bitcast.341, f32[256]{0:T(256)S(1)} %bitcast.338, ...), kind=kLoop, calls=%fused_computation.310 | loop fusion | flops 2686976 | bytes 1856512 | tf_op jit(solution)/shard_map/add | solution.py:275
  59.7 0.4 collective-permute-start.7
  60.1 2.8 %collective-permute-done.9 = bf16[358,256]{1,0:T(8,128)(2,1)S(1)} collective-permute-done((bf16[358,256]{1,0:T(8,128)(2,1)S(1)}, bf16[358,256]{1,0:T(8,128)(2,1)S(1)}, u32[]{:S(2)}, u32[]{:S(2)}) %collective-permute-start.9) | collective-permute-done | bytes 183328 | tf_op jit(solution)/shard_map/ppermute | solution.py:70
  62.9 4.7 %collective-permute-done.8 = bf16[358,256]{1,0:T(8,128)(2,1)S(1)} collective-permute-done((bf16[358,256]{1,0:T(8,128)(2,1)S(1)}, bf16[358,256]{1,0:T(8,128)(2,1)S(1)}, u32[]{:S(2)}, u32[]{:S(2)}) %collective-permute-start.8) | collective-permute-done | bytes 183328 | tf_op jit(solution)/shard_map/ppermute | solution.py:70
  67.6 0.6 copy-done.9
  68.3 0.7 copy-done.10
  69.0 0.7 pad_maximum_fusion.6
  69.7 2.3 %gather_fusion = f32[4,51,256]{2,1,0:T(8,128)} fusion(f32[4,51,256]{2,1,0:T(8,128)} %pad_maximum_fusion.6, s32[1024]{0:T(1024)} %pad_clamp_fusion), kind=kCustom, calls=%fused_computation | custom fusion | bytes 417808 | tf_op jit(solution)/shard_map/gather | solution.py:76
  72.0 1.0 %fusion.213 = f32[51,256]{1,0:T(8,128)S(1)} fusion(f32[4,51,256]{2,1,0:T(8,128)} %gather_fusion), kind=kLoop, calls=%fused_computation.398 | loop fusion | flops 39168 | bytes 261120 | tf_op jit(solution)/shard_map/add | solution.py:77
  73.0 0.8 slice.1296
  73.8 0.8 slice.1297
  74.7 0.8 slice.1298
  75.5 0.9 %convert_add_fusion.3 = f32[128,256]{1,0:T(8,128)S(1)} fusion(f32[512,256]{1,0:T(8,128)S(1)} %dynamic-slice_add_fusion, s32[]{:T(128)S(6)} %select_n.108, bf16[358,256]{1,0:T(8,128)(2,1)} %copy-done.8, bf16[358,256]{1,0:T(8,128)(2,1)} %copy-done.9, bf16[358,256]{1,0:T(8,128)(2,1)} %copy-done.10), kind=kLoop, calls=%fused_computation.377 | loop fusion | flops 196608 | bytes 458756 | tf_op jit(solution)/shard_map/add | solution.py:72
  76.6 2.8 %collective-permute-start.10 = (bf16[230,256]{1,0:T(8,128)(2,1)S(1)}, bf16[230,256]{1,0:T(8,128)(2,1)S(1)}, u32[]{:S(2)}, u32[]{:S(2)}) collective-permute-start(bf16[230,256]{1,0:T(8,128)(2,1)S(1)} %pad_maximum_fusion.7), channel_id=1, source_target_pairs={{0,8},{1,9},{2,10},{3,11},{4,12},{5,13},{6,14},{7,15},{8,0},{9,1},... | collective-permute-start | bytes 353288 | tf_op jit(solution)/shard_map/ppermute | solution.py:120
  79.4 1.0 %fusion.18 = bf16[4,256,256]{2,1,0:T(8,128)(2,1)} fusion(f32[1,256,256]{2,1,0:T(8,128)S(1)} %copy-done.5, f32[1,256,256]{2,1,0:T(8,128)S(1)} %copy-done.4, f32[1,256,256]{2,1,0:T(8,128)S(1)} %multiply_add_fusion.4, f32[1,256,256]{2,1,0:T(8,128)S(1)} %copy-done.3, f32[4,131,256]{2,1,0:T(8,128)S(1)} %get-tuple-element.80, ...), kind=kLoop, calls=%fused_computation.129 | loop fusion | flops 2359296 | bytes 3170306 | tf_op jit(solution)/shard_map/convert_element_type | solution.py:278
  80.4 5.0 %collective-permute-done.10 = bf16[230,256]{1,0:T(8,128)(2,1)S(1)} collective-permute-done((bf16[230,256]{1,0:T(8,128)(2,1)S(1)}, bf16[230,256]{1,0:T(8,128)(2,1)S(1)}, u32[]{:S(2)}, u32[]{:S(2)}) %collective-permute-start.10) | collective-permute-done | bytes 117792 | tf_op jit(solution)/shard_map/ppermute | solution.py:120
  85.4 0.6 fusion.212
  86.0 0.6 convert_add_fusion.7
  86.6 0.6 copy.30
  (239 shorter events, 3.3 us)
Async XLA Ops:
  0.6 15.1 %copy-start = (bf16[256,1024]{1,0:T(8,128)(2,1)S(1)}, bf16[256,1024]{1,0:T(8,128)(2,1)}, u32[]{:S(2)}) copy-start(bf16[256,1024]{1,0:T(8,128)(2,1)} %param.12) | copy-start | bytes 1572868
  1.8 6.7 %collective-permute-start = (bf16[3,256,256]{2,1,0:T(8,128)(2,1)S(1)}, bf16[3,256,256]{2,1,0:T(8,128)(2,1)S(1)}, u32[]{:S(2)}, u32[]{:S(2)}) collective-permute-start(bf16[3,256,256]{2,1,0:T(8,128)(2,1)S(1)} %get-tuple-element.92), channel_id=1, source_target_pairs={{0,1},{1,2},{2,3},{3,4},{4,5},{5,6},{6,7},{7,8},{8,9},{9,10},{10,1... | collective-permute-start | bytes 1179656 | tf_op jit(solution)/shard_map/ppermute | solution.py:21
  4.2 5.7 %collective-permute-start.1 = (bf16[3,256,256]{2,1,0:T(8,128)(2,1)S(1)}, bf16[3,256,256]{2,1,0:T(8,128)(2,1)S(1)}, u32[]{:S(2)}, u32[]{:S(2)}) collective-permute-start(bf16[3,256,256]{2,1,0:T(8,128)(2,1)S(1)} %get-tuple-element.91), channel_id=1, source_target_pairs={{1,0},{2,1},{3,2},{4,3},{5,4},{6,5},{7,6},{8,7},{9,8},{10,9},{11,1... | collective-permute-start | bytes 1179656 | tf_op jit(solution)/shard_map/ppermute | solution.py:24
  7.0 7.9 %copy-start.24 = (f32[1,1,256]{2,1,0:T(1,128)}, f32[1,1,256]{2,1,0:T(1,128)S(1)}, u32[]{:S(2)}) copy-start(f32[1,1,256]{2,1,0:T(1,128)S(1)} %get-tuple-element.109) | copy-start | bytes 3076
  7.0 7.9 %copy-start.26 = (f32[1,1,256]{2,1,0:T(1,128)}, f32[1,1,256]{2,1,0:T(1,128)S(1)}, u32[]{:S(2)}) copy-start(f32[1,1,256]{2,1,0:T(1,128)S(1)} %get-tuple-element.110) | copy-start | bytes 3076
  7.0 7.9 %copy-start.28 = (f32[1,1,256]{2,1,0:T(1,128)}, f32[1,1,256]{2,1,0:T(1,128)S(1)}, u32[]{:S(2)}) copy-start(f32[1,1,256]{2,1,0:T(1,128)S(1)} %get-tuple-element.111) | copy-start | bytes 3076
  7.0 7.9 %copy-start.30 = (f32[1,1,256]{2,1,0:T(1,128)}, f32[1,1,256]{2,1,0:T(1,128)S(1)}, u32[]{:S(2)}) copy-start(f32[1,1,256]{2,1,0:T(1,128)S(1)} %get-tuple-element.112) | copy-start | bytes 3076
  7.0 7.9 %copy-start.32 = (f32[1,1,256]{2,1,0:T(1,128)}, f32[1,1,256]{2,1,0:T(1,128)S(1)}, u32[]{:S(2)}) copy-start(f32[1,1,256]{2,1,0:T(1,128)S(1)} %get-tuple-element.113) | copy-start | bytes 3076
  7.0 7.9 %copy-start.34 = (f32[1,1,256]{2,1,0:T(1,128)}, f32[1,1,256]{2,1,0:T(1,128)S(1)}, u32[]{:S(2)}) copy-start(f32[1,1,256]{2,1,0:T(1,128)S(1)} %get-tuple-element.114) | copy-start | bytes 3076
  7.0 7.9 %copy-start.36 = (f32[1,1,256]{2,1,0:T(1,128)}, f32[1,1,256]{2,1,0:T(1,128)S(1)}, u32[]{:S(2)}) copy-start(f32[1,1,256]{2,1,0:T(1,128)S(1)} %get-tuple-element.115) | copy-start | bytes 3076
  7.0 7.9 %copy-start.52 = (f32[1,1,256]{2,1,0:T(1,128)}, f32[1,1,256]{2,1,0:T(1,128)S(1)}, u32[]{:S(2)}) copy-start(f32[1,1,256]{2,1,0:T(1,128)S(1)} %get-tuple-element.116) | copy-start | bytes 3076
  7.0 7.9 %copy-start.54 = (f32[1,1,256]{2,1,0:T(1,128)}, f32[1,1,256]{2,1,0:T(1,128)S(1)}, u32[]{:S(2)}) copy-start(f32[1,1,256]{2,1,0:T(1,128)S(1)} %get-tuple-element.117) | copy-start | bytes 3076
  7.0 7.9 %copy-start.56 = (f32[1,1,256]{2,1,0:T(1,128)}, f32[1,1,256]{2,1,0:T(1,128)S(1)}, u32[]{:S(2)}) copy-start(f32[1,1,256]{2,1,0:T(1,128)S(1)} %get-tuple-element.118) | copy-start | bytes 3076
  7.1 7.9 %copy-start.58 = (f32[1,1,256]{2,1,0:T(1,128)}, f32[1,1,256]{2,1,0:T(1,128)S(1)}, u32[]{:S(2)}) copy-start(f32[1,1,256]{2,1,0:T(1,128)S(1)} %get-tuple-element.119) | copy-start | bytes 3076
  7.1 7.9 %copy-start.60 = (f32[1,1,256]{2,1,0:T(1,128)}, f32[1,1,256]{2,1,0:T(1,128)S(1)}, u32[]{:S(2)}) copy-start(f32[1,1,256]{2,1,0:T(1,128)S(1)} %get-tuple-element.120) | copy-start | bytes 3076
  7.1 7.9 %copy-start.62 = (f32[1,1,256]{2,1,0:T(1,128)}, f32[1,1,256]{2,1,0:T(1,128)S(1)}, u32[]{:S(2)}) copy-start(f32[1,1,256]{2,1,0:T(1,128)S(1)} %get-tuple-element.121) | copy-start | bytes 3076
  7.7 7.2 %copy-start.12 = (f32[1,1,256]{2,1,0:T(1,128)}, f32[1,1,256]{2,1,0:T(1,128)S(1)}, u32[]{:S(2)}) copy-start(f32[1,1,256]{2,1,0:T(1,128)S(1)} %get-tuple-element.147) | copy-start | bytes 3076
  7.7 7.2 %copy-start.14 = (f32[1,1,256]{2,1,0:T(1,128)}, f32[1,1,256]{2,1,0:T(1,128)S(1)}, u32[]{:S(2)}) copy-start(f32[1,1,256]{2,1,0:T(1,128)S(1)} %get-tuple-element.148) | copy-start | bytes 3076
  7.7 7.2 %copy-start.16 = (f32[1,1,256]{2,1,0:T(1,128)}, f32[1,1,256]{2,1,0:T(1,128)S(1)}, u32[]{:S(2)}) copy-start(f32[1,1,256]{2,1,0:T(1,128)S(1)} %get-tuple-element.149) | copy-start | bytes 3076
  7.7 7.2 %copy-start.20 = (f32[1,1,256]{2,1,0:T(1,128)}, f32[1,1,256]{2,1,0:T(1,128)S(1)}, u32[]{:S(2)}) copy-start(f32[1,1,256]{2,1,0:T(1,128)S(1)} %get-tuple-element.150) | copy-start | bytes 3076
  7.7 7.2 %copy-start.22 = (f32[1,1,256]{2,1,0:T(1,128)}, f32[1,1,256]{2,1,0:T(1,128)S(1)}, u32[]{:S(2)}) copy-start(f32[1,1,256]{2,1,0:T(1,128)S(1)} %get-tuple-element.151) | copy-start | bytes 3076
  7.8 7.2 %copy-start.38 = (f32[1,1,256]{2,1,0:T(1,128)}, f32[1,1,256]{2,1,0:T(1,128)S(1)}, u32[]{:S(2)}) copy-start(f32[1,1,256]{2,1,0:T(1,128)S(1)} %get-tuple-element.142) | copy-start | bytes 3076
  7.8 7.2 %copy-start.40 = (f32[1,1,256]{2,1,0:T(1,128)}, f32[1,1,256]{2,1,0:T(1,128)S(1)}, u32[]{:S(2)}) copy-start(f32[1,1,256]{2,1,0:T(1,128)S(1)} %get-tuple-element.143) | copy-start | bytes 3076
  7.8 7.2 %copy-start.42 = (f32[1,1,256]{2,1,0:T(1,128)}, f32[1,1,256]{2,1,0:T(1,128)S(1)}, u32[]{:S(2)}) copy-start(f32[1,1,256]{2,1,0:T(1,128)S(1)} %get-tuple-element.144) | copy-start | bytes 3076
  7.8 7.2 %copy-start.44 = (f32[1,1,256]{2,1,0:T(1,128)}, f32[1,1,256]{2,1,0:T(1,128)S(1)}, u32[]{:S(2)}) copy-start(f32[1,1,256]{2,1,0:T(1,128)S(1)} %get-tuple-element.145) | copy-start | bytes 3076
  8.4 6.7 %copy-start.64 = (f32[1,1,256]{2,1,0:T(1,128)}, f32[1,1,256]{2,1,0:T(1,128)S(1)}, u32[]{:S(2)}) copy-start(f32[1,1,256]{2,1,0:T(1,128)S(1)} %get-tuple-element.131) | copy-start | bytes 3076
  8.4 6.7 %copy-start.66 = (f32[1,1,256]{2,1,0:T(1,128)}, f32[1,1,256]{2,1,0:T(1,128)S(1)}, u32[]{:S(2)}) copy-start(f32[1,1,256]{2,1,0:T(1,128)S(1)} %get-tuple-element.132) | copy-start | bytes 3076
  8.4 6.7 %copy-start.68 = (f32[1,1,256]{2,1,0:T(1,128)}, f32[1,1,256]{2,1,0:T(1,128)S(1)}, u32[]{:S(2)}) copy-start(f32[1,1,256]{2,1,0:T(1,128)S(1)} %get-tuple-element.133) | copy-start | bytes 3076
  8.4 6.7 %copy-start.70 = (f32[1,1,256]{2,1,0:T(1,128)}, f32[1,1,256]{2,1,0:T(1,128)S(1)}, u32[]{:S(2)}) copy-start(f32[1,1,256]{2,1,0:T(1,128)S(1)} %get-tuple-element.134) | copy-start | bytes 3076
  8.4 6.7 %copy-start.72 = (f32[1,1,256]{2,1,0:T(1,128)}, f32[1,1,256]{2,1,0:T(1,128)S(1)}, u32[]{:S(2)}) copy-start(f32[1,1,256]{2,1,0:T(1,128)S(1)} %get-tuple-element.135) | copy-start | bytes 3076
  8.4 6.7 %copy-start.74 = (f32[1,1,256]{2,1,0:T(1,128)}, f32[1,1,256]{2,1,0:T(1,128)S(1)}, u32[]{:S(2)}) copy-start(f32[1,1,256]{2,1,0:T(1,128)S(1)} %get-tuple-element.136) | copy-start | bytes 3076
  8.4 6.7 %copy-start.76 = (f32[1,1,256]{2,1,0:T(1,128)}, f32[1,1,256]{2,1,0:T(1,128)S(1)}, u32[]{:S(2)}) copy-start(f32[1,1,256]{2,1,0:T(1,128)S(1)} %get-tuple-element.137) | copy-start | bytes 3076
  8.5 6.7 %copy-start.78 = (f32[1,1,256]{2,1,0:T(1,128)}, f32[1,1,256]{2,1,0:T(1,128)S(1)}, u32[]{:S(2)}) copy-start(f32[1,1,256]{2,1,0:T(1,128)S(1)} %get-tuple-element.123) | copy-start | bytes 3076
  8.5 6.7 %copy-start.81 = (f32[1,1,256]{2,1,0:T(1,128)}, f32[1,1,256]{2,1,0:T(1,128)S(1)}, u32[]{:S(2)}) copy-start(f32[1,1,256]{2,1,0:T(1,128)S(1)} %get-tuple-element.124) | copy-start | bytes 3076
  8.5 6.7 %copy-start.83 = (f32[1,1,256]{2,1,0:T(1,128)}, f32[1,1,256]{2,1,0:T(1,128)S(1)}, u32[]{:S(2)}) copy-start(f32[1,1,256]{2,1,0:T(1,128)S(1)} %get-tuple-element.125) | copy-start | bytes 3076
  26.6 19.4 %collective-permute-start.6 = (f32[51,256]{1,0:T(8,128)S(1)}, f32[51,256]{1,0:T(8,128)S(1)}, u32[]{:S(2)}, u32[]{:S(2)}) collective-permute-start(f32[51,256]{1,0:T(8,128)S(1)} %concatenate.19), channel_id=1, source_target_pairs={{0,1},{1,0},{2,3},{3,2},{4,5},{5,4},{6,7},{7,6},{8,9},{9,8},{10,11... | collective-permute-start | bytes 156680 | tf_op jit(solution)/shard_map/ppermute | solution.py:112
  35.8 13.8 %collective-permute-start.5 = (f32[512,256]{1,0:T(8,128)S(1)}, f32[512,256]{1,0:T(8,128)S(1)}, u32[]{:S(2)}, u32[]{:S(2)}) collective-permute-start(f32[512,256]{1,0:T(8,128)S(1)} %constant_dynamic-slice_fusion), channel_id=1, source_target_pairs={{0,1},{1,0},{2,3},{3,2},{4,5},{5,4},{6,7},{7,6},{8,9},{9,8},{10,11... | collective-permute-start | bytes 1572872 | tf_op jit(solution)/shard_map/ppermute | solution.py:112
  37.9 11.8 %collective-permute-start.4 = (f32[4,128,256]{2,1,0:T(8,128)S(1)}, f32[4,128,256]{2,1,0:T(8,128)S(1)}, u32[]{:S(2)}, u32[]{:S(2)}) collective-permute-start(f32[4,128,256]{2,1,0:T(8,128)S(1)} %constant_dynamic-slice_fusion.1), channel_id=1, source_target_pairs={{0,1},{1,0},{2,3},{3,2},{4,5},{5,4},{6,7},{7,6},{8,9},{9,8},{10,11... | collective-permute-start | bytes 1572872 | tf_op jit(solution)/shard_map/ppermute | solution.py:112
  38.1 7.8 %copy-start.92 = (f32[256]{0:T(256)S(1)}, f32[256]{0:T(256)}, u32[]{:S(2)}) copy-start(f32[256]{0:T(256)} %param.14) | copy-start | bytes 3076
  38.2 7.9 %collective-permute-start.2 = (bf16[3,256,256]{2,1,0:T(8,128)(2,1)S(1)}, bf16[3,256,256]{2,1,0:T(8,128)(2,1)S(1)}, u32[]{:S(2)}, u32[]{:S(2)}) collective-permute-start(bf16[3,256,256]{2,1,0:T(8,128)(2,1)S(1)} %get-tuple-element.89), channel_id=1, source_target_pairs={{0,1},{1,2},{2,3},{3,4},{4,5},{5,6},{6,7},{7,8},{8,9},{9,10},{10,1... | collective-permute-start | bytes 1179656 | tf_op jit(solution)/shard_map/ppermute | solution.py:141
  40.8 5.4 %collective-permute-start.3 = (bf16[3,256,256]{2,1,0:T(8,128)(2,1)S(1)}, bf16[3,256,256]{2,1,0:T(8,128)(2,1)S(1)}, u32[]{:S(2)}, u32[]{:S(2)}) collective-permute-start(bf16[3,256,256]{2,1,0:T(8,128)(2,1)S(1)} %get-tuple-element.90), channel_id=1, source_target_pairs={{1,0},{2,1},{3,2},{4,3},{5,4},{6,5},{7,6},{8,7},{9,8},{10,9},{11,1... | collective-permute-start | bytes 1179656 | tf_op jit(solution)/shard_map/ppermute | solution.py:142
  49.9 13.0 %collective-permute-start.9 = (bf16[358,256]{1,0:T(8,128)(2,1)S(1)}, bf16[358,256]{1,0:T(8,128)(2,1)S(1)}, u32[]{:S(2)}, u32[]{:S(2)}) collective-permute-start(bf16[358,256]{1,0:T(8,128)(2,1)S(1)} %get-tuple-element.101), channel_id=1, source_target_pairs={{0,6},{1,7},{2,4},{3,5},{4,2},{5,3},{6,0},{7,1},{8,14},{9,15},{10,... | collective-permute-start | bytes 549896 | tf_op jit(solution)/shard_map/ppermute | solution.py:70
  59.5 8.1 %collective-permute-start.8 = (bf16[358,256]{1,0:T(8,128)(2,1)S(1)}, bf16[358,256]{1,0:T(8,128)(2,1)S(1)}, u32[]{:S(2)}, u32[]{:S(2)}) collective-permute-start(bf16[358,256]{1,0:T(8,128)(2,1)S(1)} %get-tuple-element.102), channel_id=1, source_target_pairs={{0,2},{1,3},{2,0},{3,1},{4,6},{5,7},{6,4},{7,5},{8,10},{9,11},{10,... | collective-permute-start | bytes 549896 | tf_op jit(solution)/shard_map/ppermute | solution.py:70
  59.7 8.5 %collective-permute-start.7 = (bf16[358,256]{1,0:T(8,128)(2,1)S(1)}, bf16[358,256]{1,0:T(8,128)(2,1)S(1)}, u32[]{:S(2)}, u32[]{:S(2)}) collective-permute-start(bf16[358,256]{1,0:T(8,128)(2,1)S(1)} %get-tuple-element.100), channel_id=1, source_target_pairs={{0,4},{1,5},{2,6},{3,7},{4,0},{5,1},{6,2},{7,3},{8,12},{9,13},{10,... | collective-permute-start | bytes 549896 | tf_op jit(solution)/shard_map/ppermute | solution.py:70
  72.0 7.4 %copy-start.3 = (f32[1,256,256]{2,1,0:T(8,128)S(1)}, f32[1,256,256]{2,1,0:T(8,128)}, u32[]{:S(2)}) copy-start(f32[1,256,256]{2,1,0:T(8,128)} %fusion.197) | copy-start | bytes 786436
  72.0 7.4 %copy-start.4 = (f32[1,256,256]{2,1,0:T(8,128)S(1)}, f32[1,256,256]{2,1,0:T(8,128)}, u32[]{:S(2)}) copy-start(f32[1,256,256]{2,1,0:T(8,128)} %multiply_add_fusion.3) | copy-start | bytes 786436
  72.0 7.4 %copy-start.5 = (f32[1,256,256]{2,1,0:T(8,128)S(1)}, f32[1,256,256]{2,1,0:T(8,128)}, u32[]{:S(2)}) copy-start(f32[1,256,256]{2,1,0:T(8,128)} %fusion.179) | copy-start | bytes 786436
  76.6 8.8 %collective-permute-start.10 = (bf16[230,256]{1,0:T(8,128)(2,1)S(1)}, bf16[230,256]{1,0:T(8,128)(2,1)S(1)}, u32[]{:S(2)}, u32[]{:S(2)}) collective-permute-start(bf16[230,256]{1,0:T(8,128)(2,1)S(1)} %pad_maximum_fusion.7), channel_id=1, source_target_pairs={{0,8},{1,9},{2,10},{3,11},{4,12},{5,13},{6,14},{7,15},{8,0},{9,1},... | collective-permute-start | bytes 353288 | tf_op jit(solution)/shard_map/ppermute | solution.py:120
  (59 other events, 260.0 us)

commit v20 on v18

--- a/solution.py
+++ b/solution.py
@@ -181,7 +181,14 @@
     grad_norm = grad_norm.reshape(image_rows, TILE_COLS, channels)
     image_tile = lax.dynamic_slice_in_dim(image, first_col, TILE_COLS, axis=1)
     out_tile = (image_tile.astype(jnp.float32) + 1.0 * layer_scale * branch).astype(jnp.bfloat16)
-    block_out = lax.dynamic_update_slice_in_dim(image, out_tile, first_col, axis=1)
+    tile_index = first_col // TILE_COLS
+    tiles = image_cols // TILE_COLS
+    block_out = image
+    for tile in range(tiles):
+        placed = jnp.concatenate(
+            [image[:, : tile * TILE_COLS], out_tile, image[:, (tile + 1) * TILE_COLS :]], axis=1
+        )
+        block_out = jnp.where(tile_index == tile, placed, block_out)
     scale_grad = jnp.sum(1.0 * branch * upstream, axis=(0, 1))
     gain_grad = jnp.sum(grad_norm * standard, axis=(0, 1))
     grad_std = grad_norm * ln_gain
@@ -203,16 +210,18 @@
         ((half_width, half_width), (2 * half_width, 2 * half_width), (0, 0)),
     )
     own = depthwise(tile_padded, flipped, image_rows, span)
-    tile_index = first_col // TILE_COLS
     own_full = jnp.zeros((image_rows, image_cols, channels), jnp.float32)
     for tile in range(image_cols // TILE_COLS):
         left = tile * TILE_COLS - half_width
         lo, hi = max(left, 0), min(left + span, image_cols)
         placed = jnp.pad(own[:, lo - left : hi - left], ((0, 0), (lo, image_cols - hi), (0, 0)))
         own_full = jnp.where(tile_index == tile, placed, own_full)
-    grad_conv = lax.dynamic_update_slice_in_dim(
-        jnp.zeros_like(image), grad_tile, first_col, axis=1
-    )
+    grad_conv = jnp.zeros_like(image)
+    for tile in range(tiles):
+        placed = jnp.pad(
+            grad_tile, ((0, 0), (tile * TILE_COLS, image_cols - (tile + 1) * TILE_COLS), (0, 0))
+        )
+        grad_conv = jnp.where(tile_index == tile, placed, grad_conv)
     low, high = halo_rows(grad_conv, "row", half_width)
     edge = ((0, 0), (half_width, half_width), (0, 0))
     low = jnp.pad(low.astype(jnp.float32), edge)

time: 79.8 us -> 80.4 us (level)
  starting transfers between devices: 27.6 us -> 24.1 us
  local copies, waits for them, and re-layouts: 7.63 us -> 11 us
  other arithmetic: 18.6 us -> 21.2 us
  waiting for transfers between devices: 16 us -> 14 us
    slice x3, local copies, waits for them, and re-layouts: 0.61 us -> 3.5 us  [depthwise(): kernel[row_tap, col_tap]]
    ppermute x3, starting transfers between devices: 6.2 us -> 3.83 us  [halving_reduce(): got_q, got_r, got_whole = lax.ppermute((give_q, give_r, whole), axis, pairs)]
    ppermute x1, waiting for transfers between devices: 2.01 us -> 0.01 us  [padded_2(): lax.ppermute(lax.slice_in_dim(block, 0, width, axis=dim), axis, backward)]
    unnamed x183 -> x178, local copies, waits for them, and re-layouts: 3.24 us -> 1.75 us
    ppermute x3, starting transfers between devices: 13.8 us -> 12.5 us  [halving_reduce(): got = lax.ppermute(sent, axis, pairs)]
    slice x1, local copies, waits for them, and re-layouts: 0.05 us -> 1.25 us  [padded_2(): lax.slice_in_dim(block, 0, width, axis=dim)]
    select_n x0 -> x2, other arithmetic: none -> 1.15 us  [the longest x1 1.01 us: shards(): block_out = jnp.where(tile_index == tile, placed, block_out)]
    reduce_sum x0 -> x1, other arithmetic: none -> 0.86 us  [shards(): scale_grad = jnp.sum(1.0 * branch * upstream, axis=(0, 1))]
  transfers between devices with their start and end apart: 10 -> 10, of which waited for: 4 -> 3; matrix products, arithmetic and copies ran while one was open for 16% -> 22% of each run, Pallas kernels for 0% -> 0%
where the time goes in v20:
time: 80.4 us; the launch traced here: 79.9 us
  starting transfers between devices  24.1 us (30%)
  other arithmetic  21.2 us (26%)
  waiting for transfers between devices  14 us (17%)
  local copies, waits for them, and re-layouts  11 us (14%)
  matrix products  6.47 us (8%)
  between operations  3.08 us (4%)
    ppermute x3, waiting for transfers between devices, halving_reduce(): got = lax.ppermute(sent, axis, pairs)  14 us
    ppermute x3, starting transfers between devices, halving_reduce(): got = lax.ppermute(sent, axis, pairs)  12.5 us
    reduce_sum x1, other arithmetic, shards(): centre = jnp.mean(filtered, axis=-1, keepdims=True)  4.53 us
    ppermute x3, starting transfers between devices, halving_reduce(): got_q, got_r, got_whole = lax.ppermute((give_q, give_r, whole), axis, pairs)  3.83 us
    slice x3, local copies, waits for them, and re-layouts, depthwise(): kernel[row_tap, col_tap]  3.5 us
    add x1, other arithmetic, depthwise(): total + padded[row_tap:row_tap + image_rows, col_tap:col_tap + image_cols...  3.37 us
    reduce_sum x3, other arithmetic, kernel_terms(): jnp.sum(padded[row_tap:row_tap + image_rows, col_tap:col_tap + image_cols...  3.25 us
    add x4, other arithmetic, shards(): total + line[col_tap:col_tap + image_cols] * flipped[row_tap, col_tap]  2.66 us
  transfers between devices with their start and end apart: 10, of which 3 were waited for; matrix products, arithmetic and copies ran while one was open for 22% of the time, Pallas kernels for 0%

profile of v20, /device:TPU:0, one launch (start us, length us, event | category | flops | bytes accessed | tf_op | source)
XLA Modules:
  0.0 79.9 jit_solution(9639049926204614550)
XLA Ops:
  0.7 1.3 %fusion.222 = (bf16[3,256,256]{2,1,0:T(8,128)(2,1)S(1)}, bf16[3,256,256]{2,1,0:T(8,128)(2,1)S(1)}) fusion(bf16[4,256,256]{2,1,0:T(8,128)(2,1)} %param.8), kind=kLoop, calls=%fused_computation.410 | loop fusion | bytes 1572864 | tf_op jit(solution)/shard_map/slice | solution.py:24
  1.9 2.4 %collective-permute-start = (bf16[3,256,256]{2,1,0:T(8,128)(2,1)S(1)}, bf16[3,256,256]{2,1,0:T(8,128)(2,1)S(1)}, u32[]{:S(2)}, u32[]{:S(2)}) collective-permute-start(bf16[3,256,256]{2,1,0:T(8,128)(2,1)S(1)} %get-tuple-element.94), channel_id=1, source_target_pairs={{0,1},{1,2},{2,3},{3,4},{4,5},{5,6},{6,7},{7,8},{8,9},{9,10},{10,1... | collective-permute-start | bytes 1179656 | tf_op jit(solution)/shard_map/ppermute | solution.py:21
  4.3 1.3 %collective-permute-start.1 = (bf16[3,256,256]{2,1,0:T(8,128)(2,1)S(1)}, bf16[3,256,256]{2,1,0:T(8,128)(2,1)S(1)}, u32[]{:S(2)}, u32[]{:S(2)}) collective-permute-start(bf16[3,256,256]{2,1,0:T(8,128)(2,1)S(1)} %get-tuple-element.93), channel_id=1, source_target_pairs={{1,0},{2,1},{3,2},{4,3},{5,4},{6,5},{7,6},{8,7},{9,8},{10,9},{11,1... | collective-permute-start | bytes 1179656 | tf_op jit(solution)/shard_map/ppermute | solution.py:24
  5.6 1.0 %fusion.226 = (f32[1,1,256]{2,1,0:T(1,128)S(1)}, f32[1,1,256]{2,1,0:T(1,128)S(1)}, f32[1,1,256]{2,1,0:T(1,128)S(1)}, f32[1,1,256]{2,1,0:T(1,128)S(1)}, f32[1,1,2...) fusion(f32[7,7,256]{2,1,0:T(8,128)} %param.10), kind=kLoop, calls=%fused_computation.414 | loop fusion | bytes 38912 | tf_op jit(solution)/shard_map/slice | solution.py:122
  6.7 1.6 %fusion.227 = (f32[1,1,256]{2,1,0:T(1,128)S(1)}, f32[1,1,256]{2,1,0:T(1,128)S(1)}, f32[1,1,256]{2,1,0:T(1,128)S(1)}, f32[1,1,256]{2,1,0:T(1,128)S(1)}, f32[1,1,2...) fusion(f32[7,7,256]{2,1,0:T(8,128)} %param.10), kind=kLoop, calls=%fused_computation.415 | loop fusion | bytes 38912 | tf_op jit(solution)/shard_map/slice | solution.py:122
  8.5 1.3 %bitcast_reduce_fusion = (s32[]{:T(128)}, s32[]{:T(128)}) fusion(s32[1,2]{1,0:T(1,128)} %param.9), kind=kLoop, calls=%fused_computation.401 | loop fusion | flops 7 | bytes 16 | tf_op jit(solution)/shard_map/shards/reduce | solution.py:146
  10.5 0.9 %fusion.228 = (f32[1,1,256]{2,1,0:T(1,128)S(1)}, f32[1,1,256]{2,1,0:T(1,128)S(1)}, f32[1,1,256]{2,1,0:T(1,128)S(1)}, f32[1,1,256]{2,1,0:T(1,128)S(1)}, f32[1,1,2...) fusion(f32[7,7,256]{2,1,0:T(8,128)} %param.10), kind=kLoop, calls=%fused_computation.416 | loop fusion | bytes 22528 | tf_op jit(solution)/shard_map/slice | solution.py:122
  11.5 0.8 %fusion.221 = (bf16[4,128,256]{2,1,0:T(8,128)(2,1)}, bf16[4,128,256]{2,1,0:T(8,128)(2,1)}) fusion(bf16[4,256,256]{2,1,0:T(8,128)(2,1)S(1)} %copy-done.1), kind=kLoop, calls=%fused_computation.409 | loop fusion | bytes 1048576 | tf_op jit(solution)/shard_map/slice | solution.py:189
  12.4 0.3 fusion.23
  12.9 4.5 %fusion.218 = (f32[4,128]{1,0:T(4,128)S(1)}, f32[4,128,256]{2,1,0:T(8,128)S(1)}) fusion(f32[256]{0:T(256)S(1)} %bitcast.237, f32[10,134,256]{2,1,0:T(8,128)S(1)} %fusion.23, f32[256]{0:T(256)S(1)} %bitcast.242, f32[256]{0:T(256)S(1)} %bitcast.187, f32[256]{0:T(256)S(1)} %bitcast.192, f32[256]{0:T(256)S(1)} %bitcast.197, f32[256]{0:T(256)S(1)} %bitcast.202, ...), kind=kLoop, calls=%fused_computation.406 | loop fusion | flops 12844544 | bytes 26266624 | tf_op jit(solution)/shard_map/reduce_sum | solution.py:151
  17.7 0.2 multiply_reduce_fusion.3
  17.9 0.2 multiply_convert_fusion.3
  18.2 1.9 %fusion.11 = (bf16[1024,512]{0,1:T(8,128)(2,1)}, f32[512,1024]{1,0:T(8,128)S(1)}) fusion(bf16[512,256]{1,0:T(8,128)(2,1)S(1)} %bitcast.167, bf16[256,1024]{1,0:T(8,128)(2,1)S(1)} %copy-done), kind=kOutput, calls=%fused_computation.112 | convolution fusion | flops 273154048 | bytes 3932160 | tf_op jit(solution)/shard_map/dot_general | solution.py:161
  20.0 0.8 fusion.19
  20.8 0.2 copy-done.2
  21.1 0.9 %fusion.124 = (f32[256]{0:T(256)S(1)}, bf16[4,128,256]{2,1,0:T(8,128)(2,1)S(1)}, bf16[4,128,256]{2,1,0:T(8,128)(2,1)}) fusion(bf16[4,256,256]{2,1,0:T(8,128)(2,1)S(1)} %copy-done.2, s32[]{:T(128)S(6)} %select_n.98, f32[512,256]{1,0:T(8,128)S(1)} %fusion.19, f32[256]{0:T(256)S(1)} %copy-done.85, bf16[4,256,256]{2,1,0:T(8,128)(2,1)S(1)} %copy-done.1), kind=kLoop, calls=%fused_computation.236 | loop fusion | flops 1179392 | bytes 1574916 | tf_op jit(solution)/shard_map/reduce_sum | solution.py:192
  21.9 1.5 %fusion.6 = bf16[512,1024]{1,0:T(8,128)(2,1)S(1)} fusion(f32[512,1024]{1,0:T(8,128)S(1)} %get-tuple-element.154, bf16[512,256]{1,0:T(8,128)(2,1)S(1)} %bitcast.165, bf16[1024,256]{1,0:T(8,128)(2,1)S(1)} %copy-done.86), kind=kOutput, calls=%fused_computation.107 | convolution fusion | flops 278396928 | bytes 3932160 | tf_op jit(solution)/shard_map/dot_general | solution.py:164
  23.4 0.6 multiply_reduce_fusion.2
  24.0 0.3 multiply_reduce_fusion
  24.4 1.5 %fusion.172 = (f32[256]{0:T(256)S(1)}, f32[256]{0:T(256)S(1)}, f32[256]{0:T(256)S(1)}, f32[256]{0:T(256)S(1)}, f32[256]{0:T(256)S(1)}, /*index=5*/f32[256]{0:T(2...) fusion(f32[10,134,256]{2,1,0:T(8,128)S(1)} %fusion.23, ...), kind=kLoop, calls=%fused_computation.284 | loop fusion | flops 5893632 | bytes 10775552 | tf_op jit(solution)/shard_map/reduce_sum | solution.py:132
  25.9 1.0 %fusion.173 = (f32[256]{0:T(256)S(1)}, f32[256]{0:T(256)S(1)}, f32[256]{0:T(256)S(1)}, f32[256]{0:T(256)S(1)}, f32[256]{0:T(256)S(1)}, /*index=5*/f32[256]{0:T(2...) fusion(bf16[4,128,256]{2,1,0:T(8,128)(2,1)S(1)} %get-tuple-elem, ...), kind=kLoop, calls=%fused_computation.285 | loop fusion | flops 4845056 | bytes 9717760 | tf_op jit(solution)/shard_map/reduce_sum | solution.py:132
  26.9 0.7 fusion.171
  27.7 0.8 %copy.22 = bf16[512,256]{0,1:T(8,128)(2,1)} copy(bf16[512,256]{1,0:T(8,128)(2,1)S(1)} %bitcast.168) | data formatting | bytes 524288 | tf_op jit(solution)/shard_map/reshape | solution.py:159
  28.5 0.2 concatenate.24
  28.7 3.7 %collective-permute-start.6 = (f32[51,256]{1,0:T(8,128)S(1)}, f32[51,256]{1,0:T(8,128)S(1)}, u32[]{:S(2)}, u32[]{:S(2)}) collective-permute-start(f32[51,256]{1,0:T(8,128)S(1)} %concatenate.24), channel_id=1, source_target_pairs={{0,1},{1,0},{2,3},{3,2},{4,5},{5,4},{6,7},{7,6},{8,9},{9,8},{10,11... | collective-permute-start | bytes 156680 | tf_op jit(solution)/shard_map/ppermute | solution.py:69
  32.4 1.5 %copy.25 = bf16[1024,512]{1,0:T(8,128)(2,1)S(1)} copy(bf16[1024,512]{0,1:T(8,128)(2,1)} %get-tuple-element.153) | data formatting | bytes 2097152 | tf_op jit(solution)/shard_map/convert_element_type | solution.py:162
  33.9 1.4 %convolution_bitcast_fusion = f32[2,2,2,2,64,256]{5,4,0,1,2,3:T(8,128)S(1)} fusion(bf16[2,2,2,2,64,512]{5,4,3,2,1,0:T(8,128)(2,1)S(1)} %bitcast.163, bf16[512,256,1,1,1,1]{1,0,5,4,3,2:T(8,128)(2,1)} %bitcast.166), kind=kOutput, calls=%fused_computation.119 | convolution fusion | flops 268435456 | bytes 2359296 | tf_op jit(solution)/shard_map/dot_general | solution.py:177
  35.5 0.7 copy-done.7
  36.2 0.4 copy-done.88
  36.6 0.4 fusion.15
  37.9 2.5 %collective-permute-start.2 = (bf16[3,256,256]{2,1,0:T(8,128)(2,1)S(1)}, bf16[3,256,256]{2,1,0:T(8,128)(2,1)S(1)}, u32[]{:S(2)}, u32[]{:S(2)}) collective-permute-start(bf16[3,256,256]{2,1,0:T(8,128)(2,1)S(1)} %get-tuple-element.89), channel_id=1, source_target_pairs={{0,1},{1,2},{2,3},{3,4},{4,5},{5,6},{6,7},{7,8},{8,9},{9,10},{10,1... | collective-permute-start | bytes 1179656 | tf_op jit(solution)/shard_map/ppermute | solution.py:98
  40.4 1.5 %collective-permute-start.3 = (bf16[3,256,256]{2,1,0:T(8,128)(2,1)S(1)}, bf16[3,256,256]{2,1,0:T(8,128)(2,1)S(1)}, u32[]{:S(2)}, u32[]{:S(2)}) collective-permute-start(bf16[3,256,256]{2,1,0:T(8,128)(2,1)S(1)} %get-tuple-element.90), channel_id=1, source_target_pairs={{1,0},{2,1},{3,2},{4,3},{5,4},{6,5},{7,6},{8,7},{9,8},{10,9},{11,1... | collective-permute-start | bytes 1179656 | tf_op jit(solution)/shard_map/ppermute | solution.py:99
  42.3 3.4 %fusion.117 = f32[4,134,256]{2,1,0:T(8,128)S(1)} fusion(f32[4,128,256]{2,1,0:T(8,128)S(1)} %convert_element_type.173, f32[256]{0:T(256)S(1)} %bitcast.178, f32[256]{0:T(256)S(1)} %bitcast.183, f32[256]{0:T(256)S(1)} %bitcast.213, f32[256]{0:T(256)S(1)} %bitcast.233, f32[256]{0:T(256)S(1)} %bitcast.228, f32[256]{0:T(256)S(1)} %bitcast.223, ...), kind=kLoop, calls=%fused_computation.229 | loop fusion | flops 13309952 | bytes 1123328 | tf_op jit(solution)/shard_map/add | solution.py:120
  45.8 1.0 %maximum_select_fusion = bf16[4,256,256]{2,1,0:T(8,128)(2,1)} fusion(bf16[4,128,256]{2,1,0:T(8,128)(2,1)S(1)} %copy-done.5, bf16[4,128,256]{2,1,0:T(8,128)(2,1)S(1)} %copy-done.4, bf16[4,256,256]{2,1,0:T(8,128)(2,1)S(1)} %copy-done.1, bf16[4,128,256]{2,1,0:T(8,128)(2,1)S(1)} %copy-done.3, pred[]{:T(512)S(6)} %eq.7, pred[]{:T(512)S(6)} %eq.6), kind=kLoop, calls=%fused_computation.286 | loop fusion | flops 2621440 | bytes 1835010 | tf_op jit(solution)/shard_map/jit(_where)/select_n | solution.py:191
  47.0 0.7 multiply_add_fusion.4
  47.9 4.5 %collective-permute-start.7 = (bf16[614,256]{1,0:T(8,128)(2,1)S(1)}, bf16[614,256]{1,0:T(8,128)(2,1)S(1)}, u32[]{:S(2)}, u32[]{:S(2)}) collective-permute-start(bf16[614,256]{1,0:T(8,128)(2,1)S(1)} %pad_maximum_fusion), channel_id=1, source_target_pairs={{0,2},{1,3},{2,0},{3,1},{4,6},{5,7},{6,4},{7,5},{8,10},{9,11},{10,... | collective-permute-start | bytes 943112 | tf_op jit(solution)/shard_map/ppermute | solution.py:77
  52.4 0.7 fusion.196
  53.1 0.7 multiply_add_fusion.3
  53.7 4.4 %collective-permute-done.7 = bf16[614,256]{1,0:T(8,128)(2,1)S(1)} collective-permute-done((bf16[614,256]{1,0:T(8,128)(2,1)S(1)}, bf16[614,256]{1,0:T(8,128)(2,1)S(1)}, u32[]{:S(2)}, u32[]{:S(2)}) %collective-permute-start.7) | collective-permute-done | bytes 314400 | tf_op jit(solution)/shard_map/ppermute | solution.py:77
  58.4 5.2 %collective-permute-start.8 = (bf16[358,256]{1,0:T(8,128)(2,1)S(1)}, bf16[358,256]{1,0:T(8,128)(2,1)S(1)}, u32[]{:S(2)}, u32[]{:S(2)}) collective-permute-start(bf16[358,256]{1,0:T(8,128)(2,1)S(1)} %pad_maximum_fusion.1), channel_id=1, source_target_pairs={{0,4},{1,5},{2,6},{3,7},{4,0},{5,1},{6,2},{7,3},{8,12},{9,13},{10,... | collective-permute-start | bytes 549896 | tf_op jit(solution)/shard_map/ppermute | solution.py:77
  63.6 0.7 fusion.178
  64.3 4.8 %collective-permute-done.8 = bf16[358,256]{1,0:T(8,128)(2,1)S(1)} collective-permute-done((bf16[358,256]{1,0:T(8,128)(2,1)S(1)}, bf16[358,256]{1,0:T(8,128)(2,1)S(1)}, u32[]{:S(2)}, u32[]{:S(2)}) %collective-permute-start.8) | collective-permute-done | bytes 183328 | tf_op jit(solution)/shard_map/ppermute | solution.py:77
  69.2 2.8 %collective-permute-start.9 = (bf16[230,256]{1,0:T(8,128)(2,1)S(1)}, bf16[230,256]{1,0:T(8,128)(2,1)S(1)}, u32[]{:S(2)}, u32[]{:S(2)}) collective-permute-start(bf16[230,256]{1,0:T(8,128)(2,1)S(1)} %pad_maximum_fusion.2), channel_id=1, source_target_pairs={{0,8},{1,9},{2,10},{3,11},{4,12},{5,13},{6,14},{7,15},{8,0},{9,1},... | collective-permute-start | bytes 353288 | tf_op jit(solution)/shard_map/ppermute | solution.py:77
  72.0 1.1 %fusion.18 = bf16[4,256,256]{2,1,0:T(8,128)(2,1)} fusion(f32[1,256,256]{2,1,0:T(8,128)S(1)} %fusion.178, f32[1,256,256]{2,1,0:T(8,128)S(1)} %multiply_add_fusion.3, f32[1,256,256]{2,1,0:T(8,128)S(1)} %multiply_add_fusion.4, f32[1,256,256]{2,1,0:T(8,128)S(1)} %fusion.196, f32[4,131,256]{2,1,0:T(8,128)S(1)} %get-tuple-element.86, ...), kind=kLoop, calls=%fused_computation.128 | loop fusion | flops 2359296 | bytes 3170306 | tf_op jit(solution)/shard_map/convert_element_type | solution.py:244
  73.1 4.8 %collective-permute-done.9 = bf16[230,256]{1,0:T(8,128)(2,1)S(1)} collective-permute-done((bf16[230,256]{1,0:T(8,128)(2,1)S(1)}, bf16[230,256]{1,0:T(8,128)(2,1)S(1)}, u32[]{:S(2)}, u32[]{:S(2)}) %collective-permute-start.9) | collective-permute-done | bytes 117792 | tf_op jit(solution)/shard_map/ppermute | solution.py:77
  78.0 0.6 fusion.213
  78.6 0.6 convert_add_fusion.8
  79.2 0.6 copy.30
  (223 shorter events, 1.9 us)
Async XLA Ops:
  0.6 17.5 %copy-start = (bf16[256,1024]{1,0:T(8,128)(2,1)S(1)}, bf16[256,1024]{1,0:T(8,128)(2,1)}, u32[]{:S(2)}) copy-start(bf16[256,1024]{1,0:T(8,128)(2,1)} %param.12) | copy-start | bytes 1572868
  0.6 10.8 %copy-start.1 = (bf16[4,256,256]{2,1,0:T(8,128)(2,1)S(1)}, bf16[4,256,256]{2,1,0:T(8,128)(2,1)}, u32[]{:S(2)}) copy-start(bf16[4,256,256]{2,1,0:T(8,128)(2,1)} %param.8) | copy-start | bytes 1572868
  1.9 10.5 %collective-permute-start = (bf16[3,256,256]{2,1,0:T(8,128)(2,1)S(1)}, bf16[3,256,256]{2,1,0:T(8,128)(2,1)S(1)}, u32[]{:S(2)}, u32[]{:S(2)}) collective-permute-start(bf16[3,256,256]{2,1,0:T(8,128)(2,1)S(1)} %get-tuple-element.94), channel_id=1, source_target_pairs={{0,1},{1,2},{2,3},{3,4},{4,5},{5,6},{6,7},{7,8},{8,9},{9,10},{10,1... | collective-permute-start | bytes 1179656 | tf_op jit(solution)/shard_map/ppermute | solution.py:21
  4.3 8.1 %collective-permute-start.1 = (bf16[3,256,256]{2,1,0:T(8,128)(2,1)S(1)}, bf16[3,256,256]{2,1,0:T(8,128)(2,1)S(1)}, u32[]{:S(2)}, u32[]{:S(2)}) collective-permute-start(bf16[3,256,256]{2,1,0:T(8,128)(2,1)S(1)} %get-tuple-element.93), channel_id=1, source_target_pairs={{1,0},{2,1},{3,2},{4,3},{5,4},{6,5},{7,6},{8,7},{9,8},{10,9},{11,1... | collective-permute-start | bytes 1179656 | tf_op jit(solution)/shard_map/ppermute | solution.py:24
  6.6 6.1 %copy-start.26 = (f32[1,1,256]{2,1,0:T(1,128)}, f32[1,1,256]{2,1,0:T(1,128)S(1)}, u32[]{:S(2)}) copy-start(f32[1,1,256]{2,1,0:T(1,128)S(1)} %get-tuple-element.107) | copy-start | bytes 3076
  6.6 6.1 %copy-start.28 = (f32[1,1,256]{2,1,0:T(1,128)}, f32[1,1,256]{2,1,0:T(1,128)S(1)}, u32[]{:S(2)}) copy-start(f32[1,1,256]{2,1,0:T(1,128)S(1)} %get-tuple-element.108) | copy-start | bytes 3076
  6.6 6.1 %copy-start.30 = (f32[1,1,256]{2,1,0:T(1,128)}, f32[1,1,256]{2,1,0:T(1,128)S(1)}, u32[]{:S(2)}) copy-start(f32[1,1,256]{2,1,0:T(1,128)S(1)} %get-tuple-element.109) | copy-start | bytes 3076
  6.6 6.1 %copy-start.32 = (f32[1,1,256]{2,1,0:T(1,128)}, f32[1,1,256]{2,1,0:T(1,128)S(1)}, u32[]{:S(2)}) copy-start(f32[1,1,256]{2,1,0:T(1,128)S(1)} %get-tuple-element.110) | copy-start | bytes 3076
  6.6 6.1 %copy-start.34 = (f32[1,1,256]{2,1,0:T(1,128)}, f32[1,1,256]{2,1,0:T(1,128)S(1)}, u32[]{:S(2)}) copy-start(f32[1,1,256]{2,1,0:T(1,128)S(1)} %get-tuple-element.111) | copy-start | bytes 3076
  6.6 6.1 %copy-start.36 = (f32[1,1,256]{2,1,0:T(1,128)}, f32[1,1,256]{2,1,0:T(1,128)S(1)}, u32[]{:S(2)}) copy-start(f32[1,1,256]{2,1,0:T(1,128)S(1)} %get-tuple-element.112) | copy-start | bytes 3076
  6.7 6.1 %copy-start.38 = (f32[1,1,256]{2,1,0:T(1,128)}, f32[1,1,256]{2,1,0:T(1,128)S(1)}, u32[]{:S(2)}) copy-start(f32[1,1,256]{2,1,0:T(1,128)S(1)} %get-tuple-element.113) | copy-start | bytes 3076
  8.3 9.1 %copy-start.20 = (f32[1,1,256]{2,1,0:T(1,128)}, f32[1,1,256]{2,1,0:T(1,128)S(1)}, u32[]{:S(2)}) copy-start(f32[1,1,256]{2,1,0:T(1,128)S(1)} %get-tuple-element.136) | copy-start | bytes 3076
  8.3 9.1 %copy-start.22 = (f32[1,1,256]{2,1,0:T(1,128)}, f32[1,1,256]{2,1,0:T(1,128)S(1)}, u32[]{:S(2)}) copy-start(f32[1,1,256]{2,1,0:T(1,128)S(1)} %get-tuple-element.137) | copy-start | bytes 3076
  8.3 9.1 %copy-start.24 = (f32[1,1,256]{2,1,0:T(1,128)}, f32[1,1,256]{2,1,0:T(1,128)S(1)}, u32[]{:S(2)}) copy-start(f32[1,1,256]{2,1,0:T(1,128)S(1)} %get-tuple-element.138) | copy-start | bytes 3076
  8.3 9.1 %copy-start.48 = (f32[1,1,256]{2,1,0:T(1,128)}, f32[1,1,256]{2,1,0:T(1,128)S(1)}, u32[]{:S(2)}) copy-start(f32[1,1,256]{2,1,0:T(1,128)S(1)} %get-tuple-element.129) | copy-start | bytes 3076
  8.4 9.1 %copy-start.50 = (f32[1,1,256]{2,1,0:T(1,128)}, f32[1,1,256]{2,1,0:T(1,128)S(1)}, u32[]{:S(2)}) copy-start(f32[1,1,256]{2,1,0:T(1,128)S(1)} %get-tuple-element.130) | copy-start | bytes 3076
  8.4 9.1 %copy-start.52 = (f32[1,1,256]{2,1,0:T(1,128)}, f32[1,1,256]{2,1,0:T(1,128)S(1)}, u32[]{:S(2)}) copy-start(f32[1,1,256]{2,1,0:T(1,128)S(1)} %get-tuple-element.131) | copy-start | bytes 3076
  8.4 9.1 %copy-start.54 = (f32[1,1,256]{2,1,0:T(1,128)}, f32[1,1,256]{2,1,0:T(1,128)S(1)}, u32[]{:S(2)}) copy-start(f32[1,1,256]{2,1,0:T(1,128)S(1)} %get-tuple-element.132) | copy-start | bytes 3076
  8.4 9.1 %copy-start.56 = (f32[1,1,256]{2,1,0:T(1,128)}, f32[1,1,256]{2,1,0:T(1,128)S(1)}, u32[]{:S(2)}) copy-start(f32[1,1,256]{2,1,0:T(1,128)S(1)} %get-tuple-element.133) | copy-start | bytes 3076
  8.4 9.1 %copy-start.58 = (f32[1,1,256]{2,1,0:T(1,128)}, f32[1,1,256]{2,1,0:T(1,128)S(1)}, u32[]{:S(2)}) copy-start(f32[1,1,256]{2,1,0:T(1,128)S(1)} %get-tuple-element.134) | copy-start | bytes 3076
  8.4 9.1 %copy-start.60 = (f32[1,1,256]{2,1,0:T(1,128)}, f32[1,1,256]{2,1,0:T(1,128)S(1)}, u32[]{:S(2)}) copy-start(f32[1,1,256]{2,1,0:T(1,128)S(1)} %get-tuple-element.135) | copy-start | bytes 3076
  8.4 9.1 %copy-start.74 = (f32[1,1,256]{2,1,0:T(1,128)}, f32[1,1,256]{2,1,0:T(1,128)S(1)}, u32[]{:S(2)}) copy-start(f32[1,1,256]{2,1,0:T(1,128)S(1)} %get-tuple-element.121) | copy-start | bytes 3076
  8.4 9.1 %copy-start.76 = (f32[1,1,256]{2,1,0:T(1,128)}, f32[1,1,256]{2,1,0:T(1,128)S(1)}, u32[]{:S(2)}) copy-start(f32[1,1,256]{2,1,0:T(1,128)S(1)} %get-tuple-element.122) | copy-start | bytes 3076
  8.4 9.1 %copy-start.78 = (f32[1,1,256]{2,1,0:T(1,128)}, f32[1,1,256]{2,1,0:T(1,128)S(1)}, u32[]{:S(2)}) copy-start(f32[1,1,256]{2,1,0:T(1,128)S(1)} %get-tuple-element.123) | copy-start | bytes 3076
  8.4 9.1 %copy-start.80 = (f32[1,1,256]{2,1,0:T(1,128)}, f32[1,1,256]{2,1,0:T(1,128)S(1)}, u32[]{:S(2)}) copy-start(f32[1,1,256]{2,1,0:T(1,128)S(1)} %get-tuple-element.124) | copy-start | bytes 3076
  8.5 9.1 %copy-start.82 = (f32[1,1,256]{2,1,0:T(1,128)}, f32[1,1,256]{2,1,0:T(1,128)S(1)}, u32[]{:S(2)}) copy-start(f32[1,1,256]{2,1,0:T(1,128)S(1)} %get-tuple-element.125) | copy-start | bytes 3076
  8.5 9.1 %copy-start.83 = (f32[1,1,256]{2,1,0:T(1,128)}, f32[1,1,256]{2,1,0:T(1,128)S(1)}, u32[]{:S(2)}) copy-start(f32[1,1,256]{2,1,0:T(1,128)S(1)} %get-tuple-element.126) | copy-start | bytes 3076
  11.4 6.1 %copy-start.8 = (f32[1,1,256]{2,1,0:T(1,128)}, f32[1,1,256]{2,1,0:T(1,128)S(1)}, u32[]{:S(2)}) copy-start(f32[1,1,256]{2,1,0:T(1,128)S(1)} %get-tuple-element.144) | copy-start | bytes 3076
  11.4 6.1 %copy-start.10 = (f32[1,1,256]{2,1,0:T(1,128)}, f32[1,1,256]{2,1,0:T(1,128)S(1)}, u32[]{:S(2)}) copy-start(f32[1,1,256]{2,1,0:T(1,128)S(1)} %get-tuple-element.145) | copy-start | bytes 3076
  11.4 6.1 %copy-start.12 = (f32[1,1,256]{2,1,0:T(1,128)}, f32[1,1,256]{2,1,0:T(1,128)S(1)}, u32[]{:S(2)}) copy-start(f32[1,1,256]{2,1,0:T(1,128)S(1)} %get-tuple-element.146) | copy-start | bytes 3076
  11.4 6.1 %copy-start.14 = (f32[1,1,256]{2,1,0:T(1,128)}, f32[1,1,256]{2,1,0:T(1,128)S(1)}, u32[]{:S(2)}) copy-start(f32[1,1,256]{2,1,0:T(1,128)S(1)} %get-tuple-element.147) | copy-start | bytes 3076
  11.5 6.1 %copy-start.16 = (f32[1,1,256]{2,1,0:T(1,128)}, f32[1,1,256]{2,1,0:T(1,128)S(1)}, u32[]{:S(2)}) copy-start(f32[1,1,256]{2,1,0:T(1,128)S(1)} %get-tuple-element.148) | copy-start | bytes 3076
  11.5 6.1 %copy-start.18 = (f32[1,1,256]{2,1,0:T(1,128)}, f32[1,1,256]{2,1,0:T(1,128)S(1)}, u32[]{:S(2)}) copy-start(f32[1,1,256]{2,1,0:T(1,128)S(1)} %get-tuple-element.149) | copy-start | bytes 3076
  11.5 6.1 %copy-start.40 = (f32[1,1,256]{2,1,0:T(1,128)}, f32[1,1,256]{2,1,0:T(1,128)S(1)}, u32[]{:S(2)}) copy-start(f32[1,1,256]{2,1,0:T(1,128)S(1)} %get-tuple-element.140) | copy-start | bytes 3076
  11.5 6.1 %copy-start.42 = (f32[1,1,256]{2,1,0:T(1,128)}, f32[1,1,256]{2,1,0:T(1,128)S(1)}, u32[]{:S(2)}) copy-start(f32[1,1,256]{2,1,0:T(1,128)S(1)} %get-tuple-element.141) | copy-start | bytes 3076
  11.5 6.1 %copy-start.44 = (f32[1,1,256]{2,1,0:T(1,128)}, f32[1,1,256]{2,1,0:T(1,128)S(1)}, u32[]{:S(2)}) copy-start(f32[1,1,256]{2,1,0:T(1,128)S(1)} %get-tuple-element.142) | copy-start | bytes 3076
  11.5 6.1 %copy-start.46 = (f32[1,1,256]{2,1,0:T(1,128)}, f32[1,1,256]{2,1,0:T(1,128)S(1)}, u32[]{:S(2)}) copy-start(f32[1,1,256]{2,1,0:T(1,128)S(1)} %get-tuple-element.143) | copy-start | bytes 3076
  28.7 18.1 %collective-permute-start.6 = (f32[51,256]{1,0:T(8,128)S(1)}, f32[51,256]{1,0:T(8,128)S(1)}, u32[]{:S(2)}, u32[]{:S(2)}) collective-permute-start(f32[51,256]{1,0:T(8,128)S(1)} %concatenate.24), channel_id=1, source_target_pairs={{0,1},{1,0},{2,3},{3,2},{4,5},{5,4},{6,7},{7,6},{8,9},{9,8},{10,11... | collective-permute-start | bytes 156680 | tf_op jit(solution)/shard_map/ppermute | solution.py:69
  35.4 12.2 %collective-permute-start.5 = (f32[512,256]{1,0:T(8,128)S(1)}, f32[512,256]{1,0:T(8,128)S(1)}, u32[]{:S(2)}, u32[]{:S(2)}) collective-permute-start(f32[512,256]{1,0:T(8,128)S(1)} %constant_dynamic-slice_fusion), channel_id=1, source_target_pairs={{0,1},{1,0},{2,3},{3,2},{4,5},{5,4},{6,7},{7,6},{8,9},{9,8},{10,11... | collective-permute-start | bytes 1572872 | tf_op jit(solution)/shard_map/ppermute | solution.py:69
  37.5 10.2 %collective-permute-start.4 = (f32[4,128,256]{2,1,0:T(8,128)S(1)}, f32[4,128,256]{2,1,0:T(8,128)S(1)}, u32[]{:S(2)}, u32[]{:S(2)}) collective-permute-start(f32[4,128,256]{2,1,0:T(8,128)S(1)} %constant_dynamic-slice_fusion.1), channel_id=1, source_target_pairs={{0,1},{1,0},{2,3},{3,2},{4,5},{5,4},{6,7},{7,6},{8,9},{9,8},{10,11... | collective-permute-start | bytes 1572872 | tf_op jit(solution)/shard_map/ppermute | solution.py:69
  37.8 8.0 %copy-start.3 = (bf16[4,128,256]{2,1,0:T(8,128)(2,1)S(1)}, bf16[4,128,256]{2,1,0:T(8,128)(2,1)}, u32[]{:S(2)}) copy-start(bf16[4,128,256]{2,1,0:T(8,128)(2,1)} %get-tuple-element.91) | copy-start | bytes 786436
  37.8 8.0 %copy-start.4 = (bf16[4,128,256]{2,1,0:T(8,128)(2,1)S(1)}, bf16[4,128,256]{2,1,0:T(8,128)(2,1)}, u32[]{:S(2)}) copy-start(bf16[4,128,256]{2,1,0:T(8,128)(2,1)} %get-tuple-element.92) | copy-start | bytes 786436
  37.8 8.0 %copy-start.5 = (bf16[4,128,256]{2,1,0:T(8,128)(2,1)S(1)}, bf16[4,128,256]{2,1,0:T(8,128)(2,1)}, u32[]{:S(2)}) copy-start(bf16[4,128,256]{2,1,0:T(8,128)(2,1)} %get-tuple-element.150) | copy-start | bytes 786436
  37.9 8.9 %collective-permute-start.2 = (bf16[3,256,256]{2,1,0:T(8,128)(2,1)S(1)}, bf16[3,256,256]{2,1,0:T(8,128)(2,1)S(1)}, u32[]{:S(2)}, u32[]{:S(2)}) collective-permute-start(bf16[3,256,256]{2,1,0:T(8,128)(2,1)S(1)} %get-tuple-element.89), channel_id=1, source_target_pairs={{0,1},{1,2},{2,3},{3,4},{4,5},{5,6},{6,7},{7,8},{8,9},{9,10},{10,1... | collective-permute-start | bytes 1179656 | tf_op jit(solution)/shard_map/ppermute | solution.py:98
  40.4 6.5 %collective-permute-start.3 = (bf16[3,256,256]{2,1,0:T(8,128)(2,1)S(1)}, bf16[3,256,256]{2,1,0:T(8,128)(2,1)S(1)}, u32[]{:S(2)}, u32[]{:S(2)}) collective-permute-start(bf16[3,256,256]{2,1,0:T(8,128)(2,1)S(1)} %get-tuple-element.90), channel_id=1, source_target_pairs={{1,0},{2,1},{3,2},{4,3},{5,4},{6,5},{7,6},{8,7},{9,8},{10,9},{11,1... | collective-permute-start | bytes 1179656 | tf_op jit(solution)/shard_map/ppermute | solution.py:99
  47.9 10.2 %collective-permute-start.7 = (bf16[614,256]{1,0:T(8,128)(2,1)S(1)}, bf16[614,256]{1,0:T(8,128)(2,1)S(1)}, u32[]{:S(2)}, u32[]{:S(2)}) collective-permute-start(bf16[614,256]{1,0:T(8,128)(2,1)S(1)} %pad_maximum_fusion), channel_id=1, source_target_pairs={{0,2},{1,3},{2,0},{3,1},{4,6},{5,7},{6,4},{7,5},{8,10},{9,11},{10,... | collective-permute-start | bytes 943112 | tf_op jit(solution)/shard_map/ppermute | solution.py:77
  58.4 10.7 %collective-permute-start.8 = (bf16[358,256]{1,0:T(8,128)(2,1)S(1)}, bf16[358,256]{1,0:T(8,128)(2,1)S(1)}, u32[]{:S(2)}, u32[]{:S(2)}) collective-permute-start(bf16[358,256]{1,0:T(8,128)(2,1)S(1)} %pad_maximum_fusion.1), channel_id=1, source_target_pairs={{0,4},{1,5},{2,6},{3,7},{4,0},{5,1},{6,2},{7,3},{8,12},{9,13},{10,... | collective-permute-start | bytes 549896 | tf_op jit(solution)/shard_map/ppermute | solution.py:77
  69.2 8.7 %collective-permute-start.9 = (bf16[230,256]{1,0:T(8,128)(2,1)S(1)}, bf16[230,256]{1,0:T(8,128)(2,1)S(1)}, u32[]{:S(2)}, u32[]{:S(2)}) collective-permute-start(bf16[230,256]{1,0:T(8,128)(2,1)S(1)} %pad_maximum_fusion.2), channel_id=1, source_target_pairs={{0,8},{1,9},{2,10},{3,11},{4,12},{5,13},{6,14},{7,15},{8,0},{9,1},... | collective-permute-start | bytes 353288 | tf_op jit(solution)/shard_map/ppermute | solution.py:77
  (51 other events, 227.5 us)

commit v21 on v18

--- a/solution.py
+++ b/solution.py
@@ -210,10 +210,23 @@
         lo, hi = max(left, 0), min(left + span, image_cols)
         placed = jnp.pad(own[:, lo - left : hi - left], ((0, 0), (lo, image_cols - hi), (0, 0)))
         own_full = jnp.where(tile_index == tile, placed, own_full)
-    grad_conv = lax.dynamic_update_slice_in_dim(
-        jnp.zeros_like(image), grad_tile, first_col, axis=1
-    )
-    low, high = halo_rows(grad_conv, "row", half_width)
+    tiles = image_cols // TILE_COLS
+    marker = jnp.full((image_rows, 16, channels), first_col // TILE_COLS, jnp.bfloat16)
+    tagged = jnp.concatenate([grad_tile, marker], axis=1)
+    low_tagged, high_tagged = halo_rows(tagged, "row", half_width)
+
+    def spread(rows_tagged):
+        which = rows_tagged[0, TILE_COLS, 0]
+        spread_rows = jnp.zeros((half_width, image_cols, channels), jnp.bfloat16)
+        for tile in range(tiles):
+            placed = jnp.pad(
+                rows_tagged[:, :TILE_COLS],
+                ((0, 0), (tile * TILE_COLS, image_cols - (tile + 1) * TILE_COLS), (0, 0)),
+            )
+            spread_rows = jnp.where(which == tile, placed, spread_rows)
+        return spread_rows
+
+    low, high = spread(low_tagged), spread(high_tagged)
     edge = ((0, 0), (half_width, half_width), (0, 0))
     low = jnp.pad(low.astype(jnp.float32), edge)
     high = jnp.pad(high.astype(jnp.float32), edge)

time: 79.8 us -> 90.2 us (1.13)
  local copies, waits for them, and re-layouts: 7.63 us -> 15.7 us
  starting transfers between devices: 27.6 us -> 23.6 us
  between operations: 3.16 us -> 5.9 us
  other arithmetic: 18.6 us -> 21.2 us
  waiting for transfers between devices: 16 us -> 17.1 us
    ppermute x1, starting transfers between devices: 2.42 us -> 9.22 us  [halo_rows(): lax.ppermute(lax.slice_in_dim(block, block.shape[0] - width, None, axis=0...]
    ppermute x3, starting transfers between devices: 13.8 us -> 7.6 us  [halving_reduce(): got = lax.ppermute(sent, axis, pairs)]
    ppermute x3, starting transfers between devices: 6.2 us -> 1.87 us  [halving_reduce(): got_q, got_r, got_whole = lax.ppermute((give_q, give_r, whole), axis, pairs)]
    slice x0 -> x4, local copies, waits for them, and re-layouts: none -> 4.25 us  [the longest x2 2.36 us: spread(): which = rows_tagged[0, TILE_COLS, 0]]
    concatenate x1, local copies, waits for them, and re-layouts: 0.18 us -> 2.91 us  [shards(): jnp.concatenate([kernel_grad, gain_grad[None], scale_grad[None]], axis=0)]
    reduce_sum x3, other arithmetic: 3.28 us -> 5.04 us  [kernel_terms(): jnp.sum(padded[row_tap:row_tap + image_rows, col_tap:col_tap + image_cols...]
    add x4, other arithmetic: 0.13 us -> 1.18 us  [halving_reduce(): quartered = keep_q + got_q.astype(jnp.float32)]
    dot_general x1, matrix products: 1.38 us -> 0.43 us  [shards(): lax.dot_general(act_flat, grad_flat, (((0,), (0,)), ((), ())), preferred_...]
  transfers between devices with their start and end apart: 10 -> 10, of which waited for: 4 -> 5; matrix products, arithmetic and copies ran while one was open for 16% -> 23% of each run, Pallas kernels for 0% -> 0%
where the time goes in v21:
time: 90.2 us; the launch traced here: 89.7 us
  starting transfers between devices  23.6 us (26%)
  other arithmetic  21.2 us (24%)
  waiting for transfers between devices  17.1 us (19%)
  local copies, waits for them, and re-layouts  15.7 us (17%)
  matrix products  6.06 us (7%)
  between operations  5.9 us (7%)
    ppermute x3, waiting for transfers between devices, halving_reduce(): got = lax.ppermute(sent, axis, pairs)  13.9 us
    ppermute x1, starting transfers between devices, halo_rows(): lax.ppermute(lax.slice_in_dim(block, block.shape[0] - width, None, axis=0...  9.22 us
    ppermute x3, starting transfers between devices, halving_reduce(): got = lax.ppermute(sent, axis, pairs)  7.6 us
    reduce_sum x3, other arithmetic, kernel_terms(): jnp.sum(padded[row_tap:row_tap + image_rows, col_tap:col_tap + image_cols...  5.04 us
    reduce_sum x1, other arithmetic, shards(): centre = jnp.mean(filtered, axis=-1, keepdims=True)  3.86 us
    add x4, other arithmetic, shards(): total + line[col_tap:col_tap + image_cols] * flipped[row_tap, col_tap]  3.38 us
    concatenate x1, local copies, waits for them, and re-layouts, shards(): jnp.concatenate([kernel_grad, gain_grad[None], scale_grad[None]], axis=0)  2.91 us
    add x1, other arithmetic, depthwise(): total + padded[row_tap:row_tap + image_rows, col_tap:col_tap + image_cols...  2.69 us
  transfers between devices with their start and end apart: 10, of which 5 were waited for; matrix products, arithmetic and copies ran while one was open for 23% of the time, Pallas kernels for 0%

profile of v21, /device:TPU:0, one launch (start us, length us, event | category | flops | bytes accessed | tf_op | source)
XLA Modules:
  0.0 89.7 jit_solution(8852965067973260757)
XLA Ops:
  0.7 1.1 %copy.37 = bf16[4,256,256]{2,1,0:T(8,128)(2,1)S(1)} copy(bf16[4,256,256]{2,1,0:T(8,128)(2,1)} %param.8) | data formatting | bytes 1048576
  1.8 2.4 %collective-permute-start = (bf16[3,256,256]{2,1,0:T(8,128)(2,1)S(1)}, bf16[3,256,256]{2,1,0:T(8,128)(2,1)S(1)}, u32[]{:S(2)}, u32[]{:S(2)}) collective-permute-start(bf16[3,256,256]{2,1,0:T(8,128)(2,1)S(1)} %get-tuple-element.90), channel_id=1, source_target_pairs={{0,1},{1,2},{2,3},{3,4},{4,5},{5,6},{6,7},{7,8},{8,9},{9,10},{10,1... | collective-permute-start | bytes 1179656 | tf_op jit(solution)/shard_map/ppermute | solution.py:21
  4.2 1.3 %collective-permute-start.1 = (bf16[3,256,256]{2,1,0:T(8,128)(2,1)S(1)}, bf16[3,256,256]{2,1,0:T(8,128)(2,1)S(1)}, u32[]{:S(2)}, u32[]{:S(2)}) collective-permute-start(bf16[3,256,256]{2,1,0:T(8,128)(2,1)S(1)} %get-tuple-element.89), channel_id=1, source_target_pairs={{1,0},{2,1},{3,2},{4,3},{5,4},{6,5},{7,6},{8,7},{9,8},{10,9},{11,1... | collective-permute-start | bytes 1179656 | tf_op jit(solution)/shard_map/ppermute | solution.py:24
  5.5 0.7 bitcast_reduce_fusion
  7.3 2.6 %collective-permute-done.1 = bf16[3,256,256]{2,1,0:T(8,128)(2,1)S(1)} collective-permute-done((bf16[3,256,256]{2,1,0:T(8,128)(2,1)S(1)}, bf16[3,256,256]{2,1,0:T(8,128)(2,1)S(1)}, u32[]{:S(2)}, u32[]{:S(2)}) %collective-permute-start.1) | collective-permute-done | bytes 393248 | tf_op jit(solution)/shard_map/ppermute | solution.py:24
  10.3 3.9 %fusion.219 = (f32[4,128]{1,0:T(4,128)S(1)}, f32[4,128,256]{2,1,0:T(8,128)S(1)}) fusion(f32[256]{0:T(256)S(1)} %bitcast.211, f32[10,134,256]{2,1,0:T(8,128)S(1)} %fusion.23, f32[256]{0:T(256)S(1)} %bitcast.216, f32[256]{0:T(256)S(1)} %bitcast.181, f32[256]{0:T(256)S(1)} %bitcast.186, f32[256]{0:T(256)S(1)} %bitcast.191, f32[256]{0:T(256)S(1)} %bitcast.196, ...), kind=kLoop, calls=%fused_computation.408 | loop fusion | flops 12844544 | bytes 26266624 | tf_op jit(solution)/shard_map/reduce_sum | solution.py:151
  14.6 0.8 copy.22
  15.5 1.8 %fusion.11 = (bf16[1024,512]{0,1:T(8,128)(2,1)}, f32[512,1024]{1,0:T(8,128)S(1)}) fusion(bf16[512,256]{1,0:T(8,128)(2,1)S(1)} %bitcast.172, bf16[256,1024]{1,0:T(8,128)(2,1)S(1)} %copy-done), kind=kOutput, calls=%fused_computation.112 | convolution fusion | flops 273154048 | bytes 3932160 | tf_op jit(solution)/shard_map/dot_general | solution.py:161
  17.3 1.4 %fusion.124 = (f32[256]{0:T(256)}, bf16[4,128,256]{2,1,0:T(8,128)(2,1)S(1)}, f32[512,256]{1,0:T(8,128)S(1)}) fusion(bf16[4,256,256]{2,1,0:T(8,128)(2,1)S(1)} %copy-done.3, s32[]{:T(128)S(6)} %select_n.106, f32[256]{0:T(256)S(1)} %copy-done.83, bf16[1024,256]{1,0:T(8,128)(2,1)S(1)} %copy-done.7, f32[512,1024]{1,0:T(8,128)S(1)} %get-tuple-element.152), kind=kOutput, calls=%fused_computation.236 | convolution fusion | flops 273809152 | bytes 3672068 | tf_op jit(solution)/shard_map/dot_general | solution.py:163
  18.7 0.7 copy-done.5
  19.4 1.4 %fusion.6 = bf16[512,1024]{1,0:T(8,128)(2,1)S(1)} fusion(f32[512,1024]{1,0:T(8,128)S(1)} %get-tuple-element.152, bf16[512,256]{1,0:T(8,128)(2,1)S(1)} %bitcast.168, bf16[1024,256]{1,0:T(8,128)(2,1)S(1)} %copy-done.7), kind=kOutput, calls=%fused_computation.107 | convolution fusion | flops 278396928 | bytes 3932160 | tf_op jit(solution)/shard_map/dot_general | solution.py:164
  20.9 0.6 multiply_reduce_fusion.2
  21.5 0.8 multiply_reduce_fusion
  22.3 1.8 %fusion.171 = (f32[256]{0:T(256)}, f32[256]{0:T(256)}, f32[256]{0:T(256)}, f32[256]{0:T(256)}, f32[256]{0:T(256)}, /*index=5*/f32[256]{0:T(256)}, f32[256]{0:T(2...) fusion(f32[10,134,256]{2,1,0:T(8,128)S(1)} %fusion.23, ...), kind=kLoop, calls=%fused_computation.283 | loop fusion | flops 4584192 | bytes 8148992 | tf_op jit(solution)/shard_map/reduce_sum | solution.py:132
  24.1 1.6 %fusion.173 = (f32[256]{0:T(256)}, f32[256]{0:T(256)}, f32[256]{0:T(256)}, f32[256]{0:T(256)}, f32[256]{0:T(256)}, /*index=5*/f32[256]{0:T(256)}, f32[256]{0:T(2...) fusion(bf16[4,128,256]{2,1,0:T(8,128)(2,1)S(1)} %get-tuple-elem, ...), kind=kLoop, calls=%fused_computation.285 | loop fusion | flops 4845056 | bytes 9717760 | tf_op jit(solution)/shard_map/reduce_sum | solution.py:132
  25.8 1.6 %fusion.172 = (f32[256]{0:T(256)}, f32[256]{0:T(256)}, f32[256]{0:T(256)}, f32[256]{0:T(256)}, f32[256]{0:T(256)}, /*index=5*/f32[256]{0:T(256)}, f32[256]{0:T(2...) fusion(bf16[4,128,256]{2,1,0:T(8,128)(2,1)S(1)} %get-tuple-elem, ...), kind=kLoop, calls=%fused_computation.284 | loop fusion | flops 4845056 | bytes 9717760 | tf_op jit(solution)/shard_map/reduce_sum | solution.py:132
  27.5 0.8 pad_slice_fusion.50
  28.3 1.3 %collective-permute-start.3 = (bf16[3,144,256]{2,1,0:T(8,128)(2,1)}, bf16[3,144,256]{2,1,0:T(8,128)(2,1)}, u32[]{:S(2)}, u32[]{:S(2)}) collective-permute-start(bf16[3,144,256]{2,1,0:T(8,128)(2,1)} %get-tuple-element.92), channel_id=1, source_target_pairs={{1,0},{2,1},{3,2},{4,3},{5,4},{6,5},{7,6},{8,7},{9,8},{10,9},{11,1... | collective-permute-start | bytes 663560 | tf_op jit(solution)/shard_map/ppermute | solution.py:99
  29.5 9.2 %collective-permute-start.2 = (bf16[3,144,256]{2,1,0:T(8,128)(2,1)}, bf16[3,144,256]{2,1,0:T(8,128)(2,1)}, u32[]{:S(2)}, u32[]{:S(2)}) collective-permute-start(bf16[3,144,256]{2,1,0:T(8,128)(2,1)} %get-tuple-element.91), channel_id=1, source_target_pairs={{0,1},{1,2},{2,3},{3,4},{4,5},{5,6},{6,7},{7,8},{8,9},{9,10},{10,1... | collective-permute-start | bytes 663560 | tf_op jit(solution)/shard_map/ppermute | solution.py:98
  39.1 2.7 %fusion.117 = f32[4,134,256]{2,1,0:T(8,128)S(1)} fusion(f32[4,128,256]{2,1,0:T(8,128)S(1)} %convert_element_type.178, f32[256]{0:T(256)S(1)} %bitcast.207, f32[256]{0:T(256)S(1)} %bitcast.247, f32[256]{0:T(256)S(1)} %bitcast.222, f32[256]{0:T(256)S(1)} %bitcast.242, f32[256]{0:T(256)S(1)} %bitcast.237, f32[256]{0:T(256)S(1)} %bitcast.232, ...), kind=kLoop, calls=%fused_computation.229 | loop fusion | flops 13309952 | bytes 1123328 | tf_op jit(solution)/shard_map/add | solution.py:120
  41.8 0.9 %fusion.220 = (f32[4,131,256]{2,1,0:T(8,128)S(1)}, f32[4,131,256]{2,1,0:T(8,128)}) fusion(f32[4,134,256]{2,1,0:T(8,128)S(1)} %fusion.117), kind=kLoop, calls=%fused_computation.409 | loop fusion | bytes 2146304 | tf_op jit(solution)/shard_map/slice | solution.py:211
  42.7 0.4 fusion.15
  43.3 0.8 constant_dynamic-slice_fusion.1
  44.1 1.3 %collective-permute-start.4 = (f32[4,128,256]{2,1,0:T(8,128)}, f32[4,128,256]{2,1,0:T(8,128)}, u32[]{:S(2)}, u32[]{:S(2)}) collective-permute-start(f32[4,128,256]{2,1,0:T(8,128)} %constant_dynamic-slice_fusion.1), channel_id=1, source_target_pairs={{0,1},{1,0},{2,3},{3,2},{4,5},{5,4},{6,7},{7,6},{8,9},{9,8},{10,11... | collective-permute-start | bytes 1572872 | tf_op jit(solution)/shard_map/ppermute | solution.py:69
  45.4 1.5 %copy.25 = bf16[1024,512]{1,0:T(8,128)(2,1)S(1)} copy(bf16[1024,512]{0,1:T(8,128)(2,1)} %get-tuple-element.151) | data formatting | bytes 2097152 | tf_op jit(solution)/shard_map/convert_element_type | solution.py:162
  47.0 0.4 convolution_bitcast_fusion
  48.3 2.9 %concatenate.20 = f32[51,256]{1,0:T(8,128)S(1)} concatenate(f32[1,256]{1,0:T(1,128)S(1)} %bitcast.379, f32[1,256]{1,0:T(1,128)S(1)} %bitcast.380, f32[1,256]{1,0:T(1,128)S(1)} %bitcast.381, f32[1,256]{1,0:T(1,128)S(1)} %bitcast.382, f32[1,256]{1,0:T(1,128)S(1)} %bitcast.383, f32[1,256]{1,0:T(1,128)S(1)} %bitcast.384, f32[1,256]{1,0:T(1,128)S(1)} %bitcast.385, ...), dimensions={0} | concatenate | bytes 104448 | tf_op jit(solution)/shard_map/concatenate | solution.py:197
  51.3 0.5 collective-permute-start.5
  51.9 0.6 collective-permute-done.6
  52.5 1.2 %slice.1277 = bf16[1,1,1]{2,1,0:T(2,128)(2,1)} slice(bf16[3,144,256]{2,1,0:T(8,128)(2,1)} %collective-permute-done.3), slice={[0:1], [128:129], [0:1]} | slice | bytes 4 | tf_op jit(solution)/shard_map/slice | solution.py:219
  55.0 1.2 %slice.1272 = bf16[1,1,1]{2,1,0:T(2,128)(2,1)} slice(bf16[3,144,256]{2,1,0:T(8,128)(2,1)} %collective-permute-done.2), slice={[0:1], [128:129], [0:1]} | slice | bytes 4 | tf_op jit(solution)/shard_map/slice | solution.py:219
  57.5 0.9 %slice.1278 = bf16[3,128,256]{2,1,0:T(8,128)(2,1)S(1)} slice(bf16[3,144,256]{2,1,0:T(8,128)(2,1)} %collective-permute-done.3), slice={[0:3], [0:128], [0:256]} | slice | bytes 393216 | tf_op jit(solution)/shard_map/slice | solution.py:223
  58.5 0.9 %slice.1273 = bf16[3,128,256]{2,1,0:T(8,128)(2,1)S(1)} slice(bf16[3,144,256]{2,1,0:T(8,128)(2,1)} %collective-permute-done.2), slice={[0:3], [0:128], [0:256]} | slice | bytes 393216 | tf_op jit(solution)/shard_map/slice | solution.py:223
  59.6 1.4 %multiply_add_fusion.3 = f32[1,256,256]{2,1,0:T(8,128)S(1)} fusion(f32[3,256,256]{2,1,0:T(8,128)S(1)} %select_convert_fusion, f32[3,256,256]{2,1,0:T(8,128)S(1)} %select_convert_fusion.1, f32[256]{0:T(256)} %bitcast.293, f32[256]{0:T(256)} %bitcast.289, f32[256]{0:T(256)} %bitcast.285, f32[256]{0:T(256)} %bitcast.281, f32[256]{0:T(256)} %bitcast.305, ...), kind=kLoop, calls=%fused_computation.353 | loop fusion | flops 2686976 | bytes 2642944 | tf_op jit(solution)/shard_map/add | solution.py:245
  61.2 1.1 %dynamic-slice_add_fusion.1 = f32[4,128,256]{2,1,0:T(8,128)S(1)} fusion(f32[4,128,256]{2,1,0:T(8,128)} %collective-permute-done.4, f32[4,256,256]{2,1,0:T(8,128)S(1)} %bitcast.163, s32[]{:T(128)S(6)} %select_n.121), kind=kLoop, calls=%fused_computation.288 | loop fusion | flops 131072 | bytes 1572868 | tf_op jit(solution)/shard_map/add | solution.py:88
  62.6 3.4 %collective-permute-start.7 = (bf16[614,256]{1,0:T(8,128)(2,1)S(1)}, bf16[614,256]{1,0:T(8,128)(2,1)S(1)}, u32[]{:S(2)}, u32[]{:S(2)}) collective-permute-start(bf16[614,256]{1,0:T(8,128)(2,1)S(1)} %pad_maximum_fusion), channel_id=1, source_target_pairs={{0,2},{1,3},{2,0},{3,1},{4,6},{5,7},{6,4},{7,5},{8,10},{9,11},{10,... | collective-permute-start | bytes 943112 | tf_op jit(solution)/shard_map/ppermute | solution.py:77
  66.1 0.7 fusion.179
  66.9 0.7 multiply_add_fusion.4
  67.5 6.2 %collective-permute-done.7 = bf16[614,256]{1,0:T(8,128)(2,1)S(1)} collective-permute-done((bf16[614,256]{1,0:T(8,128)(2,1)S(1)}, bf16[614,256]{1,0:T(8,128)(2,1)S(1)}, u32[]{:S(2)}, u32[]{:S(2)}) %collective-permute-start.7) | collective-permute-done | bytes 314400 | tf_op jit(solution)/shard_map/ppermute | solution.py:77
  73.9 1.6 %collective-permute-start.8 = (bf16[358,256]{1,0:T(8,128)(2,1)S(1)}, bf16[358,256]{1,0:T(8,128)(2,1)S(1)}, u32[]{:S(2)}, u32[]{:S(2)}) collective-permute-start(bf16[358,256]{1,0:T(8,128)(2,1)S(1)} %pad_maximum_fusion.1), channel_id=1, source_target_pairs={{0,4},{1,5},{2,6},{3,7},{4,0},{5,1},{6,2},{7,3},{8,12},{9,13},{10,... | collective-permute-start | bytes 549896 | tf_op jit(solution)/shard_map/ppermute | solution.py:77
  75.6 0.7 fusion.197
  76.3 3.9 %collective-permute-done.8 = bf16[358,256]{1,0:T(8,128)(2,1)S(1)} collective-permute-done((bf16[358,256]{1,0:T(8,128)(2,1)S(1)}, bf16[358,256]{1,0:T(8,128)(2,1)S(1)}, u32[]{:S(2)}, u32[]{:S(2)}) %collective-permute-start.8) | collective-permute-done | bytes 183328 | tf_op jit(solution)/shard_map/ppermute | solution.py:77
  80.4 2.6 %collective-permute-start.9 = (bf16[230,256]{1,0:T(8,128)(2,1)S(1)}, bf16[230,256]{1,0:T(8,128)(2,1)S(1)}, u32[]{:S(2)}, u32[]{:S(2)}) collective-permute-start(bf16[230,256]{1,0:T(8,128)(2,1)S(1)} %pad_maximum_fusion.2), channel_id=1, source_target_pairs={{0,8},{1,9},{2,10},{3,11},{4,12},{5,13},{6,14},{7,15},{8,0},{9,1},... | collective-permute-start | bytes 353288 | tf_op jit(solution)/shard_map/ppermute | solution.py:77
  82.9 1.0 %fusion.18 = bf16[4,256,256]{2,1,0:T(8,128)(2,1)} fusion(f32[1,256,256]{2,1,0:T(8,128)S(1)} %fusion.179, f32[1,256,256]{2,1,0:T(8,128)S(1)} %multiply_add_fusion.3, f32[1,256,256]{2,1,0:T(8,128)S(1)} %multiply_add_fusion.4, f32[1,256,256]{2,1,0:T(8,128)S(1)} %fusion.197, f32[4,131,256]{2,1,0:T(8,128)S(1)} %copy-done.2, ...), kind=kLoop, calls=%fused_computation.128 | loop fusion | flops 2359296 | bytes 3170306 | tf_op jit(solution)/shard_map/convert_element_type | solution.py:248
  83.9 3.8 %collective-permute-done.9 = bf16[230,256]{1,0:T(8,128)(2,1)S(1)} collective-permute-done((bf16[230,256]{1,0:T(8,128)(2,1)S(1)}, bf16[230,256]{1,0:T(8,128)(2,1)S(1)}, u32[]{:S(2)}, u32[]{:S(2)}) %collective-permute-start.9) | collective-permute-done | bytes 117792 | tf_op jit(solution)/shard_map/ppermute | solution.py:77
  87.8 0.6 fusion.214
  88.4 0.6 convert_add_fusion.8
  89.0 0.6 copy.30
  (283 shorter events, 2.7 us)
Async XLA Ops:
  0.6 14.9 %copy-start = (bf16[256,1024]{1,0:T(8,128)(2,1)S(1)}, bf16[256,1024]{1,0:T(8,128)(2,1)}, u32[]{:S(2)}) copy-start(bf16[256,1024]{1,0:T(8,128)(2,1)} %param.12) | copy-start | bytes 1572868
  1.8 5.5 %collective-permute-start = (bf16[3,256,256]{2,1,0:T(8,128)(2,1)S(1)}, bf16[3,256,256]{2,1,0:T(8,128)(2,1)S(1)}, u32[]{:S(2)}, u32[]{:S(2)}) collective-permute-start(bf16[3,256,256]{2,1,0:T(8,128)(2,1)S(1)} %get-tuple-element.90), channel_id=1, source_target_pairs={{0,1},{1,2},{2,3},{3,4},{4,5},{5,6},{6,7},{7,8},{8,9},{9,10},{10,1... | collective-permute-start | bytes 1179656 | tf_op jit(solution)/shard_map/ppermute | solution.py:21
  4.2 5.7 %collective-permute-start.1 = (bf16[3,256,256]{2,1,0:T(8,128)(2,1)S(1)}, bf16[3,256,256]{2,1,0:T(8,128)(2,1)S(1)}, u32[]{:S(2)}, u32[]{:S(2)}) collective-permute-start(bf16[3,256,256]{2,1,0:T(8,128)(2,1)S(1)} %get-tuple-element.89), channel_id=1, source_target_pairs={{1,0},{2,1},{3,2},{4,3},{5,4},{6,5},{7,6},{8,7},{9,8},{10,9},{11,1... | collective-permute-start | bytes 1179656 | tf_op jit(solution)/shard_map/ppermute | solution.py:24
  6.9 31.9 %copy-start.22 = (f32[1,1,256]{2,1,0:T(1,128)}, f32[1,1,256]{2,1,0:T(1,128)S(1)}, u32[]{:S(2)}) copy-start(f32[1,1,256]{2,1,0:T(1,128)S(1)} %get-tuple-element.105) | copy-start | bytes 3076
  6.9 31.9 %copy-start.24 = (f32[1,1,256]{2,1,0:T(1,128)}, f32[1,1,256]{2,1,0:T(1,128)S(1)}, u32[]{:S(2)}) copy-start(f32[1,1,256]{2,1,0:T(1,128)S(1)} %get-tuple-element.106) | copy-start | bytes 3076
  6.9 31.8 %copy-start.26 = (f32[1,1,256]{2,1,0:T(1,128)}, f32[1,1,256]{2,1,0:T(1,128)S(1)}, u32[]{:S(2)}) copy-start(f32[1,1,256]{2,1,0:T(1,128)S(1)} %get-tuple-element.107) | copy-start | bytes 3076
  6.9 31.8 %copy-start.28 = (f32[1,1,256]{2,1,0:T(1,128)}, f32[1,1,256]{2,1,0:T(1,128)S(1)}, u32[]{:S(2)}) copy-start(f32[1,1,256]{2,1,0:T(1,128)S(1)} %get-tuple-element.108) | copy-start | bytes 3076
  7.0 31.8 %copy-start.30 = (f32[1,1,256]{2,1,0:T(1,128)}, f32[1,1,256]{2,1,0:T(1,128)S(1)}, u32[]{:S(2)}) copy-start(f32[1,1,256]{2,1,0:T(1,128)S(1)} %get-tuple-element.109) | copy-start | bytes 3076
  7.0 31.8 %copy-start.32 = (f32[1,1,256]{2,1,0:T(1,128)}, f32[1,1,256]{2,1,0:T(1,128)S(1)}, u32[]{:S(2)}) copy-start(f32[1,1,256]{2,1,0:T(1,128)S(1)} %get-tuple-element.110) | copy-start | bytes 3076
  7.0 31.8 %copy-start.34 = (f32[1,1,256]{2,1,0:T(1,128)}, f32[1,1,256]{2,1,0:T(1,128)S(1)}, u32[]{:S(2)}) copy-start(f32[1,1,256]{2,1,0:T(1,128)S(1)} %get-tuple-element.111) | copy-start | bytes 3076
  7.0 31.8 %copy-start.50 = (f32[1,1,256]{2,1,0:T(1,128)}, f32[1,1,256]{2,1,0:T(1,128)S(1)}, u32[]{:S(2)}) copy-start(f32[1,1,256]{2,1,0:T(1,128)S(1)} %get-tuple-element.112) | copy-start | bytes 3076
  7.0 31.8 %copy-start.52 = (f32[1,1,256]{2,1,0:T(1,128)}, f32[1,1,256]{2,1,0:T(1,128)S(1)}, u32[]{:S(2)}) copy-start(f32[1,1,256]{2,1,0:T(1,128)S(1)} %get-tuple-element.113) | copy-start | bytes 3076
  7.0 31.8 %copy-start.54 = (f32[1,1,256]{2,1,0:T(1,128)}, f32[1,1,256]{2,1,0:T(1,128)S(1)}, u32[]{:S(2)}) copy-start(f32[1,1,256]{2,1,0:T(1,128)S(1)} %get-tuple-element.114) | copy-start | bytes 3076
  7.0 31.8 %copy-start.56 = (f32[1,1,256]{2,1,0:T(1,128)}, f32[1,1,256]{2,1,0:T(1,128)S(1)}, u32[]{:S(2)}) copy-start(f32[1,1,256]{2,1,0:T(1,128)S(1)} %get-tuple-element.115) | copy-start | bytes 3076
  7.0 31.8 %copy-start.58 = (f32[1,1,256]{2,1,0:T(1,128)}, f32[1,1,256]{2,1,0:T(1,128)S(1)}, u32[]{:S(2)}) copy-start(f32[1,1,256]{2,1,0:T(1,128)S(1)} %get-tuple-element.116) | copy-start | bytes 3076
  7.0 31.8 %copy-start.60 = (f32[1,1,256]{2,1,0:T(1,128)}, f32[1,1,256]{2,1,0:T(1,128)S(1)}, u32[]{:S(2)}) copy-start(f32[1,1,256]{2,1,0:T(1,128)S(1)} %get-tuple-element.117) | copy-start | bytes 3076
  7.1 31.8 %copy-start.10 = (f32[1,1,256]{2,1,0:T(1,128)}, f32[1,1,256]{2,1,0:T(1,128)S(1)}, u32[]{:S(2)}) copy-start(f32[1,1,256]{2,1,0:T(1,128)S(1)} %get-tuple-element.137) | copy-start | bytes 3076
  7.1 31.8 %copy-start.12 = (f32[1,1,256]{2,1,0:T(1,128)}, f32[1,1,256]{2,1,0:T(1,128)S(1)}, u32[]{:S(2)}) copy-start(f32[1,1,256]{2,1,0:T(1,128)S(1)} %get-tuple-element.142) | copy-start | bytes 3076
  7.1 31.8 %copy-start.14 = (f32[1,1,256]{2,1,0:T(1,128)}, f32[1,1,256]{2,1,0:T(1,128)S(1)}, u32[]{:S(2)}) copy-start(f32[1,1,256]{2,1,0:T(1,128)S(1)} %get-tuple-element.143) | copy-start | bytes 3076
  7.1 31.8 %copy-start.16 = (f32[1,1,256]{2,1,0:T(1,128)}, f32[1,1,256]{2,1,0:T(1,128)S(1)}, u32[]{:S(2)}) copy-start(f32[1,1,256]{2,1,0:T(1,128)S(1)} %get-tuple-element.144) | copy-start | bytes 3076
  7.1 31.8 %copy-start.18 = (f32[1,1,256]{2,1,0:T(1,128)}, f32[1,1,256]{2,1,0:T(1,128)S(1)}, u32[]{:S(2)}) copy-start(f32[1,1,256]{2,1,0:T(1,128)S(1)} %get-tuple-element.145) | copy-start | bytes 3076
  7.1 31.8 %copy-start.36 = (f32[1,1,256]{2,1,0:T(1,128)}, f32[1,1,256]{2,1,0:T(1,128)S(1)}, u32[]{:S(2)}) copy-start(f32[1,1,256]{2,1,0:T(1,128)S(1)} %get-tuple-element.138) | copy-start | bytes 3076
  7.1 31.8 %copy-start.38 = (f32[1,1,256]{2,1,0:T(1,128)}, f32[1,1,256]{2,1,0:T(1,128)S(1)}, u32[]{:S(2)}) copy-start(f32[1,1,256]{2,1,0:T(1,128)S(1)} %get-tuple-element.139) | copy-start | bytes 3076
  7.1 31.8 %copy-start.40 = (f32[1,1,256]{2,1,0:T(1,128)}, f32[1,1,256]{2,1,0:T(1,128)S(1)}, u32[]{:S(2)}) copy-start(f32[1,1,256]{2,1,0:T(1,128)S(1)} %get-tuple-element.140) | copy-start | bytes 3076
  7.1 31.8 %copy-start.42 = (f32[1,1,256]{2,1,0:T(1,128)}, f32[1,1,256]{2,1,0:T(1,128)S(1)}, u32[]{:S(2)}) copy-start(f32[1,1,256]{2,1,0:T(1,128)S(1)} %get-tuple-element.141) | copy-start | bytes 3076
  7.2 31.8 %copy-start.20 = (f32[1,1,256]{2,1,0:T(1,128)}, f32[1,1,256]{2,1,0:T(1,128)S(1)}, u32[]{:S(2)}) copy-start(f32[1,1,256]{2,1,0:T(1,128)S(1)} %get-tuple-element.118) | copy-start | bytes 3076
  7.2 31.8 %copy-start.44 = (f32[1,1,256]{2,1,0:T(1,128)}, f32[1,1,256]{2,1,0:T(1,128)S(1)}, u32[]{:S(2)}) copy-start(f32[1,1,256]{2,1,0:T(1,128)S(1)} %get-tuple-element.134) | copy-start | bytes 3076
  7.2 31.8 %copy-start.46 = (f32[1,1,256]{2,1,0:T(1,128)}, f32[1,1,256]{2,1,0:T(1,128)S(1)}, u32[]{:S(2)}) copy-start(f32[1,1,256]{2,1,0:T(1,128)S(1)} %get-tuple-element.135) | copy-start | bytes 3076
  7.2 31.8 %copy-start.48 = (f32[1,1,256]{2,1,0:T(1,128)}, f32[1,1,256]{2,1,0:T(1,128)S(1)}, u32[]{:S(2)}) copy-start(f32[1,1,256]{2,1,0:T(1,128)S(1)} %get-tuple-element.136) | copy-start | bytes 3076
  7.2 31.8 %copy-start.62 = (f32[1,1,256]{2,1,0:T(1,128)}, f32[1,1,256]{2,1,0:T(1,128)S(1)}, u32[]{:S(2)}) copy-start(f32[1,1,256]{2,1,0:T(1,128)S(1)} %get-tuple-element.119) | copy-start | bytes 3076
  7.3 31.8 %copy-start.64 = (f32[1,1,256]{2,1,0:T(1,128)}, f32[1,1,256]{2,1,0:T(1,128)S(1)}, u32[]{:S(2)}) copy-start(f32[1,1,256]{2,1,0:T(1,128)S(1)} %get-tuple-element.127) | copy-start | bytes 3076
  7.3 31.8 %copy-start.66 = (f32[1,1,256]{2,1,0:T(1,128)}, f32[1,1,256]{2,1,0:T(1,128)S(1)}, u32[]{:S(2)}) copy-start(f32[1,1,256]{2,1,0:T(1,128)S(1)} %get-tuple-element.128) | copy-start | bytes 3076
  7.3 31.8 %copy-start.68 = (f32[1,1,256]{2,1,0:T(1,128)}, f32[1,1,256]{2,1,0:T(1,128)S(1)}, u32[]{:S(2)}) copy-start(f32[1,1,256]{2,1,0:T(1,128)S(1)} %get-tuple-element.129) | copy-start | bytes 3076
  7.3 31.8 %copy-start.70 = (f32[1,1,256]{2,1,0:T(1,128)}, f32[1,1,256]{2,1,0:T(1,128)S(1)}, u32[]{:S(2)}) copy-start(f32[1,1,256]{2,1,0:T(1,128)S(1)} %get-tuple-element.130) | copy-start | bytes 3076
  7.3 31.8 %copy-start.72 = (f32[1,1,256]{2,1,0:T(1,128)}, f32[1,1,256]{2,1,0:T(1,128)S(1)}, u32[]{:S(2)}) copy-start(f32[1,1,256]{2,1,0:T(1,128)S(1)} %get-tuple-element.131) | copy-start | bytes 3076
  7.3 31.8 %copy-start.74 = (f32[1,1,256]{2,1,0:T(1,128)}, f32[1,1,256]{2,1,0:T(1,128)S(1)}, u32[]{:S(2)}) copy-start(f32[1,1,256]{2,1,0:T(1,128)S(1)} %get-tuple-element.132) | copy-start | bytes 3076
  7.3 31.8 %copy-start.76 = (f32[1,1,256]{2,1,0:T(1,128)}, f32[1,1,256]{2,1,0:T(1,128)S(1)}, u32[]{:S(2)}) copy-start(f32[1,1,256]{2,1,0:T(1,128)S(1)} %get-tuple-element.133) | copy-start | bytes 3076
  25.7 13.3 %copy-start.82 = (f32[1,1,256]{2,1,0:T(1,128)S(1)}, f32[1,1,256]{2,1,0:T(1,128)}, u32[]{:S(2)}) copy-start(f32[1,1,256]{2,1,0:T(1,128)} %copy-done.81) | copy-start | bytes 3076
  27.4 15.7 %copy-start.1 = (bf16[4,256,256]{2,1,0:T(8,128)(2,1)}, bf16[4,256,256]{2,1,0:T(8,128)(2,1)S(1)}, u32[]{:S(2)}) copy-start(bf16[4,256,256]{2,1,0:T(8,128)(2,1)S(1)} %fusion.175) | copy-start | bytes 1572868
  27.5 15.3 %copy-start.8 = (bf16[512,256]{0,1:T(8,128)(2,1)S(1)}, bf16[512,256]{0,1:T(8,128)(2,1)}, u32[]{:S(2)}) copy-start(bf16[512,256]{0,1:T(8,128)(2,1)} %copy.22) | copy-start | bytes 786436
  28.3 24.3 %collective-permute-start.3 = (bf16[3,144,256]{2,1,0:T(8,128)(2,1)}, bf16[3,144,256]{2,1,0:T(8,128)(2,1)}, u32[]{:S(2)}, u32[]{:S(2)}) collective-permute-start(bf16[3,144,256]{2,1,0:T(8,128)(2,1)} %get-tuple-element.92), channel_id=1, source_target_pairs={{1,0},{2,1},{3,2},{4,3},{5,4},{6,5},{7,6},{8,7},{9,8},{10,9},{11,1... | collective-permute-start | bytes 663560 | tf_op jit(solution)/shard_map/ppermute | solution.py:99
  29.5 25.5 %collective-permute-start.2 = (bf16[3,144,256]{2,1,0:T(8,128)(2,1)}, bf16[3,144,256]{2,1,0:T(8,128)(2,1)}, u32[]{:S(2)}, u32[]{:S(2)}) collective-permute-start(bf16[3,144,256]{2,1,0:T(8,128)(2,1)} %get-tuple-element.91), channel_id=1, source_target_pairs={{0,1},{1,2},{2,3},{3,4},{4,5},{5,6},{6,7},{7,8},{8,9},{9,10},{10,1... | collective-permute-start | bytes 663560 | tf_op jit(solution)/shard_map/ppermute | solution.py:98
  44.1 17.0 %collective-permute-start.4 = (f32[4,128,256]{2,1,0:T(8,128)}, f32[4,128,256]{2,1,0:T(8,128)}, u32[]{:S(2)}, u32[]{:S(2)}) collective-permute-start(f32[4,128,256]{2,1,0:T(8,128)} %constant_dynamic-slice_fusion.1), channel_id=1, source_target_pairs={{0,1},{1,0},{2,3},{3,2},{4,5},{5,4},{6,7},{7,6},{8,9},{9,8},{10,11... | collective-permute-start | bytes 1572872 | tf_op jit(solution)/shard_map/ppermute | solution.py:69
  51.2 1.3 %collective-permute-start.6 = (f32[51,256]{1,0:T(8,128)S(1)}, f32[51,256]{1,0:T(8,128)S(1)}, u32[]{:S(2)}, u32[]{:S(2)}) collective-permute-start(f32[51,256]{1,0:T(8,128)S(1)} %concatenate.20), channel_id=1, source_target_pairs={{0,1},{1,0},{2,3},{3,2},{4,5},{5,4},{6,7},{7,6},{8,9},{9,8},{10,11... | collective-permute-start | bytes 156680 | tf_op jit(solution)/shard_map/ppermute | solution.py:69
  51.3 11.0 %collective-permute-start.5 = (f32[512,256]{1,0:T(8,128)S(1)}, f32[512,256]{1,0:T(8,128)S(1)}, u32[]{:S(2)}, u32[]{:S(2)}) collective-permute-start(f32[512,256]{1,0:T(8,128)S(1)} %constant_dynamic-slice_fusion), channel_id=1, source_target_pairs={{0,1},{1,0},{2,3},{3,2},{4,5},{5,4},{6,7},{7,6},{8,9},{9,8},{10,11... | collective-permute-start | bytes 1572872 | tf_op jit(solution)/shard_map/ppermute | solution.py:69
  62.6 11.2 %collective-permute-start.7 = (bf16[614,256]{1,0:T(8,128)(2,1)S(1)}, bf16[614,256]{1,0:T(8,128)(2,1)S(1)}, u32[]{:S(2)}, u32[]{:S(2)}) collective-permute-start(bf16[614,256]{1,0:T(8,128)(2,1)S(1)} %pad_maximum_fusion), channel_id=1, source_target_pairs={{0,2},{1,3},{2,0},{3,1},{4,6},{5,7},{6,4},{7,5},{8,10},{9,11},{10,... | collective-permute-start | bytes 943112 | tf_op jit(solution)/shard_map/ppermute | solution.py:77
  73.9 6.2 %collective-permute-start.8 = (bf16[358,256]{1,0:T(8,128)(2,1)S(1)}, bf16[358,256]{1,0:T(8,128)(2,1)S(1)}, u32[]{:S(2)}, u32[]{:S(2)}) collective-permute-start(bf16[358,256]{1,0:T(8,128)(2,1)S(1)} %pad_maximum_fusion.1), channel_id=1, source_target_pairs={{0,4},{1,5},{2,6},{3,7},{4,0},{5,1},{6,2},{7,3},{8,12},{9,13},{10,... | collective-permute-start | bytes 549896 | tf_op jit(solution)/shard_map/ppermute | solution.py:77
  80.4 7.4 %collective-permute-start.9 = (bf16[230,256]{1,0:T(8,128)(2,1)S(1)}, bf16[230,256]{1,0:T(8,128)(2,1)S(1)}, u32[]{:S(2)}, u32[]{:S(2)}) collective-permute-start(bf16[230,256]{1,0:T(8,128)(2,1)S(1)} %pad_maximum_fusion.2), channel_id=1, source_target_pairs={{0,8},{1,9},{2,10},{3,11},{4,12},{5,13},{6,14},{7,15},{8,0},{9,1},... | collective-permute-start | bytes 353288 | tf_op jit(solution)/shard_map/ppermute | solution.py:77
  (80 other events, 328.6 us)

commit v22 on v18

--- a/solution.py
+++ b/solution.py
@@ -100,6 +100,14 @@
     return low, high
 
 
+def pick_cols(values, tile_index, start_of, width):
+    chosen = None
+    for tile in range(start_of):
+        piece = lax.slice_in_dim(values, tile * TILE_COLS, tile * TILE_COLS + width, axis=1)
+        chosen = piece if chosen is None else jnp.where(tile_index == tile, piece, chosen)
+    return chosen
+
+
 def gelu_value(inputs):
     tangent = jnp.tanh(ROOT_TWO_PI * (inputs + CUBIC_TERM * inputs * inputs * inputs))
     return 0.5 * inputs * (1.0 + tangent)
@@ -146,14 +154,16 @@
     first_col = jnp.argmax(tissue.reshape(-1)).astype(jnp.int32) * TILE_COLS
     extended = padded_2(image, (("row", 0),), half_width)
     padded = jnp.pad(extended, ((0, 0), (half_width, half_width), (0, 0)))
-    window = lax.dynamic_slice_in_dim(padded, first_col, span, axis=1).astype(jnp.float32)
+    tile_count = image_cols // TILE_COLS
+    tile_at = first_col // TILE_COLS
+    window = pick_cols(padded, tile_at, tile_count, span).astype(jnp.float32)
     filtered = depthwise(window, kernel, image_rows, TILE_COLS)
     centre = jnp.mean(filtered, axis=-1, keepdims=True)
     centered = filtered - centre
     inv_std = lax.rsqrt(jnp.mean(centered * centered, axis=-1, keepdims=True) + EPSILON)
     standard = centered * inv_std
     normed = (standard * ln_gain).astype(jnp.bfloat16)
-    upstream = lax.dynamic_slice_in_dim(cotangent, first_col, TILE_COLS, axis=1).astype(jnp.float32)
+    upstream = pick_cols(cotangent, tile_at, tile_count, TILE_COLS).astype(jnp.float32)
     grad_out = (1.0 * layer_scale * upstream).astype(jnp.bfloat16)
 
     normed_flat = normed.reshape(-1, channels)
@@ -179,7 +189,7 @@
     )
     branch = branch.reshape(image_rows, TILE_COLS, channels)
     grad_norm = grad_norm.reshape(image_rows, TILE_COLS, channels)
-    image_tile = lax.dynamic_slice_in_dim(image, first_col, TILE_COLS, axis=1)
+    image_tile = pick_cols(image, tile_at, tile_count, TILE_COLS)
     out_tile = (image_tile.astype(jnp.float32) + 1.0 * layer_scale * branch).astype(jnp.bfloat16)
     block_out = lax.dynamic_update_slice_in_dim(image, out_tile, first_col, axis=1)
     scale_grad = jnp.sum(1.0 * branch * upstream, axis=(0, 1))

time: 79.8 us -> 79.1 us (level)
  waiting for transfers between devices: 16 us -> 15 us
  starting transfers between devices: 27.6 us -> 26.7 us
  other arithmetic: 18.6 us -> 19.4 us
    ppermute x3, starting transfers between devices: 13.8 us -> 13 us  [halving_reduce(): got = lax.ppermute(sent, axis, pairs)]
    slice x1 -> x2, local copies, waits for them, and re-layouts: 0.05 us -> 0.88 us  [the longest x1 0.83 us: pick_cols(): lax.slice_in_dim(values, tile * TILE_COLS, tile * TILE_COLS + width, axis=1)]
    ppermute x1, waiting for transfers between devices: 2.01 us -> 1.19 us  [padded_2(): lax.ppermute(lax.slice_in_dim(block, 0, width, axis=dim), axis, backward)]
  transfers between devices with their start and end apart: 10 -> 10, of which waited for: 4 -> 4; matrix products, arithmetic and copies ran while one was open for 16% -> 18% of each run, Pallas kernels for 0% -> 0%
where the time goes in v22:
time: 79.1 us; the launch traced here: 78.8 us
  starting transfers between devices  26.7 us (34%)
  other arithmetic  19.4 us (25%)
  waiting for transfers between devices  15 us (19%)
  local copies, waits for them, and re-layouts  7.94 us (10%)
  matrix products  6.51 us (8%)
  between operations  3.16 us (4%)
    ppermute x3, waiting for transfers between devices, halving_reduce(): got = lax.ppermute(sent, axis, pairs)  13.8 us
    ppermute x3, starting transfers between devices, halving_reduce(): got = lax.ppermute(sent, axis, pairs)  13 us
    ppermute x3, starting transfers between devices, halving_reduce(): got_q, got_r, got_whole = lax.ppermute((give_q, give_r, whole), axis, pairs)  6.21 us
    reduce_sum x1, other arithmetic, shards(): centre = jnp.mean(filtered, axis=-1, keepdims=True)  4.53 us
    add x1, other arithmetic, depthwise(): total + padded[row_tap:row_tap + image_rows, col_tap:col_tap + image_cols...  3.41 us
    reduce_sum x3, other arithmetic, kernel_terms(): jnp.sum(padded[row_tap:row_tap + image_rows, col_tap:col_tap + image_cols...  3.22 us
    add x4, other arithmetic, shards(): total + line[col_tap:col_tap + image_cols] * flipped[row_tap, col_tap]  2.66 us
    unnamed x183, local copies, waits for them, and re-layouts  2.55 us
  transfers between devices with their start and end apart: 10, of which 4 were waited for; matrix products, arithmetic and copies ran while one was open for 18% of the time, Pallas kernels for 0%

profile of v22, /device:TPU:0, one launch (start us, length us, event | category | flops | bytes accessed | tf_op | source)
XLA Modules:
  0.0 78.8 jit_solution(5469829581528041576)
XLA Ops:
  0.7 1.1 %copy.38 = bf16[4,256,256]{2,1,0:T(8,128)(2,1)S(1)} copy(bf16[4,256,256]{2,1,0:T(8,128)(2,1)} %param.8) | data formatting | bytes 1048576
  1.8 2.4 %collective-permute-start = (bf16[3,256,256]{2,1,0:T(8,128)(2,1)S(1)}, bf16[3,256,256]{2,1,0:T(8,128)(2,1)S(1)}, u32[]{:S(2)}, u32[]{:S(2)}) collective-permute-start(bf16[3,256,256]{2,1,0:T(8,128)(2,1)S(1)} %get-tuple-element.93), channel_id=1, source_target_pairs={{0,1},{1,2},{2,3},{3,4},{4,5},{5,6},{6,7},{7,8},{8,9},{9,10},{10,1... | collective-permute-start | bytes 1179656 | tf_op jit(solution)/shard_map/ppermute | solution.py:21
  4.2 1.3 %collective-permute-start.1 = (bf16[3,256,256]{2,1,0:T(8,128)(2,1)S(1)}, bf16[3,256,256]{2,1,0:T(8,128)(2,1)S(1)}, u32[]{:S(2)}, u32[]{:S(2)}) collective-permute-start(bf16[3,256,256]{2,1,0:T(8,128)(2,1)S(1)} %get-tuple-element.94), channel_id=1, source_target_pairs={{1,0},{2,1},{3,2},{4,3},{5,4},{6,5},{7,6},{8,7},{9,8},{10,9},{11,1... | collective-permute-start | bytes 1179656 | tf_op jit(solution)/shard_map/ppermute | solution.py:24
  5.5 0.7 bitcast_reduce_fusion
  7.0 0.6 fusion.227
  7.9 0.8 %fusion.220 = (bf16[4,128,256]{2,1,0:T(8,128)(2,1)}, bf16[4,128,256]{2,1,0:T(8,128)(2,1)}) fusion(bf16[4,256,256]{2,1,0:T(8,128)(2,1)S(1)} %copy.38), kind=kLoop, calls=%fused_computation.406 | loop fusion | bytes 1048576 | tf_op jit(solution)/shard_map/slice | solution.py:106
  8.7 1.2 %collective-permute-done.1 = bf16[3,256,256]{2,1,0:T(8,128)(2,1)S(1)} collective-permute-done((bf16[3,256,256]{2,1,0:T(8,128)(2,1)S(1)}, bf16[3,256,256]{2,1,0:T(8,128)(2,1)S(1)}, u32[]{:S(2)}, u32[]{:S(2)}) %collective-permute-start.1) | collective-permute-done | bytes 393248 | tf_op jit(solution)/shard_map/ppermute | solution.py:24
  9.9 0.3 fusion.17
  10.2 0.1 fusion.23
  10.8 4.5 %fusion.217 = (f32[4,128]{1,0:T(4,128)S(1)}, f32[4,128,256]{2,1,0:T(8,128)S(1)}) fusion(f32[256]{0:T(256)S(1)} %bitcast.237, f32[10,134,256]{2,1,0:T(8,128)S(1)} %fusion.23, f32[256]{0:T(256)S(1)} %bitcast.242, f32[256]{0:T(256)S(1)} %bitcast.187, f32[256]{0:T(256)S(1)} %bitcast.192, f32[256]{0:T(256)S(1)} %bitcast.197, f32[256]{0:T(256)S(1)} %bitcast.202, ...), kind=kLoop, calls=%fused_computation.403 | loop fusion | flops 12844544 | bytes 26266624 | tf_op jit(solution)/shard_map/reduce_sum | solution.py:161
  15.3 0.2 multiply_reduce_fusion.3
  15.6 0.2 multiply_convert_fusion.3
  15.8 1.9 %fusion.12 = (bf16[1024,512]{0,1:T(8,128)(2,1)}, f32[512,1024]{1,0:T(8,128)S(1)}) fusion(bf16[512,256]{1,0:T(8,128)(2,1)S(1)} %bitcast.165, bf16[256,1024]{1,0:T(8,128)(2,1)S(1)} %copy-done), kind=kOutput, calls=%fused_computation.115 | convolution fusion | flops 273154048 | bytes 3932160 | tf_op jit(solution)/shard_map/dot_general | solution.py:171
  17.7 0.8 %fusion.122 = (f32[256]{0:T(256)S(1)}, bf16[4,128,256]{2,1,0:T(8,128)(2,1)S(1)}, f32[512,256]{1,0:T(8,128)S(1)}) fusion(bf16[4,256,256]{2,1,0:T(8,128)(2,1)S(1)} %copy-done.2, pred[]{:T(512)S(6)} %eq.6, f32[256]{0:T(256)S(1)} %copy-done.87, bf16[1024,256]{1,0:T(8,128)(2,1)S(1)} %copy-done.6, f32[512,1024]{1,0:T(8,128)S(1)} %get-tuple-element.156), kind=kOutput, calls=%fused_computation.233 | convolution fusion | flops 273940224 | bytes 3934209 | tf_op jit(solution)/shard_map/dot_general | solution.py:173
  18.5 1.4 %fusion.7 = bf16[512,1024]{1,0:T(8,128)(2,1)S(1)} fusion(f32[512,1024]{1,0:T(8,128)S(1)} %get-tuple-element.156, bf16[512,256]{1,0:T(8,128)(2,1)S(1)} %bitcast.167, bf16[1024,256]{1,0:T(8,128)(2,1)S(1)} %copy-done.6), kind=kOutput, calls=%fused_computation.110 | convolution fusion | flops 278396928 | bytes 3932160 | tf_op jit(solution)/shard_map/dot_general | solution.py:174
  20.0 0.6 multiply_reduce_fusion.2
  20.6 0.3 multiply_reduce_fusion
  20.9 1.2 %fusion.169 = (f32[256]{0:T(256)S(1)}, f32[256]{0:T(256)S(1)}, f32[256]{0:T(256)S(1)}, f32[256]{0:T(256)S(1)}, f32[256]{0:T(256)S(1)}, /*index=5*/f32[256]{0:T(2...) fusion(f32[10,134,256]{2,1,0:T(8,128)S(1)} %fusion.23, ...), kind=kLoop, calls=%fused_computation.280 | loop fusion | flops 4584192 | bytes 8148992 | tf_op jit(solution)/shard_map/reduce_sum | solution.py:140
  22.2 1.0 %fusion.170 = (f32[256]{0:T(256)S(1)}, f32[256]{0:T(256)S(1)}, f32[256]{0:T(256)S(1)}, f32[256]{0:T(256)S(1)}, f32[256]{0:T(256)S(1)}, /*index=5*/f32[256]{0:T(2...) fusion(bf16[4,128,256]{2,1,0:T(8,128)(2,1)S(1)} %get-tuple-elem, ...), kind=kLoop, calls=%fused_computation.281 | loop fusion | flops 4845056 | bytes 9717760 | tf_op jit(solution)/shard_map/reduce_sum | solution.py:140
  23.2 1.0 %fusion.171 = (f32[256]{0:T(256)S(1)}, f32[256]{0:T(256)S(1)}, f32[256]{0:T(256)S(1)}, f32[256]{0:T(256)S(1)}, f32[256]{0:T(256)S(1)}, /*index=5*/f32[256]{0:T(2...) fusion(bf16[4,128,256]{2,1,0:T(8,128)(2,1)S(1)} %get-tuple-elem, ...), kind=kLoop, calls=%fused_computation.282 | loop fusion | flops 4845056 | bytes 9717760 | tf_op jit(solution)/shard_map/reduce_sum | solution.py:140
  24.2 0.8 %copy.22 = bf16[512,256]{0,1:T(8,128)(2,1)} copy(bf16[512,256]{1,0:T(8,128)(2,1)S(1)} %bitcast.166) | data formatting | bytes 524288 | tf_op jit(solution)/shard_map/reshape | solution.py:169
  25.0 0.2 concatenate.16
  25.2 6.0 %collective-permute-start.6 = (f32[51,256]{1,0:T(8,128)S(1)}, f32[51,256]{1,0:T(8,128)S(1)}, u32[]{:S(2)}, u32[]{:S(2)}) collective-permute-start(f32[51,256]{1,0:T(8,128)S(1)} %concatenate.16), channel_id=1, source_target_pairs={{0,1},{1,0},{2,3},{3,2},{4,5},{5,4},{6,7},{7,6},{8,9},{9,8},{10,11... | collective-permute-start | bytes 156680 | tf_op jit(solution)/shard_map/ppermute | solution.py:69
  31.2 1.7 %copy.25 = bf16[1024,512]{1,0:T(8,128)(2,1)S(1)} copy(bf16[1024,512]{0,1:T(8,128)(2,1)} %get-tuple-element.155) | data formatting | bytes 2097152 | tf_op jit(solution)/shard_map/convert_element_type | solution.py:172
  32.9 1.4 %convolution_bitcast_fusion = f32[2,2,2,2,64,256]{5,4,0,1,2,3:T(8,128)S(1)} fusion(bf16[2,2,2,2,64,512]{5,4,3,2,1,0:T(8,128)(2,1)S(1)} %bitcast.162, bf16[512,256,1,1,1,1]{1,0,5,4,3,2:T(8,128)(2,1)} %bitcast.168), kind=kOutput, calls=%fused_computation.121 | convolution fusion | flops 268435456 | bytes 2359296 | tf_op jit(solution)/shard_map/dot_general | solution.py:187
  34.3 0.1 copy.26
  34.5 0.7 copy-done.7
  35.2 0.4 copy-done.90
  35.6 0.4 fusion.18
  36.0 0.1 copy.24
  36.9 2.5 %collective-permute-start.2 = (bf16[3,256,256]{2,1,0:T(8,128)(2,1)S(1)}, bf16[3,256,256]{2,1,0:T(8,128)(2,1)S(1)}, u32[]{:S(2)}, u32[]{:S(2)}) collective-permute-start(bf16[3,256,256]{2,1,0:T(8,128)(2,1)S(1)} %get-tuple-element.89), channel_id=1, source_target_pairs={{0,1},{1,2},{2,3},{3,4},{4,5},{5,6},{6,7},{7,8},{8,9},{9,10},{10,1... | collective-permute-start | bytes 1179656 | tf_op jit(solution)/shard_map/ppermute | solution.py:98
  39.4 1.3 %collective-permute-start.3 = (bf16[3,256,256]{2,1,0:T(8,128)(2,1)S(1)}, bf16[3,256,256]{2,1,0:T(8,128)(2,1)S(1)}, u32[]{:S(2)}, u32[]{:S(2)}) collective-permute-start(bf16[3,256,256]{2,1,0:T(8,128)(2,1)S(1)} %get-tuple-element.90), channel_id=1, source_target_pairs={{1,0},{2,1},{3,2},{4,3},{5,4},{6,5},{7,6},{8,7},{9,8},{10,9},{11,1... | collective-permute-start | bytes 1179656 | tf_op jit(solution)/shard_map/ppermute | solution.py:99
  41.1 3.4 %fusion.115 = f32[4,134,256]{2,1,0:T(8,128)S(1)} fusion(f32[4,128,256]{2,1,0:T(8,128)S(1)} %get-tuple-element.95, f32[256]{0:T(256)S(1)} %bitcast.178, f32[256]{0:T(256)S(1)} %bitcast.183, f32[256]{0:T(256)S(1)} %bitcast.213, f32[256]{0:T(256)S(1)} %bitcast.233, f32[256]{0:T(256)S(1)} %bitcast.228, f32[256]{0:T(256)S(1)} %bitcast.223, f32[256]{0:T(256)S(1)} %bitcast.218, ...), kind=kLoop, calls=%fused_computation.226 | loop fusion | flops 13309952 | bytes 1123328 | tf_op jit(solution)/shard_map/add | solution.py:128
  44.6 0.8 %fusion.173 = bf16[4,256,256]{2,1,0:T(8,128)(2,1)S(1)} fusion(bf16[4,256,256]{2,1,0:T(8,128)(2,1)S(1)} %copy.38, s32[]{:T(128)S(6)} %select_n.101, f32[4,128,256]{2,1,0:T(8,128)S(1)} %bitcast.163, f32[256]{0:T(256)} %param.14, bf16[4,128,256]{2,1,0:T(8,128)(2,1)S(1)} %copy-done.4, bf16[4,128,256]{2,1,0:T(8,128)(2,1)S(1)} %copy-done.3, pred[]{:T(512)S(6)} %eq.6), kind=kLoop, calls=%fused_computation.296 | loop fusion | flops 655360 | bytes 1311749 | tf_op jit(solution)/shard_map/dynamic_update_slice | solution.py:194
  45.6 0.7 multiply_add_fusion.4
  46.6 4.8 %collective-permute-start.7 = (bf16[614,256]{1,0:T(8,128)(2,1)S(1)}, bf16[614,256]{1,0:T(8,128)(2,1)S(1)}, u32[]{:S(2)}, u32[]{:S(2)}) collective-permute-start(bf16[614,256]{1,0:T(8,128)(2,1)S(1)} %pad_maximum_fusion), channel_id=1, source_target_pairs={{0,2},{1,3},{2,0},{3,1},{4,6},{5,7},{6,4},{7,5},{8,10},{9,11},{10,... | collective-permute-start | bytes 943112 | tf_op jit(solution)/shard_map/ppermute | solution.py:77
  51.4 0.7 fusion.195
  52.0 0.7 multiply_add_fusion.3
  52.7 4.4 %collective-permute-done.7 = bf16[614,256]{1,0:T(8,128)(2,1)S(1)} collective-permute-done((bf16[614,256]{1,0:T(8,128)(2,1)S(1)}, bf16[614,256]{1,0:T(8,128)(2,1)S(1)}, u32[]{:S(2)}, u32[]{:S(2)}) %collective-permute-start.7) | collective-permute-done | bytes 314400 | tf_op jit(solution)/shard_map/ppermute | solution.py:77
  57.3 5.3 %collective-permute-start.8 = (bf16[358,256]{1,0:T(8,128)(2,1)S(1)}, bf16[358,256]{1,0:T(8,128)(2,1)S(1)}, u32[]{:S(2)}, u32[]{:S(2)}) collective-permute-start(bf16[358,256]{1,0:T(8,128)(2,1)S(1)} %pad_maximum_fusion.1), channel_id=1, source_target_pairs={{0,4},{1,5},{2,6},{3,7},{4,0},{5,1},{6,2},{7,3},{8,12},{9,13},{10,... | collective-permute-start | bytes 549896 | tf_op jit(solution)/shard_map/ppermute | solution.py:77
  62.7 0.7 fusion.177
  63.3 4.7 %collective-permute-done.8 = bf16[358,256]{1,0:T(8,128)(2,1)S(1)} collective-permute-done((bf16[358,256]{1,0:T(8,128)(2,1)S(1)}, bf16[358,256]{1,0:T(8,128)(2,1)S(1)}, u32[]{:S(2)}, u32[]{:S(2)}) %collective-permute-start.8) | collective-permute-done | bytes 183328 | tf_op jit(solution)/shard_map/ppermute | solution.py:77
  68.2 2.8 %collective-permute-start.9 = (bf16[230,256]{1,0:T(8,128)(2,1)S(1)}, bf16[230,256]{1,0:T(8,128)(2,1)S(1)}, u32[]{:S(2)}, u32[]{:S(2)}) collective-permute-start(bf16[230,256]{1,0:T(8,128)(2,1)S(1)} %pad_maximum_fusion.2), channel_id=1, source_target_pairs={{0,8},{1,9},{2,10},{3,11},{4,12},{5,13},{6,14},{7,15},{8,0},{9,1},... | collective-permute-start | bytes 353288 | tf_op jit(solution)/shard_map/ppermute | solution.py:77
  71.0 1.1 %fusion.21 = bf16[4,256,256]{2,1,0:T(8,128)(2,1)} fusion(f32[1,256,256]{2,1,0:T(8,128)S(1)} %fusion.177, f32[1,256,256]{2,1,0:T(8,128)S(1)} %multiply_add_fusion.3, f32[1,256,256]{2,1,0:T(8,128)S(1)} %multiply_add_fusion.4, f32[1,256,256]{2,1,0:T(8,128)S(1)} %fusion.195, f32[4,131,256]{2,1,0:T(8,128)S(1)} %get-tuple-element.86, ...), kind=kLoop, calls=%fused_computation.129 | loop fusion | flops 2359296 | bytes 3170306 | tf_op jit(solution)/shard_map/convert_element_type | solution.py:245
  72.1 4.7 %collective-permute-done.9 = bf16[230,256]{1,0:T(8,128)(2,1)S(1)} collective-permute-done((bf16[230,256]{1,0:T(8,128)(2,1)S(1)}, bf16[230,256]{1,0:T(8,128)(2,1)S(1)}, u32[]{:S(2)}, u32[]{:S(2)}) %collective-permute-start.9) | collective-permute-done | bytes 117792 | tf_op jit(solution)/shard_map/ppermute | solution.py:77
  76.9 0.6 fusion.212
  77.5 0.6 convert_add_fusion.8
  78.1 0.6 copy.30
  (228 shorter events, 1.7 us)
Async XLA Ops:
  0.6 15.2 %copy-start = (bf16[256,1024]{1,0:T(8,128)(2,1)S(1)}, bf16[256,1024]{1,0:T(8,128)(2,1)}, u32[]{:S(2)}) copy-start(bf16[256,1024]{1,0:T(8,128)(2,1)} %param.12) | copy-start | bytes 1572868
  0.6 4.9 %copy-start.88 = (s32[1,2]{1,0:T(1,128)S(1)}, s32[1,2]{1,0:T(1,128)}, u32[]{:S(2)}) copy-start(s32[1,2]{1,0:T(1,128)} %param.9) | copy-start | bytes 28
  0.7 6.2 %copy-start.8 = (f32[7,7,256]{2,1,0:T(8,128)S(1)}, f32[7,7,256]{2,1,0:T(8,128)}, u32[]{:S(2)}) copy-start(f32[7,7,256]{2,1,0:T(8,128)} %param.10) | copy-start | bytes 150532
  1.8 6.9 %collective-permute-start = (bf16[3,256,256]{2,1,0:T(8,128)(2,1)S(1)}, bf16[3,256,256]{2,1,0:T(8,128)(2,1)S(1)}, u32[]{:S(2)}, u32[]{:S(2)}) collective-permute-start(bf16[3,256,256]{2,1,0:T(8,128)(2,1)S(1)} %get-tuple-element.93), channel_id=1, source_target_pairs={{0,1},{1,2},{2,3},{3,4},{4,5},{5,6},{6,7},{7,8},{8,9},{9,10},{10,1... | collective-permute-start | bytes 1179656 | tf_op jit(solution)/shard_map/ppermute | solution.py:21
  4.2 5.7 %collective-permute-start.1 = (bf16[3,256,256]{2,1,0:T(8,128)(2,1)S(1)}, bf16[3,256,256]{2,1,0:T(8,128)(2,1)S(1)}, u32[]{:S(2)}, u32[]{:S(2)}) collective-permute-start(bf16[3,256,256]{2,1,0:T(8,128)(2,1)S(1)} %get-tuple-element.94), channel_id=1, source_target_pairs={{1,0},{2,1},{3,2},{4,3},{5,4},{6,5},{7,6},{8,7},{9,8},{10,9},{11,1... | collective-permute-start | bytes 1179656 | tf_op jit(solution)/shard_map/ppermute | solution.py:24
  10.7 4.8 %copy-start.77 = (f32[256]{0:T(256)S(1)}, f32[256]{0:T(256)}, u32[]{:S(2)}) copy-start(f32[256]{0:T(256)} %param.11) | copy-start | bytes 3076
  25.2 20.3 %collective-permute-start.6 = (f32[51,256]{1,0:T(8,128)S(1)}, f32[51,256]{1,0:T(8,128)S(1)}, u32[]{:S(2)}, u32[]{:S(2)}) collective-permute-start(f32[51,256]{1,0:T(8,128)S(1)} %concatenate.16), channel_id=1, source_target_pairs={{0,1},{1,0},{2,3},{3,2},{4,5},{5,4},{6,7},{7,6},{8,9},{9,8},{10,11... | collective-permute-start | bytes 156680 | tf_op jit(solution)/shard_map/ppermute | solution.py:69
  34.5 11.8 %collective-permute-start.5 = (f32[512,256]{1,0:T(8,128)S(1)}, f32[512,256]{1,0:T(8,128)S(1)}, u32[]{:S(2)}, u32[]{:S(2)}) collective-permute-start(f32[512,256]{1,0:T(8,128)S(1)} %constant_dynamic-slice_fusion), channel_id=1, source_target_pairs={{0,1},{1,0},{2,3},{3,2},{4,5},{5,4},{6,7},{7,6},{8,9},{9,8},{10,11... | collective-permute-start | bytes 1572872 | tf_op jit(solution)/shard_map/ppermute | solution.py:69
  36.1 4.6 %copy-start.10 = (f32[1,1,256]{2,1,0:T(1,128)S(1)}, f32[1,1,256]{2,1,0:T(1,128)}, u32[]{:S(2)}) copy-start(f32[1,1,256]{2,1,0:T(1,128)} %copy-done.9) | copy-start | bytes 3076
  36.1 4.6 %copy-start.12 = (f32[1,1,256]{2,1,0:T(1,128)S(1)}, f32[1,1,256]{2,1,0:T(1,128)}, u32[]{:S(2)}) copy-start(f32[1,1,256]{2,1,0:T(1,128)} %copy-done.11) | copy-start | bytes 3076
  36.2 4.6 %copy-start.14 = (f32[1,1,256]{2,1,0:T(1,128)S(1)}, f32[1,1,256]{2,1,0:T(1,128)}, u32[]{:S(2)}) copy-start(f32[1,1,256]{2,1,0:T(1,128)} %copy-done.13) | copy-start | bytes 3076
  36.2 4.6 %copy-start.16 = (f32[1,1,256]{2,1,0:T(1,128)S(1)}, f32[1,1,256]{2,1,0:T(1,128)}, u32[]{:S(2)}) copy-start(f32[1,1,256]{2,1,0:T(1,128)} %copy-done.15) | copy-start | bytes 3076
  36.2 4.6 %copy-start.18 = (f32[1,1,256]{2,1,0:T(1,128)S(1)}, f32[1,1,256]{2,1,0:T(1,128)}, u32[]{:S(2)}) copy-start(f32[1,1,256]{2,1,0:T(1,128)} %copy-done.17) | copy-start | bytes 3076
  36.2 4.6 %copy-start.20 = (f32[1,1,256]{2,1,0:T(1,128)S(1)}, f32[1,1,256]{2,1,0:T(1,128)}, u32[]{:S(2)}) copy-start(f32[1,1,256]{2,1,0:T(1,128)} %copy-done.19) | copy-start | bytes 3076
  36.2 4.6 %copy-start.22 = (f32[1,1,256]{2,1,0:T(1,128)S(1)}, f32[1,1,256]{2,1,0:T(1,128)}, u32[]{:S(2)}) copy-start(f32[1,1,256]{2,1,0:T(1,128)} %copy-done.21) | copy-start | bytes 3076
  36.2 4.6 %copy-start.24 = (f32[1,1,256]{2,1,0:T(1,128)S(1)}, f32[1,1,256]{2,1,0:T(1,128)}, u32[]{:S(2)}) copy-start(f32[1,1,256]{2,1,0:T(1,128)} %copy-done.23) | copy-start | bytes 3076
  36.2 4.6 %copy-start.26 = (f32[1,1,256]{2,1,0:T(1,128)S(1)}, f32[1,1,256]{2,1,0:T(1,128)}, u32[]{:S(2)}) copy-start(f32[1,1,256]{2,1,0:T(1,128)} %copy-done.25) | copy-start | bytes 3076
  36.2 4.6 %copy-start.28 = (f32[1,1,256]{2,1,0:T(1,128)S(1)}, f32[1,1,256]{2,1,0:T(1,128)}, u32[]{:S(2)}) copy-start(f32[1,1,256]{2,1,0:T(1,128)} %copy-done.27) | copy-start | bytes 3076
  36.2 4.6 %copy-start.30 = (f32[1,1,256]{2,1,0:T(1,128)S(1)}, f32[1,1,256]{2,1,0:T(1,128)}, u32[]{:S(2)}) copy-start(f32[1,1,256]{2,1,0:T(1,128)} %copy-done.29) | copy-start | bytes 3076
  36.2 4.6 %copy-start.32 = (f32[1,1,256]{2,1,0:T(1,128)S(1)}, f32[1,1,256]{2,1,0:T(1,128)}, u32[]{:S(2)}) copy-start(f32[1,1,256]{2,1,0:T(1,128)} %copy-done.31) | copy-start | bytes 3076
  36.3 4.6 %copy-start.34 = (f32[1,1,256]{2,1,0:T(1,128)S(1)}, f32[1,1,256]{2,1,0:T(1,128)}, u32[]{:S(2)}) copy-start(f32[1,1,256]{2,1,0:T(1,128)} %copy-done.33) | copy-start | bytes 3076
  36.3 4.6 %copy-start.36 = (f32[1,1,256]{2,1,0:T(1,128)S(1)}, f32[1,1,256]{2,1,0:T(1,128)}, u32[]{:S(2)}) copy-start(f32[1,1,256]{2,1,0:T(1,128)} %copy-done.35) | copy-start | bytes 3076
  36.3 4.6 %copy-start.38 = (f32[1,1,256]{2,1,0:T(1,128)S(1)}, f32[1,1,256]{2,1,0:T(1,128)}, u32[]{:S(2)}) copy-start(f32[1,1,256]{2,1,0:T(1,128)} %copy-done.37) | copy-start | bytes 3076
  36.3 4.6 %copy-start.40 = (f32[1,1,256]{2,1,0:T(1,128)S(1)}, f32[1,1,256]{2,1,0:T(1,128)}, u32[]{:S(2)}) copy-start(f32[1,1,256]{2,1,0:T(1,128)} %copy-done.39) | copy-start | bytes 3076
  36.3 4.6 %copy-start.42 = (f32[1,1,256]{2,1,0:T(1,128)S(1)}, f32[1,1,256]{2,1,0:T(1,128)}, u32[]{:S(2)}) copy-start(f32[1,1,256]{2,1,0:T(1,128)} %copy-done.41) | copy-start | bytes 3076
  36.3 4.6 %copy-start.44 = (f32[1,1,256]{2,1,0:T(1,128)S(1)}, f32[1,1,256]{2,1,0:T(1,128)}, u32[]{:S(2)}) copy-start(f32[1,1,256]{2,1,0:T(1,128)} %copy-done.43) | copy-start | bytes 3076
  36.3 4.6 %copy-start.46 = (f32[1,1,256]{2,1,0:T(1,128)S(1)}, f32[1,1,256]{2,1,0:T(1,128)}, u32[]{:S(2)}) copy-start(f32[1,1,256]{2,1,0:T(1,128)} %copy-done.45) | copy-start | bytes 3076
  36.3 4.6 %copy-start.48 = (f32[1,1,256]{2,1,0:T(1,128)S(1)}, f32[1,1,256]{2,1,0:T(1,128)}, u32[]{:S(2)}) copy-start(f32[1,1,256]{2,1,0:T(1,128)} %copy-done.47) | copy-start | bytes 3076
  36.3 4.6 %copy-start.50 = (f32[1,1,256]{2,1,0:T(1,128)S(1)}, f32[1,1,256]{2,1,0:T(1,128)}, u32[]{:S(2)}) copy-start(f32[1,1,256]{2,1,0:T(1,128)} %copy-done.49) | copy-start | bytes 3076
  36.3 4.6 %copy-start.52 = (f32[1,1,256]{2,1,0:T(1,128)S(1)}, f32[1,1,256]{2,1,0:T(1,128)}, u32[]{:S(2)}) copy-start(f32[1,1,256]{2,1,0:T(1,128)} %copy-done.51) | copy-start | bytes 3076
  36.4 4.6 %copy-start.54 = (f32[1,1,256]{2,1,0:T(1,128)S(1)}, f32[1,1,256]{2,1,0:T(1,128)}, u32[]{:S(2)}) copy-start(f32[1,1,256]{2,1,0:T(1,128)} %copy-done.53) | copy-start | bytes 3076
  36.4 4.6 %copy-start.56 = (f32[1,1,256]{2,1,0:T(1,128)S(1)}, f32[1,1,256]{2,1,0:T(1,128)}, u32[]{:S(2)}) copy-start(f32[1,1,256]{2,1,0:T(1,128)} %copy-done.55) | copy-start | bytes 3076
  36.4 4.6 %copy-start.58 = (f32[1,1,256]{2,1,0:T(1,128)S(1)}, f32[1,1,256]{2,1,0:T(1,128)}, u32[]{:S(2)}) copy-start(f32[1,1,256]{2,1,0:T(1,128)} %copy-done.57) | copy-start | bytes 3076
  36.4 4.6 %copy-start.60 = (f32[1,1,256]{2,1,0:T(1,128)S(1)}, f32[1,1,256]{2,1,0:T(1,128)}, u32[]{:S(2)}) copy-start(f32[1,1,256]{2,1,0:T(1,128)} %copy-done.59) | copy-start | bytes 3076
  36.4 4.6 %copy-start.62 = (f32[1,1,256]{2,1,0:T(1,128)S(1)}, f32[1,1,256]{2,1,0:T(1,128)}, u32[]{:S(2)}) copy-start(f32[1,1,256]{2,1,0:T(1,128)} %copy-done.61) | copy-start | bytes 3076
  36.4 4.6 %copy-start.64 = (f32[1,1,256]{2,1,0:T(1,128)S(1)}, f32[1,1,256]{2,1,0:T(1,128)}, u32[]{:S(2)}) copy-start(f32[1,1,256]{2,1,0:T(1,128)} %copy-done.63) | copy-start | bytes 3076
  36.4 4.6 %copy-start.66 = (f32[1,1,256]{2,1,0:T(1,128)S(1)}, f32[1,1,256]{2,1,0:T(1,128)}, u32[]{:S(2)}) copy-start(f32[1,1,256]{2,1,0:T(1,128)} %copy-done.65) | copy-start | bytes 3076
  36.4 4.6 %copy-start.68 = (f32[1,1,256]{2,1,0:T(1,128)S(1)}, f32[1,1,256]{2,1,0:T(1,128)}, u32[]{:S(2)}) copy-start(f32[1,1,256]{2,1,0:T(1,128)} %copy-done.67) | copy-start | bytes 3076
  36.4 4.6 %copy-start.70 = (f32[1,1,256]{2,1,0:T(1,128)S(1)}, f32[1,1,256]{2,1,0:T(1,128)}, u32[]{:S(2)}) copy-start(f32[1,1,256]{2,1,0:T(1,128)} %copy-done.69) | copy-start | bytes 3076
  36.4 4.6 %copy-start.72 = (f32[1,1,256]{2,1,0:T(1,128)S(1)}, f32[1,1,256]{2,1,0:T(1,128)}, u32[]{:S(2)}) copy-start(f32[1,1,256]{2,1,0:T(1,128)} %copy-done.71) | copy-start | bytes 3076
  36.6 9.8 %collective-permute-start.4 = (f32[4,128,256]{2,1,0:T(8,128)S(1)}, f32[4,128,256]{2,1,0:T(8,128)S(1)}, u32[]{:S(2)}, u32[]{:S(2)}) collective-permute-start(f32[4,128,256]{2,1,0:T(8,128)S(1)} %constant_dynamic-slice_fusion.1), channel_id=1, source_target_pairs={{0,1},{1,0},{2,3},{3,2},{4,5},{5,4},{6,7},{7,6},{8,9},{9,8},{10,11... | collective-permute-start | bytes 1572872 | tf_op jit(solution)/shard_map/ppermute | solution.py:69
  36.8 7.8 %copy-start.3 = (bf16[4,128,256]{2,1,0:T(8,128)(2,1)S(1)}, bf16[4,128,256]{2,1,0:T(8,128)(2,1)}, u32[]{:S(2)}) copy-start(bf16[4,128,256]{2,1,0:T(8,128)(2,1)} %get-tuple-element.91) | copy-start | bytes 786436
  36.8 7.8 %copy-start.4 = (bf16[4,128,256]{2,1,0:T(8,128)(2,1)S(1)}, bf16[4,128,256]{2,1,0:T(8,128)(2,1)}, u32[]{:S(2)}) copy-start(bf16[4,128,256]{2,1,0:T(8,128)(2,1)} %get-tuple-element.92) | copy-start | bytes 786436
  36.9 8.6 %collective-permute-start.2 = (bf16[3,256,256]{2,1,0:T(8,128)(2,1)S(1)}, bf16[3,256,256]{2,1,0:T(8,128)(2,1)S(1)}, u32[]{:S(2)}, u32[]{:S(2)}) collective-permute-start(bf16[3,256,256]{2,1,0:T(8,128)(2,1)S(1)} %get-tuple-element.89), channel_id=1, source_target_pairs={{0,1},{1,2},{2,3},{3,4},{4,5},{5,6},{6,7},{7,8},{8,9},{9,10},{10,1... | collective-permute-start | bytes 1179656 | tf_op jit(solution)/shard_map/ppermute | solution.py:98
  39.4 6.1 %collective-permute-start.3 = (bf16[3,256,256]{2,1,0:T(8,128)(2,1)S(1)}, bf16[3,256,256]{2,1,0:T(8,128)(2,1)S(1)}, u32[]{:S(2)}, u32[]{:S(2)}) collective-permute-start(bf16[3,256,256]{2,1,0:T(8,128)(2,1)S(1)} %get-tuple-element.90), channel_id=1, source_target_pairs={{1,0},{2,1},{3,2},{4,3},{5,4},{6,5},{7,6},{8,7},{9,8},{10,9},{11,1... | collective-permute-start | bytes 1179656 | tf_op jit(solution)/shard_map/ppermute | solution.py:99
  46.6 10.5 %collective-permute-start.7 = (bf16[614,256]{1,0:T(8,128)(2,1)S(1)}, bf16[614,256]{1,0:T(8,128)(2,1)S(1)}, u32[]{:S(2)}, u32[]{:S(2)}) collective-permute-start(bf16[614,256]{1,0:T(8,128)(2,1)S(1)} %pad_maximum_fusion), channel_id=1, source_target_pairs={{0,2},{1,3},{2,0},{3,1},{4,6},{5,7},{6,4},{7,5},{8,10},{9,11},{10,... | collective-permute-start | bytes 943112 | tf_op jit(solution)/shard_map/ppermute | solution.py:77
  57.3 10.7 %collective-permute-start.8 = (bf16[358,256]{1,0:T(8,128)(2,1)S(1)}, bf16[358,256]{1,0:T(8,128)(2,1)S(1)}, u32[]{:S(2)}, u32[]{:S(2)}) collective-permute-start(bf16[358,256]{1,0:T(8,128)(2,1)S(1)} %pad_maximum_fusion.1), channel_id=1, source_target_pairs={{0,4},{1,5},{2,6},{3,7},{4,0},{5,1},{6,2},{7,3},{8,12},{9,13},{10,... | collective-permute-start | bytes 549896 | tf_op jit(solution)/shard_map/ppermute | solution.py:77
  68.2 8.6 %collective-permute-start.9 = (bf16[230,256]{1,0:T(8,128)(2,1)S(1)}, bf16[230,256]{1,0:T(8,128)(2,1)S(1)}, u32[]{:S(2)}, u32[]{:S(2)}) collective-permute-start(bf16[230,256]{1,0:T(8,128)(2,1)S(1)} %pad_maximum_fusion.2), channel_id=1, source_target_pairs={{0,8},{1,9},{2,10},{3,11},{4,12},{5,13},{6,14},{7,15},{8,0},{9,1},... | collective-permute-start | bytes 353288 | tf_op jit(solution)/shard_map/ppermute | solution.py:77
  (53 other events, 160.7 us)

commit v23 on v22

--- a/solution.py
+++ b/solution.py
@@ -191,7 +191,12 @@
     grad_norm = grad_norm.reshape(image_rows, TILE_COLS, channels)
     image_tile = pick_cols(image, tile_at, tile_count, TILE_COLS)
     out_tile = (image_tile.astype(jnp.float32) + 1.0 * layer_scale * branch).astype(jnp.bfloat16)
-    block_out = lax.dynamic_update_slice_in_dim(image, out_tile, first_col, axis=1)
+    block_out = image
+    for tile in range(tile_count):
+        placed = jnp.concatenate(
+            [image[:, : tile * TILE_COLS], out_tile, image[:, (tile + 1) * TILE_COLS :]], axis=1
+        )
+        block_out = jnp.where(tile_at == tile, placed, block_out)
     scale_grad = jnp.sum(1.0 * branch * upstream, axis=(0, 1))
     gain_grad = jnp.sum(grad_norm * standard, axis=(0, 1))
     grad_std = grad_norm * ln_gain
@@ -220,9 +225,12 @@
         lo, hi = max(left, 0), min(left + span, image_cols)
         placed = jnp.pad(own[:, lo - left : hi - left], ((0, 0), (lo, image_cols - hi), (0, 0)))
         own_full = jnp.where(tile_index == tile, placed, own_full)
-    grad_conv = lax.dynamic_update_slice_in_dim(
-        jnp.zeros_like(image), grad_tile, first_col, axis=1
-    )
+    grad_conv = jnp.zeros_like(image)
+    for tile in range(tile_count):
+        placed = jnp.pad(
+            grad_tile, ((0, 0), (tile * TILE_COLS, image_cols - (tile + 1) * TILE_COLS), (0, 0))
+        )
+        grad_conv = jnp.where(tile_at == tile, placed, grad_conv)
     low, high = halo_rows(grad_conv, "row", half_width)
     edge = ((0, 0), (half_width, half_width), (0, 0))
     low = jnp.pad(low.astype(jnp.float32), edge)

time: 79.1 us -> 80.8 us (1.021)
  local copies, waits for them, and re-layouts: 7.94 us -> 11.2 us
  starting transfers between devices: 26.7 us -> 24.1 us
  other arithmetic: 19.4 us -> 21.4 us
  waiting for transfers between devices: 15 us -> 14 us
    slice x3, local copies, waits for them, and re-layouts: 0.61 us -> 3.5 us  [depthwise(): kernel[row_tap, col_tap]]
    ppermute x3, starting transfers between devices: 6.21 us -> 3.83 us  [halving_reduce(): got_q, got_r, got_whole = lax.ppermute((give_q, give_r, whole), axis, pairs)]
    slice x1, local copies, waits for them, and re-layouts: 0.05 us -> 1.25 us  [padded_2(): lax.slice_in_dim(block, block.shape[dim] - width, None, axis=dim)]
    ppermute x1, waiting for transfers between devices: 1.19 us -> 0.01 us  [padded_2(): lax.ppermute(lax.slice_in_dim(block, 0, width, axis=dim), axis, backward)]
    select_n x0 -> x2, other arithmetic: none -> 1.15 us  [the longest x1 1.01 us: shards(): block_out = jnp.where(tile_at == tile, placed, block_out)]
    reduce_sum x0 -> x1, other arithmetic: none -> 0.93 us  [shards(): scale_grad = jnp.sum(1.0 * branch * upstream, axis=(0, 1))]
    unnamed x183 -> x178, local copies, waits for them, and re-layouts: 2.55 us -> 1.75 us
  transfers between devices with their start and end apart: 10 -> 10, of which waited for: 4 -> 3; matrix products, arithmetic and copies ran while one was open for 18% -> 22% of each run, Pallas kernels for 0% -> 0%
where the time goes in v23:
time: 80.8 us; the launch traced here: 80.2 us
  starting transfers between devices  24.1 us (30%)
  other arithmetic  21.4 us (26%)
  waiting for transfers between devices  14 us (17%)
  local copies, waits for them, and re-layouts  11.2 us (14%)
  matrix products  6.48 us (8%)
  between operations  3.08 us (4%)
    ppermute x3, waiting for transfers between devices, halving_reduce(): got = lax.ppermute(sent, axis, pairs)  14 us
    ppermute x3, starting transfers between devices, halving_reduce(): got = lax.ppermute(sent, axis, pairs)  12.7 us
    reduce_sum x1, other arithmetic, shards(): centre = jnp.mean(filtered, axis=-1, keepdims=True)  4.53 us
    ppermute x3, starting transfers between devices, halving_reduce(): got_q, got_r, got_whole = lax.ppermute((give_q, give_r, whole), axis, pairs)  3.83 us
    slice x3, local copies, waits for them, and re-layouts, depthwise(): kernel[row_tap, col_tap]  3.5 us
    add x1, other arithmetic, depthwise(): total + padded[row_tap:row_tap + image_rows, col_tap:col_tap + image_cols...  3.37 us
    reduce_sum x3, other arithmetic, kernel_terms(): jnp.sum(padded[row_tap:row_tap + image_rows, col_tap:col_tap + image_cols...  3.25 us
    add x4, other arithmetic, shards(): total + line[col_tap:col_tap + image_cols] * flipped[row_tap, col_tap]  2.66 us
  transfers between devices with their start and end apart: 10, of which 3 were waited for; matrix products, arithmetic and copies ran while one was open for 22% of the time, Pallas kernels for 0%

profile of v23, /device:TPU:0, one launch (start us, length us, event | category | flops | bytes accessed | tf_op | source)
XLA Modules:
  0.0 80.2 jit_solution(15566793705550757520)
XLA Ops:
  0.7 1.3 %fusion.220 = (bf16[3,256,256]{2,1,0:T(8,128)(2,1)S(1)}, bf16[3,256,256]{2,1,0:T(8,128)(2,1)S(1)}) fusion(bf16[4,256,256]{2,1,0:T(8,128)(2,1)} %param.8), kind=kLoop, calls=%fused_computation.408 | loop fusion | bytes 1572864 | tf_op jit(solution)/shard_map/slice | solution.py:22
  1.9 2.4 %collective-permute-start = (bf16[3,256,256]{2,1,0:T(8,128)(2,1)S(1)}, bf16[3,256,256]{2,1,0:T(8,128)(2,1)S(1)}, u32[]{:S(2)}, u32[]{:S(2)}) collective-permute-start(bf16[3,256,256]{2,1,0:T(8,128)(2,1)S(1)} %get-tuple-element.93), channel_id=1, source_target_pairs={{0,1},{1,2},{2,3},{3,4},{4,5},{5,6},{6,7},{7,8},{8,9},{9,10},{10,1... | collective-permute-start | bytes 1179656 | tf_op jit(solution)/shard_map/ppermute | solution.py:21
  4.3 1.3 %collective-permute-start.1 = (bf16[3,256,256]{2,1,0:T(8,128)(2,1)S(1)}, bf16[3,256,256]{2,1,0:T(8,128)(2,1)S(1)}, u32[]{:S(2)}, u32[]{:S(2)}) collective-permute-start(bf16[3,256,256]{2,1,0:T(8,128)(2,1)S(1)} %get-tuple-element.94), channel_id=1, source_target_pairs={{1,0},{2,1},{3,2},{4,3},{5,4},{6,5},{7,6},{8,7},{9,8},{10,9},{11,1... | collective-permute-start | bytes 1179656 | tf_op jit(solution)/shard_map/ppermute | solution.py:24
  5.6 1.3 %bitcast_reduce_fusion = (s32[]{:T(128)}, s32[]{:T(128)}) fusion(s32[1,2]{1,0:T(1,128)} %param.9), kind=kLoop, calls=%fused_computation.399 | loop fusion | flops 7 | bytes 16 | tf_op jit(solution)/shard_map/shards/reduce | solution.py:154
  7.6 1.0 %fusion.224 = (f32[1,1,256]{2,1,0:T(1,128)S(1)}, f32[1,1,256]{2,1,0:T(1,128)S(1)}, f32[1,1,256]{2,1,0:T(1,128)S(1)}, f32[1,1,256]{2,1,0:T(1,128)S(1)}, f32[1,1,2...) fusion(f32[7,7,256]{2,1,0:T(8,128)} %param.10), kind=kLoop, calls=%fused_computation.412 | loop fusion | bytes 38912 | tf_op jit(solution)/shard_map/slice | solution.py:130
  8.7 1.6 %fusion.225 = (f32[1,1,256]{2,1,0:T(1,128)S(1)}, f32[1,1,256]{2,1,0:T(1,128)S(1)}, f32[1,1,256]{2,1,0:T(1,128)S(1)}, f32[1,1,256]{2,1,0:T(1,128)S(1)}, f32[1,1,2...) fusion(f32[7,7,256]{2,1,0:T(8,128)} %param.10), kind=kLoop, calls=%fused_computation.413 | loop fusion | bytes 38912 | tf_op jit(solution)/shard_map/slice | solution.py:130
  10.5 0.9 %fusion.226 = (f32[1,1,256]{2,1,0:T(1,128)S(1)}, f32[1,1,256]{2,1,0:T(1,128)S(1)}, f32[1,1,256]{2,1,0:T(1,128)S(1)}, f32[1,1,256]{2,1,0:T(1,128)S(1)}, f32[1,1,2...) fusion(f32[7,7,256]{2,1,0:T(8,128)} %param.10), kind=kLoop, calls=%fused_computation.414 | loop fusion | bytes 22528 | tf_op jit(solution)/shard_map/slice | solution.py:130
  11.5 0.8 %fusion.219 = (bf16[4,128,256]{2,1,0:T(8,128)(2,1)}, bf16[4,128,256]{2,1,0:T(8,128)(2,1)}) fusion(bf16[4,256,256]{2,1,0:T(8,128)(2,1)S(1)} %copy-done.1), kind=kLoop, calls=%fused_computation.407 | loop fusion | bytes 1048576 | tf_op jit(solution)/shard_map/slice | solution.py:106
  12.4 0.3 fusion.17
  13.2 4.5 %fusion.216 = (f32[4,128]{1,0:T(4,128)S(1)}, f32[4,128,256]{2,1,0:T(8,128)S(1)}) fusion(f32[256]{0:T(256)S(1)} %bitcast.237, f32[10,134,256]{2,1,0:T(8,128)S(1)} %fusion.23, f32[256]{0:T(256)S(1)} %bitcast.242, f32[256]{0:T(256)S(1)} %bitcast.187, f32[256]{0:T(256)S(1)} %bitcast.192, f32[256]{0:T(256)S(1)} %bitcast.197, f32[256]{0:T(256)S(1)} %bitcast.202, ...), kind=kLoop, calls=%fused_computation.404 | loop fusion | flops 12844544 | bytes 26266624 | tf_op jit(solution)/shard_map/reduce_sum | solution.py:161
  17.8 0.2 multiply_reduce_fusion.3
  18.0 0.2 multiply_convert_fusion.3
  18.3 1.9 %fusion.12 = (bf16[1024,512]{0,1:T(8,128)(2,1)}, f32[512,1024]{1,0:T(8,128)S(1)}) fusion(bf16[512,256]{1,0:T(8,128)(2,1)S(1)} %bitcast.165, bf16[256,1024]{1,0:T(8,128)(2,1)S(1)} %copy-done), kind=kOutput, calls=%fused_computation.115 | convolution fusion | flops 273154048 | bytes 3932160 | tf_op jit(solution)/shard_map/dot_general | solution.py:171
  20.1 0.8 fusion.22
  20.9 0.2 copy-done.2
  21.2 0.9 %fusion.122 = (f32[256]{0:T(256)S(1)}, bf16[4,128,256]{2,1,0:T(8,128)(2,1)S(1)}, bf16[4,128,256]{2,1,0:T(8,128)(2,1)}) fusion(bf16[4,256,256]{2,1,0:T(8,128)(2,1)S(1)} %copy-done.2, pred[]{:T(512)S(6)} %eq.6, f32[512,256]{1,0:T(8,128)S(1)} %fusion.22, f32[256]{0:T(256)S(1)} %copy-done.85, bf16[4,256,256]{2,1,0:T(8,128)(2,1)S(1)} %copy-done.1), kind=kLoop, calls=%fused_computation.233 | loop fusion | flops 1441536 | bytes 2099201 | tf_op jit(solution)/shard_map/reduce_sum | solution.py:200
  22.1 1.4 %fusion.7 = bf16[512,1024]{1,0:T(8,128)(2,1)S(1)} fusion(f32[512,1024]{1,0:T(8,128)S(1)} %get-tuple-element.154, bf16[512,256]{1,0:T(8,128)(2,1)S(1)} %bitcast.167, bf16[1024,256]{1,0:T(8,128)(2,1)S(1)} %copy-done.86), kind=kOutput, calls=%fused_computation.110 | convolution fusion | flops 278396928 | bytes 3932160 | tf_op jit(solution)/shard_map/dot_general | solution.py:174
  23.6 0.6 multiply_reduce_fusion.2
  24.2 0.3 multiply_reduce_fusion
  24.6 1.5 %fusion.170 = (f32[256]{0:T(256)S(1)}, f32[256]{0:T(256)S(1)}, f32[256]{0:T(256)S(1)}, f32[256]{0:T(256)S(1)}, f32[256]{0:T(256)S(1)}, /*index=5*/f32[256]{0:T(2...) fusion(f32[10,134,256]{2,1,0:T(8,128)S(1)} %fusion.23, ...), kind=kLoop, calls=%fused_computation.281 | loop fusion | flops 5893632 | bytes 10775552 | tf_op jit(solution)/shard_map/reduce_sum | solution.py:140
  26.1 1.0 %fusion.171 = (f32[256]{0:T(256)S(1)}, f32[256]{0:T(256)S(1)}, f32[256]{0:T(256)S(1)}, f32[256]{0:T(256)S(1)}, f32[256]{0:T(256)S(1)}, /*index=5*/f32[256]{0:T(2...) fusion(bf16[4,128,256]{2,1,0:T(8,128)(2,1)S(1)} %get-tuple-elem, ...), kind=kLoop, calls=%fused_computation.282 | loop fusion | flops 4845056 | bytes 9717760 | tf_op jit(solution)/shard_map/reduce_sum | solution.py:140
  27.1 0.7 fusion.169
  27.8 0.8 %copy.22 = bf16[512,256]{0,1:T(8,128)(2,1)} copy(bf16[512,256]{1,0:T(8,128)(2,1)S(1)} %bitcast.166) | data formatting | bytes 524288 | tf_op jit(solution)/shard_map/reshape | solution.py:169
  28.7 0.2 concatenate.24
  28.9 3.7 %collective-permute-start.6 = (f32[51,256]{1,0:T(8,128)S(1)}, f32[51,256]{1,0:T(8,128)S(1)}, u32[]{:S(2)}, u32[]{:S(2)}) collective-permute-start(f32[51,256]{1,0:T(8,128)S(1)} %concatenate.24), channel_id=1, source_target_pairs={{0,1},{1,0},{2,3},{3,2},{4,5},{5,4},{6,7},{7,6},{8,9},{9,8},{10,11... | collective-permute-start | bytes 156680 | tf_op jit(solution)/shard_map/ppermute | solution.py:69
  32.6 1.7 %copy.25 = bf16[1024,512]{1,0:T(8,128)(2,1)S(1)} copy(bf16[1024,512]{0,1:T(8,128)(2,1)} %get-tuple-element.153) | data formatting | bytes 2097152 | tf_op jit(solution)/shard_map/convert_element_type | solution.py:172
  34.2 1.4 %convolution_bitcast_fusion = f32[2,2,2,2,64,256]{5,4,0,1,2,3:T(8,128)S(1)} fusion(bf16[2,2,2,2,64,512]{5,4,3,2,1,0:T(8,128)(2,1)S(1)} %bitcast.163, bf16[512,256,1,1,1,1]{1,0,5,4,3,2:T(8,128)(2,1)} %bitcast.168), kind=kOutput, calls=%fused_computation.121 | convolution fusion | flops 268435456 | bytes 2359296 | tf_op jit(solution)/shard_map/dot_general | solution.py:187
  35.9 0.7 copy-done.7
  36.6 0.4 copy-done.88
  36.9 0.4 fusion.18
  38.2 2.6 %collective-permute-start.2 = (bf16[3,256,256]{2,1,0:T(8,128)(2,1)S(1)}, bf16[3,256,256]{2,1,0:T(8,128)(2,1)S(1)}, u32[]{:S(2)}, u32[]{:S(2)}) collective-permute-start(bf16[3,256,256]{2,1,0:T(8,128)(2,1)S(1)} %get-tuple-element.89), channel_id=1, source_target_pairs={{0,1},{1,2},{2,3},{3,4},{4,5},{5,6},{6,7},{7,8},{8,9},{9,10},{10,1... | collective-permute-start | bytes 1179656 | tf_op jit(solution)/shard_map/ppermute | solution.py:98
  40.8 1.3 %collective-permute-start.3 = (bf16[3,256,256]{2,1,0:T(8,128)(2,1)S(1)}, bf16[3,256,256]{2,1,0:T(8,128)(2,1)S(1)}, u32[]{:S(2)}, u32[]{:S(2)}) collective-permute-start(bf16[3,256,256]{2,1,0:T(8,128)(2,1)S(1)} %get-tuple-element.90), channel_id=1, source_target_pairs={{1,0},{2,1},{3,2},{4,3},{5,4},{6,5},{7,6},{8,7},{9,8},{10,9},{11,1... | collective-permute-start | bytes 1179656 | tf_op jit(solution)/shard_map/ppermute | solution.py:99
  42.5 3.4 %fusion.115 = f32[4,134,256]{2,1,0:T(8,128)S(1)} fusion(f32[4,128,256]{2,1,0:T(8,128)S(1)} %convert_element_type.173, f32[256]{0:T(256)S(1)} %bitcast.178, f32[256]{0:T(256)S(1)} %bitcast.183, f32[256]{0:T(256)S(1)} %bitcast.213, f32[256]{0:T(256)S(1)} %bitcast.233, f32[256]{0:T(256)S(1)} %bitcast.228, f32[256]{0:T(256)S(1)} %bitcast.223, ...), kind=kLoop, calls=%fused_computation.226 | loop fusion | flops 13309952 | bytes 1123328 | tf_op jit(solution)/shard_map/add | solution.py:128
  46.0 1.0 %maximum_select_fusion = bf16[4,256,256]{2,1,0:T(8,128)(2,1)} fusion(bf16[4,128,256]{2,1,0:T(8,128)(2,1)S(1)} %copy-done.5, bf16[4,128,256]{2,1,0:T(8,128)(2,1)S(1)} %copy-done.4, bf16[4,256,256]{2,1,0:T(8,128)(2,1)S(1)} %copy-done.1, bf16[4,128,256]{2,1,0:T(8,128)(2,1)S(1)} %copy-done.3, pred[]{:T(512)S(6)} %eq.7, pred[]{:T(512)S(6)} %eq.6), kind=kLoop, calls=%fused_computation.283 | loop fusion | flops 2621440 | bytes 1835010 | tf_op jit(solution)/shard_map/jit(_where)/select_n | solution.py:199
  47.1 0.7 multiply_add_fusion.4
  48.1 4.6 %collective-permute-start.7 = (bf16[614,256]{1,0:T(8,128)(2,1)S(1)}, bf16[614,256]{1,0:T(8,128)(2,1)S(1)}, u32[]{:S(2)}, u32[]{:S(2)}) collective-permute-start(bf16[614,256]{1,0:T(8,128)(2,1)S(1)} %pad_maximum_fusion), channel_id=1, source_target_pairs={{0,2},{1,3},{2,0},{3,1},{4,6},{5,7},{6,4},{7,5},{8,10},{9,11},{10,... | collective-permute-start | bytes 943112 | tf_op jit(solution)/shard_map/ppermute | solution.py:77
  52.8 0.7 fusion.194
  53.4 0.7 multiply_add_fusion.3
  54.1 4.4 %collective-permute-done.7 = bf16[614,256]{1,0:T(8,128)(2,1)S(1)} collective-permute-done((bf16[614,256]{1,0:T(8,128)(2,1)S(1)}, bf16[614,256]{1,0:T(8,128)(2,1)S(1)}, u32[]{:S(2)}, u32[]{:S(2)}) %collective-permute-start.7) | collective-permute-done | bytes 314400 | tf_op jit(solution)/shard_map/ppermute | solution.py:77
  58.7 5.3 %collective-permute-start.8 = (bf16[358,256]{1,0:T(8,128)(2,1)S(1)}, bf16[358,256]{1,0:T(8,128)(2,1)S(1)}, u32[]{:S(2)}, u32[]{:S(2)}) collective-permute-start(bf16[358,256]{1,0:T(8,128)(2,1)S(1)} %pad_maximum_fusion.1), channel_id=1, source_target_pairs={{0,4},{1,5},{2,6},{3,7},{4,0},{5,1},{6,2},{7,3},{8,12},{9,13},{10,... | collective-permute-start | bytes 549896 | tf_op jit(solution)/shard_map/ppermute | solution.py:77
  64.0 0.7 fusion.176
  64.6 4.8 %collective-permute-done.8 = bf16[358,256]{1,0:T(8,128)(2,1)S(1)} collective-permute-done((bf16[358,256]{1,0:T(8,128)(2,1)S(1)}, bf16[358,256]{1,0:T(8,128)(2,1)S(1)}, u32[]{:S(2)}, u32[]{:S(2)}) %collective-permute-start.8) | collective-permute-done | bytes 183328 | tf_op jit(solution)/shard_map/ppermute | solution.py:77
  69.6 2.8 %collective-permute-start.9 = (bf16[230,256]{1,0:T(8,128)(2,1)S(1)}, bf16[230,256]{1,0:T(8,128)(2,1)S(1)}, u32[]{:S(2)}, u32[]{:S(2)}) collective-permute-start(bf16[230,256]{1,0:T(8,128)(2,1)S(1)} %pad_maximum_fusion.2), channel_id=1, source_target_pairs={{0,8},{1,9},{2,10},{3,11},{4,12},{5,13},{6,14},{7,15},{8,0},{9,1},... | collective-permute-start | bytes 353288 | tf_op jit(solution)/shard_map/ppermute | solution.py:77
  72.4 1.1 %fusion.21 = bf16[4,256,256]{2,1,0:T(8,128)(2,1)} fusion(f32[1,256,256]{2,1,0:T(8,128)S(1)} %fusion.176, f32[1,256,256]{2,1,0:T(8,128)S(1)} %multiply_add_fusion.3, f32[1,256,256]{2,1,0:T(8,128)S(1)} %multiply_add_fusion.4, f32[1,256,256]{2,1,0:T(8,128)S(1)} %fusion.194, f32[4,131,256]{2,1,0:T(8,128)S(1)} %get-tuple-element.86, ...), kind=kLoop, calls=%fused_computation.129 | loop fusion | flops 2359296 | bytes 3170306 | tf_op jit(solution)/shard_map/convert_element_type | solution.py:253
  73.5 4.8 %collective-permute-done.9 = bf16[230,256]{1,0:T(8,128)(2,1)S(1)} collective-permute-done((bf16[230,256]{1,0:T(8,128)(2,1)S(1)}, bf16[230,256]{1,0:T(8,128)(2,1)S(1)}, u32[]{:S(2)}, u32[]{:S(2)}) %collective-permute-start.9) | collective-permute-done | bytes 117792 | tf_op jit(solution)/shard_map/ppermute | solution.py:77
  78.3 0.6 fusion.211
  79.0 0.6 convert_add_fusion.8
  79.6 0.6 copy.30
  (224 shorter events, 2.0 us)
Async XLA Ops:
  0.6 17.6 %copy-start = (bf16[256,1024]{1,0:T(8,128)(2,1)S(1)}, bf16[256,1024]{1,0:T(8,128)(2,1)}, u32[]{:S(2)}) copy-start(bf16[256,1024]{1,0:T(8,128)(2,1)} %param.12) | copy-start | bytes 1572868
  0.6 10.8 %copy-start.1 = (bf16[4,256,256]{2,1,0:T(8,128)(2,1)S(1)}, bf16[4,256,256]{2,1,0:T(8,128)(2,1)}, u32[]{:S(2)}) copy-start(bf16[4,256,256]{2,1,0:T(8,128)(2,1)} %param.8) | copy-start | bytes 1572868
  1.9 10.5 %collective-permute-start = (bf16[3,256,256]{2,1,0:T(8,128)(2,1)S(1)}, bf16[3,256,256]{2,1,0:T(8,128)(2,1)S(1)}, u32[]{:S(2)}, u32[]{:S(2)}) collective-permute-start(bf16[3,256,256]{2,1,0:T(8,128)(2,1)S(1)} %get-tuple-element.93), channel_id=1, source_target_pairs={{0,1},{1,2},{2,3},{3,4},{4,5},{5,6},{6,7},{7,8},{8,9},{9,10},{10,1... | collective-permute-start | bytes 1179656 | tf_op jit(solution)/shard_map/ppermute | solution.py:21
  4.3 8.1 %collective-permute-start.1 = (bf16[3,256,256]{2,1,0:T(8,128)(2,1)S(1)}, bf16[3,256,256]{2,1,0:T(8,128)(2,1)S(1)}, u32[]{:S(2)}, u32[]{:S(2)}) collective-permute-start(bf16[3,256,256]{2,1,0:T(8,128)(2,1)S(1)} %get-tuple-element.94), channel_id=1, source_target_pairs={{1,0},{2,1},{3,2},{4,3},{5,4},{6,5},{7,6},{8,7},{9,8},{10,9},{11,1... | collective-permute-start | bytes 1179656 | tf_op jit(solution)/shard_map/ppermute | solution.py:24
  13.2 4.8 %copy-start.84 = (f32[256]{0:T(256)S(1)}, f32[256]{0:T(256)}, u32[]{:S(2)}) copy-start(f32[256]{0:T(256)} %param.11) | copy-start | bytes 3076
  28.9 18.1 %collective-permute-start.6 = (f32[51,256]{1,0:T(8,128)S(1)}, f32[51,256]{1,0:T(8,128)S(1)}, u32[]{:S(2)}, u32[]{:S(2)}) collective-permute-start(f32[51,256]{1,0:T(8,128)S(1)} %concatenate.24), channel_id=1, source_target_pairs={{0,1},{1,0},{2,3},{3,2},{4,5},{5,4},{6,7},{7,6},{8,9},{9,8},{10,11... | collective-permute-start | bytes 156680 | tf_op jit(solution)/shard_map/ppermute | solution.py:69
  35.8 12.0 %collective-permute-start.5 = (f32[512,256]{1,0:T(8,128)S(1)}, f32[512,256]{1,0:T(8,128)S(1)}, u32[]{:S(2)}, u32[]{:S(2)}) collective-permute-start(f32[512,256]{1,0:T(8,128)S(1)} %constant_dynamic-slice_fusion), channel_id=1, source_target_pairs={{0,1},{1,0},{2,3},{3,2},{4,5},{5,4},{6,7},{7,6},{8,9},{9,8},{10,11... | collective-permute-start | bytes 1572872 | tf_op jit(solution)/shard_map/ppermute | solution.py:69
  37.5 4.6 %copy-start.9 = (f32[1,1,256]{2,1,0:T(1,128)S(1)}, f32[1,1,256]{2,1,0:T(1,128)}, u32[]{:S(2)}) copy-start(f32[1,1,256]{2,1,0:T(1,128)} %copy-done.8) | copy-start | bytes 3076
  37.5 4.6 %copy-start.11 = (f32[1,1,256]{2,1,0:T(1,128)S(1)}, f32[1,1,256]{2,1,0:T(1,128)}, u32[]{:S(2)}) copy-start(f32[1,1,256]{2,1,0:T(1,128)} %copy-done.10) | copy-start | bytes 3076
  37.5 4.6 %copy-start.13 = (f32[1,1,256]{2,1,0:T(1,128)S(1)}, f32[1,1,256]{2,1,0:T(1,128)}, u32[]{:S(2)}) copy-start(f32[1,1,256]{2,1,0:T(1,128)} %copy-done.12) | copy-start | bytes 3076
  37.5 4.6 %copy-start.15 = (f32[1,1,256]{2,1,0:T(1,128)S(1)}, f32[1,1,256]{2,1,0:T(1,128)}, u32[]{:S(2)}) copy-start(f32[1,1,256]{2,1,0:T(1,128)} %copy-done.14) | copy-start | bytes 3076
  37.5 4.6 %copy-start.17 = (f32[1,1,256]{2,1,0:T(1,128)S(1)}, f32[1,1,256]{2,1,0:T(1,128)}, u32[]{:S(2)}) copy-start(f32[1,1,256]{2,1,0:T(1,128)} %copy-done.16) | copy-start | bytes 3076
  37.5 4.6 %copy-start.19 = (f32[1,1,256]{2,1,0:T(1,128)S(1)}, f32[1,1,256]{2,1,0:T(1,128)}, u32[]{:S(2)}) copy-start(f32[1,1,256]{2,1,0:T(1,128)} %copy-done.18) | copy-start | bytes 3076
  37.5 4.6 %copy-start.21 = (f32[1,1,256]{2,1,0:T(1,128)S(1)}, f32[1,1,256]{2,1,0:T(1,128)}, u32[]{:S(2)}) copy-start(f32[1,1,256]{2,1,0:T(1,128)} %copy-done.20) | copy-start | bytes 3076
  37.6 4.6 %copy-start.23 = (f32[1,1,256]{2,1,0:T(1,128)S(1)}, f32[1,1,256]{2,1,0:T(1,128)}, u32[]{:S(2)}) copy-start(f32[1,1,256]{2,1,0:T(1,128)} %copy-done.22) | copy-start | bytes 3076
  37.6 4.6 %copy-start.25 = (f32[1,1,256]{2,1,0:T(1,128)S(1)}, f32[1,1,256]{2,1,0:T(1,128)}, u32[]{:S(2)}) copy-start(f32[1,1,256]{2,1,0:T(1,128)} %copy-done.24) | copy-start | bytes 3076
  37.6 4.6 %copy-start.27 = (f32[1,1,256]{2,1,0:T(1,128)S(1)}, f32[1,1,256]{2,1,0:T(1,128)}, u32[]{:S(2)}) copy-start(f32[1,1,256]{2,1,0:T(1,128)} %copy-done.26) | copy-start | bytes 3076
  37.6 4.6 %copy-start.29 = (f32[1,1,256]{2,1,0:T(1,128)S(1)}, f32[1,1,256]{2,1,0:T(1,128)}, u32[]{:S(2)}) copy-start(f32[1,1,256]{2,1,0:T(1,128)} %copy-done.28) | copy-start | bytes 3076
  37.6 4.6 %copy-start.31 = (f32[1,1,256]{2,1,0:T(1,128)S(1)}, f32[1,1,256]{2,1,0:T(1,128)}, u32[]{:S(2)}) copy-start(f32[1,1,256]{2,1,0:T(1,128)} %copy-done.30) | copy-start | bytes 3076
  37.6 4.6 %copy-start.33 = (f32[1,1,256]{2,1,0:T(1,128)S(1)}, f32[1,1,256]{2,1,0:T(1,128)}, u32[]{:S(2)}) copy-start(f32[1,1,256]{2,1,0:T(1,128)} %copy-done.32) | copy-start | bytes 3076
  37.6 4.6 %copy-start.35 = (f32[1,1,256]{2,1,0:T(1,128)S(1)}, f32[1,1,256]{2,1,0:T(1,128)}, u32[]{:S(2)}) copy-start(f32[1,1,256]{2,1,0:T(1,128)} %copy-done.34) | copy-start | bytes 3076
  37.6 4.6 %copy-start.37 = (f32[1,1,256]{2,1,0:T(1,128)S(1)}, f32[1,1,256]{2,1,0:T(1,128)}, u32[]{:S(2)}) copy-start(f32[1,1,256]{2,1,0:T(1,128)} %copy-done.36) | copy-start | bytes 3076
  37.6 4.6 %copy-start.39 = (f32[1,1,256]{2,1,0:T(1,128)S(1)}, f32[1,1,256]{2,1,0:T(1,128)}, u32[]{:S(2)}) copy-start(f32[1,1,256]{2,1,0:T(1,128)} %copy-done.38) | copy-start | bytes 3076
  37.6 4.6 %copy-start.41 = (f32[1,1,256]{2,1,0:T(1,128)S(1)}, f32[1,1,256]{2,1,0:T(1,128)}, u32[]{:S(2)}) copy-start(f32[1,1,256]{2,1,0:T(1,128)} %copy-done.40) | copy-start | bytes 3076
  37.7 4.6 %copy-start.43 = (f32[1,1,256]{2,1,0:T(1,128)S(1)}, f32[1,1,256]{2,1,0:T(1,128)}, u32[]{:S(2)}) copy-start(f32[1,1,256]{2,1,0:T(1,128)} %copy-done.42) | copy-start | bytes 3076
  37.7 4.6 %copy-start.45 = (f32[1,1,256]{2,1,0:T(1,128)S(1)}, f32[1,1,256]{2,1,0:T(1,128)}, u32[]{:S(2)}) copy-start(f32[1,1,256]{2,1,0:T(1,128)} %copy-done.44) | copy-start | bytes 3076
  37.7 4.6 %copy-start.47 = (f32[1,1,256]{2,1,0:T(1,128)S(1)}, f32[1,1,256]{2,1,0:T(1,128)}, u32[]{:S(2)}) copy-start(f32[1,1,256]{2,1,0:T(1,128)} %copy-done.46) | copy-start | bytes 3076
  37.7 4.6 %copy-start.49 = (f32[1,1,256]{2,1,0:T(1,128)S(1)}, f32[1,1,256]{2,1,0:T(1,128)}, u32[]{:S(2)}) copy-start(f32[1,1,256]{2,1,0:T(1,128)} %copy-done.48) | copy-start | bytes 3076
  37.7 4.6 %copy-start.51 = (f32[1,1,256]{2,1,0:T(1,128)S(1)}, f32[1,1,256]{2,1,0:T(1,128)}, u32[]{:S(2)}) copy-start(f32[1,1,256]{2,1,0:T(1,128)} %copy-done.50) | copy-start | bytes 3076
  37.7 4.6 %copy-start.53 = (f32[1,1,256]{2,1,0:T(1,128)S(1)}, f32[1,1,256]{2,1,0:T(1,128)}, u32[]{:S(2)}) copy-start(f32[1,1,256]{2,1,0:T(1,128)} %copy-done.52) | copy-start | bytes 3076
  37.7 4.6 %copy-start.55 = (f32[1,1,256]{2,1,0:T(1,128)S(1)}, f32[1,1,256]{2,1,0:T(1,128)}, u32[]{:S(2)}) copy-start(f32[1,1,256]{2,1,0:T(1,128)} %copy-done.54) | copy-start | bytes 3076
  37.7 4.6 %copy-start.57 = (f32[1,1,256]{2,1,0:T(1,128)S(1)}, f32[1,1,256]{2,1,0:T(1,128)}, u32[]{:S(2)}) copy-start(f32[1,1,256]{2,1,0:T(1,128)} %copy-done.56) | copy-start | bytes 3076
  37.7 4.6 %copy-start.59 = (f32[1,1,256]{2,1,0:T(1,128)S(1)}, f32[1,1,256]{2,1,0:T(1,128)}, u32[]{:S(2)}) copy-start(f32[1,1,256]{2,1,0:T(1,128)} %copy-done.58) | copy-start | bytes 3076
  37.7 4.6 %copy-start.61 = (f32[1,1,256]{2,1,0:T(1,128)S(1)}, f32[1,1,256]{2,1,0:T(1,128)}, u32[]{:S(2)}) copy-start(f32[1,1,256]{2,1,0:T(1,128)} %copy-done.60) | copy-start | bytes 3076
  37.8 4.6 %copy-start.63 = (f32[1,1,256]{2,1,0:T(1,128)S(1)}, f32[1,1,256]{2,1,0:T(1,128)}, u32[]{:S(2)}) copy-start(f32[1,1,256]{2,1,0:T(1,128)} %copy-done.62) | copy-start | bytes 3076
  37.8 4.6 %copy-start.65 = (f32[1,1,256]{2,1,0:T(1,128)S(1)}, f32[1,1,256]{2,1,0:T(1,128)}, u32[]{:S(2)}) copy-start(f32[1,1,256]{2,1,0:T(1,128)} %copy-done.64) | copy-start | bytes 3076
  37.8 4.6 %copy-start.67 = (f32[1,1,256]{2,1,0:T(1,128)S(1)}, f32[1,1,256]{2,1,0:T(1,128)}, u32[]{:S(2)}) copy-start(f32[1,1,256]{2,1,0:T(1,128)} %copy-done.66) | copy-start | bytes 3076
  37.8 4.6 %copy-start.69 = (f32[1,1,256]{2,1,0:T(1,128)S(1)}, f32[1,1,256]{2,1,0:T(1,128)}, u32[]{:S(2)}) copy-start(f32[1,1,256]{2,1,0:T(1,128)} %copy-done.68) | copy-start | bytes 3076
  37.8 4.6 %copy-start.71 = (f32[1,1,256]{2,1,0:T(1,128)S(1)}, f32[1,1,256]{2,1,0:T(1,128)}, u32[]{:S(2)}) copy-start(f32[1,1,256]{2,1,0:T(1,128)} %copy-done.70) | copy-start | bytes 3076
  37.9 10.0 %collective-permute-start.4 = (f32[4,128,256]{2,1,0:T(8,128)S(1)}, f32[4,128,256]{2,1,0:T(8,128)S(1)}, u32[]{:S(2)}, u32[]{:S(2)}) collective-permute-start(f32[4,128,256]{2,1,0:T(8,128)S(1)} %constant_dynamic-slice_fusion.1), channel_id=1, source_target_pairs={{0,1},{1,0},{2,3},{3,2},{4,5},{5,4},{6,7},{7,6},{8,9},{9,8},{10,11... | collective-permute-start | bytes 1572872 | tf_op jit(solution)/shard_map/ppermute | solution.py:69
  38.1 7.8 %copy-start.3 = (bf16[4,128,256]{2,1,0:T(8,128)(2,1)S(1)}, bf16[4,128,256]{2,1,0:T(8,128)(2,1)}, u32[]{:S(2)}) copy-start(bf16[4,128,256]{2,1,0:T(8,128)(2,1)} %get-tuple-element.91) | copy-start | bytes 786436
  38.1 7.8 %copy-start.4 = (bf16[4,128,256]{2,1,0:T(8,128)(2,1)S(1)}, bf16[4,128,256]{2,1,0:T(8,128)(2,1)}, u32[]{:S(2)}) copy-start(bf16[4,128,256]{2,1,0:T(8,128)(2,1)} %get-tuple-element.92) | copy-start | bytes 786436
  38.2 7.8 %copy-start.5 = (bf16[4,128,256]{2,1,0:T(8,128)(2,1)S(1)}, bf16[4,128,256]{2,1,0:T(8,128)(2,1)}, u32[]{:S(2)}) copy-start(bf16[4,128,256]{2,1,0:T(8,128)(2,1)} %get-tuple-element.150) | copy-start | bytes 786436
  38.2 8.8 %collective-permute-start.2 = (bf16[3,256,256]{2,1,0:T(8,128)(2,1)S(1)}, bf16[3,256,256]{2,1,0:T(8,128)(2,1)S(1)}, u32[]{:S(2)}, u32[]{:S(2)}) collective-permute-start(bf16[3,256,256]{2,1,0:T(8,128)(2,1)S(1)} %get-tuple-element.89), channel_id=1, source_target_pairs={{0,1},{1,2},{2,3},{3,4},{4,5},{5,6},{6,7},{7,8},{8,9},{9,10},{10,1... | collective-permute-start | bytes 1179656 | tf_op jit(solution)/shard_map/ppermute | solution.py:98
  40.8 6.3 %collective-permute-start.3 = (bf16[3,256,256]{2,1,0:T(8,128)(2,1)S(1)}, bf16[3,256,256]{2,1,0:T(8,128)(2,1)S(1)}, u32[]{:S(2)}, u32[]{:S(2)}) collective-permute-start(bf16[3,256,256]{2,1,0:T(8,128)(2,1)S(1)} %get-tuple-element.90), channel_id=1, source_target_pairs={{1,0},{2,1},{3,2},{4,3},{5,4},{6,5},{7,6},{8,7},{9,8},{10,9},{11,1... | collective-permute-start | bytes 1179656 | tf_op jit(solution)/shard_map/ppermute | solution.py:99
  48.1 10.4 %collective-permute-start.7 = (bf16[614,256]{1,0:T(8,128)(2,1)S(1)}, bf16[614,256]{1,0:T(8,128)(2,1)S(1)}, u32[]{:S(2)}, u32[]{:S(2)}) collective-permute-start(bf16[614,256]{1,0:T(8,128)(2,1)S(1)} %pad_maximum_fusion), channel_id=1, source_target_pairs={{0,2},{1,3},{2,0},{3,1},{4,6},{5,7},{6,4},{7,5},{8,10},{9,11},{10,... | collective-permute-start | bytes 943112 | tf_op jit(solution)/shard_map/ppermute | solution.py:77
  58.7 10.7 %collective-permute-start.8 = (bf16[358,256]{1,0:T(8,128)(2,1)S(1)}, bf16[358,256]{1,0:T(8,128)(2,1)S(1)}, u32[]{:S(2)}, u32[]{:S(2)}) collective-permute-start(bf16[358,256]{1,0:T(8,128)(2,1)S(1)} %pad_maximum_fusion.1), channel_id=1, source_target_pairs={{0,4},{1,5},{2,6},{3,7},{4,0},{5,1},{6,2},{7,3},{8,12},{9,13},{10,... | collective-permute-start | bytes 549896 | tf_op jit(solution)/shard_map/ppermute | solution.py:77
  69.6 8.7 %collective-permute-start.9 = (bf16[230,256]{1,0:T(8,128)(2,1)S(1)}, bf16[230,256]{1,0:T(8,128)(2,1)S(1)}, u32[]{:S(2)}, u32[]{:S(2)}) collective-permute-start(bf16[230,256]{1,0:T(8,128)(2,1)S(1)} %pad_maximum_fusion.2), channel_id=1, source_target_pairs={{0,8},{1,9},{2,10},{3,11},{4,12},{5,13},{6,14},{7,15},{8,0},{9,1},... | collective-permute-start | bytes 353288 | tf_op jit(solution)/shard_map/ppermute | solution.py:77
  (51 other events, 146.5 us)

commit v24 on v22

--- a/solution.py
+++ b/solution.py
@@ -87,7 +87,6 @@
             whole = mine + theirs
         quartered = keep_q + got_q.astype(jnp.float32)
         rows = keep_r + got_r.astype(jnp.float32)
-        quartered, rows, whole = lax.optimization_barrier((quartered, rows, whole))
     return quartered, rows, whole
 
 

time: 79.1 us -> 90.4 us (1.14)
  local copies, waits for them, and re-layouts: 7.94 us -> 15 us
  other arithmetic: 19.4 us -> 21.7 us
  matrix products: 6.51 us -> 8.05 us
    concatenate x1, local copies, waits for them, and re-layouts: 0.18 us -> 3.55 us  [shards(): jnp.concatenate([kernel_grad, gain_grad[None], scale_grad[None]], axis=0)]
    reduce_sum x3, other arithmetic: 3.22 us -> 5.04 us  [kernel_terms(): jnp.sum(padded[row_tap:row_tap + image_rows, col_tap:col_tap + image_cols...]
    dot_general x1, matrix products: 0.83 us -> 2.12 us  [shards(): branch = jnp.dot(act_flat, w_out, preferred_element_type=jnp.float32)]
    add x4, other arithmetic: 0.76 us -> 1.8 us  [halving_reduce(): rows = keep_r + got_r.astype(jnp.float32)]
    unnamed x183 -> x225, local copies, waits for them, and re-layouts: 2.55 us -> 3.37 us
  transfers between devices with their start and end apart: 10 -> 10, of which waited for: 4 -> 5; matrix products, arithmetic and copies ran while one was open for 18% -> 21% of each run, Pallas kernels for 0% -> 0%
where the time goes in v24:
time: 90.4 us; the launch traced here: 89.9 us
  starting transfers between devices  27.3 us (30%)
  other arithmetic  21.7 us (24%)
  local copies, waits for them, and re-layouts  15 us (17%)
  waiting for transfers between devices  14.9 us (16%)
  matrix products  8.05 us (9%)
  between operations  3.04 us (3%)
    ppermute x3, waiting for transfers between devices, halving_reduce(): got = lax.ppermute(sent, axis, pairs)  13.8 us
    ppermute x3, starting transfers between devices, halving_reduce(): got = lax.ppermute(sent, axis, pairs)  13.7 us
    ppermute x3, starting transfers between devices, halving_reduce(): got_q, got_r, got_whole = lax.ppermute((give_q, give_r, whole), axis, pairs)  6.52 us
    reduce_sum x3, other arithmetic, kernel_terms(): jnp.sum(padded[row_tap:row_tap + image_rows, col_tap:col_tap + image_cols...  5.04 us
    reduce_sum x1, other arithmetic, shards(): centre = jnp.mean(filtered, axis=-1, keepdims=True)  3.85 us
    add x1, other arithmetic, depthwise(): total + padded[row_tap:row_tap + image_rows, col_tap:col_tap + image_cols...  3.66 us
    concatenate x1, local copies, waits for them, and re-layouts, shards(): jnp.concatenate([kernel_grad, gain_grad[None], scale_grad[None]], axis=0)  3.55 us
    unnamed x225, local copies, waits for them, and re-layouts  3.37 us
  transfers between devices with their start and end apart: 10, of which 5 were waited for; matrix products, arithmetic and copies ran while one was open for 21% of the time, Pallas kernels for 0%

profile of v24, /device:TPU:0, one launch (start us, length us, event | category | flops | bytes accessed | tf_op | source)
XLA Modules:
  0.0 89.9 jit_solution(4486935870089281553)
XLA Ops:
  0.7 1.1 %copy.38 = bf16[4,256,256]{2,1,0:T(8,128)(2,1)S(1)} copy(bf16[4,256,256]{2,1,0:T(8,128)(2,1)} %param.8) | data formatting | bytes 1048576
  1.8 2.4 %collective-permute-start = (bf16[3,256,256]{2,1,0:T(8,128)(2,1)S(1)}, bf16[3,256,256]{2,1,0:T(8,128)(2,1)S(1)}, u32[]{:S(2)}, u32[]{:S(2)}) collective-permute-start(bf16[3,256,256]{2,1,0:T(8,128)(2,1)S(1)} %get-tuple-element.75), channel_id=1, source_target_pairs={{0,1},{1,2},{2,3},{3,4},{4,5},{5,6},{6,7},{7,8},{8,9},{9,10},{10,1... | collective-permute-start | bytes 1179656 | tf_op jit(solution)/shard_map/ppermute | solution.py:21
  4.2 1.3 %collective-permute-start.1 = (bf16[3,256,256]{2,1,0:T(8,128)(2,1)S(1)}, bf16[3,256,256]{2,1,0:T(8,128)(2,1)S(1)}, u32[]{:S(2)}, u32[]{:S(2)}) collective-permute-start(bf16[3,256,256]{2,1,0:T(8,128)(2,1)S(1)} %get-tuple-element.76), channel_id=1, source_target_pairs={{1,0},{2,1},{3,2},{4,3},{5,4},{6,5},{7,6},{8,7},{9,8},{10,9},{11,1... | collective-permute-start | bytes 1179656 | tf_op jit(solution)/shard_map/ppermute | solution.py:24
  5.5 0.7 bitcast_reduce_fusion
  6.8 0.6 fusion.228
  7.5 0.7 fusion.229
  8.3 0.7 fusion.225
  9.0 0.9 collective-permute-done.1
  9.9 0.3 fusion.17
  11.1 3.9 %fusion.222 = (f32[4,128]{1,0:T(4,128)S(1)}, f32[4,128,256]{2,1,0:T(8,128)S(1)}) fusion(f32[256]{0:T(256)S(1)} %bitcast.237, f32[10,134,256]{2,1,0:T(8,128)S(1)} %fusion.23, f32[256]{0:T(256)S(1)} %bitcast.242, f32[256]{0:T(256)S(1)} %bitcast.187, f32[256]{0:T(256)S(1)} %bitcast.192, f32[256]{0:T(256)S(1)} %bitcast.197, f32[256]{0:T(256)S(1)} %bitcast.202, ...), kind=kLoop, calls=%fused_computation.407 | loop fusion | flops 12844544 | bytes 26266624 | tf_op jit(solution)/shard_map/reduce_sum | solution.py:160
  15.0 0.2 multiply_reduce_fusion.3
  15.5 0.9 copy.22
  16.4 1.8 %fusion.12 = (bf16[1024,512]{0,1:T(8,128)(2,1)}, f32[512,1024]{1,0:T(8,128)S(1)}) fusion(bf16[512,256]{1,0:T(8,128)(2,1)S(1)} %bitcast.167, bf16[256,1024]{1,0:T(8,128)(2,1)S(1)} %copy-done), kind=kOutput, calls=%fused_computation.115 | convolution fusion | flops 273154048 | bytes 3932160 | tf_op jit(solution)/shard_map/dot_general | solution.py:170
  18.2 2.1 %fusion.122 = (f32[256]{0:T(256)}, bf16[4,128,256]{2,1,0:T(8,128)(2,1)S(1)}, f32[512,256]{1,0:T(8,128)}) fusion(bf16[4,256,256]{2,1,0:T(8,128)(2,1)S(1)} %copy-done.5, pred[]{:T(512)S(6)} %eq.6, f32[256]{0:T(256)S(1)} %copy-done.92, bf16[1024,256]{1,0:T(8,128)(2,1)S(1)} %copy-done.10, f32[512,1024]{1,0:T(8,128)S(1)} %get-tuple-element.132), kind=kOutput, calls=%fused_computation.233 | convolution fusion | flops 273940224 | bytes 3934209 | tf_op jit(solution)/shard_map/dot_general | solution.py:172
  20.3 1.4 %fusion.7 = bf16[512,1024]{1,0:T(8,128)(2,1)S(1)} fusion(f32[512,1024]{1,0:T(8,128)S(1)} %get-tuple-element.132, bf16[512,256]{1,0:T(8,128)(2,1)S(1)} %bitcast.168, bf16[1024,256]{1,0:T(8,128)(2,1)S(1)} %copy-done.10), kind=kOutput, calls=%fused_computation.110 | convolution fusion | flops 278396928 | bytes 3932160 | tf_op jit(solution)/shard_map/dot_general | solution.py:173
  21.8 0.6 multiply_reduce_fusion.2
  22.3 0.8 multiply_reduce_fusion
  23.2 1.8 %fusion.169 = (f32[256]{0:T(256)}, f32[256]{0:T(256)}, f32[256]{0:T(256)}, f32[256]{0:T(256)}, f32[256]{0:T(256)}, /*index=5*/f32[256]{0:T(256)}, f32[256]{0:T(2...) fusion(f32[10,134,256]{2,1,0:T(8,128)S(1)} %fusion.23, ...), kind=kLoop, calls=%fused_computation.280 | loop fusion | flops 4584192 | bytes 8148992 | tf_op jit(solution)/shard_map/reduce_sum | solution.py:139
  25.0 1.6 %fusion.170 = (f32[256]{0:T(256)}, f32[256]{0:T(256)}, f32[256]{0:T(256)}, f32[256]{0:T(256)}, f32[256]{0:T(256)}, /*index=5*/f32[256]{0:T(256)}, f32[256]{0:T(2...) fusion(bf16[4,128,256]{2,1,0:T(8,128)(2,1)S(1)} %get-tuple-elem, ...), kind=kLoop, calls=%fused_computation.281 | loop fusion | flops 4845056 | bytes 9717760 | tf_op jit(solution)/shard_map/reduce_sum | solution.py:139
  26.6 1.6 %fusion.171 = (f32[256]{0:T(256)}, f32[256]{0:T(256)}, f32[256]{0:T(256)}, f32[256]{0:T(256)}, f32[256]{0:T(256)}, /*index=5*/f32[256]{0:T(256)}, f32[256]{0:T(2...) fusion(bf16[4,128,256]{2,1,0:T(8,128)(2,1)S(1)} %get-tuple-elem, ...), kind=kLoop, calls=%fused_computation.282 | loop fusion | flops 4845056 | bytes 9717760 | tf_op jit(solution)/shard_map/reduce_sum | solution.py:139
  28.2 0.5 fusion.18
  28.8 0.8 constant_dynamic-slice_fusion.1
  29.6 6.0 %collective-permute-start.4 = (f32[4,128,256]{2,1,0:T(8,128)}, f32[4,128,256]{2,1,0:T(8,128)S(1)}, u32[]{:S(2)}, u32[]{:S(2)}) collective-permute-start(f32[4,128,256]{2,1,0:T(8,128)} %constant_dynamic-slice_fusion.1), channel_id=1, source_target_pairs={{0,1},{1,0},{2,3},{3,2},{4,5},{5,4},{6,7},{7,6},{8,9},{9,8},{10,11... | collective-permute-start | bytes 1572872 | tf_op jit(solution)/shard_map/ppermute | solution.py:69
  35.6 2.3 %copy.25 = bf16[1024,512]{1,0:T(8,128)(2,1)} copy(bf16[1024,512]{0,1:T(8,128)(2,1)} %get-tuple-element.131) | data formatting | bytes 2097152 | tf_op jit(solution)/shard_map/convert_element_type | solution.py:171
  37.9 1.7 %convolution_bitcast_fusion = f32[2,2,2,2,64,256]{5,4,0,1,2,3:T(8,128)S(1)} fusion(bf16[2,2,2,2,64,512]{5,4,3,2,1,0:T(8,128)(2,1)} %bitcast.163, bf16[512,256,1,1,1,1]{1,0,5,4,3,2:T(8,128)(2,1)S(1)} %bitcast.169), kind=kOutput, calls=%fused_computation.121 | convolution fusion | flops 268435456 | bytes 2359296 | tf_op jit(solution)/shard_map/dot_general | solution.py:186
  40.0 1.0 %copy-done.2 = f32[2,2,2,2,64,256]{5,4,3,2,1,0:T(8,128)} copy-done((f32[2,2,2,2,64,256]{5,4,3,2,1,0:T(8,128)}, f32[2,2,2,2,64,256]{5,4,3,2,1,0:T(8,128)S(1)}, u32[]{:S(2)}) %copy-start.2) | copy-done | bytes 1048600
  41.0 0.9 constant_dynamic-slice_fusion
  42.2 3.6 %concatenate.16 = f32[51,256]{1,0:T(8,128)S(1)} concatenate(f32[1,256]{1,0:T(1,128)} %bitcast.393, f32[1,256]{1,0:T(1,128)} %bitcast.394, f32[1,256]{1,0:T(1,128)} %bitcast.395, f32[1,256]{1,0:T(1,128)} %bitcast.396, f32[1,256]{1,0:T(1,128)} %bitcast.397, f32[1,256]{1,0:T(1,128)} %bitcast.398, f32[1,256]{1,0:T(1,128)} %bitcast.399, f32[1,256]{1,0:T(1,128)} %bitcast.400, ...), dimensions={0} | concatenate | bytes 104448 | tf_op jit(solution)/shard_map/concatenate | solution.py:206
  45.7 0.5 collective-permute-start.6
  46.5 2.1 %collective-permute-start.2 = (bf16[3,256,256]{2,1,0:T(8,128)(2,1)S(1)}, bf16[3,256,256]{2,1,0:T(8,128)(2,1)S(1)}, u32[]{:S(2)}, u32[]{:S(2)}) collective-permute-start(bf16[3,256,256]{2,1,0:T(8,128)(2,1)S(1)} %get-tuple-element.71), channel_id=1, source_target_pairs={{0,1},{1,2},{2,3},{3,4},{4,5},{5,6},{6,7},{7,8},{8,9},{9,10},{10,1... | collective-permute-start | bytes 1179656 | tf_op jit(solution)/shard_map/ppermute | solution.py:97
  48.6 1.3 %collective-permute-start.3 = (bf16[3,256,256]{2,1,0:T(8,128)(2,1)S(1)}, bf16[3,256,256]{2,1,0:T(8,128)(2,1)S(1)}, u32[]{:S(2)}, u32[]{:S(2)}) collective-permute-start(bf16[3,256,256]{2,1,0:T(8,128)(2,1)S(1)} %get-tuple-element.72), channel_id=1, source_target_pairs={{1,0},{2,1},{3,2},{4,3},{5,4},{6,5},{7,6},{8,7},{9,8},{10,9},{11,1... | collective-permute-start | bytes 1179656 | tf_op jit(solution)/shard_map/ppermute | solution.py:98
  49.9 3.7 %fusion.115 = f32[4,134,256]{2,1,0:T(8,128)S(1)} fusion(f32[4,128,256]{2,1,0:T(8,128)S(1)} %get-tuple-element.77, f32[256]{0:T(256)S(1)} %bitcast.178, f32[256]{0:T(256)S(1)} %bitcast.183, f32[256]{0:T(256)S(1)} %bitcast.213, f32[256]{0:T(256)S(1)} %bitcast.233, f32[256]{0:T(256)S(1)} %bitcast.228, f32[256]{0:T(256)S(1)} %bitcast.223, f32[256]{0:T(256)S(1)} %bitcast.218, ...), kind=kLoop, calls=%fused_computation.226 | loop fusion | flops 13309952 | bytes 1123328 | tf_op jit(solution)/shard_map/add | solution.py:127
  54.4 0.7 multiply_add_fusion.4
  55.3 0.3 copy-done.3
  55.6 1.1 %dynamic-slice_add_fusion = f32[512,256]{1,0:T(8,128)S(1)} fusion(f32[512,256]{1,0:T(8,128)} %collective-permute-done.5, f32[1024,256]{1,0:T(8,128)S(1)} %bitcast.162, s32[]{:T(128)S(6)} %select_n.111), kind=kLoop, calls=%fused_computation.284 | loop fusion | flops 131072 | bytes 1572868 | tf_op jit(solution)/shard_map/add | solution.py:89
  56.8 5.7 %collective-permute-start.7 = (bf16[614,256]{1,0:T(8,128)(2,1)S(1)}, bf16[614,256]{1,0:T(8,128)(2,1)S(1)}, u32[]{:S(2)}, u32[]{:S(2)}) collective-permute-start(bf16[614,256]{1,0:T(8,128)(2,1)S(1)} %pad_maximum_fusion), channel_id=1, source_target_pairs={{0,2},{1,3},{2,0},{3,1},{4,6},{5,7},{6,4},{7,5},{8,10},{9,11},{10,... | collective-permute-start | bytes 943112 | tf_op jit(solution)/shard_map/ppermute | solution.py:77
  62.5 0.7 fusion.195
  63.3 0.7 multiply_add_fusion.3
  64.0 4.2 %collective-permute-done.7 = bf16[614,256]{1,0:T(8,128)(2,1)S(1)} collective-permute-done((bf16[614,256]{1,0:T(8,128)(2,1)S(1)}, bf16[614,256]{1,0:T(8,128)(2,1)S(1)}, u32[]{:S(2)}, u32[]{:S(2)}) %collective-permute-start.7) | collective-permute-done | bytes 314400 | tf_op jit(solution)/shard_map/ppermute | solution.py:77
  68.4 5.3 %collective-permute-start.8 = (bf16[358,256]{1,0:T(8,128)(2,1)S(1)}, bf16[358,256]{1,0:T(8,128)(2,1)S(1)}, u32[]{:S(2)}, u32[]{:S(2)}) collective-permute-start(bf16[358,256]{1,0:T(8,128)(2,1)S(1)} %pad_maximum_fusion.1), channel_id=1, source_target_pairs={{0,4},{1,5},{2,6},{3,7},{4,0},{5,1},{6,2},{7,3},{8,12},{9,13},{10,... | collective-permute-start | bytes 549896 | tf_op jit(solution)/shard_map/ppermute | solution.py:77
  73.7 0.7 fusion.177
  74.4 4.7 %collective-permute-done.8 = bf16[358,256]{1,0:T(8,128)(2,1)S(1)} collective-permute-done((bf16[358,256]{1,0:T(8,128)(2,1)S(1)}, bf16[358,256]{1,0:T(8,128)(2,1)S(1)}, u32[]{:S(2)}, u32[]{:S(2)}) %collective-permute-start.8) | collective-permute-done | bytes 183328 | tf_op jit(solution)/shard_map/ppermute | solution.py:77
  79.3 2.8 %collective-permute-start.9 = (bf16[230,256]{1,0:T(8,128)(2,1)S(1)}, bf16[230,256]{1,0:T(8,128)(2,1)S(1)}, u32[]{:S(2)}, u32[]{:S(2)}) collective-permute-start(bf16[230,256]{1,0:T(8,128)(2,1)S(1)} %pad_maximum_fusion.2), channel_id=1, source_target_pairs={{0,8},{1,9},{2,10},{3,11},{4,12},{5,13},{6,14},{7,15},{8,0},{9,1},... | collective-permute-start | bytes 353288 | tf_op jit(solution)/shard_map/ppermute | solution.py:77
  82.1 1.1 %fusion.21 = bf16[4,256,256]{2,1,0:T(8,128)(2,1)} fusion(f32[1,256,256]{2,1,0:T(8,128)S(1)} %fusion.177, f32[1,256,256]{2,1,0:T(8,128)S(1)} %multiply_add_fusion.3, f32[1,256,256]{2,1,0:T(8,128)S(1)} %multiply_add_fusion.4, f32[1,256,256]{2,1,0:T(8,128)S(1)} %fusion.195, f32[4,131,256]{2,1,0:T(8,128)S(1)} %get-tuple-element.68, ...), kind=kLoop, calls=%fused_computation.129 | loop fusion | flops 2359296 | bytes 3170306 | tf_op jit(solution)/shard_map/convert_element_type | solution.py:244
  83.2 4.8 %collective-permute-done.9 = bf16[230,256]{1,0:T(8,128)(2,1)S(1)} collective-permute-done((bf16[230,256]{1,0:T(8,128)(2,1)S(1)}, bf16[230,256]{1,0:T(8,128)(2,1)S(1)}, u32[]{:S(2)}, u32[]{:S(2)}) %collective-permute-start.9) | collective-permute-done | bytes 117792 | tf_op jit(solution)/shard_map/ppermute | solution.py:77
  88.0 0.6 copy.30
  88.7 0.6 fusion.213
  89.3 0.6 convert_add_fusion.8
  (267 shorter events, 2.7 us)
Async XLA Ops:
  0.6 15.7 %copy-start = (bf16[256,1024]{1,0:T(8,128)(2,1)S(1)}, bf16[256,1024]{1,0:T(8,128)(2,1)}, u32[]{:S(2)}) copy-start(bf16[256,1024]{1,0:T(8,128)(2,1)} %param.12) | copy-start | bytes 1572868
  0.6 4.9 %copy-start.111 = (s32[1,2]{1,0:T(1,128)S(1)}, s32[1,2]{1,0:T(1,128)}, u32[]{:S(2)}) copy-start(s32[1,2]{1,0:T(1,128)} %param.9) | copy-start | bytes 28
  0.7 6.2 %copy-start.12 = (f32[7,7,256]{2,1,0:T(8,128)S(1)}, f32[7,7,256]{2,1,0:T(8,128)}, u32[]{:S(2)}) copy-start(f32[7,7,256]{2,1,0:T(8,128)} %param.10) | copy-start | bytes 150532
  1.8 7.2 %collective-permute-start = (bf16[3,256,256]{2,1,0:T(8,128)(2,1)S(1)}, bf16[3,256,256]{2,1,0:T(8,128)(2,1)S(1)}, u32[]{:S(2)}, u32[]{:S(2)}) collective-permute-start(bf16[3,256,256]{2,1,0:T(8,128)(2,1)S(1)} %get-tuple-element.75), channel_id=1, source_target_pairs={{0,1},{1,2},{2,3},{3,4},{4,5},{5,6},{6,7},{7,8},{8,9},{9,10},{10,1... | collective-permute-start | bytes 1179656 | tf_op jit(solution)/shard_map/ppermute | solution.py:21
  4.2 5.7 %collective-permute-start.1 = (bf16[3,256,256]{2,1,0:T(8,128)(2,1)S(1)}, bf16[3,256,256]{2,1,0:T(8,128)(2,1)S(1)}, u32[]{:S(2)}, u32[]{:S(2)}) collective-permute-start(bf16[3,256,256]{2,1,0:T(8,128)(2,1)S(1)} %get-tuple-element.76), channel_id=1, source_target_pairs={{1,0},{2,1},{3,2},{4,3},{5,4},{6,5},{7,6},{8,7},{9,8},{10,9},{11,1... | collective-permute-start | bytes 1179656 | tf_op jit(solution)/shard_map/ppermute | solution.py:24
  7.5 3.1 %copy-start.23 = (f32[1,1,256]{2,1,0:T(1,128)}, f32[1,1,256]{2,1,0:T(1,128)S(1)}, u32[]{:S(2)}) copy-start(f32[1,1,256]{2,1,0:T(1,128)S(1)} %get-tuple-element.87) | copy-start | bytes 3076
  7.5 3.1 %copy-start.25 = (f32[1,1,256]{2,1,0:T(1,128)}, f32[1,1,256]{2,1,0:T(1,128)S(1)}, u32[]{:S(2)}) copy-start(f32[1,1,256]{2,1,0:T(1,128)S(1)} %get-tuple-element.88) | copy-start | bytes 3076
  7.5 3.1 %copy-start.27 = (f32[1,1,256]{2,1,0:T(1,128)}, f32[1,1,256]{2,1,0:T(1,128)S(1)}, u32[]{:S(2)}) copy-start(f32[1,1,256]{2,1,0:T(1,128)S(1)} %get-tuple-element.89) | copy-start | bytes 3076
  11.1 4.1 %copy-start.69 = (f32[256]{0:T(256)S(1)}, f32[256]{0:T(256)}, u32[]{:S(2)}) copy-start(f32[256]{0:T(256)} %param.11) | copy-start | bytes 3076
  28.8 9.1 %copy-start.9 = (bf16[4,128,256]{2,1,0:T(8,128)(2,1)S(1)}, bf16[4,128,256]{2,1,0:T(8,128)(2,1)}, u32[]{:S(2)}) copy-start(bf16[4,128,256]{2,1,0:T(8,128)(2,1)} %copy-done.8) | copy-start | bytes 786436
  29.6 25.5 %collective-permute-start.4 = (f32[4,128,256]{2,1,0:T(8,128)}, f32[4,128,256]{2,1,0:T(8,128)S(1)}, u32[]{:S(2)}, u32[]{:S(2)}) collective-permute-start(f32[4,128,256]{2,1,0:T(8,128)} %constant_dynamic-slice_fusion.1), channel_id=1, source_target_pairs={{0,1},{1,0},{2,3},{3,2},{4,5},{5,4},{6,7},{7,6},{8,9},{9,8},{10,11... | collective-permute-start | bytes 1572872 | tf_op jit(solution)/shard_map/ppermute | solution.py:69
  41.0 8.9 %copy-start.14 = (f32[1,1,256]{2,1,0:T(1,128)S(1)}, f32[1,1,256]{2,1,0:T(1,128)}, u32[]{:S(2)}) copy-start(f32[1,1,256]{2,1,0:T(1,128)} %copy-done.13) | copy-start | bytes 3076
  41.0 8.9 %copy-start.16 = (f32[1,1,256]{2,1,0:T(1,128)S(1)}, f32[1,1,256]{2,1,0:T(1,128)}, u32[]{:S(2)}) copy-start(f32[1,1,256]{2,1,0:T(1,128)} %copy-done.15) | copy-start | bytes 3076
  41.0 8.9 %copy-start.18 = (f32[1,1,256]{2,1,0:T(1,128)S(1)}, f32[1,1,256]{2,1,0:T(1,128)}, u32[]{:S(2)}) copy-start(f32[1,1,256]{2,1,0:T(1,128)} %copy-done.17) | copy-start | bytes 3076
  41.0 8.9 %copy-start.20 = (f32[1,1,256]{2,1,0:T(1,128)S(1)}, f32[1,1,256]{2,1,0:T(1,128)}, u32[]{:S(2)}) copy-start(f32[1,1,256]{2,1,0:T(1,128)} %copy-done.19) | copy-start | bytes 3076
  41.0 8.9 %copy-start.22 = (f32[1,1,256]{2,1,0:T(1,128)S(1)}, f32[1,1,256]{2,1,0:T(1,128)}, u32[]{:S(2)}) copy-start(f32[1,1,256]{2,1,0:T(1,128)} %copy-done.21) | copy-start | bytes 3076
  41.0 8.9 %copy-start.24 = (f32[1,1,256]{2,1,0:T(1,128)S(1)}, f32[1,1,256]{2,1,0:T(1,128)}, u32[]{:S(2)}) copy-start(f32[1,1,256]{2,1,0:T(1,128)} %copy-done.23) | copy-start | bytes 3076
  41.0 8.9 %copy-start.26 = (f32[1,1,256]{2,1,0:T(1,128)S(1)}, f32[1,1,256]{2,1,0:T(1,128)}, u32[]{:S(2)}) copy-start(f32[1,1,256]{2,1,0:T(1,128)} %copy-done.25) | copy-start | bytes 3076
  41.0 8.9 %copy-start.28 = (f32[1,1,256]{2,1,0:T(1,128)S(1)}, f32[1,1,256]{2,1,0:T(1,128)}, u32[]{:S(2)}) copy-start(f32[1,1,256]{2,1,0:T(1,128)} %copy-done.27) | copy-start | bytes 3076
  41.9 13.4 %collective-permute-start.5 = (f32[512,256]{1,0:T(8,128)}, f32[512,256]{1,0:T(8,128)}, u32[]{:S(2)}, u32[]{:S(2)}) collective-permute-start(f32[512,256]{1,0:T(8,128)} %constant_dynamic-slice_fusion), channel_id=1, source_target_pairs={{0,1},{1,0},{2,3},{3,2},{4,5},{5,4},{6,7},{7,6},{8,9},{9,8},{10,11... | collective-permute-start | bytes 1572872 | tf_op jit(solution)/shard_map/ppermute | solution.py:69
  45.7 8.2 %collective-permute-start.6 = (f32[51,256]{1,0:T(8,128)S(1)}, f32[51,256]{1,0:T(8,128)S(1)}, u32[]{:S(2)}, u32[]{:S(2)}) collective-permute-start(f32[51,256]{1,0:T(8,128)S(1)} %concatenate.16), channel_id=1, source_target_pairs={{0,1},{1,0},{2,3},{3,2},{4,5},{5,4},{6,7},{7,6},{8,9},{9,8},{10,11... | collective-permute-start | bytes 156680 | tf_op jit(solution)/shard_map/ppermute | solution.py:69
  46.4 7.3 %copy-start.4 = (f32[512,256]{1,0:T(8,128)S(1)}, f32[512,256]{1,0:T(8,128)}, u32[]{:S(2)}) copy-start(f32[512,256]{1,0:T(8,128)} %get-tuple-element.128) | copy-start | bytes 1572868
  46.4 7.3 %copy-start.7 = (bf16[4,128,256]{2,1,0:T(8,128)(2,1)S(1)}, bf16[4,128,256]{2,1,0:T(8,128)(2,1)}, u32[]{:S(2)}) copy-start(bf16[4,128,256]{2,1,0:T(8,128)(2,1)} %get-tuple-element.74) | copy-start | bytes 786436
  46.4 7.3 %copy-start.93 = (f32[256]{0:T(256)S(1)}, f32[256]{0:T(256)}, u32[]{:S(2)}) copy-start(f32[256]{0:T(256)} %param.14) | copy-start | bytes 3076
  46.5 7.5 %collective-permute-start.2 = (bf16[3,256,256]{2,1,0:T(8,128)(2,1)S(1)}, bf16[3,256,256]{2,1,0:T(8,128)(2,1)S(1)}, u32[]{:S(2)}, u32[]{:S(2)}) collective-permute-start(bf16[3,256,256]{2,1,0:T(8,128)(2,1)S(1)} %get-tuple-element.71), channel_id=1, source_target_pairs={{0,1},{1,2},{2,3},{3,4},{4,5},{5,6},{6,7},{7,8},{8,9},{9,10},{10,1... | collective-permute-start | bytes 1179656 | tf_op jit(solution)/shard_map/ppermute | solution.py:97
  48.6 5.6 %collective-permute-start.3 = (bf16[3,256,256]{2,1,0:T(8,128)(2,1)S(1)}, bf16[3,256,256]{2,1,0:T(8,128)(2,1)S(1)}, u32[]{:S(2)}, u32[]{:S(2)}) collective-permute-start(bf16[3,256,256]{2,1,0:T(8,128)(2,1)S(1)} %get-tuple-element.72), channel_id=1, source_target_pairs={{1,0},{2,1},{3,2},{4,3},{5,4},{6,5},{7,6},{8,7},{9,8},{10,9},{11,1... | collective-permute-start | bytes 1179656 | tf_op jit(solution)/shard_map/ppermute | solution.py:98
  55.1 7.4 %copy-start.56 = (f32[1,1,256]{2,1,0:T(1,128)S(1)}, f32[1,1,256]{2,1,0:T(1,128)}, u32[]{:S(2)}) copy-start(f32[1,1,256]{2,1,0:T(1,128)} %get-tuple-element.92) | copy-start | bytes 3076
  55.1 7.4 %copy-start.58 = (f32[1,1,256]{2,1,0:T(1,128)S(1)}, f32[1,1,256]{2,1,0:T(1,128)}, u32[]{:S(2)}) copy-start(f32[1,1,256]{2,1,0:T(1,128)} %get-tuple-element.93) | copy-start | bytes 3076
  55.1 7.4 %copy-start.60 = (f32[1,1,256]{2,1,0:T(1,128)S(1)}, f32[1,1,256]{2,1,0:T(1,128)}, u32[]{:S(2)}) copy-start(f32[1,1,256]{2,1,0:T(1,128)} %get-tuple-element.94) | copy-start | bytes 3076
  55.1 7.4 %copy-start.62 = (f32[1,1,256]{2,1,0:T(1,128)S(1)}, f32[1,1,256]{2,1,0:T(1,128)}, u32[]{:S(2)}) copy-start(f32[1,1,256]{2,1,0:T(1,128)} %get-tuple-element.95) | copy-start | bytes 3076
  55.1 7.4 %copy-start.64 = (f32[1,1,256]{2,1,0:T(1,128)S(1)}, f32[1,1,256]{2,1,0:T(1,128)}, u32[]{:S(2)}) copy-start(f32[1,1,256]{2,1,0:T(1,128)} %get-tuple-element.96) | copy-start | bytes 3076
  55.1 7.4 %copy-start.66 = (f32[1,1,256]{2,1,0:T(1,128)S(1)}, f32[1,1,256]{2,1,0:T(1,128)}, u32[]{:S(2)}) copy-start(f32[1,1,256]{2,1,0:T(1,128)} %get-tuple-element.97) | copy-start | bytes 3076
  55.1 7.4 %copy-start.68 = (f32[1,1,256]{2,1,0:T(1,128)S(1)}, f32[1,1,256]{2,1,0:T(1,128)}, u32[]{:S(2)}) copy-start(f32[1,1,256]{2,1,0:T(1,128)} %get-tuple-element.99) | copy-start | bytes 3076
  55.3 7.9 %copy-start.34 = (f32[1,1,256]{2,1,0:T(1,128)S(1)}, f32[1,1,256]{2,1,0:T(1,128)}, u32[]{:S(2)}) copy-start(f32[1,1,256]{2,1,0:T(1,128)} %copy-done.33) | copy-start | bytes 3076
  55.3 7.9 %copy-start.36 = (f32[1,1,256]{2,1,0:T(1,128)S(1)}, f32[1,1,256]{2,1,0:T(1,128)}, u32[]{:S(2)}) copy-start(f32[1,1,256]{2,1,0:T(1,128)} %copy-done.35) | copy-start | bytes 3076
  55.3 7.9 %copy-start.38 = (f32[1,1,256]{2,1,0:T(1,128)S(1)}, f32[1,1,256]{2,1,0:T(1,128)}, u32[]{:S(2)}) copy-start(f32[1,1,256]{2,1,0:T(1,128)} %copy-done.37) | copy-start | bytes 3076
  55.3 7.9 %copy-start.40 = (f32[1,1,256]{2,1,0:T(1,128)S(1)}, f32[1,1,256]{2,1,0:T(1,128)}, u32[]{:S(2)}) copy-start(f32[1,1,256]{2,1,0:T(1,128)} %copy-done.39) | copy-start | bytes 3076
  56.8 11.4 %collective-permute-start.7 = (bf16[614,256]{1,0:T(8,128)(2,1)S(1)}, bf16[614,256]{1,0:T(8,128)(2,1)S(1)}, u32[]{:S(2)}, u32[]{:S(2)}) collective-permute-start(bf16[614,256]{1,0:T(8,128)(2,1)S(1)} %pad_maximum_fusion), channel_id=1, source_target_pairs={{0,2},{1,3},{2,0},{3,1},{4,6},{5,7},{6,4},{7,5},{8,10},{9,11},{10,... | collective-permute-start | bytes 943112 | tf_op jit(solution)/shard_map/ppermute | solution.py:77
  63.2 10.5 %copy-start.42 = (f32[1,1,256]{2,1,0:T(1,128)S(1)}, f32[1,1,256]{2,1,0:T(1,128)}, u32[]{:S(2)}) copy-start(f32[1,1,256]{2,1,0:T(1,128)} %get-tuple-element.107) | copy-start | bytes 3076
  63.2 10.5 %copy-start.44 = (f32[1,1,256]{2,1,0:T(1,128)S(1)}, f32[1,1,256]{2,1,0:T(1,128)}, u32[]{:S(2)}) copy-start(f32[1,1,256]{2,1,0:T(1,128)} %get-tuple-element.108) | copy-start | bytes 3076
  63.2 10.5 %copy-start.46 = (f32[1,1,256]{2,1,0:T(1,128)S(1)}, f32[1,1,256]{2,1,0:T(1,128)}, u32[]{:S(2)}) copy-start(f32[1,1,256]{2,1,0:T(1,128)} %get-tuple-element.109) | copy-start | bytes 3076
  63.2 10.4 %copy-start.48 = (f32[1,1,256]{2,1,0:T(1,128)S(1)}, f32[1,1,256]{2,1,0:T(1,128)}, u32[]{:S(2)}) copy-start(f32[1,1,256]{2,1,0:T(1,128)} %get-tuple-element.110) | copy-start | bytes 3076
  63.3 10.4 %copy-start.50 = (f32[1,1,256]{2,1,0:T(1,128)S(1)}, f32[1,1,256]{2,1,0:T(1,128)}, u32[]{:S(2)}) copy-start(f32[1,1,256]{2,1,0:T(1,128)} %get-tuple-element.111) | copy-start | bytes 3076
  63.3 10.4 %copy-start.52 = (f32[1,1,256]{2,1,0:T(1,128)S(1)}, f32[1,1,256]{2,1,0:T(1,128)}, u32[]{:S(2)}) copy-start(f32[1,1,256]{2,1,0:T(1,128)} %get-tuple-element.112) | copy-start | bytes 3076
  63.3 10.4 %copy-start.54 = (f32[1,1,256]{2,1,0:T(1,128)S(1)}, f32[1,1,256]{2,1,0:T(1,128)}, u32[]{:S(2)}) copy-start(f32[1,1,256]{2,1,0:T(1,128)} %get-tuple-element.113) | copy-start | bytes 3076
  68.3 13.8 %copy-start.6 = (bf16[4,256,256]{2,1,0:T(8,128)(2,1)S(1)}, bf16[4,256,256]{2,1,0:T(8,128)(2,1)}, u32[]{:S(2)}) copy-start(bf16[4,256,256]{2,1,0:T(8,128)(2,1)} %param.15) | copy-start | bytes 1572868
  68.4 10.7 %collective-permute-start.8 = (bf16[358,256]{1,0:T(8,128)(2,1)S(1)}, bf16[358,256]{1,0:T(8,128)(2,1)S(1)}, u32[]{:S(2)}, u32[]{:S(2)}) collective-permute-start(bf16[358,256]{1,0:T(8,128)(2,1)S(1)} %pad_maximum_fusion.1), channel_id=1, source_target_pairs={{0,4},{1,5},{2,6},{3,7},{4,0},{5,1},{6,2},{7,3},{8,12},{9,13},{10,... | collective-permute-start | bytes 549896 | tf_op jit(solution)/shard_map/ppermute | solution.py:77
  79.3 8.7 %collective-permute-start.9 = (bf16[230,256]{1,0:T(8,128)(2,1)S(1)}, bf16[230,256]{1,0:T(8,128)(2,1)S(1)}, u32[]{:S(2)}, u32[]{:S(2)}) collective-permute-start(bf16[230,256]{1,0:T(8,128)(2,1)S(1)} %pad_maximum_fusion.2), channel_id=1, source_target_pairs={{0,8},{1,9},{2,10},{3,11},{4,12},{5,13},{6,14},{7,15},{8,0},{9,1},... | collective-permute-start | bytes 353288 | tf_op jit(solution)/shard_map/ppermute | solution.py:77
  (74 other events, 124.9 us)
